TPU v7x, 32 devices: a whole 2x2x4 slice. The times are simulated.
32 devices in a mesh: seq: 8 (over y, x, core), clip: 4 (over z).
Axes of the slice: x: 2, y: 2, z: 4, core: 2. Of those that a mesh axis runs over, the one named last changes fastest.
Arguments:
- raw_tokens: bfloat16 [4, 4096, 1024], P('clip', 'seq'), may hold values from -6 to 6
- teacher: bfloat16 [4, 4096, 1024], P('clip', 'seq'), may hold values from -6 to 6
- keep_rows: int32 [4, 1536], P('clip', 'seq'), may hold values from -1 to 511, as said below
- w_qkv: bfloat16 [1024, 1536], replicated, may hold values from -4 to 4
- w_out: bfloat16 [512, 1024], replicated, may hold values from -0.25 to 0.25
- ln_gain: float32 [1024], replicated, may hold values from 0.1 to 1.9
Outputs:
- align_loss: float32 [], replicated
- grad_qkv: float32 [1572864], P(('seq', 'clip'))
- grad_out: float32 [524288], P(('seq', 'clip'))
- grad_gain: float32 [1024], replicated
Inputs may be any that keep to these rules, and one draw needn't show every extreme that they name: `keep_rows`: in each clip, block s of 192 entries lists its kept local indices (0 to 511) in ascending order followed by -1; the blocks' counts of kept patches lie between 64 and 192 and sum to 1024, and some block of every clip keeps exactly 192.
All inputs are finite; a program needn't handle non-finite values.
Results may differ from a plain program's by a relative error of at most 0.023.
Values may be sent and summed in bfloat16 or wider, within the bound.
No kernel may reach another device: no remote copies, remote signals or barrier semaphores. Data moves between devices by JAX's collectives and lax.ppermute only.
A program may use at most 128 MiB of HBM per device.

v0:
```python
import jax
import jax.numpy as jnp
from jax import lax
from jax.sharding import PartitionSpec as P

HEAD_DIM = 64
TOK_DEV = 128


def shifted(value, axis, steps):
    count = lax.axis_size(axis)
    pairs = [(source, (source + steps) % count) for source in range(count)]
    return lax.ppermute(value, axis, pairs)


def layer_norm(tokens, ln_gain):
    values = tokens.astype(jnp.float32)
    center = values - jnp.mean(values, axis=-1, keepdims=True)
    spread = jnp.mean(center * center, axis=-1, keepdims=True)
    normed = center * lax.rsqrt(spread + 1e-05)
    return (normed, (normed * ln_gain).astype(jnp.bfloat16))


def align_terms(student, target):
    target_f = target.astype(jnp.float32)
    inv_y = lax.rsqrt(jnp.sum(student * student, axis=-1, keepdims=True) + 1e-06)
    inv_t = lax.rsqrt(jnp.sum(target_f * target_f, axis=-1, keepdims=True) + 1e-06)
    differ = student * inv_y - target_f * inv_t
    token_loss = jnp.sum(differ * differ, axis=-1)
    slopes = 2.0 * differ
    grad_y = inv_y * slopes - student * (inv_y * inv_y * inv_y) * jnp.sum(
        slopes * student, axis=-1, keepdims=True
    )
    return (token_loss, grad_y)


def key_mask(key_count, rows, heads):
    slot_idx = jnp.arange(rows, dtype=jnp.int32)
    halves = slot_idx[None, :] < key_count[:, None]
    return jnp.repeat(halves, heads // 2, axis=0)


def head_scores(queries, pair_rows, key_count):
    rows = pair_rows.shape[0]
    heads = queries.shape[1]
    split_kv = pair_rows.reshape(rows, heads, 2, HEAD_DIM)
    scores = (
        jnp.einsum("qhd,khd->hqk", queries, split_kv[:, :, 0], preferred_element_type=jnp.float32)
        * 0.125
    )
    mask_rows = key_mask(key_count, rows, heads)
    return (jnp.where(mask_rows[:, None, :], scores, -1e30), split_kv)


def absorb(state, queries, pair_rows, key_count):
    row_max, row_sum, blended = state
    scores, split_kv = head_scores(queries, pair_rows, key_count)
    new_max = jnp.maximum(row_max, jnp.max(scores, axis=2))
    rescale = jnp.exp(row_max - new_max)
    weights = jnp.exp(scores - new_max[:, :, None])
    row_sum = row_sum * rescale + jnp.sum(weights, axis=2)
    blended = blended * rescale[:, :, None] + jnp.einsum(
        "hqk,khd->hqd",
        weights.astype(jnp.bfloat16),
        split_kv[:, :, 1],
        preferred_element_type=jnp.float32,
    )
    return (new_max, row_sum, blended)


def contribution(queries, grad_heads, log_total, row_dot, pair_rows, key_count):
    scores, split_kv = head_scores(queries, pair_rows, key_count)
    prob_full = jnp.exp(scores - log_total[:, :, None])
    d_value = jnp.einsum(
        "hqk,qhd->khd",
        prob_full.astype(jnp.bfloat16),
        grad_heads,
        preferred_element_type=jnp.float32,
    )
    d_prob = jnp.einsum(
        "qhd,khd->hqk", grad_heads, split_kv[:, :, 1], preferred_element_type=jnp.float32
    )
    d_score = (prob_full * (d_prob - row_dot[:, :, None])).astype(jnp.bfloat16)
    d_query = 0.125 * jnp.einsum(
        "hqk,khd->qhd", d_score, split_kv[:, :, 0], preferred_element_type=jnp.float32
    )
    d_key = 0.125 * jnp.einsum("hqk,qhd->khd", d_score, queries, preferred_element_type=jnp.float32)
    rows = pair_rows.shape[0]
    return (d_query, jnp.stack([d_key, d_value], axis=2).reshape(rows, -1))


def move_keys(pair_rows):
    moved = shifted(pair_rows, "seq", 1)
    return moved


def move_grads(accum):
    moved = shifted(accum.astype(jnp.bfloat16), "seq", 1).astype(accum.dtype)
    return moved


def per_device(raw_tokens, teacher, keep_rows, w_qkv, w_out, ln_gain):
    shards = lax.axis_size("seq")
    my_index = lax.axis_index("seq")
    row_ids = keep_rows[0]
    list_slots = row_ids.shape[0]
    is_kept = row_ids >= 0
    kept_count = jnp.sum(is_kept.astype(jnp.int32))
    safe_ids = jnp.maximum(row_ids, 0)
    kept_tokens = jnp.where(is_kept[:, None], raw_tokens[0][safe_ids], jnp.zeros((), jnp.bfloat16))
    kept_target = jnp.where(is_kept[:, None], teacher[0][safe_ids], jnp.zeros((), jnp.bfloat16))
    count_table = lax.all_gather(kept_count.reshape(1), "seq", axis=0, tiled=True)
    shard_ids = jnp.arange(shards, dtype=jnp.int32)
    per_peer = -(-list_slots // shards)
    starts = jnp.cumsum(count_table) - count_table
    before = jnp.sum(jnp.where(shard_ids < my_index, count_table, 0))
    slot_ids = jnp.arange(per_peer, dtype=jnp.int32)
    pick = (shard_ids[:, None] - before) % shards + slot_ids[None, :] * shards
    pick_ok = pick < kept_count
    pick_safe = jnp.minimum(pick, list_slots - 1)
    send_tokens = jnp.where(
        pick_ok[:, :, None], kept_tokens[pick_safe], jnp.zeros((), jnp.bfloat16)
    )
    send_target = jnp.where(
        pick_ok[:, :, None], kept_target[pick_safe], jnp.zeros((), jnp.bfloat16)
    )
    got_tokens, got_target = (
        lax.all_to_all(send_tokens, "seq", split_axis=0, concat_axis=0, tiled=True),
        lax.all_to_all(send_target, "seq", split_axis=0, concat_axis=0, tiled=True),
    )
    from_pick = (my_index - starts[:, None]) % shards + slot_ids[None, :] * shards
    from_ok = from_pick < count_table[:, None]
    place = jnp.where(from_ok, (starts[:, None] + from_pick) // shards, TOK_DEV).reshape(-1)
    width = got_tokens.shape[2]
    tokens = (
        jnp.zeros((TOK_DEV, width), jnp.bfloat16)
        .at[place]
        .set(got_tokens.reshape(-1, width), mode="drop")
    )
    target = (
        jnp.zeros((TOK_DEV, width), jnp.bfloat16)
        .at[place]
        .set(got_target.reshape(-1, width), mode="drop")
    )
    live_count = jnp.full((), TOK_DEV, jnp.int32)
    anchor_table = jnp.full((shards,), TOK_DEV, jnp.int32)

    def counts_at(step):
        front_count = jnp.sum(jnp.where(shard_ids == (my_index - step) % shards, anchor_table, 0))
        return jnp.stack([front_count, front_count])

    rows = tokens.shape[0]
    inner = w_out.shape[0]
    heads = inner // HEAD_DIM
    normed, hidden = layer_norm(tokens, ln_gain)
    projected = jnp.dot(hidden, w_qkv, preferred_element_type=jnp.float32)
    queries = projected[:, :inner].astype(jnp.bfloat16).reshape(rows, heads, HEAD_DIM)
    pair_rows = projected[:, inner:].astype(jnp.bfloat16)
    start_state = (
        jnp.full((heads, rows), -1e30, jnp.float32),
        jnp.zeros((heads, rows), jnp.float32),
        jnp.zeros((heads, rows, HEAD_DIM), jnp.float32),
    )
    steps_ids = jnp.arange(1, shards, dtype=jnp.int32)
    own_count = counts_at(jnp.zeros((), jnp.int32))
    state = absorb(start_state, queries, pair_rows, own_count)

    def forward_step(carry, step):
        travel_rows, inner_state = carry
        travel_rows = move_keys(travel_rows)
        inner_state = absorb(inner_state, queries, travel_rows, counts_at(step))
        return ((travel_rows, inner_state), travel_rows)

    (unused_rows, state), stored_rows = lax.scan(forward_step, (pair_rows, state), steps_ids)
    row_max, row_sum, blended = state
    log_total = row_max + jnp.log(row_sum)
    attended = (
        (blended / row_sum[:, :, None]).transpose(1, 0, 2).reshape(rows, inner).astype(jnp.bfloat16)
    )
    student = tokens.astype(jnp.float32) + jnp.dot(
        attended, w_out, preferred_element_type=jnp.float32
    )
    token_loss, grad_y = align_terms(student, target)
    is_live = jnp.arange(rows, dtype=jnp.int32) < live_count
    token_loss = jnp.where(is_live, token_loss, 0.0)
    grad_b = jnp.where(is_live[:, None], grad_y, 0.0).astype(jnp.bfloat16)
    grad_wout = jnp.dot(attended.T, grad_b, preferred_element_type=jnp.float32)
    grad_heads = (
        jnp.dot(grad_b, w_out.T, preferred_element_type=jnp.float32)
        .astype(jnp.bfloat16)
        .reshape(rows, heads, HEAD_DIM)
    )
    row_dot = jnp.sum(
        grad_heads.astype(jnp.float32)
        * attended.reshape(rows, heads, HEAD_DIM).astype(jnp.float32),
        axis=2,
    ).T
    d_query, accum = contribution(queries, grad_heads, log_total, row_dot, pair_rows, own_count)

    def backward_step(carry, stored):
        query_sum, travel_grads = carry
        block_rows, step = stored
        travel_grads = move_grads(travel_grads)
        part_query, part_pairs = contribution(
            queries, grad_heads, log_total, row_dot, block_rows, counts_at(step)
        )
        return ((query_sum + part_query, travel_grads + part_pairs), None)

    (d_query, accum), unused_out = lax.scan(
        backward_step, (d_query, accum), (stored_rows, steps_ids)
    )
    accum = move_grads(accum)
    d_proj = jnp.concatenate([d_query.reshape(rows, inner), accum], axis=1).astype(jnp.bfloat16)
    grad_wqkv = jnp.dot(hidden.T, d_proj, preferred_element_type=jnp.float32)
    d_hidden = jnp.dot(d_proj, w_qkv.T, preferred_element_type=jnp.float32)
    grad_ln = jnp.sum(d_hidden * normed, axis=0)
    loss_part = jnp.sum(token_loss)
    loss_total, grad_gain = lax.psum((loss_part, grad_ln), ("seq", "clip"))
    grad_qkv, grad_out = (
        lax.psum_scatter(grad_wqkv.reshape(-1), ("seq", "clip"), scatter_dimension=0, tiled=True),
        lax.psum_scatter(grad_wout.reshape(-1), ("seq", "clip"), scatter_dimension=0, tiled=True),
    )
    count_all = shards * lax.axis_size("clip") * TOK_DEV
    return (loss_total / count_all, grad_qkv, grad_out, grad_gain)


def solution(mesh):
    placed = (P("clip", "seq", None), P("clip", "seq", None), P("clip", "seq"), P(), P(), P())
    return jax.shard_map(
        per_device,
        mesh=mesh,
        in_specs=placed,
        out_specs=(P(), P(("seq", "clip")), P(("seq", "clip")), P()),
        check_vma=False,
    )
```

profile of v0, /device:TPU:0, one launch (start us, length us, event | category | flops | bytes accessed | tf_op | source)
XLA Modules:
  0.0 467.7 jit_solution(4523291267699020806)
XLA Ops:
  12.1 9.5 %all-reduce = s32[8]{0:T(128)S(1)} all-reduce(s32[8]{0:T(128)S(1)} %dynamic-update-slice), channel_id=1, replica_groups=mesh['seq'=8,'clip'=4] {'seq'}, use_global_device_ids=true, to_apply=%add | all-reduce | flops 8 | bytes 64
  24.9 3.4 gather_fusion.2
  28.3 3.4 gather_fusion
  31.8 2.0 broadcast_select_fusion
  33.8 3.1 gather_fusion.3
  38.6 2.1 broadcast_select_fusion.2
  40.8 3.5 all-to-all-start
  48.9 3.6 all-to-all-done
  52.5 4.1 all-to-all-start.1
  65.4 2.1 scatter_custom_fusion.1
  68.2 80.9 %while.36 = (s32[]{:T(128)}, bf16[128,1024]{0,1:T(8,128)(2,1)}, f32[8,128]{1,0:T(8,128)S(1)}, f32[8,128]{1,0:T(8,128)S(1)}, f32[8,128,64]{1,2,0:T(8,128)}, /*ind...) while((s32[]{:T(128)}, bf16[128,1024]{0,1:T(8,128)(2,1)}, ...), condition=%wide.region_13.14_spmd.clone, body=%wide.region_9.13_spmd.clone.sunk | while | flops 34605352 | bytes 4655954 | solution.py:174
  71.8 3.3 collective-permute-done
  83.0 3.6 collective-permute-done
  94.5 3.6 collective-permute-done
  106.1 3.6 collective-permute-done
  117.6 3.6 collective-permute-done
  129.2 3.6 collective-permute-done
  140.8 3.6 collective-permute-done
  162.3 94.8 %while.37 = (s32[]{:T(128)}, f32[128,8,64]{0,2,1:T(8,128)}, bf16[128,1024]{0,1:T(8,128)(2,1)}, bf16[7,128,1024]{1,2,0:T(8,128)(2,1)}, s32[7]{0:T(128)}, /*index=...) while((s32[]{:T(128)}, f32[128,8,64]{0,2,1:T(8,128)}, ...), condition=%wide.region_24.25_spmd.clone, body=%wide.region_22.24_spmd.clone.sunk | while | flops 85524776 | bytes 10103662 | solution.py:209
  171.7 1.9 fusion.107
  184.7 1.9 fusion.107
  198.0 1.9 fusion.107
  201.7 3.3 collective-permute-start.1
  214.3 1.9 fusion.107
  227.4 1.9 fusion.107
  240.4 1.9 fusion.107
  253.5 1.9 fusion.107
  264.7 3.8 fusion.40
  268.5 6.9 %reshape.396 = f32[1572864]{0:T(1024)} reshape(f32[1024,1536]{1,0:T(8,128)} %fusion.40) | data formatting | bytes 12582912 | tf_op jit(solution)/shard_map/reshape | solution.py:220
  276.7 2.1 fusion.23
  278.8 42.3 %all-reduce.3 = (f32[]{:T(128)}, f32[1024]{0:T(1024)}) all-reduce(f32[]{:T(128)} %select_reduce_fusion, f32[1024]{0:T(1024)S(1)} %fusion.23), channel_id=1, replica_groups=mesh['seq'=8,'clip'=4] {'seq','clip'}, use_global_device_ids=true, to_apply=%region_19.20 | all-reduce | flops 1025 | bytes 8200 | tf_op jit(solution)/shard_map/psum | solution.py:218
  321.8 134.8 %all-reduce.7.cloned.1.call-done = (f32[1572864]{0:T(1024)}, f32[524288]{0:T(1024)}) async-done(((f32[1572864]{0:T(1024)}, f32[524288]{0:T(1024)}), (f32[1572864]{0:T(1024)}, f32[524288]{0:T(1024)})) %all-reduce.7.cloned.1.call-update) | async-done | bytes 8388624
  (346 shorter events, 173.3 us)
Async XLA Ops:
  7.2 51.8 %copy-start = (bf16[1024,1536]{1,0:T(8,128)(2,1)S(1)}, bf16[1024,1536]{1,0:T(8,128)(2,1)}, u32[]{:S(2)}) copy-start(bf16[1024,1536]{1,0:T(8,128)(2,1)} %param.13) | copy-start | bytes 9437188
  38.6 20.3 %copy-start.15 = (f32[1024]{0:T(1024)S(1)}, f32[1024]{0:T(1024)}, u32[]{:S(2)}) copy-start(f32[1024]{0:T(1024)} %param.15) | copy-start | bytes 12292
  40.8 11.7 %all-to-all-start = ((bf16[8,24,1024]{2,1,0:T(8,128)(2,1)}), bf16[8,24,1024]{2,1,0:T(8,128)(2,1)S(1)}, u32[]{:S(2)}, u32[]{:S(2)}) async-start(bf16[8,24,1024]{2,1,0:T(8,128)(2,1)} %get-tuple-element.410), calls=%async_computation | async-start | bytes 786432 | tf_op jit(solution)/shard_map/all_to_all | solution.py:128
  48.9 10.7 %copy-start.27 = (s32[192,1]{0,1:T(1,128)}, s32[192,1]{0,1:T(1,128)S(1)}, u32[]{:S(2)}) copy-start(s32[192,1]{0,1:T(1,128)S(1)} %compare_select_fusion.3) | copy-start | bytes 2308
  52.5 4.2 copy-start.13
  52.5 12.8 %all-to-all-start.1 = ((bf16[8,24,1024]{2,1,0:T(8,128)(2,1)}), bf16[8,24,1024]{2,1,0:T(8,128)(2,1)}, u32[]{:S(2)}, u32[]{:S(2)}) async-start(bf16[8,24,1024]{2,1,0:T(8,128)(2,1)} %get-tuple-element.409), calls=%async_computation.1 | async-start | bytes 786432 | tf_op jit(solution)/shard_map/all_to_all | solution.py:129
  56.6 400.0 %all-reduce.7.cloned.1.call-start = ((), (), s32[]{:S(2)}) async-start(), calls=%async_computation.2 | async-start | bytes 16777216
  59.0 3.3 copy-start.30
  61.5 3.8 copy-start.9
  67.6 85.7 %copy-start.22 = (f32[128]{0:T(128)}, f32[128]{0:T(128)S(1)}, u32[]{:S(2)}) copy-start(f32[128]{0:T(128)S(1)} %add_rsqrt_fusion) | copy-start | bytes 1540
  68.2 6.9 %collective-permute-start = (bf16[128,1024]{0,1:T(8,128)(2,1)}, bf16[128,1024]{0,1:T(8,128)(2,1)S(1)}, u32[]{:S(2)}, u32[]{:S(2)}) collective-permute-start(bf16[128,1024]{0,1:T(8,128)(2,1)} %get-tuple-element.561), channel_id=1, source_target_pairs={{0,4},{4,8},{8,12},{12,16},{16,20},{20,24},{24,28},{28,0},{1,5},{5... | collective-permute-start | bytes 786440 | tf_op jit(solution)/shard_map/while/body/eval_jaxpr/ppermute | solution.py:13
  79.7 6.9 %collective-permute-start = (bf16[128,1024]{0,1:T(8,128)(2,1)}, bf16[128,1024]{0,1:T(8,128)(2,1)S(1)}, u32[]{:S(2)}, u32[]{:S(2)}) collective-permute-start(bf16[128,1024]{0,1:T(8,128)(2,1)} %get-tuple-element.561), channel_id=1, source_target_pairs={{0,4},{4,8},{8,12},{12,16},{16,20},{20,24},{24,28},{28,0},{1,5},{5... | collective-permute-start | bytes 786440 | tf_op jit(solution)/shard_map/while/body/eval_jaxpr/ppermute | solution.py:13
  91.3 6.9 %collective-permute-start = (bf16[128,1024]{0,1:T(8,128)(2,1)}, bf16[128,1024]{0,1:T(8,128)(2,1)S(1)}, u32[]{:S(2)}, u32[]{:S(2)}) collective-permute-start(bf16[128,1024]{0,1:T(8,128)(2,1)} %get-tuple-element.561), channel_id=1, source_target_pairs={{0,4},{4,8},{8,12},{12,16},{16,20},{20,24},{24,28},{28,0},{1,5},{5... | collective-permute-start | bytes 786440 | tf_op jit(solution)/shard_map/while/body/eval_jaxpr/ppermute | solution.py:13
  102.8 6.9 %collective-permute-start = (bf16[128,1024]{0,1:T(8,128)(2,1)}, bf16[128,1024]{0,1:T(8,128)(2,1)S(1)}, u32[]{:S(2)}, u32[]{:S(2)}) collective-permute-start(bf16[128,1024]{0,1:T(8,128)(2,1)} %get-tuple-element.561), channel_id=1, source_target_pairs={{0,4},{4,8},{8,12},{12,16},{16,20},{20,24},{24,28},{28,0},{1,5},{5... | collective-permute-start | bytes 786440 | tf_op jit(solution)/shard_map/while/body/eval_jaxpr/ppermute | solution.py:13
  114.4 6.9 %collective-permute-start = (bf16[128,1024]{0,1:T(8,128)(2,1)}, bf16[128,1024]{0,1:T(8,128)(2,1)S(1)}, u32[]{:S(2)}, u32[]{:S(2)}) collective-permute-start(bf16[128,1024]{0,1:T(8,128)(2,1)} %get-tuple-element.561), channel_id=1, source_target_pairs={{0,4},{4,8},{8,12},{12,16},{16,20},{20,24},{24,28},{28,0},{1,5},{5... | collective-permute-start | bytes 786440 | tf_op jit(solution)/shard_map/while/body/eval_jaxpr/ppermute | solution.py:13
  125.9 6.9 %collective-permute-start = (bf16[128,1024]{0,1:T(8,128)(2,1)}, bf16[128,1024]{0,1:T(8,128)(2,1)S(1)}, u32[]{:S(2)}, u32[]{:S(2)}) collective-permute-start(bf16[128,1024]{0,1:T(8,128)(2,1)} %get-tuple-element.561), channel_id=1, source_target_pairs={{0,4},{4,8},{8,12},{12,16},{16,20},{20,24},{24,28},{28,0},{1,5},{5... | collective-permute-start | bytes 786440 | tf_op jit(solution)/shard_map/while/body/eval_jaxpr/ppermute | solution.py:13
  137.5 6.9 %collective-permute-start = (bf16[128,1024]{0,1:T(8,128)(2,1)}, bf16[128,1024]{0,1:T(8,128)(2,1)S(1)}, u32[]{:S(2)}, u32[]{:S(2)}) collective-permute-start(bf16[128,1024]{0,1:T(8,128)(2,1)} %get-tuple-element.561), channel_id=1, source_target_pairs={{0,4},{4,8},{8,12},{12,16},{16,20},{20,24},{24,28},{28,0},{1,5},{5... | collective-permute-start | bytes 786440 | tf_op jit(solution)/shard_map/while/body/eval_jaxpr/ppermute | solution.py:13
  149.0 3.5 copy-start.8
  149.0 4.8 %copy-start.12 = (bf16[512,1024]{1,0:T(8,128)(2,1)S(1)}, bf16[512,1024]{1,0:T(8,128)(2,1)}, u32[]{:S(2)}) copy-start(bf16[512,1024]{1,0:T(8,128)(2,1)} %param.14) | copy-start | bytes 3145732
  149.0 4.8 %copy-start.28 = (pred[128]{0:T(512)(128)(4,1)S(1)}, pred[128]{0:T(512)(128)(4,1)}, u32[]{:S(2)}) copy-start(pred[128]{0:T(512)(128)(4,1)} %iota_compare_fusion.3) | copy-start | bytes 388
  152.5 3.6 copy-start.2
  156.0 3.4 copy-start.10
  162.3 97.6 %copy-start.21 = (f32[128]{0:T(128)S(1)}, f32[128]{0:T(128)}, u32[]{:S(2)}) copy-start(f32[128]{0:T(128)} %copy-done.20) | copy-start | bytes 1540
  162.3 97.6 %copy-start.23 = (f32[128]{0:T(128)S(1)}, f32[128]{0:T(128)}, u32[]{:S(2)}) copy-start(f32[128]{0:T(128)} %copy-done.22) | copy-start | bytes 1540
  162.3 11.3 %collective-permute-start.1 = (bf16[128,1024]{0,1:T(8,128)(2,1)}, bf16[128,1024]{0,1:T(8,128)(2,1)}, u32[]{:S(2)}, u32[]{:S(2)}) collective-permute-start(bf16[128,1024]{0,1:T(8,128)(2,1)} %get-tuple-element.602), channel_id=1, source_target_pairs={{0,4},{4,8},{8,12},{12,16},{16,20},{20,24},{24,28},{28,0},{1,5},{5... | collective-permute-start | bytes 786440 | tf_op jit(solution)/shard_map/while/body/eval_jaxpr/ppermute | solution.py:13
  175.4 11.3 %collective-permute-start.1 = (bf16[128,1024]{0,1:T(8,128)(2,1)}, bf16[128,1024]{0,1:T(8,128)(2,1)}, u32[]{:S(2)}, u32[]{:S(2)}) collective-permute-start(bf16[128,1024]{0,1:T(8,128)(2,1)} %get-tuple-element.602), channel_id=1, source_target_pairs={{0,4},{4,8},{8,12},{12,16},{16,20},{20,24},{24,28},{28,0},{1,5},{5... | collective-permute-start | bytes 786440 | tf_op jit(solution)/shard_map/while/body/eval_jaxpr/ppermute | solution.py:13
  188.4 11.6 %collective-permute-start.1 = (bf16[128,1024]{0,1:T(8,128)(2,1)}, bf16[128,1024]{0,1:T(8,128)(2,1)}, u32[]{:S(2)}, u32[]{:S(2)}) collective-permute-start(bf16[128,1024]{0,1:T(8,128)(2,1)} %get-tuple-element.602), channel_id=1, source_target_pairs={{0,4},{4,8},{8,12},{12,16},{16,20},{20,24},{24,28},{28,0},{1,5},{5... | collective-permute-start | bytes 786440 | tf_op jit(solution)/shard_map/while/body/eval_jaxpr/ppermute | solution.py:13
  201.7 14.6 %collective-permute-start.1 = (bf16[128,1024]{0,1:T(8,128)(2,1)}, bf16[128,1024]{0,1:T(8,128)(2,1)}, u32[]{:S(2)}, u32[]{:S(2)}) collective-permute-start(bf16[128,1024]{0,1:T(8,128)(2,1)} %get-tuple-element.602), channel_id=1, source_target_pairs={{0,4},{4,8},{8,12},{12,16},{16,20},{20,24},{24,28},{28,0},{1,5},{5... | collective-permute-start | bytes 786440 | tf_op jit(solution)/shard_map/while/body/eval_jaxpr/ppermute | solution.py:13
  218.0 11.3 %collective-permute-start.1 = (bf16[128,1024]{0,1:T(8,128)(2,1)}, bf16[128,1024]{0,1:T(8,128)(2,1)}, u32[]{:S(2)}, u32[]{:S(2)}) collective-permute-start(bf16[128,1024]{0,1:T(8,128)(2,1)} %get-tuple-element.602), channel_id=1, source_target_pairs={{0,4},{4,8},{8,12},{12,16},{16,20},{20,24},{24,28},{28,0},{1,5},{5... | collective-permute-start | bytes 786440 | tf_op jit(solution)/shard_map/while/body/eval_jaxpr/ppermute | solution.py:13
  231.1 11.3 %collective-permute-start.1 = (bf16[128,1024]{0,1:T(8,128)(2,1)}, bf16[128,1024]{0,1:T(8,128)(2,1)}, u32[]{:S(2)}, u32[]{:S(2)}) collective-permute-start(bf16[128,1024]{0,1:T(8,128)(2,1)} %get-tuple-element.602), channel_id=1, source_target_pairs={{0,4},{4,8},{8,12},{12,16},{16,20},{20,24},{24,28},{28,0},{1,5},{5... | collective-permute-start | bytes 786440 | tf_op jit(solution)/shard_map/while/body/eval_jaxpr/ppermute | solution.py:13
  244.1 11.3 %collective-permute-start.1 = (bf16[128,1024]{0,1:T(8,128)(2,1)}, bf16[128,1024]{0,1:T(8,128)(2,1)}, u32[]{:S(2)}, u32[]{:S(2)}) collective-permute-start(bf16[128,1024]{0,1:T(8,128)(2,1)} %get-tuple-element.602), channel_id=1, source_target_pairs={{0,4},{4,8},{8,12},{12,16},{16,20},{20,24},{24,28},{28,0},{1,5},{5... | collective-permute-start | bytes 786440 | tf_op jit(solution)/shard_map/while/body/eval_jaxpr/ppermute | solution.py:13
  257.1 6.9 %collective-permute-start.2 = (bf16[128,1024]{0,1:T(8,128)(2,1)}, bf16[128,1024]{0,1:T(8,128)(2,1)S(1)}, u32[]{:S(2)}, u32[]{:S(2)}) collective-permute-start(bf16[128,1024]{0,1:T(8,128)(2,1)} %get-tuple-element.277), channel_id=1, source_target_pairs={{0,4},{4,8},{8,12},{12,16},{16,20},{20,24},{24,28},{28,0},{1,5},{5... | collective-permute-start | bytes 786440 | tf_op jit(solution)/shard_map/ppermute | solution.py:13
  (23 other events, 34.5 us)
Sparse Core Ops, SparseCore 0:
  275.6 180.9 all-reduce.6
where the time goes:
time: 471 us; the launch traced here: 468 us
  waiting for transfers between devices  164 us (35%)
  local copies, waits for them, and re-layouts  80.6 us (17%)
  matrix products  74.6 us (16%)
  other arithmetic  57.4 us (12%)
  blocking collectives  51.8 us (11%)
  between operations  16.3 us (3%)
  starting transfers between devices  13.3 us (3%)
  loops' own time  9.76 us (2%)
    unnamed x2, waiting for transfers between devices  135 us
    psum x1, blocking collectives, per_device(): loss_total, grad_gain = lax.psum((loss_part, grad_ln), ('seq', 'clip'))  42.3 us
    ppermute x15, waiting for transfers between devices, shifted(): return lax.ppermute(value, axis, pairs)  25.5 us
    dot_general x15, matrix products, head_scores(): jnp.einsum('qhd,khd->hqk', queries, split_kv[:, :, 0], preferred_element_...  19.1 us
    dynamic_slice x14, local copies, waits for them, and re-layouts, per_device(): lax.scan(forward_step, (pair_rows, state), steps_ids)  17 us
    dot_general x8, matrix products, contribution(): jnp.einsum('hqk,khd->qhd', d_score, split_kv[:, :, 0], preferred_element_...  14.3 us
    dot_general x8, matrix products, absorb(): jnp.einsum('hqk,khd->hqd', weights.astype(jnp.bfloat16), split_kv[:, :, 1...  13.9 us
    unnamed x68, local copies, waits for them, and re-layouts  12.5 us
  transfers between devices with their start and end apart: 18, of which 10 were waited for; matrix products, arithmetic and copies ran while one was open for 24% of the time, Pallas kernels for 0%

commit v1 on v0

--- a/solution.py
+++ b/solution.py
@@ -217,8 +217,8 @@
     loss_part = jnp.sum(token_loss)
     loss_total, grad_gain = lax.psum((loss_part, grad_ln), ("seq", "clip"))
     grad_qkv, grad_out = (
-        lax.psum_scatter(grad_wqkv.reshape(-1), ("seq", "clip"), scatter_dimension=0, tiled=True),
-        lax.psum_scatter(grad_wout.reshape(-1), ("seq", "clip"), scatter_dimension=0, tiled=True),
+        lax.psum_scatter(grad_wqkv, ("seq", "clip"), scatter_dimension=0, tiled=True).astype(jnp.float32).reshape(-1),
+        lax.psum_scatter(grad_wout, ("seq", "clip"), scatter_dimension=0, tiled=True).astype(jnp.float32).reshape(-1),
     )
     count_all = shards * lax.axis_size("clip") * TOK_DEV
     return (loss_total / count_all, grad_qkv, grad_out, grad_gain)

time: 471 us -> 442 us (0.938)
  waiting for transfers between devices: 164 us -> 145 us
  local copies, waits for them, and re-layouts: 80.6 us -> 70.1 us
    unnamed x2, waiting for transfers between devices: 135 us -> 0.03 us
    reduce_scatter x0 -> x2, waiting for transfers between devices: none -> 105 us  [the longest x1 105 us: per_device(): lax.psum_scatter(grad_wqkv, ('seq', 'clip'), scatter_dimension=0, tiled=T...]
    ppermute x15, waiting for transfers between devices: 25.5 us -> 32.6 us  [shifted(): return lax.ppermute(value, axis, pairs)]
    reshape x1, local copies, waits for them, and re-layouts: 6.93 us -> 1.62 us  [per_device(): lax.psum_scatter(grad_wqkv, ('seq', 'clip'), scatter_dimension=0, tiled=T...]
    unnamed x68 -> x82, local copies, waits for them, and re-layouts: 12.5 us -> 11.7 us
  transfers between devices with their start and end apart: 18 -> 19, of which waited for: 10 -> 11; matrix products, arithmetic and copies ran while one was open for 24% -> 27% of each run, Pallas kernels for 0% -> 0%
where the time goes in v1:
time: 442 us; the launch traced here: 439 us
  waiting for transfers between devices  145 us (33%)
  matrix products  77.3 us (17%)
  local copies, waits for them, and re-layouts  70.1 us (16%)
  other arithmetic  57.2 us (13%)
  blocking collectives  49.9 us (11%)
  between operations  16.4 us (4%)
  starting transfers between devices  13.3 us (3%)
  loops' own time  9.97 us (2%)
    reduce_scatter x1, waiting for transfers between devices, per_device(): lax.psum_scatter(grad_wqkv, ('seq', 'clip'), scatter_dimension=0, tiled=T...  105 us
    psum x1, blocking collectives, per_device(): loss_total, grad_gain = lax.psum((loss_part, grad_ln), ('seq', 'clip'))  40.5 us
    ppermute x15, waiting for transfers between devices, shifted(): return lax.ppermute(value, axis, pairs)  32.6 us
    dot_general x15, matrix products, head_scores(): jnp.einsum('qhd,khd->hqk', queries, split_kv[:, :, 0], preferred_element_...  19.2 us
    dot_general x8, matrix products, absorb(): jnp.einsum('hqk,khd->hqd', weights.astype(jnp.bfloat16), split_kv[:, :, 1...  15 us
    dot_general x8, matrix products, contribution(): jnp.einsum('hqk,khd->qhd', d_score, split_kv[:, :, 0], preferred_element_...  14.6 us
    dynamic_slice x14, local copies, waits for them, and re-layouts, per_device(): lax.scan(forward_step, (pair_rows, state), steps_ids)  12.8 us
    add x7, other arithmetic, backward_step(): return ((query_sum + part_query, travel_grads + part_pairs), None)  12.4 us
  transfers between devices with their start and end apart: 19, of which 11 were waited for; matrix products, arithmetic and copies ran while one was open for 27% of the time, Pallas kernels for 0%

profile of v1, /device:TPU:0, one launch (start us, length us, event | category | flops | bytes accessed | tf_op | source)
XLA Modules:
  0.0 438.9 jit_solution(11118792729399718866)
XLA Ops:
  12.1 9.5 %all-reduce = s32[8]{0:T(128)S(1)} all-reduce(s32[8]{0:T(128)S(1)} %dynamic-update-slice), channel_id=1, replica_groups=mesh['seq'=8,'clip'=4] {'seq'}, use_global_device_ids=true, to_apply=%add | all-reduce | flops 8 | bytes 64
  25.0 3.4 gather_fusion.2
  28.4 3.4 gather_fusion
  31.8 2.0 broadcast_select_fusion
  33.8 3.1 gather_fusion.3
  38.6 2.1 broadcast_select_fusion.2
  40.8 3.5 all-to-all-start
  48.8 3.7 all-to-all-done
  52.5 4.1 all-to-all-start.1
  61.2 3.8 all-to-all-done.1
  75.8 81.1 %while.36 = (s32[]{:T(128)}, bf16[128,1024]{0,1:T(8,128)(2,1)}, f32[8,128]{1,0:T(8,128)S(1)}, f32[8,128]{1,0:T(8,128)S(1)}, f32[8,128,64]{1,2,0:T(8,128)}, /*ind...) while((s32[]{:T(128)}, bf16[128,1024]{0,1:T(8,128)(2,1)}, ...), condition=%wide.region_13.14_spmd.clone, body=%wide.region_9.13_spmd.clone.sunk | while | flops 34605352 | bytes 4655954 | solution.py:174
  78.5 4.2 collective-permute-done
  90.0 4.2 collective-permute-done
  101.6 4.2 collective-permute-done
  113.2 4.2 collective-permute-done
  124.8 4.2 collective-permute-done
  136.4 4.2 collective-permute-done
  148.0 4.2 collective-permute-done
  172.1 94.0 %while.37 = (s32[]{:T(128)}, f32[128,8,64]{0,2,1:T(8,128)}, bf16[128,1024]{0,1:T(8,128)(2,1)}, bf16[7,128,1024]{1,2,0:T(8,128)(2,1)}, s32[7]{0:T(128)}, /*index=...) while((s32[]{:T(128)}, f32[128,8,64]{0,2,1:T(8,128)}, ...), condition=%wide.region_24.25_spmd.clone, body=%wide.region_22.24_spmd.clone.sunk | while | flops 85524776 | bytes 10103662 | solution.py:209
  181.6 2.0 fusion.108
  194.7 2.0 fusion.108
  207.8 2.0 fusion.108
  211.5 2.2 collective-permute-start.1
  236.2 2.0 fusion.108
  249.3 2.0 fusion.108
  262.3 2.0 fusion.108
  266.1 3.2 collective-permute-start.2
  270.2 3.0 collective-permute-done.2
  273.9 4.7 %fusion.40 = f32[1024,1536]{1,0:T(8,128)} fusion(bf16[128,1024]{0,1:T(8,128)(2,1)S(1)} %collective-permute-done.2, bf16[128,512]{0,1:T(8,128)(2,1)S(1)} %bitcast.191, bf16[128,1024]{1,0:T(8,128)(2,1)} %copy-done.4, f32[1024]{0:T(1024)S(1)} %copy-done.17, f32[128]{0:T(128)} %copy-done.20, f32[128]{0:T(128)S(1)} %copy-done.19), kind=kOutput, calls=%fused_computation.93 | convolution fusion | flops 404094976 | bytes 6951936 | tf_op jit(solution)/shard_map/dot_general | solution.py:214
  279.9 2.1 fusion.23
  282.0 40.5 %all-reduce.1 = (f32[]{:T(128)}, f32[1024]{0:T(1024)}) all-reduce(f32[]{:T(128)} %select_reduce_fusion, f32[1024]{0:T(1024)S(1)} %fusion.23), channel_id=1, replica_groups=mesh['seq'=8,'clip'=4] {'seq','clip'}, use_global_device_ids=true, to_apply=%region_19.20 | all-reduce | flops 1025 | bytes 8200 | tf_op jit(solution)/shard_map/psum | solution.py:218
  324.6 104.7 %reduce-scatter.3.cloned.1.call-done = f32[32,1536]{1,0:T(8,128)} async-done(((f32[1024,1536]{1,0:T(8,128)}), f32[32,1536]{1,0:T(8,128)}) %reduce-scatter.3.cloned.1.call-update) | async-done | bytes 196624 | tf_op jit(solution)/shard_map/reduce_scatter | solution.py:220
  (363 shorter events, 172.5 us)
Async XLA Ops:
  7.2 52.6 %copy-start = (bf16[1024,1536]{1,0:T(8,128)(2,1)S(1)}, bf16[1024,1536]{1,0:T(8,128)(2,1)}, u32[]{:S(2)}) copy-start(bf16[1024,1536]{1,0:T(8,128)(2,1)} %param.13) | copy-start | bytes 9437188
  8.0 14.8 %copy-start.35 = (pred[192]{0:T(512)(128)(4,1)}, pred[192]{0:T(512)(128)(4,1)S(1)}, u32[]{:S(2)}) copy-start(pred[192]{0:T(512)(128)(4,1)S(1)} %compare_reduce_fusion) | copy-start | bytes 580
  38.6 21.2 %copy-start.17 = (f32[1024]{0:T(1024)S(1)}, f32[1024]{0:T(1024)}, u32[]{:S(2)}) copy-start(f32[1024]{0:T(1024)} %param.15) | copy-start | bytes 12292
  40.8 11.7 %all-to-all-start = ((bf16[8,24,1024]{2,1,0:T(8,128)(2,1)}), bf16[8,24,1024]{2,1,0:T(8,128)(2,1)S(1)}, u32[]{:S(2)}, u32[]{:S(2)}) async-start(bf16[8,24,1024]{2,1,0:T(8,128)(2,1)} %get-tuple-element.399), calls=%async_computation | async-start | bytes 786432 | tf_op jit(solution)/shard_map/all_to_all | solution.py:128
  52.5 12.5 %all-to-all-start.1 = ((bf16[8,24,1024]{2,1,0:T(8,128)(2,1)}), bf16[8,24,1024]{2,1,0:T(8,128)(2,1)}, u32[]{:S(2)}, u32[]{:S(2)}) async-start(bf16[8,24,1024]{2,1,0:T(8,128)(2,1)} %get-tuple-element.398), calls=%async_computation.1 | async-start | bytes 786432 | tf_op jit(solution)/shard_map/all_to_all | solution.py:129
  56.6 266.5 %reduce-scatter.5.cloned.1.call-start = ((), (), s32[]{:S(2)}) async-start(), calls=%async_computation.5 | async-start | bytes 2162688 | tf_op jit(solution)/shard_map/reduce_scatter | solution.py:221
  60.5 11.4 %copy-start.38 = (pred[2,128]{1,0:T(4,128)(4,1)S(1)}, pred[2,128]{1,0:T(4,128)(4,1)}, u32[]{:S(2)}) copy-start(pred[2,128]{1,0:T(4,128)(4,1)} %iota_compare_fusion.2) | copy-start | bytes 772
  61.2 14.6 %copy-start.37 = (s32[7]{0:T(128)S(1)}, s32[7]{0:T(128)}, u32[]{:S(2)}) copy-start(s32[7]{0:T(128)} %iota_add_fusion) | copy-start | bytes 88
  66.9 8.9 %copy-start.8 = (bf16[128,1024]{1,0:T(8,128)(2,1)}, bf16[128,1024]{1,0:T(8,128)(2,1)S(1)}, u32[]{:S(2)}) copy-start(bf16[128,1024]{1,0:T(8,128)(2,1)S(1)} %scatter_custom_fusion.1) | copy-start | bytes 786436
  75.8 6.9 %collective-permute-start = (bf16[128,1024]{0,1:T(8,128)(2,1)}, bf16[128,1024]{0,1:T(8,128)(2,1)S(1)}, u32[]{:S(2)}, u32[]{:S(2)}) collective-permute-start(bf16[128,1024]{0,1:T(8,128)(2,1)} %get-tuple-element.550), channel_id=1, source_target_pairs={{0,4},{4,8},{8,12},{12,16},{16,20},{20,24},{24,28},{28,0},{1,5},{5... | collective-permute-start | bytes 786440 | tf_op jit(solution)/shard_map/while/body/eval_jaxpr/ppermute | solution.py:13
  87.4 6.9 %collective-permute-start = (bf16[128,1024]{0,1:T(8,128)(2,1)}, bf16[128,1024]{0,1:T(8,128)(2,1)S(1)}, u32[]{:S(2)}, u32[]{:S(2)}) collective-permute-start(bf16[128,1024]{0,1:T(8,128)(2,1)} %get-tuple-element.550), channel_id=1, source_target_pairs={{0,4},{4,8},{8,12},{12,16},{16,20},{20,24},{24,28},{28,0},{1,5},{5... | collective-permute-start | bytes 786440 | tf_op jit(solution)/shard_map/while/body/eval_jaxpr/ppermute | solution.py:13
  98.9 6.9 %collective-permute-start = (bf16[128,1024]{0,1:T(8,128)(2,1)}, bf16[128,1024]{0,1:T(8,128)(2,1)S(1)}, u32[]{:S(2)}, u32[]{:S(2)}) collective-permute-start(bf16[128,1024]{0,1:T(8,128)(2,1)} %get-tuple-element.550), channel_id=1, source_target_pairs={{0,4},{4,8},{8,12},{12,16},{16,20},{20,24},{24,28},{28,0},{1,5},{5... | collective-permute-start | bytes 786440 | tf_op jit(solution)/shard_map/while/body/eval_jaxpr/ppermute | solution.py:13
  110.5 6.9 %collective-permute-start = (bf16[128,1024]{0,1:T(8,128)(2,1)}, bf16[128,1024]{0,1:T(8,128)(2,1)S(1)}, u32[]{:S(2)}, u32[]{:S(2)}) collective-permute-start(bf16[128,1024]{0,1:T(8,128)(2,1)} %get-tuple-element.550), channel_id=1, source_target_pairs={{0,4},{4,8},{8,12},{12,16},{16,20},{20,24},{24,28},{28,0},{1,5},{5... | collective-permute-start | bytes 786440 | tf_op jit(solution)/shard_map/while/body/eval_jaxpr/ppermute | solution.py:13
  122.1 6.9 %collective-permute-start = (bf16[128,1024]{0,1:T(8,128)(2,1)}, bf16[128,1024]{0,1:T(8,128)(2,1)S(1)}, u32[]{:S(2)}, u32[]{:S(2)}) collective-permute-start(bf16[128,1024]{0,1:T(8,128)(2,1)} %get-tuple-element.550), channel_id=1, source_target_pairs={{0,4},{4,8},{8,12},{12,16},{16,20},{20,24},{24,28},{28,0},{1,5},{5... | collective-permute-start | bytes 786440 | tf_op jit(solution)/shard_map/while/body/eval_jaxpr/ppermute | solution.py:13
  133.7 6.9 %collective-permute-start = (bf16[128,1024]{0,1:T(8,128)(2,1)}, bf16[128,1024]{0,1:T(8,128)(2,1)S(1)}, u32[]{:S(2)}, u32[]{:S(2)}) collective-permute-start(bf16[128,1024]{0,1:T(8,128)(2,1)} %get-tuple-element.550), channel_id=1, source_target_pairs={{0,4},{4,8},{8,12},{12,16},{16,20},{20,24},{24,28},{28,0},{1,5},{5... | collective-permute-start | bytes 786440 | tf_op jit(solution)/shard_map/while/body/eval_jaxpr/ppermute | solution.py:13
  145.3 6.9 %collective-permute-start = (bf16[128,1024]{0,1:T(8,128)(2,1)}, bf16[128,1024]{0,1:T(8,128)(2,1)S(1)}, u32[]{:S(2)}, u32[]{:S(2)}) collective-permute-start(bf16[128,1024]{0,1:T(8,128)(2,1)} %get-tuple-element.550), channel_id=1, source_target_pairs={{0,4},{4,8},{8,12},{12,16},{16,20},{20,24},{24,28},{28,0},{1,5},{5... | collective-permute-start | bytes 786440 | tf_op jit(solution)/shard_map/while/body/eval_jaxpr/ppermute | solution.py:13
  164.0 5.1 %copy-start.7 = (f32[128,1024]{1,0:T(8,128)S(1)}, f32[128,1024]{1,0:T(8,128)}, u32[]{:S(2)}) copy-start(f32[128,1024]{1,0:T(8,128)} %copy-done.6) | copy-start | bytes 1572868
  164.0 5.1 %copy-start.10 = (bf16[128,1024]{1,0:T(8,128)(2,1)S(1)}, bf16[128,1024]{1,0:T(8,128)(2,1)}, u32[]{:S(2)}) copy-start(bf16[128,1024]{1,0:T(8,128)(2,1)} %copy-done.8) | copy-start | bytes 786436
  164.0 5.1 %copy-start.13 = (bf16[8,128,64]{1,2,0:T(8,128)(2,1)S(1)}, bf16[8,128,64]{1,2,0:T(8,128)(2,1)}, u32[]{:S(2)}) copy-start(bf16[8,128,64]{1,2,0:T(8,128)(2,1)} %copy-done.12) | copy-start | bytes 393220
  164.0 5.1 %copy-start.23 = (f32[128]{0:T(128)S(1)}, f32[128]{0:T(128)}, u32[]{:S(2)}) copy-start(f32[128]{0:T(128)} %copy-done.22) | copy-start | bytes 1540
  164.0 5.1 %copy-start.25 = (f32[128]{0:T(128)S(1)}, f32[128]{0:T(128)}, u32[]{:S(2)}) copy-start(f32[128]{0:T(128)} %add_rsqrt_fusion) | copy-start | bytes 1540
  164.0 5.1 %copy-start.27 = (f32[128]{0:T(128)S(1)}, f32[128]{0:T(128)}, u32[]{:S(2)}) copy-start(f32[128]{0:T(128)} %copy-done.26) | copy-start | bytes 1540
  171.9 257.4 %reduce-scatter.3.cloned.1.call-start = ((), (), s32[]{:S(2)}) async-start(), calls=%async_computation.4 | async-start | bytes 6488064 | tf_op jit(solution)/shard_map/reduce_scatter | solution.py:220
  172.1 101.8 %copy-start.19 = (f32[128]{0:T(128)S(1)}, f32[128]{0:T(128)}, u32[]{:S(2)}) copy-start(f32[128]{0:T(128)} %copy-done.18) | copy-start | bytes 1540
  172.1 11.4 %collective-permute-start.1 = (bf16[128,1024]{0,1:T(8,128)(2,1)}, bf16[128,1024]{0,1:T(8,128)(2,1)}, u32[]{:S(2)}, u32[]{:S(2)}) collective-permute-start(bf16[128,1024]{0,1:T(8,128)(2,1)} %get-tuple-element.591), channel_id=1, source_target_pairs={{0,4},{4,8},{8,12},{12,16},{16,20},{20,24},{24,28},{28,0},{1,5},{5... | collective-permute-start | bytes 786440 | tf_op jit(solution)/shard_map/while/body/eval_jaxpr/ppermute | solution.py:13
  185.3 11.3 %collective-permute-start.1 = (bf16[128,1024]{0,1:T(8,128)(2,1)}, bf16[128,1024]{0,1:T(8,128)(2,1)}, u32[]{:S(2)}, u32[]{:S(2)}) collective-permute-start(bf16[128,1024]{0,1:T(8,128)(2,1)} %get-tuple-element.591), channel_id=1, source_target_pairs={{0,4},{4,8},{8,12},{12,16},{16,20},{20,24},{24,28},{28,0},{1,5},{5... | collective-permute-start | bytes 786440 | tf_op jit(solution)/shard_map/while/body/eval_jaxpr/ppermute | solution.py:13
  198.4 11.3 %collective-permute-start.1 = (bf16[128,1024]{0,1:T(8,128)(2,1)}, bf16[128,1024]{0,1:T(8,128)(2,1)}, u32[]{:S(2)}, u32[]{:S(2)}) collective-permute-start(bf16[128,1024]{0,1:T(8,128)(2,1)} %get-tuple-element.591), channel_id=1, source_target_pairs={{0,4},{4,8},{8,12},{12,16},{16,20},{20,24},{24,28},{28,0},{1,5},{5... | collective-permute-start | bytes 786440 | tf_op jit(solution)/shard_map/while/body/eval_jaxpr/ppermute | solution.py:13
  211.5 13.5 %collective-permute-start.1 = (bf16[128,1024]{0,1:T(8,128)(2,1)}, bf16[128,1024]{0,1:T(8,128)(2,1)}, u32[]{:S(2)}, u32[]{:S(2)}) collective-permute-start(bf16[128,1024]{0,1:T(8,128)(2,1)} %get-tuple-element.591), channel_id=1, source_target_pairs={{0,4},{4,8},{8,12},{12,16},{16,20},{20,24},{24,28},{28,0},{1,5},{5... | collective-permute-start | bytes 786440 | tf_op jit(solution)/shard_map/while/body/eval_jaxpr/ppermute | solution.py:13
  226.8 11.3 %collective-permute-start.1 = (bf16[128,1024]{0,1:T(8,128)(2,1)}, bf16[128,1024]{0,1:T(8,128)(2,1)}, u32[]{:S(2)}, u32[]{:S(2)}) collective-permute-start(bf16[128,1024]{0,1:T(8,128)(2,1)} %get-tuple-element.591), channel_id=1, source_target_pairs={{0,4},{4,8},{8,12},{12,16},{16,20},{20,24},{24,28},{28,0},{1,5},{5... | collective-permute-start | bytes 786440 | tf_op jit(solution)/shard_map/while/body/eval_jaxpr/ppermute | solution.py:13
  239.9 11.3 %collective-permute-start.1 = (bf16[128,1024]{0,1:T(8,128)(2,1)}, bf16[128,1024]{0,1:T(8,128)(2,1)}, u32[]{:S(2)}, u32[]{:S(2)}) collective-permute-start(bf16[128,1024]{0,1:T(8,128)(2,1)} %get-tuple-element.591), channel_id=1, source_target_pairs={{0,4},{4,8},{8,12},{12,16},{16,20},{20,24},{24,28},{28,0},{1,5},{5... | collective-permute-start | bytes 786440 | tf_op jit(solution)/shard_map/while/body/eval_jaxpr/ppermute | solution.py:13
  253.0 11.3 %collective-permute-start.1 = (bf16[128,1024]{0,1:T(8,128)(2,1)}, bf16[128,1024]{0,1:T(8,128)(2,1)}, u32[]{:S(2)}, u32[]{:S(2)}) collective-permute-start(bf16[128,1024]{0,1:T(8,128)(2,1)} %get-tuple-element.591), channel_id=1, source_target_pairs={{0,4},{4,8},{8,12},{12,16},{16,20},{20,24},{24,28},{28,0},{1,5},{5... | collective-permute-start | bytes 786440 | tf_op jit(solution)/shard_map/while/body/eval_jaxpr/ppermute | solution.py:13
  266.1 7.1 %collective-permute-start.2 = (bf16[128,1024]{0,1:T(8,128)(2,1)}, bf16[128,1024]{0,1:T(8,128)(2,1)S(1)}, u32[]{:S(2)}, u32[]{:S(2)}) collective-permute-start(bf16[128,1024]{0,1:T(8,128)(2,1)} %get-tuple-element.277), channel_id=1, source_target_pairs={{0,4},{4,8},{8,12},{12,16},{16,20},{20,24},{24,28},{28,0},{1,5},{5... | collective-permute-start | bytes 786440 | tf_op jit(solution)/shard_map/ppermute | solution.py:13
  (32 other events, 73.5 us)
Sparse Core Ops, SparseCore 0:
  172.0 138.1 reduce-scatter.4
  316.7 112.5 reduce-scatter.2

commit v2 on v1

--- a/solution.py
+++ b/solution.py
@@ -217,8 +217,8 @@
     loss_part = jnp.sum(token_loss)
     loss_total, grad_gain = lax.psum((loss_part, grad_ln), ("seq", "clip"))
     grad_qkv, grad_out = (
-        lax.psum_scatter(grad_wqkv, ("seq", "clip"), scatter_dimension=0, tiled=True).astype(jnp.float32).reshape(-1),
-        lax.psum_scatter(grad_wout, ("seq", "clip"), scatter_dimension=0, tiled=True).astype(jnp.float32).reshape(-1),
+        lax.psum_scatter(grad_wqkv.astype(jnp.bfloat16), ("seq", "clip"), scatter_dimension=0, tiled=True).astype(jnp.float32).reshape(-1),
+        lax.psum_scatter(grad_wout.astype(jnp.bfloat16), ("seq", "clip"), scatter_dimension=0, tiled=True).astype(jnp.float32).reshape(-1),
     )
     count_all = shards * lax.axis_size("clip") * TOK_DEV
     return (loss_total / count_all, grad_qkv, grad_out, grad_gain)

time: 442 us -> 427 us (0.966)
  waiting for transfers between devices: 145 us -> 124 us
    reduce_scatter x2, waiting for transfers between devices: 105 us -> 88.9 us  [the longest x1 88.9 us: per_device(): lax.psum_scatter(grad_wqkv.astype(jnp.bfloat16), ('seq', 'clip'), scatter...]
    ppermute x15, waiting for transfers between devices: 32.6 us -> 27.7 us  [shifted(): return lax.ppermute(value, axis, pairs)]
    dynamic_slice x14, local copies, waits for them, and re-layouts: 12.8 us -> 17.5 us  [per_device(): lax.scan(forward_step, (pair_rows, state), steps_ids)]
    unnamed x82 -> x50, local copies, waits for them, and re-layouts: 11.7 us -> 9.84 us
  transfers between devices with their start and end apart: 19 -> 19, of which waited for: 11 -> 11; matrix products, arithmetic and copies ran while one was open for 27% -> 29% of each run, Pallas kernels for 0% -> 0%
where the time goes in v2:
time: 427 us; the launch traced here: 424 us
  waiting for transfers between devices  124 us (29%)
  matrix products  76.7 us (18%)
  local copies, waits for them, and re-layouts  73.8 us (17%)
  other arithmetic  60.1 us (14%)
  blocking collectives  50 us (12%)
  between operations  16.2 us (4%)
  starting transfers between devices  13.3 us (3%)
  loops' own time  9.97 us (2%)
    reduce_scatter x1, waiting for transfers between devices, per_device(): lax.psum_scatter(grad_wqkv.astype(jnp.bfloat16), ('seq', 'clip'), scatter...  88.9 us
    psum x1, blocking collectives, per_device(): loss_total, grad_gain = lax.psum((loss_part, grad_ln), ('seq', 'clip'))  40.6 us
    ppermute x15, waiting for transfers between devices, shifted(): return lax.ppermute(value, axis, pairs)  27.7 us
    dot_general x15, matrix products, head_scores(): jnp.einsum('qhd,khd->hqk', queries, split_kv[:, :, 0], preferred_element_...  19.2 us
    dynamic_slice x14, local copies, waits for them, and re-layouts, per_device(): lax.scan(forward_step, (pair_rows, state), steps_ids)  17.5 us
    dot_general x8, matrix products, contribution(): jnp.einsum('hqk,khd->qhd', d_score, split_kv[:, :, 0], preferred_element_...  15.4 us
    dot_general x8, matrix products, absorb(): jnp.einsum('hqk,khd->hqd', weights.astype(jnp.bfloat16), split_kv[:, :, 1...  15.1 us
    add x7, other arithmetic, backward_step(): return ((query_sum + part_query, travel_grads + part_pairs), None)  12.2 us
  transfers between devices with their start and end apart: 19, of which 11 were waited for; matrix products, arithmetic and copies ran while one was open for 29% of the time, Pallas kernels for 0%

profile of v2, /device:TPU:0, one launch (start us, length us, event | category | flops | bytes accessed | tf_op | source)
XLA Modules:
  0.0 424.0 jit_solution(6162317109594614015)
XLA Ops:
  12.1 9.5 %all-reduce = s32[8]{0:T(128)S(1)} all-reduce(s32[8]{0:T(128)S(1)} %dynamic-update-slice), channel_id=1, replica_groups=mesh['seq'=8,'clip'=4] {'seq'}, use_global_device_ids=true, to_apply=%add | all-reduce | flops 8 | bytes 64
  25.0 3.4 gather_fusion.2
  28.4 3.4 gather_fusion
  31.8 2.0 broadcast_select_fusion
  33.8 3.1 gather_fusion.3
  38.6 2.1 broadcast_select_fusion.2
  40.8 3.5 all-to-all-start
  48.9 3.6 all-to-all-done
  52.5 4.1 all-to-all-start.1
  61.3 3.7 all-to-all-done.1
  64.9 2.5 scatter_custom_fusion.1
  77.3 81.3 %while.36 = (s32[]{:T(128)}, bf16[128,1024]{0,1:T(8,128)(2,1)}, f32[8,128]{1,0:T(8,128)S(1)}, f32[8,128]{1,0:T(8,128)S(1)}, f32[8,128,64]{1,2,0:T(8,128)}, /*ind...) while((s32[]{:T(128)}, bf16[128,1024]{0,1:T(8,128)(2,1)}, ...), condition=%wide.region_13.14_spmd.clone, body=%wide.region_9.13_spmd.clone.sunk | while | flops 34605352 | bytes 4655954 | solution.py:174
  80.6 3.6 collective-permute-done
  92.2 3.6 collective-permute-done
  103.8 3.6 collective-permute-done
  115.4 3.6 collective-permute-done
  127.1 3.6 collective-permute-done
  138.7 3.6 collective-permute-done
  150.3 3.6 collective-permute-done
  174.8 93.8 %while.37 = (s32[]{:T(128)}, f32[128,8,64]{0,2,1:T(8,128)}, bf16[128,1024]{0,1:T(8,128)(2,1)}, bf16[7,128,1024]{1,2,0:T(8,128)(2,1)}, s32[7]{0:T(128)}, /*index=...) while((s32[]{:T(128)}, f32[128,8,64]{0,2,1:T(8,128)}, ...), condition=%wide.region_24.25_spmd.clone, body=%wide.region_22.24_spmd.clone.sunk | while | flops 85524776 | bytes 10103662 | solution.py:209
  197.3 1.9 fusion.108
  210.4 1.9 fusion.108
  214.1 2.2 collective-permute-start.1
  225.6 1.9 fusion.108
  238.7 1.9 fusion.108
  251.8 1.9 fusion.108
  268.5 3.2 collective-permute-start.2
  272.7 2.8 collective-permute-done.2
  276.2 3.8 convolution_convert_fusion
  280.6 2.1 fusion.23
  282.8 40.6 %all-reduce.1 = (f32[]{:T(128)}, f32[1024]{0:T(1024)}) all-reduce(f32[]{:T(128)} %select_reduce_fusion, f32[1024]{0:T(1024)S(1)} %fusion.23), channel_id=1, replica_groups=mesh['seq'=8,'clip'=4] {'seq','clip'}, use_global_device_ids=true, to_apply=%region_19.20 | all-reduce | flops 1025 | bytes 8200 | tf_op jit(solution)/shard_map/psum | solution.py:218
  325.4 88.9 %reduce-scatter.3.cloned.1.call-done = bf16[32,1536]{1,0:T(8,128)(2,1)} async-done(((bf16[1024,1536]{1,0:T(8,128)(2,1)}), bf16[32,1536]{1,0:T(8,128)(2,1)}) %reduce-scatter.3.cloned.1.call-update) | async-done | bytes 98320 | tf_op jit(solution)/shard_map/reduce_scatter | solution.py:220
  (333 shorter events, 179.0 us)
Async XLA Ops:
  7.2 52.7 %copy-start = (bf16[1024,1536]{1,0:T(8,128)(2,1)S(1)}, bf16[1024,1536]{1,0:T(8,128)(2,1)}, u32[]{:S(2)}) copy-start(bf16[1024,1536]{1,0:T(8,128)(2,1)} %param.13) | copy-start | bytes 9437188
  36.9 23.0 %copy-start.14 = (f32[1024]{0:T(1024)S(1)}, f32[1024]{0:T(1024)}, u32[]{:S(2)}) copy-start(f32[1024]{0:T(1024)} %param.15) | copy-start | bytes 12292
  40.8 11.7 %all-to-all-start = ((bf16[8,24,1024]{2,1,0:T(8,128)(2,1)}), bf16[8,24,1024]{2,1,0:T(8,128)(2,1)S(1)}, u32[]{:S(2)}, u32[]{:S(2)}) async-start(bf16[8,24,1024]{2,1,0:T(8,128)(2,1)} %get-tuple-element.399), calls=%async_computation | async-start | bytes 786432 | tf_op jit(solution)/shard_map/all_to_all | solution.py:128
  52.5 12.5 %all-to-all-start.1 = ((bf16[8,24,1024]{2,1,0:T(8,128)(2,1)}), bf16[8,24,1024]{2,1,0:T(8,128)(2,1)}, u32[]{:S(2)}, u32[]{:S(2)}) async-start(bf16[8,24,1024]{2,1,0:T(8,128)(2,1)} %get-tuple-element.398), calls=%async_computation.1 | async-start | bytes 786432 | tf_op jit(solution)/shard_map/all_to_all | solution.py:129
  56.6 267.4 %reduce-scatter.5.cloned.1.call-start = ((), (), s32[]{:S(2)}) async-start(), calls=%async_computation.5 | async-start | bytes 1081344 | tf_op jit(solution)/shard_map/reduce_scatter | solution.py:221
  58.6 13.0 %copy-start.4 = (bf16[128,1024]{1,0:T(8,128)(2,1)}, bf16[128,1024]{1,0:T(8,128)(2,1)S(1)}, u32[]{:S(2)}) copy-start(bf16[128,1024]{1,0:T(8,128)(2,1)S(1)} %scatter_custom_fusion) | copy-start | bytes 786436
  59.9 13.4 %copy-start.22 = (pred[2,128]{1,0:T(4,128)(4,1)S(1)}, pred[2,128]{1,0:T(4,128)(4,1)}, u32[]{:S(2)}) copy-start(pred[2,128]{1,0:T(4,128)(4,1)} %iota_compare_fusion.2) | copy-start | bytes 772
  77.3 6.9 %collective-permute-start = (bf16[128,1024]{0,1:T(8,128)(2,1)}, bf16[128,1024]{0,1:T(8,128)(2,1)S(1)}, u32[]{:S(2)}, u32[]{:S(2)}) collective-permute-start(bf16[128,1024]{0,1:T(8,128)(2,1)} %get-tuple-element.550), channel_id=1, source_target_pairs={{0,4},{4,8},{8,12},{12,16},{16,20},{20,24},{24,28},{28,0},{1,5},{5... | collective-permute-start | bytes 786440 | tf_op jit(solution)/shard_map/while/body/eval_jaxpr/ppermute | solution.py:13
  88.9 6.9 %collective-permute-start = (bf16[128,1024]{0,1:T(8,128)(2,1)}, bf16[128,1024]{0,1:T(8,128)(2,1)S(1)}, u32[]{:S(2)}, u32[]{:S(2)}) collective-permute-start(bf16[128,1024]{0,1:T(8,128)(2,1)} %get-tuple-element.550), channel_id=1, source_target_pairs={{0,4},{4,8},{8,12},{12,16},{16,20},{20,24},{24,28},{28,0},{1,5},{5... | collective-permute-start | bytes 786440 | tf_op jit(solution)/shard_map/while/body/eval_jaxpr/ppermute | solution.py:13
  100.5 6.9 %collective-permute-start = (bf16[128,1024]{0,1:T(8,128)(2,1)}, bf16[128,1024]{0,1:T(8,128)(2,1)S(1)}, u32[]{:S(2)}, u32[]{:S(2)}) collective-permute-start(bf16[128,1024]{0,1:T(8,128)(2,1)} %get-tuple-element.550), channel_id=1, source_target_pairs={{0,4},{4,8},{8,12},{12,16},{16,20},{20,24},{24,28},{28,0},{1,5},{5... | collective-permute-start | bytes 786440 | tf_op jit(solution)/shard_map/while/body/eval_jaxpr/ppermute | solution.py:13
  112.1 6.9 %collective-permute-start = (bf16[128,1024]{0,1:T(8,128)(2,1)}, bf16[128,1024]{0,1:T(8,128)(2,1)S(1)}, u32[]{:S(2)}, u32[]{:S(2)}) collective-permute-start(bf16[128,1024]{0,1:T(8,128)(2,1)} %get-tuple-element.550), channel_id=1, source_target_pairs={{0,4},{4,8},{8,12},{12,16},{16,20},{20,24},{24,28},{28,0},{1,5},{5... | collective-permute-start | bytes 786440 | tf_op jit(solution)/shard_map/while/body/eval_jaxpr/ppermute | solution.py:13
  123.7 6.9 %collective-permute-start = (bf16[128,1024]{0,1:T(8,128)(2,1)}, bf16[128,1024]{0,1:T(8,128)(2,1)S(1)}, u32[]{:S(2)}, u32[]{:S(2)}) collective-permute-start(bf16[128,1024]{0,1:T(8,128)(2,1)} %get-tuple-element.550), channel_id=1, source_target_pairs={{0,4},{4,8},{8,12},{12,16},{16,20},{20,24},{24,28},{28,0},{1,5},{5... | collective-permute-start | bytes 786440 | tf_op jit(solution)/shard_map/while/body/eval_jaxpr/ppermute | solution.py:13
  135.3 6.9 %collective-permute-start = (bf16[128,1024]{0,1:T(8,128)(2,1)}, bf16[128,1024]{0,1:T(8,128)(2,1)S(1)}, u32[]{:S(2)}, u32[]{:S(2)}) collective-permute-start(bf16[128,1024]{0,1:T(8,128)(2,1)} %get-tuple-element.550), channel_id=1, source_target_pairs={{0,4},{4,8},{8,12},{12,16},{16,20},{20,24},{24,28},{28,0},{1,5},{5... | collective-permute-start | bytes 786440 | tf_op jit(solution)/shard_map/while/body/eval_jaxpr/ppermute | solution.py:13
  147.0 6.9 %collective-permute-start = (bf16[128,1024]{0,1:T(8,128)(2,1)}, bf16[128,1024]{0,1:T(8,128)(2,1)S(1)}, u32[]{:S(2)}, u32[]{:S(2)}) collective-permute-start(bf16[128,1024]{0,1:T(8,128)(2,1)} %get-tuple-element.550), channel_id=1, source_target_pairs={{0,4},{4,8},{8,12},{12,16},{16,20},{20,24},{24,28},{28,0},{1,5},{5... | collective-permute-start | bytes 786440 | tf_op jit(solution)/shard_map/while/body/eval_jaxpr/ppermute | solution.py:13
  158.6 4.7 %copy-start.6 = (bf16[128,1024]{1,0:T(8,128)(2,1)S(1)}, bf16[128,1024]{1,0:T(8,128)(2,1)}, u32[]{:S(2)}) copy-start(bf16[128,1024]{1,0:T(8,128)(2,1)} %scatter_custom_fusion.1) | copy-start | bytes 786436
  158.6 4.7 %copy-start.17 = (f32[128]{0:T(128)S(1)}, f32[128]{0:T(128)}, u32[]{:S(2)}) copy-start(f32[128]{0:T(128)} %add_rsqrt_fusion) | copy-start | bytes 1540
  158.6 4.7 %copy-start.20 = (pred[128]{0:T(512)(128)(4,1)S(1)}, pred[128]{0:T(512)(128)(4,1)}, u32[]{:S(2)}) copy-start(pred[128]{0:T(512)(128)(4,1)} %iota_compare_fusion.3) | copy-start | bytes 388
  158.6 5.7 %copy-start.7 = (bf16[512,1024]{1,0:T(8,128)(2,1)S(1)}, bf16[512,1024]{1,0:T(8,128)(2,1)}, u32[]{:S(2)}) copy-start(bf16[512,1024]{1,0:T(8,128)(2,1)} %param.14) | copy-start | bytes 3145732
  158.6 7.8 %copy-start.2 = (f32[8,128,64]{1,2,0:T(8,128)S(1)}, f32[8,128,64]{1,2,0:T(8,128)}, u32[]{:S(2)}) copy-start(f32[8,128,64]{1,2,0:T(8,128)} %get-tuple-element.272) | copy-start | bytes 786436
  166.4 5.9 %copy-start.9 = (bf16[128,1024]{1,0:T(8,128)(2,1)S(1)}, bf16[128,1024]{1,0:T(8,128)(2,1)}, u32[]{:S(2)}) copy-start(bf16[128,1024]{1,0:T(8,128)(2,1)} %copy-done.8) | copy-start | bytes 786436
  166.4 5.9 %copy-start.11 = (bf16[8,128,64]{1,2,0:T(8,128)(2,1)S(1)}, bf16[8,128,64]{1,2,0:T(8,128)(2,1)}, u32[]{:S(2)}) copy-start(bf16[8,128,64]{1,2,0:T(8,128)(2,1)} %copy-done.10) | copy-start | bytes 393220
  174.5 239.8 %reduce-scatter.3.cloned.1.call-start = ((), (), s32[]{:S(2)}) async-start(), calls=%async_computation.4 | async-start | bytes 3244032 | tf_op jit(solution)/shard_map/reduce_scatter | solution.py:220
  174.8 101.4 %copy-start.16 = (f32[128]{0:T(128)S(1)}, f32[128]{0:T(128)}, u32[]{:S(2)}) copy-start(f32[128]{0:T(128)} %copy-done.15) | copy-start | bytes 1540
  174.8 11.4 %collective-permute-start.1 = (bf16[128,1024]{0,1:T(8,128)(2,1)}, bf16[128,1024]{0,1:T(8,128)(2,1)}, u32[]{:S(2)}, u32[]{:S(2)}) collective-permute-start(bf16[128,1024]{0,1:T(8,128)(2,1)} %get-tuple-element.591), channel_id=1, source_target_pairs={{0,4},{4,8},{8,12},{12,16},{16,20},{20,24},{24,28},{28,0},{1,5},{5... | collective-permute-start | bytes 786440 | tf_op jit(solution)/shard_map/while/body/eval_jaxpr/ppermute | solution.py:13
  187.9 11.3 %collective-permute-start.1 = (bf16[128,1024]{0,1:T(8,128)(2,1)}, bf16[128,1024]{0,1:T(8,128)(2,1)}, u32[]{:S(2)}, u32[]{:S(2)}) collective-permute-start(bf16[128,1024]{0,1:T(8,128)(2,1)} %get-tuple-element.591), channel_id=1, source_target_pairs={{0,4},{4,8},{8,12},{12,16},{16,20},{20,24},{24,28},{28,0},{1,5},{5... | collective-permute-start | bytes 786440 | tf_op jit(solution)/shard_map/while/body/eval_jaxpr/ppermute | solution.py:13
  201.0 11.3 %collective-permute-start.1 = (bf16[128,1024]{0,1:T(8,128)(2,1)}, bf16[128,1024]{0,1:T(8,128)(2,1)}, u32[]{:S(2)}, u32[]{:S(2)}) collective-permute-start(bf16[128,1024]{0,1:T(8,128)(2,1)} %get-tuple-element.591), channel_id=1, source_target_pairs={{0,4},{4,8},{8,12},{12,16},{16,20},{20,24},{24,28},{28,0},{1,5},{5... | collective-permute-start | bytes 786440 | tf_op jit(solution)/shard_map/while/body/eval_jaxpr/ppermute | solution.py:13
  214.1 13.5 %collective-permute-start.1 = (bf16[128,1024]{0,1:T(8,128)(2,1)}, bf16[128,1024]{0,1:T(8,128)(2,1)}, u32[]{:S(2)}, u32[]{:S(2)}) collective-permute-start(bf16[128,1024]{0,1:T(8,128)(2,1)} %get-tuple-element.591), channel_id=1, source_target_pairs={{0,4},{4,8},{8,12},{12,16},{16,20},{20,24},{24,28},{28,0},{1,5},{5... | collective-permute-start | bytes 786440 | tf_op jit(solution)/shard_map/while/body/eval_jaxpr/ppermute | solution.py:13
  229.3 11.3 %collective-permute-start.1 = (bf16[128,1024]{0,1:T(8,128)(2,1)}, bf16[128,1024]{0,1:T(8,128)(2,1)}, u32[]{:S(2)}, u32[]{:S(2)}) collective-permute-start(bf16[128,1024]{0,1:T(8,128)(2,1)} %get-tuple-element.591), channel_id=1, source_target_pairs={{0,4},{4,8},{8,12},{12,16},{16,20},{20,24},{24,28},{28,0},{1,5},{5... | collective-permute-start | bytes 786440 | tf_op jit(solution)/shard_map/while/body/eval_jaxpr/ppermute | solution.py:13
  242.4 11.3 %collective-permute-start.1 = (bf16[128,1024]{0,1:T(8,128)(2,1)}, bf16[128,1024]{0,1:T(8,128)(2,1)}, u32[]{:S(2)}, u32[]{:S(2)}) collective-permute-start(bf16[128,1024]{0,1:T(8,128)(2,1)} %get-tuple-element.591), channel_id=1, source_target_pairs={{0,4},{4,8},{8,12},{12,16},{16,20},{20,24},{24,28},{28,0},{1,5},{5... | collective-permute-start | bytes 786440 | tf_op jit(solution)/shard_map/while/body/eval_jaxpr/ppermute | solution.py:13
  255.5 11.3 %collective-permute-start.1 = (bf16[128,1024]{0,1:T(8,128)(2,1)}, bf16[128,1024]{0,1:T(8,128)(2,1)}, u32[]{:S(2)}, u32[]{:S(2)}) collective-permute-start(bf16[128,1024]{0,1:T(8,128)(2,1)} %get-tuple-element.591), channel_id=1, source_target_pairs={{0,4},{4,8},{8,12},{12,16},{16,20},{20,24},{24,28},{28,0},{1,5},{5... | collective-permute-start | bytes 786440 | tf_op jit(solution)/shard_map/while/body/eval_jaxpr/ppermute | solution.py:13
  268.5 6.9 %collective-permute-start.2 = (bf16[128,1024]{0,1:T(8,128)(2,1)}, bf16[128,1024]{0,1:T(8,128)(2,1)S(1)}, u32[]{:S(2)}, u32[]{:S(2)}) collective-permute-start(bf16[128,1024]{0,1:T(8,128)(2,1)} %get-tuple-element.277), channel_id=1, source_target_pairs={{0,4},{4,8},{8,12},{12,16},{16,20},{20,24},{24,28},{28,0},{1,5},{5... | collective-permute-start | bytes 786440 | tf_op jit(solution)/shard_map/ppermute | solution.py:13
  276.2 4.5 %copy-start.19 = (f32[128]{0:T(128)S(1)}, f32[128]{0:T(128)}, u32[]{:S(2)}) copy-start(f32[128]{0:T(128)} %copy-done.18) | copy-start | bytes 1540
  (16 other events, 32.9 us)
Sparse Core Ops, SparseCore 0:
  174.7 135.4 reduce-scatter.4
  316.5 97.7 reduce-scatter.2

commit v3 on v2

--- a/solution.py
+++ b/solution.py
@@ -97,6 +97,44 @@
 def move_grads(accum):
     moved = shifted(accum.astype(jnp.bfloat16), "seq", 1).astype(accum.dtype)
     return moved
+
+
+def halving_scatter(parts):
+    seq_n = lax.axis_size("seq")
+    clip_n = lax.axis_size("clip")
+    seq_bits = seq_n.bit_length() - 1
+    clip_bits = clip_n.bit_length() - 1
+    assert (1 << seq_bits) == seq_n and (1 << clip_bits) == clip_n
+    blocks = seq_n * clip_n
+    sizes = [p.size // blocks for p in parts]
+    flat = jnp.concatenate([p.reshape(blocks, -1) for p in parts], axis=1)
+    data = flat.reshape([2] * (seq_bits + clip_bits) + [flat.shape[1]])
+    seq_me = lax.axis_index("seq")
+    clip_me = lax.axis_index("clip")
+    order = [("seq", bit) for bit in range(seq_bits)] + [("clip", bit) for bit in range(clip_bits)]
+    dims = {}
+    for bit in range(seq_bits):
+        dims[("seq", bit)] = seq_bits - 1 - bit
+    for bit in range(clip_bits):
+        dims[("clip", bit)] = seq_bits + clip_bits - 1 - bit
+    removed = []
+    for axis, bit in order:
+        dim = dims[(axis, bit)] - sum(1 for r in removed if r < dims[(axis, bit)])
+        me = seq_me if axis == "seq" else clip_me
+        mine = (me >> bit) & 1
+        keep = lax.dynamic_index_in_dim(data, mine, axis=dim, keepdims=False)
+        give = lax.dynamic_index_in_dim(data, 1 - mine, axis=dim, keepdims=False)
+        count = seq_n if axis == "seq" else clip_n
+        pairs = [(src, src ^ (1 << bit)) for src in range(count)]
+        got = lax.ppermute(give.astype(jnp.bfloat16), axis, pairs)
+        data = keep + got.astype(jnp.float32)
+        removed.append(dims[(axis, bit)])
+    out = []
+    start = 0
+    for size in sizes:
+        out.append(data[start:start + size])
+        start += size
+    return out
 
 
 def per_device(raw_tokens, teacher, keep_rows, w_qkv, w_out, ln_gain):
@@ -216,10 +254,7 @@
     grad_ln = jnp.sum(d_hidden * normed, axis=0)
     loss_part = jnp.sum(token_loss)
     loss_total, grad_gain = lax.psum((loss_part, grad_ln), ("seq", "clip"))
-    grad_qkv, grad_out = (
-        lax.psum_scatter(grad_wqkv.astype(jnp.bfloat16), ("seq", "clip"), scatter_dimension=0, tiled=True).astype(jnp.float32).reshape(-1),
-        lax.psum_scatter(grad_wout.astype(jnp.bfloat16), ("seq", "clip"), scatter_dimension=0, tiled=True).astype(jnp.float32).reshape(-1),
-    )
+    grad_qkv, grad_out = halving_scatter([grad_wqkv, grad_wout])
     count_all = shards * lax.axis_size("clip") * TOK_DEV
     return (loss_total / count_all, grad_qkv, grad_out, grad_gain)
 

time: 427 us -> 421 us (0.986)
  waiting for transfers between devices: 124 us -> 77.1 us
  local copies, waits for them, and re-layouts: 73.8 us -> 112 us
  between operations: 16.2 us -> 2.89 us
  other arithmetic: 60.1 us -> 69.3 us
  starting transfers between devices: 13.3 us -> 18.1 us
    reduce_scatter x2 -> x0, waiting for transfers between devices: 88.9 us -> none  [the longest x1 88.9 us: per_device(): lax.psum_scatter(grad_wqkv.astype(jnp.bfloat16), ('seq', 'clip'), scatter...]
    ppermute x0 -> x5, waiting for transfers between devices: none -> 47.9 us  [halving_scatter(): got = lax.ppermute(give.astype(jnp.bfloat16), axis, pairs)]
    concatenate x0 -> x3, local copies, waits for them, and re-layouts: none -> 16.8 us  [halving_scatter(): flat = jnp.concatenate([p.reshape(blocks, -1) for p in parts], axis=1)]
    unnamed x50 -> x64, local copies, waits for them, and re-layouts: 9.84 us -> 23.4 us
    add x0 -> x5, other arithmetic: none -> 11.6 us  [halving_scatter(): data = keep + got.astype(jnp.float32)]
    convert_element_type x0 -> x5, local copies, waits for them, and re-layouts: none -> 9.48 us  [halving_scatter(): got = lax.ppermute(give.astype(jnp.bfloat16), axis, pairs)]
    ppermute x0 -> x5, starting transfers between devices: none -> 4.79 us  [halving_scatter(): got = lax.ppermute(give.astype(jnp.bfloat16), axis, pairs)]
    reduce_sum x15 -> x14, other arithmetic: 9.47 us -> 8.84 us  [counts_at(): jnp.sum(jnp.where(shard_ids == (my_index - step) % shards, anchor_table, 0))]
  transfers between devices with their start and end apart: 19 -> 22, of which waited for: 11 -> 12; matrix products, arithmetic and copies ran while one was open for 29% -> 28% of each run, Pallas kernels for 0% -> 0%
where the time goes in v3:
time: 421 us; the launch traced here: 418 us
  local copies, waits for them, and re-layouts  112 us (27%)
  matrix products  79.1 us (19%)
  waiting for transfers between devices  77.1 us (18%)
  other arithmetic  69.3 us (16%)
  blocking collectives  49.6 us (12%)
  starting transfers between devices  18.1 us (4%)
  loops' own time  9.33 us (2%)
    ppermute x5, waiting for transfers between devices, halving_scatter(): got = lax.ppermute(give.astype(jnp.bfloat16), axis, pairs)  47.9 us
    psum x1, blocking collectives, per_device(): loss_total, grad_gain = lax.psum((loss_part, grad_ln), ('seq', 'clip'))  40.2 us
    ppermute x15, waiting for transfers between devices, shifted(): return lax.ppermute(value, axis, pairs)  25 us
    unnamed x64, local copies, waits for them, and re-layouts  23.4 us
    dot_general x15, matrix products, head_scores(): jnp.einsum('qhd,khd->hqk', queries, split_kv[:, :, 0], preferred_element_...  19.2 us
    concatenate x3, local copies, waits for them, and re-layouts, halving_scatter(): flat = jnp.concatenate([p.reshape(blocks, -1) for p in parts], axis=1)  16.8 us
    dynamic_slice x14, local copies, waits for them, and re-layouts, per_device(): lax.scan(forward_step, (pair_rows, state), steps_ids)  16.6 us
    dot_general x8, matrix products, contribution(): jnp.einsum('hqk,khd->qhd', d_score, split_kv[:, :, 0], preferred_element_...  15.4 us
  transfers between devices with their start and end apart: 22, of which 12 were waited for; matrix products, arithmetic and copies ran while one was open for 28% of the time, Pallas kernels for 0%

profile of v3, /device:TPU:0, one launch (start us, length us, event | category | flops | bytes accessed | tf_op | source)
XLA Modules:
  0.0 417.5 jit_solution(7985684225570983820)
XLA Ops:
  5.6 9.5 %all-reduce = s32[8]{0:T(128)S(1)} all-reduce(s32[8]{0:T(128)S(1)} %dynamic-update-slice), channel_id=1, replica_groups=mesh['seq'=8,'clip'=4] {'seq'}, use_global_device_ids=true, to_apply=%add | all-reduce | flops 8 | bytes 64
  19.0 3.4 gather_fusion.2
  22.4 3.4 gather_fusion
  27.9 3.1 gather_fusion.3
  32.8 2.1 broadcast_select_fusion.2
  34.9 3.5 all-to-all-start
  42.4 4.2 %all-to-all-done = bf16[8,24,1024]{2,1,0:T(8,128)(2,1)S(1)} async-done(((bf16[8,24,1024]{2,1,0:T(8,128)(2,1)}), bf16[8,24,1024]{2,1,0:T(8,128)(2,1)S(1)}, u32[]{:S(2)}, u32[]{:S(2)}) %all-to-all-start) | async-done | bytes 393248 | tf_op jit(solution)/shard_map/all_to_all | solution.py:166
  46.6 4.1 all-to-all-start.1
  64.9 81.0 %while.36 = (s32[]{:T(128)}, bf16[128,1024]{0,1:T(8,128)(2,1)}, f32[8,128]{1,0:T(8,128)S(1)}, f32[8,128]{1,0:T(8,128)S(1)}, f32[8,128,64]{1,2,0:T(8,128)}, /*ind...) while((s32[]{:T(128)}, bf16[128,1024]{0,1:T(8,128)(2,1)}, ...), condition=%wide.region_13.14_spmd.clone, body=%wide.region_9.13_spmd.clone.sunk | while | flops 34605352 | bytes 4655954 | solution.py:212
  68.5 3.3 collective-permute-done
  79.7 3.6 collective-permute-done
  91.3 3.6 collective-permute-done
  102.9 3.6 collective-permute-done
  114.4 3.6 collective-permute-done
  126.0 3.6 collective-permute-done
  137.6 3.6 collective-permute-done
  161.2 93.3 %while.37 = (s32[]{:T(128)}, f32[128,8,64]{0,2,1:T(8,128)}, bf16[128,1024]{0,1:T(8,128)(2,1)}, bf16[7,128,1024]{1,2,0:T(8,128)(2,1)}, s32[7]{0:T(128)}, /*index=...) while((s32[]{:T(128)}, f32[128,8,64]{0,2,1:T(8,128)}, ...), condition=%wide.region_24.25_spmd.clone, body=%wide.region_22.24_spmd.clone.sunk | while | flops 85524776 | bytes 10103662 | solution.py:247
  200.0 3.3 collective-permute-start.1
  257.4 3.1 fusion.58
  260.5 4.0 concatenate.14
  264.6 4.7 %fusion.44 = f32[1024,1536]{1,0:T(8,128)} fusion(bf16[128,1024]{0,1:T(8,128)(2,1)} %collective-permute-done.2, bf16[128,512]{0,1:T(8,128)(2,1)S(1)} %bitcast.205, bf16[128,1024]{1,0:T(8,128)(2,1)S(1)} %copy-done.6, f32[1024]{0:T(1024)S(1)} %copy-done.16, f32[128]{0:T(128)S(1)} %copy-done.20, f32[128]{0:T(128)S(1)} %copy-done.18), kind=kOutput, calls=%fused_computation.109 | convolution fusion | flops 404094976 | bytes 6951936 | tf_op jit(solution)/shard_map/dot_general | solution.py:252
  269.3 9.8 %concatenate.13 = f32[2,2,2,2,2,49152]{5,4,3,2,1,0:T(2,128)} reshape(f32[1024,1536]{1,0:T(8,128)} %fusion.44) | data formatting | bytes 12582912 | tf_op jit(solution)/shard_map/concatenate | solution.py:110
  279.1 11.2 %copy_dynamic-update-slice_fusion = f32[2,2,2,2,2,65536]{5,3,4,0,1,2:T(2,128)} fusion(f32[2,2,2,2,2,49152]{5,4,3,2,1,0:T(2,128)} %concatenate.13), kind=kLoop, calls=%fused_computation.47 | loop fusion | bytes 12582912
  290.3 3.0 copy_dynamic-update-slice_fusion.1
  293.2 4.9 %fusion.20 = bf16[2,2,2,2,65536]{4,2,3,0,1:T(2,128)(2,1)} fusion(f32[2,2,2,2,2,65536]{5,3,4,0,1,2:T(2,128)} %copy_dynamic-update-slice_fusion.1, s32[]{:T(128)S(6)} %select_n.201), kind=kLoop, calls=%fused_computation.51 | loop fusion | bytes 4194308 | tf_op jit(solution)/shard_map/convert_element_type | solution.py:129
  298.2 4.5 %collective-permute-done.3 = bf16[2,2,2,2,65536]{4,2,3,0,1:T(2,128)(2,1)} collective-permute-done((bf16[2,2,2,2,65536]{4,2,3,0,1:T(2,128)(2,1)}, bf16[2,2,2,2,65536]{4,2,3,0,1:T(2,128)(2,1)}, u32[]{:S(2)}, u32[]{:S(2)}) %collective-permute-start.3) | collective-permute-done | bytes 2097184 | tf_op jit(solution)/shard_map/ppermute | solution.py:129
  302.7 5.0 %bitcast_add_fusion.1 = f32[2,2,2,2,65536]{4,2,3,0,1:T(2,128)S(1)} fusion(bf16[2,2,2,2,65536]{4,2,3,0,1:T(2,128)(2,1)} %collective-permute-done.3, f32[2,2,2,2,2,65536]{5,3,4,0,1,2:T(2,128)} %copy_dynamic-update-slice_fusion.1, s32[]{:T(128)S(6)} %select_n.200), kind=kLoop, calls=%fused_computation.48 | loop fusion | flops 2097152 | bytes 10485764 | tf_op jit(solution)/shard_map/add | solution.py:130
  311.3 25.5 %collective-permute-done.4 = bf16[2,2,2,65536]{3,1,2,0:T(2,128)(2,1)} collective-permute-done((bf16[2,2,2,65536]{3,1,2,0:T(2,128)(2,1)}, bf16[2,2,2,65536]{3,1,2,0:T(2,128)(2,1)}, u32[]{:S(2)}, u32[]{:S(2)}) %collective-permute-start.4) | collective-permute-done | bytes 1048608 | tf_op jit(solution)/shard_map/ppermute | solution.py:129
  336.8 3.3 bitcast_add_fusion.2
  345.1 11.1 %collective-permute-done.5 = bf16[2,2,65536]{2,0,1:T(2,128)(2,1)} collective-permute-done((bf16[2,2,65536]{2,0,1:T(2,128)(2,1)}, bf16[2,2,65536]{2,0,1:T(2,128)(2,1)}, u32[]{:S(2)}, u32[]{:S(2)}) %collective-permute-start.5) | collective-permute-done | bytes 524320 | tf_op jit(solution)/shard_map/ppermute | solution.py:129
  363.8 40.2 %all-reduce.1 = (f32[]{:T(128)}, f32[1024]{0:T(1024)}) all-reduce(f32[]{:T(128)} %select_reduce_fusion, f32[1024]{0:T(1024)S(1)} %fusion.24), channel_id=1, replica_groups=mesh['seq'=8,'clip'=4] {'seq','clip'}, use_global_device_ids=true, to_apply=%region_19.20 | all-reduce | flops 1025 | bytes 8200 | tf_op jit(solution)/shard_map/psum | solution.py:256
  408.3 6.8 %collective-permute-done.7 = bf16[65536]{0:T(1024)(128)(2,1)S(1)} collective-permute-done((bf16[65536]{0:T(1024)(128)(2,1)S(1)}, bf16[65536]{0:T(1024)(128)(2,1)S(1)}, u32[]{:S(2)}, u32[]{:S(2)}) %collective-permute-start.7) | collective-permute-done | bytes 131104 | tf_op jit(solution)/shard_map/ppermute | solution.py:129
  (363 shorter events, 206.8 us)
Async XLA Ops:
  0.6 52.4 %copy-start = (bf16[1024,1536]{1,0:T(8,128)(2,1)S(1)}, bf16[1024,1536]{1,0:T(8,128)(2,1)}, u32[]{:S(2)}) copy-start(bf16[1024,1536]{1,0:T(8,128)(2,1)} %param.13) | copy-start | bytes 9437188
  31.0 22.1 %copy-start.16 = (f32[1024]{0:T(1024)S(1)}, f32[1024]{0:T(1024)}, u32[]{:S(2)}) copy-start(f32[1024]{0:T(1024)} %param.15) | copy-start | bytes 12292
  34.9 11.7 %all-to-all-start = ((bf16[8,24,1024]{2,1,0:T(8,128)(2,1)}), bf16[8,24,1024]{2,1,0:T(8,128)(2,1)S(1)}, u32[]{:S(2)}, u32[]{:S(2)}) async-start(bf16[8,24,1024]{2,1,0:T(8,128)(2,1)} %get-tuple-element.399), calls=%async_computation | async-start | bytes 786432 | tf_op jit(solution)/shard_map/all_to_all | solution.py:166
  42.4 13.9 %copy-start.26 = (s32[192,1]{0,1:T(1,128)}, s32[192,1]{0,1:T(1,128)S(1)}, u32[]{:S(2)}) copy-start(s32[192,1]{0,1:T(1,128)S(1)} %compare_select_fusion.3) | copy-start | bytes 2308
  46.6 15.4 %all-to-all-start.1 = ((bf16[8,24,1024]{2,1,0:T(8,128)(2,1)}), bf16[8,24,1024]{2,1,0:T(8,128)(2,1)}, u32[]{:S(2)}, u32[]{:S(2)}) async-start(bf16[8,24,1024]{2,1,0:T(8,128)(2,1)} %get-tuple-element.398), calls=%async_computation.1 | async-start | bytes 786432 | tf_op jit(solution)/shard_map/all_to_all | solution.py:167
  64.3 87.0 %copy-start.22 = (f32[128]{0:T(128)}, f32[128]{0:T(128)S(1)}, u32[]{:S(2)}) copy-start(f32[128]{0:T(128)S(1)} %add_rsqrt_fusion) | copy-start | bytes 1540
  64.9 6.9 %collective-permute-start = (bf16[128,1024]{0,1:T(8,128)(2,1)}, bf16[128,1024]{0,1:T(8,128)(2,1)S(1)}, u32[]{:S(2)}, u32[]{:S(2)}) collective-permute-start(bf16[128,1024]{0,1:T(8,128)(2,1)} %get-tuple-element.552), channel_id=1, source_target_pairs={{0,4},{4,8},{8,12},{12,16},{16,20},{20,24},{24,28},{28,0},{1,5},{5... | collective-permute-start | bytes 786440 | tf_op jit(solution)/shard_map/while/body/eval_jaxpr/ppermute | solution.py:13
  76.4 6.9 %collective-permute-start = (bf16[128,1024]{0,1:T(8,128)(2,1)}, bf16[128,1024]{0,1:T(8,128)(2,1)S(1)}, u32[]{:S(2)}, u32[]{:S(2)}) collective-permute-start(bf16[128,1024]{0,1:T(8,128)(2,1)} %get-tuple-element.552), channel_id=1, source_target_pairs={{0,4},{4,8},{8,12},{12,16},{16,20},{20,24},{24,28},{28,0},{1,5},{5... | collective-permute-start | bytes 786440 | tf_op jit(solution)/shard_map/while/body/eval_jaxpr/ppermute | solution.py:13
  88.0 6.9 %collective-permute-start = (bf16[128,1024]{0,1:T(8,128)(2,1)}, bf16[128,1024]{0,1:T(8,128)(2,1)S(1)}, u32[]{:S(2)}, u32[]{:S(2)}) collective-permute-start(bf16[128,1024]{0,1:T(8,128)(2,1)} %get-tuple-element.552), channel_id=1, source_target_pairs={{0,4},{4,8},{8,12},{12,16},{16,20},{20,24},{24,28},{28,0},{1,5},{5... | collective-permute-start | bytes 786440 | tf_op jit(solution)/shard_map/while/body/eval_jaxpr/ppermute | solution.py:13
  99.6 6.9 %collective-permute-start = (bf16[128,1024]{0,1:T(8,128)(2,1)}, bf16[128,1024]{0,1:T(8,128)(2,1)S(1)}, u32[]{:S(2)}, u32[]{:S(2)}) collective-permute-start(bf16[128,1024]{0,1:T(8,128)(2,1)} %get-tuple-element.552), channel_id=1, source_target_pairs={{0,4},{4,8},{8,12},{12,16},{16,20},{20,24},{24,28},{28,0},{1,5},{5... | collective-permute-start | bytes 786440 | tf_op jit(solution)/shard_map/while/body/eval_jaxpr/ppermute | solution.py:13
  111.2 6.9 %collective-permute-start = (bf16[128,1024]{0,1:T(8,128)(2,1)}, bf16[128,1024]{0,1:T(8,128)(2,1)S(1)}, u32[]{:S(2)}, u32[]{:S(2)}) collective-permute-start(bf16[128,1024]{0,1:T(8,128)(2,1)} %get-tuple-element.552), channel_id=1, source_target_pairs={{0,4},{4,8},{8,12},{12,16},{16,20},{20,24},{24,28},{28,0},{1,5},{5... | collective-permute-start | bytes 786440 | tf_op jit(solution)/shard_map/while/body/eval_jaxpr/ppermute | solution.py:13
  122.7 6.9 %collective-permute-start = (bf16[128,1024]{0,1:T(8,128)(2,1)}, bf16[128,1024]{0,1:T(8,128)(2,1)S(1)}, u32[]{:S(2)}, u32[]{:S(2)}) collective-permute-start(bf16[128,1024]{0,1:T(8,128)(2,1)} %get-tuple-element.552), channel_id=1, source_target_pairs={{0,4},{4,8},{8,12},{12,16},{16,20},{20,24},{24,28},{28,0},{1,5},{5... | collective-permute-start | bytes 786440 | tf_op jit(solution)/shard_map/while/body/eval_jaxpr/ppermute | solution.py:13
  134.3 6.9 %collective-permute-start = (bf16[128,1024]{0,1:T(8,128)(2,1)}, bf16[128,1024]{0,1:T(8,128)(2,1)S(1)}, u32[]{:S(2)}, u32[]{:S(2)}) collective-permute-start(bf16[128,1024]{0,1:T(8,128)(2,1)} %get-tuple-element.552), channel_id=1, source_target_pairs={{0,4},{4,8},{8,12},{12,16},{16,20},{20,24},{24,28},{28,0},{1,5},{5... | collective-permute-start | bytes 786440 | tf_op jit(solution)/shard_map/while/body/eval_jaxpr/ppermute | solution.py:13
  145.9 8.1 %copy-start.2 = (f32[8,128,64]{1,2,0:T(8,128)S(1)}, f32[8,128,64]{1,2,0:T(8,128)}, u32[]{:S(2)}) copy-start(f32[8,128,64]{1,2,0:T(8,128)} %get-tuple-element.272) | copy-start | bytes 786436
  161.2 11.1 %collective-permute-start.1 = (bf16[128,1024]{0,1:T(8,128)(2,1)}, bf16[128,1024]{0,1:T(8,128)(2,1)}, u32[]{:S(2)}, u32[]{:S(2)}) collective-permute-start(bf16[128,1024]{0,1:T(8,128)(2,1)} %get-tuple-element.593), channel_id=1, source_target_pairs={{0,4},{4,8},{8,12},{12,16},{16,20},{20,24},{24,28},{28,0},{1,5},{5... | collective-permute-start | bytes 786440 | tf_op jit(solution)/shard_map/while/body/eval_jaxpr/ppermute | solution.py:13
  174.1 11.1 %collective-permute-start.1 = (bf16[128,1024]{0,1:T(8,128)(2,1)}, bf16[128,1024]{0,1:T(8,128)(2,1)}, u32[]{:S(2)}, u32[]{:S(2)}) collective-permute-start(bf16[128,1024]{0,1:T(8,128)(2,1)} %get-tuple-element.593), channel_id=1, source_target_pairs={{0,4},{4,8},{8,12},{12,16},{16,20},{20,24},{24,28},{28,0},{1,5},{5... | collective-permute-start | bytes 786440 | tf_op jit(solution)/shard_map/while/body/eval_jaxpr/ppermute | solution.py:13
  186.9 11.4 %collective-permute-start.1 = (bf16[128,1024]{0,1:T(8,128)(2,1)}, bf16[128,1024]{0,1:T(8,128)(2,1)}, u32[]{:S(2)}, u32[]{:S(2)}) collective-permute-start(bf16[128,1024]{0,1:T(8,128)(2,1)} %get-tuple-element.593), channel_id=1, source_target_pairs={{0,4},{4,8},{8,12},{12,16},{16,20},{20,24},{24,28},{28,0},{1,5},{5... | collective-permute-start | bytes 786440 | tf_op jit(solution)/shard_map/while/body/eval_jaxpr/ppermute | solution.py:13
  200.0 14.4 %collective-permute-start.1 = (bf16[128,1024]{0,1:T(8,128)(2,1)}, bf16[128,1024]{0,1:T(8,128)(2,1)}, u32[]{:S(2)}, u32[]{:S(2)}) collective-permute-start(bf16[128,1024]{0,1:T(8,128)(2,1)} %get-tuple-element.593), channel_id=1, source_target_pairs={{0,4},{4,8},{8,12},{12,16},{16,20},{20,24},{24,28},{28,0},{1,5},{5... | collective-permute-start | bytes 786440 | tf_op jit(solution)/shard_map/while/body/eval_jaxpr/ppermute | solution.py:13
  216.1 11.1 %collective-permute-start.1 = (bf16[128,1024]{0,1:T(8,128)(2,1)}, bf16[128,1024]{0,1:T(8,128)(2,1)}, u32[]{:S(2)}, u32[]{:S(2)}) collective-permute-start(bf16[128,1024]{0,1:T(8,128)(2,1)} %get-tuple-element.593), channel_id=1, source_target_pairs={{0,4},{4,8},{8,12},{12,16},{16,20},{20,24},{24,28},{28,0},{1,5},{5... | collective-permute-start | bytes 786440 | tf_op jit(solution)/shard_map/while/body/eval_jaxpr/ppermute | solution.py:13
  228.9 11.1 %collective-permute-start.1 = (bf16[128,1024]{0,1:T(8,128)(2,1)}, bf16[128,1024]{0,1:T(8,128)(2,1)}, u32[]{:S(2)}, u32[]{:S(2)}) collective-permute-start(bf16[128,1024]{0,1:T(8,128)(2,1)} %get-tuple-element.593), channel_id=1, source_target_pairs={{0,4},{4,8},{8,12},{12,16},{16,20},{20,24},{24,28},{28,0},{1,5},{5... | collective-permute-start | bytes 786440 | tf_op jit(solution)/shard_map/while/body/eval_jaxpr/ppermute | solution.py:13
  241.7 11.1 %collective-permute-start.1 = (bf16[128,1024]{0,1:T(8,128)(2,1)}, bf16[128,1024]{0,1:T(8,128)(2,1)}, u32[]{:S(2)}, u32[]{:S(2)}) collective-permute-start(bf16[128,1024]{0,1:T(8,128)(2,1)} %get-tuple-element.593), channel_id=1, source_target_pairs={{0,4},{4,8},{8,12},{12,16},{16,20},{20,24},{24,28},{28,0},{1,5},{5... | collective-permute-start | bytes 786440 | tf_op jit(solution)/shard_map/while/body/eval_jaxpr/ppermute | solution.py:13
  254.6 10.0 %collective-permute-start.2 = (bf16[128,1024]{0,1:T(8,128)(2,1)}, bf16[128,1024]{0,1:T(8,128)(2,1)}, u32[]{:S(2)}, u32[]{:S(2)}) collective-permute-start(bf16[128,1024]{0,1:T(8,128)(2,1)} %get-tuple-element.277), channel_id=1, source_target_pairs={{0,4},{4,8},{8,12},{12,16},{16,20},{20,24},{24,28},{28,0},{1,5},{5... | collective-permute-start | bytes 786440 | tf_op jit(solution)/shard_map/ppermute | solution.py:13
  257.4 7.2 %copy-start.6 = (bf16[128,1024]{1,0:T(8,128)(2,1)S(1)}, bf16[128,1024]{1,0:T(8,128)(2,1)}, u32[]{:S(2)}) copy-start(bf16[128,1024]{1,0:T(8,128)(2,1)} %copy-done.5) | copy-start | bytes 786436
  257.4 7.2 %copy-start.18 = (f32[128]{0:T(128)S(1)}, f32[128]{0:T(128)}, u32[]{:S(2)}) copy-start(f32[128]{0:T(128)} %copy-done.17) | copy-start | bytes 1540
  257.4 7.2 %copy-start.20 = (f32[128]{0:T(128)S(1)}, f32[128]{0:T(128)}, u32[]{:S(2)}) copy-start(f32[128]{0:T(128)} %copy-done.19) | copy-start | bytes 1540
  279.1 11.2 %copy-start.7 = (f32[2,2,2,2,2,16384]{5,4,3,2,1,0:T(2,128)S(1)}, f32[2,2,2,2,2,16384]{5,4,3,2,1,0:T(2,128)}, u32[]{:S(2)}) copy-start(f32[2,2,2,2,2,16384]{5,4,3,2,1,0:T(2,128)} %concatenate.14) | copy-start | bytes 6291460
  298.2 4.5 %collective-permute-start.3 = (bf16[2,2,2,2,65536]{4,2,3,0,1:T(2,128)(2,1)}, bf16[2,2,2,2,65536]{4,2,3,0,1:T(2,128)(2,1)}, u32[]{:S(2)}, u32[]{:S(2)}) collective-permute-start(bf16[2,2,2,2,65536]{4,2,3,0,1:T(2,128)(2,1)} %fusion.20), channel_id=1, source_target_pairs={{0,4},{4,0},{8,12},{12,8},{16,20},{20,16},{24,28},{28,24},{1,5},{5... | collective-permute-start | bytes 6291464 | tf_op jit(solution)/shard_map/ppermute | solution.py:129
  311.3 25.5 %collective-permute-start.4 = (bf16[2,2,2,65536]{3,1,2,0:T(2,128)(2,1)}, bf16[2,2,2,65536]{3,1,2,0:T(2,128)(2,1)}, u32[]{:S(2)}, u32[]{:S(2)}) collective-permute-start(bf16[2,2,2,65536]{3,1,2,0:T(2,128)(2,1)} %fusion.27), channel_id=1, source_target_pairs={{0,8},{4,12},{8,0},{12,4},{16,24},{20,28},{24,16},{28,20},{1,9},{5... | collective-permute-start | bytes 3145736 | tf_op jit(solution)/shard_map/ppermute | solution.py:129
  311.3 33.2 %copy-start.28 = (f32[128]{0:T(128)S(1)}, f32[128]{0:T(128)}, u32[]{:S(2)}) copy-start(f32[128]{0:T(128)} %get-tuple-element.349) | copy-start | bytes 1540
  342.6 13.6 %collective-permute-start.5 = (bf16[2,2,65536]{2,0,1:T(2,128)(2,1)}, bf16[2,2,65536]{2,0,1:T(2,128)(2,1)}, u32[]{:S(2)}, u32[]{:S(2)}) collective-permute-start(bf16[2,2,65536]{2,0,1:T(2,128)(2,1)} %fusion.35), channel_id=1, source_target_pairs={{0,16},{4,20},{8,24},{12,28},{16,0},{20,4},{24,8},{28,12},{1,17},{... | collective-permute-start | bytes 1572872 | tf_op jit(solution)/shard_map/ppermute | solution.py:129
  360.0 44.5 %collective-permute-start.6 = (bf16[2,65536]{1,0:T(2,128)(2,1)}, bf16[2,65536]{1,0:T(2,128)(2,1)}, u32[]{:S(2)}, u32[]{:S(2)}) collective-permute-start(bf16[2,65536]{1,0:T(2,128)(2,1)} %fusion.41), channel_id=1, source_target_pairs={{0,1},{1,0},{2,3},{3,2},{4,5},{5,4},{6,7},{7,6},{8,9},{9,8},{10,11... | collective-permute-start | bytes 786440 | tf_op jit(solution)/shard_map/ppermute | solution.py:129
  406.8 8.3 %collective-permute-start.7 = (bf16[65536]{0:T(1024)(128)(2,1)S(1)}, bf16[65536]{0:T(1024)(128)(2,1)S(1)}, u32[]{:S(2)}, u32[]{:S(2)}) collective-permute-start(bf16[65536]{0:T(1024)(128)(2,1)S(1)} %convert_reduce_fusion.1), channel_id=1, source_target_pairs={{0,2},{1,3},{2,0},{3,1},{4,6},{5,7},{6,4},{7,5},{8,10},{9,11},{10,... | collective-permute-start | bytes 393224 | tf_op jit(solution)/shard_map/ppermute | solution.py:129
  (26 other events, 66.7 us)

commit v4 on v2

--- a/solution.py
+++ b/solution.py
@@ -97,6 +97,48 @@
 def move_grads(accum):
     moved = shifted(accum.astype(jnp.bfloat16), "seq", 1).astype(accum.dtype)
     return moved
+
+
+def exchange_bits():
+    seq_bits = lax.axis_size("seq").bit_length() - 1
+    clip_bits = lax.axis_size("clip").bit_length() - 1
+    assert (1 << seq_bits) == lax.axis_size("seq")
+    assert (1 << clip_bits) == lax.axis_size("clip")
+    return seq_bits, clip_bits
+
+
+def exchange_order(values):
+    seq_bits, clip_bits = exchange_bits()
+    total = seq_bits + clip_bits
+    lead = values.shape[0]
+    split = values.reshape([lead] + [2] * total + [-1])
+    seq_dims = [1 + seq_bits - 1 - bit for bit in range(seq_bits)]
+    clip_dims = [1 + seq_bits + clip_bits - 1 - bit for bit in range(clip_bits)]
+    perm = [0] + seq_dims + clip_dims + [total + 1]
+    return split.transpose(perm).reshape(values.shape)
+
+
+def halving_scatter(grad_wqkv, grad_wout, small):
+    seq_bits, clip_bits = exchange_bits()
+    total = seq_bits + clip_bits
+    first = grad_wqkv.reshape([2] * total + [-1, grad_wqkv.shape[1]])
+    second = grad_wout.reshape([2] * total + [-1, grad_wout.shape[1]])
+    order = [("seq", bit) for bit in range(seq_bits)] + [("clip", bit) for bit in range(clip_bits)]
+    for axis, bit in order:
+        mine = (lax.axis_index(axis) >> bit) & 1
+        count = lax.axis_size(axis)
+        pairs = [(src, src ^ (1 << bit)) for src in range(count)]
+        keep_a = lax.dynamic_index_in_dim(first, mine, axis=0, keepdims=False)
+        give_a = lax.dynamic_index_in_dim(first, 1 - mine, axis=0, keepdims=False)
+        keep_b = lax.dynamic_index_in_dim(second, mine, axis=0, keepdims=False)
+        give_b = lax.dynamic_index_in_dim(second, 1 - mine, axis=0, keepdims=False)
+        got_a, got_b, got_s = lax.ppermute(
+            (give_a.astype(jnp.bfloat16), give_b.astype(jnp.bfloat16), small), axis, pairs
+        )
+        first = keep_a + got_a.astype(jnp.float32)
+        second = keep_b + got_b.astype(jnp.float32)
+        small = small + got_s
+    return (first, second, small)
 
 
 def per_device(raw_tokens, teacher, keep_rows, w_qkv, w_out, ln_gain):
@@ -142,13 +184,6 @@
         .at[place]
         .set(got_target.reshape(-1, width), mode="drop")
     )
-    live_count = jnp.full((), TOK_DEV, jnp.int32)
-    anchor_table = jnp.full((shards,), TOK_DEV, jnp.int32)
-
-    def counts_at(step):
-        front_count = jnp.sum(jnp.where(shard_ids == (my_index - step) % shards, anchor_table, 0))
-        return jnp.stack([front_count, front_count])
-
     rows = tokens.shape[0]
     inner = w_out.shape[0]
     heads = inner // HEAD_DIM
@@ -156,23 +191,19 @@
     projected = jnp.dot(hidden, w_qkv, preferred_element_type=jnp.float32)
     queries = projected[:, :inner].astype(jnp.bfloat16).reshape(rows, heads, HEAD_DIM)
     pair_rows = projected[:, inner:].astype(jnp.bfloat16)
-    start_state = (
-        jnp.full((heads, rows), -1e30, jnp.float32),
-        jnp.zeros((heads, rows), jnp.float32),
-        jnp.zeros((heads, rows, HEAD_DIM), jnp.float32),
-    )
-    steps_ids = jnp.arange(1, shards, dtype=jnp.int32)
-    own_count = counts_at(jnp.zeros((), jnp.int32))
-    state = absorb(start_state, queries, pair_rows, own_count)
-
-    def forward_step(carry, step):
-        travel_rows, inner_state = carry
-        travel_rows = move_keys(travel_rows)
-        inner_state = absorb(inner_state, queries, travel_rows, counts_at(step))
-        return ((travel_rows, inner_state), travel_rows)
-
-    (unused_rows, state), stored_rows = lax.scan(forward_step, (pair_rows, state), steps_ids)
-    row_max, row_sum, blended = state
+    gathered = jnp.stack([pair_rows] + [shifted(pair_rows, "seq", step) for step in range(1, shards)])
+    split_kv = gathered.reshape(shards * rows, heads, 2, HEAD_DIM)
+    all_keys = split_kv[:, :, 0]
+    all_values = split_kv[:, :, 1]
+    scores = (
+        jnp.einsum("qhd,khd->hqk", queries, all_keys, preferred_element_type=jnp.float32) * 0.125
+    )
+    row_max = jnp.max(scores, axis=2)
+    weights = jnp.exp(scores - row_max[:, :, None])
+    row_sum = jnp.sum(weights, axis=2)
+    blended = jnp.einsum(
+        "hqk,khd->hqd", weights.astype(jnp.bfloat16), all_values, preferred_element_type=jnp.float32
+    )
     log_total = row_max + jnp.log(row_sum)
     attended = (
         (blended / row_sum[:, :, None]).transpose(1, 0, 2).reshape(rows, inner).astype(jnp.bfloat16)
@@ -181,10 +212,8 @@
         attended, w_out, preferred_element_type=jnp.float32
     )
     token_loss, grad_y = align_terms(student, target)
-    is_live = jnp.arange(rows, dtype=jnp.int32) < live_count
-    token_loss = jnp.where(is_live, token_loss, 0.0)
-    grad_b = jnp.where(is_live[:, None], grad_y, 0.0).astype(jnp.bfloat16)
-    grad_wout = jnp.dot(attended.T, grad_b, preferred_element_type=jnp.float32)
+    grad_b = grad_y.astype(jnp.bfloat16)
+    grad_wout = jnp.dot(exchange_order(attended).T, grad_b, preferred_element_type=jnp.float32)
     grad_heads = (
         jnp.dot(grad_b, w_out.T, preferred_element_type=jnp.float32)
         .astype(jnp.bfloat16)
@@ -195,33 +224,31 @@
         * attended.reshape(rows, heads, HEAD_DIM).astype(jnp.float32),
         axis=2,
     ).T
-    d_query, accum = contribution(queries, grad_heads, log_total, row_dot, pair_rows, own_count)
-
-    def backward_step(carry, stored):
-        query_sum, travel_grads = carry
-        block_rows, step = stored
-        travel_grads = move_grads(travel_grads)
-        part_query, part_pairs = contribution(
-            queries, grad_heads, log_total, row_dot, block_rows, counts_at(step)
-        )
-        return ((query_sum + part_query, travel_grads + part_pairs), None)
-
-    (d_query, accum), unused_out = lax.scan(
-        backward_step, (d_query, accum), (stored_rows, steps_ids)
-    )
-    accum = move_grads(accum)
+    prob_full = jnp.exp(scores - log_total[:, :, None])
+    d_value = jnp.einsum(
+        "hqk,qhd->khd", prob_full.astype(jnp.bfloat16), grad_heads, preferred_element_type=jnp.float32
+    )
+    d_prob = jnp.einsum(
+        "qhd,khd->hqk", grad_heads, all_values, preferred_element_type=jnp.float32
+    )
+    d_score = (prob_full * (d_prob - row_dot[:, :, None])).astype(jnp.bfloat16)
+    d_query = 0.125 * jnp.einsum(
+        "hqk,khd->qhd", d_score, all_keys, preferred_element_type=jnp.float32
+    )
+    d_key = 0.125 * jnp.einsum("hqk,qhd->khd", d_score, queries, preferred_element_type=jnp.float32)
+    d_pairs = jnp.stack([d_key, d_value], axis=2).reshape(shards, rows, 2 * inner)
+    accum = d_pairs[0]
+    for step in range(1, shards):
+        accum = accum + shifted(d_pairs[step].astype(jnp.bfloat16), "seq", -step).astype(jnp.float32)
     d_proj = jnp.concatenate([d_query.reshape(rows, inner), accum], axis=1).astype(jnp.bfloat16)
-    grad_wqkv = jnp.dot(hidden.T, d_proj, preferred_element_type=jnp.float32)
+    grad_wqkv = jnp.dot(exchange_order(hidden).T, d_proj, preferred_element_type=jnp.float32)
     d_hidden = jnp.dot(d_proj, w_qkv.T, preferred_element_type=jnp.float32)
     grad_ln = jnp.sum(d_hidden * normed, axis=0)
     loss_part = jnp.sum(token_loss)
-    loss_total, grad_gain = lax.psum((loss_part, grad_ln), ("seq", "clip"))
-    grad_qkv, grad_out = (
-        lax.psum_scatter(grad_wqkv.astype(jnp.bfloat16), ("seq", "clip"), scatter_dimension=0, tiled=True).astype(jnp.float32).reshape(-1),
-        lax.psum_scatter(grad_wout.astype(jnp.bfloat16), ("seq", "clip"), scatter_dimension=0, tiled=True).astype(jnp.float32).reshape(-1),
-    )
+    small = jnp.concatenate([grad_ln, loss_part.reshape(1)])
+    grad_qkv, grad_out, small = halving_scatter(grad_wqkv, grad_wout, small)
     count_all = shards * lax.axis_size("clip") * TOK_DEV
-    return (loss_total / count_all, grad_qkv, grad_out, grad_gain)
+    return (small[-1] / count_all, grad_qkv.reshape(-1), grad_out.reshape(-1), small[:-1])
 
 
 def solution(mesh):

time: 427 us -> 286 us (0.67)
  matrix products: 76.7 us -> 16.4 us
  waiting for transfers between devices: 124 us -> 69.2 us
  local copies, waits for them, and re-layouts: 73.8 us -> 120 us
  blocking collectives: 50 us -> 9.46 us
  other arithmetic: 60.1 us -> 27.3 us
  starting transfers between devices: 13.3 us -> 38.5 us
  between operations: 16.2 us -> 3.12 us
  loops' own time: 9.97 us -> 0 us
    reduce_scatter x2 -> x0, waiting for transfers between devices: 88.9 us -> none  [the longest x1 88.9 us: per_device(): lax.psum_scatter(grad_wqkv.astype(jnp.bfloat16), ('seq', 'clip'), scatter...]
    dot_general x57 -> x8, matrix products: 71.1 us -> 13.1 us  [the longest x1 3.41 us: per_device(): jnp.einsum('hqk,khd->qhd', d_score, all_keys, preferred_element_type=jnp....]
    ppermute x0 -> x15, waiting for transfers between devices: none -> 43.2 us  [halving_scatter(): lax.ppermute((give_a.astype(jnp.bfloat16), give_b.astype(jnp.bfloat16), s...]
    psum x1 -> x0, blocking collectives: 40.6 us -> none  [per_device(): loss_total, grad_gain = lax.psum((loss_part, grad_ln), ('seq', 'clip'))]
    unnamed x50 -> x87, local copies, waits for them, and re-layouts: 9.84 us -> 44 us
    dynamic_slice x21 -> x0, local copies, waits for them, and re-layouts: 24.3 us -> none  [the longest x14 17.5 us: per_device(): lax.scan(forward_step, (pair_rows, state), steps_ids)]
    slice x0 -> x12, local copies, waits for them, and re-layouts: none -> 22.9 us  [the longest x8 11.1 us: per_device(): d_pairs[step].astype(jnp.bfloat16)]
    convert_element_type x0 -> x18, local copies, waits for them, and re-layouts: none -> 18.5 us  [the longest x7 12.7 us: per_device(): d_pairs[step].astype(jnp.bfloat16)]
  transfers between devices with their start and end apart: 19 -> 31, of which waited for: 11 -> 14; matrix products, arithmetic and copies ran while one was open for 29% -> 22% of each run, Pallas kernels for 0% -> 0%
where the time goes in v4:
time: 286 us; the launch traced here: 284 us
  local copies, waits for them, and re-layouts  120 us (42%)
  waiting for transfers between devices  69.2 us (24%)
  starting transfers between devices  38.5 us (13%)
  other arithmetic  27.3 us (10%)
  matrix products  16.4 us (6%)
  blocking collectives  9.46 us (3%)
  between operations  3.12 us (1%)
    unnamed x87, local copies, waits for them, and re-layouts  44 us
    ppermute x15, waiting for transfers between devices, halving_scatter(): lax.ppermute((give_a.astype(jnp.bfloat16), give_b.astype(jnp.bfloat16), s...  43.2 us
    ppermute x14, waiting for transfers between devices, shifted(): return lax.ppermute(value, axis, pairs)  19.9 us
    ppermute x15, starting transfers between devices, halving_scatter(): lax.ppermute((give_a.astype(jnp.bfloat16), give_b.astype(jnp.bfloat16), s...  15.8 us
    ppermute x14, starting transfers between devices, shifted(): return lax.ppermute(value, axis, pairs)  15.1 us
    convert_element_type x7, local copies, waits for them, and re-layouts, per_device(): d_pairs[step].astype(jnp.bfloat16)  12.7 us
    slice x8, local copies, waits for them, and re-layouts, per_device(): d_pairs[step].astype(jnp.bfloat16)  11.1 us
    slice x1, local copies, waits for them, and re-layouts, per_device(): all_values = split_kv[:, :, 1]  9.82 us
  transfers between devices with their start and end apart: 31, of which 14 were waited for; matrix products, arithmetic and copies ran while one was open for 22% of the time, Pallas kernels for 0%

profile of v4, /device:TPU:0, one launch (start us, length us, event | category | flops | bytes accessed | tf_op | source)
XLA Modules:
  0.0 284.1 jit_solution(8734427686865846496)
XLA Ops:
  5.6 9.5 %all-reduce = s32[8]{0:T(128)S(1)} all-reduce(s32[8]{0:T(128)S(1)} %dynamic-update-slice), channel_id=1, replica_groups=mesh['seq'=8,'clip'=4] {'seq'}, use_global_device_ids=true, to_apply=%add | all-reduce | flops 8 | bytes 64
  18.4 3.4 %gather_fusion.2 = bf16[192,1024]{1,0:T(8,128)(2,1)} fusion(bf16[512,1024]{1,0:T(8,128)(2,1)} %bitcast.166, s32[1024]{0:T(1024)S(1)} %get-tuple-element.32), kind=kCustom, calls=%fused_computation.2 | custom fusion | bytes 787200 | tf_op jit(solution)/shard_map/gather | solution.py:153
  21.9 3.4 %gather_fusion = bf16[192,1024]{1,0:T(8,128)(2,1)} fusion(bf16[512,1024]{1,0:T(8,128)(2,1)} %bitcast.167, s32[1024]{0:T(1024)S(1)} %get-tuple-element.32), kind=kCustom, calls=%fused_computation | custom fusion | bytes 787200 | tf_op jit(solution)/shard_map/gather | solution.py:152
  27.3 3.1 %gather_fusion.3 = bf16[192,1024]{1,0:T(8,128)(2,1)} fusion(bf16[192,1024]{1,0:T(8,128)(2,1)} %get-tuple-element.22, s32[1024]{0:T(1024)S(1)} %get-tuple-element.31), kind=kCustom, calls=%fused_computation.3 | custom fusion | bytes 787200 | tf_op jit(solution)/shard_map/gather | solution.py:167
  32.2 2.2 broadcast_select_fusion.2
  34.4 3.5 %all-to-all-start = ((bf16[8,24,1024]{2,1,0:T(8,128)(2,1)}), bf16[8,24,1024]{2,1,0:T(8,128)(2,1)S(1)}, u32[]{:S(2)}, u32[]{:S(2)}) async-start(bf16[8,24,1024]{2,1,0:T(8,128)(2,1)} %get-tuple-element.18), calls=%async_computation | async-start | bytes 786432 | tf_op jit(solution)/shard_map/all_to_all | solution.py:170
  40.0 6.1 %all-to-all-done = bf16[8,24,1024]{2,1,0:T(8,128)(2,1)S(1)} async-done(((bf16[8,24,1024]{2,1,0:T(8,128)(2,1)}), bf16[8,24,1024]{2,1,0:T(8,128)(2,1)S(1)}, u32[]{:S(2)}, u32[]{:S(2)}) %all-to-all-start) | async-done | bytes 393248 | tf_op jit(solution)/shard_map/all_to_all | solution.py:170
  46.1 4.1 %all-to-all-start.1 = ((bf16[8,24,1024]{2,1,0:T(8,128)(2,1)}), bf16[8,24,1024]{2,1,0:T(8,128)(2,1)}, u32[]{:S(2)}, u32[]{:S(2)}) async-start(bf16[8,24,1024]{2,1,0:T(8,128)(2,1)} %get-tuple-element.17), calls=%async_computation.1 | async-start | bytes 786432 | tf_op jit(solution)/shard_map/all_to_all | solution.py:171
  54.2 2.8 collective-permute-start.5
  59.8 2.5 scatter_custom_fusion.1
  66.1 9.5 %collective-permute-done = bf16[128,1024]{1,0:T(8,128)(2,1)} collective-permute-done((bf16[128,1024]{1,0:T(8,128)(2,1)}, bf16[128,1024]{1,0:T(8,128)(2,1)}, u32[]{:S(2)}, u32[]{:S(2)}) %collective-permute-start) | collective-permute-done | bytes 262176 | tf_op jit(solution)/shard_map/ppermute | solution.py:13
  77.2 2.6 collective-permute-start.6
  81.5 2.9 %collective-permute-done.2 = bf16[128,1024]{1,0:T(8,128)(2,1)S(1)} collective-permute-done((bf16[128,1024]{1,0:T(8,128)(2,1)}, bf16[128,1024]{1,0:T(8,128)(2,1)S(1)}, u32[]{:S(2)}, u32[]{:S(2)}) %collective-permute-start.2) | collective-permute-done | bytes 262176 | tf_op jit(solution)/shard_map/ppermute | solution.py:13
  90.9 8.8 %reshape.475 = bf16[1024,8,2,64]{3,2,1,0:T(2,128)(2,1)} reshape(bf16[8,128,1024]{2,1,0:T(8,128)(2,1)} %bitcast_dynamic-update-slice_fusion) | data formatting | bytes 4194304 | tf_op jit(solution)/shard_map/reshape | solution.py:195
  99.7 9.8 %fusion.70 = (bf16[1024,8,1,64]{3,2,1,0:T(2,128)(2,1)}, bf16[1024,8,1,64]{3,2,1,0:T(2,128)(2,1)}) fusion(bf16[1024,8,2,64]{3,2,1,0:T(2,128)(2,1)} %reshape.475), kind=kLoop, calls=%fused_computation.153 | loop fusion | bytes 4194304 | tf_op jit(solution)/shard_map/slice | solution.py:197
  109.6 10.2 %copy.46 = bf16[1024,8,1,64]{0,3,1,2:T(8,128)(2,1)} copy(bf16[1024,8,1,64]{3,2,1,0:T(2,128)(2,1)} %get-tuple-element.8) | data formatting | bytes 2097152
  119.8 10.2 %copy.45 = bf16[1024,8,1,64]{0,3,1,2:T(8,128)(2,1)} copy(bf16[1024,8,1,64]{3,2,1,0:T(2,128)(2,1)} %get-tuple-element.9) | data formatting | bytes 2097152
  140.7 3.3 %fusion.12 = f32[1024,8,1,64]{0,3,1,2:T(8,128)S(1)} fusion(bf16[128,8,64]{0,2,1:T(8,128)(2,1)S(1)} %bitcast.168, f32[8,128,1024]{2,1,0:T(8,128)} %copy-done.1, f32[8,128]{1,0:T(8,128)S(1)} %log_add_fusion), kind=kOutput, calls=%fused_computation.27 | convolution fusion | flops 137363456 | bytes 6426624 | tf_op jit(solution)/shard_map/hqk,qhd->khd/dot_general | solution.py:228
  176.1 2.9 %collective-permute-start.12 = (bf16[128,1024]{1,0:T(8,128)(2,1)}, bf16[128,1024]{1,0:T(8,128)(2,1)}, u32[]{:S(2)}, u32[]{:S(2)}) collective-permute-start(bf16[128,1024]{1,0:T(8,128)(2,1)} %copy.34), channel_id=1, source_target_pairs={{0,8},{4,12},{8,16},{12,20},{16,24},{20,28},{24,0},{28,4},{1,9},{5... | collective-permute-start | bytes 786440 | tf_op jit(solution)/shard_map/ppermute | solution.py:13
  179.0 2.6 collective-permute-start.7
  181.7 3.4 %fusion.20 = bf16[8,64,128]{2,1,0:T(8,128)(2,1)} fusion(bf16[8,128,1024]{2,1,0:T(8,128)(2,1)} %copy-done.4, bf16[1024,8,1,64]{0,3,1,2:T(8,128)(2,1)} %copy.45), kind=kOutput, calls=%fused_computation.37 | convolution fusion | flops 134348800 | bytes 3276800 | tf_op jit(solution)/shard_map/hqk,khd->qhd/dot_general | solution.py:235
  190.1 3.6 %collective-permute-done.10 = bf16[128,1024]{1,0:T(8,128)(2,1)} collective-permute-done((bf16[128,1024]{1,0:T(8,128)(2,1)}, bf16[128,1024]{1,0:T(8,128)(2,1)}, u32[]{:S(2)}, u32[]{:S(2)}) %collective-permute-start.10) | collective-permute-done | bytes 262176 | tf_op jit(solution)/shard_map/ppermute | solution.py:13
  193.7 4.0 %collective-permute-done.11 = bf16[128,1024]{1,0:T(8,128)(2,1)} collective-permute-done((bf16[128,1024]{1,0:T(8,128)(2,1)}, bf16[128,1024]{1,0:T(8,128)(2,1)}, u32[]{:S(2)}, u32[]{:S(2)}) %collective-permute-start.11) | collective-permute-done | bytes 262176 | tf_op jit(solution)/shard_map/ppermute | solution.py:13
  201.3 2.6 copy-done.3
  212.2 2.9 %bitcast_add_fusion = f32[2,2,2,2,32,1536]{5,4,3,2,1,0:T(8,128)S(1)} fusion(bf16[2,2,2,2,32,1536]{5,4,3,2,1,0:T(8,128)(2,1)} %collective-permute-done.19, f32[2,2,2,2,2,32,1536]{6,5,4,3,2,1,0:T(8,128)} %copy-done.3, s32[]{:T(128)S(6)} %select_n.145), kind=kLoop, calls=%fused_computation.17 | loop fusion | flops 1572864 | bytes 7864324 | tf_op jit(solution)/shard_map/add | solution.py:138
  219.3 21.4 %collective-permute-done.25 = bf16[2,2,2,16,1024]{4,3,2,1,0:T(8,128)(2,1)S(1)} collective-permute-done((bf16[2,2,2,16,1024]{4,3,2,1,0:T(8,128)(2,1)S(1)}, bf16[2,2,2,16,1024]{4,3,2,1,0:T(8,128)(2,1)S(1)}, u32[]{:S(2)}, u32[]{:S(2)}) %collective-permute-start.25) | collective-permute-done | bytes 262176 | tf_op jit(solution)/shard_map/ppermute | solution.py:135
  246.7 3.4 %collective-permute-done.15 = f32[1025]{0:T(1024)S(1)} collective-permute-done((f32[1025]{0:T(1024)S(1)}, f32[1025]{0:T(1024)S(1)}, u32[]{:S(2)}, u32[]{:S(2)}) %collective-permute-start.15) | collective-permute-done | bytes 4132 | tf_op jit(solution)/shard_map/ppermute | solution.py:135
  250.6 4.6 %collective-permute-done.16 = f32[1025]{0:T(1024)S(1)} collective-permute-done((f32[1025]{0:T(1024)S(1)}, f32[1025]{0:T(1024)S(1)}, u32[]{:S(2)}, u32[]{:S(2)}) %collective-permute-start.16) | collective-permute-done | bytes 4132 | tf_op jit(solution)/shard_map/ppermute | solution.py:135
  258.9 2.6 collective-permute-start.18
  271.2 2.6 collective-permute-start.28
  273.9 2.5 collective-permute-done.22
  278.4 3.9 %collective-permute-done.23 = bf16[32,1536]{1,0:T(8,128)(2,1)S(1)} collective-permute-done((bf16[32,1536]{1,0:T(8,128)(2,1)S(1)}, bf16[32,1536]{1,0:T(8,128)(2,1)S(1)}, u32[]{:S(2)}, u32[]{:S(2)}) %collective-permute-start.23) | collective-permute-done | bytes 98336 | tf_op jit(solution)/shard_map/ppermute | solution.py:135
  (223 shorter events, 119.9 us)
Async XLA Ops:
  34.4 11.7 %all-to-all-start = ((bf16[8,24,1024]{2,1,0:T(8,128)(2,1)}), bf16[8,24,1024]{2,1,0:T(8,128)(2,1)S(1)}, u32[]{:S(2)}, u32[]{:S(2)}) async-start(bf16[8,24,1024]{2,1,0:T(8,128)(2,1)} %get-tuple-element.18), calls=%async_computation | async-start | bytes 786432 | tf_op jit(solution)/shard_map/all_to_all | solution.py:170
  46.1 13.7 %all-to-all-start.1 = ((bf16[8,24,1024]{2,1,0:T(8,128)(2,1)}), bf16[8,24,1024]{2,1,0:T(8,128)(2,1)}, u32[]{:S(2)}, u32[]{:S(2)}) async-start(bf16[8,24,1024]{2,1,0:T(8,128)(2,1)} %get-tuple-element.17), calls=%async_computation.1 | async-start | bytes 786432 | tf_op jit(solution)/shard_map/all_to_all | solution.py:171
  54.2 34.3 %collective-permute-start.5 = (bf16[128,1024]{1,0:T(8,128)(2,1)}, bf16[128,1024]{1,0:T(8,128)(2,1)}, u32[]{:S(2)}, u32[]{:S(2)}) collective-permute-start(bf16[128,1024]{1,0:T(8,128)(2,1)} %slice.81), channel_id=1, source_target_pairs={{0,24},{4,28},{8,0},{12,4},{16,8},{20,12},{24,16},{28,20},{1,25},{... | collective-permute-start | bytes 786440 | tf_op jit(solution)/shard_map/ppermute | solution.py:13
  57.0 29.8 %collective-permute-start.4 = (bf16[128,1024]{1,0:T(8,128)(2,1)}, bf16[128,1024]{1,0:T(8,128)(2,1)}, u32[]{:S(2)}, u32[]{:S(2)}) collective-permute-start(bf16[128,1024]{1,0:T(8,128)(2,1)} %slice.81), channel_id=1, source_target_pairs={{0,20},{4,24},{8,28},{12,0},{16,4},{20,8},{24,12},{28,16},{1,21},{... | collective-permute-start | bytes 786440 | tf_op jit(solution)/shard_map/ppermute | solution.py:13
  57.0 28.1 %collective-permute-start.3 = (bf16[128,1024]{1,0:T(8,128)(2,1)}, bf16[128,1024]{1,0:T(8,128)(2,1)}, u32[]{:S(2)}, u32[]{:S(2)}) collective-permute-start(bf16[128,1024]{1,0:T(8,128)(2,1)} %slice.81), channel_id=1, source_target_pairs={{0,16},{4,20},{8,24},{12,28},{16,0},{20,4},{24,8},{28,12},{1,17},{... | collective-permute-start | bytes 786440 | tf_op jit(solution)/shard_map/ppermute | solution.py:13
  58.5 18.7 %collective-permute-start.1 = (bf16[128,1024]{1,0:T(8,128)(2,1)}, bf16[128,1024]{1,0:T(8,128)(2,1)}, u32[]{:S(2)}, u32[]{:S(2)}) collective-permute-start(bf16[128,1024]{1,0:T(8,128)(2,1)} %slice.81), channel_id=1, source_target_pairs={{0,8},{4,12},{8,16},{12,20},{16,24},{20,28},{24,0},{28,4},{1,9},{5... | collective-permute-start | bytes 786440 | tf_op jit(solution)/shard_map/ppermute | solution.py:13
  58.5 17.0 %collective-permute-start = (bf16[128,1024]{1,0:T(8,128)(2,1)}, bf16[128,1024]{1,0:T(8,128)(2,1)}, u32[]{:S(2)}, u32[]{:S(2)}) collective-permute-start(bf16[128,1024]{1,0:T(8,128)(2,1)} %slice.81), channel_id=1, source_target_pairs={{0,4},{4,8},{8,12},{12,16},{16,20},{20,24},{24,28},{28,0},{1,5},{5... | collective-permute-start | bytes 786440 | tf_op jit(solution)/shard_map/ppermute | solution.py:13
  66.1 64.0 %copy-start.20 = (bf16[128,512]{0,1:T(8,128)(2,1)}, bf16[128,512]{0,1:T(8,128)(2,1)S(1)}, u32[]{:S(2)}) copy-start(bf16[128,512]{0,1:T(8,128)(2,1)S(1)} %copy.18) | copy-start | bytes 393220
  75.5 8.8 %collective-permute-start.2 = (bf16[128,1024]{1,0:T(8,128)(2,1)}, bf16[128,1024]{1,0:T(8,128)(2,1)S(1)}, u32[]{:S(2)}, u32[]{:S(2)}) collective-permute-start(bf16[128,1024]{1,0:T(8,128)(2,1)} %slice.81), channel_id=1, source_target_pairs={{0,12},{4,16},{8,20},{12,24},{16,28},{20,0},{24,4},{28,8},{1,13},{... | collective-permute-start | bytes 786440 | tf_op jit(solution)/shard_map/ppermute | solution.py:13
  77.2 12.9 %collective-permute-start.6 = (bf16[128,1024]{1,0:T(8,128)(2,1)}, bf16[128,1024]{1,0:T(8,128)(2,1)S(1)}, u32[]{:S(2)}, u32[]{:S(2)}) collective-permute-start(bf16[128,1024]{1,0:T(8,128)(2,1)} %slice.81), channel_id=1, source_target_pairs={{0,28},{4,0},{8,4},{12,8},{16,12},{20,16},{24,20},{28,24},{1,29},{... | collective-permute-start | bytes 786440 | tf_op jit(solution)/shard_map/ppermute | solution.py:13
  153.1 26.0 %collective-permute-start.8 = (bf16[128,1024]{1,0:T(8,128)(2,1)}, bf16[128,1024]{1,0:T(8,128)(2,1)}, u32[]{:S(2)}, u32[]{:S(2)}) collective-permute-start(bf16[128,1024]{1,0:T(8,128)(2,1)} %copy.26), channel_id=1, source_target_pairs={{0,24},{4,28},{8,0},{12,4},{16,8},{20,12},{24,16},{28,20},{1,25},{... | collective-permute-start | bytes 786440 | tf_op jit(solution)/shard_map/ppermute | solution.py:13
  154.9 24.2 %collective-permute-start.9 = (bf16[128,1024]{1,0:T(8,128)(2,1)}, bf16[128,1024]{1,0:T(8,128)(2,1)}, u32[]{:S(2)}, u32[]{:S(2)}) collective-permute-start(bf16[128,1024]{1,0:T(8,128)(2,1)} %copy.28), channel_id=1, source_target_pairs={{0,20},{4,24},{8,28},{12,0},{16,4},{20,8},{24,12},{28,16},{1,21},{... | collective-permute-start | bytes 786440 | tf_op jit(solution)/shard_map/ppermute | solution.py:13
  174.1 19.6 %collective-permute-start.10 = (bf16[128,1024]{1,0:T(8,128)(2,1)}, bf16[128,1024]{1,0:T(8,128)(2,1)}, u32[]{:S(2)}, u32[]{:S(2)}) collective-permute-start(bf16[128,1024]{1,0:T(8,128)(2,1)} %copy.30), channel_id=1, source_target_pairs={{0,16},{4,20},{8,24},{12,28},{16,0},{20,4},{24,8},{28,12},{1,17},{... | collective-permute-start | bytes 786440 | tf_op jit(solution)/shard_map/ppermute | solution.py:13
  174.6 23.0 %collective-permute-start.11 = (bf16[128,1024]{1,0:T(8,128)(2,1)}, bf16[128,1024]{1,0:T(8,128)(2,1)}, u32[]{:S(2)}, u32[]{:S(2)}) collective-permute-start(bf16[128,1024]{1,0:T(8,128)(2,1)} %copy.32), channel_id=1, source_target_pairs={{0,12},{4,16},{8,20},{12,24},{16,28},{20,0},{24,4},{28,8},{1,13},{... | collective-permute-start | bytes 786440 | tf_op jit(solution)/shard_map/ppermute | solution.py:13
  176.1 21.6 %collective-permute-start.12 = (bf16[128,1024]{1,0:T(8,128)(2,1)}, bf16[128,1024]{1,0:T(8,128)(2,1)}, u32[]{:S(2)}, u32[]{:S(2)}) collective-permute-start(bf16[128,1024]{1,0:T(8,128)(2,1)} %copy.34), channel_id=1, source_target_pairs={{0,8},{4,12},{8,16},{12,20},{16,24},{20,28},{24,0},{28,4},{1,9},{5... | collective-permute-start | bytes 786440 | tf_op jit(solution)/shard_map/ppermute | solution.py:13
  179.0 18.6 %collective-permute-start.13 = (bf16[128,1024]{1,0:T(8,128)(2,1)}, bf16[128,1024]{1,0:T(8,128)(2,1)}, u32[]{:S(2)}, u32[]{:S(2)}) collective-permute-start(bf16[128,1024]{1,0:T(8,128)(2,1)} %copy.36), channel_id=1, source_target_pairs={{0,4},{4,8},{8,12},{12,16},{16,20},{20,24},{24,28},{28,0},{1,5},{5... | collective-permute-start | bytes 786440 | tf_op jit(solution)/shard_map/ppermute | solution.py:13
  179.0 18.6 %collective-permute-start.7 = (bf16[128,1024]{1,0:T(8,128)(2,1)}, bf16[128,1024]{1,0:T(8,128)(2,1)}, u32[]{:S(2)}, u32[]{:S(2)}) collective-permute-start(bf16[128,1024]{1,0:T(8,128)(2,1)} %copy.23), channel_id=1, source_target_pairs={{0,28},{4,0},{8,4},{12,8},{16,12},{20,16},{24,20},{28,24},{1,29},{... | collective-permute-start | bytes 786440 | tf_op jit(solution)/shard_map/ppermute | solution.py:13
  205.3 6.9 %collective-permute-start.19 = (bf16[2,2,2,2,32,1536]{5,4,3,2,1,0:T(8,128)(2,1)}, bf16[2,2,2,2,32,1536]{5,4,3,2,1,0:T(8,128)(2,1)}, u32[]{:S(2)}, u32[]{:S(2)}) collective-permute-start(bf16[2,2,2,2,32,1536]{5,4,3,2,1,0:T(8,128)(2,1)} %fusion.15), channel_id=1, source_target_pairs={{0,4},{4,0},{8,12},{12,8},{16,20},{20,16},{24,28},{28,24},{1,5},{5... | collective-permute-start | bytes 4718600 | tf_op jit(solution)/shard_map/ppermute | solution.py:135
  208.2 2.4 collective-permute-start.24
  215.2 26.8 %collective-permute-start.20 = (bf16[2,2,2,32,1536]{4,3,2,1,0:T(8,128)(2,1)S(1)}, bf16[2,2,2,32,1536]{4,3,2,1,0:T(8,128)(2,1)S(1)}, u32[]{:S(2)}, u32[]{:S(2)}) collective-permute-start(bf16[2,2,2,32,1536]{4,3,2,1,0:T(8,128)(2,1)S(1)} %fusion.32), channel_id=1, source_target_pairs={{0,8},{4,12},{8,0},{12,4},{16,24},{20,28},{24,16},{28,20},{1,9},{5... | collective-permute-start | bytes 2359304 | tf_op jit(solution)/shard_map/ppermute | solution.py:135
  215.3 25.4 %collective-permute-start.25 = (bf16[2,2,2,16,1024]{4,3,2,1,0:T(8,128)(2,1)S(1)}, bf16[2,2,2,16,1024]{4,3,2,1,0:T(8,128)(2,1)S(1)}, u32[]{:S(2)}, u32[]{:S(2)}) collective-permute-start(bf16[2,2,2,16,1024]{4,3,2,1,0:T(8,128)(2,1)S(1)} %fusion.45), channel_id=1, source_target_pairs={{0,8},{4,12},{8,0},{12,4},{16,24},{20,28},{24,16},{28,20},{1,9},{5... | collective-permute-start | bytes 786440 | tf_op jit(solution)/shard_map/ppermute | solution.py:135
  219.2 26.5 %collective-permute-start.14 = (f32[1025]{0:T(1024)S(1)}, f32[1025]{0:T(1024)S(1)}, u32[]{:S(2)}, u32[]{:S(2)}) collective-permute-start(f32[1025]{0:T(1024)S(1)} %pad_maximum_fusion.4), channel_id=1, source_target_pairs={{0,4},{4,0},{8,12},{12,8},{16,20},{20,16},{24,28},{28,24},{1,5},{5... | collective-permute-start | bytes 12308 | tf_op jit(solution)/shard_map/ppermute | solution.py:135
  241.5 23.8 %collective-permute-start.26 = (bf16[2,2,16,1024]{3,2,1,0:T(8,128)(2,1)}, bf16[2,2,16,1024]{3,2,1,0:T(8,128)(2,1)}, u32[]{:S(2)}, u32[]{:S(2)}) collective-permute-start(bf16[2,2,16,1024]{3,2,1,0:T(8,128)(2,1)} %fusion.51), channel_id=1, source_target_pairs={{0,16},{4,20},{8,24},{12,28},{16,0},{20,4},{24,8},{28,12},{1,17},{... | collective-permute-start | bytes 393224 | tf_op jit(solution)/shard_map/ppermute | solution.py:135
  244.2 23.8 %collective-permute-start.21 = (bf16[2,2,32,1536]{3,2,1,0:T(8,128)(2,1)}, bf16[2,2,32,1536]{3,2,1,0:T(8,128)(2,1)S(1)}, u32[]{:S(2)}, u32[]{:S(2)}) collective-permute-start(bf16[2,2,32,1536]{3,2,1,0:T(8,128)(2,1)} %fusion.42), channel_id=1, source_target_pairs={{0,16},{4,20},{8,24},{12,28},{16,0},{20,4},{24,8},{28,12},{1,17},{... | collective-permute-start | bytes 1179656 | tf_op jit(solution)/shard_map/ppermute | solution.py:135
  246.4 3.7 %collective-permute-start.15 = (f32[1025]{0:T(1024)S(1)}, f32[1025]{0:T(1024)S(1)}, u32[]{:S(2)}, u32[]{:S(2)}) collective-permute-start(f32[1025]{0:T(1024)S(1)} %fusion.65), channel_id=1, source_target_pairs={{0,8},{4,12},{8,0},{12,4},{16,24},{20,28},{24,16},{28,20},{1,9},{5... | collective-permute-start | bytes 12308 | tf_op jit(solution)/shard_map/ppermute | solution.py:135
  250.1 5.2 %collective-permute-start.16 = (f32[1025]{0:T(1024)S(1)}, f32[1025]{0:T(1024)S(1)}, u32[]{:S(2)}, u32[]{:S(2)}) collective-permute-start(f32[1025]{0:T(1024)S(1)} %add.309), channel_id=1, source_target_pairs={{0,16},{4,20},{8,24},{12,28},{16,0},{20,4},{24,8},{28,12},{1,17},{... | collective-permute-start | bytes 12308 | tf_op jit(solution)/shard_map/ppermute | solution.py:135
  255.3 3.7 %collective-permute-start.17 = (f32[1025]{0:T(1024)S(1)}, f32[1025]{0:T(1024)S(1)}, u32[]{:S(2)}, u32[]{:S(2)}) collective-permute-start(f32[1025]{0:T(1024)S(1)} %add.310), channel_id=1, source_target_pairs={{0,1},{1,0},{2,3},{3,2},{4,5},{5,4},{6,7},{7,6},{8,9},{9,8},{10,11... | collective-permute-start | bytes 12308 | tf_op jit(solution)/shard_map/ppermute | solution.py:135
  258.9 4.5 %collective-permute-start.18 = (f32[1025]{0:T(1024)S(1)}, f32[1025]{0:T(1024)S(1)}, u32[]{:S(2)}, u32[]{:S(2)}) collective-permute-start(f32[1025]{0:T(1024)S(1)} %add.311), channel_id=1, source_target_pairs={{0,2},{1,3},{2,0},{3,1},{4,6},{5,7},{6,4},{7,5},{8,10},{9,11},{10,... | collective-permute-start | bytes 12308 | tf_op jit(solution)/shard_map/ppermute | solution.py:135
  266.3 4.9 %collective-permute-start.27 = (bf16[2,16,1024]{2,1,0:T(8,128)(2,1)S(1)}, bf16[2,16,1024]{2,1,0:T(8,128)(2,1)S(1)}, u32[]{:S(2)}, u32[]{:S(2)}) collective-permute-start(bf16[2,16,1024]{2,1,0:T(8,128)(2,1)S(1)} %fusion.59), channel_id=1, source_target_pairs={{0,1},{1,0},{2,3},{3,2},{4,5},{5,4},{6,7},{7,6},{8,9},{9,8},{10,11... | collective-permute-start | bytes 196616 | tf_op jit(solution)/shard_map/ppermute | solution.py:135
  269.2 7.1 %collective-permute-start.22 = (bf16[2,32,1536]{2,1,0:T(8,128)(2,1)S(1)}, bf16[2,32,1536]{2,1,0:T(8,128)(2,1)S(1)}, u32[]{:S(2)}, u32[]{:S(2)}) collective-permute-start(bf16[2,32,1536]{2,1,0:T(8,128)(2,1)S(1)} %fusion.50), channel_id=1, source_target_pairs={{0,1},{1,0},{2,3},{3,2},{4,5},{5,4},{6,7},{7,6},{8,9},{9,8},{10,11... | collective-permute-start | bytes 589832 | tf_op jit(solution)/shard_map/ppermute | solution.py:135
  271.2 6.5 %collective-permute-start.28 = (bf16[16,1024]{1,0:T(8,128)(2,1)S(1)}, bf16[16,1024]{1,0:T(8,128)(2,1)S(1)}, u32[]{:S(2)}, u32[]{:S(2)}) collective-permute-start(bf16[16,1024]{1,0:T(8,128)(2,1)S(1)} %fusion.61), channel_id=1, source_target_pairs={{0,2},{1,3},{2,0},{3,1},{4,6},{5,7},{6,4},{7,5},{8,10},{9,11},{10,... | collective-permute-start | bytes 98312 | tf_op jit(solution)/shard_map/ppermute | solution.py:135
  276.4 5.8 %collective-permute-start.23 = (bf16[32,1536]{1,0:T(8,128)(2,1)S(1)}, bf16[32,1536]{1,0:T(8,128)(2,1)S(1)}, u32[]{:S(2)}, u32[]{:S(2)}) collective-permute-start(bf16[32,1536]{1,0:T(8,128)(2,1)S(1)} %fusion.58), channel_id=1, source_target_pairs={{0,2},{1,3},{2,0},{3,1},{4,6},{5,7},{6,4},{7,5},{8,10},{9,11},{10,... | collective-permute-start | bytes 294920 | tf_op jit(solution)/shard_map/ppermute | solution.py:135
  (36 other events, 146.8 us)

commit v5 on v4

--- a/solution.py
+++ b/solution.py
@@ -188,21 +188,26 @@
     inner = w_out.shape[0]
     heads = inner // HEAD_DIM
     normed, hidden = layer_norm(tokens, ln_gain)
-    projected = jnp.dot(hidden, w_qkv, preferred_element_type=jnp.float32)
-    queries = projected[:, :inner].astype(jnp.bfloat16).reshape(rows, heads, HEAD_DIM)
-    pair_rows = projected[:, inner:].astype(jnp.bfloat16)
-    gathered = jnp.stack([pair_rows] + [shifted(pair_rows, "seq", step) for step in range(1, shards)])
-    split_kv = gathered.reshape(shards * rows, heads, 2, HEAD_DIM)
-    all_keys = split_kv[:, :, 0]
-    all_values = split_kv[:, :, 1]
-    scores = (
-        jnp.einsum("qhd,khd->hqk", queries, all_keys, preferred_element_type=jnp.float32) * 0.125
-    )
+    queries = (
+        jnp.dot(hidden, w_qkv[:, :inner], preferred_element_type=jnp.float32)
+        .astype(jnp.bfloat16)
+        .reshape(rows, heads, HEAD_DIM)
+        .transpose(1, 0, 2)
+    )
+    pair_cols = jnp.dot(w_qkv[:, inner:].T, hidden.T, preferred_element_type=jnp.float32).astype(
+        jnp.bfloat16
+    )
+    gathered = jnp.stack([pair_cols] + [shifted(pair_cols, "seq", step) for step in range(1, shards)])
+    split_kv = gathered.reshape(shards, heads, 2, HEAD_DIM, rows).transpose(1, 2, 3, 0, 4)
+    split_kv = split_kv.reshape(heads, 2, HEAD_DIM, shards * rows)
+    keys_t = split_kv[:, 0]
+    values_t = split_kv[:, 1]
+    scores = jnp.einsum("hqd,hdk->hqk", queries, keys_t, preferred_element_type=jnp.float32) * 0.125
     row_max = jnp.max(scores, axis=2)
     weights = jnp.exp(scores - row_max[:, :, None])
     row_sum = jnp.sum(weights, axis=2)
     blended = jnp.einsum(
-        "hqk,khd->hqd", weights.astype(jnp.bfloat16), all_values, preferred_element_type=jnp.float32
+        "hqk,hdk->hqd", weights.astype(jnp.bfloat16), values_t, preferred_element_type=jnp.float32
     )
     log_total = row_max + jnp.log(row_sum)
     attended = (
@@ -218,29 +223,27 @@
         jnp.dot(grad_b, w_out.T, preferred_element_type=jnp.float32)
         .astype(jnp.bfloat16)
         .reshape(rows, heads, HEAD_DIM)
+        .transpose(1, 0, 2)
     )
     row_dot = jnp.sum(
         grad_heads.astype(jnp.float32)
-        * attended.reshape(rows, heads, HEAD_DIM).astype(jnp.float32),
+        * attended.reshape(rows, heads, HEAD_DIM).transpose(1, 0, 2).astype(jnp.float32),
         axis=2,
-    ).T
+    )
     prob_full = jnp.exp(scores - log_total[:, :, None])
-    d_value = jnp.einsum(
-        "hqk,qhd->khd", prob_full.astype(jnp.bfloat16), grad_heads, preferred_element_type=jnp.float32
-    )
-    d_prob = jnp.einsum(
-        "qhd,khd->hqk", grad_heads, all_values, preferred_element_type=jnp.float32
-    )
+    d_value_t = jnp.einsum(
+        "hqd,hqk->hdk", grad_heads, prob_full.astype(jnp.bfloat16), preferred_element_type=jnp.float32
+    )
+    d_prob = jnp.einsum("hqd,hdk->hqk", grad_heads, values_t, preferred_element_type=jnp.float32)
     d_score = (prob_full * (d_prob - row_dot[:, :, None])).astype(jnp.bfloat16)
-    d_query = 0.125 * jnp.einsum(
-        "hqk,khd->qhd", d_score, all_keys, preferred_element_type=jnp.float32
-    )
-    d_key = 0.125 * jnp.einsum("hqk,qhd->khd", d_score, queries, preferred_element_type=jnp.float32)
-    d_pairs = jnp.stack([d_key, d_value], axis=2).reshape(shards, rows, 2 * inner)
+    d_query = 0.125 * jnp.einsum("hqk,hdk->qhd", d_score, keys_t, preferred_element_type=jnp.float32)
+    d_key_t = 0.125 * jnp.einsum("hqd,hqk->hdk", queries, d_score, preferred_element_type=jnp.float32)
+    d_pairs = jnp.stack([d_key_t, d_value_t], axis=1).reshape(heads, 2, HEAD_DIM, shards, rows)
+    d_pairs = d_pairs.transpose(3, 0, 1, 2, 4).reshape(shards, 2 * inner, rows)
     accum = d_pairs[0]
     for step in range(1, shards):
         accum = accum + shifted(d_pairs[step].astype(jnp.bfloat16), "seq", -step).astype(jnp.float32)
-    d_proj = jnp.concatenate([d_query.reshape(rows, inner), accum], axis=1).astype(jnp.bfloat16)
+    d_proj = jnp.concatenate([d_query.reshape(rows, inner), accum.T], axis=1).astype(jnp.bfloat16)
     grad_wqkv = jnp.dot(exchange_order(hidden).T, d_proj, preferred_element_type=jnp.float32)
     d_hidden = jnp.dot(d_proj, w_qkv.T, preferred_element_type=jnp.float32)
     grad_ln = jnp.sum(d_hidden * normed, axis=0)

time: 286 us -> 222 us (0.78)
  local copies, waits for them, and re-layouts: 120 us -> 52.8 us
  waiting for transfers between devices: 69.2 us -> 77.8 us
  other arithmetic: 27.3 us -> 19.3 us
    unnamed x87 -> x69, local copies, waits for them, and re-layouts: 44 us -> 11 us
    slice x4 -> x0, local copies, waits for them, and re-layouts: 13.2 us -> none  [the longest x1 9.82 us: per_device(): all_values = split_kv[:, :, 1]]
    slice x8 -> x1, local copies, waits for them, and re-layouts: 11.1 us -> 1.21 us  [per_device(): d_pairs[step].astype(jnp.bfloat16)]
    ppermute x0 -> x7, local copies, waits for them, and re-layouts: none -> 7.82 us  [shifted(): return lax.ppermute(value, axis, pairs)]
    reshape x1, local copies, waits for them, and re-layouts: 8.85 us -> 2.82 us  [per_device(): split_kv = split_kv.reshape(heads, 2, HEAD_DIM, shards * rows)]
    ppermute x14, waiting for transfers between devices: 19.9 us -> 24.6 us  [shifted(): return lax.ppermute(value, axis, pairs)]
    transpose x0 -> x2, other arithmetic: none -> 4.34 us  [the longest x1 2.58 us: per_device(): d_pairs = d_pairs.transpose(3, 0, 1, 2, 4).reshape(shards, 2 * inner, rows)]
    another operation x4 -> x2, other arithmetic: 3.55 us -> 0.42 us
  transfers between devices with their start and end apart: 31 -> 31, of which waited for: 14 -> 15; matrix products, arithmetic and copies ran while one was open for 22% -> 18% of each run, Pallas kernels for 0% -> 0%
where the time goes in v5:
time: 222 us; the launch traced here: 221 us
  waiting for transfers between devices  77.8 us (35%)
  local copies, waits for them, and re-layouts  52.8 us (24%)
  starting transfers between devices  41 us (18%)
  other arithmetic  19.3 us (9%)
  matrix products  17.7 us (8%)
  blocking collectives  9.46 us (4%)
  between operations  3.32 us (1%)
    ppermute x15, waiting for transfers between devices, halving_scatter(): lax.ppermute((give_a.astype(jnp.bfloat16), give_b.astype(jnp.bfloat16), s...  45.2 us
    ppermute x14, waiting for transfers between devices, shifted(): return lax.ppermute(value, axis, pairs)  24.6 us
    ppermute x14, starting transfers between devices, shifted(): return lax.ppermute(value, axis, pairs)  17.7 us
    ppermute x15, starting transfers between devices, halving_scatter(): lax.ppermute((give_a.astype(jnp.bfloat16), give_b.astype(jnp.bfloat16), s...  16.4 us
    convert_element_type x7, local copies, waits for them, and re-layouts, per_device(): d_pairs[step].astype(jnp.bfloat16)  11.6 us
    unnamed x69, local copies, waits for them, and re-layouts  11 us
    unnamed x1, blocking collectives  9.46 us
    all_to_all x1, waiting for transfers between devices, per_device(): lax.all_to_all(send_tokens, 'seq', split_axis=0, concat_axis=0, tiled=True)  8 us
  transfers between devices with their start and end apart: 31, of which 15 were waited for; matrix products, arithmetic and copies ran while one was open for 18% of the time, Pallas kernels for 0%

profile of v5, /device:TPU:0, one launch (start us, length us, event | category | flops | bytes accessed | tf_op | source)
XLA Modules:
  0.0 221.3 jit_solution(11836846071213673389)
XLA Ops:
  5.5 9.5 %all-reduce = s32[8]{0:T(128)S(1)} all-reduce(s32[8]{0:T(128)S(1)} %dynamic-update-slice), channel_id=1, replica_groups=mesh['seq'=8,'clip'=4] {'seq'}, use_global_device_ids=true, to_apply=%add | all-reduce | flops 8 | bytes 64
  22.5 3.5 %all-to-all-start = ((bf16[8,24,1024]{2,1,0:T(8,128)(2,1)}), bf16[8,24,1024]{2,1,0:T(8,128)(2,1)S(1)}, u32[]{:S(2)}, u32[]{:S(2)}) async-start(bf16[8,24,1024]{2,1,0:T(8,128)(2,1)} %get-tuple-element.16), calls=%async_computation | async-start | bytes 786432 | tf_op jit(solution)/shard_map/all_to_all | solution.py:170
  26.3 8.0 %all-to-all-done = bf16[8,24,1024]{2,1,0:T(8,128)(2,1)S(1)} async-done(((bf16[8,24,1024]{2,1,0:T(8,128)(2,1)}), bf16[8,24,1024]{2,1,0:T(8,128)(2,1)S(1)}, u32[]{:S(2)}, u32[]{:S(2)}) %all-to-all-start) | async-done | bytes 393248 | tf_op jit(solution)/shard_map/all_to_all | solution.py:170
  34.3 3.5 %all-to-all-start.1 = ((bf16[8,24,1024]{2,1,0:T(8,128)(2,1)}), bf16[8,24,1024]{2,1,0:T(8,128)(2,1)S(1)}, u32[]{:S(2)}, u32[]{:S(2)}) async-start(bf16[8,24,1024]{2,1,0:T(8,128)(2,1)} %get-tuple-element.15), calls=%async_computation.1 | async-start | bytes 786432 | tf_op jit(solution)/shard_map/all_to_all | solution.py:171
  39.8 2.8 %fusion.18 = bf16[1024,128]{0,1:T(8,128)(2,1)} fusion(bf16[128,1024]{1,0:T(8,128)(2,1)S(1)} %fusion.28, bf16[1024,1536]{1,0:T(8,128)(2,1)} %param.9), kind=kOutput, calls=%fused_computation.32 | convolution fusion | flops 268566528 | bytes 2621440 | tf_op jit(solution)/shard_map/dot_general | solution.py:197
  43.8 2.7 %collective-permute-start.6 = (bf16[1024,128]{0,1:T(8,128)(2,1)}, bf16[1024,128]{0,1:T(8,128)(2,1)}, u32[]{:S(2)}, u32[]{:S(2)}) collective-permute-start(bf16[1024,128]{0,1:T(8,128)(2,1)} %fusion.18), channel_id=1, source_target_pairs={{0,28},{4,0},{8,4},{12,8},{16,12},{20,16},{24,20},{28,24},{1,29},{... | collective-permute-start | bytes 786440 | tf_op jit(solution)/shard_map/ppermute | solution.py:13
  52.4 10.8 %collective-permute-done.1 = bf16[1024,128]{0,1:T(8,128)(2,1)} collective-permute-done((bf16[1024,128]{0,1:T(8,128)(2,1)}, bf16[1024,128]{0,1:T(8,128)(2,1)}, u32[]{:S(2)}, u32[]{:S(2)}) %collective-permute-start.1) | collective-permute-done | bytes 262176 | tf_op jit(solution)/shard_map/ppermute | solution.py:13
  63.2 2.2 collective-permute-start.5
  75.6 3.1 %copy.30 = bf16[8,2,64,8,128]{4,3,2,0,1:T(8,128)(2,1)} copy(bf16[8,2,64,8,128]{4,2,1,0,3:T(8,128)(2,1)S(1)} %bitcast.180) | data formatting | bytes 4194304 | tf_op jit(solution)/shard_map/transpose | solution.py:201
  78.7 2.8 %reshape.427 = bf16[8,2,64,1024]{3,2,0,1:T(8,128)(2,1)S(1)} reshape(bf16[8,2,64,8,128]{4,3,2,0,1:T(8,128)(2,1)} %copy.30) | data formatting | bytes 4194304 | tf_op jit(solution)/shard_map/reshape | solution.py:202
  88.6 3.3 %fusion.3 = f32[8,64,1024]{2,1,0:T(8,128)S(1)} fusion(bf16[8,128,64]{1,2,0:T(8,128)(2,1)S(1)} %bitcast.181, f32[8,128,1024]{2,1,0:T(8,128)} %copy-done.2, f32[8,128]{1,0:T(8,128)S(1)} %log_add_fusion), kind=kOutput, calls=%fused_computation.16 | convolution fusion | flops 137363456 | bytes 6426624 | tf_op jit(solution)/shard_map/hqd,hqk->hdk/dot_general | solution.py:234
  101.0 3.4 %collective-permute-start.8 = (bf16[1024,128]{0,1:T(8,128)(2,1)}, bf16[1024,128]{0,1:T(8,128)(2,1)}, u32[]{:S(2)}, u32[]{:S(2)}) collective-permute-start(bf16[1024,128]{0,1:T(8,128)(2,1)} %copy.37), channel_id=1, source_target_pairs={{0,24},{4,28},{8,0},{12,4},{16,8},{20,12},{24,16},{28,20},{1,25},{... | collective-permute-start | bytes 786440 | tf_op jit(solution)/shard_map/ppermute | solution.py:13
  104.5 1.8 copy.38
  109.7 1.8 copy.35
  113.3 1.8 copy.41
  120.5 2.6 %collective-permute-start.7 = (bf16[1024,128]{0,1:T(8,128)(2,1)}, bf16[1024,128]{0,1:T(8,128)(2,1)}, u32[]{:S(2)}, u32[]{:S(2)}) collective-permute-start(bf16[1024,128]{0,1:T(8,128)(2,1)} %copy.35), channel_id=1, source_target_pairs={{0,28},{4,0},{8,4},{12,8},{16,12},{20,16},{24,20},{28,24},{1,29},{... | collective-permute-start | bytes 786440 | tf_op jit(solution)/shard_map/ppermute | solution.py:13
  123.1 2.1 fusion.21
  125.3 2.6 %maximum_bitcast_fusion = f32[8,8,2,64,128]{4,3,2,1,0:T(8,128)S(1)} fusion(f32[8,1,64,8,128]{4,2,1,0,3:T(8,128)} %copy-done.6, f32[8,1,64,8,128]{4,2,1,0,3:T(8,128)} %copy-done.5), kind=kLoop, calls=%fused_computation.6 | loop fusion | flops 1048576 | bytes 8388608 | tf_op jit(solution)/shard_map/transpose | solution.py:242
  128.1 10.3 %collective-permute-done.10 = bf16[1024,128]{0,1:T(8,128)(2,1)} collective-permute-done((bf16[1024,128]{0,1:T(8,128)(2,1)}, bf16[1024,128]{0,1:T(8,128)(2,1)}, u32[]{:S(2)}, u32[]{:S(2)}) %collective-permute-start.10) | collective-permute-done | bytes 262176 | tf_op jit(solution)/shard_map/ppermute | solution.py:13
  143.0 2.6 %copy-done.4 = f32[2,2,2,2,2,32,1536]{6,5,4,3,2,1,0:T(8,128)} copy-done((f32[2,2,2,2,2,32,1536]{6,5,4,3,2,1,0:T(8,128)}, f32[2,2,2,2,2,32,1536]{6,5,4,3,2,1,0:T(8,128)S(1)}, u32[]{:S(2)}) %copy-start.4) | copy-done | bytes 6291480
  148.3 3.0 %collective-permute-done.24 = bf16[2,2,2,2,16,1024]{5,4,3,2,1,0:T(8,128)(2,1)} collective-permute-done((bf16[2,2,2,2,16,1024]{5,4,3,2,1,0:T(8,128)(2,1)S(1)}, bf16[2,2,2,2,16,1024]{5,4,3,2,1,0:T(8,128)(2,1)}, u32[]{:S(2)}, u32[]{:S(2)}) %collective-permute-start.24) | collective-permute-done | bytes 524320 | tf_op jit(solution)/shard_map/ppermute | solution.py:135
  152.6 3.0 %bitcast_add_fusion = f32[2,2,2,2,32,1536]{5,4,3,2,1,0:T(8,128)S(1)} fusion(bf16[2,2,2,2,32,1536]{5,4,3,2,1,0:T(8,128)(2,1)} %collective-permute-done.19, f32[2,2,2,2,2,32,1536]{6,5,4,3,2,1,0:T(8,128)} %copy-done.4, s32[]{:T(128)S(6)} %select_n.145), kind=kLoop, calls=%fused_computation.14 | loop fusion | flops 1572864 | bytes 7864324 | tf_op jit(solution)/shard_map/add | solution.py:138
  155.9 2.1 collective-permute-start.25
  159.8 21.2 %collective-permute-done.25 = bf16[2,2,2,16,1024]{4,3,2,1,0:T(8,128)(2,1)S(1)} collective-permute-done((bf16[2,2,2,16,1024]{4,3,2,1,0:T(8,128)(2,1)S(1)}, bf16[2,2,2,16,1024]{4,3,2,1,0:T(8,128)(2,1)S(1)}, u32[]{:S(2)}, u32[]{:S(2)}) %collective-permute-start.25) | collective-permute-done | bytes 262176 | tf_op jit(solution)/shard_map/ppermute | solution.py:135
  184.6 3.4 %collective-permute-done.15 = f32[1025]{0:T(1024)S(1)} collective-permute-done((f32[1025]{0:T(1024)S(1)}, f32[1025]{0:T(1024)S(1)}, u32[]{:S(2)}, u32[]{:S(2)}) %collective-permute-start.15) | collective-permute-done | bytes 4132 | tf_op jit(solution)/shard_map/ppermute | solution.py:135
  188.4 6.1 %collective-permute-done.16 = f32[1025]{0:T(1024)S(1)} collective-permute-done((f32[1025]{0:T(1024)S(1)}, f32[1025]{0:T(1024)S(1)}, u32[]{:S(2)}, u32[]{:S(2)}) %collective-permute-start.16) | collective-permute-done | bytes 4132 | tf_op jit(solution)/shard_map/ppermute | solution.py:135
  196.1 2.1 collective-permute-done.17
  198.1 2.6 %collective-permute-start.18 = (f32[1025]{0:T(1024)S(1)}, f32[1025]{0:T(1024)S(1)}, u32[]{:S(2)}, u32[]{:S(2)}) collective-permute-start(f32[1025]{0:T(1024)S(1)} %add.311), channel_id=1, source_target_pairs={{0,2},{1,3},{2,0},{3,1},{4,6},{5,7},{6,4},{7,5},{8,10},{9,11},{10,... | collective-permute-start | bytes 12308 | tf_op jit(solution)/shard_map/ppermute | solution.py:135
  200.7 2.0 collective-permute-done.18
  206.8 2.0 collective-permute-done.27
  208.9 2.7 %collective-permute-start.28 = (bf16[16,1024]{1,0:T(8,128)(2,1)S(1)}, bf16[16,1024]{1,0:T(8,128)(2,1)S(1)}, u32[]{:S(2)}, u32[]{:S(2)}) collective-permute-start(bf16[16,1024]{1,0:T(8,128)(2,1)S(1)} %fusion.54), channel_id=1, source_target_pairs={{0,2},{1,3},{2,0},{3,1},{4,6},{5,7},{6,4},{7,5},{8,10},{9,11},{10,... | collective-permute-start | bytes 98312 | tf_op jit(solution)/shard_map/ppermute | solution.py:135
  215.5 4.0 %collective-permute-done.23 = bf16[32,1536]{1,0:T(8,128)(2,1)S(1)} collective-permute-done((bf16[32,1536]{1,0:T(8,128)(2,1)S(1)}, bf16[32,1536]{1,0:T(8,128)(2,1)S(1)}, u32[]{:S(2)}, u32[]{:S(2)}) %collective-permute-start.23) | collective-permute-done | bytes 98336 | tf_op jit(solution)/shard_map/ppermute | solution.py:135
  (207 shorter events, 82.6 us)
Async XLA Ops:
  21.5 18.0 %copy-start.16 = (f32[1024]{0:T(1024)S(1)}, f32[1024]{0:T(1024)}, u32[]{:S(2)}) copy-start(f32[1024]{0:T(1024)} %param.11) | copy-start | bytes 12292
  22.5 11.7 %all-to-all-start = ((bf16[8,24,1024]{2,1,0:T(8,128)(2,1)}), bf16[8,24,1024]{2,1,0:T(8,128)(2,1)S(1)}, u32[]{:S(2)}, u32[]{:S(2)}) async-start(bf16[8,24,1024]{2,1,0:T(8,128)(2,1)} %get-tuple-element.16), calls=%async_computation | async-start | bytes 786432 | tf_op jit(solution)/shard_map/all_to_all | solution.py:170
  34.3 15.9 %all-to-all-start.1 = ((bf16[8,24,1024]{2,1,0:T(8,128)(2,1)}), bf16[8,24,1024]{2,1,0:T(8,128)(2,1)S(1)}, u32[]{:S(2)}, u32[]{:S(2)}) async-start(bf16[8,24,1024]{2,1,0:T(8,128)(2,1)} %get-tuple-element.15), calls=%async_computation.1 | async-start | bytes 786432 | tf_op jit(solution)/shard_map/all_to_all | solution.py:171
  43.8 30.6 %collective-permute-start.6 = (bf16[1024,128]{0,1:T(8,128)(2,1)}, bf16[1024,128]{0,1:T(8,128)(2,1)}, u32[]{:S(2)}, u32[]{:S(2)}) collective-permute-start(bf16[1024,128]{0,1:T(8,128)(2,1)} %fusion.18), channel_id=1, source_target_pairs={{0,28},{4,0},{8,4},{12,8},{16,12},{20,16},{24,20},{28,24},{1,29},{... | collective-permute-start | bytes 786440 | tf_op jit(solution)/shard_map/ppermute | solution.py:13
  46.4 21.6 %collective-permute-start.3 = (bf16[1024,128]{0,1:T(8,128)(2,1)}, bf16[1024,128]{0,1:T(8,128)(2,1)}, u32[]{:S(2)}, u32[]{:S(2)}) collective-permute-start(bf16[1024,128]{0,1:T(8,128)(2,1)} %fusion.18), channel_id=1, source_target_pairs={{0,16},{4,20},{8,24},{12,28},{16,0},{20,4},{24,8},{28,12},{1,17},{... | collective-permute-start | bytes 786440 | tf_op jit(solution)/shard_map/ppermute | solution.py:13
  47.0 22.2 %collective-permute-start.2 = (bf16[1024,128]{0,1:T(8,128)(2,1)}, bf16[1024,128]{0,1:T(8,128)(2,1)}, u32[]{:S(2)}, u32[]{:S(2)}) collective-permute-start(bf16[1024,128]{0,1:T(8,128)(2,1)} %fusion.18), channel_id=1, source_target_pairs={{0,12},{4,16},{8,20},{12,24},{16,28},{20,0},{24,4},{28,8},{1,13},{... | collective-permute-start | bytes 786440 | tf_op jit(solution)/shard_map/ppermute | solution.py:13
  47.1 16.1 %collective-permute-start.1 = (bf16[1024,128]{0,1:T(8,128)(2,1)}, bf16[1024,128]{0,1:T(8,128)(2,1)}, u32[]{:S(2)}, u32[]{:S(2)}) collective-permute-start(bf16[1024,128]{0,1:T(8,128)(2,1)} %fusion.18), channel_id=1, source_target_pairs={{0,8},{4,12},{8,16},{12,20},{16,24},{20,28},{24,0},{28,4},{1,9},{5... | collective-permute-start | bytes 786440 | tf_op jit(solution)/shard_map/ppermute | solution.py:13
  47.6 19.0 %collective-permute-start = (bf16[1024,128]{0,1:T(8,128)(2,1)}, bf16[1024,128]{0,1:T(8,128)(2,1)}, u32[]{:S(2)}, u32[]{:S(2)}) collective-permute-start(bf16[1024,128]{0,1:T(8,128)(2,1)} %fusion.18), channel_id=1, source_target_pairs={{0,4},{4,8},{8,12},{12,16},{16,20},{20,24},{24,28},{28,0},{1,5},{5... | collective-permute-start | bytes 786440 | tf_op jit(solution)/shard_map/ppermute | solution.py:13
  63.2 8.5 %collective-permute-start.5 = (bf16[1024,128]{0,1:T(8,128)(2,1)}, bf16[1024,128]{0,1:T(8,128)(2,1)}, u32[]{:S(2)}, u32[]{:S(2)}) collective-permute-start(bf16[1024,128]{0,1:T(8,128)(2,1)} %fusion.18), channel_id=1, source_target_pairs={{0,24},{4,28},{8,0},{12,4},{16,8},{20,12},{24,16},{28,20},{1,25},{... | collective-permute-start | bytes 786440 | tf_op jit(solution)/shard_map/ppermute | solution.py:13
  66.5 6.6 %collective-permute-start.4 = (bf16[1024,128]{0,1:T(8,128)(2,1)}, bf16[1024,128]{0,1:T(8,128)(2,1)}, u32[]{:S(2)}, u32[]{:S(2)}) collective-permute-start(bf16[1024,128]{0,1:T(8,128)(2,1)} %fusion.18), channel_id=1, source_target_pairs={{0,20},{4,24},{8,28},{12,0},{16,4},{20,8},{24,12},{28,16},{1,21},{... | collective-permute-start | bytes 786440 | tf_op jit(solution)/shard_map/ppermute | solution.py:13
  101.0 19.4 %collective-permute-start.8 = (bf16[1024,128]{0,1:T(8,128)(2,1)}, bf16[1024,128]{0,1:T(8,128)(2,1)}, u32[]{:S(2)}, u32[]{:S(2)}) collective-permute-start(bf16[1024,128]{0,1:T(8,128)(2,1)} %copy.37), channel_id=1, source_target_pairs={{0,24},{4,28},{8,0},{12,4},{16,8},{20,12},{24,16},{28,20},{1,25},{... | collective-permute-start | bytes 786440 | tf_op jit(solution)/shard_map/ppermute | solution.py:13
  106.3 14.2 %collective-permute-start.9 = (bf16[1024,128]{0,1:T(8,128)(2,1)}, bf16[1024,128]{0,1:T(8,128)(2,1)}, u32[]{:S(2)}, u32[]{:S(2)}) collective-permute-start(bf16[1024,128]{0,1:T(8,128)(2,1)} %copy.38), channel_id=1, source_target_pairs={{0,20},{4,24},{8,28},{12,0},{16,4},{20,8},{24,12},{28,16},{1,21},{... | collective-permute-start | bytes 786440 | tf_op jit(solution)/shard_map/ppermute | solution.py:13
  117.7 20.7 %collective-permute-start.10 = (bf16[1024,128]{0,1:T(8,128)(2,1)}, bf16[1024,128]{0,1:T(8,128)(2,1)}, u32[]{:S(2)}, u32[]{:S(2)}) collective-permute-start(bf16[1024,128]{0,1:T(8,128)(2,1)} %copy.39), channel_id=1, source_target_pairs={{0,16},{4,20},{8,24},{12,28},{16,0},{20,4},{24,8},{28,12},{1,17},{... | collective-permute-start | bytes 786440 | tf_op jit(solution)/shard_map/ppermute | solution.py:13
  119.3 20.9 %collective-permute-start.11 = (bf16[1024,128]{0,1:T(8,128)(2,1)}, bf16[1024,128]{0,1:T(8,128)(2,1)}, u32[]{:S(2)}, u32[]{:S(2)}) collective-permute-start(bf16[1024,128]{0,1:T(8,128)(2,1)} %copy.40), channel_id=1, source_target_pairs={{0,12},{4,16},{8,20},{12,24},{16,28},{20,0},{24,4},{28,8},{1,13},{... | collective-permute-start | bytes 786440 | tf_op jit(solution)/shard_map/ppermute | solution.py:13
  119.3 20.9 %collective-permute-start.12 = (bf16[1024,128]{0,1:T(8,128)(2,1)}, bf16[1024,128]{0,1:T(8,128)(2,1)}, u32[]{:S(2)}, u32[]{:S(2)}) collective-permute-start(bf16[1024,128]{0,1:T(8,128)(2,1)} %copy.41), channel_id=1, source_target_pairs={{0,8},{4,12},{8,16},{12,20},{16,24},{20,28},{24,0},{28,4},{1,9},{5... | collective-permute-start | bytes 786440 | tf_op jit(solution)/shard_map/ppermute | solution.py:13
  120.5 19.8 %collective-permute-start.13 = (bf16[1024,128]{0,1:T(8,128)(2,1)}, bf16[1024,128]{0,1:T(8,128)(2,1)}, u32[]{:S(2)}, u32[]{:S(2)}) collective-permute-start(bf16[1024,128]{0,1:T(8,128)(2,1)} %copy.42), channel_id=1, source_target_pairs={{0,4},{4,8},{8,12},{12,16},{16,20},{20,24},{24,28},{28,0},{1,5},{5... | collective-permute-start | bytes 786440 | tf_op jit(solution)/shard_map/ppermute | solution.py:13
  120.5 19.8 %collective-permute-start.7 = (bf16[1024,128]{0,1:T(8,128)(2,1)}, bf16[1024,128]{0,1:T(8,128)(2,1)}, u32[]{:S(2)}, u32[]{:S(2)}) collective-permute-start(bf16[1024,128]{0,1:T(8,128)(2,1)} %copy.35), channel_id=1, source_target_pairs={{0,28},{4,0},{8,4},{12,8},{16,12},{20,16},{24,20},{28,24},{1,29},{... | collective-permute-start | bytes 786440 | tf_op jit(solution)/shard_map/ppermute | solution.py:13
  147.1 5.5 %collective-permute-start.19 = (bf16[2,2,2,2,32,1536]{5,4,3,2,1,0:T(8,128)(2,1)}, bf16[2,2,2,2,32,1536]{5,4,3,2,1,0:T(8,128)(2,1)}, u32[]{:S(2)}, u32[]{:S(2)}) collective-permute-start(bf16[2,2,2,2,32,1536]{5,4,3,2,1,0:T(8,128)(2,1)} %fusion.13), channel_id=1, source_target_pairs={{0,4},{4,0},{8,12},{12,8},{16,20},{20,16},{24,28},{28,24},{1,5},{5... | collective-permute-start | bytes 4718600 | tf_op jit(solution)/shard_map/ppermute | solution.py:135
  147.8 3.6 %collective-permute-start.24 = (bf16[2,2,2,2,16,1024]{5,4,3,2,1,0:T(8,128)(2,1)S(1)}, bf16[2,2,2,2,16,1024]{5,4,3,2,1,0:T(8,128)(2,1)}, u32[]{:S(2)}, u32[]{:S(2)}) collective-permute-start(bf16[2,2,2,2,16,1024]{5,4,3,2,1,0:T(8,128)(2,1)S(1)} %fusion.32), channel_id=1, source_target_pairs={{0,4},{4,0},{8,12},{12,8},{16,20},{20,16},{24,28},{28,24},{1,5},{5... | collective-permute-start | bytes 1572872 | tf_op jit(solution)/shard_map/ppermute | solution.py:135
  155.7 25.9 %collective-permute-start.20 = (bf16[2,2,2,32,1536]{4,3,2,1,0:T(8,128)(2,1)S(1)}, bf16[2,2,2,32,1536]{4,3,2,1,0:T(8,128)(2,1)S(1)}, u32[]{:S(2)}, u32[]{:S(2)}) collective-permute-start(bf16[2,2,2,32,1536]{4,3,2,1,0:T(8,128)(2,1)S(1)} %fusion.24), channel_id=1, source_target_pairs={{0,8},{4,12},{8,0},{12,4},{16,24},{20,28},{24,16},{28,20},{1,9},{5... | collective-permute-start | bytes 2359304 | tf_op jit(solution)/shard_map/ppermute | solution.py:135
  155.9 25.1 %collective-permute-start.25 = (bf16[2,2,2,16,1024]{4,3,2,1,0:T(8,128)(2,1)S(1)}, bf16[2,2,2,16,1024]{4,3,2,1,0:T(8,128)(2,1)S(1)}, u32[]{:S(2)}, u32[]{:S(2)}) collective-permute-start(bf16[2,2,2,16,1024]{4,3,2,1,0:T(8,128)(2,1)S(1)} %fusion.37), channel_id=1, source_target_pairs={{0,8},{4,12},{8,0},{12,4},{16,24},{20,28},{24,16},{28,20},{1,9},{5... | collective-permute-start | bytes 786440 | tf_op jit(solution)/shard_map/ppermute | solution.py:135
  159.8 23.8 %collective-permute-start.14 = (f32[1025]{0:T(1024)S(1)}, f32[1025]{0:T(1024)S(1)}, u32[]{:S(2)}, u32[]{:S(2)}) collective-permute-start(f32[1025]{0:T(1024)S(1)} %pad_maximum_fusion.3), channel_id=1, source_target_pairs={{0,4},{4,0},{8,12},{12,8},{16,20},{20,16},{24,28},{28,24},{1,5},{5... | collective-permute-start | bytes 12308 | tf_op jit(solution)/shard_map/ppermute | solution.py:135
  181.1 23.4 %collective-permute-start.26 = (bf16[2,2,16,1024]{3,2,1,0:T(8,128)(2,1)S(1)}, bf16[2,2,16,1024]{3,2,1,0:T(8,128)(2,1)S(1)}, u32[]{:S(2)}, u32[]{:S(2)}) collective-permute-start(bf16[2,2,16,1024]{3,2,1,0:T(8,128)(2,1)S(1)} %fusion.44), channel_id=1, source_target_pairs={{0,16},{4,20},{8,24},{12,28},{16,0},{20,4},{24,8},{28,12},{1,17},{... | collective-permute-start | bytes 393224 | tf_op jit(solution)/shard_map/ppermute | solution.py:135
  181.9 24.3 %collective-permute-start.21 = (bf16[2,2,32,1536]{3,2,1,0:T(8,128)(2,1)S(1)}, bf16[2,2,32,1536]{3,2,1,0:T(8,128)(2,1)S(1)}, u32[]{:S(2)}, u32[]{:S(2)}) collective-permute-start(bf16[2,2,32,1536]{3,2,1,0:T(8,128)(2,1)S(1)} %fusion.33), channel_id=1, source_target_pairs={{0,16},{4,20},{8,24},{12,28},{16,0},{20,4},{24,8},{28,12},{1,17},{... | collective-permute-start | bytes 1179656 | tf_op jit(solution)/shard_map/ppermute | solution.py:135
  184.2 3.7 %collective-permute-start.15 = (f32[1025]{0:T(1024)S(1)}, f32[1025]{0:T(1024)S(1)}, u32[]{:S(2)}, u32[]{:S(2)}) collective-permute-start(f32[1025]{0:T(1024)S(1)} %fusion.58), channel_id=1, source_target_pairs={{0,8},{4,12},{8,0},{12,4},{16,24},{20,28},{24,16},{28,20},{1,9},{5... | collective-permute-start | bytes 12308 | tf_op jit(solution)/shard_map/ppermute | solution.py:135
  187.9 6.6 %collective-permute-start.16 = (f32[1025]{0:T(1024)S(1)}, f32[1025]{0:T(1024)S(1)}, u32[]{:S(2)}, u32[]{:S(2)}) collective-permute-start(f32[1025]{0:T(1024)S(1)} %add.309), channel_id=1, source_target_pairs={{0,16},{4,20},{8,24},{12,28},{16,0},{20,4},{24,8},{28,12},{1,17},{... | collective-permute-start | bytes 12308 | tf_op jit(solution)/shard_map/ppermute | solution.py:135
  194.5 3.7 %collective-permute-start.17 = (f32[1025]{0:T(1024)S(1)}, f32[1025]{0:T(1024)S(1)}, u32[]{:S(2)}, u32[]{:S(2)}) collective-permute-start(f32[1025]{0:T(1024)S(1)} %add.310), channel_id=1, source_target_pairs={{0,1},{1,0},{2,3},{3,2},{4,5},{5,4},{6,7},{7,6},{8,9},{9,8},{10,11... | collective-permute-start | bytes 12308 | tf_op jit(solution)/shard_map/ppermute | solution.py:135
  198.1 4.5 %collective-permute-start.18 = (f32[1025]{0:T(1024)S(1)}, f32[1025]{0:T(1024)S(1)}, u32[]{:S(2)}, u32[]{:S(2)}) collective-permute-start(f32[1025]{0:T(1024)S(1)} %add.311), channel_id=1, source_target_pairs={{0,2},{1,3},{2,0},{3,1},{4,6},{5,7},{6,4},{7,5},{8,10},{9,11},{10,... | collective-permute-start | bytes 12308 | tf_op jit(solution)/shard_map/ppermute | solution.py:135
  204.5 4.3 %collective-permute-start.27 = (bf16[2,16,1024]{2,1,0:T(8,128)(2,1)S(1)}, bf16[2,16,1024]{2,1,0:T(8,128)(2,1)S(1)}, u32[]{:S(2)}, u32[]{:S(2)}) collective-permute-start(bf16[2,16,1024]{2,1,0:T(8,128)(2,1)S(1)} %fusion.52), channel_id=1, source_target_pairs={{0,1},{1,0},{2,3},{3,2},{4,5},{5,4},{6,7},{7,6},{8,9},{9,8},{10,11... | collective-permute-start | bytes 196616 | tf_op jit(solution)/shard_map/ppermute | solution.py:135
  206.3 6.8 %collective-permute-start.22 = (bf16[2,32,1536]{2,1,0:T(8,128)(2,1)S(1)}, bf16[2,32,1536]{2,1,0:T(8,128)(2,1)S(1)}, u32[]{:S(2)}, u32[]{:S(2)}) collective-permute-start(bf16[2,32,1536]{2,1,0:T(8,128)(2,1)S(1)} %fusion.43), channel_id=1, source_target_pairs={{0,1},{1,0},{2,3},{3,2},{4,5},{5,4},{6,7},{7,6},{8,9},{9,8},{10,11... | collective-permute-start | bytes 589832 | tf_op jit(solution)/shard_map/ppermute | solution.py:135
  208.9 5.9 %collective-permute-start.28 = (bf16[16,1024]{1,0:T(8,128)(2,1)S(1)}, bf16[16,1024]{1,0:T(8,128)(2,1)S(1)}, u32[]{:S(2)}, u32[]{:S(2)}) collective-permute-start(bf16[16,1024]{1,0:T(8,128)(2,1)S(1)} %fusion.54), channel_id=1, source_target_pairs={{0,2},{1,3},{2,0},{3,1},{4,6},{5,7},{6,4},{7,5},{8,10},{9,11},{10,... | collective-permute-start | bytes 98312 | tf_op jit(solution)/shard_map/ppermute | solution.py:135
  213.2 6.3 %collective-permute-start.23 = (bf16[32,1536]{1,0:T(8,128)(2,1)S(1)}, bf16[32,1536]{1,0:T(8,128)(2,1)S(1)}, u32[]{:S(2)}, u32[]{:S(2)}) collective-permute-start(bf16[32,1536]{1,0:T(8,128)(2,1)S(1)} %fusion.51), channel_id=1, source_target_pairs={{0,2},{1,3},{2,0},{3,1},{4,6},{5,7},{6,4},{7,5},{8,10},{9,11},{10,... | collective-permute-start | bytes 294920 | tf_op jit(solution)/shard_map/ppermute | solution.py:135
  (27 other events, 142.7 us)

commit v6 on v5

--- a/solution.py
+++ b/solution.py
@@ -118,27 +118,55 @@
     return split.transpose(perm).reshape(values.shape)
 
 
-def halving_scatter(grad_wqkv, grad_wout, small):
+def halving_scatter(grad, small=None):
     seq_bits, clip_bits = exchange_bits()
     total = seq_bits + clip_bits
-    first = grad_wqkv.reshape([2] * total + [-1, grad_wqkv.shape[1]])
-    second = grad_wout.reshape([2] * total + [-1, grad_wout.shape[1]])
-    order = [("seq", bit) for bit in range(seq_bits)] + [("clip", bit) for bit in range(clip_bits)]
-    for axis, bit in order:
-        mine = (lax.axis_index(axis) >> bit) & 1
-        count = lax.axis_size(axis)
-        pairs = [(src, src ^ (1 << bit)) for src in range(count)]
-        keep_a = lax.dynamic_index_in_dim(first, mine, axis=0, keepdims=False)
-        give_a = lax.dynamic_index_in_dim(first, 1 - mine, axis=0, keepdims=False)
-        keep_b = lax.dynamic_index_in_dim(second, mine, axis=0, keepdims=False)
-        give_b = lax.dynamic_index_in_dim(second, 1 - mine, axis=0, keepdims=False)
-        got_a, got_b, got_s = lax.ppermute(
-            (give_a.astype(jnp.bfloat16), give_b.astype(jnp.bfloat16), small), axis, pairs
+    data = grad.reshape([2] * total + [-1, grad.shape[1]])
+    order_a = list(range(seq_bits))
+    order_b = [0] + list(range(seq_bits - 1, 0, -1))
+    core_bit = lax.axis_index("seq") & 1
+    left_a = list(range(seq_bits))
+    left_b = list(range(seq_bits))
+    for step in range(seq_bits):
+        bit_a, bit_b = order_a[step], order_b[step]
+        dim_a, dim_b = left_a.index(bit_a), left_b.index(bit_b)
+        me = lax.axis_index("seq")
+        mine_a = (me >> bit_a) & 1
+        mine_b = (me >> bit_b) & 1
+        pairs = []
+        for src in range(lax.axis_size("seq")):
+            bit = bit_a if (src & 1) == 0 else bit_b
+            pairs.append((src, src ^ (1 << bit)))
+        keep = jnp.where(
+            core_bit == 0,
+            lax.dynamic_index_in_dim(data, mine_a, axis=dim_a, keepdims=False),
+            lax.dynamic_index_in_dim(data, mine_b, axis=dim_b, keepdims=False),
         )
-        first = keep_a + got_a.astype(jnp.float32)
-        second = keep_b + got_b.astype(jnp.float32)
-        small = small + got_s
-    return (first, second, small)
+        give = jnp.where(
+            core_bit == 0,
+            lax.dynamic_index_in_dim(data, 1 - mine_a, axis=dim_a, keepdims=False),
+            lax.dynamic_index_in_dim(data, 1 - mine_b, axis=dim_b, keepdims=False),
+        )
+        left_a.pop(dim_a)
+        left_b.pop(dim_b)
+        if small is None:
+            got = lax.ppermute(give.astype(jnp.bfloat16), "seq", pairs)
+        else:
+            got, got_small = lax.ppermute((give.astype(jnp.bfloat16), small), "seq", pairs)
+            small = small + got_small
+        data = keep + got.astype(jnp.float32)
+    for bit in range(clip_bits):
+        mine = (lax.axis_index("clip") >> bit) & 1
+        pairs = [(src, src ^ (1 << bit)) for src in range(lax.axis_size("clip"))]
+        keep = lax.dynamic_index_in_dim(data, mine, axis=0, keepdims=False)
+        give = lax.dynamic_index_in_dim(data, 1 - mine, axis=0, keepdims=False)
+        if small is None:
+            got = lax.ppermute(give.astype(jnp.bfloat16), "clip", pairs)
+        else:
+            got, got_small = lax.ppermute((give.astype(jnp.bfloat16), small), "clip", pairs)
+            small = small + got_small
+        data = keep + got.astype(jnp.float32)
+    return data, small
 
 
 def per_device(raw_tokens, teacher, keep_rows, w_qkv, w_out, ln_gain):
@@ -249,7 +277,8 @@
     grad_ln = jnp.sum(d_hidden * normed, axis=0)
     loss_part = jnp.sum(token_loss)
     small = jnp.concatenate([grad_ln, loss_part.reshape(1)])
-    grad_qkv, grad_out, small = halving_scatter(grad_wqkv, grad_wout, small)
+    grad_out, unused = halving_scatter(grad_wout)
+    grad_qkv, small = halving_scatter(grad_wqkv, small)
     count_all = shards * lax.axis_size("clip") * TOK_DEV
     return (small[-1] / count_all, grad_qkv.reshape(-1), grad_out.reshape(-1), small[:-1])
 

time: 222 us -> 208 us (0.937)
  waiting for transfers between devices: 77.8 us -> 61.7 us
    ppermute x15, waiting for transfers between devices: 45.2 us -> 29.1 us  [the longest x3 13.8 us: halving_scatter(): got = lax.ppermute(give.astype(jnp.bfloat16), 'seq', pairs)]
    unnamed x69 -> x73, local copies, waits for them, and re-layouts: 11 us -> 11.1 us
  transfers between devices with their start and end apart: 31 -> 31, of which waited for: 15 -> 14; matrix products, arithmetic and copies ran while one was open for 18% -> 20% of each run, Pallas kernels for 0% -> 0%
where the time goes in v6:
time: 208 us; the launch traced here: 207 us
  waiting for transfers between devices  61.7 us (30%)
  local copies, waits for them, and re-layouts  52.7 us (25%)
  starting transfers between devices  42.3 us (20%)
  other arithmetic  19.8 us (10%)
  matrix products  17.7 us (9%)
  blocking collectives  9.46 us (5%)
  between operations  3.34 us (2%)
    ppermute x14, waiting for transfers between devices, shifted(): return lax.ppermute(value, axis, pairs)  24.6 us
    ppermute x14, starting transfers between devices, shifted(): return lax.ppermute(value, axis, pairs)  17.7 us
    ppermute x3, waiting for transfers between devices, halving_scatter(): got = lax.ppermute(give.astype(jnp.bfloat16), 'seq', pairs)  13.8 us
    convert_element_type x7, local copies, waits for them, and re-layouts, per_device(): d_pairs[step].astype(jnp.bfloat16)  11.7 us
    unnamed x73, local copies, waits for them, and re-layouts  11.1 us
    unnamed x1, blocking collectives  9.46 us
    all_to_all x1, waiting for transfers between devices, per_device(): lax.all_to_all(send_tokens, 'seq', split_axis=0, concat_axis=0, tiled=True)  8 us
    ppermute x7, local copies, waits for them, and re-layouts, shifted(): return lax.ppermute(value, axis, pairs)  7.82 us
  transfers between devices with their start and end apart: 31, of which 14 were waited for; matrix products, arithmetic and copies ran while one was open for 20% of the time, Pallas kernels for 0%

profile of v6, /device:TPU:0, one launch (start us, length us, event | category | flops | bytes accessed | tf_op | source)
XLA Modules:
  0.0 207.0 jit_solution(8504225513725370248)
XLA Ops:
  5.5 9.5 %all-reduce = s32[8]{0:T(128)S(1)} all-reduce(s32[8]{0:T(128)S(1)} %dynamic-update-slice), channel_id=1, replica_groups=mesh['seq'=8,'clip'=4] {'seq'}, use_global_device_ids=true, to_apply=%add | all-reduce | flops 8 | bytes 64
  22.5 3.5 %all-to-all-start = ((bf16[8,24,1024]{2,1,0:T(8,128)(2,1)}), bf16[8,24,1024]{2,1,0:T(8,128)(2,1)S(1)}, u32[]{:S(2)}, u32[]{:S(2)}) async-start(bf16[8,24,1024]{2,1,0:T(8,128)(2,1)} %get-tuple-element.16), calls=%async_computation | async-start | bytes 786432 | tf_op jit(solution)/shard_map/all_to_all | solution.py:198
  26.3 8.0 %all-to-all-done = bf16[8,24,1024]{2,1,0:T(8,128)(2,1)S(1)} async-done(((bf16[8,24,1024]{2,1,0:T(8,128)(2,1)}), bf16[8,24,1024]{2,1,0:T(8,128)(2,1)S(1)}, u32[]{:S(2)}, u32[]{:S(2)}) %all-to-all-start) | async-done | bytes 393248 | tf_op jit(solution)/shard_map/all_to_all | solution.py:198
  34.3 3.5 %all-to-all-start.1 = ((bf16[8,24,1024]{2,1,0:T(8,128)(2,1)}), bf16[8,24,1024]{2,1,0:T(8,128)(2,1)S(1)}, u32[]{:S(2)}, u32[]{:S(2)}) async-start(bf16[8,24,1024]{2,1,0:T(8,128)(2,1)} %get-tuple-element.15), calls=%async_computation.1 | async-start | bytes 786432 | tf_op jit(solution)/shard_map/all_to_all | solution.py:199
  39.8 2.8 %fusion.20 = bf16[1024,128]{0,1:T(8,128)(2,1)} fusion(bf16[128,1024]{1,0:T(8,128)(2,1)S(1)} %fusion.29, bf16[1024,1536]{1,0:T(8,128)(2,1)} %param.9), kind=kOutput, calls=%fused_computation.34 | convolution fusion | flops 268566528 | bytes 2621440 | tf_op jit(solution)/shard_map/dot_general | solution.py:225
  43.8 2.7 %collective-permute-start.6 = (bf16[1024,128]{0,1:T(8,128)(2,1)}, bf16[1024,128]{0,1:T(8,128)(2,1)}, u32[]{:S(2)}, u32[]{:S(2)}) collective-permute-start(bf16[1024,128]{0,1:T(8,128)(2,1)} %fusion.20), channel_id=1, source_target_pairs={{0,28},{4,0},{8,4},{12,8},{16,12},{20,16},{24,20},{28,24},{1,29},{... | collective-permute-start | bytes 786440 | tf_op jit(solution)/shard_map/ppermute | solution.py:13
  52.4 10.8 %collective-permute-done.1 = bf16[1024,128]{0,1:T(8,128)(2,1)} collective-permute-done((bf16[1024,128]{0,1:T(8,128)(2,1)}, bf16[1024,128]{0,1:T(8,128)(2,1)}, u32[]{:S(2)}, u32[]{:S(2)}) %collective-permute-start.1) | collective-permute-done | bytes 262176 | tf_op jit(solution)/shard_map/ppermute | solution.py:13
  63.2 2.2 %collective-permute-start.5 = (bf16[1024,128]{0,1:T(8,128)(2,1)}, bf16[1024,128]{0,1:T(8,128)(2,1)}, u32[]{:S(2)}, u32[]{:S(2)}) collective-permute-start(bf16[1024,128]{0,1:T(8,128)(2,1)} %fusion.20), channel_id=1, source_target_pairs={{0,24},{4,28},{8,0},{12,4},{16,8},{20,12},{24,16},{28,20},{1,25},{... | collective-permute-start | bytes 786440 | tf_op jit(solution)/shard_map/ppermute | solution.py:13
  75.6 3.1 %copy.30 = bf16[8,2,64,8,128]{4,3,2,0,1:T(8,128)(2,1)} copy(bf16[8,2,64,8,128]{4,2,1,0,3:T(8,128)(2,1)S(1)} %bitcast.196) | data formatting | bytes 4194304 | tf_op jit(solution)/shard_map/transpose | solution.py:229
  78.7 2.8 %reshape.433 = bf16[8,2,64,1024]{3,2,0,1:T(8,128)(2,1)S(1)} reshape(bf16[8,2,64,8,128]{4,3,2,0,1:T(8,128)(2,1)} %copy.30) | data formatting | bytes 4194304 | tf_op jit(solution)/shard_map/reshape | solution.py:230
  88.6 3.3 %fusion.3 = f32[8,64,1024]{2,1,0:T(8,128)S(1)} fusion(bf16[8,128,64]{1,2,0:T(8,128)(2,1)S(1)} %bitcast.197, f32[8,128,1024]{2,1,0:T(8,128)} %copy-done.2, f32[8,128]{1,0:T(8,128)S(1)} %log_add_fusion), kind=kOutput, calls=%fused_computation.16 | convolution fusion | flops 137363456 | bytes 6426624 | tf_op jit(solution)/shard_map/hqd,hqk->hdk/dot_general | solution.py:262
  101.0 3.4 %collective-permute-start.8 = (bf16[1024,128]{0,1:T(8,128)(2,1)}, bf16[1024,128]{0,1:T(8,128)(2,1)}, u32[]{:S(2)}, u32[]{:S(2)}) collective-permute-start(bf16[1024,128]{0,1:T(8,128)(2,1)} %copy.37), channel_id=1, source_target_pairs={{0,24},{4,28},{8,0},{12,4},{16,8},{20,12},{24,16},{28,20},{1,25},{... | collective-permute-start | bytes 786440 | tf_op jit(solution)/shard_map/ppermute | solution.py:13
  104.5 1.8 copy.38
  113.3 1.8 copy.41
  120.5 2.6 %collective-permute-start.7 = (bf16[1024,128]{0,1:T(8,128)(2,1)}, bf16[1024,128]{0,1:T(8,128)(2,1)}, u32[]{:S(2)}, u32[]{:S(2)}) collective-permute-start(bf16[1024,128]{0,1:T(8,128)(2,1)} %copy.35), channel_id=1, source_target_pairs={{0,28},{4,0},{8,4},{12,8},{16,12},{20,16},{24,20},{28,24},{1,29},{... | collective-permute-start | bytes 786440 | tf_op jit(solution)/shard_map/ppermute | solution.py:13
  123.2 2.1 fusion.23
  125.4 2.6 %maximum_bitcast_fusion = f32[8,8,2,64,128]{4,3,2,1,0:T(8,128)S(1)} fusion(f32[8,1,64,8,128]{4,2,1,0,3:T(8,128)} %copy-done.6, f32[8,1,64,8,128]{4,2,1,0,3:T(8,128)} %copy-done.5), kind=kLoop, calls=%fused_computation.6 | loop fusion | flops 1048576 | bytes 8388608 | tf_op jit(solution)/shard_map/transpose | solution.py:270
  128.2 10.3 %collective-permute-done.10 = bf16[1024,128]{0,1:T(8,128)(2,1)} collective-permute-done((bf16[1024,128]{0,1:T(8,128)(2,1)}, bf16[1024,128]{0,1:T(8,128)(2,1)}, u32[]{:S(2)}, u32[]{:S(2)}) %collective-permute-start.10) | collective-permute-done | bytes 262176 | tf_op jit(solution)/shard_map/ppermute | solution.py:13
  143.0 2.6 %copy-done.4 = f32[2,2,2,2,2,32,1536]{6,5,4,3,2,1,0:T(8,128)} copy-done((f32[2,2,2,2,2,32,1536]{6,5,4,3,2,1,0:T(8,128)}, f32[2,2,2,2,2,32,1536]{6,5,4,3,2,1,0:T(8,128)S(1)}, u32[]{:S(2)}) %copy-start.4) | copy-done | bytes 6291480
  148.4 3.0 %collective-permute-done.24 = bf16[2,2,2,2,16,1024]{5,4,3,2,1,0:T(8,128)(2,1)} collective-permute-done((bf16[2,2,2,2,16,1024]{5,4,3,2,1,0:T(8,128)(2,1)S(1)}, bf16[2,2,2,2,16,1024]{5,4,3,2,1,0:T(8,128)(2,1)}, u32[]{:S(2)}, u32[]{:S(2)}) %collective-permute-start.24) | collective-permute-done | bytes 524320 | tf_op jit(solution)/shard_map/ppermute | solution.py:153
  152.7 3.0 %bitcast_add_fusion = f32[2,2,2,2,32,1536]{5,4,3,2,1,0:T(8,128)S(1)} fusion(bf16[2,2,2,2,32,1536]{5,4,3,2,1,0:T(8,128)(2,1)} %collective-permute-done.19, f32[2,2,2,2,2,32,1536]{6,5,4,3,2,1,0:T(8,128)} %copy-done.4, s32[]{:T(128)S(6)} %select_n.229), kind=kLoop, calls=%fused_computation.14 | loop fusion | flops 1572864 | bytes 7864324 | tf_op jit(solution)/shard_map/add | solution.py:157
  156.0 2.1 collective-permute-start.25
  160.0 10.7 %collective-permute-done.25 = bf16[2,2,2,16,1024]{4,3,2,1,0:T(8,128)(2,1)S(1)} collective-permute-done((bf16[2,2,2,16,1024]{4,3,2,1,0:T(8,128)(2,1)S(1)}, bf16[2,2,2,16,1024]{4,3,2,1,0:T(8,128)(2,1)S(1)}, u32[]{:S(2)}, u32[]{:S(2)}) %collective-permute-start.25) | collective-permute-done | bytes 262176 | tf_op jit(solution)/shard_map/ppermute | solution.py:153
  174.3 3.8 %collective-permute-done.15 = f32[1025]{0:T(1024)S(1)} collective-permute-done((f32[1025]{0:T(1024)S(1)}, f32[1025]{0:T(1024)S(1)}, u32[]{:S(2)}, u32[]{:S(2)}) %collective-permute-start.15) | collective-permute-done | bytes 4132 | tf_op jit(solution)/shard_map/ppermute | solution.py:155
  178.6 3.2 %collective-permute-done.16 = f32[1025]{0:T(1024)S(1)} collective-permute-done((f32[1025]{0:T(1024)S(1)}, f32[1025]{0:T(1024)S(1)}, u32[]{:S(2)}, u32[]{:S(2)}) %collective-permute-start.16) | collective-permute-done | bytes 4132 | tf_op jit(solution)/shard_map/ppermute | solution.py:155
  183.3 2.1 collective-permute-done.17
  185.4 2.6 %collective-permute-start.18 = (f32[1025]{0:T(1024)S(1)}, f32[1025]{0:T(1024)S(1)}, u32[]{:S(2)}, u32[]{:S(2)}) collective-permute-start(f32[1025]{0:T(1024)S(1)} %add.325), channel_id=1, source_target_pairs={{0,2},{1,3},{2,0},{3,1},{4,6},{5,7},{6,4},{7,5},{8,10},{9,11},{10,... | collective-permute-start | bytes 12308 | tf_op jit(solution)/shard_map/ppermute | solution.py:166
  188.0 2.0 collective-permute-done.18
  194.2 2.0 collective-permute-done.27
  196.2 3.3 %collective-permute-start.28 = (bf16[16,1024]{1,0:T(8,128)(2,1)S(1)}, bf16[16,1024]{1,0:T(8,128)(2,1)S(1)}, u32[]{:S(2)}, u32[]{:S(2)}) collective-permute-start(bf16[16,1024]{1,0:T(8,128)(2,1)S(1)} %fusion.56), channel_id=1, source_target_pairs={{0,2},{1,3},{2,0},{3,1},{4,6},{5,7},{6,4},{7,5},{8,10},{9,11},{10,... | collective-permute-start | bytes 98312 | tf_op jit(solution)/shard_map/ppermute | solution.py:164
  199.6 2.6 %collective-permute-start.23 = (bf16[32,1536]{1,0:T(8,128)(2,1)S(1)}, bf16[32,1536]{1,0:T(8,128)(2,1)S(1)}, u32[]{:S(2)}, u32[]{:S(2)}) collective-permute-start(bf16[32,1536]{1,0:T(8,128)(2,1)S(1)} %fusion.53), channel_id=1, source_target_pairs={{0,2},{1,3},{2,0},{3,1},{4,6},{5,7},{6,4},{7,5},{8,10},{9,11},{10,... | collective-permute-start | bytes 294920 | tf_op jit(solution)/shard_map/ppermute | solution.py:166
  202.9 2.3 %collective-permute-done.23 = bf16[32,1536]{1,0:T(8,128)(2,1)S(1)} collective-permute-done((bf16[32,1536]{1,0:T(8,128)(2,1)S(1)}, bf16[32,1536]{1,0:T(8,128)(2,1)S(1)}, u32[]{:S(2)}, u32[]{:S(2)}) %collective-permute-start.23) | collective-permute-done | bytes 98336 | tf_op jit(solution)/shard_map/ppermute | solution.py:166
  (211 shorter events, 81.5 us)
Async XLA Ops:
  21.5 18.0 %copy-start.18 = (f32[1024]{0:T(1024)S(1)}, f32[1024]{0:T(1024)}, u32[]{:S(2)}) copy-start(f32[1024]{0:T(1024)} %param.11) | copy-start | bytes 12292
  22.5 11.7 %all-to-all-start = ((bf16[8,24,1024]{2,1,0:T(8,128)(2,1)}), bf16[8,24,1024]{2,1,0:T(8,128)(2,1)S(1)}, u32[]{:S(2)}, u32[]{:S(2)}) async-start(bf16[8,24,1024]{2,1,0:T(8,128)(2,1)} %get-tuple-element.16), calls=%async_computation | async-start | bytes 786432 | tf_op jit(solution)/shard_map/all_to_all | solution.py:198
  34.3 15.9 %all-to-all-start.1 = ((bf16[8,24,1024]{2,1,0:T(8,128)(2,1)}), bf16[8,24,1024]{2,1,0:T(8,128)(2,1)S(1)}, u32[]{:S(2)}, u32[]{:S(2)}) async-start(bf16[8,24,1024]{2,1,0:T(8,128)(2,1)} %get-tuple-element.15), calls=%async_computation.1 | async-start | bytes 786432 | tf_op jit(solution)/shard_map/all_to_all | solution.py:199
  43.8 30.6 %collective-permute-start.6 = (bf16[1024,128]{0,1:T(8,128)(2,1)}, bf16[1024,128]{0,1:T(8,128)(2,1)}, u32[]{:S(2)}, u32[]{:S(2)}) collective-permute-start(bf16[1024,128]{0,1:T(8,128)(2,1)} %fusion.20), channel_id=1, source_target_pairs={{0,28},{4,0},{8,4},{12,8},{16,12},{20,16},{24,20},{28,24},{1,29},{... | collective-permute-start | bytes 786440 | tf_op jit(solution)/shard_map/ppermute | solution.py:13
  46.4 21.6 %collective-permute-start.3 = (bf16[1024,128]{0,1:T(8,128)(2,1)}, bf16[1024,128]{0,1:T(8,128)(2,1)}, u32[]{:S(2)}, u32[]{:S(2)}) collective-permute-start(bf16[1024,128]{0,1:T(8,128)(2,1)} %fusion.20), channel_id=1, source_target_pairs={{0,16},{4,20},{8,24},{12,28},{16,0},{20,4},{24,8},{28,12},{1,17},{... | collective-permute-start | bytes 786440 | tf_op jit(solution)/shard_map/ppermute | solution.py:13
  47.0 22.2 %collective-permute-start.2 = (bf16[1024,128]{0,1:T(8,128)(2,1)}, bf16[1024,128]{0,1:T(8,128)(2,1)}, u32[]{:S(2)}, u32[]{:S(2)}) collective-permute-start(bf16[1024,128]{0,1:T(8,128)(2,1)} %fusion.20), channel_id=1, source_target_pairs={{0,12},{4,16},{8,20},{12,24},{16,28},{20,0},{24,4},{28,8},{1,13},{... | collective-permute-start | bytes 786440 | tf_op jit(solution)/shard_map/ppermute | solution.py:13
  47.1 16.1 %collective-permute-start.1 = (bf16[1024,128]{0,1:T(8,128)(2,1)}, bf16[1024,128]{0,1:T(8,128)(2,1)}, u32[]{:S(2)}, u32[]{:S(2)}) collective-permute-start(bf16[1024,128]{0,1:T(8,128)(2,1)} %fusion.20), channel_id=1, source_target_pairs={{0,8},{4,12},{8,16},{12,20},{16,24},{20,28},{24,0},{28,4},{1,9},{5... | collective-permute-start | bytes 786440 | tf_op jit(solution)/shard_map/ppermute | solution.py:13
  47.5 19.0 %collective-permute-start = (bf16[1024,128]{0,1:T(8,128)(2,1)}, bf16[1024,128]{0,1:T(8,128)(2,1)}, u32[]{:S(2)}, u32[]{:S(2)}) collective-permute-start(bf16[1024,128]{0,1:T(8,128)(2,1)} %fusion.20), channel_id=1, source_target_pairs={{0,4},{4,8},{8,12},{12,16},{16,20},{20,24},{24,28},{28,0},{1,5},{5... | collective-permute-start | bytes 786440 | tf_op jit(solution)/shard_map/ppermute | solution.py:13
  63.2 8.5 %collective-permute-start.5 = (bf16[1024,128]{0,1:T(8,128)(2,1)}, bf16[1024,128]{0,1:T(8,128)(2,1)}, u32[]{:S(2)}, u32[]{:S(2)}) collective-permute-start(bf16[1024,128]{0,1:T(8,128)(2,1)} %fusion.20), channel_id=1, source_target_pairs={{0,24},{4,28},{8,0},{12,4},{16,8},{20,12},{24,16},{28,20},{1,25},{... | collective-permute-start | bytes 786440 | tf_op jit(solution)/shard_map/ppermute | solution.py:13
  66.5 6.6 %collective-permute-start.4 = (bf16[1024,128]{0,1:T(8,128)(2,1)}, bf16[1024,128]{0,1:T(8,128)(2,1)}, u32[]{:S(2)}, u32[]{:S(2)}) collective-permute-start(bf16[1024,128]{0,1:T(8,128)(2,1)} %fusion.20), channel_id=1, source_target_pairs={{0,20},{4,24},{8,28},{12,0},{16,4},{20,8},{24,12},{28,16},{1,21},{... | collective-permute-start | bytes 786440 | tf_op jit(solution)/shard_map/ppermute | solution.py:13
  101.0 19.5 %collective-permute-start.8 = (bf16[1024,128]{0,1:T(8,128)(2,1)}, bf16[1024,128]{0,1:T(8,128)(2,1)}, u32[]{:S(2)}, u32[]{:S(2)}) collective-permute-start(bf16[1024,128]{0,1:T(8,128)(2,1)} %copy.37), channel_id=1, source_target_pairs={{0,24},{4,28},{8,0},{12,4},{16,8},{20,12},{24,16},{28,20},{1,25},{... | collective-permute-start | bytes 786440 | tf_op jit(solution)/shard_map/ppermute | solution.py:13
  106.3 14.2 %collective-permute-start.9 = (bf16[1024,128]{0,1:T(8,128)(2,1)}, bf16[1024,128]{0,1:T(8,128)(2,1)}, u32[]{:S(2)}, u32[]{:S(2)}) collective-permute-start(bf16[1024,128]{0,1:T(8,128)(2,1)} %copy.38), channel_id=1, source_target_pairs={{0,20},{4,24},{8,28},{12,0},{16,4},{20,8},{24,12},{28,16},{1,21},{... | collective-permute-start | bytes 786440 | tf_op jit(solution)/shard_map/ppermute | solution.py:13
  117.8 20.7 %collective-permute-start.10 = (bf16[1024,128]{0,1:T(8,128)(2,1)}, bf16[1024,128]{0,1:T(8,128)(2,1)}, u32[]{:S(2)}, u32[]{:S(2)}) collective-permute-start(bf16[1024,128]{0,1:T(8,128)(2,1)} %copy.39), channel_id=1, source_target_pairs={{0,16},{4,20},{8,24},{12,28},{16,0},{20,4},{24,8},{28,12},{1,17},{... | collective-permute-start | bytes 786440 | tf_op jit(solution)/shard_map/ppermute | solution.py:13
  119.3 20.9 %collective-permute-start.11 = (bf16[1024,128]{0,1:T(8,128)(2,1)}, bf16[1024,128]{0,1:T(8,128)(2,1)}, u32[]{:S(2)}, u32[]{:S(2)}) collective-permute-start(bf16[1024,128]{0,1:T(8,128)(2,1)} %copy.40), channel_id=1, source_target_pairs={{0,12},{4,16},{8,20},{12,24},{16,28},{20,0},{24,4},{28,8},{1,13},{... | collective-permute-start | bytes 786440 | tf_op jit(solution)/shard_map/ppermute | solution.py:13
  119.3 20.9 %collective-permute-start.12 = (bf16[1024,128]{0,1:T(8,128)(2,1)}, bf16[1024,128]{0,1:T(8,128)(2,1)}, u32[]{:S(2)}, u32[]{:S(2)}) collective-permute-start(bf16[1024,128]{0,1:T(8,128)(2,1)} %copy.41), channel_id=1, source_target_pairs={{0,8},{4,12},{8,16},{12,20},{16,24},{20,28},{24,0},{28,4},{1,9},{5... | collective-permute-start | bytes 786440 | tf_op jit(solution)/shard_map/ppermute | solution.py:13
  120.5 19.8 %collective-permute-start.13 = (bf16[1024,128]{0,1:T(8,128)(2,1)}, bf16[1024,128]{0,1:T(8,128)(2,1)}, u32[]{:S(2)}, u32[]{:S(2)}) collective-permute-start(bf16[1024,128]{0,1:T(8,128)(2,1)} %copy.42), channel_id=1, source_target_pairs={{0,4},{4,8},{8,12},{12,16},{16,20},{20,24},{24,28},{28,0},{1,5},{5... | collective-permute-start | bytes 786440 | tf_op jit(solution)/shard_map/ppermute | solution.py:13
  120.5 19.8 %collective-permute-start.7 = (bf16[1024,128]{0,1:T(8,128)(2,1)}, bf16[1024,128]{0,1:T(8,128)(2,1)}, u32[]{:S(2)}, u32[]{:S(2)}) collective-permute-start(bf16[1024,128]{0,1:T(8,128)(2,1)} %copy.35), channel_id=1, source_target_pairs={{0,28},{4,0},{8,4},{12,8},{16,12},{20,16},{24,20},{28,24},{1,29},{... | collective-permute-start | bytes 786440 | tf_op jit(solution)/shard_map/ppermute | solution.py:13
  147.2 5.5 %collective-permute-start.19 = (bf16[2,2,2,2,32,1536]{5,4,3,2,1,0:T(8,128)(2,1)}, bf16[2,2,2,2,32,1536]{5,4,3,2,1,0:T(8,128)(2,1)}, u32[]{:S(2)}, u32[]{:S(2)}) collective-permute-start(bf16[2,2,2,2,32,1536]{5,4,3,2,1,0:T(8,128)(2,1)} %fusion.13), channel_id=1, source_target_pairs={{0,4},{4,0},{8,12},{12,8},{16,20},{20,16},{24,28},{28,24},{1,5},{5... | collective-permute-start | bytes 4718600 | tf_op jit(solution)/shard_map/ppermute | solution.py:155
  147.9 3.6 %collective-permute-start.24 = (bf16[2,2,2,2,16,1024]{5,4,3,2,1,0:T(8,128)(2,1)S(1)}, bf16[2,2,2,2,16,1024]{5,4,3,2,1,0:T(8,128)(2,1)}, u32[]{:S(2)}, u32[]{:S(2)}) collective-permute-start(bf16[2,2,2,2,16,1024]{5,4,3,2,1,0:T(8,128)(2,1)S(1)} %fusion.33), channel_id=1, source_target_pairs={{0,4},{4,0},{8,12},{12,8},{16,20},{20,16},{24,28},{28,24},{1,5},{5... | collective-permute-start | bytes 1572872 | tf_op jit(solution)/shard_map/ppermute | solution.py:153
  155.9 15.6 %collective-permute-start.20 = (bf16[2,2,2,32,1536]{4,3,2,1,0:T(8,128)(2,1)S(1)}, bf16[2,2,2,32,1536]{4,3,2,1,0:T(8,128)(2,1)S(1)}, u32[]{:S(2)}, u32[]{:S(2)}) collective-permute-start(bf16[2,2,2,32,1536]{4,3,2,1,0:T(8,128)(2,1)S(1)} %fusion.14), channel_id=1, source_target_pairs={{0,8},{4,20},{8,0},{12,28},{16,24},{20,4},{24,16},{28,12},{1,9},{5... | collective-permute-start | bytes 2359304 | tf_op jit(solution)/shard_map/ppermute | solution.py:155
  156.0 14.7 %collective-permute-start.25 = (bf16[2,2,2,16,1024]{4,3,2,1,0:T(8,128)(2,1)S(1)}, bf16[2,2,2,16,1024]{4,3,2,1,0:T(8,128)(2,1)S(1)}, u32[]{:S(2)}, u32[]{:S(2)}) collective-permute-start(bf16[2,2,2,16,1024]{4,3,2,1,0:T(8,128)(2,1)S(1)} %fusion.34), channel_id=1, source_target_pairs={{0,8},{4,20},{8,0},{12,28},{16,24},{20,4},{24,16},{28,12},{1,9},{5... | collective-permute-start | bytes 786440 | tf_op jit(solution)/shard_map/ppermute | solution.py:153
  159.9 13.6 %collective-permute-start.14 = (f32[1025]{0:T(1024)S(1)}, f32[1025]{0:T(1024)S(1)}, u32[]{:S(2)}, u32[]{:S(2)}) collective-permute-start(f32[1025]{0:T(1024)S(1)} %pad_maximum_fusion.3), channel_id=1, source_target_pairs={{0,4},{4,0},{8,12},{12,8},{16,20},{20,16},{24,28},{28,24},{1,5},{5... | collective-permute-start | bytes 12308 | tf_op jit(solution)/shard_map/ppermute | solution.py:155
  170.9 20.8 %collective-permute-start.26 = (bf16[2,2,16,1024]{3,2,1,0:T(8,128)(2,1)S(1)}, bf16[2,2,16,1024]{3,2,1,0:T(8,128)(2,1)S(1)}, u32[]{:S(2)}, u32[]{:S(2)}) collective-permute-start(bf16[2,2,16,1024]{3,2,1,0:T(8,128)(2,1)S(1)} %fusion.46), channel_id=1, source_target_pairs={{0,16},{4,12},{8,24},{12,4},{16,0},{20,28},{24,8},{28,20},{1,17},{... | collective-permute-start | bytes 393224 | tf_op jit(solution)/shard_map/ppermute | solution.py:153
  171.9 21.5 %collective-permute-start.21 = (bf16[2,2,32,1536]{3,2,1,0:T(8,128)(2,1)S(1)}, bf16[2,2,32,1536]{3,2,1,0:T(8,128)(2,1)S(1)}, u32[]{:S(2)}, u32[]{:S(2)}) collective-permute-start(bf16[2,2,32,1536]{3,2,1,0:T(8,128)(2,1)S(1)} %fusion.36), channel_id=1, source_target_pairs={{0,16},{4,12},{8,24},{12,4},{16,0},{20,28},{24,8},{28,20},{1,17},{... | collective-permute-start | bytes 1179656 | tf_op jit(solution)/shard_map/ppermute | solution.py:155
  174.2 3.9 %collective-permute-start.15 = (f32[1025]{0:T(1024)S(1)}, f32[1025]{0:T(1024)S(1)}, u32[]{:S(2)}, u32[]{:S(2)}) collective-permute-start(f32[1025]{0:T(1024)S(1)} %fusion.60), channel_id=1, source_target_pairs={{0,8},{4,20},{8,0},{12,28},{16,24},{20,4},{24,16},{28,12},{1,9},{5... | collective-permute-start | bytes 12308 | tf_op jit(solution)/shard_map/ppermute | solution.py:155
  178.1 3.7 %collective-permute-start.16 = (f32[1025]{0:T(1024)S(1)}, f32[1025]{0:T(1024)S(1)}, u32[]{:S(2)}, u32[]{:S(2)}) collective-permute-start(f32[1025]{0:T(1024)S(1)} %add.323), channel_id=1, source_target_pairs={{0,16},{4,12},{8,24},{12,4},{16,0},{20,28},{24,8},{28,20},{1,17},{... | collective-permute-start | bytes 12308 | tf_op jit(solution)/shard_map/ppermute | solution.py:155
  181.7 3.7 %collective-permute-start.17 = (f32[1025]{0:T(1024)S(1)}, f32[1025]{0:T(1024)S(1)}, u32[]{:S(2)}, u32[]{:S(2)}) collective-permute-start(f32[1025]{0:T(1024)S(1)} %add.324), channel_id=1, source_target_pairs={{0,1},{1,0},{2,3},{3,2},{4,5},{5,4},{6,7},{7,6},{8,9},{9,8},{10,11... | collective-permute-start | bytes 12308 | tf_op jit(solution)/shard_map/ppermute | solution.py:166
  185.4 4.6 %collective-permute-start.18 = (f32[1025]{0:T(1024)S(1)}, f32[1025]{0:T(1024)S(1)}, u32[]{:S(2)}, u32[]{:S(2)}) collective-permute-start(f32[1025]{0:T(1024)S(1)} %add.325), channel_id=1, source_target_pairs={{0,2},{1,3},{2,0},{3,1},{4,6},{5,7},{6,4},{7,5},{8,10},{9,11},{10,... | collective-permute-start | bytes 12308 | tf_op jit(solution)/shard_map/ppermute | solution.py:166
  191.8 4.3 %collective-permute-start.27 = (bf16[2,16,1024]{2,1,0:T(8,128)(2,1)S(1)}, bf16[2,16,1024]{2,1,0:T(8,128)(2,1)S(1)}, u32[]{:S(2)}, u32[]{:S(2)}) collective-permute-start(bf16[2,16,1024]{2,1,0:T(8,128)(2,1)S(1)} %fusion.54), channel_id=1, source_target_pairs={{0,1},{1,0},{2,3},{3,2},{4,5},{5,4},{6,7},{7,6},{8,9},{9,8},{10,11... | collective-permute-start | bytes 196616 | tf_op jit(solution)/shard_map/ppermute | solution.py:164
  193.6 5.9 %collective-permute-start.22 = (bf16[2,32,1536]{2,1,0:T(8,128)(2,1)S(1)}, bf16[2,32,1536]{2,1,0:T(8,128)(2,1)S(1)}, u32[]{:S(2)}, u32[]{:S(2)}) collective-permute-start(bf16[2,32,1536]{2,1,0:T(8,128)(2,1)S(1)} %fusion.45), channel_id=1, source_target_pairs={{0,1},{1,0},{2,3},{3,2},{4,5},{5,4},{6,7},{7,6},{8,9},{9,8},{10,11... | collective-permute-start | bytes 589832 | tf_op jit(solution)/shard_map/ppermute | solution.py:166
  196.2 6.0 %collective-permute-start.28 = (bf16[16,1024]{1,0:T(8,128)(2,1)S(1)}, bf16[16,1024]{1,0:T(8,128)(2,1)S(1)}, u32[]{:S(2)}, u32[]{:S(2)}) collective-permute-start(bf16[16,1024]{1,0:T(8,128)(2,1)S(1)} %fusion.56), channel_id=1, source_target_pairs={{0,2},{1,3},{2,0},{3,1},{4,6},{5,7},{6,4},{7,5},{8,10},{9,11},{10,... | collective-permute-start | bytes 98312 | tf_op jit(solution)/shard_map/ppermute | solution.py:164
  199.6 5.6 %collective-permute-start.23 = (bf16[32,1536]{1,0:T(8,128)(2,1)S(1)}, bf16[32,1536]{1,0:T(8,128)(2,1)S(1)}, u32[]{:S(2)}, u32[]{:S(2)}) collective-permute-start(bf16[32,1536]{1,0:T(8,128)(2,1)S(1)} %fusion.53), channel_id=1, source_target_pairs={{0,2},{1,3},{2,0},{3,1},{4,6},{5,7},{6,4},{7,5},{8,10},{9,11},{10,... | collective-permute-start | bytes 294920 | tf_op jit(solution)/shard_map/ppermute | solution.py:166
  (29 other events, 143.3 us)

commit v7 on v6

--- a/solution.py
+++ b/solution.py
@@ -179,7 +179,9 @@
     safe_ids = jnp.maximum(row_ids, 0)
     kept_tokens = jnp.where(is_kept[:, None], raw_tokens[0][safe_ids], jnp.zeros((), jnp.bfloat16))
     kept_target = jnp.where(is_kept[:, None], teacher[0][safe_ids], jnp.zeros((), jnp.bfloat16))
-    count_table = lax.all_gather(kept_count.reshape(1), "seq", axis=0, tiled=True)
+    count_table = lax.all_to_all(
+        jnp.broadcast_to(kept_count.reshape(1, 1), (shards, 1)), "seq", 0, 0, tiled=True
+    ).reshape(shards)
     shard_ids = jnp.arange(shards, dtype=jnp.int32)
     per_peer = -(-list_slots // shards)
     starts = jnp.cumsum(count_table) - count_table
@@ -225,7 +227,9 @@
     pair_cols = jnp.dot(w_qkv[:, inner:].T, hidden.T, preferred_element_type=jnp.float32).astype(
         jnp.bfloat16
     )
-    gathered = jnp.stack([pair_cols] + [shifted(pair_cols, "seq", step) for step in range(1, shards)])
+    gathered = lax.all_to_all(
+        jnp.broadcast_to(pair_cols[None], (shards,) + pair_cols.shape), "seq", 0, 0, tiled=True
+    )
     split_kv = gathered.reshape(shards, heads, 2, HEAD_DIM, rows).transpose(1, 2, 3, 0, 4)
     split_kv = split_kv.reshape(heads, 2, HEAD_DIM, shards * rows)
     keys_t = split_kv[:, 0]
@@ -267,10 +271,9 @@
     d_query = 0.125 * jnp.einsum("hqk,hdk->qhd", d_score, keys_t, preferred_element_type=jnp.float32)
     d_key_t = 0.125 * jnp.einsum("hqd,hqk->hdk", queries, d_score, preferred_element_type=jnp.float32)
     d_pairs = jnp.stack([d_key_t, d_value_t], axis=1).reshape(heads, 2, HEAD_DIM, shards, rows)
-    d_pairs = d_pairs.transpose(3, 0, 1, 2, 4).reshape(shards, 2 * inner, rows)
-    accum = d_pairs[0]
-    for step in range(1, shards):
-        accum = accum + shifted(d_pairs[step].astype(jnp.bfloat16), "seq", -step).astype(jnp.float32)
+    d_pairs = d_pairs.transpose(3, 0, 1, 2, 4).reshape(shards, 2 * inner, rows).astype(jnp.bfloat16)
+    returned = lax.all_to_all(d_pairs, "seq", 0, 0, tiled=True)
+    accum = jnp.sum(returned.astype(jnp.float32), axis=0)
     d_proj = jnp.concatenate([d_query.reshape(rows, inner), accum.T], axis=1).astype(jnp.bfloat16)
     grad_wqkv = jnp.dot(exchange_order(hidden).T, d_proj, preferred_element_type=jnp.float32)
     d_hidden = jnp.dot(d_proj, w_qkv.T, preferred_element_type=jnp.float32)

time: 208 us -> 184 us (0.88)
  local copies, waits for them, and re-layouts: 52.7 us -> 31.3 us
  blocking collectives: 9.46 us -> 0 us
  starting transfers between devices: 42.3 us -> 36.3 us
  waiting for transfers between devices: 61.7 us -> 67 us
  matrix products: 17.7 us -> 21.5 us
  other arithmetic: 19.8 us -> 23.2 us
    all_to_all x0 -> x3, waiting for transfers between devices: none -> 41.7 us  [the longest x1 20.9 us: per_device(): returned = lax.all_to_all(d_pairs, 'seq', 0, 0, tiled=True)]
    ppermute x14 -> x0, waiting for transfers between devices: 24.6 us -> none  [shifted(): return lax.ppermute(value, axis, pairs)]
    ppermute x14 -> x0, starting transfers between devices: 17.7 us -> none  [shifted(): return lax.ppermute(value, axis, pairs)]
    all_to_all x0 -> x3, starting transfers between devices: none -> 13.3 us  [the longest x1 5.17 us: per_device(): lax.all_to_all(jnp.broadcast_to(kept_count.reshape(1, 1), (shards, 1)), '...]
    ppermute x3, waiting for transfers between devices: 13.8 us -> 1.87 us  [halving_scatter(): got = lax.ppermute(give.astype(jnp.bfloat16), 'seq', pairs)]
    convert_element_type x7 -> x0, local copies, waits for them, and re-layouts: 11.7 us -> none  [per_device(): d_pairs[step].astype(jnp.bfloat16)]
    unnamed x1 -> x0, blocking collectives: 9.46 us -> none
    ppermute x7 -> x0, local copies, waits for them, and re-layouts: 7.82 us -> none  [shifted(): return lax.ppermute(value, axis, pairs)]
  transfers between devices with their start and end apart: 31 -> 20, of which waited for: 14 -> 12; matrix products, arithmetic and copies ran while one was open for 20% -> 19% of each run, Pallas kernels for 0% -> 0%
where the time goes in v7:
time: 184 us; the launch traced here: 182 us
  waiting for transfers between devices  67 us (36%)
  starting transfers between devices  36.3 us (20%)
  local copies, waits for them, and re-layouts  31.3 us (17%)
  other arithmetic  23.2 us (13%)
  matrix products  21.5 us (12%)
  between operations  3.15 us (2%)
    all_to_all x1, waiting for transfers between devices, per_device(): returned = lax.all_to_all(d_pairs, 'seq', 0, 0, tiled=True)  20.9 us
    all_to_all x1, waiting for transfers between devices, per_device(): lax.all_to_all(jnp.broadcast_to(pair_cols[None], (shards,) + pair_cols.sh...  19.1 us
    ppermute x6, waiting for transfers between devices, halving_scatter(): lax.ppermute((give.astype(jnp.bfloat16), small), 'seq', pairs)  8.47 us
    all_to_all x1, waiting for transfers between devices, per_device(): lax.all_to_all(send_tokens, 'seq', split_axis=0, concat_axis=0, tiled=True)  8.09 us
    add x9, other arithmetic, halving_scatter(): data = keep + got.astype(jnp.float32)  7.24 us
    unnamed x69, local copies, waits for them, and re-layouts  6.07 us
    ppermute x4, starting transfers between devices, halving_scatter(): lax.ppermute((give.astype(jnp.bfloat16), small), 'clip', pairs)  5.45 us
    all_to_all x1, starting transfers between devices, per_device(): lax.all_to_all(jnp.broadcast_to(kept_count.reshape(1, 1), (shards, 1)), '...  5.17 us
  transfers between devices with their start and end apart: 20, of which 12 were waited for; matrix products, arithmetic and copies ran while one was open for 19% of the time, Pallas kernels for 0%

profile of v7, /device:TPU:0, one launch (start us, length us, event | category | flops | bytes accessed | tf_op | source)
XLA Modules:
  0.0 182.4 jit_solution(14820866439162609611)
XLA Ops:
  3.4 5.2 %all-to-all-start = ((s32[8,1,1]{2,1,0:T(1,128)}), s32[8,1,1]{2,1,0:T(1,128)S(1)}, u32[]{:S(2)}, u32[]{:S(2)}) async-start(s32[8,1,1]{2,1,0:T(1,128)} %broadcast_in_dim.42), calls=%async_computation | async-start | bytes 8192 | tf_op jit(solution)/shard_map/all_to_all | solution.py:182
  11.4 1.7 all-to-all-done
  18.9 3.5 %all-to-all-start.1 = ((bf16[8,24,1024]{2,1,0:T(8,128)(2,1)}), bf16[8,24,1024]{2,1,0:T(8,128)(2,1)S(1)}, u32[]{:S(2)}, u32[]{:S(2)}) async-start(bf16[8,24,1024]{2,1,0:T(8,128)(2,1)} %get-tuple-element.9), calls=%async_computation.1 | async-start | bytes 786432 | tf_op jit(solution)/shard_map/all_to_all | solution.py:200
  22.6 8.1 %all-to-all-done.1 = bf16[8,24,1024]{2,1,0:T(8,128)(2,1)S(1)} async-done(((bf16[8,24,1024]{2,1,0:T(8,128)(2,1)}), bf16[8,24,1024]{2,1,0:T(8,128)(2,1)S(1)}, u32[]{:S(2)}, u32[]{:S(2)}) %all-to-all-start.1) | async-done | bytes 393248 | tf_op jit(solution)/shard_map/all_to_all | solution.py:200
  30.6 3.5 %all-to-all-start.3 = ((bf16[8,24,1024]{2,1,0:T(8,128)(2,1)}), bf16[8,24,1024]{2,1,0:T(8,128)(2,1)S(1)}, u32[]{:S(2)}, u32[]{:S(2)}) async-start(bf16[8,24,1024]{2,1,0:T(8,128)(2,1)} %get-tuple-element.8), calls=%async_computation.3 | async-start | bytes 786432 | tf_op jit(solution)/shard_map/all_to_all | solution.py:201
  36.9 2.0 %fusion.23 = bf16[1024,128]{0,1:T(8,128)(2,1)S(1)} fusion(bf16[128,1024]{1,0:T(8,128)(2,1)S(1)} %fusion.32, bf16[1024,1536]{1,0:T(8,128)(2,1)} %param.9), kind=kOutput, calls=%fused_computation.35 | convolution fusion | flops 268566528 | bytes 2621440 | tf_op jit(solution)/shard_map/dot_general | solution.py:227
  39.1 3.3 %all-to-all-done.3 = bf16[8,24,1024]{2,1,0:T(8,128)(2,1)S(1)} async-done(((bf16[8,24,1024]{2,1,0:T(8,128)(2,1)}), bf16[8,24,1024]{2,1,0:T(8,128)(2,1)S(1)}, u32[]{:S(2)}, u32[]{:S(2)}) %all-to-all-start.3) | async-done | bytes 393248 | tf_op jit(solution)/shard_map/all_to_all | solution.py:201
  42.4 1.6 broadcast_in_dim.48
  44.0 3.6 %all-to-all-start.2 = ((bf16[8,1024,128]{2,1,0:T(8,128)(2,1)}), bf16[8,1024,128]{2,1,0:T(8,128)(2,1)S(1)}, u32[]{:S(2)}, u32[]{:S(2)}) async-start(bf16[8,1024,128]{2,1,0:T(8,128)(2,1)} %broadcast_in_dim.48), calls=%async_computation.2 | async-start | bytes 4194304 | tf_op jit(solution)/shard_map/all_to_all | solution.py:230
  47.6 2.5 %scatter_custom_fusion.1 = bf16[128,1024]{1,0:T(8,128)(2,1)} fusion(s32[192]{0:T(256)S(1)} %bitcast.199, bf16[192,1024]{1,0:T(8,128)(2,1)} %bitcast.192, bf16[]{:T(256)} %constant.157.clone.1), kind=kCustom, calls=%fused_computation.96 | custom fusion | bytes 262656 | tf_op jit(solution)/shard_map/scatter | solution.py:215
  50.1 2.3 %convolution_convert_fusion.1 = bf16[128,512]{1,0:T(8,128)(2,1)} fusion(bf16[128,1024]{1,0:T(8,128)(2,1)} %copy-done.16, bf16[1024,1536]{1,0:T(8,128)(2,1)} %param.9), kind=kOutput, calls=%fused_computation.38 | convolution fusion | flops 134283264 | bytes 1441792 | tf_op jit(solution)/shard_map/dot_general | solution.py:222
  55.1 19.1 %all-to-all-done.2 = bf16[8,1024,128]{2,1,0:T(8,128)(2,1)S(1)} async-done(((bf16[8,1024,128]{2,1,0:T(8,128)(2,1)}), bf16[8,1024,128]{2,1,0:T(8,128)(2,1)S(1)}, u32[]{:S(2)}, u32[]{:S(2)}) %all-to-all-start.2) | async-done | bytes 2097184 | tf_op jit(solution)/shard_map/all_to_all | solution.py:230
  74.2 3.1 %copy.36 = bf16[8,2,64,8,128]{4,3,2,0,1:T(8,128)(2,1)} copy(bf16[8,2,64,8,128]{4,2,1,0,3:T(8,128)(2,1)S(1)} %bitcast.175) | data formatting | bytes 4194304 | tf_op jit(solution)/shard_map/transpose | solution.py:233
  77.3 2.8 %reshape.415 = bf16[8,2,64,1024]{3,2,0,1:T(8,128)(2,1)S(1)} reshape(bf16[8,2,64,8,128]{4,3,2,0,1:T(8,128)(2,1)} %copy.36) | data formatting | bytes 4194304 | tf_op jit(solution)/shard_map/reshape | solution.py:234
  81.9 1.7 fusion.45
  86.3 3.4 %fusion.16 = bf16[8,64,1024]{2,1,0:T(8,128)(2,1)S(1)} fusion(bf16[8,128,64]{1,2,0:T(8,128)(2,1)S(1)} %bitcast.180, f32[8,128,1024]{2,1,0:T(8,128)} %copy-done.1, f32[8,128]{1,0:T(8,128)S(1)} %log_add_fusion), kind=kOutput, calls=%fused_computation.30 | convolution fusion | flops 137887744 | bytes 5378048 | tf_op jit(solution)/shard_map/hqd,hqk->hdk/dot_general | solution.py:266
  89.6 2.7 %multiply_convert_fusion = bf16[8,128,1024]{2,1,0:T(8,128)(2,1)S(1)} fusion(f32[8,128,1024]{2,1,0:T(8,128)S(1)} %copy-done.2, bf16[8,128,64]{1,2,0:T(8,128)(2,1)S(1)} %bitcast.181, f32[8,128]{1,0:T(8,128)S(1)} %multiply_reduce_fusion.4, f32[8,128]{1,0:T(8,128)S(1)} %log_add_fusion, bf16[8,2,64,1024]{3,2,0,1:T(8,128)(2,1)} %copy-done.6), kind=kOutput, calls=%fused_computation.6 | convolution fusion | flops 139460608 | bytes 7479296 | tf_op jit(solution)/shard_map/hqd,hdk->hqk/dot_general | solution.py:269
  95.4 4.6 %all-to-all-start.4 = ((bf16[8,1024,128]{2,1,0:T(8,128)(2,1)}), bf16[8,1024,128]{2,1,0:T(8,128)(2,1)}, u32[]{:S(2)}, u32[]{:S(2)}) async-start(bf16[8,1024,128]{2,1,0:T(8,128)(2,1)} %bitcast.174), calls=%async_computation.4 | async-start | bytes 4194304 | tf_op jit(solution)/shard_map/all_to_all | solution.py:275
  100.0 1.8 copy.43
  101.7 2.7 %fusion.26 = bf16[8,64,128]{2,1,0:T(8,128)(2,1)} fusion(bf16[8,128,1024]{2,1,0:T(8,128)(2,1)S(1)} %multiply_convert_fusion, bf16[8,2,64,1024]{3,2,0,1:T(8,128)(2,1)} %copy-done.6), kind=kOutput, calls=%fused_computation.39 | convolution fusion | flops 134348800 | bytes 3276800 | tf_op jit(solution)/shard_map/hqk,hdk->qhd/dot_general | solution.py:271
  105.5 20.9 %all-to-all-done.4 = bf16[8,1024,128]{2,1,0:T(8,128)(2,1)} async-done(((bf16[8,1024,128]{2,1,0:T(8,128)(2,1)}), bf16[8,1024,128]{2,1,0:T(8,128)(2,1)}, u32[]{:S(2)}, u32[]{:S(2)}) %all-to-all-start.4) | async-done | bytes 2097184 | tf_op jit(solution)/shard_map/all_to_all | solution.py:275
  126.4 2.0 %reduce.1 = bf16[1024,128]{1,0:T(8,128)(2,1)S(1)} reduce(bf16[8,1024,128]{2,1,0:T(8,128)(2,1)} %all-to-all-done.4, bf16[]{:T(256)} %constant.157.clone.1), dimensions={0}, to_apply=%region_13.14.clone | reduce | flops 917504 | bytes 2359298 | tf_op jit(solution)/shard_map/reduce_sum | solution.py:276
  133.6 1.9 %collective-permute-done.10 = bf16[2,2,2,2,16,1024]{5,4,3,2,1,0:T(8,128)(2,1)S(1)} collective-permute-done((bf16[2,2,2,2,16,1024]{5,4,3,2,1,0:T(8,128)(2,1)S(1)}, bf16[2,2,2,2,16,1024]{5,4,3,2,1,0:T(8,128)(2,1)S(1)}, u32[]{:S(2)}, u32[]{:S(2)}) %collective-permute-start.10) | collective-permute-done | bytes 524320 | tf_op jit(solution)/shard_map/ppermute | solution.py:153
  137.4 2.9 %bitcast_add_fusion = f32[2,2,2,2,32,1536]{5,4,3,2,1,0:T(8,128)S(1)} fusion(bf16[2,2,2,2,32,1536]{5,4,3,2,1,0:T(8,128)(2,1)} %collective-permute-done.5, f32[2,2,2,2,2,32,1536]{6,5,4,3,2,1,0:T(8,128)} %copy-done.5, s32[]{:T(128)S(6)} %select_n.233), kind=kLoop, calls=%fused_computation.13 | loop fusion | flops 1572864 | bytes 7864324 | tf_op jit(solution)/shard_map/add | solution.py:157
  140.3 1.6 copy-done.3
  146.4 3.0 %fusion.22 = f32[1024]{0:T(1024)S(1)} fusion(bf16[1024,1536]{1,0:T(8,128)(2,1)} %param.9, bf16[128,1024]{1,0:T(8,128)(2,1)S(1)} %scatter_custom_fusion, f32[128]{0:T(128)S(1)} %copy-done.32, f32[128]{0:T(128)S(1)} %broadcast_multiply_fusion.1, bf16[128,1024]{1,0:T(8,128)(2,1)S(1)} %bitcast.187, bf16[128,512]{1,0:T(8,128)(2,1)S(1)} %copy.42), kind=kOutput, calls=%fused_computation.34 | convolution fusion | flops 404093952 | bytes 3806208 | tf_op jit(solution)/shard_map/dot_general | solution.py:279
  150.1 6.6 %collective-permute-done.6 = bf16[2,2,2,32,1536]{4,3,2,1,0:T(8,128)(2,1)} collective-permute-done((bf16[2,2,2,32,1536]{4,3,2,1,0:T(8,128)(2,1)}, bf16[2,2,2,32,1536]{4,3,2,1,0:T(8,128)(2,1)}, u32[]{:S(2)}, u32[]{:S(2)}) %collective-permute-start.6) | collective-permute-done | bytes 786464 | tf_op jit(solution)/shard_map/ppermute | solution.py:155
  156.7 1.6 fusion.15
  161.3 1.6 collective-permute-start.13
  166.4 1.6 collective-permute-start.8
  168.9 2.6 %collective-permute-start.14 = (bf16[16,1024]{1,0:T(8,128)(2,1)S(1)}, bf16[16,1024]{1,0:T(8,128)(2,1)S(1)}, u32[]{:S(2)}, u32[]{:S(2)}) collective-permute-start(bf16[16,1024]{1,0:T(8,128)(2,1)S(1)} %fusion.58), channel_id=1, source_target_pairs={{0,2},{1,3},{2,0},{3,1},{4,6},{5,7},{6,4},{7,5},{8,10},{9,11},{10,... | collective-permute-start | bytes 98312 | tf_op jit(solution)/shard_map/ppermute | solution.py:164
  172.3 2.6 %collective-permute-start.4 = (f32[1025]{0:T(1024)S(1)}, f32[1025]{0:T(1024)S(1)}, u32[]{:S(2)}, u32[]{:S(2)}) collective-permute-start(f32[1025]{0:T(1024)S(1)} %add.301), channel_id=1, source_target_pairs={{0,2},{1,3},{2,0},{3,1},{4,6},{5,7},{6,4},{7,5},{8,10},{9,11},{10,... | collective-permute-start | bytes 12308 | tf_op jit(solution)/shard_map/ppermute | solution.py:166
  (170 shorter events, 51.5 us)
Async XLA Ops:
  0.6 8.6 %copy-start = (bf16[1,512,1024]{2,1,0:T(8,128)(2,1)S(1)}, bf16[1,512,1024]{2,1,0:T(8,128)(2,1)}, u32[]{:S(2)}) copy-start(bf16[1,512,1024]{2,1,0:T(8,128)(2,1)} %param.7) | copy-start | bytes 3145732
  0.6 9.6 %copy-start.7 = (bf16[1,512,1024]{2,1,0:T(8,128)(2,1)S(1)}, bf16[1,512,1024]{2,1,0:T(8,128)(2,1)}, u32[]{:S(2)}) copy-start(bf16[1,512,1024]{2,1,0:T(8,128)(2,1)} %param.6) | copy-start | bytes 3145732
  3.4 9.8 %all-to-all-start = ((s32[8,1,1]{2,1,0:T(1,128)}), s32[8,1,1]{2,1,0:T(1,128)S(1)}, u32[]{:S(2)}, u32[]{:S(2)}) async-start(s32[8,1,1]{2,1,0:T(1,128)} %broadcast_in_dim.42), calls=%async_computation | async-start | bytes 8192 | tf_op jit(solution)/shard_map/all_to_all | solution.py:182
  16.9 19.1 %copy-start.22 = (f32[1024]{0:T(1024)S(1)}, f32[1024]{0:T(1024)}, u32[]{:S(2)}) copy-start(f32[1024]{0:T(1024)} %param.11) | copy-start | bytes 12292
  18.9 11.7 %all-to-all-start.1 = ((bf16[8,24,1024]{2,1,0:T(8,128)(2,1)}), bf16[8,24,1024]{2,1,0:T(8,128)(2,1)S(1)}, u32[]{:S(2)}, u32[]{:S(2)}) async-start(bf16[8,24,1024]{2,1,0:T(8,128)(2,1)} %get-tuple-element.9), calls=%async_computation.1 | async-start | bytes 786432 | tf_op jit(solution)/shard_map/all_to_all | solution.py:200
  30.6 11.7 %all-to-all-start.3 = ((bf16[8,24,1024]{2,1,0:T(8,128)(2,1)}), bf16[8,24,1024]{2,1,0:T(8,128)(2,1)S(1)}, u32[]{:S(2)}, u32[]{:S(2)}) async-start(bf16[8,24,1024]{2,1,0:T(8,128)(2,1)} %get-tuple-element.8), calls=%async_computation.3 | async-start | bytes 786432 | tf_op jit(solution)/shard_map/all_to_all | solution.py:201
  35.9 8.1 %copy-start.31 = (f32[128]{0:T(128)}, f32[128]{0:T(128)S(1)}, u32[]{:S(2)}) copy-start(f32[128]{0:T(128)S(1)} %add_rsqrt_fusion.2) | copy-start | bytes 1540
  44.0 30.2 %all-to-all-start.2 = ((bf16[8,1024,128]{2,1,0:T(8,128)(2,1)}), bf16[8,1024,128]{2,1,0:T(8,128)(2,1)S(1)}, u32[]{:S(2)}, u32[]{:S(2)}) async-start(bf16[8,1024,128]{2,1,0:T(8,128)(2,1)} %broadcast_in_dim.48), calls=%async_computation.2 | async-start | bytes 4194304 | tf_op jit(solution)/shard_map/all_to_all | solution.py:230
  53.4 26.7 %copy-start.13 = (bf16[128,512]{0,1:T(8,128)(2,1)}, bf16[128,512]{0,1:T(8,128)(2,1)S(1)}, u32[]{:S(2)}) copy-start(bf16[128,512]{0,1:T(8,128)(2,1)S(1)} %copy.37) | copy-start | bytes 393220
  83.6 2.6 %copy-start.21 = (f32[8,128,64]{1,2,0:T(8,128)S(1)}, f32[8,128,64]{1,2,0:T(8,128)}, u32[]{:S(2)}) copy-start(f32[8,128,64]{1,2,0:T(8,128)} %get-tuple-element.21) | copy-start | bytes 786436
  86.2 3.5 %copy-start.2 = (f32[8,128,1024]{2,1,0:T(8,128)S(1)}, f32[8,128,1024]{2,1,0:T(8,128)}, u32[]{:S(2)}) copy-start(f32[8,128,1024]{2,1,0:T(8,128)} %copy-done.1) | copy-start | bytes 12582916
  89.6 2.7 %copy-start.14 = (bf16[128,512]{0,1:T(8,128)(2,1)S(1)}, bf16[128,512]{0,1:T(8,128)(2,1)}, u32[]{:S(2)}) copy-start(bf16[128,512]{0,1:T(8,128)(2,1)} %copy-done.13) | copy-start | bytes 393220
  95.4 31.0 %all-to-all-start.4 = ((bf16[8,1024,128]{2,1,0:T(8,128)(2,1)}), bf16[8,1024,128]{2,1,0:T(8,128)(2,1)}, u32[]{:S(2)}, u32[]{:S(2)}) async-start(bf16[8,1024,128]{2,1,0:T(8,128)(2,1)} %bitcast.174), calls=%async_computation.4 | async-start | bytes 4194304 | tf_op jit(solution)/shard_map/all_to_all | solution.py:275
  104.4 24.1 %copy-start.17 = (bf16[128,1024]{0,1:T(8,128)(2,1)S(1)}, bf16[128,1024]{0,1:T(8,128)(2,1)}, u32[]{:S(2)}) copy-start(bf16[128,1024]{0,1:T(8,128)(2,1)} %copy.43) | copy-start | bytes 786436
  129.5 4.0 %copy-start.5 = (f32[2,2,2,2,2,32,1536]{6,5,4,3,2,1,0:T(8,128)}, f32[2,2,2,2,2,32,1536]{6,5,4,3,2,1,0:T(8,128)S(1)}, u32[]{:S(2)}) copy-start(f32[2,2,2,2,2,32,1536]{6,5,4,3,2,1,0:T(8,128)S(1)} %fusion.40) | copy-start | bytes 18874372
  130.9 6.5 %collective-permute-start.5 = (bf16[2,2,2,2,32,1536]{5,4,3,2,1,0:T(8,128)(2,1)}, bf16[2,2,2,2,32,1536]{5,4,3,2,1,0:T(8,128)(2,1)}, u32[]{:S(2)}, u32[]{:S(2)}) collective-permute-start(bf16[2,2,2,2,32,1536]{5,4,3,2,1,0:T(8,128)(2,1)} %fusion.13), channel_id=1, source_target_pairs={{0,4},{4,0},{8,12},{12,8},{16,20},{20,16},{24,28},{28,24},{1,5},{5... | collective-permute-start | bytes 4718600 | tf_op jit(solution)/shard_map/ppermute | solution.py:155
  133.5 2.0 %collective-permute-start.10 = (bf16[2,2,2,2,16,1024]{5,4,3,2,1,0:T(8,128)(2,1)S(1)}, bf16[2,2,2,2,16,1024]{5,4,3,2,1,0:T(8,128)(2,1)S(1)}, u32[]{:S(2)}, u32[]{:S(2)}) collective-permute-start(bf16[2,2,2,2,16,1024]{5,4,3,2,1,0:T(8,128)(2,1)S(1)} %fusion.36), channel_id=1, source_target_pairs={{0,4},{4,0},{8,12},{12,8},{16,20},{20,16},{24,28},{28,24},{1,5},{5... | collective-permute-start | bytes 1572872 | tf_op jit(solution)/shard_map/ppermute | solution.py:153
  136.9 7.7 %collective-permute-start.11 = (bf16[2,2,2,16,1024]{4,3,2,1,0:T(8,128)(2,1)S(1)}, bf16[2,2,2,16,1024]{4,3,2,1,0:T(8,128)(2,1)}, u32[]{:S(2)}, u32[]{:S(2)}) collective-permute-start(bf16[2,2,2,16,1024]{4,3,2,1,0:T(8,128)(2,1)S(1)} %fusion.37), channel_id=1, source_target_pairs={{0,8},{4,20},{8,0},{12,28},{16,24},{20,4},{24,16},{28,12},{1,9},{5... | collective-permute-start | bytes 786440 | tf_op jit(solution)/shard_map/ppermute | solution.py:153
  142.0 4.4 %copy-start.32 = (f32[128]{0:T(128)S(1)}, f32[128]{0:T(128)}, u32[]{:S(2)}) copy-start(f32[128]{0:T(128)} %copy-done.31) | copy-start | bytes 1540
  143.0 13.7 %collective-permute-start.6 = (bf16[2,2,2,32,1536]{4,3,2,1,0:T(8,128)(2,1)}, bf16[2,2,2,32,1536]{4,3,2,1,0:T(8,128)(2,1)}, u32[]{:S(2)}, u32[]{:S(2)}) collective-permute-start(bf16[2,2,2,32,1536]{4,3,2,1,0:T(8,128)(2,1)} %fusion.14), channel_id=1, source_target_pairs={{0,8},{4,20},{8,0},{12,28},{16,24},{20,4},{24,16},{28,12},{1,9},{5... | collective-permute-start | bytes 2359304 | tf_op jit(solution)/shard_map/ppermute | solution.py:155
  144.5 12.2 %copy-start.4 = (f32[2,2,2,2,32,1536]{5,4,3,2,1,0:T(8,128)S(1)}, f32[2,2,2,2,32,1536]{5,4,3,2,1,0:T(8,128)}, u32[]{:S(2)}) copy-start(f32[2,2,2,2,32,1536]{5,4,3,2,1,0:T(8,128)} %copy-done.3) | copy-start | bytes 9437188
  145.8 13.3 %collective-permute-start.12 = (bf16[2,2,16,1024]{3,2,1,0:T(8,128)(2,1)S(1)}, bf16[2,2,16,1024]{3,2,1,0:T(8,128)(2,1)S(1)}, u32[]{:S(2)}, u32[]{:S(2)}) collective-permute-start(bf16[2,2,16,1024]{3,2,1,0:T(8,128)(2,1)S(1)} %fusion.48), channel_id=1, source_target_pairs={{0,16},{4,12},{8,24},{12,4},{16,0},{20,28},{24,8},{28,20},{1,17},{... | collective-permute-start | bytes 393224 | tf_op jit(solution)/shard_map/ppermute | solution.py:153
  150.1 9.1 %collective-permute-start = (f32[1025]{0:T(1024)S(1)}, f32[1025]{0:T(1024)S(1)}, u32[]{:S(2)}, u32[]{:S(2)}) collective-permute-start(f32[1025]{0:T(1024)S(1)} %pad_maximum_fusion.4), channel_id=1, source_target_pairs={{0,4},{4,0},{8,12},{12,8},{16,20},{20,16},{24,28},{28,24},{1,5},{5... | collective-permute-start | bytes 12308 | tf_op jit(solution)/shard_map/ppermute | solution.py:155
  158.3 7.8 %collective-permute-start.7 = (bf16[2,2,32,1536]{3,2,1,0:T(8,128)(2,1)S(1)}, bf16[2,2,32,1536]{3,2,1,0:T(8,128)(2,1)S(1)}, u32[]{:S(2)}, u32[]{:S(2)}) collective-permute-start(bf16[2,2,32,1536]{3,2,1,0:T(8,128)(2,1)S(1)} %fusion.39), channel_id=1, source_target_pairs={{0,16},{4,12},{8,24},{12,4},{16,0},{20,28},{24,8},{28,20},{1,17},{... | collective-permute-start | bytes 1179656 | tf_op jit(solution)/shard_map/ppermute | solution.py:155
  159.8 3.9 %collective-permute-start.1 = (f32[1025]{0:T(1024)S(1)}, f32[1025]{0:T(1024)S(1)}, u32[]{:S(2)}, u32[]{:S(2)}) collective-permute-start(f32[1025]{0:T(1024)S(1)} %fusion.62), channel_id=1, source_target_pairs={{0,8},{4,20},{8,0},{12,28},{16,24},{20,4},{24,16},{28,12},{1,9},{5... | collective-permute-start | bytes 12308 | tf_op jit(solution)/shard_map/ppermute | solution.py:155
  161.3 6.8 %collective-permute-start.13 = (bf16[2,16,1024]{2,1,0:T(8,128)(2,1)S(1)}, bf16[2,16,1024]{2,1,0:T(8,128)(2,1)S(1)}, u32[]{:S(2)}, u32[]{:S(2)}) collective-permute-start(bf16[2,16,1024]{2,1,0:T(8,128)(2,1)S(1)} %fusion.56), channel_id=1, source_target_pairs={{0,1},{1,0},{2,3},{3,2},{4,5},{5,4},{6,7},{7,6},{8,9},{9,8},{10,11... | collective-permute-start | bytes 196616 | tf_op jit(solution)/shard_map/ppermute | solution.py:164
  163.7 4.4 %collective-permute-start.2 = (f32[1025]{0:T(1024)S(1)}, f32[1025]{0:T(1024)S(1)}, u32[]{:S(2)}, u32[]{:S(2)}) collective-permute-start(f32[1025]{0:T(1024)S(1)} %add.299), channel_id=1, source_target_pairs={{0,16},{4,12},{8,24},{12,4},{16,0},{20,28},{24,8},{28,20},{1,17},{... | collective-permute-start | bytes 12308 | tf_op jit(solution)/shard_map/ppermute | solution.py:155
  166.4 8.5 %collective-permute-start.8 = (bf16[2,32,1536]{2,1,0:T(8,128)(2,1)S(1)}, bf16[2,32,1536]{2,1,0:T(8,128)(2,1)S(1)}, u32[]{:S(2)}, u32[]{:S(2)}) collective-permute-start(bf16[2,32,1536]{2,1,0:T(8,128)(2,1)S(1)} %fusion.47), channel_id=1, source_target_pairs={{0,1},{1,0},{2,3},{3,2},{4,5},{5,4},{6,7},{7,6},{8,9},{9,8},{10,11... | collective-permute-start | bytes 589832 | tf_op jit(solution)/shard_map/ppermute | solution.py:166
  168.1 4.3 %collective-permute-start.3 = (f32[1025]{0:T(1024)S(1)}, f32[1025]{0:T(1024)S(1)}, u32[]{:S(2)}, u32[]{:S(2)}) collective-permute-start(f32[1025]{0:T(1024)S(1)} %add.300), channel_id=1, source_target_pairs={{0,1},{1,0},{2,3},{3,2},{4,5},{5,4},{6,7},{7,6},{8,9},{9,8},{10,11... | collective-permute-start | bytes 12308 | tf_op jit(solution)/shard_map/ppermute | solution.py:166
  168.9 6.5 %collective-permute-start.14 = (bf16[16,1024]{1,0:T(8,128)(2,1)S(1)}, bf16[16,1024]{1,0:T(8,128)(2,1)S(1)}, u32[]{:S(2)}, u32[]{:S(2)}) collective-permute-start(bf16[16,1024]{1,0:T(8,128)(2,1)S(1)} %fusion.58), channel_id=1, source_target_pairs={{0,2},{1,3},{2,0},{3,1},{4,6},{5,7},{6,4},{7,5},{8,10},{9,11},{10,... | collective-permute-start | bytes 98312 | tf_op jit(solution)/shard_map/ppermute | solution.py:164
  172.3 5.1 %collective-permute-start.4 = (f32[1025]{0:T(1024)S(1)}, f32[1025]{0:T(1024)S(1)}, u32[]{:S(2)}, u32[]{:S(2)}) collective-permute-start(f32[1025]{0:T(1024)S(1)} %add.301), channel_id=1, source_target_pairs={{0,2},{1,3},{2,0},{3,1},{4,6},{5,7},{6,4},{7,5},{8,10},{9,11},{10,... | collective-permute-start | bytes 12308 | tf_op jit(solution)/shard_map/ppermute | solution.py:166
  175.0 5.6 %collective-permute-start.9 = (bf16[32,1536]{1,0:T(8,128)(2,1)S(1)}, bf16[32,1536]{1,0:T(8,128)(2,1)S(1)}, u32[]{:S(2)}, u32[]{:S(2)}) collective-permute-start(bf16[32,1536]{1,0:T(8,128)(2,1)S(1)} %fusion.55), channel_id=1, source_target_pairs={{0,2},{1,3},{2,0},{3,1},{4,6},{5,7},{6,4},{7,5},{8,10},{9,11},{10,... | collective-permute-start | bytes 294920 | tf_op jit(solution)/shard_map/ppermute | solution.py:166
  (21 other events, 32.6 us)

commit v8 on v7

--- a/solution.py
+++ b/solution.py
@@ -169,6 +169,30 @@
     return data, small
 
 
+def xor_pairs(mask):
+    count = lax.axis_size("seq")
+    return [(src, src ^ mask) for src in range(count)]
+
+
+def gather_blocks(block):
+    half = lax.axis_size("seq") // 2
+    same_core = [block] + [lax.ppermute(block, "seq", xor_pairs(2 * k)) for k in range(1, half)]
+    group = jnp.stack(same_core)
+    other = lax.ppermute(group, "seq", xor_pairs(1))
+    return jnp.concatenate([group, other], axis=0)
+
+
+def return_blocks(parts):
+    half = lax.axis_size("seq") // 2
+    got = lax.ppermute(parts[half:], "seq", xor_pairs(1))
+    summed = parts[:half].astype(jnp.float32) + got.astype(jnp.float32)
+    accum = summed[0]
+    for k in range(1, half):
+        sent = lax.ppermute(summed[k].astype(jnp.bfloat16), "seq", xor_pairs(2 * k))
+        accum = accum + sent.astype(jnp.float32)
+    return accum
+
+
 def per_device(raw_tokens, teacher, keep_rows, w_qkv, w_out, ln_gain):
     shards = lax.axis_size("seq")
     my_index = lax.axis_index("seq")
@@ -227,9 +251,7 @@
     pair_cols = jnp.dot(w_qkv[:, inner:].T, hidden.T, preferred_element_type=jnp.float32).astype(
         jnp.bfloat16
     )
-    gathered = lax.all_to_all(
-        jnp.broadcast_to(pair_cols[None], (shards,) + pair_cols.shape), "seq", 0, 0, tiled=True
-    )
+    gathered = gather_blocks(pair_cols)
     split_kv = gathered.reshape(shards, heads, 2, HEAD_DIM, rows).transpose(1, 2, 3, 0, 4)
     split_kv = split_kv.reshape(heads, 2, HEAD_DIM, shards * rows)
     keys_t = split_kv[:, 0]
@@ -272,8 +294,7 @@
     d_key_t = 0.125 * jnp.einsum("hqd,hqk->hdk", queries, d_score, preferred_element_type=jnp.float32)
     d_pairs = jnp.stack([d_key_t, d_value_t], axis=1).reshape(heads, 2, HEAD_DIM, shards, rows)
     d_pairs = d_pairs.transpose(3, 0, 1, 2, 4).reshape(shards, 2 * inner, rows).astype(jnp.bfloat16)
-    returned = lax.all_to_all(d_pairs, "seq", 0, 0, tiled=True)
-    accum = jnp.sum(returned.astype(jnp.float32), axis=0)
+    accum = return_blocks(d_pairs)
     d_proj = jnp.concatenate([d_query.reshape(rows, inner), accum.T], axis=1).astype(jnp.bfloat16)
     grad_wqkv = jnp.dot(exchange_order(hidden).T, d_proj, preferred_element_type=jnp.float32)
     d_hidden = jnp.dot(d_proj, w_qkv.T, preferred_element_type=jnp.float32)

time: 184 us -> 179 us (0.973)
  waiting for transfers between devices: 67 us -> 47.4 us
  local copies, waits for them, and re-layouts: 31.3 us -> 46 us
  other arithmetic: 23.2 us -> 25.8 us
    all_to_all x2 -> x0, waiting for transfers between devices: 40 us -> none  [the longest x1 20.9 us: per_device(): returned = lax.all_to_all(d_pairs, 'seq', 0, 0, tiled=True)]
    ppermute x0 -> x8, waiting for transfers between devices: none -> 20.3 us  [the longest x3 10.5 us: return_blocks(): sent = lax.ppermute(summed[k].astype(jnp.bfloat16), 'seq', xor_pairs(2 * k))]
    all_to_all x2 -> x0, starting transfers between devices: 8.17 us -> none  [the longest x1 4.57 us: per_device(): returned = lax.all_to_all(d_pairs, 'seq', 0, 0, tiled=True)]
    ppermute x0 -> x8, starting transfers between devices: none -> 7.57 us  [the longest x3 3.56 us: gather_blocks(): lax.ppermute(block, 'seq', xor_pairs(2 * k))]
    ppermute x0 -> x4, local copies, waits for them, and re-layouts: none -> 4.69 us  [the longest x3 3.08 us: gather_blocks(): lax.ppermute(block, 'seq', xor_pairs(2 * k))]
    unnamed x69 -> x73, local copies, waits for them, and re-layouts: 6.07 us -> 10.3 us
    slice x0 -> x2, local copies, waits for them, and re-layouts: none -> 3.86 us  [return_blocks(): got = lax.ppermute(parts[half:], 'seq', xor_pairs(1))]
    convert_element_type x0 -> x2, local copies, waits for them, and re-layouts: none -> 3.82 us  [the longest x1 2.87 us: return_blocks(): summed = parts[:half].astype(jnp.float32) + got.astype(jnp.float32)]
  transfers between devices with their start and end apart: 20 -> 26, of which waited for: 12 -> 16; matrix products, arithmetic and copies ran while one was open for 19% -> 20% of each run, Pallas kernels for 0% -> 0%
where the time goes in v8:
time: 179 us; the launch traced here: 178 us
  waiting for transfers between devices  47.4 us (26%)
  local copies, waits for them, and re-layouts  46 us (26%)
  starting transfers between devices  36.1 us (20%)
  other arithmetic  25.8 us (14%)
  matrix products  19.9 us (11%)
  between operations  3.14 us (2%)
    ppermute x3, waiting for transfers between devices, return_blocks(): sent = lax.ppermute(summed[k].astype(jnp.bfloat16), 'seq', xor_pairs(2 * k))  10.5 us
    unnamed x73, local copies, waits for them, and re-layouts  10.3 us
    ppermute x3, waiting for transfers between devices, gather_blocks(): lax.ppermute(block, 'seq', xor_pairs(2 * k))  9.76 us
    ppermute x6, waiting for transfers between devices, halving_scatter(): lax.ppermute((give.astype(jnp.bfloat16), small), 'seq', pairs)  8.84 us
    all_to_all x1, waiting for transfers between devices, per_device(): lax.all_to_all(send_tokens, 'seq', split_axis=0, concat_axis=0, tiled=True)  8.09 us
    ppermute x4, starting transfers between devices, halving_scatter(): lax.ppermute((give.astype(jnp.bfloat16), small), 'clip', pairs)  6.03 us
    add x9, other arithmetic, halving_scatter(): data = keep + got.astype(jnp.float32)  5.75 us
    all_to_all x1, starting transfers between devices, per_device(): lax.all_to_all(jnp.broadcast_to(kept_count.reshape(1, 1), (shards, 1)), '...  5.17 us
  transfers between devices with their start and end apart: 26, of which 16 were waited for; matrix products, arithmetic and copies ran while one was open for 20% of the time, Pallas kernels for 0%

profile of v8, /device:TPU:0, one launch (start us, length us, event | category | flops | bytes accessed | tf_op | source)
XLA Modules:
  0.0 178.4 jit_solution(10093026132201472463)
XLA Ops:
  3.4 5.2 %all-to-all-start = ((s32[8,1,1]{2,1,0:T(1,128)}), s32[8,1,1]{2,1,0:T(1,128)S(1)}, u32[]{:S(2)}, u32[]{:S(2)}) async-start(s32[8,1,1]{2,1,0:T(1,128)} %broadcast_in_dim.40), calls=%async_computation | async-start | bytes 8192 | tf_op jit(solution)/shard_map/all_to_all | solution.py:206
  9.2 3.9 %all-to-all-done = s32[8,1,1]{2,1,0:T(1,128)S(1)} async-done(((s32[8,1,1]{2,1,0:T(1,128)}), s32[8,1,1]{2,1,0:T(1,128)S(1)}, u32[]{:S(2)}, u32[]{:S(2)}) %all-to-all-start) | async-done | bytes 64 | tf_op jit(solution)/shard_map/all_to_all | solution.py:206
  21.1 3.5 %all-to-all-start.1 = ((bf16[8,24,1024]{2,1,0:T(8,128)(2,1)}), bf16[8,24,1024]{2,1,0:T(8,128)(2,1)S(1)}, u32[]{:S(2)}, u32[]{:S(2)}) async-start(bf16[8,24,1024]{2,1,0:T(8,128)(2,1)} %get-tuple-element.16), calls=%async_computation.1 | async-start | bytes 786432 | tf_op jit(solution)/shard_map/all_to_all | solution.py:224
  24.7 8.1 %all-to-all-done.1 = bf16[8,24,1024]{2,1,0:T(8,128)(2,1)S(1)} async-done(((bf16[8,24,1024]{2,1,0:T(8,128)(2,1)}), bf16[8,24,1024]{2,1,0:T(8,128)(2,1)S(1)}, u32[]{:S(2)}, u32[]{:S(2)}) %all-to-all-start.1) | async-done | bytes 393248 | tf_op jit(solution)/shard_map/all_to_all | solution.py:224
  32.8 3.5 %all-to-all-start.2 = ((bf16[8,24,1024]{2,1,0:T(8,128)(2,1)}), bf16[8,24,1024]{2,1,0:T(8,128)(2,1)S(1)}, u32[]{:S(2)}, u32[]{:S(2)}) async-start(bf16[8,24,1024]{2,1,0:T(8,128)(2,1)} %get-tuple-element.15), calls=%async_computation.2 | async-start | bytes 786432 | tf_op jit(solution)/shard_map/all_to_all | solution.py:225
  38.3 2.1 %fusion.19 = bf16[128,1024]{1,0:T(8,128)(2,1)S(1)} fusion(bf16[128,1024]{1,0:T(8,128)(2,1)S(1)} %fusion.29, bf16[1024,1536]{1,0:T(8,128)(2,1)} %param.9), kind=kOutput, calls=%fused_computation.34 | convolution fusion | flops 268566528 | bytes 2621440 | tf_op jit(solution)/shard_map/dot_general | solution.py:251
  40.5 2.9 %collective-permute-start.2 = (bf16[1024,128]{0,1:T(8,128)(2,1)S(1)}, bf16[1024,128]{0,1:T(8,128)(2,1)S(1)}, u32[]{:S(2)}, u32[]{:S(2)}) collective-permute-start(bf16[1024,128]{0,1:T(8,128)(2,1)S(1)} %bitcast.223), channel_id=1, source_target_pairs={{0,24},{4,28},{8,16},{12,20},{16,8},{20,12},{24,0},{28,4},{1,25},{... | collective-permute-start | bytes 786440 | tf_op jit(solution)/shard_map/ppermute | solution.py:179
  44.5 1.6 scatter_custom_fusion.1
  46.2 4.4 %collective-permute-done.2 = bf16[1024,128]{0,1:T(8,128)(2,1)S(1)} collective-permute-done((bf16[1024,128]{0,1:T(8,128)(2,1)S(1)}, bf16[1024,128]{0,1:T(8,128)(2,1)S(1)}, u32[]{:S(2)}, u32[]{:S(2)}) %collective-permute-start.2) | collective-permute-done | bytes 262176 | tf_op jit(solution)/shard_map/ppermute | solution.py:179
  50.6 5.2 %collective-permute-done.1 = bf16[1024,128]{0,1:T(8,128)(2,1)S(1)} collective-permute-done((bf16[1024,128]{0,1:T(8,128)(2,1)S(1)}, bf16[1024,128]{0,1:T(8,128)(2,1)S(1)}, u32[]{:S(2)}, u32[]{:S(2)}) %collective-permute-start.1) | collective-permute-done | bytes 262176 | tf_op jit(solution)/shard_map/ppermute | solution.py:179
  60.2 1.8 %copy.49 = bf16[1024,128]{1,0:T(8,128)(2,1)} copy(bf16[1024,128]{0,1:T(8,128)(2,1)} %copy-done.15) | data formatting | bytes 524288 | tf_op jit(solution)/shard_map/ppermute | solution.py:179
  67.1 4.7 %copy.53 = bf16[8,2,64,8,128]{4,3,2,0,1:T(8,128)(2,1)} copy(bf16[8,2,64,8,128]{4,2,1,0,3:T(8,128)(2,1)} %bitcast.209) | data formatting | bytes 4194304 | tf_op jit(solution)/shard_map/transpose | solution.py:255
  71.8 2.8 %reshape.427 = bf16[8,2,64,1024]{3,2,0,1:T(8,128)(2,1)S(1)} reshape(bf16[8,2,64,8,128]{4,3,2,0,1:T(8,128)(2,1)} %copy.53) | data formatting | bytes 4194304 | tf_op jit(solution)/shard_map/reshape | solution.py:256
  77.4 1.7 fusion.47
  81.6 3.4 %fusion.16 = bf16[8,64,1024]{2,1,0:T(8,128)(2,1)S(1)} fusion(bf16[8,128,64]{1,2,0:T(8,128)(2,1)S(1)} %bitcast.210, f32[8,128,1024]{2,1,0:T(8,128)} %copy-done.2, f32[8,128]{1,0:T(8,128)S(1)} %log_add_fusion), kind=kOutput, calls=%fused_computation.31 | convolution fusion | flops 137887744 | bytes 5378048 | tf_op jit(solution)/shard_map/hqd,hqk->hdk/dot_general | solution.py:288
  85.0 2.6 %multiply_convert_fusion = bf16[8,128,1024]{2,1,0:T(8,128)(2,1)S(1)} fusion(f32[8,128,1024]{2,1,0:T(8,128)S(1)} %copy-done.3, bf16[8,128,64]{1,2,0:T(8,128)(2,1)S(1)} %bitcast.211, f32[8,128]{1,0:T(8,128)S(1)} %multiply_reduce_fusion.4, f32[8,128]{1,0:T(8,128)S(1)} %log_add_fusion, bf16[8,2,64,1024]{3,2,0,1:T(8,128)(2,1)} %copy-done.7), kind=kOutput, calls=%fused_computation.6 | convolution fusion | flops 139460608 | bytes 7479296 | tf_op jit(solution)/shard_map/hqd,hdk->hqk/dot_general | solution.py:291
  90.9 2.4 %copy.58 = bf16[4,1024,128]{1,2,0:T(8,128)(2,1)} copy(bf16[4,1024,128]{2,1,0:T(8,128)(2,1)} %bitcast.208) | data formatting | bytes 2097152 | tf_op jit(solution)/shard_map/slice | solution.py:187
  94.6 2.7 %bitcast_convert_fusion = f32[4,1024,128]{2,1,0:T(8,128)} fusion(bf16[4,8,2,64,128]{4,3,2,1,0:T(8,128)(2,1)} %get-tuple-element.11), kind=kLoop, calls=%fused_computation.43 | loop fusion | flops 524288 | bytes 3145728 | tf_op jit(solution)/shard_map/convert_element_type | solution.py:188
  97.3 2.9 %copy.59 = f32[4,1024,128]{1,2,0:T(8,128)} copy(f32[4,1024,128]{2,1,0:T(8,128)} %bitcast_convert_fusion) | data formatting | bytes 4194304 | tf_op jit(solution)/shard_map/convert_element_type | solution.py:188
  100.2 3.9 %fusion.69 = (bf16[4,1024,128]{1,2,0:T(8,128)(2,1)S(1)}, f32[4,1024,128]{1,2,0:T(8,128)}) fusion(f32[4,1024,128]{1,2,0:T(8,128)} %copy.59, bf16[4,1024,128]{1,2,0:T(8,128)(2,1)} %collective-permute-done.4), kind=kLoop, calls=%fused_computation.161 | loop fusion | flops 1572864 | bytes 6291456 | tf_op jit(solution)/shard_map/convert.8
  111.0 3.5 %collective-permute-done.5 = bf16[1024,128]{0,1:T(8,128)(2,1)} collective-permute-done((bf16[1024,128]{0,1:T(8,128)(2,1)}, bf16[1024,128]{0,1:T(8,128)(2,1)}, u32[]{:S(2)}, u32[]{:S(2)}) %collective-permute-start.5) | collective-permute-done | bytes 262176 | tf_op jit(solution)/shard_map/ppermute | solution.py:191
  114.5 5.7 %collective-permute-done.7 = bf16[1024,128]{0,1:T(8,128)(2,1)} collective-permute-done((bf16[1024,128]{0,1:T(8,128)(2,1)}, bf16[1024,128]{0,1:T(8,128)(2,1)}, u32[]{:S(2)}, u32[]{:S(2)}) %collective-permute-start.7) | collective-permute-done | bytes 262176 | tf_op jit(solution)/shard_map/ppermute | solution.py:191
  124.6 2.6 %copy-done.6 = f32[2,2,2,2,2,32,1536]{6,5,4,3,2,1,0:T(8,128)} copy-done((f32[2,2,2,2,2,32,1536]{6,5,4,3,2,1,0:T(8,128)}, f32[2,2,2,2,2,32,1536]{6,5,4,3,2,1,0:T(8,128)S(1)}, u32[]{:S(2)}) %copy-start.6) | copy-done | bytes 6291480
  130.0 3.0 %collective-permute-done.18 = bf16[2,2,2,2,16,1024]{5,4,3,2,1,0:T(8,128)(2,1)} collective-permute-done((bf16[2,2,2,2,16,1024]{5,4,3,2,1,0:T(8,128)(2,1)S(1)}, bf16[2,2,2,2,16,1024]{5,4,3,2,1,0:T(8,128)(2,1)}, u32[]{:S(2)}, u32[]{:S(2)}) %collective-permute-start.18) | collective-permute-done | bytes 524320 | tf_op jit(solution)/shard_map/ppermute | solution.py:153
  135.6 2.9 %bitcast_add_fusion = f32[2,2,2,2,32,1536]{5,4,3,2,1,0:T(8,128)S(1)} fusion(bf16[2,2,2,2,32,1536]{5,4,3,2,1,0:T(8,128)(2,1)} %collective-permute-done.13, f32[2,2,2,2,2,32,1536]{6,5,4,3,2,1,0:T(8,128)} %copy-done.6, s32[]{:T(128)S(6)} %select_n.233), kind=kLoop, calls=%fused_computation.13 | loop fusion | flops 1572864 | bytes 7864324 | tf_op jit(solution)/shard_map/add | solution.py:157
  138.5 1.6 copy-done.4
  143.5 3.3 %fusion.22 = f32[1024]{0:T(1024)S(1)} fusion(bf16[1024,1536]{1,0:T(8,128)(2,1)} %param.9, bf16[128,1024]{1,0:T(8,128)(2,1)S(1)} %scatter_custom_fusion, f32[128]{0:T(128)S(1)} %copy-done.32, f32[128]{0:T(128)S(1)} %broadcast_multiply_fusion.1, bf16[128,1024]{1,0:T(8,128)(2,1)S(1)} %copy-done.18, bf16[128,512]{1,0:T(8,128)(2,1)S(1)} %copy-done.20), kind=kOutput, calls=%fused_computation.35 | convolution fusion | flops 404093952 | bytes 3806208 | tf_op jit(solution)/shard_map/dot_general | solution.py:300
  147.6 6.2 %collective-permute-done.14 = bf16[2,2,2,32,1536]{4,3,2,1,0:T(8,128)(2,1)S(1)} collective-permute-done((bf16[2,2,2,32,1536]{4,3,2,1,0:T(8,128)(2,1)S(1)}, bf16[2,2,2,32,1536]{4,3,2,1,0:T(8,128)(2,1)S(1)}, u32[]{:S(2)}, u32[]{:S(2)}) %collective-permute-start.14) | collective-permute-done | bytes 786464 | tf_op jit(solution)/shard_map/ppermute | solution.py:155
  157.1 1.6 collective-permute-start.21
  162.3 1.6 collective-permute-start.16
  165.4 2.6 %collective-permute-start.22 = (bf16[16,1024]{1,0:T(8,128)(2,1)S(1)}, bf16[16,1024]{1,0:T(8,128)(2,1)S(1)}, u32[]{:S(2)}, u32[]{:S(2)}) collective-permute-start(bf16[16,1024]{1,0:T(8,128)(2,1)S(1)} %fusion.60), channel_id=1, source_target_pairs={{0,2},{1,3},{2,0},{3,1},{4,6},{5,7},{6,4},{7,5},{8,10},{9,11},{10,... | collective-permute-start | bytes 98312 | tf_op jit(solution)/shard_map/ppermute | solution.py:164
  168.2 2.6 %collective-permute-start.12 = (f32[1025]{0:T(1024)S(1)}, f32[1025]{0:T(1024)S(1)}, u32[]{:S(2)}, u32[]{:S(2)}) collective-permute-start(f32[1025]{0:T(1024)S(1)} %add.317), channel_id=1, source_target_pairs={{0,2},{1,3},{2,0},{3,1},{4,6},{5,7},{6,4},{7,5},{8,10},{9,11},{10,... | collective-permute-start | bytes 12308 | tf_op jit(solution)/shard_map/ppermute | solution.py:166
  (195 shorter events, 68.8 us)
Async XLA Ops:
  0.6 15.2 %copy-start = (bf16[1,512,1024]{2,1,0:T(8,128)(2,1)S(1)}, bf16[1,512,1024]{2,1,0:T(8,128)(2,1)}, u32[]{:S(2)}) copy-start(bf16[1,512,1024]{2,1,0:T(8,128)(2,1)} %param.7) | copy-start | bytes 3145732
  0.6 16.2 %copy-start.9 = (bf16[1,512,1024]{2,1,0:T(8,128)(2,1)S(1)}, bf16[1,512,1024]{2,1,0:T(8,128)(2,1)}, u32[]{:S(2)}) copy-start(bf16[1,512,1024]{2,1,0:T(8,128)(2,1)} %param.6) | copy-start | bytes 3145732
  3.4 9.8 %all-to-all-start = ((s32[8,1,1]{2,1,0:T(1,128)}), s32[8,1,1]{2,1,0:T(1,128)S(1)}, u32[]{:S(2)}, u32[]{:S(2)}) async-start(s32[8,1,1]{2,1,0:T(1,128)} %broadcast_in_dim.40), calls=%async_computation | async-start | bytes 8192 | tf_op jit(solution)/shard_map/all_to_all | solution.py:206
  20.1 18.0 %copy-start.22 = (f32[1024]{0:T(1024)S(1)}, f32[1024]{0:T(1024)}, u32[]{:S(2)}) copy-start(f32[1024]{0:T(1024)} %param.11) | copy-start | bytes 12292
  21.1 11.7 %all-to-all-start.1 = ((bf16[8,24,1024]{2,1,0:T(8,128)(2,1)}), bf16[8,24,1024]{2,1,0:T(8,128)(2,1)S(1)}, u32[]{:S(2)}, u32[]{:S(2)}) async-start(bf16[8,24,1024]{2,1,0:T(8,128)(2,1)} %get-tuple-element.16), calls=%async_computation.1 | async-start | bytes 786432 | tf_op jit(solution)/shard_map/all_to_all | solution.py:224
  32.8 11.7 %all-to-all-start.2 = ((bf16[8,24,1024]{2,1,0:T(8,128)(2,1)}), bf16[8,24,1024]{2,1,0:T(8,128)(2,1)S(1)}, u32[]{:S(2)}, u32[]{:S(2)}) async-start(bf16[8,24,1024]{2,1,0:T(8,128)(2,1)} %get-tuple-element.15), calls=%async_computation.2 | async-start | bytes 786432 | tf_op jit(solution)/shard_map/all_to_all | solution.py:225
  38.3 18.7 %copy-start.12 = (bf16[128,1024]{1,0:T(8,128)(2,1)}, bf16[128,1024]{1,0:T(8,128)(2,1)S(1)}, u32[]{:S(2)}) copy-start(bf16[128,1024]{1,0:T(8,128)(2,1)S(1)} %fusion.29) | copy-start | bytes 786436
  40.5 10.1 %collective-permute-start.2 = (bf16[1024,128]{0,1:T(8,128)(2,1)S(1)}, bf16[1024,128]{0,1:T(8,128)(2,1)S(1)}, u32[]{:S(2)}, u32[]{:S(2)}) collective-permute-start(bf16[1024,128]{0,1:T(8,128)(2,1)S(1)} %bitcast.223), channel_id=1, source_target_pairs={{0,24},{4,28},{8,16},{12,20},{16,8},{20,12},{24,0},{28,4},{1,25},{... | collective-permute-start | bytes 786440 | tf_op jit(solution)/shard_map/ppermute | solution.py:179
  43.4 12.4 %collective-permute-start.1 = (bf16[1024,128]{0,1:T(8,128)(2,1)S(1)}, bf16[1024,128]{0,1:T(8,128)(2,1)S(1)}, u32[]{:S(2)}, u32[]{:S(2)}) collective-permute-start(bf16[1024,128]{0,1:T(8,128)(2,1)S(1)} %bitcast.224), channel_id=1, source_target_pairs={{0,16},{4,20},{8,24},{12,28},{16,0},{20,4},{24,8},{28,12},{1,17},{... | collective-permute-start | bytes 786440 | tf_op jit(solution)/shard_map/ppermute | solution.py:179
  43.9 12.0 %collective-permute-start = (bf16[1024,128]{0,1:T(8,128)(2,1)S(1)}, bf16[1024,128]{0,1:T(8,128)(2,1)S(1)}, u32[]{:S(2)}, u32[]{:S(2)}) collective-permute-start(bf16[1024,128]{0,1:T(8,128)(2,1)S(1)} %bitcast.225), channel_id=1, source_target_pairs={{0,8},{4,12},{8,0},{12,4},{16,24},{20,28},{24,16},{28,20},{1,9},{5... | collective-permute-start | bytes 786440 | tf_op jit(solution)/shard_map/ppermute | solution.py:179
  57.1 7.4 %collective-permute-start.3 = (bf16[4,1024,128]{1,2,0:T(8,128)(2,1)}, bf16[4,1024,128]{1,2,0:T(8,128)(2,1)}, u32[]{:S(2)}, u32[]{:S(2)}) collective-permute-start(bf16[4,1024,128]{1,2,0:T(8,128)(2,1)} %pad_maximum_fusion), channel_id=1, source_target_pairs={{0,4},{4,0},{8,12},{12,8},{16,20},{20,16},{24,28},{28,24},{1,5},{5... | collective-permute-start | bytes 3145736 | tf_op jit(solution)/shard_map/ppermute | solution.py:181
  58.9 21.4 %copy-start.23 = (f32[128]{0:T(128)}, f32[128]{0:T(128)S(1)}, u32[]{:S(2)}) copy-start(f32[128]{0:T(128)S(1)} %add_rsqrt_fusion) | copy-start | bytes 1540
  93.2 6.9 %collective-permute-start.4 = (bf16[4,1024,128]{1,2,0:T(8,128)(2,1)}, bf16[4,1024,128]{1,2,0:T(8,128)(2,1)}, u32[]{:S(2)}, u32[]{:S(2)}) collective-permute-start(bf16[4,1024,128]{1,2,0:T(8,128)(2,1)} %copy.58), channel_id=1, source_target_pairs={{0,4},{4,0},{8,12},{12,8},{16,20},{20,16},{24,28},{28,24},{1,5},{5... | collective-permute-start | bytes 3145736 | tf_op jit(solution)/shard_map/ppermute | solution.py:187
  105.0 9.5 %collective-permute-start.5 = (bf16[1024,128]{0,1:T(8,128)(2,1)}, bf16[1024,128]{0,1:T(8,128)(2,1)}, u32[]{:S(2)}, u32[]{:S(2)}) collective-permute-start(bf16[1024,128]{0,1:T(8,128)(2,1)} %get-tuple-element.12), channel_id=1, source_target_pairs={{0,8},{4,12},{8,0},{12,4},{16,24},{20,28},{24,16},{28,20},{1,9},{5... | collective-permute-start | bytes 786440 | tf_op jit(solution)/shard_map/ppermute | solution.py:191
  106.5 13.7 %collective-permute-start.7 = (bf16[1024,128]{0,1:T(8,128)(2,1)}, bf16[1024,128]{0,1:T(8,128)(2,1)}, u32[]{:S(2)}, u32[]{:S(2)}) collective-permute-start(bf16[1024,128]{0,1:T(8,128)(2,1)} %get-tuple-element.13), channel_id=1, source_target_pairs={{0,24},{4,28},{8,16},{12,20},{16,8},{20,12},{24,0},{28,4},{1,25},{... | collective-permute-start | bytes 786440 | tf_op jit(solution)/shard_map/ppermute | solution.py:191
  107.9 15.8 %copy-start.16 = (bf16[128,1024]{0,1:T(8,128)(2,1)S(1)}, bf16[128,1024]{0,1:T(8,128)(2,1)}, u32[]{:S(2)}) copy-start(bf16[128,1024]{0,1:T(8,128)(2,1)} %copy.61) | copy-start | bytes 786436
  107.9 13.6 %collective-permute-start.6 = (bf16[1024,128]{0,1:T(8,128)(2,1)}, bf16[1024,128]{0,1:T(8,128)(2,1)}, u32[]{:S(2)}, u32[]{:S(2)}) collective-permute-start(bf16[1024,128]{0,1:T(8,128)(2,1)} %get-tuple-element.14), channel_id=1, source_target_pairs={{0,16},{4,20},{8,24},{12,28},{16,0},{20,4},{24,8},{28,12},{1,17},{... | collective-permute-start | bytes 786440 | tf_op jit(solution)/shard_map/ppermute | solution.py:191
  128.8 6.9 %collective-permute-start.13 = (bf16[2,2,2,2,32,1536]{5,4,3,2,1,0:T(8,128)(2,1)}, bf16[2,2,2,2,32,1536]{5,4,3,2,1,0:T(8,128)(2,1)}, u32[]{:S(2)}, u32[]{:S(2)}) collective-permute-start(bf16[2,2,2,2,32,1536]{5,4,3,2,1,0:T(8,128)(2,1)} %fusion.13), channel_id=1, source_target_pairs={{0,4},{4,0},{8,12},{12,8},{16,20},{20,16},{24,28},{28,24},{1,5},{5... | collective-permute-start | bytes 4718600 | tf_op jit(solution)/shard_map/ppermute | solution.py:155
  129.5 3.6 %collective-permute-start.18 = (bf16[2,2,2,2,16,1024]{5,4,3,2,1,0:T(8,128)(2,1)S(1)}, bf16[2,2,2,2,16,1024]{5,4,3,2,1,0:T(8,128)(2,1)}, u32[]{:S(2)}, u32[]{:S(2)}) collective-permute-start(bf16[2,2,2,2,16,1024]{5,4,3,2,1,0:T(8,128)(2,1)S(1)} %fusion.33), channel_id=1, source_target_pairs={{0,4},{4,0},{8,12},{12,8},{16,20},{20,16},{24,28},{28,24},{1,5},{5... | collective-permute-start | bytes 1572872 | tf_op jit(solution)/shard_map/ppermute | solution.py:153
  135.0 6.8 %collective-permute-start.19 = (bf16[2,2,2,16,1024]{4,3,2,1,0:T(8,128)(2,1)}, bf16[2,2,2,16,1024]{4,3,2,1,0:T(8,128)(2,1)}, u32[]{:S(2)}, u32[]{:S(2)}) collective-permute-start(bf16[2,2,2,16,1024]{4,3,2,1,0:T(8,128)(2,1)} %fusion.38), channel_id=1, source_target_pairs={{0,8},{4,20},{8,0},{12,28},{16,24},{20,4},{24,16},{28,12},{1,9},{5... | collective-permute-start | bytes 786440 | tf_op jit(solution)/shard_map/ppermute | solution.py:153
  140.3 13.5 %collective-permute-start.14 = (bf16[2,2,2,32,1536]{4,3,2,1,0:T(8,128)(2,1)S(1)}, bf16[2,2,2,32,1536]{4,3,2,1,0:T(8,128)(2,1)S(1)}, u32[]{:S(2)}, u32[]{:S(2)}) collective-permute-start(bf16[2,2,2,32,1536]{4,3,2,1,0:T(8,128)(2,1)S(1)} %fusion.14), channel_id=1, source_target_pairs={{0,8},{4,20},{8,0},{12,28},{16,24},{20,4},{24,16},{28,12},{1,9},{5... | collective-permute-start | bytes 2359304 | tf_op jit(solution)/shard_map/ppermute | solution.py:155
  142.9 12.9 %collective-permute-start.20 = (bf16[2,2,16,1024]{3,2,1,0:T(8,128)(2,1)S(1)}, bf16[2,2,16,1024]{3,2,1,0:T(8,128)(2,1)S(1)}, u32[]{:S(2)}, u32[]{:S(2)}) collective-permute-start(bf16[2,2,16,1024]{3,2,1,0:T(8,128)(2,1)S(1)} %fusion.50), channel_id=1, source_target_pairs={{0,16},{4,12},{8,24},{12,4},{16,0},{20,28},{24,8},{28,20},{1,17},{... | collective-permute-start | bytes 393224 | tf_op jit(solution)/shard_map/ppermute | solution.py:153
  147.5 8.3 %collective-permute-start.8 = (f32[1025]{0:T(1024)S(1)}, f32[1025]{0:T(1024)S(1)}, u32[]{:S(2)}, u32[]{:S(2)}) collective-permute-start(f32[1025]{0:T(1024)S(1)} %pad_maximum_fusion.4), channel_id=1, source_target_pairs={{0,4},{4,0},{8,12},{12,8},{16,20},{20,16},{24,28},{28,24},{1,5},{5... | collective-permute-start | bytes 12308 | tf_op jit(solution)/shard_map/ppermute | solution.py:155
  154.3 7.9 %collective-permute-start.15 = (bf16[2,2,32,1536]{3,2,1,0:T(8,128)(2,1)S(1)}, bf16[2,2,32,1536]{3,2,1,0:T(8,128)(2,1)S(1)}, u32[]{:S(2)}, u32[]{:S(2)}) collective-permute-start(bf16[2,2,32,1536]{3,2,1,0:T(8,128)(2,1)S(1)} %fusion.40), channel_id=1, source_target_pairs={{0,16},{4,12},{8,24},{12,4},{16,0},{20,28},{24,8},{28,20},{1,17},{... | collective-permute-start | bytes 1179656 | tf_op jit(solution)/shard_map/ppermute | solution.py:155
  156.5 3.7 %collective-permute-start.9 = (f32[1025]{0:T(1024)S(1)}, f32[1025]{0:T(1024)S(1)}, u32[]{:S(2)}, u32[]{:S(2)}) collective-permute-start(f32[1025]{0:T(1024)S(1)} %fusion.64), channel_id=1, source_target_pairs={{0,8},{4,20},{8,0},{12,28},{16,24},{20,4},{24,16},{28,12},{1,9},{5... | collective-permute-start | bytes 12308 | tf_op jit(solution)/shard_map/ppermute | solution.py:155
  157.1 6.9 %collective-permute-start.21 = (bf16[2,16,1024]{2,1,0:T(8,128)(2,1)S(1)}, bf16[2,16,1024]{2,1,0:T(8,128)(2,1)S(1)}, u32[]{:S(2)}, u32[]{:S(2)}) collective-permute-start(bf16[2,16,1024]{2,1,0:T(8,128)(2,1)S(1)} %fusion.58), channel_id=1, source_target_pairs={{0,1},{1,0},{2,3},{3,2},{4,5},{5,4},{6,7},{7,6},{8,9},{9,8},{10,11... | collective-permute-start | bytes 196616 | tf_op jit(solution)/shard_map/ppermute | solution.py:164
  160.2 3.8 %collective-permute-start.10 = (f32[1025]{0:T(1024)S(1)}, f32[1025]{0:T(1024)S(1)}, u32[]{:S(2)}, u32[]{:S(2)}) collective-permute-start(f32[1025]{0:T(1024)S(1)} %add.315), channel_id=1, source_target_pairs={{0,16},{4,12},{8,24},{12,4},{16,0},{20,28},{24,8},{28,20},{1,17},{... | collective-permute-start | bytes 12308 | tf_op jit(solution)/shard_map/ppermute | solution.py:155
  162.3 8.5 %collective-permute-start.16 = (bf16[2,32,1536]{2,1,0:T(8,128)(2,1)S(1)}, bf16[2,32,1536]{2,1,0:T(8,128)(2,1)S(1)}, u32[]{:S(2)}, u32[]{:S(2)}) collective-permute-start(bf16[2,32,1536]{2,1,0:T(8,128)(2,1)S(1)} %fusion.49), channel_id=1, source_target_pairs={{0,1},{1,0},{2,3},{3,2},{4,5},{5,4},{6,7},{7,6},{8,9},{9,8},{10,11... | collective-permute-start | bytes 589832 | tf_op jit(solution)/shard_map/ppermute | solution.py:166
  164.0 4.2 %collective-permute-start.11 = (f32[1025]{0:T(1024)S(1)}, f32[1025]{0:T(1024)S(1)}, u32[]{:S(2)}, u32[]{:S(2)}) collective-permute-start(f32[1025]{0:T(1024)S(1)} %add.316), channel_id=1, source_target_pairs={{0,1},{1,0},{2,3},{3,2},{4,5},{5,4},{6,7},{7,6},{8,9},{9,8},{10,11... | collective-permute-start | bytes 12308 | tf_op jit(solution)/shard_map/ppermute | solution.py:166
  165.4 5.9 %collective-permute-start.22 = (bf16[16,1024]{1,0:T(8,128)(2,1)S(1)}, bf16[16,1024]{1,0:T(8,128)(2,1)S(1)}, u32[]{:S(2)}, u32[]{:S(2)}) collective-permute-start(bf16[16,1024]{1,0:T(8,128)(2,1)S(1)} %fusion.60), channel_id=1, source_target_pairs={{0,2},{1,3},{2,0},{3,1},{4,6},{5,7},{6,4},{7,5},{8,10},{9,11},{10,... | collective-permute-start | bytes 98312 | tf_op jit(solution)/shard_map/ppermute | solution.py:164
  168.2 5.0 %collective-permute-start.12 = (f32[1025]{0:T(1024)S(1)}, f32[1025]{0:T(1024)S(1)}, u32[]{:S(2)}, u32[]{:S(2)}) collective-permute-start(f32[1025]{0:T(1024)S(1)} %add.317), channel_id=1, source_target_pairs={{0,2},{1,3},{2,0},{3,1},{4,6},{5,7},{6,4},{7,5},{8,10},{9,11},{10,... | collective-permute-start | bytes 12308 | tf_op jit(solution)/shard_map/ppermute | solution.py:166
  170.9 5.6 %collective-permute-start.17 = (bf16[32,1536]{1,0:T(8,128)(2,1)S(1)}, bf16[32,1536]{1,0:T(8,128)(2,1)S(1)}, u32[]{:S(2)}, u32[]{:S(2)}) collective-permute-start(bf16[32,1536]{1,0:T(8,128)(2,1)S(1)} %fusion.57), channel_id=1, source_target_pairs={{0,2},{1,3},{2,0},{3,1},{4,6},{5,7},{6,4},{7,5},{8,10},{9,11},{10,... | collective-permute-start | bytes 294920 | tf_op jit(solution)/shard_map/ppermute | solution.py:166
  (27 other events, 100.5 us)

commit v9 on v8

--- a/solution.py
+++ b/solution.py
@@ -295,13 +295,14 @@
     d_pairs = jnp.stack([d_key_t, d_value_t], axis=1).reshape(heads, 2, HEAD_DIM, shards, rows)
     d_pairs = d_pairs.transpose(3, 0, 1, 2, 4).reshape(shards, 2 * inner, rows).astype(jnp.bfloat16)
     accum = return_blocks(d_pairs)
+    grad_out, unused = halving_scatter(grad_wout)
+    grad_out, accum = lax.optimization_barrier((grad_out, accum))
     d_proj = jnp.concatenate([d_query.reshape(rows, inner), accum.T], axis=1).astype(jnp.bfloat16)
     grad_wqkv = jnp.dot(exchange_order(hidden).T, d_proj, preferred_element_type=jnp.float32)
     d_hidden = jnp.dot(d_proj, w_qkv.T, preferred_element_type=jnp.float32)
     grad_ln = jnp.sum(d_hidden * normed, axis=0)
     loss_part = jnp.sum(token_loss)
     small = jnp.concatenate([grad_ln, loss_part.reshape(1)])
-    grad_out, unused = halving_scatter(grad_wout)
     grad_qkv, small = halving_scatter(grad_wqkv, small)
     count_all = shards * lax.axis_size("clip") * TOK_DEV
     return (small[-1] / count_all, grad_qkv.reshape(-1), grad_out.reshape(-1), small[:-1])

time: 179 us -> 187 us (1.045)
  waiting for transfers between devices: 47.4 us -> 68.1 us
  local copies, waits for them, and re-layouts: 46 us -> 39.6 us
  matrix products: 19.9 us -> 15.8 us
  other arithmetic: 25.8 us -> 22 us
    ppermute x6, waiting for transfers between devices: 8.84 us -> 24.6 us  [halving_scatter(): lax.ppermute((give.astype(jnp.bfloat16), small), 'seq', pairs)]
    ppermute x4, waiting for transfers between devices: 2.99 us -> 7.95 us  [halving_scatter(): lax.ppermute((give.astype(jnp.bfloat16), small), 'clip', pairs)]
    unnamed x73 -> x51, local copies, waits for them, and re-layouts: 10.3 us -> 5.42 us
    dot_general x1, matrix products: 3.35 us -> 1.14 us  [per_device(): d_hidden = jnp.dot(d_proj, w_qkv.T, preferred_element_type=jnp.float32)]
    ppermute x4, starting transfers between devices: 6.03 us -> 4.01 us  [halving_scatter(): lax.ppermute((give.astype(jnp.bfloat16), small), 'clip', pairs)]
    add x9 -> x10, other arithmetic: 5.75 us -> 4.12 us  [halving_scatter(): data = keep + got.astype(jnp.float32)]
  transfers between devices with their start and end apart: 26 -> 26, of which waited for: 16 -> 18; matrix products, arithmetic and copies ran while one was open for 20% -> 22% of each run, Pallas kernels for 0% -> 0%
where the time goes in v9:
time: 187 us; the launch traced here: 186 us
  waiting for transfers between devices  68.1 us (36%)
  local copies, waits for them, and re-layouts  39.6 us (21%)
  starting transfers between devices  37.1 us (20%)
  other arithmetic  22 us (12%)
  matrix products  15.8 us (8%)
  between operations  3.14 us (2%)
    ppermute x6, waiting for transfers between devices, halving_scatter(): lax.ppermute((give.astype(jnp.bfloat16), small), 'seq', pairs)  24.6 us
    ppermute x3, waiting for transfers between devices, return_blocks(): sent = lax.ppermute(summed[k].astype(jnp.bfloat16), 'seq', xor_pairs(2 * k))  10.3 us
    ppermute x3, waiting for transfers between devices, gather_blocks(): lax.ppermute(block, 'seq', xor_pairs(2 * k))  9.77 us
    all_to_all x1, waiting for transfers between devices, per_device(): lax.all_to_all(send_tokens, 'seq', split_axis=0, concat_axis=0, tiled=True)  8.09 us
    ppermute x4, waiting for transfers between devices, halving_scatter(): lax.ppermute((give.astype(jnp.bfloat16), small), 'clip', pairs)  7.95 us
    ppermute x6, starting transfers between devices, halving_scatter(): lax.ppermute((give.astype(jnp.bfloat16), small), 'seq', pairs)  6.2 us
    unnamed x51, local copies, waits for them, and re-layouts  5.42 us
    all_to_all x1, starting transfers between devices, per_device(): lax.all_to_all(jnp.broadcast_to(kept_count.reshape(1, 1), (shards, 1)), '...  5.17 us
  transfers between devices with their start and end apart: 26, of which 18 were waited for; matrix products, arithmetic and copies ran while one was open for 22% of the time, Pallas kernels for 0%

profile of v9, /device:TPU:0, one launch (start us, length us, event | category | flops | bytes accessed | tf_op | source)
XLA Modules:
  0.0 185.8 jit_solution(17051391793719432673)
XLA Ops:
  3.4 5.2 %all-to-all-start = ((s32[8,1,1]{2,1,0:T(1,128)}), s32[8,1,1]{2,1,0:T(1,128)S(1)}, u32[]{:S(2)}, u32[]{:S(2)}) async-start(s32[8,1,1]{2,1,0:T(1,128)} %broadcast_in_dim.40), calls=%async_computation | async-start | bytes 8192 | tf_op jit(solution)/shard_map/all_to_all | solution.py:206
  9.2 3.9 %all-to-all-done = s32[8,1,1]{2,1,0:T(1,128)S(1)} async-done(((s32[8,1,1]{2,1,0:T(1,128)}), s32[8,1,1]{2,1,0:T(1,128)S(1)}, u32[]{:S(2)}, u32[]{:S(2)}) %all-to-all-start) | async-done | bytes 64 | tf_op jit(solution)/shard_map/all_to_all | solution.py:206
  21.1 3.5 %all-to-all-start.1 = ((bf16[8,24,1024]{2,1,0:T(8,128)(2,1)}), bf16[8,24,1024]{2,1,0:T(8,128)(2,1)S(1)}, u32[]{:S(2)}, u32[]{:S(2)}) async-start(bf16[8,24,1024]{2,1,0:T(8,128)(2,1)} %get-tuple-element.20), calls=%async_computation.1 | async-start | bytes 786432 | tf_op jit(solution)/shard_map/all_to_all | solution.py:224
  24.7 8.1 %all-to-all-done.1 = bf16[8,24,1024]{2,1,0:T(8,128)(2,1)S(1)} async-done(((bf16[8,24,1024]{2,1,0:T(8,128)(2,1)}), bf16[8,24,1024]{2,1,0:T(8,128)(2,1)S(1)}, u32[]{:S(2)}, u32[]{:S(2)}) %all-to-all-start.1) | async-done | bytes 393248 | tf_op jit(solution)/shard_map/all_to_all | solution.py:224
  32.8 3.5 %all-to-all-start.2 = ((bf16[8,24,1024]{2,1,0:T(8,128)(2,1)}), bf16[8,24,1024]{2,1,0:T(8,128)(2,1)S(1)}, u32[]{:S(2)}, u32[]{:S(2)}) async-start(bf16[8,24,1024]{2,1,0:T(8,128)(2,1)} %get-tuple-element.19), calls=%async_computation.2 | async-start | bytes 786432 | tf_op jit(solution)/shard_map/all_to_all | solution.py:225
  38.4 2.1 %fusion.19 = bf16[128,1024]{1,0:T(8,128)(2,1)S(1)} fusion(bf16[128,1024]{1,0:T(8,128)(2,1)S(1)} %fusion.29, bf16[1024,1536]{1,0:T(8,128)(2,1)} %param.9), kind=kOutput, calls=%fused_computation.34 | convolution fusion | flops 268566528 | bytes 2621440 | tf_op jit(solution)/shard_map/dot_general | solution.py:251
  40.5 2.9 %collective-permute-start.2 = (bf16[1024,128]{0,1:T(8,128)(2,1)S(1)}, bf16[1024,128]{0,1:T(8,128)(2,1)S(1)}, u32[]{:S(2)}, u32[]{:S(2)}) collective-permute-start(bf16[1024,128]{0,1:T(8,128)(2,1)S(1)} %bitcast.217), channel_id=1, source_target_pairs={{0,24},{4,28},{8,16},{12,20},{16,8},{20,12},{24,0},{28,4},{1,25},{... | collective-permute-start | bytes 786440 | tf_op jit(solution)/shard_map/ppermute | solution.py:179
  44.6 1.6 scatter_custom_fusion.1
  46.2 4.4 %collective-permute-done.2 = bf16[1024,128]{0,1:T(8,128)(2,1)S(1)} collective-permute-done((bf16[1024,128]{0,1:T(8,128)(2,1)S(1)}, bf16[1024,128]{0,1:T(8,128)(2,1)S(1)}, u32[]{:S(2)}, u32[]{:S(2)}) %collective-permute-start.2) | collective-permute-done | bytes 262176 | tf_op jit(solution)/shard_map/ppermute | solution.py:179
  50.6 5.2 %collective-permute-done.1 = bf16[1024,128]{0,1:T(8,128)(2,1)S(1)} collective-permute-done((bf16[1024,128]{0,1:T(8,128)(2,1)S(1)}, bf16[1024,128]{0,1:T(8,128)(2,1)S(1)}, u32[]{:S(2)}, u32[]{:S(2)}) %collective-permute-start.1) | collective-permute-done | bytes 262176 | tf_op jit(solution)/shard_map/ppermute | solution.py:179
  62.8 1.6 copy.52
  65.5 4.7 %copy.53 = bf16[8,2,64,8,128]{4,3,2,0,1:T(8,128)(2,1)} copy(bf16[8,2,64,8,128]{4,2,1,0,3:T(8,128)(2,1)} %bitcast.203) | data formatting | bytes 4194304 | tf_op jit(solution)/shard_map/transpose | solution.py:255
  70.2 2.8 %reshape.427 = bf16[8,2,64,1024]{3,2,0,1:T(8,128)(2,1)S(1)} reshape(bf16[8,2,64,8,128]{4,3,2,0,1:T(8,128)(2,1)} %copy.53) | data formatting | bytes 4194304 | tf_op jit(solution)/shard_map/reshape | solution.py:256
  75.8 1.7 fusion.45
  80.7 3.4 %fusion.16 = bf16[8,64,1024]{2,1,0:T(8,128)(2,1)S(1)} fusion(bf16[8,128,64]{1,2,0:T(8,128)(2,1)S(1)} %bitcast.204, f32[8,128,1024]{2,1,0:T(8,128)} %copy-done.2, f32[8,128]{1,0:T(8,128)S(1)} %log_add_fusion), kind=kOutput, calls=%fused_computation.31 | convolution fusion | flops 137887744 | bytes 5378048 | tf_op jit(solution)/shard_map/hqd,hqk->hdk/dot_general | solution.py:288
  89.3 3.2 %collective-permute-done.5 = bf16[2,2,2,16,1024]{4,3,2,1,0:T(8,128)(2,1)S(1)} collective-permute-done((bf16[2,2,2,16,1024]{4,3,2,1,0:T(8,128)(2,1)S(1)}, bf16[2,2,2,16,1024]{4,3,2,1,0:T(8,128)(2,1)S(1)}, u32[]{:S(2)}, u32[]{:S(2)}) %collective-permute-start.5) | collective-permute-done | bytes 262176 | tf_op jit(solution)/shard_map/ppermute | solution.py:153
  96.0 2.3 %copy.59 = bf16[4,1024,128]{1,2,0:T(8,128)(2,1)} copy(bf16[4,1024,128]{2,1,0:T(8,128)(2,1)} %bitcast.202) | data formatting | bytes 2097152 | tf_op jit(solution)/shard_map/slice | solution.py:187
  98.3 1.8 copy.62
  101.9 1.6 collective-permute-start.7
  105.1 2.9 %copy.60 = f32[4,1024,128]{1,2,0:T(8,128)} copy(f32[4,1024,128]{2,1,0:T(8,128)} %bitcast_convert_fusion) | data formatting | bytes 4194304 | tf_op jit(solution)/shard_map/convert_element_type | solution.py:188
  109.5 2.6 %collective-permute-start.8 = (bf16[16,1024]{1,0:T(8,128)(2,1)}, bf16[16,1024]{1,0:T(8,128)(2,1)}, u32[]{:S(2)}, u32[]{:S(2)}) collective-permute-start(bf16[16,1024]{1,0:T(8,128)(2,1)} %fusion.57), channel_id=1, source_target_pairs={{0,2},{1,3},{2,0},{3,1},{4,6},{5,7},{6,4},{7,5},{8,10},{9,11},{10,... | collective-permute-start | bytes 98312 | tf_op jit(solution)/shard_map/ppermute | solution.py:164
  112.1 3.7 %fusion.66 = (bf16[4,1024,128]{1,2,0:T(8,128)(2,1)S(1)}, f32[4,1024,128]{1,2,0:T(8,128)}) fusion(f32[4,1024,128]{1,2,0:T(8,128)} %copy.60, bf16[4,1024,128]{1,2,0:T(8,128)(2,1)} %collective-permute-done.9), kind=kLoop, calls=%fused_computation.159 | loop fusion | flops 1572864 | bytes 6291456 | tf_op jit(solution)/shard_map/convert.8
  122.0 4.1 %collective-permute-done.10 = bf16[1024,128]{0,1:T(8,128)(2,1)S(1)} collective-permute-done((bf16[1024,128]{0,1:T(8,128)(2,1)}, bf16[1024,128]{0,1:T(8,128)(2,1)S(1)}, u32[]{:S(2)}, u32[]{:S(2)}) %collective-permute-start.10) | collective-permute-done | bytes 262176 | tf_op jit(solution)/shard_map/ppermute | solution.py:191
  126.2 4.7 %collective-permute-done.12 = bf16[1024,128]{0,1:T(8,128)(2,1)S(1)} collective-permute-done((bf16[1024,128]{0,1:T(8,128)(2,1)}, bf16[1024,128]{0,1:T(8,128)(2,1)S(1)}, u32[]{:S(2)}, u32[]{:S(2)}) %collective-permute-start.12) | collective-permute-done | bytes 262176 | tf_op jit(solution)/shard_map/ppermute | solution.py:191
  134.9 3.4 %collective-permute-done.18 = bf16[2,2,2,2,32,1536]{5,4,3,2,1,0:T(8,128)(2,1)S(1)} collective-permute-done((bf16[2,2,2,2,32,1536]{5,4,3,2,1,0:T(8,128)(2,1)S(1)}, bf16[2,2,2,2,32,1536]{5,4,3,2,1,0:T(8,128)(2,1)S(1)}, u32[]{:S(2)}, u32[]{:S(2)}) %collective-permute-start.18) | collective-permute-done | bytes 1572896 | tf_op jit(solution)/shard_map/ppermute | solution.py:155
  140.5 10.5 %collective-permute-done.19 = bf16[2,2,2,32,1536]{4,3,2,1,0:T(8,128)(2,1)S(1)} collective-permute-done((bf16[2,2,2,32,1536]{4,3,2,1,0:T(8,128)(2,1)S(1)}, bf16[2,2,2,32,1536]{4,3,2,1,0:T(8,128)(2,1)S(1)}, u32[]{:S(2)}, u32[]{:S(2)}) %collective-permute-start.19) | collective-permute-done | bytes 786464 | tf_op jit(solution)/shard_map/ppermute | solution.py:155
  153.0 6.3 %collective-permute-done.20 = bf16[2,2,32,1536]{3,2,1,0:T(8,128)(2,1)S(1)} collective-permute-done((bf16[2,2,32,1536]{3,2,1,0:T(8,128)(2,1)S(1)}, bf16[2,2,32,1536]{3,2,1,0:T(8,128)(2,1)S(1)}, u32[]{:S(2)}, u32[]{:S(2)}) %collective-permute-start.20) | collective-permute-done | bytes 393248 | tf_op jit(solution)/shard_map/ppermute | solution.py:155
  162.0 3.3 %collective-permute-done.21 = bf16[2,32,1536]{2,1,0:T(8,128)(2,1)S(1)} collective-permute-done((bf16[2,32,1536]{2,1,0:T(8,128)(2,1)S(1)}, bf16[2,32,1536]{2,1,0:T(8,128)(2,1)S(1)}, u32[]{:S(2)}, u32[]{:S(2)}) %collective-permute-start.21) | collective-permute-done | bytes 196640 | tf_op jit(solution)/shard_map/ppermute | solution.py:166
  168.1 2.2 %collective-permute-done.14 = f32[1025]{0:T(1024)S(1)} collective-permute-done((f32[1025]{0:T(1024)S(1)}, f32[1025]{0:T(1024)S(1)}, u32[]{:S(2)}, u32[]{:S(2)}) %collective-permute-start.14) | collective-permute-done | bytes 4132 | tf_op jit(solution)/shard_map/ppermute | solution.py:155
  171.7 2.2 %collective-permute-done.15 = f32[1025]{0:T(1024)S(1)} collective-permute-done((f32[1025]{0:T(1024)S(1)}, f32[1025]{0:T(1024)S(1)}, u32[]{:S(2)}, u32[]{:S(2)}) %collective-permute-start.15) | collective-permute-done | bytes 4132 | tf_op jit(solution)/shard_map/ppermute | solution.py:155
  174.4 3.2 %collective-permute-done.16 = f32[1025]{0:T(1024)S(1)} collective-permute-done((f32[1025]{0:T(1024)S(1)}, f32[1025]{0:T(1024)S(1)}, u32[]{:S(2)}, u32[]{:S(2)}) %collective-permute-start.16) | collective-permute-done | bytes 4132 | tf_op jit(solution)/shard_map/ppermute | solution.py:166
  177.6 2.4 %collective-permute-start.17 = (f32[1025]{0:T(1024)S(1)}, f32[1025]{0:T(1024)S(1)}, u32[]{:S(2)}, u32[]{:S(2)}) collective-permute-start(f32[1025]{0:T(1024)S(1)} %add.332), channel_id=1, source_target_pairs={{0,2},{1,3},{2,0},{3,1},{4,6},{5,7},{6,4},{7,5},{8,10},{9,11},{10,... | collective-permute-start | bytes 12308 | tf_op jit(solution)/shard_map/ppermute | solution.py:166
  (173 shorter events, 67.6 us)
Async XLA Ops:
  0.6 15.2 %copy-start = (bf16[1,512,1024]{2,1,0:T(8,128)(2,1)S(1)}, bf16[1,512,1024]{2,1,0:T(8,128)(2,1)}, u32[]{:S(2)}) copy-start(bf16[1,512,1024]{2,1,0:T(8,128)(2,1)} %param.7) | copy-start | bytes 3145732
  0.6 16.2 %copy-start.7 = (bf16[1,512,1024]{2,1,0:T(8,128)(2,1)S(1)}, bf16[1,512,1024]{2,1,0:T(8,128)(2,1)}, u32[]{:S(2)}) copy-start(bf16[1,512,1024]{2,1,0:T(8,128)(2,1)} %param.6) | copy-start | bytes 3145732
  3.4 9.8 %all-to-all-start = ((s32[8,1,1]{2,1,0:T(1,128)}), s32[8,1,1]{2,1,0:T(1,128)S(1)}, u32[]{:S(2)}, u32[]{:S(2)}) async-start(s32[8,1,1]{2,1,0:T(1,128)} %broadcast_in_dim.40), calls=%async_computation | async-start | bytes 8192 | tf_op jit(solution)/shard_map/all_to_all | solution.py:206
  20.1 18.1 %copy-start.18 = (f32[1024]{0:T(1024)S(1)}, f32[1024]{0:T(1024)}, u32[]{:S(2)}) copy-start(f32[1024]{0:T(1024)} %param.11) | copy-start | bytes 12292
  21.1 11.7 %all-to-all-start.1 = ((bf16[8,24,1024]{2,1,0:T(8,128)(2,1)}), bf16[8,24,1024]{2,1,0:T(8,128)(2,1)S(1)}, u32[]{:S(2)}, u32[]{:S(2)}) async-start(bf16[8,24,1024]{2,1,0:T(8,128)(2,1)} %get-tuple-element.20), calls=%async_computation.1 | async-start | bytes 786432 | tf_op jit(solution)/shard_map/all_to_all | solution.py:224
  32.8 11.7 %all-to-all-start.2 = ((bf16[8,24,1024]{2,1,0:T(8,128)(2,1)}), bf16[8,24,1024]{2,1,0:T(8,128)(2,1)S(1)}, u32[]{:S(2)}, u32[]{:S(2)}) async-start(bf16[8,24,1024]{2,1,0:T(8,128)(2,1)} %get-tuple-element.19), calls=%async_computation.2 | async-start | bytes 786432 | tf_op jit(solution)/shard_map/all_to_all | solution.py:225
  38.4 18.7 %copy-start.11 = (bf16[128,1024]{1,0:T(8,128)(2,1)}, bf16[128,1024]{1,0:T(8,128)(2,1)S(1)}, u32[]{:S(2)}) copy-start(bf16[128,1024]{1,0:T(8,128)(2,1)S(1)} %fusion.29) | copy-start | bytes 786436
  40.5 10.1 %collective-permute-start.2 = (bf16[1024,128]{0,1:T(8,128)(2,1)S(1)}, bf16[1024,128]{0,1:T(8,128)(2,1)S(1)}, u32[]{:S(2)}, u32[]{:S(2)}) collective-permute-start(bf16[1024,128]{0,1:T(8,128)(2,1)S(1)} %bitcast.217), channel_id=1, source_target_pairs={{0,24},{4,28},{8,16},{12,20},{16,8},{20,12},{24,0},{28,4},{1,25},{... | collective-permute-start | bytes 786440 | tf_op jit(solution)/shard_map/ppermute | solution.py:179
  43.4 12.4 %collective-permute-start.1 = (bf16[1024,128]{0,1:T(8,128)(2,1)S(1)}, bf16[1024,128]{0,1:T(8,128)(2,1)S(1)}, u32[]{:S(2)}, u32[]{:S(2)}) collective-permute-start(bf16[1024,128]{0,1:T(8,128)(2,1)S(1)} %bitcast.218), channel_id=1, source_target_pairs={{0,16},{4,20},{8,24},{12,28},{16,0},{20,4},{24,8},{28,12},{1,17},{... | collective-permute-start | bytes 786440 | tf_op jit(solution)/shard_map/ppermute | solution.py:179
  44.0 12.0 %collective-permute-start = (bf16[1024,128]{0,1:T(8,128)(2,1)S(1)}, bf16[1024,128]{0,1:T(8,128)(2,1)S(1)}, u32[]{:S(2)}, u32[]{:S(2)}) collective-permute-start(bf16[1024,128]{0,1:T(8,128)(2,1)S(1)} %bitcast.219), channel_id=1, source_target_pairs={{0,8},{4,12},{8,0},{12,4},{16,24},{20,28},{24,16},{28,20},{1,9},{5... | collective-permute-start | bytes 786440 | tf_op jit(solution)/shard_map/ppermute | solution.py:179
  57.1 5.8 %collective-permute-start.3 = (bf16[4,1024,128]{1,2,0:T(8,128)(2,1)}, bf16[4,1024,128]{1,2,0:T(8,128)(2,1)}, u32[]{:S(2)}, u32[]{:S(2)}) collective-permute-start(bf16[4,1024,128]{1,2,0:T(8,128)(2,1)} %pad_maximum_fusion), channel_id=1, source_target_pairs={{0,4},{4,0},{8,12},{12,8},{16,20},{20,16},{24,28},{28,24},{1,5},{5... | collective-permute-start | bytes 3145736 | tf_op jit(solution)/shard_map/ppermute | solution.py:181
  80.1 5.6 %collective-permute-start.4 = (bf16[2,2,2,2,16,1024]{5,4,3,2,1,0:T(8,128)(2,1)S(1)}, bf16[2,2,2,2,16,1024]{5,4,3,2,1,0:T(8,128)(2,1)S(1)}, u32[]{:S(2)}, u32[]{:S(2)}) collective-permute-start(bf16[2,2,2,2,16,1024]{5,4,3,2,1,0:T(8,128)(2,1)S(1)} %fusion.33), channel_id=1, source_target_pairs={{0,4},{4,0},{8,12},{12,8},{16,20},{20,16},{24,28},{28,24},{1,5},{5... | collective-permute-start | bytes 1572872 | tf_op jit(solution)/shard_map/ppermute | solution.py:153
  86.0 6.4 %collective-permute-start.5 = (bf16[2,2,2,16,1024]{4,3,2,1,0:T(8,128)(2,1)S(1)}, bf16[2,2,2,16,1024]{4,3,2,1,0:T(8,128)(2,1)S(1)}, u32[]{:S(2)}, u32[]{:S(2)}) collective-permute-start(bf16[2,2,2,16,1024]{4,3,2,1,0:T(8,128)(2,1)S(1)} %fusion.37), channel_id=1, source_target_pairs={{0,8},{4,20},{8,0},{12,28},{16,24},{20,4},{24,16},{28,12},{1,9},{5... | collective-permute-start | bytes 786440 | tf_op jit(solution)/shard_map/ppermute | solution.py:153
  93.3 6.8 %collective-permute-start.6 = (bf16[2,2,16,1024]{3,2,1,0:T(8,128)(2,1)S(1)}, bf16[2,2,16,1024]{3,2,1,0:T(8,128)(2,1)}, u32[]{:S(2)}, u32[]{:S(2)}) collective-permute-start(bf16[2,2,16,1024]{3,2,1,0:T(8,128)(2,1)S(1)} %fusion.48), channel_id=1, source_target_pairs={{0,16},{4,12},{8,24},{12,4},{16,0},{20,28},{24,8},{28,20},{1,17},{... | collective-permute-start | bytes 393224 | tf_op jit(solution)/shard_map/ppermute | solution.py:153
  98.3 13.9 %collective-permute-start.9 = (bf16[4,1024,128]{1,2,0:T(8,128)(2,1)}, bf16[4,1024,128]{1,2,0:T(8,128)(2,1)}, u32[]{:S(2)}, u32[]{:S(2)}) collective-permute-start(bf16[4,1024,128]{1,2,0:T(8,128)(2,1)} %copy.59), channel_id=1, source_target_pairs={{0,4},{4,0},{8,12},{12,8},{16,20},{20,16},{24,28},{28,24},{1,5},{5... | collective-permute-start | bytes 3145736 | tf_op jit(solution)/shard_map/ppermute | solution.py:187
  101.9 6.1 %collective-permute-start.7 = (bf16[2,16,1024]{2,1,0:T(8,128)(2,1)S(1)}, bf16[2,16,1024]{2,1,0:T(8,128)(2,1)}, u32[]{:S(2)}, u32[]{:S(2)}) collective-permute-start(bf16[2,16,1024]{2,1,0:T(8,128)(2,1)S(1)} %fusion.56), channel_id=1, source_target_pairs={{0,1},{1,0},{2,3},{3,2},{4,5},{5,4},{6,7},{7,6},{8,9},{9,8},{10,11... | collective-permute-start | bytes 196616 | tf_op jit(solution)/shard_map/ppermute | solution.py:164
  109.5 11.7 %collective-permute-start.8 = (bf16[16,1024]{1,0:T(8,128)(2,1)}, bf16[16,1024]{1,0:T(8,128)(2,1)}, u32[]{:S(2)}, u32[]{:S(2)}) collective-permute-start(bf16[16,1024]{1,0:T(8,128)(2,1)} %fusion.57), channel_id=1, source_target_pairs={{0,2},{1,3},{2,0},{3,1},{4,6},{5,7},{6,4},{7,5},{8,10},{9,11},{10,... | collective-permute-start | bytes 98312 | tf_op jit(solution)/shard_map/ppermute | solution.py:164
  116.8 9.4 %collective-permute-start.10 = (bf16[1024,128]{0,1:T(8,128)(2,1)}, bf16[1024,128]{0,1:T(8,128)(2,1)S(1)}, u32[]{:S(2)}, u32[]{:S(2)}) collective-permute-start(bf16[1024,128]{0,1:T(8,128)(2,1)} %get-tuple-element.16), channel_id=1, source_target_pairs={{0,8},{4,12},{8,0},{12,4},{16,24},{20,28},{24,16},{28,20},{1,9},{5... | collective-permute-start | bytes 786440 | tf_op jit(solution)/shard_map/ppermute | solution.py:191
  117.4 13.5 %collective-permute-start.12 = (bf16[1024,128]{0,1:T(8,128)(2,1)}, bf16[1024,128]{0,1:T(8,128)(2,1)S(1)}, u32[]{:S(2)}, u32[]{:S(2)}) collective-permute-start(bf16[1024,128]{0,1:T(8,128)(2,1)} %get-tuple-element.17), channel_id=1, source_target_pairs={{0,24},{4,28},{8,16},{12,20},{16,8},{20,12},{24,0},{28,4},{1,25},{... | collective-permute-start | bytes 786440 | tf_op jit(solution)/shard_map/ppermute | solution.py:191
  118.8 14.8 %copy-start.14 = (bf16[128,1024]{0,1:T(8,128)(2,1)S(1)}, bf16[128,1024]{0,1:T(8,128)(2,1)}, u32[]{:S(2)}) copy-start(bf16[128,1024]{0,1:T(8,128)(2,1)} %copy.62) | copy-start | bytes 786436
  118.8 13.5 %collective-permute-start.11 = (bf16[1024,128]{0,1:T(8,128)(2,1)}, bf16[1024,128]{0,1:T(8,128)(2,1)}, u32[]{:S(2)}, u32[]{:S(2)}) collective-permute-start(bf16[1024,128]{0,1:T(8,128)(2,1)} %get-tuple-element.18), channel_id=1, source_target_pairs={{0,16},{4,20},{8,24},{12,28},{16,0},{20,4},{24,8},{28,12},{1,17},{... | collective-permute-start | bytes 786440 | tf_op jit(solution)/shard_map/ppermute | solution.py:191
  134.8 3.5 %collective-permute-start.18 = (bf16[2,2,2,2,32,1536]{5,4,3,2,1,0:T(8,128)(2,1)S(1)}, bf16[2,2,2,2,32,1536]{5,4,3,2,1,0:T(8,128)(2,1)S(1)}, u32[]{:S(2)}, u32[]{:S(2)}) collective-permute-start(bf16[2,2,2,2,32,1536]{5,4,3,2,1,0:T(8,128)(2,1)S(1)} %fusion.13), channel_id=1, source_target_pairs={{0,4},{4,0},{8,12},{12,8},{16,20},{20,16},{24,28},{28,24},{1,5},{5... | collective-permute-start | bytes 4718600 | tf_op jit(solution)/shard_map/ppermute | solution.py:155
  138.9 12.1 %collective-permute-start.19 = (bf16[2,2,2,32,1536]{4,3,2,1,0:T(8,128)(2,1)S(1)}, bf16[2,2,2,32,1536]{4,3,2,1,0:T(8,128)(2,1)S(1)}, u32[]{:S(2)}, u32[]{:S(2)}) collective-permute-start(bf16[2,2,2,32,1536]{4,3,2,1,0:T(8,128)(2,1)S(1)} %fusion.14), channel_id=1, source_target_pairs={{0,8},{4,20},{8,0},{12,28},{16,24},{20,4},{24,16},{28,12},{1,9},{5... | collective-permute-start | bytes 2359304 | tf_op jit(solution)/shard_map/ppermute | solution.py:155
  151.5 7.8 %collective-permute-start.20 = (bf16[2,2,32,1536]{3,2,1,0:T(8,128)(2,1)S(1)}, bf16[2,2,32,1536]{3,2,1,0:T(8,128)(2,1)S(1)}, u32[]{:S(2)}, u32[]{:S(2)}) collective-permute-start(bf16[2,2,32,1536]{3,2,1,0:T(8,128)(2,1)S(1)} %fusion.39), channel_id=1, source_target_pairs={{0,16},{4,12},{8,24},{12,4},{16,0},{20,28},{24,8},{28,20},{1,17},{... | collective-permute-start | bytes 1179656 | tf_op jit(solution)/shard_map/ppermute | solution.py:155
  159.5 5.7 %collective-permute-start.21 = (bf16[2,32,1536]{2,1,0:T(8,128)(2,1)S(1)}, bf16[2,32,1536]{2,1,0:T(8,128)(2,1)S(1)}, u32[]{:S(2)}, u32[]{:S(2)}) collective-permute-start(bf16[2,32,1536]{2,1,0:T(8,128)(2,1)S(1)} %fusion.47), channel_id=1, source_target_pairs={{0,1},{1,0},{2,3},{3,2},{4,5},{5,4},{6,7},{7,6},{8,9},{9,8},{10,11... | collective-permute-start | bytes 589832 | tf_op jit(solution)/shard_map/ppermute | solution.py:166
  160.1 24.6 %copy-start.1 = (bf16[1,512,1024]{2,1,0:T(8,128)(2,1)S(1)}, bf16[1,512,1024]{2,1,0:T(8,128)(2,1)}, u32[]{:S(2)}) copy-start(bf16[1,512,1024]{2,1,0:T(8,128)(2,1)} %param.7) | copy-start | bytes 3145732
  161.9 4.0 %collective-permute-start.13 = (f32[1025]{0:T(1024)S(1)}, f32[1025]{0:T(1024)S(1)}, u32[]{:S(2)}, u32[]{:S(2)}) collective-permute-start(f32[1025]{0:T(1024)S(1)} %pad_maximum_fusion.4), channel_id=1, source_target_pairs={{0,4},{4,0},{8,12},{12,8},{16,20},{20,16},{24,28},{28,24},{1,5},{5... | collective-permute-start | bytes 12308 | tf_op jit(solution)/shard_map/ppermute | solution.py:155
  165.3 18.6 %collective-permute-start.22 = (bf16[32,1536]{1,0:T(8,128)(2,1)S(1)}, bf16[32,1536]{1,0:T(8,128)(2,1)S(1)}, u32[]{:S(2)}, u32[]{:S(2)}) collective-permute-start(bf16[32,1536]{1,0:T(8,128)(2,1)S(1)} %fusion.55), channel_id=1, source_target_pairs={{0,2},{1,3},{2,0},{3,1},{4,6},{5,7},{6,4},{7,5},{8,10},{9,11},{10,... | collective-permute-start | bytes 294920 | tf_op jit(solution)/shard_map/ppermute | solution.py:166
  166.6 3.7 %collective-permute-start.14 = (f32[1025]{0:T(1024)S(1)}, f32[1025]{0:T(1024)S(1)}, u32[]{:S(2)}, u32[]{:S(2)}) collective-permute-start(f32[1025]{0:T(1024)S(1)} %fusion.61), channel_id=1, source_target_pairs={{0,8},{4,20},{8,0},{12,28},{16,24},{20,4},{24,16},{28,12},{1,9},{5... | collective-permute-start | bytes 12308 | tf_op jit(solution)/shard_map/ppermute | solution.py:155
  170.3 3.7 %collective-permute-start.15 = (f32[1025]{0:T(1024)S(1)}, f32[1025]{0:T(1024)S(1)}, u32[]{:S(2)}, u32[]{:S(2)}) collective-permute-start(f32[1025]{0:T(1024)S(1)} %add.330), channel_id=1, source_target_pairs={{0,16},{4,12},{8,24},{12,4},{16,0},{20,28},{24,8},{28,20},{1,17},{... | collective-permute-start | bytes 12308 | tf_op jit(solution)/shard_map/ppermute | solution.py:155
  173.9 3.7 %collective-permute-start.16 = (f32[1025]{0:T(1024)S(1)}, f32[1025]{0:T(1024)S(1)}, u32[]{:S(2)}, u32[]{:S(2)}) collective-permute-start(f32[1025]{0:T(1024)S(1)} %add.331), channel_id=1, source_target_pairs={{0,1},{1,0},{2,3},{3,2},{4,5},{5,4},{6,7},{7,6},{8,9},{9,8},{10,11... | collective-permute-start | bytes 12308 | tf_op jit(solution)/shard_map/ppermute | solution.py:166
  177.6 4.6 %collective-permute-start.17 = (f32[1025]{0:T(1024)S(1)}, f32[1025]{0:T(1024)S(1)}, u32[]{:S(2)}, u32[]{:S(2)}) collective-permute-start(f32[1025]{0:T(1024)S(1)} %add.332), channel_id=1, source_target_pairs={{0,2},{1,3},{2,0},{3,1},{4,6},{5,7},{6,4},{7,5},{8,10},{9,11},{10,... | collective-permute-start | bytes 12308 | tf_op jit(solution)/shard_map/ppermute | solution.py:166
  (16 other events, 62.9 us)

commit v10 on v8

--- a/solution.py
+++ b/solution.py
@@ -252,16 +252,21 @@
         jnp.bfloat16
     )
     gathered = gather_blocks(pair_cols)
-    split_kv = gathered.reshape(shards, heads, 2, HEAD_DIM, rows).transpose(1, 2, 3, 0, 4)
-    split_kv = split_kv.reshape(heads, 2, HEAD_DIM, shards * rows)
-    keys_t = split_kv[:, 0]
-    values_t = split_kv[:, 1]
-    scores = jnp.einsum("hqd,hdk->hqk", queries, keys_t, preferred_element_type=jnp.float32) * 0.125
-    row_max = jnp.max(scores, axis=2)
-    weights = jnp.exp(scores - row_max[:, :, None])
-    row_sum = jnp.sum(weights, axis=2)
-    blended = jnp.einsum(
-        "hqk,hdk->hqd", weights.astype(jnp.bfloat16), values_t, preferred_element_type=jnp.float32
+    split_kv = gathered.reshape(shards, heads, 2, HEAD_DIM, rows)
+    keys_b = split_kv[:, :, 0]
+    values_b = split_kv[:, :, 1]
+    queries_b = jnp.broadcast_to(queries[None], (shards,) + queries.shape)
+    scores = (
+        jnp.einsum("ihqd,ihdt->ihqt", queries_b, keys_b, preferred_element_type=jnp.float32) * 0.125
+    )
+    row_max = jnp.max(scores, axis=(0, 3))
+    weights = jnp.exp(scores - row_max[None, :, :, None])
+    row_sum = jnp.sum(weights, axis=(0, 3))
+    blended = jnp.sum(
+        jnp.einsum(
+            "ihqt,ihdt->ihqd", weights.astype(jnp.bfloat16), values_b, preferred_element_type=jnp.float32
+        ),
+        axis=0,
     )
     log_total = row_max + jnp.log(row_sum)
     attended = (
@@ -284,16 +289,20 @@
         * attended.reshape(rows, heads, HEAD_DIM).transpose(1, 0, 2).astype(jnp.float32),
         axis=2,
     )
-    prob_full = jnp.exp(scores - log_total[:, :, None])
-    d_value_t = jnp.einsum(
-        "hqd,hqk->hdk", grad_heads, prob_full.astype(jnp.bfloat16), preferred_element_type=jnp.float32
-    )
-    d_prob = jnp.einsum("hqd,hdk->hqk", grad_heads, values_t, preferred_element_type=jnp.float32)
-    d_score = (prob_full * (d_prob - row_dot[:, :, None])).astype(jnp.bfloat16)
-    d_query = 0.125 * jnp.einsum("hqk,hdk->qhd", d_score, keys_t, preferred_element_type=jnp.float32)
-    d_key_t = 0.125 * jnp.einsum("hqd,hqk->hdk", queries, d_score, preferred_element_type=jnp.float32)
-    d_pairs = jnp.stack([d_key_t, d_value_t], axis=1).reshape(heads, 2, HEAD_DIM, shards, rows)
-    d_pairs = d_pairs.transpose(3, 0, 1, 2, 4).reshape(shards, 2 * inner, rows).astype(jnp.bfloat16)
+    prob_full = jnp.exp(scores - log_total[None, :, :, None])
+    grad_heads_b = jnp.broadcast_to(grad_heads[None], (shards,) + grad_heads.shape)
+    d_value_b = jnp.einsum(
+        "ihqd,ihqt->ihdt", grad_heads_b, prob_full.astype(jnp.bfloat16), preferred_element_type=jnp.float32
+    )
+    d_prob = jnp.einsum("ihqd,ihdt->ihqt", grad_heads_b, values_b, preferred_element_type=jnp.float32)
+    d_score = (prob_full * (d_prob - row_dot[None, :, :, None])).astype(jnp.bfloat16)
+    d_query = 0.125 * jnp.sum(
+        jnp.einsum("ihqt,ihdt->ihqd", d_score, keys_b, preferred_element_type=jnp.float32), axis=0
+    ).transpose(1, 0, 2)
+    d_key_b = 0.125 * jnp.einsum(
+        "ihqd,ihqt->ihdt", queries_b, d_score, preferred_element_type=jnp.float32
+    )
+    d_pairs = jnp.stack([d_key_b, d_value_b], axis=2).reshape(shards, 2 * inner, rows).astype(jnp.bfloat16)
     accum = return_blocks(d_pairs)
     d_proj = jnp.concatenate([d_query.reshape(rows, inner), accum.T], axis=1).astype(jnp.bfloat16)
     grad_wqkv = jnp.dot(exchange_order(hidden).T, d_proj, preferred_element_type=jnp.float32)

time: 179 us -> 173 us (0.966)
  local copies, waits for them, and re-layouts: 46 us -> 39.9 us
    transpose x1 -> x0, local copies, waits for them, and re-layouts: 4.66 us -> none  [per_device(): gathered.reshape(shards, heads, 2, HEAD_DIM, rows).transpose(1, 2, 3, 0, 4)]
    convert_element_type x1 -> x2, local copies, waits for them, and re-layouts: 2.87 us -> 6.04 us  [return_blocks(): summed = parts[:half].astype(jnp.float32) + got.astype(jnp.float32)]
    convert_element_type x2 -> x0, other arithmetic: 2.88 us -> none  [the longest x1 2.69 us: return_blocks(): summed = parts[:half].astype(jnp.float32) + got.astype(jnp.float32)]
    reshape x1 -> x0, local copies, waits for them, and re-layouts: 2.82 us -> none  [per_device(): split_kv = split_kv.reshape(heads, 2, HEAD_DIM, shards * rows)]
    unnamed x73 -> x69, local copies, waits for them, and re-layouts: 10.3 us -> 8.53 us
    another operation x2 -> x3, other arithmetic: 4.04 us -> 5.61 us
  transfers between devices with their start and end apart: 26 -> 26, of which waited for: 16 -> 16; matrix products, arithmetic and copies ran while one was open for 20% -> 21% of each run, Pallas kernels for 0% -> 0%
where the time goes in v10:
time: 173 us; the launch traced here: 172 us
  waiting for transfers between devices  47.7 us (28%)
  local copies, waits for them, and re-layouts  39.9 us (23%)
  starting transfers between devices  36.1 us (21%)
  other arithmetic  24.3 us (14%)
  matrix products  21.2 us (12%)
  between operations  3.09 us (2%)
    ppermute x3, waiting for transfers between devices, return_blocks(): sent = lax.ppermute(summed[k].astype(jnp.bfloat16), 'seq', xor_pairs(2 * k))  10.8 us
    ppermute x3, waiting for transfers between devices, gather_blocks(): lax.ppermute(block, 'seq', xor_pairs(2 * k))  9.76 us
    ppermute x6, waiting for transfers between devices, halving_scatter(): lax.ppermute((give.astype(jnp.bfloat16), small), 'seq', pairs)  8.78 us
    unnamed x69, local copies, waits for them, and re-layouts  8.53 us
    all_to_all x1, waiting for transfers between devices, per_device(): lax.all_to_all(send_tokens, 'seq', split_axis=0, concat_axis=0, tiled=True)  8.09 us
    ppermute x4, starting transfers between devices, halving_scatter(): lax.ppermute((give.astype(jnp.bfloat16), small), 'clip', pairs)  6.04 us
    convert_element_type x2, local copies, waits for them, and re-layouts, return_blocks(): summed = parts[:half].astype(jnp.float32) + got.astype(jnp.float32)  6.04 us
    add x9, other arithmetic, halving_scatter(): data = keep + got.astype(jnp.float32)  5.75 us
  transfers between devices with their start and end apart: 26, of which 16 were waited for; matrix products, arithmetic and copies ran while one was open for 21% of the time, Pallas kernels for 0%

profile of v10, /device:TPU:0, one launch (start us, length us, event | category | flops | bytes accessed | tf_op | source)
XLA Modules:
  0.0 172.2 jit_solution(9322093543821846798)
XLA Ops:
  3.4 5.2 %all-to-all-start = ((s32[8,1,1]{2,1,0:T(1,128)}), s32[8,1,1]{2,1,0:T(1,128)S(1)}, u32[]{:S(2)}, u32[]{:S(2)}) async-start(s32[8,1,1]{2,1,0:T(1,128)} %broadcast_in_dim.44), calls=%async_computation | async-start | bytes 8192 | tf_op jit(solution)/shard_map/all_to_all | solution.py:206
  9.2 3.9 %all-to-all-done = s32[8,1,1]{2,1,0:T(1,128)S(1)} async-done(((s32[8,1,1]{2,1,0:T(1,128)}), s32[8,1,1]{2,1,0:T(1,128)S(1)}, u32[]{:S(2)}, u32[]{:S(2)}) %all-to-all-start) | async-done | bytes 64 | tf_op jit(solution)/shard_map/all_to_all | solution.py:206
  21.1 3.5 %all-to-all-start.1 = ((bf16[8,24,1024]{2,1,0:T(8,128)(2,1)}), bf16[8,24,1024]{2,1,0:T(8,128)(2,1)S(1)}, u32[]{:S(2)}, u32[]{:S(2)}) async-start(bf16[8,24,1024]{2,1,0:T(8,128)(2,1)} %get-tuple-element.16), calls=%async_computation.1 | async-start | bytes 786432 | tf_op jit(solution)/shard_map/all_to_all | solution.py:224
  24.7 8.1 %all-to-all-done.1 = bf16[8,24,1024]{2,1,0:T(8,128)(2,1)S(1)} async-done(((bf16[8,24,1024]{2,1,0:T(8,128)(2,1)}), bf16[8,24,1024]{2,1,0:T(8,128)(2,1)S(1)}, u32[]{:S(2)}, u32[]{:S(2)}) %all-to-all-start.1) | async-done | bytes 393248 | tf_op jit(solution)/shard_map/all_to_all | solution.py:224
  32.8 3.5 %all-to-all-start.2 = ((bf16[8,24,1024]{2,1,0:T(8,128)(2,1)}), bf16[8,24,1024]{2,1,0:T(8,128)(2,1)S(1)}, u32[]{:S(2)}, u32[]{:S(2)}) async-start(bf16[8,24,1024]{2,1,0:T(8,128)(2,1)} %get-tuple-element.15), calls=%async_computation.2 | async-start | bytes 786432 | tf_op jit(solution)/shard_map/all_to_all | solution.py:225
  38.3 2.1 %fusion.23 = bf16[128,1024]{1,0:T(8,128)(2,1)S(1)} fusion(bf16[128,1024]{1,0:T(8,128)(2,1)S(1)} %fusion.36, bf16[1024,1536]{1,0:T(8,128)(2,1)} %param.9), kind=kOutput, calls=%fused_computation.37 | convolution fusion | flops 268566528 | bytes 2621440 | tf_op jit(solution)/shard_map/dot_general | solution.py:251
  40.5 2.9 %collective-permute-start.2 = (bf16[1024,128]{0,1:T(8,128)(2,1)S(1)}, bf16[1024,128]{0,1:T(8,128)(2,1)S(1)}, u32[]{:S(2)}, u32[]{:S(2)}) collective-permute-start(bf16[1024,128]{0,1:T(8,128)(2,1)S(1)} %bitcast.217), channel_id=1, source_target_pairs={{0,24},{4,28},{8,16},{12,20},{16,8},{20,12},{24,0},{28,4},{1,25},{... | collective-permute-start | bytes 786440 | tf_op jit(solution)/shard_map/ppermute | solution.py:179
  44.5 1.6 scatter_custom_fusion.1
  46.2 4.4 %collective-permute-done.2 = bf16[1024,128]{0,1:T(8,128)(2,1)S(1)} collective-permute-done((bf16[1024,128]{0,1:T(8,128)(2,1)S(1)}, bf16[1024,128]{0,1:T(8,128)(2,1)S(1)}, u32[]{:S(2)}, u32[]{:S(2)}) %collective-permute-start.2) | collective-permute-done | bytes 262176 | tf_op jit(solution)/shard_map/ppermute | solution.py:179
  50.6 5.2 %collective-permute-done.1 = bf16[1024,128]{0,1:T(8,128)(2,1)S(1)} collective-permute-done((bf16[1024,128]{0,1:T(8,128)(2,1)S(1)}, bf16[1024,128]{0,1:T(8,128)(2,1)S(1)}, u32[]{:S(2)}, u32[]{:S(2)}) %collective-permute-start.1) | collective-permute-done | bytes 262176 | tf_op jit(solution)/shard_map/ppermute | solution.py:179
  60.2 1.8 %copy.79 = bf16[1024,128]{1,0:T(8,128)(2,1)} copy(bf16[1024,128]{0,1:T(8,128)(2,1)} %copy-done.14) | data formatting | bytes 524288 | tf_op jit(solution)/shard_map/ppermute | solution.py:179
  63.1 2.3 %copy.82 = bf16[4,1024,128]{2,1,0:T(8,128)(2,1)} copy(bf16[4,1024,128]{1,2,0:T(8,128)(2,1)} %collective-permute-done.3) | data formatting | bytes 2097152 | tf_op jit(solution)/shard_map/ppermute | solution.py:181
  69.6 1.6 fusion.58
  73.7 3.9 %fusion.19 = bf16[8,8,1,64,128]{4,3,1,0,2:T(8,128)(2,1)S(1)} fusion(f32[8,8,128,128]{2,3,1,0:T(8,128)} %copy-done.2, f32[8,128]{1,0:T(8,128)S(1)} %log_add_fusion, bf16[8,128,64]{1,2,0:T(8,128)(2,1)S(1)} %bitcast.204), kind=kOutput, calls=%fused_computation.33 | convolution fusion | flops 137887744 | bytes 5378048 | tf_op jit(solution)/shard_map/ihqd,ihqt->ihdt/dot_general | solution.py:294
  77.6 2.6 %multiply_convert_fusion = bf16[8,8,128,128]{2,3,1,0:T(8,128)(2,1)S(1)} fusion(f32[8,8,128,128]{2,3,1,0:T(8,128)S(1)} %copy-done.3, f32[8,128]{1,0:T(8,128)S(1)} %multiply_reduce_fusion.4, f32[8,128]{1,0:T(8,128)S(1)} %log_add_fusion, bf16[8,8,2,64,128]{4,3,2,1,0:T(8,128)(2,1)} %copy-done.8, bf16[8,128,64]{1,2,0:T(8,128)(2,1)S(1)} %bitcast.205), kind=kOutput, calls=%fused_computation.6 | convolution fusion | flops 139460608 | bytes 7479296 | tf_op jit(solution)/shard_map/ihqd,ihdt->ihqt/dot_general | solution.py:297
  81.8 1.5 pad_maximum_fusion
  84.4 2.3 %copy.96 = bf16[4,1024,128]{1,2,0:T(8,128)(2,1)} copy(bf16[4,1024,128]{2,1,0:T(8,128)(2,1)} %bitcast.203) | data formatting | bytes 2097152 | tf_op jit(solution)/shard_map/slice | solution.py:187
  88.0 3.1 %copy.94 = f32[4,8,2,64,128]{4,3,2,1,0:T(8,128)} copy(f32[4,8,2,64,128]{4,3,1,0,2:T(8,128)} %get-tuple-element.11) | data formatting | bytes 4194304 | tf_op jit(solution)/shard_map/convert_element_type | solution.py:188
  91.2 2.9 %copy.97 = f32[4,1024,128]{1,2,0:T(8,128)} copy(f32[4,1024,128]{2,1,0:T(8,128)} %bitcast.201) | data formatting | bytes 4194304 | tf_op jit(solution)/shard_map/convert_element_type | solution.py:188
  94.1 3.9 %fusion.81 = (bf16[4,1024,128]{1,2,0:T(8,128)(2,1)S(1)}, f32[4,1024,128]{1,2,0:T(8,128)}) fusion(f32[4,1024,128]{1,2,0:T(8,128)} %copy.97, bf16[4,1024,128]{1,2,0:T(8,128)(2,1)} %collective-permute-done.4), kind=kLoop, calls=%fused_computation.172 | loop fusion | flops 1572864 | bytes 6291456 | tf_op jit(solution)/shard_map/convert.8
  104.6 3.8 %collective-permute-done.5 = bf16[1024,128]{0,1:T(8,128)(2,1)} collective-permute-done((bf16[1024,128]{0,1:T(8,128)(2,1)}, bf16[1024,128]{0,1:T(8,128)(2,1)}, u32[]{:S(2)}, u32[]{:S(2)}) %collective-permute-start.5) | collective-permute-done | bytes 262176 | tf_op jit(solution)/shard_map/ppermute | solution.py:191
  108.4 5.7 %collective-permute-done.7 = bf16[1024,128]{0,1:T(8,128)(2,1)} collective-permute-done((bf16[1024,128]{0,1:T(8,128)(2,1)}, bf16[1024,128]{0,1:T(8,128)(2,1)}, u32[]{:S(2)}, u32[]{:S(2)}) %collective-permute-start.7) | collective-permute-done | bytes 262176 | tf_op jit(solution)/shard_map/ppermute | solution.py:191
  118.5 2.6 %copy-done.6 = f32[2,2,2,2,2,32,1536]{6,5,4,3,2,1,0:T(8,128)} copy-done((f32[2,2,2,2,2,32,1536]{6,5,4,3,2,1,0:T(8,128)}, f32[2,2,2,2,2,32,1536]{6,5,4,3,2,1,0:T(8,128)S(1)}, u32[]{:S(2)}) %copy-start.6) | copy-done | bytes 6291480
  123.9 3.0 %collective-permute-done.18 = bf16[2,2,2,2,16,1024]{5,4,3,2,1,0:T(8,128)(2,1)} collective-permute-done((bf16[2,2,2,2,16,1024]{5,4,3,2,1,0:T(8,128)(2,1)S(1)}, bf16[2,2,2,2,16,1024]{5,4,3,2,1,0:T(8,128)(2,1)}, u32[]{:S(2)}, u32[]{:S(2)}) %collective-permute-start.18) | collective-permute-done | bytes 524320 | tf_op jit(solution)/shard_map/ppermute | solution.py:153
  129.5 2.9 %bitcast_add_fusion = f32[2,2,2,2,32,1536]{5,4,3,2,1,0:T(8,128)S(1)} fusion(bf16[2,2,2,2,32,1536]{5,4,3,2,1,0:T(8,128)(2,1)} %collective-permute-done.13, f32[2,2,2,2,2,32,1536]{6,5,4,3,2,1,0:T(8,128)} %copy-done.6, s32[]{:T(128)S(6)} %select_n.233), kind=kLoop, calls=%fused_computation.13 | loop fusion | flops 1572864 | bytes 7864324 | tf_op jit(solution)/shard_map/add | solution.py:157
  132.4 1.6 copy-done.4
  137.4 3.4 %fusion.26 = f32[1024]{0:T(1024)S(1)} fusion(bf16[1024,1536]{1,0:T(8,128)(2,1)} %param.9, bf16[128,1024]{1,0:T(8,128)(2,1)S(1)} %scatter_custom_fusion, f32[128]{0:T(128)S(1)} %copy-done.31, f32[128]{0:T(128)S(1)} %broadcast_multiply_fusion.1, bf16[128,1024]{1,0:T(8,128)(2,1)S(1)} %copy-done.17, bf16[128,512]{1,0:T(8,128)(2,1)S(1)} %copy-done.19), kind=kOutput, calls=%fused_computation.38 | convolution fusion | flops 404093952 | bytes 3806208 | tf_op jit(solution)/shard_map/dot_general | solution.py:309
  141.5 6.2 %collective-permute-done.14 = bf16[2,2,2,32,1536]{4,3,2,1,0:T(8,128)(2,1)S(1)} collective-permute-done((bf16[2,2,2,32,1536]{4,3,2,1,0:T(8,128)(2,1)S(1)}, bf16[2,2,2,32,1536]{4,3,2,1,0:T(8,128)(2,1)S(1)}, u32[]{:S(2)}, u32[]{:S(2)}) %collective-permute-start.14) | collective-permute-done | bytes 786464 | tf_op jit(solution)/shard_map/ppermute | solution.py:155
  151.0 1.6 collective-permute-start.21
  156.2 1.6 collective-permute-start.16
  159.3 2.6 %collective-permute-start.22 = (bf16[16,1024]{1,0:T(8,128)(2,1)S(1)}, bf16[16,1024]{1,0:T(8,128)(2,1)S(1)}, u32[]{:S(2)}, u32[]{:S(2)}) collective-permute-start(bf16[16,1024]{1,0:T(8,128)(2,1)S(1)} %fusion.72), channel_id=1, source_target_pairs={{0,2},{1,3},{2,0},{3,1},{4,6},{5,7},{6,4},{7,5},{8,10},{9,11},{10,... | collective-permute-start | bytes 98312 | tf_op jit(solution)/shard_map/ppermute | solution.py:164
  162.0 2.7 %collective-permute-start.12 = (f32[1025]{0:T(1024)S(1)}, f32[1025]{0:T(1024)S(1)}, u32[]{:S(2)}, u32[]{:S(2)}) collective-permute-start(f32[1025]{0:T(1024)S(1)} %add.317), channel_id=1, source_target_pairs={{0,2},{1,3},{2,0},{3,1},{4,6},{5,7},{6,4},{7,5},{8,10},{9,11},{10,... | collective-permute-start | bytes 12308 | tf_op jit(solution)/shard_map/ppermute | solution.py:166
  (187 shorter events, 65.1 us)
Async XLA Ops:
  0.6 15.2 %copy-start = (bf16[1,512,1024]{2,1,0:T(8,128)(2,1)S(1)}, bf16[1,512,1024]{2,1,0:T(8,128)(2,1)}, u32[]{:S(2)}) copy-start(bf16[1,512,1024]{2,1,0:T(8,128)(2,1)} %param.7) | copy-start | bytes 3145732
  0.6 16.2 %copy-start.7 = (bf16[1,512,1024]{2,1,0:T(8,128)(2,1)S(1)}, bf16[1,512,1024]{2,1,0:T(8,128)(2,1)}, u32[]{:S(2)}) copy-start(bf16[1,512,1024]{2,1,0:T(8,128)(2,1)} %param.6) | copy-start | bytes 3145732
  3.4 9.8 %all-to-all-start = ((s32[8,1,1]{2,1,0:T(1,128)}), s32[8,1,1]{2,1,0:T(1,128)S(1)}, u32[]{:S(2)}, u32[]{:S(2)}) async-start(s32[8,1,1]{2,1,0:T(1,128)} %broadcast_in_dim.44), calls=%async_computation | async-start | bytes 8192 | tf_op jit(solution)/shard_map/all_to_all | solution.py:206
  20.1 18.0 %copy-start.21 = (f32[1024]{0:T(1024)S(1)}, f32[1024]{0:T(1024)}, u32[]{:S(2)}) copy-start(f32[1024]{0:T(1024)} %param.11) | copy-start | bytes 12292
  21.1 11.7 %all-to-all-start.1 = ((bf16[8,24,1024]{2,1,0:T(8,128)(2,1)}), bf16[8,24,1024]{2,1,0:T(8,128)(2,1)S(1)}, u32[]{:S(2)}, u32[]{:S(2)}) async-start(bf16[8,24,1024]{2,1,0:T(8,128)(2,1)} %get-tuple-element.16), calls=%async_computation.1 | async-start | bytes 786432 | tf_op jit(solution)/shard_map/all_to_all | solution.py:224
  32.8 11.7 %all-to-all-start.2 = ((bf16[8,24,1024]{2,1,0:T(8,128)(2,1)}), bf16[8,24,1024]{2,1,0:T(8,128)(2,1)S(1)}, u32[]{:S(2)}, u32[]{:S(2)}) async-start(bf16[8,24,1024]{2,1,0:T(8,128)(2,1)} %get-tuple-element.15), calls=%async_computation.2 | async-start | bytes 786432 | tf_op jit(solution)/shard_map/all_to_all | solution.py:225
  38.3 18.7 %copy-start.11 = (bf16[128,1024]{1,0:T(8,128)(2,1)}, bf16[128,1024]{1,0:T(8,128)(2,1)S(1)}, u32[]{:S(2)}) copy-start(bf16[128,1024]{1,0:T(8,128)(2,1)S(1)} %fusion.36) | copy-start | bytes 786436
  40.5 10.1 %collective-permute-start.2 = (bf16[1024,128]{0,1:T(8,128)(2,1)S(1)}, bf16[1024,128]{0,1:T(8,128)(2,1)S(1)}, u32[]{:S(2)}, u32[]{:S(2)}) collective-permute-start(bf16[1024,128]{0,1:T(8,128)(2,1)S(1)} %bitcast.217), channel_id=1, source_target_pairs={{0,24},{4,28},{8,16},{12,20},{16,8},{20,12},{24,0},{28,4},{1,25},{... | collective-permute-start | bytes 786440 | tf_op jit(solution)/shard_map/ppermute | solution.py:179
  43.4 12.4 %collective-permute-start.1 = (bf16[1024,128]{0,1:T(8,128)(2,1)S(1)}, bf16[1024,128]{0,1:T(8,128)(2,1)S(1)}, u32[]{:S(2)}, u32[]{:S(2)}) collective-permute-start(bf16[1024,128]{0,1:T(8,128)(2,1)S(1)} %bitcast.218), channel_id=1, source_target_pairs={{0,16},{4,20},{8,24},{12,28},{16,0},{20,4},{24,8},{28,12},{1,17},{... | collective-permute-start | bytes 786440 | tf_op jit(solution)/shard_map/ppermute | solution.py:179
  43.9 12.0 %collective-permute-start = (bf16[1024,128]{0,1:T(8,128)(2,1)S(1)}, bf16[1024,128]{0,1:T(8,128)(2,1)S(1)}, u32[]{:S(2)}, u32[]{:S(2)}) collective-permute-start(bf16[1024,128]{0,1:T(8,128)(2,1)S(1)} %bitcast.219), channel_id=1, source_target_pairs={{0,8},{4,12},{8,0},{12,4},{16,24},{20,28},{24,16},{28,20},{1,9},{5... | collective-permute-start | bytes 786440 | tf_op jit(solution)/shard_map/ppermute | solution.py:179
  57.0 6.0 %collective-permute-start.3 = (bf16[4,1024,128]{1,2,0:T(8,128)(2,1)}, bf16[4,1024,128]{1,2,0:T(8,128)(2,1)}, u32[]{:S(2)}, u32[]{:S(2)}) collective-permute-start(bf16[4,1024,128]{1,2,0:T(8,128)(2,1)} %pad_maximum_fusion.1), channel_id=1, source_target_pairs={{0,4},{4,0},{8,12},{12,8},{16,20},{20,16},{24,28},{28,24},{1,5},{5... | collective-permute-start | bytes 3145736 | tf_op jit(solution)/shard_map/ppermute | solution.py:181
  86.7 7.4 %collective-permute-start.4 = (bf16[4,1024,128]{1,2,0:T(8,128)(2,1)}, bf16[4,1024,128]{1,2,0:T(8,128)(2,1)}, u32[]{:S(2)}, u32[]{:S(2)}) collective-permute-start(bf16[4,1024,128]{1,2,0:T(8,128)(2,1)} %copy.96), channel_id=1, source_target_pairs={{0,4},{4,0},{8,12},{12,8},{16,20},{20,16},{24,28},{28,24},{1,5},{5... | collective-permute-start | bytes 3145736 | tf_op jit(solution)/shard_map/ppermute | solution.py:187
  98.9 9.5 %collective-permute-start.5 = (bf16[1024,128]{0,1:T(8,128)(2,1)}, bf16[1024,128]{0,1:T(8,128)(2,1)}, u32[]{:S(2)}, u32[]{:S(2)}) collective-permute-start(bf16[1024,128]{0,1:T(8,128)(2,1)} %get-tuple-element.12), channel_id=1, source_target_pairs={{0,8},{4,12},{8,0},{12,4},{16,24},{20,28},{24,16},{28,20},{1,9},{5... | collective-permute-start | bytes 786440 | tf_op jit(solution)/shard_map/ppermute | solution.py:191
  100.3 13.7 %collective-permute-start.7 = (bf16[1024,128]{0,1:T(8,128)(2,1)}, bf16[1024,128]{0,1:T(8,128)(2,1)}, u32[]{:S(2)}, u32[]{:S(2)}) collective-permute-start(bf16[1024,128]{0,1:T(8,128)(2,1)} %get-tuple-element.13), channel_id=1, source_target_pairs={{0,24},{4,28},{8,16},{12,20},{16,8},{20,12},{24,0},{28,4},{1,25},{... | collective-permute-start | bytes 786440 | tf_op jit(solution)/shard_map/ppermute | solution.py:191
  101.8 15.7 %copy-start.15 = (bf16[128,1024]{0,1:T(8,128)(2,1)S(1)}, bf16[128,1024]{0,1:T(8,128)(2,1)}, u32[]{:S(2)}) copy-start(bf16[128,1024]{0,1:T(8,128)(2,1)} %copy.99) | copy-start | bytes 786436
  101.8 13.6 %collective-permute-start.6 = (bf16[1024,128]{0,1:T(8,128)(2,1)}, bf16[1024,128]{0,1:T(8,128)(2,1)}, u32[]{:S(2)}, u32[]{:S(2)}) collective-permute-start(bf16[1024,128]{0,1:T(8,128)(2,1)} %get-tuple-element.14), channel_id=1, source_target_pairs={{0,16},{4,20},{8,24},{12,28},{16,0},{20,4},{24,8},{28,12},{1,17},{... | collective-permute-start | bytes 786440 | tf_op jit(solution)/shard_map/ppermute | solution.py:191
  122.7 6.9 %collective-permute-start.13 = (bf16[2,2,2,2,32,1536]{5,4,3,2,1,0:T(8,128)(2,1)}, bf16[2,2,2,2,32,1536]{5,4,3,2,1,0:T(8,128)(2,1)}, u32[]{:S(2)}, u32[]{:S(2)}) collective-permute-start(bf16[2,2,2,2,32,1536]{5,4,3,2,1,0:T(8,128)(2,1)} %fusion.13), channel_id=1, source_target_pairs={{0,4},{4,0},{8,12},{12,8},{16,20},{20,16},{24,28},{28,24},{1,5},{5... | collective-permute-start | bytes 4718600 | tf_op jit(solution)/shard_map/ppermute | solution.py:155
  123.4 3.6 %collective-permute-start.18 = (bf16[2,2,2,2,16,1024]{5,4,3,2,1,0:T(8,128)(2,1)S(1)}, bf16[2,2,2,2,16,1024]{5,4,3,2,1,0:T(8,128)(2,1)}, u32[]{:S(2)}, u32[]{:S(2)}) collective-permute-start(bf16[2,2,2,2,16,1024]{5,4,3,2,1,0:T(8,128)(2,1)S(1)} %fusion.40), channel_id=1, source_target_pairs={{0,4},{4,0},{8,12},{12,8},{16,20},{20,16},{24,28},{28,24},{1,5},{5... | collective-permute-start | bytes 1572872 | tf_op jit(solution)/shard_map/ppermute | solution.py:153
  128.9 6.8 %collective-permute-start.19 = (bf16[2,2,2,16,1024]{4,3,2,1,0:T(8,128)(2,1)}, bf16[2,2,2,16,1024]{4,3,2,1,0:T(8,128)(2,1)}, u32[]{:S(2)}, u32[]{:S(2)}) collective-permute-start(bf16[2,2,2,16,1024]{4,3,2,1,0:T(8,128)(2,1)} %fusion.45), channel_id=1, source_target_pairs={{0,8},{4,20},{8,0},{12,28},{16,24},{20,4},{24,16},{28,12},{1,9},{5... | collective-permute-start | bytes 786440 | tf_op jit(solution)/shard_map/ppermute | solution.py:153
  134.2 13.5 %collective-permute-start.14 = (bf16[2,2,2,32,1536]{4,3,2,1,0:T(8,128)(2,1)S(1)}, bf16[2,2,2,32,1536]{4,3,2,1,0:T(8,128)(2,1)S(1)}, u32[]{:S(2)}, u32[]{:S(2)}) collective-permute-start(bf16[2,2,2,32,1536]{4,3,2,1,0:T(8,128)(2,1)S(1)} %fusion.14), channel_id=1, source_target_pairs={{0,8},{4,20},{8,0},{12,28},{16,24},{20,4},{24,16},{28,12},{1,9},{5... | collective-permute-start | bytes 2359304 | tf_op jit(solution)/shard_map/ppermute | solution.py:155
  136.8 12.9 %collective-permute-start.20 = (bf16[2,2,16,1024]{3,2,1,0:T(8,128)(2,1)S(1)}, bf16[2,2,16,1024]{3,2,1,0:T(8,128)(2,1)S(1)}, u32[]{:S(2)}, u32[]{:S(2)}) collective-permute-start(bf16[2,2,16,1024]{3,2,1,0:T(8,128)(2,1)S(1)} %fusion.62), channel_id=1, source_target_pairs={{0,16},{4,12},{8,24},{12,4},{16,0},{20,28},{24,8},{28,20},{1,17},{... | collective-permute-start | bytes 393224 | tf_op jit(solution)/shard_map/ppermute | solution.py:153
  141.4 8.3 %collective-permute-start.8 = (f32[1025]{0:T(1024)S(1)}, f32[1025]{0:T(1024)S(1)}, u32[]{:S(2)}, u32[]{:S(2)}) collective-permute-start(f32[1025]{0:T(1024)S(1)} %pad_maximum_fusion.5), channel_id=1, source_target_pairs={{0,4},{4,0},{8,12},{12,8},{16,20},{20,16},{24,28},{28,24},{1,5},{5... | collective-permute-start | bytes 12308 | tf_op jit(solution)/shard_map/ppermute | solution.py:155
  148.2 7.8 %collective-permute-start.15 = (bf16[2,2,32,1536]{3,2,1,0:T(8,128)(2,1)S(1)}, bf16[2,2,32,1536]{3,2,1,0:T(8,128)(2,1)S(1)}, u32[]{:S(2)}, u32[]{:S(2)}) collective-permute-start(bf16[2,2,32,1536]{3,2,1,0:T(8,128)(2,1)S(1)} %fusion.51), channel_id=1, source_target_pairs={{0,16},{4,12},{8,24},{12,4},{16,0},{20,28},{24,8},{28,20},{1,17},{... | collective-permute-start | bytes 1179656 | tf_op jit(solution)/shard_map/ppermute | solution.py:155
  150.4 3.7 %collective-permute-start.9 = (f32[1025]{0:T(1024)S(1)}, f32[1025]{0:T(1024)S(1)}, u32[]{:S(2)}, u32[]{:S(2)}) collective-permute-start(f32[1025]{0:T(1024)S(1)} %fusion.76), channel_id=1, source_target_pairs={{0,8},{4,20},{8,0},{12,28},{16,24},{20,4},{24,16},{28,12},{1,9},{5... | collective-permute-start | bytes 12308 | tf_op jit(solution)/shard_map/ppermute | solution.py:155
  151.0 6.9 %collective-permute-start.21 = (bf16[2,16,1024]{2,1,0:T(8,128)(2,1)S(1)}, bf16[2,16,1024]{2,1,0:T(8,128)(2,1)S(1)}, u32[]{:S(2)}, u32[]{:S(2)}) collective-permute-start(bf16[2,16,1024]{2,1,0:T(8,128)(2,1)S(1)} %fusion.70), channel_id=1, source_target_pairs={{0,1},{1,0},{2,3},{3,2},{4,5},{5,4},{6,7},{7,6},{8,9},{9,8},{10,11... | collective-permute-start | bytes 196616 | tf_op jit(solution)/shard_map/ppermute | solution.py:164
  154.1 3.8 %collective-permute-start.10 = (f32[1025]{0:T(1024)S(1)}, f32[1025]{0:T(1024)S(1)}, u32[]{:S(2)}, u32[]{:S(2)}) collective-permute-start(f32[1025]{0:T(1024)S(1)} %add.315), channel_id=1, source_target_pairs={{0,16},{4,12},{8,24},{12,4},{16,0},{20,28},{24,8},{28,20},{1,17},{... | collective-permute-start | bytes 12308 | tf_op jit(solution)/shard_map/ppermute | solution.py:155
  156.0 15.1 %copy-start.1 = (bf16[1,512,1024]{2,1,0:T(8,128)(2,1)S(1)}, bf16[1,512,1024]{2,1,0:T(8,128)(2,1)}, u32[]{:S(2)}) copy-start(bf16[1,512,1024]{2,1,0:T(8,128)(2,1)} %param.7) | copy-start | bytes 3145732
  156.2 8.5 %collective-permute-start.16 = (bf16[2,32,1536]{2,1,0:T(8,128)(2,1)S(1)}, bf16[2,32,1536]{2,1,0:T(8,128)(2,1)S(1)}, u32[]{:S(2)}, u32[]{:S(2)}) collective-permute-start(bf16[2,32,1536]{2,1,0:T(8,128)(2,1)S(1)} %fusion.61), channel_id=1, source_target_pairs={{0,1},{1,0},{2,3},{3,2},{4,5},{5,4},{6,7},{7,6},{8,9},{9,8},{10,11... | collective-permute-start | bytes 589832 | tf_op jit(solution)/shard_map/ppermute | solution.py:166
  157.9 4.1 %collective-permute-start.11 = (f32[1025]{0:T(1024)S(1)}, f32[1025]{0:T(1024)S(1)}, u32[]{:S(2)}, u32[]{:S(2)}) collective-permute-start(f32[1025]{0:T(1024)S(1)} %add.316), channel_id=1, source_target_pairs={{0,1},{1,0},{2,3},{3,2},{4,5},{5,4},{6,7},{7,6},{8,9},{9,8},{10,11... | collective-permute-start | bytes 12308 | tf_op jit(solution)/shard_map/ppermute | solution.py:166
  159.3 5.8 %collective-permute-start.22 = (bf16[16,1024]{1,0:T(8,128)(2,1)S(1)}, bf16[16,1024]{1,0:T(8,128)(2,1)S(1)}, u32[]{:S(2)}, u32[]{:S(2)}) collective-permute-start(bf16[16,1024]{1,0:T(8,128)(2,1)S(1)} %fusion.72), channel_id=1, source_target_pairs={{0,2},{1,3},{2,0},{3,1},{4,6},{5,7},{6,4},{7,5},{8,10},{9,11},{10,... | collective-permute-start | bytes 98312 | tf_op jit(solution)/shard_map/ppermute | solution.py:164
  162.0 5.0 %collective-permute-start.12 = (f32[1025]{0:T(1024)S(1)}, f32[1025]{0:T(1024)S(1)}, u32[]{:S(2)}, u32[]{:S(2)}) collective-permute-start(f32[1025]{0:T(1024)S(1)} %add.317), channel_id=1, source_target_pairs={{0,2},{1,3},{2,0},{3,1},{4,6},{5,7},{6,4},{7,5},{8,10},{9,11},{10,... | collective-permute-start | bytes 12308 | tf_op jit(solution)/shard_map/ppermute | solution.py:166
  164.8 5.6 %collective-permute-start.17 = (bf16[32,1536]{1,0:T(8,128)(2,1)S(1)}, bf16[32,1536]{1,0:T(8,128)(2,1)S(1)}, u32[]{:S(2)}, u32[]{:S(2)}) collective-permute-start(bf16[32,1536]{1,0:T(8,128)(2,1)S(1)} %fusion.69), channel_id=1, source_target_pairs={{0,2},{1,3},{2,0},{3,1},{4,6},{5,7},{6,4},{7,5},{8,10},{9,11},{10,... | collective-permute-start | bytes 294920 | tf_op jit(solution)/shard_map/ppermute | solution.py:166
  (26 other events, 99.2 us)

commit v11 on v10

--- a/solution.py
+++ b/solution.py
@@ -296,17 +296,19 @@
     )
     d_prob = jnp.einsum("ihqd,ihdt->ihqt", grad_heads_b, values_b, preferred_element_type=jnp.float32)
     d_score = (prob_full * (d_prob - row_dot[None, :, :, None])).astype(jnp.bfloat16)
-    d_query = 0.125 * jnp.sum(
-        jnp.einsum("ihqt,ihdt->ihqd", d_score, keys_b, preferred_element_type=jnp.float32), axis=0
-    ).transpose(1, 0, 2)
+    d_query_t = 0.125 * jnp.sum(
+        jnp.einsum("ihqt,ihdt->ihdq", d_score, keys_b, preferred_element_type=jnp.float32), axis=0
+    )
     d_key_b = 0.125 * jnp.einsum(
         "ihqd,ihqt->ihdt", queries_b, d_score, preferred_element_type=jnp.float32
     )
     d_pairs = jnp.stack([d_key_b, d_value_b], axis=2).reshape(shards, 2 * inner, rows).astype(jnp.bfloat16)
     accum = return_blocks(d_pairs)
-    d_proj = jnp.concatenate([d_query.reshape(rows, inner), accum.T], axis=1).astype(jnp.bfloat16)
-    grad_wqkv = jnp.dot(exchange_order(hidden).T, d_proj, preferred_element_type=jnp.float32)
-    d_hidden = jnp.dot(d_proj, w_qkv.T, preferred_element_type=jnp.float32)
+    d_proj_t = jnp.concatenate([d_query_t.reshape(inner, rows), accum], axis=0).astype(jnp.bfloat16)
+    grad_wqkv = jnp.einsum(
+        "tf,ct->fc", exchange_order(hidden), d_proj_t, preferred_element_type=jnp.float32
+    )
+    d_hidden = jnp.einsum("ct,fc->tf", d_proj_t, w_qkv, preferred_element_type=jnp.float32)
     grad_ln = jnp.sum(d_hidden * normed, axis=0)
     loss_part = jnp.sum(token_loss)
     small = jnp.concatenate([grad_ln, loss_part.reshape(1)])

time: 173 us -> 171 us (0.988)
    unnamed x69 -> x77, local copies, waits for them, and re-layouts: 8.53 us -> 13.1 us
    convert_element_type x2 -> x1, local copies, waits for them, and re-layouts: 6.04 us -> 1.73 us  [return_blocks(): summed = parts[:half].astype(jnp.float32) + got.astype(jnp.float32)]
    another operation x3, other arithmetic: 5.61 us -> 2.01 us
    slice x2 -> x1, local copies, waits for them, and re-layouts: 3.36 us -> 1.05 us  [return_blocks(): got = lax.ppermute(parts[half:], 'seq', xor_pairs(1))]
    ppermute x3, local copies, waits for them, and re-layouts: 3.09 us -> 5.39 us  [gather_blocks(): lax.ppermute(block, 'seq', xor_pairs(2 * k))]
  transfers between devices with their start and end apart: 26 -> 26, of which waited for: 16 -> 15; matrix products, arithmetic and copies ran while one was open for 21% -> 23% of each run, Pallas kernels for 0% -> 0%
where the time goes in v11:
time: 171 us; the launch traced here: 170 us
  waiting for transfers between devices  46.7 us (27%)
  local copies, waits for them, and re-layouts  40.2 us (24%)
  starting transfers between devices  36 us (21%)
  other arithmetic  23.5 us (14%)
  matrix products  20.8 us (12%)
  between operations  3.16 us (2%)
    unnamed x77, local copies, waits for them, and re-layouts  13.1 us
    ppermute x3, waiting for transfers between devices, return_blocks(): sent = lax.ppermute(summed[k].astype(jnp.bfloat16), 'seq', xor_pairs(2 * k))  12.2 us
    ppermute x6, waiting for transfers between devices, halving_scatter(): lax.ppermute((give.astype(jnp.bfloat16), small), 'seq', pairs)  9.03 us
    ppermute x3, waiting for transfers between devices, gather_blocks(): lax.ppermute(block, 'seq', xor_pairs(2 * k))  8.99 us
    all_to_all x1, waiting for transfers between devices, per_device(): lax.all_to_all(send_tokens, 'seq', split_axis=0, concat_axis=0, tiled=True)  8.09 us
    ppermute x4, starting transfers between devices, halving_scatter(): lax.ppermute((give.astype(jnp.bfloat16), small), 'clip', pairs)  6.13 us
    add x9, other arithmetic, halving_scatter(): data = keep + got.astype(jnp.float32)  6.09 us
    ppermute x3, local copies, waits for them, and re-layouts, gather_blocks(): lax.ppermute(block, 'seq', xor_pairs(2 * k))  5.39 us
  transfers between devices with their start and end apart: 26, of which 15 were waited for; matrix products, arithmetic and copies ran while one was open for 23% of the time, Pallas kernels for 0%

profile of v11, /device:TPU:0, one launch (start us, length us, event | category | flops | bytes accessed | tf_op | source)
XLA Modules:
  0.0 170.4 jit_solution(15242215524974453266)
XLA Ops:
  3.4 5.2 %all-to-all-start = ((s32[8,1,1]{2,1,0:T(1,128)}), s32[8,1,1]{2,1,0:T(1,128)S(1)}, u32[]{:S(2)}, u32[]{:S(2)}) async-start(s32[8,1,1]{2,1,0:T(1,128)} %broadcast_in_dim.44), calls=%async_computation | async-start | bytes 8192 | tf_op jit(solution)/shard_map/all_to_all | solution.py:206
  9.2 3.9 %all-to-all-done = s32[8,1,1]{2,1,0:T(1,128)S(1)} async-done(((s32[8,1,1]{2,1,0:T(1,128)}), s32[8,1,1]{2,1,0:T(1,128)S(1)}, u32[]{:S(2)}, u32[]{:S(2)}) %all-to-all-start) | async-done | bytes 64 | tf_op jit(solution)/shard_map/all_to_all | solution.py:206
  21.1 3.5 %all-to-all-start.1 = ((bf16[8,24,1024]{2,1,0:T(8,128)(2,1)}), bf16[8,24,1024]{2,1,0:T(8,128)(2,1)S(1)}, u32[]{:S(2)}, u32[]{:S(2)}) async-start(bf16[8,24,1024]{2,1,0:T(8,128)(2,1)} %get-tuple-element.16), calls=%async_computation.1 | async-start | bytes 786432 | tf_op jit(solution)/shard_map/all_to_all | solution.py:224
  24.7 8.1 %all-to-all-done.1 = bf16[8,24,1024]{2,1,0:T(8,128)(2,1)S(1)} async-done(((bf16[8,24,1024]{2,1,0:T(8,128)(2,1)}), bf16[8,24,1024]{2,1,0:T(8,128)(2,1)S(1)}, u32[]{:S(2)}, u32[]{:S(2)}) %all-to-all-start.1) | async-done | bytes 393248 | tf_op jit(solution)/shard_map/all_to_all | solution.py:224
  32.8 3.5 %all-to-all-start.2 = ((bf16[8,24,1024]{2,1,0:T(8,128)(2,1)}), bf16[8,24,1024]{2,1,0:T(8,128)(2,1)S(1)}, u32[]{:S(2)}, u32[]{:S(2)}) async-start(bf16[8,24,1024]{2,1,0:T(8,128)(2,1)} %get-tuple-element.15), calls=%async_computation.2 | async-start | bytes 786432 | tf_op jit(solution)/shard_map/all_to_all | solution.py:225
  38.9 2.1 %fusion.23 = bf16[128,1024]{1,0:T(8,128)(2,1)S(1)} fusion(bf16[128,1024]{1,0:T(8,128)(2,1)S(1)} %fusion.36, bf16[1024,1536]{1,0:T(8,128)(2,1)} %param.9), kind=kOutput, calls=%fused_computation.37 | convolution fusion | flops 268566528 | bytes 2621440 | tf_op jit(solution)/shard_map/dot_general | solution.py:251
  41.0 2.9 %collective-permute-start.2 = (bf16[1024,128]{0,1:T(8,128)(2,1)S(1)}, bf16[1024,128]{0,1:T(8,128)(2,1)S(1)}, u32[]{:S(2)}, u32[]{:S(2)}) collective-permute-start(bf16[1024,128]{0,1:T(8,128)(2,1)S(1)} %bitcast.211), channel_id=1, source_target_pairs={{0,24},{4,28},{8,16},{12,20},{16,8},{20,12},{24,0},{28,4},{1,25},{... | collective-permute-start | bytes 786440 | tf_op jit(solution)/shard_map/ppermute | solution.py:179
  45.4 2.1 %scatter_custom_fusion.1 = bf16[128,1024]{1,0:T(8,128)(2,1)} fusion(s32[192]{0:T(256)S(1)} %bitcast.228, bf16[192,1024]{1,0:T(8,128)(2,1)S(1)} %bitcast.221, bf16[]{:T(256)} %constant.157.clone.1), kind=kCustom, calls=%fused_computation.117 | custom fusion | bytes 262146 | tf_op jit(solution)/shard_map/scatter | solution.py:239
  47.5 3.6 %collective-permute-done.2 = bf16[1024,128]{0,1:T(8,128)(2,1)S(1)} collective-permute-done((bf16[1024,128]{0,1:T(8,128)(2,1)S(1)}, bf16[1024,128]{0,1:T(8,128)(2,1)S(1)}, u32[]{:S(2)}, u32[]{:S(2)}) %collective-permute-start.2) | collective-permute-done | bytes 262176 | tf_op jit(solution)/shard_map/ppermute | solution.py:179
  51.1 5.1 %collective-permute-done.1 = bf16[1024,128]{0,1:T(8,128)(2,1)S(1)} collective-permute-done((bf16[1024,128]{0,1:T(8,128)(2,1)S(1)}, bf16[1024,128]{0,1:T(8,128)(2,1)S(1)}, u32[]{:S(2)}, u32[]{:S(2)}) %collective-permute-start.1) | collective-permute-done | bytes 262176 | tf_op jit(solution)/shard_map/ppermute | solution.py:179
  61.9 1.8 %copy.73 = bf16[1024,128]{1,0:T(8,128)(2,1)} copy(bf16[1024,128]{0,1:T(8,128)(2,1)} %copy-done.18) | data formatting | bytes 524288 | tf_op jit(solution)/shard_map/ppermute | solution.py:179
  63.7 1.8 %copy.72 = bf16[1024,128]{1,0:T(8,128)(2,1)} copy(bf16[1024,128]{0,1:T(8,128)(2,1)} %copy-done.19) | data formatting | bytes 524288 | tf_op jit(solution)/shard_map/ppermute | solution.py:179
  65.5 1.8 %copy.71 = bf16[1024,128]{1,0:T(8,128)(2,1)} copy(bf16[1024,128]{0,1:T(8,128)(2,1)} %copy-done.20) | data formatting | bytes 524288 | tf_op jit(solution)/shard_map/ppermute | solution.py:179
  70.3 2.3 %copy.74 = bf16[4,1024,128]{2,1,0:T(8,128)(2,1)} copy(bf16[4,1024,128]{1,2,0:T(8,128)(2,1)} %collective-permute-done.3) | data formatting | bytes 2097152 | tf_op jit(solution)/shard_map/ppermute | solution.py:181
  76.7 1.6 fusion.57
  81.4 3.9 %fusion.19 = bf16[8,8,1,64,128]{4,3,1,0,2:T(8,128)(2,1)S(1)} fusion(f32[8,8,128,128]{2,3,1,0:T(8,128)} %copy-done.1, f32[8,128]{1,0:T(8,128)S(1)} %log_add_fusion, bf16[8,128,64]{1,2,0:T(8,128)(2,1)S(1)} %bitcast.198), kind=kOutput, calls=%fused_computation.33 | convolution fusion | flops 137887744 | bytes 5378048 | tf_op jit(solution)/shard_map/ihqd,ihqt->ihdt/dot_general | solution.py:294
  85.3 2.6 %multiply_convert_fusion = bf16[8,8,128,128]{2,3,1,0:T(8,128)(2,1)S(1)} fusion(f32[8,8,128,128]{2,3,1,0:T(8,128)S(1)} %copy-done.2, f32[8,128]{1,0:T(8,128)S(1)} %multiply_reduce_fusion.4, f32[8,128]{1,0:T(8,128)S(1)} %log_add_fusion, bf16[8,8,2,64,128]{4,3,2,1,0:T(8,128)(2,1)} %copy-done.8, bf16[8,128,64]{1,2,0:T(8,128)(2,1)S(1)} %bitcast.199), kind=kOutput, calls=%fused_computation.6 | convolution fusion | flops 139460608 | bytes 7479296 | tf_op jit(solution)/shard_map/ihqd,ihdt->ihqt/dot_general | solution.py:297
  92.6 1.8 %copy.89 = bf16[128,1024]{0,1:T(8,128)(2,1)} copy(bf16[128,1024]{1,0:T(8,128)(2,1)} %copy-done.17) | data formatting | bytes 524288 | tf_op jit(solution)/shard_map/convert_element_type | solution.py:21
  94.4 1.7 %copy.87 = f32[4,8,2,64,128]{4,3,2,1,0:T(8,128)S(1)} copy(f32[4,8,2,64,128]{4,3,1,0,2:T(8,128)} %get-tuple-element.10) | data formatting | bytes 4194304 | tf_op jit(solution)/shard_map/convert_element_type | solution.py:188
  96.2 1.7 fusion.80
  102.0 5.1 %collective-permute-done.5 = bf16[1024,128]{1,0:T(8,128)(2,1)S(1)} collective-permute-done((bf16[1024,128]{1,0:T(8,128)(2,1)S(1)}, bf16[1024,128]{1,0:T(8,128)(2,1)S(1)}, u32[]{:S(2)}, u32[]{:S(2)}) %collective-permute-start.5) | collective-permute-done | bytes 262176 | tf_op jit(solution)/shard_map/ppermute | solution.py:191
  107.2 5.7 %collective-permute-done.7 = bf16[1024,128]{1,0:T(8,128)(2,1)S(1)} collective-permute-done((bf16[1024,128]{1,0:T(8,128)(2,1)S(1)}, bf16[1024,128]{1,0:T(8,128)(2,1)S(1)}, u32[]{:S(2)}, u32[]{:S(2)}) %collective-permute-start.7) | collective-permute-done | bytes 262176 | tf_op jit(solution)/shard_map/ppermute | solution.py:191
  115.4 2.6 %copy-done.5 = f32[2,2,2,2,2,32,1536]{6,5,4,3,2,1,0:T(8,128)} copy-done((f32[2,2,2,2,2,32,1536]{6,5,4,3,2,1,0:T(8,128)}, f32[2,2,2,2,2,32,1536]{6,5,4,3,2,1,0:T(8,128)S(1)}, u32[]{:S(2)}) %copy-start.5) | copy-done | bytes 6291480
  122.1 1.7 collective-permute-done.18
  126.7 2.9 %bitcast_add_fusion = f32[2,2,2,2,32,1536]{5,4,3,2,1,0:T(8,128)S(1)} fusion(bf16[2,2,2,2,32,1536]{5,4,3,2,1,0:T(8,128)(2,1)} %collective-permute-done.13, f32[2,2,2,2,2,32,1536]{6,5,4,3,2,1,0:T(8,128)} %copy-done.5, s32[]{:T(128)S(6)} %select_n.233), kind=kLoop, calls=%fused_computation.13 | loop fusion | flops 1572864 | bytes 7864324 | tf_op jit(solution)/shard_map/add | solution.py:157
  129.6 1.6 copy-done.3
  135.3 3.6 %fusion.26 = f32[1024]{0:T(1024)S(1)} fusion(bf16[1024,1536]{1,0:T(8,128)(2,1)} %param.9, bf16[128,1024]{1,0:T(8,128)(2,1)S(1)} %scatter_custom_fusion, f32[128]{0:T(128)S(1)} %copy-done.35, f32[128]{0:T(128)S(1)} %broadcast_multiply_fusion.1, bf16[1024,128]{1,0:T(8,128)(2,1)S(1)} %fusion.44, bf16[512,128]{1,0:T(8,128)(2,1)S(1)} %bitcast.218), kind=kOutput, calls=%fused_computation.38 | convolution fusion | flops 404093952 | bytes 3806208 | tf_op jit(solution)/shard_map/ct,fc->tf/dot_general | solution.py:311
  139.6 6.2 %collective-permute-done.14 = bf16[2,2,2,32,1536]{4,3,2,1,0:T(8,128)(2,1)S(1)} collective-permute-done((bf16[2,2,2,32,1536]{4,3,2,1,0:T(8,128)(2,1)}, bf16[2,2,2,32,1536]{4,3,2,1,0:T(8,128)(2,1)S(1)}, u32[]{:S(2)}, u32[]{:S(2)}) %collective-permute-start.14) | collective-permute-done | bytes 786464 | tf_op jit(solution)/shard_map/ppermute | solution.py:155
  149.1 1.6 collective-permute-start.21
  154.4 1.6 collective-permute-start.16
  157.6 2.6 %collective-permute-start.22 = (bf16[16,1024]{1,0:T(8,128)(2,1)S(1)}, bf16[16,1024]{1,0:T(8,128)(2,1)S(1)}, u32[]{:S(2)}, u32[]{:S(2)}) collective-permute-start(bf16[16,1024]{1,0:T(8,128)(2,1)S(1)} %fusion.71), channel_id=1, source_target_pairs={{0,2},{1,3},{2,0},{3,1},{4,6},{5,7},{6,4},{7,5},{8,10},{9,11},{10,... | collective-permute-start | bytes 98312 | tf_op jit(solution)/shard_map/ppermute | solution.py:164
  160.6 2.4 %collective-permute-start.12 = (f32[1025]{0:T(1024)S(1)}, f32[1025]{0:T(1024)S(1)}, u32[]{:S(2)}, u32[]{:S(2)}) collective-permute-start(f32[1025]{0:T(1024)S(1)} %add.317), channel_id=1, source_target_pairs={{0,2},{1,3},{2,0},{3,1},{4,6},{5,7},{6,4},{7,5},{8,10},{9,11},{10,... | collective-permute-start | bytes 12308 | tf_op jit(solution)/shard_map/ppermute | solution.py:166
  (192 shorter events, 68.8 us)
Async XLA Ops:
  0.6 15.2 %copy-start = (bf16[1,512,1024]{2,1,0:T(8,128)(2,1)S(1)}, bf16[1,512,1024]{2,1,0:T(8,128)(2,1)}, u32[]{:S(2)}) copy-start(bf16[1,512,1024]{2,1,0:T(8,128)(2,1)} %param.7) | copy-start | bytes 3145732
  0.6 16.2 %copy-start.6 = (bf16[1,512,1024]{2,1,0:T(8,128)(2,1)S(1)}, bf16[1,512,1024]{2,1,0:T(8,128)(2,1)}, u32[]{:S(2)}) copy-start(bf16[1,512,1024]{2,1,0:T(8,128)(2,1)} %param.6) | copy-start | bytes 3145732
  3.4 9.8 %all-to-all-start = ((s32[8,1,1]{2,1,0:T(1,128)}), s32[8,1,1]{2,1,0:T(1,128)S(1)}, u32[]{:S(2)}, u32[]{:S(2)}) async-start(s32[8,1,1]{2,1,0:T(1,128)} %broadcast_in_dim.44), calls=%async_computation | async-start | bytes 8192 | tf_op jit(solution)/shard_map/all_to_all | solution.py:206
  20.1 18.6 %copy-start.25 = (f32[1024]{0:T(1024)S(1)}, f32[1024]{0:T(1024)}, u32[]{:S(2)}) copy-start(f32[1024]{0:T(1024)} %param.11) | copy-start | bytes 12292
  21.1 11.7 %all-to-all-start.1 = ((bf16[8,24,1024]{2,1,0:T(8,128)(2,1)}), bf16[8,24,1024]{2,1,0:T(8,128)(2,1)S(1)}, u32[]{:S(2)}, u32[]{:S(2)}) async-start(bf16[8,24,1024]{2,1,0:T(8,128)(2,1)} %get-tuple-element.16), calls=%async_computation.1 | async-start | bytes 786432 | tf_op jit(solution)/shard_map/all_to_all | solution.py:224
  32.8 12.6 %all-to-all-start.2 = ((bf16[8,24,1024]{2,1,0:T(8,128)(2,1)}), bf16[8,24,1024]{2,1,0:T(8,128)(2,1)S(1)}, u32[]{:S(2)}, u32[]{:S(2)}) async-start(bf16[8,24,1024]{2,1,0:T(8,128)(2,1)} %get-tuple-element.15), calls=%async_computation.2 | async-start | bytes 786432 | tf_op jit(solution)/shard_map/all_to_all | solution.py:225
  38.8 18.7 %copy-start.17 = (bf16[128,1024]{1,0:T(8,128)(2,1)}, bf16[128,1024]{1,0:T(8,128)(2,1)S(1)}, u32[]{:S(2)}) copy-start(bf16[128,1024]{1,0:T(8,128)(2,1)S(1)} %fusion.36) | copy-start | bytes 786436
  41.0 10.1 %collective-permute-start.2 = (bf16[1024,128]{0,1:T(8,128)(2,1)S(1)}, bf16[1024,128]{0,1:T(8,128)(2,1)S(1)}, u32[]{:S(2)}, u32[]{:S(2)}) collective-permute-start(bf16[1024,128]{0,1:T(8,128)(2,1)S(1)} %bitcast.211), channel_id=1, source_target_pairs={{0,24},{4,28},{8,16},{12,20},{16,8},{20,12},{24,0},{28,4},{1,25},{... | collective-permute-start | bytes 786440 | tf_op jit(solution)/shard_map/ppermute | solution.py:179
  43.9 12.3 %collective-permute-start.1 = (bf16[1024,128]{0,1:T(8,128)(2,1)S(1)}, bf16[1024,128]{0,1:T(8,128)(2,1)S(1)}, u32[]{:S(2)}, u32[]{:S(2)}) collective-permute-start(bf16[1024,128]{0,1:T(8,128)(2,1)S(1)} %bitcast.212), channel_id=1, source_target_pairs={{0,16},{4,20},{8,24},{12,28},{16,0},{20,4},{24,8},{28,12},{1,17},{... | collective-permute-start | bytes 786440 | tf_op jit(solution)/shard_map/ppermute | solution.py:179
  44.4 12.0 %collective-permute-start = (bf16[1024,128]{0,1:T(8,128)(2,1)S(1)}, bf16[1024,128]{0,1:T(8,128)(2,1)S(1)}, u32[]{:S(2)}, u32[]{:S(2)}) collective-permute-start(bf16[1024,128]{0,1:T(8,128)(2,1)S(1)} %bitcast.213), channel_id=1, source_target_pairs={{0,8},{4,12},{8,0},{12,4},{16,24},{20,28},{24,16},{28,20},{1,9},{5... | collective-permute-start | bytes 786440 | tf_op jit(solution)/shard_map/ppermute | solution.py:179
  57.5 12.7 %collective-permute-start.3 = (bf16[4,1024,128]{1,2,0:T(8,128)(2,1)}, bf16[4,1024,128]{1,2,0:T(8,128)(2,1)}, u32[]{:S(2)}, u32[]{:S(2)}) collective-permute-start(bf16[4,1024,128]{1,2,0:T(8,128)(2,1)} %pad_maximum_fusion.1), channel_id=1, source_target_pairs={{0,4},{4,0},{8,12},{12,8},{16,20},{20,16},{24,28},{28,24},{1,5},{5... | collective-permute-start | bytes 3145736 | tf_op jit(solution)/shard_map/ppermute | solution.py:181
  59.2 14.7 %copy-start.14 = (bf16[128,512]{0,1:T(8,128)(2,1)}, bf16[128,512]{0,1:T(8,128)(2,1)S(1)}, u32[]{:S(2)}) copy-start(bf16[128,512]{0,1:T(8,128)(2,1)S(1)} %copy.80) | copy-start | bytes 393220
  92.1 4.0 %collective-permute-start.4 = (bf16[4,1024,128]{2,1,0:T(8,128)(2,1)}, bf16[4,1024,128]{2,1,0:T(8,128)(2,1)}, u32[]{:S(2)}, u32[]{:S(2)}) collective-permute-start(bf16[4,1024,128]{2,1,0:T(8,128)(2,1)} %bitcast.35), channel_id=1, source_target_pairs={{0,4},{4,0},{8,12},{12,8},{16,20},{20,16},{24,28},{28,24},{1,5},{5... | collective-permute-start | bytes 3145736 | tf_op jit(solution)/shard_map/ppermute | solution.py:187
  97.9 9.2 %collective-permute-start.5 = (bf16[1024,128]{1,0:T(8,128)(2,1)S(1)}, bf16[1024,128]{1,0:T(8,128)(2,1)S(1)}, u32[]{:S(2)}, u32[]{:S(2)}) collective-permute-start(bf16[1024,128]{1,0:T(8,128)(2,1)S(1)} %get-tuple-element.12), channel_id=1, source_target_pairs={{0,8},{4,12},{8,0},{12,4},{16,24},{20,28},{24,16},{28,20},{1,9},{5... | collective-permute-start | bytes 786440 | tf_op jit(solution)/shard_map/ppermute | solution.py:191
  99.5 13.4 %collective-permute-start.7 = (bf16[1024,128]{1,0:T(8,128)(2,1)S(1)}, bf16[1024,128]{1,0:T(8,128)(2,1)S(1)}, u32[]{:S(2)}, u32[]{:S(2)}) collective-permute-start(bf16[1024,128]{1,0:T(8,128)(2,1)S(1)} %get-tuple-element.13), channel_id=1, source_target_pairs={{0,24},{4,28},{8,16},{12,20},{16,8},{20,12},{24,0},{28,4},{1,25},{... | collective-permute-start | bytes 786440 | tf_op jit(solution)/shard_map/ppermute | solution.py:191
  100.9 13.4 %copy-start.21 = (bf16[128,1024]{0,1:T(8,128)(2,1)S(1)}, bf16[128,1024]{0,1:T(8,128)(2,1)}, u32[]{:S(2)}) copy-start(bf16[128,1024]{0,1:T(8,128)(2,1)} %copy.89) | copy-start | bytes 786436
  100.9 13.3 %collective-permute-start.6 = (bf16[1024,128]{1,0:T(8,128)(2,1)S(1)}, bf16[1024,128]{1,0:T(8,128)(2,1)S(1)}, u32[]{:S(2)}, u32[]{:S(2)}) collective-permute-start(bf16[1024,128]{1,0:T(8,128)(2,1)S(1)} %get-tuple-element.14), channel_id=1, source_target_pairs={{0,16},{4,20},{8,24},{12,28},{16,0},{20,4},{24,8},{28,12},{1,17},{... | collective-permute-start | bytes 786440 | tf_op jit(solution)/shard_map/ppermute | solution.py:191
  119.4 7.3 %collective-permute-start.13 = (bf16[2,2,2,2,32,1536]{5,4,3,2,1,0:T(8,128)(2,1)}, bf16[2,2,2,2,32,1536]{5,4,3,2,1,0:T(8,128)(2,1)}, u32[]{:S(2)}, u32[]{:S(2)}) collective-permute-start(bf16[2,2,2,2,32,1536]{5,4,3,2,1,0:T(8,128)(2,1)} %fusion.13), channel_id=1, source_target_pairs={{0,4},{4,0},{8,12},{12,8},{16,20},{20,16},{24,28},{28,24},{1,5},{5... | collective-permute-start | bytes 4718600 | tf_op jit(solution)/shard_map/ppermute | solution.py:155
  121.5 2.2 %collective-permute-start.18 = (bf16[2,2,2,2,16,1024]{5,4,3,2,1,0:T(8,128)(2,1)S(1)}, bf16[2,2,2,2,16,1024]{5,4,3,2,1,0:T(8,128)(2,1)}, u32[]{:S(2)}, u32[]{:S(2)}) collective-permute-start(bf16[2,2,2,2,16,1024]{5,4,3,2,1,0:T(8,128)(2,1)S(1)} %fusion.40), channel_id=1, source_target_pairs={{0,4},{4,0},{8,12},{12,8},{16,20},{20,16},{24,28},{28,24},{1,5},{5... | collective-permute-start | bytes 1572872 | tf_op jit(solution)/shard_map/ppermute | solution.py:153
  126.0 7.6 %collective-permute-start.19 = (bf16[2,2,2,16,1024]{4,3,2,1,0:T(8,128)(2,1)}, bf16[2,2,2,16,1024]{4,3,2,1,0:T(8,128)(2,1)}, u32[]{:S(2)}, u32[]{:S(2)}) collective-permute-start(bf16[2,2,2,16,1024]{4,3,2,1,0:T(8,128)(2,1)} %fusion.45), channel_id=1, source_target_pairs={{0,8},{4,20},{8,0},{12,28},{16,24},{20,4},{24,16},{28,12},{1,9},{5... | collective-permute-start | bytes 786440 | tf_op jit(solution)/shard_map/ppermute | solution.py:153
  132.2 13.6 %collective-permute-start.14 = (bf16[2,2,2,32,1536]{4,3,2,1,0:T(8,128)(2,1)}, bf16[2,2,2,32,1536]{4,3,2,1,0:T(8,128)(2,1)S(1)}, u32[]{:S(2)}, u32[]{:S(2)}) collective-permute-start(bf16[2,2,2,32,1536]{4,3,2,1,0:T(8,128)(2,1)} %fusion.14), channel_id=1, source_target_pairs={{0,8},{4,20},{8,0},{12,28},{16,24},{20,4},{24,16},{28,12},{1,9},{5... | collective-permute-start | bytes 2359304 | tf_op jit(solution)/shard_map/ppermute | solution.py:155
  134.7 13.1 %collective-permute-start.20 = (bf16[2,2,16,1024]{3,2,1,0:T(8,128)(2,1)S(1)}, bf16[2,2,16,1024]{3,2,1,0:T(8,128)(2,1)S(1)}, u32[]{:S(2)}, u32[]{:S(2)}) collective-permute-start(bf16[2,2,16,1024]{3,2,1,0:T(8,128)(2,1)S(1)} %fusion.61), channel_id=1, source_target_pairs={{0,16},{4,12},{8,24},{12,4},{16,0},{20,28},{24,8},{28,20},{1,17},{... | collective-permute-start | bytes 393224 | tf_op jit(solution)/shard_map/ppermute | solution.py:153
  139.6 8.3 %collective-permute-start.8 = (f32[1025]{0:T(1024)S(1)}, f32[1025]{0:T(1024)S(1)}, u32[]{:S(2)}, u32[]{:S(2)}) collective-permute-start(f32[1025]{0:T(1024)S(1)} %pad_maximum_fusion.5), channel_id=1, source_target_pairs={{0,4},{4,0},{8,12},{12,8},{16,20},{20,16},{24,28},{28,24},{1,5},{5... | collective-permute-start | bytes 12308 | tf_op jit(solution)/shard_map/ppermute | solution.py:155
  146.3 7.9 %collective-permute-start.15 = (bf16[2,2,32,1536]{3,2,1,0:T(8,128)(2,1)S(1)}, bf16[2,2,32,1536]{3,2,1,0:T(8,128)(2,1)S(1)}, u32[]{:S(2)}, u32[]{:S(2)}) collective-permute-start(bf16[2,2,32,1536]{3,2,1,0:T(8,128)(2,1)S(1)} %fusion.51), channel_id=1, source_target_pairs={{0,16},{4,12},{8,24},{12,4},{16,0},{20,28},{24,8},{28,20},{1,17},{... | collective-permute-start | bytes 1179656 | tf_op jit(solution)/shard_map/ppermute | solution.py:155
  148.5 3.9 %collective-permute-start.9 = (f32[1025]{0:T(1024)S(1)}, f32[1025]{0:T(1024)S(1)}, u32[]{:S(2)}, u32[]{:S(2)}) collective-permute-start(f32[1025]{0:T(1024)S(1)} %fusion.75), channel_id=1, source_target_pairs={{0,8},{4,20},{8,0},{12,28},{16,24},{20,4},{24,16},{28,12},{1,9},{5... | collective-permute-start | bytes 12308 | tf_op jit(solution)/shard_map/ppermute | solution.py:155
  149.1 6.9 %collective-permute-start.21 = (bf16[2,16,1024]{2,1,0:T(8,128)(2,1)S(1)}, bf16[2,16,1024]{2,1,0:T(8,128)(2,1)S(1)}, u32[]{:S(2)}, u32[]{:S(2)}) collective-permute-start(bf16[2,16,1024]{2,1,0:T(8,128)(2,1)S(1)} %fusion.69), channel_id=1, source_target_pairs={{0,1},{1,0},{2,3},{3,2},{4,5},{5,4},{6,7},{7,6},{8,9},{9,8},{10,11... | collective-permute-start | bytes 196616 | tf_op jit(solution)/shard_map/ppermute | solution.py:164
  152.4 3.7 %collective-permute-start.10 = (f32[1025]{0:T(1024)S(1)}, f32[1025]{0:T(1024)S(1)}, u32[]{:S(2)}, u32[]{:S(2)}) collective-permute-start(f32[1025]{0:T(1024)S(1)} %add.315), channel_id=1, source_target_pairs={{0,16},{4,12},{8,24},{12,4},{16,0},{20,28},{24,8},{28,20},{1,17},{... | collective-permute-start | bytes 12308 | tf_op jit(solution)/shard_map/ppermute | solution.py:155
  154.4 8.5 %collective-permute-start.16 = (bf16[2,32,1536]{2,1,0:T(8,128)(2,1)S(1)}, bf16[2,32,1536]{2,1,0:T(8,128)(2,1)S(1)}, u32[]{:S(2)}, u32[]{:S(2)}) collective-permute-start(bf16[2,32,1536]{2,1,0:T(8,128)(2,1)S(1)} %fusion.60), channel_id=1, source_target_pairs={{0,1},{1,0},{2,3},{3,2},{4,5},{5,4},{6,7},{7,6},{8,9},{9,8},{10,11... | collective-permute-start | bytes 589832 | tf_op jit(solution)/shard_map/ppermute | solution.py:166
  156.1 4.4 %collective-permute-start.11 = (f32[1025]{0:T(1024)S(1)}, f32[1025]{0:T(1024)S(1)}, u32[]{:S(2)}, u32[]{:S(2)}) collective-permute-start(f32[1025]{0:T(1024)S(1)} %add.316), channel_id=1, source_target_pairs={{0,1},{1,0},{2,3},{3,2},{4,5},{5,4},{6,7},{7,6},{8,9},{9,8},{10,11... | collective-permute-start | bytes 12308 | tf_op jit(solution)/shard_map/ppermute | solution.py:166
  157.6 6.0 %collective-permute-start.22 = (bf16[16,1024]{1,0:T(8,128)(2,1)S(1)}, bf16[16,1024]{1,0:T(8,128)(2,1)S(1)}, u32[]{:S(2)}, u32[]{:S(2)}) collective-permute-start(bf16[16,1024]{1,0:T(8,128)(2,1)S(1)} %fusion.71), channel_id=1, source_target_pairs={{0,2},{1,3},{2,0},{3,1},{4,6},{5,7},{6,4},{7,5},{8,10},{9,11},{10,... | collective-permute-start | bytes 98312 | tf_op jit(solution)/shard_map/ppermute | solution.py:164
  160.6 5.0 %collective-permute-start.12 = (f32[1025]{0:T(1024)S(1)}, f32[1025]{0:T(1024)S(1)}, u32[]{:S(2)}, u32[]{:S(2)}) collective-permute-start(f32[1025]{0:T(1024)S(1)} %add.317), channel_id=1, source_target_pairs={{0,2},{1,3},{2,0},{3,1},{4,6},{5,7},{6,4},{7,5},{8,10},{9,11},{10,... | collective-permute-start | bytes 12308 | tf_op jit(solution)/shard_map/ppermute | solution.py:166
  163.0 5.6 %collective-permute-start.17 = (bf16[32,1536]{1,0:T(8,128)(2,1)S(1)}, bf16[32,1536]{1,0:T(8,128)(2,1)S(1)}, u32[]{:S(2)}, u32[]{:S(2)}) collective-permute-start(bf16[32,1536]{1,0:T(8,128)(2,1)S(1)} %fusion.68), channel_id=1, source_target_pairs={{0,2},{1,3},{2,0},{3,1},{4,6},{5,7},{6,4},{7,5},{8,10},{9,11},{10,... | collective-permute-start | bytes 294920 | tf_op jit(solution)/shard_map/ppermute | solution.py:166
  (30 other events, 75.1 us)

commit v12 on v11

--- a/solution.py
+++ b/solution.py
@@ -118,55 +118,72 @@
     return split.transpose(perm).reshape(values.shape)
 
 
-def halving_scatter(grad, small=None):
+def split_wide(values):
+    high = values.astype(jnp.bfloat16)
+    low = (values - high.astype(jnp.float32)).astype(jnp.bfloat16)
+    return high, low
+
+
+def halving_round(datas, small, axis, pairs, pick):
+    keeps = [pick(data, True) for data in datas]
+    gives = [pick(data, False) for data in datas]
+    high, low = split_wide(small)
+    sizes = [give.size for give in gives]
+    packet = jnp.concatenate([give.astype(jnp.bfloat16).reshape(-1) for give in gives] + [high, low])
+    got = lax.ppermute(packet, axis, pairs)
+    out = []
+    start = 0
+    for keep, size in zip(keeps, sizes):
+        out.append(keep + got[start:start + size].reshape(keep.shape).astype(jnp.float32))
+        start += size
+    width = small.shape[0]
+    mine = high.astype(jnp.float32) + low.astype(jnp.float32)
+    theirs = got[start:start + width].astype(jnp.float32) + got[start + width:].astype(jnp.float32)
+    return out, mine + theirs
+
+
+def halving_scatter(grads, small):
     seq_bits, clip_bits = exchange_bits()
     total = seq_bits + clip_bits
-    data = grad.reshape([2] * total + [-1, grad.shape[1]])
+    datas = [grad.reshape([2] * total + [-1, grad.shape[1]]) for grad in grads]
     order_a = list(range(seq_bits))
     order_b = [0] + list(range(seq_bits - 1, 0, -1))
-    core_bit = lax.axis_index("seq") & 1
+    me = lax.axis_index("seq")
+    core_bit = me & 1
     left_a = list(range(seq_bits))
     left_b = list(range(seq_bits))
     for step in range(seq_bits):
         bit_a, bit_b = order_a[step], order_b[step]
         dim_a, dim_b = left_a.index(bit_a), left_b.index(bit_b)
-        me = lax.axis_index("seq")
         mine_a = (me >> bit_a) & 1
         mine_b = (me >> bit_b) & 1
         pairs = []
         for src in range(lax.axis_size("seq")):
             bit = bit_a if (src & 1) == 0 else bit_b
             pairs.append((src, src ^ (1 << bit)))
-        keep = jnp.where(
-            core_bit == 0,
-            lax.dynamic_index_in_dim(data, mine_a, axis=dim_a, keepdims=False),
-            lax.dynamic_index_in_dim(data, mine_b, axis=dim_b, keepdims=False),
-        )
-        give = jnp.where(
-            core_bit == 0,
-            lax.dynamic_index_in_dim(data, 1 - mine_a, axis=dim_a, keepdims=False),
-            lax.dynamic_index_in_dim(data, 1 - mine_b, axis=dim_b, keepdims=False),
-        )
+
+        def pick(data, keep, dim_a=dim_a, dim_b=dim_b, mine_a=mine_a, mine_b=mine_b):
+            side_a = mine_a if keep else 1 - mine_a
+            side_b = mine_b if keep else 1 - mine_b
+            return jnp.where(
+                core_bit == 0,
+                lax.dynamic_index_in_dim(data, side_a, axis=dim_a, keepdims=False),
+                lax.dynamic_index_in_dim(data, side_b, axis=dim_b, keepdims=False),
+            )
+
         left_a.pop(dim_a)
         left_b.pop(dim_b)
-        if small is None:
-            got = lax.ppermute(give.astype(jnp.bfloat16), "seq", pairs)
-        else:
-            got, got_small = lax.ppermute((give.astype(jnp.bfloat16), small), "seq", pairs)
-            small = small + got_small
-        data = keep + got.astype(jnp.float32)
+        datas, small = halving_round(datas, small, "seq", pairs, pick)
     for bit in range(clip_bits):
         mine = (lax.axis_index("clip") >> bit) & 1
         pairs = [(src, src ^ (1 << bit)) for src in range(lax.axis_size("clip"))]
-        keep = lax.dynamic_index_in_dim(data, mine, axis=0, keepdims=False)
-        give = lax.dynamic_index_in_dim(data, 1 - mine, axis=0, keepdims=False)
-        if small is None:
-            got = lax.ppermute(give.astype(jnp.bfloat16), "clip", pairs)
-        else:
-            got, got_small = lax.ppermute((give.astype(jnp.bfloat16), small), "clip", pairs)
-            small = small + got_small
-        data = keep + got.astype(jnp.float32)
-    return data, small
+
+        def pick(data, keep, mine=mine):
+            side = mine if keep else 1 - mine
+            return lax.dynamic_index_in_dim(data, side, axis=0, keepdims=False)
+
+        datas, small = halving_round(datas, small, "clip", pairs, pick)
+    return datas, small
 
 
 def xor_pairs(mask):
@@ -312,8 +329,7 @@
     grad_ln = jnp.sum(d_hidden * normed, axis=0)
     loss_part = jnp.sum(token_loss)
     small = jnp.concatenate([grad_ln, loss_part.reshape(1)])
-    grad_out, unused = halving_scatter(grad_wout)
-    grad_qkv, small = halving_scatter(grad_wqkv, small)
+    (grad_qkv, grad_out), small = halving_scatter([grad_wqkv, grad_wout], small)
     count_all = shards * lax.axis_size("clip") * TOK_DEV
     return (small[-1] / count_all, grad_qkv.reshape(-1), grad_out.reshape(-1), small[:-1])
 

time: 171 us -> 238 us (1.39)
  local copies, waits for them, and re-layouts: 40.2 us -> 84.8 us
  waiting for transfers between devices: 46.7 us -> 67.8 us
  other arithmetic: 23.5 us -> 35.2 us
  starting transfers between devices: 36 us -> 26.9 us
  matrix products: 20.8 us -> 18.3 us
    concatenate x0 -> x5, local copies, waits for them, and re-layouts: none -> 34.9 us  [halving_round(): jnp.concatenate([give.astype(jnp.bfloat16).reshape(-1) for give in gives]...]
    ppermute x15 -> x5, waiting for transfers between devices: 13.6 us -> 35.8 us  [halving_round(): got = lax.ppermute(packet, axis, pairs)]
    convert_element_type x6 -> x17, local copies, waits for them, and re-layouts: 1.49 us -> 13.1 us  [the longest x8 7.46 us: halving_round(): got[start:start + size].reshape(keep.shape).astype(jnp.float32)]
    convert_element_type x4 -> x18, other arithmetic: 1.9 us -> 13 us  [the longest x8 6.53 us: halving_round(): got[start:start + size].reshape(keep.shape).astype(jnp.float32)]
    ppermute x15 -> x5, starting transfers between devices: 16.3 us -> 7.22 us  [halving_round(): got = lax.ppermute(packet, axis, pairs)]
    add x14 -> x11, other arithmetic: 6.76 us -> 9.43 us  [the longest x10 9.35 us: halving_round(): keep + got[start:start + size].reshape(keep.shape).astype(jnp.float32)]
    dot_general x1, matrix products: 3.59 us -> 1.18 us  [per_device(): jnp.einsum('ct,fc->tf', d_proj_t, w_qkv, preferred_element_type=jnp.float32)]
    unnamed x77 -> x83, local copies, waits for them, and re-layouts: 13.1 us -> 13.1 us
  transfers between devices with their start and end apart: 26 -> 16, of which waited for: 15 -> 11; matrix products, arithmetic and copies ran while one was open for 23% -> 6% of each run, Pallas kernels for 0% -> 0%
where the time goes in v12:
time: 238 us; the launch traced here: 236 us
  local copies, waits for them, and re-layouts  84.8 us (36%)
  waiting for transfers between devices  67.8 us (28%)
  other arithmetic  35.2 us (15%)
  starting transfers between devices  26.9 us (11%)
  matrix products  18.3 us (8%)
  between operations  3.36 us (1%)
    ppermute x5, waiting for transfers between devices, halving_round(): got = lax.ppermute(packet, axis, pairs)  35.8 us
    concatenate x5, local copies, waits for them, and re-layouts, halving_round(): jnp.concatenate([give.astype(jnp.bfloat16).reshape(-1) for give in gives]...  34.9 us
    unnamed x83, local copies, waits for them, and re-layouts  13.1 us
    ppermute x3, waiting for transfers between devices, gather_blocks(): lax.ppermute(block, 'seq', xor_pairs(2 * k))  10.2 us
    ppermute x3, waiting for transfers between devices, return_blocks(): sent = lax.ppermute(summed[k].astype(jnp.bfloat16), 'seq', xor_pairs(2 * k))  9.87 us
    add x10, other arithmetic, halving_round(): keep + got[start:start + size].reshape(keep.shape).astype(jnp.float32)  9.35 us
    all_to_all x1, waiting for transfers between devices, per_device(): lax.all_to_all(send_tokens, 'seq', split_axis=0, concat_axis=0, tiled=True)  8 us
    convert_element_type x8, local copies, waits for them, and re-layouts, halving_round(): got[start:start + size].reshape(keep.shape).astype(jnp.float32)  7.46 us
  transfers between devices with their start and end apart: 16, of which 11 were waited for; matrix products, arithmetic and copies ran while one was open for 6% of the time, Pallas kernels for 0%

profile of v12, /device:TPU:0, one launch (start us, length us, event | category | flops | bytes accessed | tf_op | source)
XLA Modules:
  0.0 236.4 jit_solution(6932050187053149547)
XLA Ops:
  3.4 5.2 %all-to-all-start = ((s32[8,1,1]{2,1,0:T(1,128)}), s32[8,1,1]{2,1,0:T(1,128)S(1)}, u32[]{:S(2)}, u32[]{:S(2)}) async-start(s32[8,1,1]{2,1,0:T(1,128)} %broadcast_in_dim.44), calls=%async_computation | async-start | bytes 8192 | tf_op jit(solution)/shard_map/all_to_all | solution.py:223
  9.2 3.9 %all-to-all-done = s32[8,1,1]{2,1,0:T(1,128)S(1)} async-done(((s32[8,1,1]{2,1,0:T(1,128)}), s32[8,1,1]{2,1,0:T(1,128)S(1)}, u32[]{:S(2)}, u32[]{:S(2)}) %all-to-all-start) | async-done | bytes 64 | tf_op jit(solution)/shard_map/all_to_all | solution.py:223
  21.0 3.5 %all-to-all-start.1 = ((bf16[8,24,1024]{2,1,0:T(8,128)(2,1)}), bf16[8,24,1024]{2,1,0:T(8,128)(2,1)S(1)}, u32[]{:S(2)}, u32[]{:S(2)}) async-start(bf16[8,24,1024]{2,1,0:T(8,128)(2,1)} %get-tuple-element.24), calls=%async_computation.1 | async-start | bytes 786432 | tf_op jit(solution)/shard_map/all_to_all | solution.py:241
  24.7 8.0 %all-to-all-done.1 = bf16[8,24,1024]{2,1,0:T(8,128)(2,1)S(1)} async-done(((bf16[8,24,1024]{2,1,0:T(8,128)(2,1)}), bf16[8,24,1024]{2,1,0:T(8,128)(2,1)S(1)}, u32[]{:S(2)}, u32[]{:S(2)}) %all-to-all-start.1) | async-done | bytes 393248 | tf_op jit(solution)/shard_map/all_to_all | solution.py:241
  34.8 2.1 fusion.21
  38.1 2.4 %collective-permute-start.2 = (bf16[1024,128]{0,1:T(8,128)(2,1)S(1)}, bf16[1024,128]{0,1:T(8,128)(2,1)S(1)}, u32[]{:S(2)}, u32[]{:S(2)}) collective-permute-start(bf16[1024,128]{0,1:T(8,128)(2,1)S(1)} %bitcast.206), channel_id=1, source_target_pairs={{0,24},{4,28},{8,16},{12,20},{16,8},{20,12},{24,0},{28,4},{1,25},{... | collective-permute-start | bytes 786440 | tf_op jit(solution)/shard_map/ppermute | solution.py:196
  40.5 3.5 %all-to-all-start.2 = ((bf16[8,24,1024]{2,1,0:T(8,128)(2,1)}), bf16[8,24,1024]{2,1,0:T(8,128)(2,1)S(1)}, u32[]{:S(2)}, u32[]{:S(2)}) async-start(bf16[8,24,1024]{2,1,0:T(8,128)(2,1)} %get-tuple-element.23), calls=%async_computation.2 | async-start | bytes 786432 | tf_op jit(solution)/shard_map/all_to_all | solution.py:242
  44.1 2.1 collective-permute-done
  46.3 8.1 %collective-permute-done.1 = bf16[1024,128]{0,1:T(8,128)(2,1)S(1)} collective-permute-done((bf16[1024,128]{0,1:T(8,128)(2,1)S(1)}, bf16[1024,128]{0,1:T(8,128)(2,1)S(1)}, u32[]{:S(2)}, u32[]{:S(2)}) %collective-permute-start.1) | collective-permute-done | bytes 262176 | tf_op jit(solution)/shard_map/ppermute | solution.py:196
  60.0 1.8 copy.72
  64.0 2.5 %copy.74 = bf16[4,1024,128]{2,1,0:T(8,128)(2,1)} copy(bf16[4,1024,128]{1,2,0:T(8,128)(2,1)} %collective-permute-done.3) | data formatting | bytes 2097152 | tf_op jit(solution)/shard_map/ppermute | solution.py:198
  74.8 3.9 %fusion.17 = bf16[8,8,1,64,128]{4,3,1,0,2:T(8,128)(2,1)S(1)} fusion(f32[8,8,128,128]{2,3,1,0:T(8,128)} %copy-done.2, f32[8,128]{1,0:T(8,128)S(1)} %log_add_fusion, bf16[8,128,64]{1,2,0:T(8,128)(2,1)S(1)} %bitcast.185), kind=kOutput, calls=%fused_computation.32 | convolution fusion | flops 137887744 | bytes 5378048 | tf_op jit(solution)/shard_map/ihqd,ihqt->ihdt/dot_general | solution.py:311
  78.7 2.6 %multiply_convert_fusion = bf16[8,8,128,128]{2,3,1,0:T(8,128)(2,1)S(1)} fusion(f32[8,8,128,128]{2,3,1,0:T(8,128)S(1)} %copy-done.3, f32[8,128]{1,0:T(8,128)S(1)} %multiply_reduce_fusion.4, f32[8,128]{1,0:T(8,128)S(1)} %log_add_fusion, bf16[8,8,2,64,128]{4,3,2,1,0:T(8,128)(2,1)} %copy-done.9, bf16[8,128,64]{1,2,0:T(8,128)(2,1)S(1)} %bitcast.186), kind=kOutput, calls=%fused_computation.6 | convolution fusion | flops 139460608 | bytes 7479296 | tf_op jit(solution)/shard_map/ihqd,ihdt->ihqt/dot_general | solution.py:314
  86.8 1.8 copy.87
  92.8 3.4 %collective-permute-start.7 = (bf16[1024,128]{1,0:T(8,128)(2,1)S(1)}, bf16[1024,128]{1,0:T(8,128)(2,1)S(1)}, u32[]{:S(2)}, u32[]{:S(2)}) collective-permute-start(bf16[1024,128]{1,0:T(8,128)(2,1)S(1)} %get-tuple-element.21), channel_id=1, source_target_pairs={{0,24},{4,28},{8,16},{12,20},{16,8},{20,12},{24,0},{28,4},{1,25},{... | collective-permute-start | bytes 786440 | tf_op jit(solution)/shard_map/ppermute | solution.py:208
  96.7 5.1 %collective-permute-done.5 = bf16[1024,128]{1,0:T(8,128)(2,1)S(1)} collective-permute-done((bf16[1024,128]{1,0:T(8,128)(2,1)S(1)}, bf16[1024,128]{1,0:T(8,128)(2,1)S(1)}, u32[]{:S(2)}, u32[]{:S(2)}) %collective-permute-start.5) | collective-permute-done | bytes 262176 | tf_op jit(solution)/shard_map/ppermute | solution.py:208
  101.8 4.7 %collective-permute-done.6 = bf16[1024,128]{1,0:T(8,128)(2,1)S(1)} collective-permute-done((bf16[1024,128]{1,0:T(8,128)(2,1)S(1)}, bf16[1024,128]{1,0:T(8,128)(2,1)S(1)}, u32[]{:S(2)}, u32[]{:S(2)}) %collective-permute-start.6) | collective-permute-done | bytes 262176 | tf_op jit(solution)/shard_map/ppermute | solution.py:208
  110.3 2.6 %copy-done.5 = f32[2,2,2,2,2,32,1536]{6,5,4,3,2,1,0:T(8,128)} copy-done((f32[2,2,2,2,2,32,1536]{6,5,4,3,2,1,0:T(8,128)}, f32[2,2,2,2,2,32,1536]{6,5,4,3,2,1,0:T(8,128)S(1)}, u32[]{:S(2)}) %copy-start.5) | copy-done | bytes 6291480
  114.3 3.3 %convert_element_type.336 = bf16[786432]{0:T(1024)(128)(2,1)S(1)} reshape(bf16[1,2,2,2,2,32,1536]{6,5,4,3,2,1,0:T(8,128)(2,1)} %dynamic-slice_convert_fusion) | data formatting | bytes 3145728 | tf_op jit(solution)/shard_map/convert_element_type | solution.py:132
  117.6 21.1 %concatenate.45 = bf16[1050626]{0:T(1024)(128)(2,1)} concatenate(bf16[786432]{0:T(1024)(128)(2,1)S(1)} %convert_element_type.336, bf16[262144]{0:T(1024)(128)(2,1)S(1)} %bitcast.187, bf16[1025]{0:T(1024)(128)(2,1)S(1)} %fusion.72, bf16[1025]{0:T(1024)(128)(2,1)S(1)} %fusion.62), dimensions={0} | concatenate | bytes 4202504 | tf_op jit(solution)/shard_map/concatenate | solution.py:132
  138.7 4.5 %collective-permute-done.8 = bf16[1050626]{0:T(1024)(128)(2,1)} collective-permute-done((bf16[1050626]{0:T(1024)(128)(2,1)}, bf16[1050626]{0:T(1024)(128)(2,1)}, u32[]{:S(2)}, u32[]{:S(2)}) %collective-permute-start.8) | collective-permute-done | bytes 2101284 | tf_op jit(solution)/shard_map/ppermute | solution.py:133
  146.9 3.3 %slice_convert_fusion = f32[786432]{0:T(1024)} fusion(bf16[1050626]{0:T(1024)(128)(2,1)} %collective-permute-done.8), kind=kLoop, calls=%fused_computation.27 | loop fusion | flops 786432 | bytes 4718592 | tf_op jit(solution)/shard_map/convert_element_type | solution.py:137
  150.2 4.6 %reshape.476 = f32[2,2,2,2,32,1536]{5,4,3,2,1,0:T(8,128)} reshape(f32[786432]{0:T(1024)} %slice_convert_fusion) | data formatting | bytes 6291456 | tf_op jit(solution)/shard_map/convert_element_type | solution.py:137
  154.8 3.5 %bitcast_add_fusion = f32[2,2,2,2,32,1536]{5,4,3,2,1,0:T(8,128)S(1)} fusion(f32[2,2,2,2,32,1536]{5,4,3,2,1,0:T(8,128)} %reshape.476, f32[2,2,2,2,2,32,1536]{6,5,4,3,2,1,0:T(8,128)} %copy-done.5, s32[]{:T(128)S(6)} %select_n.241), kind=kLoop, calls=%fused_computation.13 | loop fusion | flops 786432 | bytes 9437188 | tf_op jit(solution)/shard_map/add | solution.py:137
  163.3 1.7 select_convert_fusion.2
  166.6 13.0 %concatenate.46 = bf16[526338]{0:T(1024)(128)(2,1)} concatenate(bf16[393216]{0:T(1024)(128)(2,1)S(1)} %select_convert_fusion, bf16[131072]{0:T(1024)(128)(2,1)} %select_convert_fusion.2, bf16[1025]{0:T(1024)(128)(2,1)S(1)} %get-tuple-element.13, bf16[1025]{0:T(1024)(128)(2,1)S(1)} %get-tuple-element.12), dimensions={0} | concatenate | bytes 2105352 | tf_op jit(solution)/shard_map/concatenate | solution.py:132
  181.3 13.4 %collective-permute-done.9 = bf16[526338]{0:T(1024)(128)(2,1)S(1)} collective-permute-done((bf16[526338]{0:T(1024)(128)(2,1)}, bf16[526338]{0:T(1024)(128)(2,1)S(1)}, u32[]{:S(2)}, u32[]{:S(2)}) %collective-permute-start.9) | collective-permute-done | bytes 1052708 | tf_op jit(solution)/shard_map/ppermute | solution.py:133
  198.5 2.8 %fusion.13 = f32[2,2,2,32,1536]{4,3,2,1,0:T(8,128)S(1)} fusion(f32[2,2,2,32,1536]{4,3,2,1,0:T(8,128)} %reshape.478, f32[2,2,2,2,32,1536]{5,4,3,2,1,0:T(8,128)} %copy-done.4, s32[]{:T(128)S(6)} %select_n.250, s32[]{:T(128)S(6)} %select_n.249, pred[]{:T(512)S(6)} %eq.5), kind=kLoop, calls=%fused_computation.29 | loop fusion | flops 786432 | bytes 6291465 | tf_op jit(solution)/shard_map/add | solution.py:137
  204.5 8.0 %collective-permute-done.10 = bf16[264194]{0:T(1024)(128)(2,1)} collective-permute-done((bf16[264194]{0:T(1024)(128)(2,1)S(1)}, bf16[264194]{0:T(1024)(128)(2,1)}, u32[]{:S(2)}, u32[]{:S(2)}) %collective-permute-start.10) | collective-permute-done | bytes 528420 | tf_op jit(solution)/shard_map/ppermute | solution.py:133
  218.8 5.2 %collective-permute-done.11 = bf16[133122]{0:T(1024)(128)(2,1)S(1)} collective-permute-done((bf16[133122]{0:T(1024)(128)(2,1)S(1)}, bf16[133122]{0:T(1024)(128)(2,1)S(1)}, u32[]{:S(2)}, u32[]{:S(2)}) %collective-permute-start.11) | collective-permute-done | bytes 266276 | tf_op jit(solution)/shard_map/ppermute | solution.py:133
  224.7 2.6 %collective-permute-start.12 = (bf16[67586]{0:T(1024)(128)(2,1)S(1)}, bf16[67586]{0:T(1024)(128)(2,1)S(1)}, u32[]{:S(2)}, u32[]{:S(2)}) collective-permute-start(bf16[67586]{0:T(1024)(128)(2,1)S(1)} %concatenate.49), channel_id=1, source_target_pairs={{0,2},{1,3},{2,0},{3,1},{4,6},{5,7},{6,4},{7,5},{8,10},{9,11},{10,... | collective-permute-start | bytes 405524 | tf_op jit(solution)/shard_map/ppermute | solution.py:133
  227.4 4.7 %collective-permute-done.12 = bf16[67586]{0:T(1024)(128)(2,1)S(1)} collective-permute-done((bf16[67586]{0:T(1024)(128)(2,1)S(1)}, bf16[67586]{0:T(1024)(128)(2,1)S(1)}, u32[]{:S(2)}, u32[]{:S(2)}) %collective-permute-start.12) | collective-permute-done | bytes 135204 | tf_op jit(solution)/shard_map/ppermute | solution.py:133
  (210 shorter events, 74.3 us)
Async XLA Ops:
  0.6 14.4 %copy-start = (bf16[1,512,1024]{2,1,0:T(8,128)(2,1)S(1)}, bf16[1,512,1024]{2,1,0:T(8,128)(2,1)}, u32[]{:S(2)}) copy-start(bf16[1,512,1024]{2,1,0:T(8,128)(2,1)} %param.6) | copy-start | bytes 3145732
  0.6 15.4 %copy-start.6 = (bf16[1,512,1024]{2,1,0:T(8,128)(2,1)S(1)}, bf16[1,512,1024]{2,1,0:T(8,128)(2,1)}, u32[]{:S(2)}) copy-start(bf16[1,512,1024]{2,1,0:T(8,128)(2,1)} %param.7) | copy-start | bytes 3145732
  3.4 9.8 %all-to-all-start = ((s32[8,1,1]{2,1,0:T(1,128)}), s32[8,1,1]{2,1,0:T(1,128)S(1)}, u32[]{:S(2)}, u32[]{:S(2)}) async-start(s32[8,1,1]{2,1,0:T(1,128)} %broadcast_in_dim.44), calls=%async_computation | async-start | bytes 8192 | tf_op jit(solution)/shard_map/all_to_all | solution.py:223
  19.2 15.3 %copy-start.23 = (f32[1024]{0:T(1024)S(1)}, f32[1024]{0:T(1024)}, u32[]{:S(2)}) copy-start(f32[1024]{0:T(1024)} %param.11) | copy-start | bytes 12292
  21.0 11.7 %all-to-all-start.1 = ((bf16[8,24,1024]{2,1,0:T(8,128)(2,1)}), bf16[8,24,1024]{2,1,0:T(8,128)(2,1)S(1)}, u32[]{:S(2)}, u32[]{:S(2)}) async-start(bf16[8,24,1024]{2,1,0:T(8,128)(2,1)} %get-tuple-element.24), calls=%async_computation.1 | async-start | bytes 786432 | tf_op jit(solution)/shard_map/all_to_all | solution.py:241
  34.6 5.9 %copy-start.32 = (f32[128]{0:T(128)}, f32[128]{0:T(128)S(1)}, u32[]{:S(2)}) copy-start(f32[128]{0:T(128)S(1)} %add_rsqrt_fusion.2) | copy-start | bytes 1540
  34.8 20.7 %copy-start.16 = (bf16[128,1024]{1,0:T(8,128)(2,1)}, bf16[128,1024]{1,0:T(8,128)(2,1)S(1)}, u32[]{:S(2)}) copy-start(bf16[128,1024]{1,0:T(8,128)(2,1)S(1)} %fusion.34) | copy-start | bytes 786436
  36.9 9.3 %collective-permute-start = (bf16[1024,128]{0,1:T(8,128)(2,1)S(1)}, bf16[1024,128]{0,1:T(8,128)(2,1)S(1)}, u32[]{:S(2)}, u32[]{:S(2)}) collective-permute-start(bf16[1024,128]{0,1:T(8,128)(2,1)S(1)} %bitcast.204), channel_id=1, source_target_pairs={{0,8},{4,12},{8,0},{12,4},{16,24},{20,28},{24,16},{28,20},{1,9},{5... | collective-permute-start | bytes 786440 | tf_op jit(solution)/shard_map/ppermute | solution.py:196
  37.6 16.8 %collective-permute-start.1 = (bf16[1024,128]{0,1:T(8,128)(2,1)S(1)}, bf16[1024,128]{0,1:T(8,128)(2,1)S(1)}, u32[]{:S(2)}, u32[]{:S(2)}) collective-permute-start(bf16[1024,128]{0,1:T(8,128)(2,1)S(1)} %bitcast.205), channel_id=1, source_target_pairs={{0,16},{4,20},{8,24},{12,28},{16,0},{20,4},{24,8},{28,12},{1,17},{... | collective-permute-start | bytes 786440 | tf_op jit(solution)/shard_map/ppermute | solution.py:196
  38.1 16.2 %collective-permute-start.2 = (bf16[1024,128]{0,1:T(8,128)(2,1)S(1)}, bf16[1024,128]{0,1:T(8,128)(2,1)S(1)}, u32[]{:S(2)}, u32[]{:S(2)}) collective-permute-start(bf16[1024,128]{0,1:T(8,128)(2,1)S(1)} %bitcast.206), channel_id=1, source_target_pairs={{0,24},{4,28},{8,16},{12,20},{16,8},{20,12},{24,0},{28,4},{1,25},{... | collective-permute-start | bytes 786440 | tf_op jit(solution)/shard_map/ppermute | solution.py:196
  40.5 16.7 %all-to-all-start.2 = ((bf16[8,24,1024]{2,1,0:T(8,128)(2,1)}), bf16[8,24,1024]{2,1,0:T(8,128)(2,1)S(1)}, u32[]{:S(2)}, u32[]{:S(2)}) async-start(bf16[8,24,1024]{2,1,0:T(8,128)(2,1)} %get-tuple-element.23), calls=%async_computation.2 | async-start | bytes 786432 | tf_op jit(solution)/shard_map/all_to_all | solution.py:242
  46.3 10.9 %copy-start.18 = (bf16[1024,128]{0,1:T(8,128)(2,1)}, bf16[1024,128]{0,1:T(8,128)(2,1)S(1)}, u32[]{:S(2)}) copy-start(bf16[1024,128]{0,1:T(8,128)(2,1)S(1)} %collective-permute-done) | copy-start | bytes 786436
  54.3 4.3 %copy-start.19 = (bf16[1024,128]{0,1:T(8,128)(2,1)}, bf16[1024,128]{0,1:T(8,128)(2,1)S(1)}, u32[]{:S(2)}) copy-start(bf16[1024,128]{0,1:T(8,128)(2,1)S(1)} %collective-permute-done.1) | copy-start | bytes 786436
  54.3 4.3 %copy-start.20 = (bf16[1024,128]{0,1:T(8,128)(2,1)}, bf16[1024,128]{0,1:T(8,128)(2,1)S(1)}, u32[]{:S(2)}) copy-start(bf16[1024,128]{0,1:T(8,128)(2,1)S(1)} %collective-permute-done.2) | copy-start | bytes 786436
  55.5 8.5 %collective-permute-start.3 = (bf16[4,1024,128]{1,2,0:T(8,128)(2,1)}, bf16[4,1024,128]{1,2,0:T(8,128)(2,1)}, u32[]{:S(2)}, u32[]{:S(2)}) collective-permute-start(bf16[4,1024,128]{1,2,0:T(8,128)(2,1)} %pad_maximum_fusion.1), channel_id=1, source_target_pairs={{0,4},{4,0},{8,12},{12,8},{16,20},{20,16},{24,28},{28,24},{1,5},{5... | collective-permute-start | bytes 3145736 | tf_op jit(solution)/shard_map/ppermute | solution.py:198
  58.8 14.8 %copy-start.24 = (f32[128]{0:T(128)}, f32[128]{0:T(128)S(1)}, u32[]{:S(2)}) copy-start(f32[128]{0:T(128)S(1)} %add_rsqrt_fusion) | copy-start | bytes 1540
  74.8 3.9 %copy-start.3 = (f32[8,8,128,128]{2,3,1,0:T(8,128)S(1)}, f32[8,8,128,128]{2,3,1,0:T(8,128)}, u32[]{:S(2)}) copy-start(f32[8,8,128,128]{2,3,1,0:T(8,128)} %copy-done.2) | copy-start | bytes 12582916
  85.4 5.4 %collective-permute-start.4 = (bf16[4,1024,128]{2,1,0:T(8,128)(2,1)}, bf16[4,1024,128]{2,1,0:T(8,128)(2,1)}, u32[]{:S(2)}, u32[]{:S(2)}) collective-permute-start(bf16[4,1024,128]{2,1,0:T(8,128)(2,1)} %bitcast.35), channel_id=1, source_target_pairs={{0,4},{4,0},{8,12},{12,8},{16,20},{20,16},{24,28},{28,24},{1,5},{5... | collective-permute-start | bytes 3145736 | tf_op jit(solution)/shard_map/ppermute | solution.py:204
  90.8 5.3 %copy-start.10 = (bf16[8,8,2,64,128]{4,3,2,1,0:T(8,128)(2,1)S(1)}, bf16[8,8,2,64,128]{4,3,2,1,0:T(8,128)(2,1)}, u32[]{:S(2)}) copy-start(bf16[8,8,2,64,128]{4,3,2,1,0:T(8,128)(2,1)} %copy-done.9) | copy-start | bytes 6291460
  92.6 9.2 %collective-permute-start.5 = (bf16[1024,128]{1,0:T(8,128)(2,1)S(1)}, bf16[1024,128]{1,0:T(8,128)(2,1)S(1)}, u32[]{:S(2)}, u32[]{:S(2)}) collective-permute-start(bf16[1024,128]{1,0:T(8,128)(2,1)S(1)} %get-tuple-element.20), channel_id=1, source_target_pairs={{0,8},{4,12},{8,0},{12,4},{16,24},{20,28},{24,16},{28,20},{1,9},{5... | collective-permute-start | bytes 786440 | tf_op jit(solution)/shard_map/ppermute | solution.py:208
  92.7 13.9 %collective-permute-start.6 = (bf16[1024,128]{1,0:T(8,128)(2,1)S(1)}, bf16[1024,128]{1,0:T(8,128)(2,1)S(1)}, u32[]{:S(2)}, u32[]{:S(2)}) collective-permute-start(bf16[1024,128]{1,0:T(8,128)(2,1)S(1)} %get-tuple-element.22), channel_id=1, source_target_pairs={{0,16},{4,20},{8,24},{12,28},{16,0},{20,4},{24,8},{28,12},{1,17},{... | collective-permute-start | bytes 786440 | tf_op jit(solution)/shard_map/ppermute | solution.py:208
  92.7 14.0 %copy-start.33 = (f32[128]{0:T(128)S(1)}, f32[128]{0:T(128)}, u32[]{:S(2)}) copy-start(f32[128]{0:T(128)} %copy-done.32) | copy-start | bytes 1540
  92.7 14.0 %copy-start.34 = (bf16[1024,1536]{1,0:T(8,128)(2,1)S(1)}, bf16[1024,1536]{1,0:T(8,128)(2,1)}, u32[]{:S(2)}) copy-start(bf16[1024,1536]{1,0:T(8,128)(2,1)} %param.9) | copy-start | bytes 9437188
  92.8 13.8 %collective-permute-start.7 = (bf16[1024,128]{1,0:T(8,128)(2,1)S(1)}, bf16[1024,128]{1,0:T(8,128)(2,1)S(1)}, u32[]{:S(2)}, u32[]{:S(2)}) collective-permute-start(bf16[1024,128]{1,0:T(8,128)(2,1)S(1)} %get-tuple-element.21), channel_id=1, source_target_pairs={{0,24},{4,28},{8,16},{12,20},{16,8},{20,12},{24,0},{28,4},{1,25},{... | collective-permute-start | bytes 786440 | tf_op jit(solution)/shard_map/ppermute | solution.py:208
  138.7 6.8 %copy-start.8 = (f32[2,2,2,2,2,16,1024]{6,5,4,3,2,1,0:T(8,128)S(1)}, f32[2,2,2,2,2,16,1024]{6,5,4,3,2,1,0:T(8,128)}, u32[]{:S(2)}) copy-start(f32[2,2,2,2,2,16,1024]{6,5,4,3,2,1,0:T(8,128)} %copy-done.7) | copy-start | bytes 6291460
  138.7 4.5 %collective-permute-start.8 = (bf16[1050626]{0:T(1024)(128)(2,1)}, bf16[1050626]{0:T(1024)(128)(2,1)}, u32[]{:S(2)}, u32[]{:S(2)}) collective-permute-start(bf16[1050626]{0:T(1024)(128)(2,1)} %concatenate.45), channel_id=1, source_target_pairs={{0,4},{4,0},{8,12},{12,8},{16,20},{20,16},{24,28},{28,24},{1,5},{5... | collective-permute-start | bytes 6303764 | tf_op jit(solution)/shard_map/ppermute | solution.py:133
  179.6 15.1 %collective-permute-start.9 = (bf16[526338]{0:T(1024)(128)(2,1)}, bf16[526338]{0:T(1024)(128)(2,1)S(1)}, u32[]{:S(2)}, u32[]{:S(2)}) collective-permute-start(bf16[526338]{0:T(1024)(128)(2,1)} %concatenate.46), channel_id=1, source_target_pairs={{0,8},{4,20},{8,0},{12,28},{16,24},{20,4},{24,16},{28,12},{1,9},{5... | collective-permute-start | bytes 3158036 | tf_op jit(solution)/shard_map/ppermute | solution.py:133
  203.2 9.4 %collective-permute-start.10 = (bf16[264194]{0:T(1024)(128)(2,1)S(1)}, bf16[264194]{0:T(1024)(128)(2,1)}, u32[]{:S(2)}, u32[]{:S(2)}) collective-permute-start(bf16[264194]{0:T(1024)(128)(2,1)S(1)} %concatenate.47), channel_id=1, source_target_pairs={{0,16},{4,12},{8,24},{12,4},{16,0},{20,28},{24,8},{28,20},{1,17},{... | collective-permute-start | bytes 1585172 | tf_op jit(solution)/shard_map/ppermute | solution.py:133
  215.8 8.4 %copy-start.12 = (f32[2,2,32,1536]{3,2,1,0:T(8,128)S(1)}, f32[2,2,32,1536]{3,2,1,0:T(8,128)}, u32[]{:S(2)}) copy-start(f32[2,2,32,1536]{3,2,1,0:T(8,128)} %copy-done.11) | copy-start | bytes 2359300
  217.2 6.8 %collective-permute-start.11 = (bf16[133122]{0:T(1024)(128)(2,1)S(1)}, bf16[133122]{0:T(1024)(128)(2,1)S(1)}, u32[]{:S(2)}, u32[]{:S(2)}) collective-permute-start(bf16[133122]{0:T(1024)(128)(2,1)S(1)} %concatenate.48), channel_id=1, source_target_pairs={{0,1},{1,0},{2,3},{3,2},{4,5},{5,4},{6,7},{7,6},{8,9},{9,8},{10,11... | collective-permute-start | bytes 798740 | tf_op jit(solution)/shard_map/ppermute | solution.py:133
  224.1 11.2 %copy-start.1 = (bf16[1,512,1024]{2,1,0:T(8,128)(2,1)S(1)}, bf16[1,512,1024]{2,1,0:T(8,128)(2,1)}, u32[]{:S(2)}) copy-start(bf16[1,512,1024]{2,1,0:T(8,128)(2,1)} %param.6) | copy-start | bytes 3145732
  224.7 7.4 %collective-permute-start.12 = (bf16[67586]{0:T(1024)(128)(2,1)S(1)}, bf16[67586]{0:T(1024)(128)(2,1)S(1)}, u32[]{:S(2)}, u32[]{:S(2)}) collective-permute-start(bf16[67586]{0:T(1024)(128)(2,1)S(1)} %concatenate.49), channel_id=1, source_target_pairs={{0,2},{1,3},{2,0},{3,1},{4,6},{5,7},{6,4},{7,5},{8,10},{9,11},{10,... | collective-permute-start | bytes 405524 | tf_op jit(solution)/shard_map/ppermute | solution.py:133
  (19 other events, 30.1 us)

commit v13 on v11

--- a/solution.py
+++ b/solution.py
@@ -182,10 +182,10 @@
     return jnp.concatenate([group, other], axis=0)
 
 
-def return_blocks(parts):
+def return_blocks(own_parts, other_parts):
     half = lax.axis_size("seq") // 2
-    got = lax.ppermute(parts[half:], "seq", xor_pairs(1))
-    summed = parts[:half].astype(jnp.float32) + got.astype(jnp.float32)
+    got = lax.ppermute(other_parts, "seq", xor_pairs(1))
+    summed = own_parts.astype(jnp.bfloat16).astype(jnp.float32) + got.astype(jnp.float32)
     accum = summed[0]
     for k in range(1, half):
         sent = lax.ppermute(summed[k].astype(jnp.bfloat16), "seq", xor_pairs(2 * k))
@@ -220,10 +220,7 @@
     send_target = jnp.where(
         pick_ok[:, :, None], kept_target[pick_safe], jnp.zeros((), jnp.bfloat16)
     )
-    got_tokens, got_target = (
-        lax.all_to_all(send_tokens, "seq", split_axis=0, concat_axis=0, tiled=True),
-        lax.all_to_all(send_target, "seq", split_axis=0, concat_axis=0, tiled=True),
-    )
+    got_tokens = lax.all_to_all(send_tokens, "seq", split_axis=0, concat_axis=0, tiled=True)
     from_pick = (my_index - starts[:, None]) % shards + slot_ids[None, :] * shards
     from_ok = from_pick < count_table[:, None]
     place = jnp.where(from_ok, (starts[:, None] + from_pick) // shards, TOK_DEV).reshape(-1)
@@ -232,11 +229,6 @@
         jnp.zeros((TOK_DEV, width), jnp.bfloat16)
         .at[place]
         .set(got_tokens.reshape(-1, width), mode="drop")
-    )
-    target = (
-        jnp.zeros((TOK_DEV, width), jnp.bfloat16)
-        .at[place]
-        .set(got_target.reshape(-1, width), mode="drop")
     )
     rows = tokens.shape[0]
     inner = w_out.shape[0]
@@ -252,6 +244,13 @@
         jnp.bfloat16
     )
     gathered = gather_blocks(pair_cols)
+    send_target, gathered = lax.optimization_barrier((send_target, gathered))
+    got_target = lax.all_to_all(send_target, "seq", split_axis=0, concat_axis=0, tiled=True)
+    target = (
+        jnp.zeros((TOK_DEV, width), jnp.bfloat16)
+        .at[place]
+        .set(got_target.reshape(-1, width), mode="drop")
+    )
     split_kv = gathered.reshape(shards, heads, 2, HEAD_DIM, rows)
     keys_b = split_kv[:, :, 0]
     values_b = split_kv[:, :, 1]
@@ -302,8 +301,10 @@
     d_key_b = 0.125 * jnp.einsum(
         "ihqd,ihqt->ihdt", queries_b, d_score, preferred_element_type=jnp.float32
     )
-    d_pairs = jnp.stack([d_key_b, d_value_b], axis=2).reshape(shards, 2 * inner, rows).astype(jnp.bfloat16)
-    accum = return_blocks(d_pairs)
+    half = shards // 2
+    own_pairs = jnp.stack([d_key_b[:half], d_value_b[:half]], axis=2).reshape(half, 2 * inner, rows)
+    other_pairs = jnp.stack([d_key_b[half:], d_value_b[half:]], axis=2).reshape(half, 2 * inner, rows)
+    accum = return_blocks(own_pairs, other_pairs.astype(jnp.bfloat16))
     d_proj_t = jnp.concatenate([d_query_t.reshape(inner, rows), accum], axis=0).astype(jnp.bfloat16)
     grad_wqkv = jnp.einsum(
         "tf,ct->fc", exchange_order(hidden), d_proj_t, preferred_element_type=jnp.float32

time: 171 us -> 164 us (0.959)
  local copies, waits for them, and re-layouts: 40.2 us -> 30.8 us
  waiting for transfers between devices: 46.7 us -> 51.8 us
  other arithmetic: 23.5 us -> 18.9 us
  starting transfers between devices: 36 us -> 38.2 us
    ppermute x4 -> x0, local copies, waits for them, and re-layouts: 7.66 us -> none  [the longest x3 5.39 us: gather_blocks(): lax.ppermute(block, 'seq', xor_pairs(2 * k))]
    all_to_all x1, waiting for transfers between devices: 0.01 us -> 3.5 us  [per_device(): lax.all_to_all(send_target, 'seq', split_axis=0, concat_axis=0, tiled=True)]
    unnamed x77 -> x60, local copies, waits for them, and re-layouts: 13.1 us -> 10 us
    optimization_barrier x0 -> x1, local copies, waits for them, and re-layouts: none -> 3.03 us  [per_device(): send_target, gathered = lax.optimization_barrier((send_target, gathered))]
    another operation x0 -> x3, local copies, waits for them, and re-layouts: none -> 2.83 us  [the longest x2 1.74 us: per_device(): jnp.stack([d_key_b[:half], d_value_b[:half]], axis=2)]
    convert_element_type x2 -> x1, local copies, waits for them, and re-layouts: 2.57 us -> 0.24 us  [return_blocks(): own_parts.astype(jnp.bfloat16).astype(jnp.float32) + got.astype(jnp.float32)]
  transfers between devices with their start and end apart: 26 -> 26, of which waited for: 15 -> 17; matrix products, arithmetic and copies ran while one was open for 23% -> 15% of each run, Pallas kernels for 0% -> 0%
where the time goes in v13:
time: 164 us
  waiting for transfers between devices  51.8 us (32%)
  starting transfers between devices  38.2 us (23%)
  local copies, waits for them, and re-layouts  30.8 us (19%)
  matrix products  20.9 us (13%)
  other arithmetic  18.9 us (12%)
  between operations  3.07 us (2%)
    ppermute x3, waiting for transfers between devices, return_blocks(): sent = lax.ppermute(summed[k].astype(jnp.bfloat16), 'seq', xor_pairs(2 * k))  11.5 us
    ppermute x3, waiting for transfers between devices, gather_blocks(): lax.ppermute(block, 'seq', xor_pairs(2 * k))  10.4 us
    unnamed x60, local copies, waits for them, and re-layouts  10 us
    all_to_all x1, waiting for transfers between devices, per_device(): lax.all_to_all(send_tokens, 'seq', split_axis=0, concat_axis=0, tiled=True)  8.09 us
    ppermute x6, waiting for transfers between devices, halving_scatter(): lax.ppermute((give.astype(jnp.bfloat16), small), 'seq', pairs)  7.4 us
    ppermute x4, starting transfers between devices, halving_scatter(): lax.ppermute((give.astype(jnp.bfloat16), small), 'clip', pairs)  6.2 us
    add x9, other arithmetic, halving_scatter(): data = keep + got.astype(jnp.float32)  5.76 us
    ppermute x6, starting transfers between devices, halving_scatter(): lax.ppermute((give.astype(jnp.bfloat16), small), 'seq', pairs)  5.29 us
  transfers between devices with their start and end apart: 26, of which 17 were waited for; matrix products, arithmetic and copies ran while one was open for 15% of the time, Pallas kernels for 0%

profile of v13, /device:TPU:0, one launch (start us, length us, event | category | flops | bytes accessed | tf_op | source)
XLA Modules:
  0.0 163.6 jit_solution(2415245035792412096)
XLA Ops:
  3.4 5.2 %all-to-all-start = ((s32[8,1,1]{2,1,0:T(1,128)}), s32[8,1,1]{2,1,0:T(1,128)S(1)}, u32[]{:S(2)}, u32[]{:S(2)}) async-start(s32[8,1,1]{2,1,0:T(1,128)} %broadcast_in_dim.46), calls=%async_computation | async-start | bytes 8192 | tf_op jit(solution)/shard_map/all_to_all | solution.py:206
  9.2 3.9 %all-to-all-done = s32[8,1,1]{2,1,0:T(1,128)S(1)} async-done(((s32[8,1,1]{2,1,0:T(1,128)}), s32[8,1,1]{2,1,0:T(1,128)S(1)}, u32[]{:S(2)}, u32[]{:S(2)}) %all-to-all-start) | async-done | bytes 64 | tf_op jit(solution)/shard_map/all_to_all | solution.py:206
  21.1 3.5 %all-to-all-start.1 = ((bf16[8,24,1024]{2,1,0:T(8,128)(2,1)}), bf16[8,24,1024]{2,1,0:T(8,128)(2,1)S(1)}, u32[]{:S(2)}, u32[]{:S(2)}) async-start(bf16[8,24,1024]{2,1,0:T(8,128)(2,1)} %get-tuple-element.21), calls=%async_computation.1 | async-start | bytes 786432 | tf_op jit(solution)/shard_map/all_to_all | solution.py:223
  24.7 8.1 %all-to-all-done.1 = bf16[8,24,1024]{2,1,0:T(8,128)(2,1)S(1)} async-done(((bf16[8,24,1024]{2,1,0:T(8,128)(2,1)}), bf16[8,24,1024]{2,1,0:T(8,128)(2,1)S(1)}, u32[]{:S(2)}, u32[]{:S(2)}) %all-to-all-start.1) | async-done | bytes 393248 | tf_op jit(solution)/shard_map/all_to_all | solution.py:223
  34.9 2.8 %constant_dynamic-update-slice_fusion.4 = (bf16[8,1024,128]{1,2,0:T(8,128)(2,1)}, bf16[128,1024]{1,0:T(8,128)(2,1)S(1)}) fusion(bf16[128,1024]{1,0:T(8,128)(2,1)S(1)} %fusion.30, bf16[1024,1536]{1,0:T(8,128)(2,1)} %param.9), kind=kOutput, calls=%fused_computation.131 | convolution fusion | flops 268566528 | bytes 2883584 | tf_op jit(solution)/shard_map/dot_general | solution.py:243
  38.8 2.4 %collective-permute-start.2 = (bf16[1024,128]{0,1:T(8,128)(2,1)S(1)}, bf16[1024,128]{0,1:T(8,128)(2,1)S(1)}, u32[]{:S(2)}, u32[]{:S(2)}) collective-permute-start(bf16[1024,128]{0,1:T(8,128)(2,1)S(1)} %bitcast.222), channel_id=1, source_target_pairs={{0,24},{4,28},{8,16},{12,20},{16,8},{20,12},{24,0},{28,4},{1,25},{... | collective-permute-start | bytes 786440 | tf_op jit(solution)/shard_map/ppermute | solution.py:179
  41.2 3.5 %collective-permute-done.1 = bf16[1024,128]{0,1:T(8,128)(2,1)S(1)} collective-permute-done((bf16[1024,128]{0,1:T(8,128)(2,1)S(1)}, bf16[1024,128]{0,1:T(8,128)(2,1)S(1)}, u32[]{:S(2)}, u32[]{:S(2)}) %collective-permute-start.1) | collective-permute-done | bytes 262176 | tf_op jit(solution)/shard_map/ppermute | solution.py:179
  44.7 2.8 %collective-permute-done = bf16[1024,128]{0,1:T(8,128)(2,1)S(1)} collective-permute-done((bf16[1024,128]{0,1:T(8,128)(2,1)S(1)}, bf16[1024,128]{0,1:T(8,128)(2,1)S(1)}, u32[]{:S(2)}, u32[]{:S(2)}) %collective-permute-start) | collective-permute-done | bytes 262176 | tf_op jit(solution)/shard_map/ppermute | solution.py:179
  47.5 4.1 %collective-permute-done.2 = bf16[1024,128]{0,1:T(8,128)(2,1)S(1)} collective-permute-done((bf16[1024,128]{0,1:T(8,128)(2,1)S(1)}, bf16[1024,128]{0,1:T(8,128)(2,1)S(1)}, u32[]{:S(2)}, u32[]{:S(2)}) %collective-permute-start.2) | collective-permute-done | bytes 262176 | tf_op jit(solution)/shard_map/ppermute | solution.py:179
  53.5 1.7 %constant_dynamic-update-slice_fusion.3 = bf16[8,1024,128]{1,2,0:T(8,128)(2,1)} fusion(bf16[8,1024,128]{1,2,0:T(8,128)(2,1)} %get-tuple-element.31, bf16[1024,128]{0,1:T(8,128)(2,1)} %copy-done.14), kind=kLoop, calls=%fused_computation.130 | loop fusion | bytes 524288
  57.6 3.0 %copy.53 = bf16[8,1024,128]{2,1,0:T(8,128)(2,1)S(1)} copy(bf16[8,1024,128]{1,2,0:T(8,128)(2,1)} %constant_dynamic-update-slice_fusion) | data formatting | bytes 4194304 | tf_op jit(solution)/shard_map/optimization_barrier | solution.py:247
  60.7 4.1 %all-to-all-start.2 = ((bf16[8,24,1024]{2,1,0:T(8,128)(2,1)}), bf16[8,24,1024]{2,1,0:T(8,128)(2,1)}, u32[]{:S(2)}, u32[]{:S(2)}) async-start(bf16[8,24,1024]{2,1,0:T(8,128)(2,1)} %get-tuple-element.7), calls=%async_computation.2 | async-start | bytes 786432 | tf_op jit(solution)/shard_map/all_to_all | solution.py:248
  67.6 1.6 fusion.51
  69.6 3.5 %all-to-all-done.2 = bf16[8,24,1024]{2,1,0:T(8,128)(2,1)} async-done(((bf16[8,24,1024]{2,1,0:T(8,128)(2,1)}), bf16[8,24,1024]{2,1,0:T(8,128)(2,1)}, u32[]{:S(2)}, u32[]{:S(2)}) %all-to-all-start.2) | async-done | bytes 393248 | tf_op jit(solution)/shard_map/all_to_all | solution.py:248
  73.2 2.1 %scatter_custom_fusion.1 = bf16[128,1024]{1,0:T(8,128)(2,1)S(1)} fusion(s32[192]{0:T(256)S(1)} %bitcast.229, bf16[192,1024]{1,0:T(8,128)(2,1)} %bitcast.23, bf16[]{:T(256)} %constant.162.clone.1), kind=kCustom, calls=%fused_computation.116 | custom fusion | bytes 262656 | tf_op jit(solution)/shard_map/scatter | solution.py:252
  77.0 3.9 %fusion.16 = bf16[8,8,64,128]{3,2,1,0:T(8,128)(2,1)S(1)} fusion(f32[8,8,128,128]{2,3,1,0:T(8,128)} %copy-done.2, f32[8,128]{1,0:T(8,128)S(1)} %log_add_fusion, bf16[8,128,64]{1,2,0:T(8,128)(2,1)S(1)} %bitcast.205), kind=kOutput, calls=%fused_computation.30 | convolution fusion | flops 137887744 | bytes 5378048 | tf_op jit(solution)/shard_map/ihqd,ihqt->ihdt/dot_general | solution.py:293
  80.9 2.6 %multiply_convert_fusion = bf16[8,8,128,128]{2,3,1,0:T(8,128)(2,1)S(1)} fusion(f32[8,8,128,128]{2,3,1,0:T(8,128)S(1)} %copy-done.3, f32[8,128]{1,0:T(8,128)S(1)} %multiply_reduce_fusion.4, f32[8,128]{1,0:T(8,128)S(1)} %log_add_fusion, bf16[8,8,2,64,128]{4,3,2,1,0:T(8,128)(2,1)} %bitcast.202, bf16[8,128,64]{1,2,0:T(8,128)(2,1)S(1)} %bitcast.206), kind=kOutput, calls=%fused_computation.6 | convolution fusion | flops 139460608 | bytes 7479296 | tf_op jit(solution)/shard_map/ihqd,ihdt->ihqt/dot_general | solution.py:296
  91.0 1.6 fusion.74
  96.7 5.1 %collective-permute-done.5 = bf16[1024,128]{1,0:T(8,128)(2,1)S(1)} collective-permute-done((bf16[1024,128]{1,0:T(8,128)(2,1)S(1)}, bf16[1024,128]{1,0:T(8,128)(2,1)S(1)}, u32[]{:S(2)}, u32[]{:S(2)}) %collective-permute-start.5) | collective-permute-done | bytes 262176 | tf_op jit(solution)/shard_map/ppermute | solution.py:191
  101.8 5.0 %collective-permute-done.7 = bf16[1024,128]{1,0:T(8,128)(2,1)S(1)} collective-permute-done((bf16[1024,128]{1,0:T(8,128)(2,1)S(1)}, bf16[1024,128]{1,0:T(8,128)(2,1)S(1)}, u32[]{:S(2)}, u32[]{:S(2)}) %collective-permute-start.7) | collective-permute-done | bytes 262176 | tf_op jit(solution)/shard_map/ppermute | solution.py:191
  110.0 2.6 %copy-done.6 = f32[2,2,2,2,2,32,1536]{6,5,4,3,2,1,0:T(8,128)} copy-done((f32[2,2,2,2,2,32,1536]{6,5,4,3,2,1,0:T(8,128)}, f32[2,2,2,2,2,32,1536]{6,5,4,3,2,1,0:T(8,128)S(1)}, u32[]{:S(2)}) %copy-start.6) | copy-done | bytes 6291480
  115.4 3.0 %collective-permute-done.18 = bf16[2,2,2,2,16,1024]{5,4,3,2,1,0:T(8,128)(2,1)} collective-permute-done((bf16[2,2,2,2,16,1024]{5,4,3,2,1,0:T(8,128)(2,1)S(1)}, bf16[2,2,2,2,16,1024]{5,4,3,2,1,0:T(8,128)(2,1)}, u32[]{:S(2)}, u32[]{:S(2)}) %collective-permute-start.18) | collective-permute-done | bytes 524320 | tf_op jit(solution)/shard_map/ppermute | solution.py:153
  120.2 2.9 %bitcast_add_fusion = f32[2,2,2,2,32,1536]{5,4,3,2,1,0:T(8,128)S(1)} fusion(bf16[2,2,2,2,32,1536]{5,4,3,2,1,0:T(8,128)(2,1)} %collective-permute-done.13, f32[2,2,2,2,2,32,1536]{6,5,4,3,2,1,0:T(8,128)} %copy-done.6, s32[]{:T(128)S(6)} %select_n.233), kind=kLoop, calls=%fused_computation.13 | loop fusion | flops 1572864 | bytes 7864324 | tf_op jit(solution)/shard_map/add | solution.py:157
  123.1 1.6 copy-done.4
  124.9 1.6 collective-permute-start.14
  129.1 3.1 %fusion.22 = f32[1024]{0:T(1024)S(1)} fusion(bf16[1024,1536]{1,0:T(8,128)(2,1)} %param.9, bf16[128,1024]{1,0:T(8,128)(2,1)S(1)} %scatter_custom_fusion, f32[128]{0:T(128)S(1)} %copy-done.27, f32[128]{0:T(128)S(1)} %broadcast_multiply_fusion.1, bf16[1024,128]{1,0:T(8,128)(2,1)S(1)} %copy-done.17, bf16[512,128]{1,0:T(8,128)(2,1)S(1)} %bitcast.216), kind=kOutput, calls=%fused_computation.34 | convolution fusion | flops 404093952 | bytes 3806208 | tf_op jit(solution)/shard_map/ct,fc->tf/dot_general | solution.py:312
  132.9 5.5 %collective-permute-done.14 = bf16[2,2,2,32,1536]{4,3,2,1,0:T(8,128)(2,1)S(1)} collective-permute-done((bf16[2,2,2,32,1536]{4,3,2,1,0:T(8,128)(2,1)S(1)}, bf16[2,2,2,32,1536]{4,3,2,1,0:T(8,128)(2,1)S(1)}, u32[]{:S(2)}, u32[]{:S(2)}) %collective-permute-start.14) | collective-permute-done | bytes 786464 | tf_op jit(solution)/shard_map/ppermute | solution.py:155
  142.7 1.6 %collective-permute-start.21 = (bf16[2,16,1024]{2,1,0:T(8,128)(2,1)S(1)}, bf16[2,16,1024]{2,1,0:T(8,128)(2,1)S(1)}, u32[]{:S(2)}, u32[]{:S(2)}) collective-permute-start(bf16[2,16,1024]{2,1,0:T(8,128)(2,1)S(1)} %fusion.63), channel_id=1, source_target_pairs={{0,1},{1,0},{2,3},{3,2},{4,5},{5,4},{6,7},{7,6},{8,9},{9,8},{10,11... | collective-permute-start | bytes 196616 | tf_op jit(solution)/shard_map/ppermute | solution.py:164
  147.0 1.6 %collective-permute-start.16 = (bf16[2,32,1536]{2,1,0:T(8,128)(2,1)S(1)}, bf16[2,32,1536]{2,1,0:T(8,128)(2,1)S(1)}, u32[]{:S(2)}, u32[]{:S(2)}) collective-permute-start(bf16[2,32,1536]{2,1,0:T(8,128)(2,1)S(1)} %fusion.54), channel_id=1, source_target_pairs={{0,1},{1,0},{2,3},{3,2},{4,5},{5,4},{6,7},{7,6},{8,9},{9,8},{10,11... | collective-permute-start | bytes 589832 | tf_op jit(solution)/shard_map/ppermute | solution.py:166
  150.3 2.6 %collective-permute-start.22 = (bf16[16,1024]{1,0:T(8,128)(2,1)S(1)}, bf16[16,1024]{1,0:T(8,128)(2,1)S(1)}, u32[]{:S(2)}, u32[]{:S(2)}) collective-permute-start(bf16[16,1024]{1,0:T(8,128)(2,1)S(1)} %fusion.65), channel_id=1, source_target_pairs={{0,2},{1,3},{2,0},{3,1},{4,6},{5,7},{6,4},{7,5},{8,10},{9,11},{10,... | collective-permute-start | bytes 98312 | tf_op jit(solution)/shard_map/ppermute | solution.py:164
  153.5 2.6 %collective-permute-start.12 = (f32[1025]{0:T(1024)S(1)}, f32[1025]{0:T(1024)S(1)}, u32[]{:S(2)}, u32[]{:S(2)}) collective-permute-start(f32[1025]{0:T(1024)S(1)} %add.317), channel_id=1, source_target_pairs={{0,2},{1,3},{2,0},{3,1},{4,6},{5,7},{6,4},{7,5},{8,10},{9,11},{10,... | collective-permute-start | bytes 12308 | tf_op jit(solution)/shard_map/ppermute | solution.py:166
  159.8 1.9 %collective-permute-done.17 = bf16[32,1536]{1,0:T(8,128)(2,1)S(1)} collective-permute-done((bf16[32,1536]{1,0:T(8,128)(2,1)S(1)}, bf16[32,1536]{1,0:T(8,128)(2,1)S(1)}, u32[]{:S(2)}, u32[]{:S(2)}) %collective-permute-start.17) | collective-permute-done | bytes 98336 | tf_op jit(solution)/shard_map/ppermute | solution.py:166
  (174 shorter events, 59.4 us)
Async XLA Ops:
  0.6 15.2 %copy-start = (bf16[1,512,1024]{2,1,0:T(8,128)(2,1)S(1)}, bf16[1,512,1024]{2,1,0:T(8,128)(2,1)}, u32[]{:S(2)}) copy-start(bf16[1,512,1024]{2,1,0:T(8,128)(2,1)} %param.6) | copy-start | bytes 3145732
  0.6 16.2 %copy-start.9 = (bf16[1,512,1024]{2,1,0:T(8,128)(2,1)S(1)}, bf16[1,512,1024]{2,1,0:T(8,128)(2,1)}, u32[]{:S(2)}) copy-start(bf16[1,512,1024]{2,1,0:T(8,128)(2,1)} %param.7) | copy-start | bytes 3145732
  3.4 9.8 %all-to-all-start = ((s32[8,1,1]{2,1,0:T(1,128)}), s32[8,1,1]{2,1,0:T(1,128)S(1)}, u32[]{:S(2)}, u32[]{:S(2)}) async-start(s32[8,1,1]{2,1,0:T(1,128)} %broadcast_in_dim.46), calls=%async_computation | async-start | bytes 8192 | tf_op jit(solution)/shard_map/all_to_all | solution.py:206
  20.1 14.6 %copy-start.21 = (f32[1024]{0:T(1024)S(1)}, f32[1024]{0:T(1024)}, u32[]{:S(2)}) copy-start(f32[1024]{0:T(1024)} %param.11) | copy-start | bytes 12292
  21.1 11.7 %all-to-all-start.1 = ((bf16[8,24,1024]{2,1,0:T(8,128)(2,1)}), bf16[8,24,1024]{2,1,0:T(8,128)(2,1)S(1)}, u32[]{:S(2)}, u32[]{:S(2)}) async-start(bf16[8,24,1024]{2,1,0:T(8,128)(2,1)} %get-tuple-element.21), calls=%async_computation.1 | async-start | bytes 786432 | tf_op jit(solution)/shard_map/all_to_all | solution.py:223
  34.6 17.1 %copy-start.26 = (f32[128]{0:T(128)}, f32[128]{0:T(128)S(1)}, u32[]{:S(2)}) copy-start(f32[128]{0:T(128)S(1)} %add_rsqrt_fusion.2) | copy-start | bytes 1540
  34.9 17.0 %copy-start.12 = (bf16[128,1024]{1,0:T(8,128)(2,1)}, bf16[128,1024]{1,0:T(8,128)(2,1)S(1)}, u32[]{:S(2)}) copy-start(bf16[128,1024]{1,0:T(8,128)(2,1)S(1)} %fusion.30) | copy-start | bytes 786436
  37.7 7.0 %collective-permute-start.1 = (bf16[1024,128]{0,1:T(8,128)(2,1)S(1)}, bf16[1024,128]{0,1:T(8,128)(2,1)S(1)}, u32[]{:S(2)}, u32[]{:S(2)}) collective-permute-start(bf16[1024,128]{0,1:T(8,128)(2,1)S(1)} %bitcast.220), channel_id=1, source_target_pairs={{0,16},{4,20},{8,24},{12,28},{16,0},{20,4},{24,8},{28,12},{1,17},{... | collective-permute-start | bytes 786440 | tf_op jit(solution)/shard_map/ppermute | solution.py:179
  38.2 9.2 %collective-permute-start = (bf16[1024,128]{0,1:T(8,128)(2,1)S(1)}, bf16[1024,128]{0,1:T(8,128)(2,1)S(1)}, u32[]{:S(2)}, u32[]{:S(2)}) collective-permute-start(bf16[1024,128]{0,1:T(8,128)(2,1)S(1)} %bitcast.221), channel_id=1, source_target_pairs={{0,8},{4,12},{8,0},{12,4},{16,24},{20,28},{24,16},{28,20},{1,9},{5... | collective-permute-start | bytes 786440 | tf_op jit(solution)/shard_map/ppermute | solution.py:179
  38.8 12.8 %collective-permute-start.2 = (bf16[1024,128]{0,1:T(8,128)(2,1)S(1)}, bf16[1024,128]{0,1:T(8,128)(2,1)S(1)}, u32[]{:S(2)}, u32[]{:S(2)}) collective-permute-start(bf16[1024,128]{0,1:T(8,128)(2,1)S(1)} %bitcast.222), channel_id=1, source_target_pairs={{0,24},{4,28},{8,16},{12,20},{16,8},{20,12},{24,0},{28,4},{1,25},{... | collective-permute-start | bytes 786440 | tf_op jit(solution)/shard_map/ppermute | solution.py:179
  51.7 4.9 %collective-permute-start.3 = (bf16[4,1024,128]{1,2,0:T(8,128)(2,1)S(1)}, bf16[4,1024,128]{1,2,0:T(8,128)(2,1)S(1)}, u32[]{:S(2)}, u32[]{:S(2)}) collective-permute-start(bf16[4,1024,128]{1,2,0:T(8,128)(2,1)S(1)} %pad_maximum_fusion), channel_id=1, source_target_pairs={{0,4},{4,0},{8,12},{12,8},{16,20},{20,16},{24,28},{28,24},{1,5},{5... | collective-permute-start | bytes 3145736 | tf_op jit(solution)/shard_map/ppermute | solution.py:181
  60.7 12.5 %all-to-all-start.2 = ((bf16[8,24,1024]{2,1,0:T(8,128)(2,1)}), bf16[8,24,1024]{2,1,0:T(8,128)(2,1)}, u32[]{:S(2)}, u32[]{:S(2)}) async-start(bf16[8,24,1024]{2,1,0:T(8,128)(2,1)} %get-tuple-element.7), calls=%async_computation.2 | async-start | bytes 786432 | tf_op jit(solution)/shard_map/all_to_all | solution.py:248
  88.0 3.0 %collective-permute-start.4 = (bf16[4,1024,128]{2,1,0:T(8,128)(2,1)}, bf16[4,1024,128]{2,1,0:T(8,128)(2,1)}, u32[]{:S(2)}, u32[]{:S(2)}) collective-permute-start(bf16[4,1024,128]{2,1,0:T(8,128)(2,1)} %bitcast.34), channel_id=1, source_target_pairs={{0,4},{4,0},{8,12},{12,8},{16,20},{20,16},{24,28},{28,24},{1,5},{5... | collective-permute-start | bytes 3145736 | tf_op jit(solution)/shard_map/ppermute | solution.py:187
  92.6 9.2 %collective-permute-start.5 = (bf16[1024,128]{1,0:T(8,128)(2,1)S(1)}, bf16[1024,128]{1,0:T(8,128)(2,1)S(1)}, u32[]{:S(2)}, u32[]{:S(2)}) collective-permute-start(bf16[1024,128]{1,0:T(8,128)(2,1)S(1)} %get-tuple-element.14), channel_id=1, source_target_pairs={{0,8},{4,12},{8,0},{12,4},{16,24},{20,28},{24,16},{28,20},{1,9},{5... | collective-permute-start | bytes 786440 | tf_op jit(solution)/shard_map/ppermute | solution.py:191
  93.3 13.6 %collective-permute-start.7 = (bf16[1024,128]{1,0:T(8,128)(2,1)S(1)}, bf16[1024,128]{1,0:T(8,128)(2,1)S(1)}, u32[]{:S(2)}, u32[]{:S(2)}) collective-permute-start(bf16[1024,128]{1,0:T(8,128)(2,1)S(1)} %get-tuple-element.15), channel_id=1, source_target_pairs={{0,24},{4,28},{8,16},{12,20},{16,8},{20,12},{24,0},{28,4},{1,25},{... | collective-permute-start | bytes 786440 | tf_op jit(solution)/shard_map/ppermute | solution.py:191
  94.7 13.5 %collective-permute-start.6 = (bf16[1024,128]{1,0:T(8,128)(2,1)S(1)}, bf16[1024,128]{1,0:T(8,128)(2,1)S(1)}, u32[]{:S(2)}, u32[]{:S(2)}) collective-permute-start(bf16[1024,128]{1,0:T(8,128)(2,1)S(1)} %get-tuple-element.16), channel_id=1, source_target_pairs={{0,16},{4,20},{8,24},{12,28},{16,0},{20,4},{24,8},{28,12},{1,17},{... | collective-permute-start | bytes 786440 | tf_op jit(solution)/shard_map/ppermute | solution.py:191
  114.1 6.1 %collective-permute-start.13 = (bf16[2,2,2,2,32,1536]{5,4,3,2,1,0:T(8,128)(2,1)}, bf16[2,2,2,2,32,1536]{5,4,3,2,1,0:T(8,128)(2,1)}, u32[]{:S(2)}, u32[]{:S(2)}) collective-permute-start(bf16[2,2,2,2,32,1536]{5,4,3,2,1,0:T(8,128)(2,1)} %fusion.13), channel_id=1, source_target_pairs={{0,4},{4,0},{8,12},{12,8},{16,20},{20,16},{24,28},{28,24},{1,5},{5... | collective-permute-start | bytes 4718600 | tf_op jit(solution)/shard_map/ppermute | solution.py:155
  114.8 3.6 %collective-permute-start.18 = (bf16[2,2,2,2,16,1024]{5,4,3,2,1,0:T(8,128)(2,1)S(1)}, bf16[2,2,2,2,16,1024]{5,4,3,2,1,0:T(8,128)(2,1)}, u32[]{:S(2)}, u32[]{:S(2)}) collective-permute-start(bf16[2,2,2,2,16,1024]{5,4,3,2,1,0:T(8,128)(2,1)S(1)} %fusion.34), channel_id=1, source_target_pairs={{0,4},{4,0},{8,12},{12,8},{16,20},{20,16},{24,28},{28,24},{1,5},{5... | collective-permute-start | bytes 1572872 | tf_op jit(solution)/shard_map/ppermute | solution.py:153
  119.7 6.8 %collective-permute-start.19 = (bf16[2,2,2,16,1024]{4,3,2,1,0:T(8,128)(2,1)S(1)}, bf16[2,2,2,16,1024]{4,3,2,1,0:T(8,128)(2,1)}, u32[]{:S(2)}, u32[]{:S(2)}) collective-permute-start(bf16[2,2,2,16,1024]{4,3,2,1,0:T(8,128)(2,1)S(1)} %fusion.39), channel_id=1, source_target_pairs={{0,8},{4,20},{8,0},{12,28},{16,24},{20,4},{24,16},{28,12},{1,9},{5... | collective-permute-start | bytes 786440 | tf_op jit(solution)/shard_map/ppermute | solution.py:153
  124.9 13.5 %collective-permute-start.14 = (bf16[2,2,2,32,1536]{4,3,2,1,0:T(8,128)(2,1)S(1)}, bf16[2,2,2,32,1536]{4,3,2,1,0:T(8,128)(2,1)S(1)}, u32[]{:S(2)}, u32[]{:S(2)}) collective-permute-start(bf16[2,2,2,32,1536]{4,3,2,1,0:T(8,128)(2,1)S(1)} %fusion.14), channel_id=1, source_target_pairs={{0,8},{4,20},{8,0},{12,28},{16,24},{20,4},{24,16},{28,12},{1,9},{5... | collective-permute-start | bytes 2359304 | tf_op jit(solution)/shard_map/ppermute | solution.py:155
  127.6 12.8 %collective-permute-start.20 = (bf16[2,2,16,1024]{3,2,1,0:T(8,128)(2,1)S(1)}, bf16[2,2,16,1024]{3,2,1,0:T(8,128)(2,1)S(1)}, u32[]{:S(2)}, u32[]{:S(2)}) collective-permute-start(bf16[2,2,16,1024]{3,2,1,0:T(8,128)(2,1)S(1)} %fusion.55), channel_id=1, source_target_pairs={{0,16},{4,12},{8,24},{12,4},{16,0},{20,28},{24,8},{28,20},{1,17},{... | collective-permute-start | bytes 393224 | tf_op jit(solution)/shard_map/ppermute | solution.py:153
  132.8 7.7 %collective-permute-start.8 = (f32[1025]{0:T(1024)S(1)}, f32[1025]{0:T(1024)S(1)}, u32[]{:S(2)}, u32[]{:S(2)}) collective-permute-start(f32[1025]{0:T(1024)S(1)} %pad_maximum_fusion.5), channel_id=1, source_target_pairs={{0,4},{4,0},{8,12},{12,8},{16,20},{20,16},{24,28},{28,24},{1,5},{5... | collective-permute-start | bytes 12308 | tf_op jit(solution)/shard_map/ppermute | solution.py:155
  138.9 7.9 %collective-permute-start.15 = (bf16[2,2,32,1536]{3,2,1,0:T(8,128)(2,1)S(1)}, bf16[2,2,32,1536]{3,2,1,0:T(8,128)(2,1)S(1)}, u32[]{:S(2)}, u32[]{:S(2)}) collective-permute-start(bf16[2,2,32,1536]{3,2,1,0:T(8,128)(2,1)S(1)} %fusion.45), channel_id=1, source_target_pairs={{0,16},{4,12},{8,24},{12,4},{16,0},{20,28},{24,8},{28,20},{1,17},{... | collective-permute-start | bytes 1179656 | tf_op jit(solution)/shard_map/ppermute | solution.py:155
  141.1 3.9 %collective-permute-start.9 = (f32[1025]{0:T(1024)S(1)}, f32[1025]{0:T(1024)S(1)}, u32[]{:S(2)}, u32[]{:S(2)}) collective-permute-start(f32[1025]{0:T(1024)S(1)} %fusion.69), channel_id=1, source_target_pairs={{0,8},{4,20},{8,0},{12,28},{16,24},{20,4},{24,16},{28,12},{1,9},{5... | collective-permute-start | bytes 12308 | tf_op jit(solution)/shard_map/ppermute | solution.py:155
  142.7 5.9 %collective-permute-start.21 = (bf16[2,16,1024]{2,1,0:T(8,128)(2,1)S(1)}, bf16[2,16,1024]{2,1,0:T(8,128)(2,1)S(1)}, u32[]{:S(2)}, u32[]{:S(2)}) collective-permute-start(bf16[2,16,1024]{2,1,0:T(8,128)(2,1)S(1)} %fusion.63), channel_id=1, source_target_pairs={{0,1},{1,0},{2,3},{3,2},{4,5},{5,4},{6,7},{7,6},{8,9},{9,8},{10,11... | collective-permute-start | bytes 196616 | tf_op jit(solution)/shard_map/ppermute | solution.py:164
  145.0 3.7 %collective-permute-start.10 = (f32[1025]{0:T(1024)S(1)}, f32[1025]{0:T(1024)S(1)}, u32[]{:S(2)}, u32[]{:S(2)}) collective-permute-start(f32[1025]{0:T(1024)S(1)} %add.315), channel_id=1, source_target_pairs={{0,16},{4,12},{8,24},{12,4},{16,0},{20,28},{24,8},{28,20},{1,17},{... | collective-permute-start | bytes 12308 | tf_op jit(solution)/shard_map/ppermute | solution.py:155
  146.8 15.6 %copy-start.1 = (bf16[1,512,1024]{2,1,0:T(8,128)(2,1)S(1)}, bf16[1,512,1024]{2,1,0:T(8,128)(2,1)}, u32[]{:S(2)}) copy-start(bf16[1,512,1024]{2,1,0:T(8,128)(2,1)} %param.6) | copy-start | bytes 3145732
  147.0 9.1 %collective-permute-start.16 = (bf16[2,32,1536]{2,1,0:T(8,128)(2,1)S(1)}, bf16[2,32,1536]{2,1,0:T(8,128)(2,1)S(1)}, u32[]{:S(2)}, u32[]{:S(2)}) collective-permute-start(bf16[2,32,1536]{2,1,0:T(8,128)(2,1)S(1)} %fusion.54), channel_id=1, source_target_pairs={{0,1},{1,0},{2,3},{3,2},{4,5},{5,4},{6,7},{7,6},{8,9},{9,8},{10,11... | collective-permute-start | bytes 589832 | tf_op jit(solution)/shard_map/ppermute | solution.py:166
  148.7 4.8 %collective-permute-start.11 = (f32[1025]{0:T(1024)S(1)}, f32[1025]{0:T(1024)S(1)}, u32[]{:S(2)}, u32[]{:S(2)}) collective-permute-start(f32[1025]{0:T(1024)S(1)} %add.316), channel_id=1, source_target_pairs={{0,1},{1,0},{2,3},{3,2},{4,5},{5,4},{6,7},{7,6},{8,9},{9,8},{10,11... | collective-permute-start | bytes 12308 | tf_op jit(solution)/shard_map/ppermute | solution.py:166
  150.3 6.3 %collective-permute-start.22 = (bf16[16,1024]{1,0:T(8,128)(2,1)S(1)}, bf16[16,1024]{1,0:T(8,128)(2,1)S(1)}, u32[]{:S(2)}, u32[]{:S(2)}) collective-permute-start(bf16[16,1024]{1,0:T(8,128)(2,1)S(1)} %fusion.65), channel_id=1, source_target_pairs={{0,2},{1,3},{2,0},{3,1},{4,6},{5,7},{6,4},{7,5},{8,10},{9,11},{10,... | collective-permute-start | bytes 98312 | tf_op jit(solution)/shard_map/ppermute | solution.py:164
  153.5 4.6 %collective-permute-start.12 = (f32[1025]{0:T(1024)S(1)}, f32[1025]{0:T(1024)S(1)}, u32[]{:S(2)}, u32[]{:S(2)}) collective-permute-start(f32[1025]{0:T(1024)S(1)} %add.317), channel_id=1, source_target_pairs={{0,2},{1,3},{2,0},{3,1},{4,6},{5,7},{6,4},{7,5},{8,10},{9,11},{10,... | collective-permute-start | bytes 12308 | tf_op jit(solution)/shard_map/ppermute | solution.py:166
  156.1 5.6 %collective-permute-start.17 = (bf16[32,1536]{1,0:T(8,128)(2,1)S(1)}, bf16[32,1536]{1,0:T(8,128)(2,1)S(1)}, u32[]{:S(2)}, u32[]{:S(2)}) collective-permute-start(bf16[32,1536]{1,0:T(8,128)(2,1)S(1)} %fusion.62), channel_id=1, source_target_pairs={{0,2},{1,3},{2,0},{3,1},{4,6},{5,7},{6,4},{7,5},{8,10},{9,11},{10,... | collective-permute-start | bytes 294920 | tf_op jit(solution)/shard_map/ppermute | solution.py:166
  (22 other events, 108.4 us)

commit v14 on v13

--- a/solution.py
+++ b/solution.py
@@ -2,6 +2,7 @@
 import jax.numpy as jnp
 from jax import lax
 from jax.sharding import PartitionSpec as P
+from jax.experimental.layout import Layout, with_layout_constraint
 
 HEAD_DIM = 64
 TOK_DEV = 128
@@ -243,6 +244,7 @@
     pair_cols = jnp.dot(w_qkv[:, inner:].T, hidden.T, preferred_element_type=jnp.float32).astype(
         jnp.bfloat16
     )
+    pair_cols = with_layout_constraint(pair_cols, Layout(major_to_minor=(0, 1)))
     gathered = gather_blocks(pair_cols)
     send_target, gathered = lax.optimization_barrier((send_target, gathered))
     got_target = lax.all_to_all(send_target, "seq", split_axis=0, concat_axis=0, tiled=True)

time: 164 us -> 169 us (1.030)
  other arithmetic: 18.9 us -> 22 us
  local copies, waits for them, and re-layouts: 30.8 us -> 32.6 us
    optimization_barrier x1 -> x0, local copies, waits for them, and re-layouts: 3.03 us -> none  [per_device(): send_target, gathered = lax.optimization_barrier((send_target, gathered))]
    unnamed x60 -> x80, local copies, waits for them, and re-layouts: 10 us -> 11.9 us
  transfers between devices with their start and end apart: 26 -> 26, of which waited for: 17 -> 15; matrix products, arithmetic and copies ran while one was open for 15% -> 17% of each run, Pallas kernels for 0% -> 0%
where the time goes in v14:
time: 169 us; the launch traced here: 168 us
  waiting for transfers between devices  50.5 us (30%)
  starting transfers between devices  38.1 us (23%)
  local copies, waits for them, and re-layouts  32.6 us (19%)
  other arithmetic  22 us (13%)
  matrix products  22 us (13%)
  between operations  3.16 us (2%)
    unnamed x80, local copies, waits for them, and re-layouts  11.9 us
    ppermute x3, waiting for transfers between devices, return_blocks(): sent = lax.ppermute(summed[k].astype(jnp.bfloat16), 'seq', xor_pairs(2 * k))  11.7 us
    ppermute x3, waiting for transfers between devices, gather_blocks(): lax.ppermute(block, 'seq', xor_pairs(2 * k))  10.7 us
    all_to_all x1, waiting for transfers between devices, per_device(): lax.all_to_all(send_tokens, 'seq', split_axis=0, concat_axis=0, tiled=True)  8.08 us
    ppermute x6, waiting for transfers between devices, halving_scatter(): lax.ppermute((give.astype(jnp.bfloat16), small), 'seq', pairs)  7.62 us
    ppermute x4, starting transfers between devices, halving_scatter(): lax.ppermute((give.astype(jnp.bfloat16), small), 'clip', pairs)  6.19 us
    add x9, other arithmetic, halving_scatter(): data = keep + got.astype(jnp.float32)  6.09 us
    all_to_all x1, starting transfers between devices, per_device(): lax.all_to_all(jnp.broadcast_to(kept_count.reshape(1, 1), (shards, 1)), '...  5.17 us
  transfers between devices with their start and end apart: 26, of which 15 were waited for; matrix products, arithmetic and copies ran while one was open for 17% of the time, Pallas kernels for 0%

profile of v14, /device:TPU:0, one launch (start us, length us, event | category | flops | bytes accessed | tf_op | source)
XLA Modules:
  0.0 168.4 jit_solution(11584413964984131504)
XLA Ops:
  3.4 5.2 %all-to-all-start = ((s32[8,1,1]{2,1,0:T(1,128)}), s32[8,1,1]{2,1,0:T(1,128)S(1)}, u32[]{:S(2)}, u32[]{:S(2)}) async-start(s32[8,1,1]{2,1,0:T(1,128)} %broadcast_in_dim.46), calls=%async_computation | async-start | bytes 8192 | tf_op jit(solution)/shard_map/all_to_all | solution.py:207
  9.2 3.9 %all-to-all-done = s32[8,1,1]{2,1,0:T(1,128)S(1)} async-done(((s32[8,1,1]{2,1,0:T(1,128)}), s32[8,1,1]{2,1,0:T(1,128)S(1)}, u32[]{:S(2)}, u32[]{:S(2)}) %all-to-all-start) | async-done | bytes 64 | tf_op jit(solution)/shard_map/all_to_all | solution.py:207
  21.1 3.5 %all-to-all-start.1 = ((bf16[8,24,1024]{2,1,0:T(8,128)(2,1)}), bf16[8,24,1024]{2,1,0:T(8,128)(2,1)S(1)}, u32[]{:S(2)}, u32[]{:S(2)}) async-start(bf16[8,24,1024]{2,1,0:T(8,128)(2,1)} %get-tuple-element.21), calls=%async_computation.1 | async-start | bytes 786432 | tf_op jit(solution)/shard_map/all_to_all | solution.py:224
  24.8 8.1 %all-to-all-done.1 = bf16[8,24,1024]{2,1,0:T(8,128)(2,1)S(1)} async-done(((bf16[8,24,1024]{2,1,0:T(8,128)(2,1)}), bf16[8,24,1024]{2,1,0:T(8,128)(2,1)S(1)}, u32[]{:S(2)}, u32[]{:S(2)}) %all-to-all-start.1) | async-done | bytes 393248 | tf_op jit(solution)/shard_map/all_to_all | solution.py:224
  35.4 2.6 %constant_dynamic-update-slice_fusion.4 = (bf16[8,1024,128]{2,1,0:T(8,128)(2,1)S(1)}, bf16[128,1024]{0,1:T(8,128)(2,1)S(1)}) fusion(bf16[128,1024]{1,0:T(8,128)(2,1)S(1)} %fusion.30, bf16[1024,1536]{1,0:T(8,128)(2,1)} %param.9), kind=kOutput, calls=%fused_computation.131 | convolution fusion | flops 268566528 | bytes 2883584 | tf_op jit(solution)/shard_map/dot_general | solution.py:244
  39.2 2.4 %collective-permute-start.2 = (bf16[1024,128]{1,0:T(8,128)(2,1)S(1)}, bf16[1024,128]{1,0:T(8,128)(2,1)S(1)}, u32[]{:S(2)}, u32[]{:S(2)}) collective-permute-start(bf16[1024,128]{1,0:T(8,128)(2,1)S(1)} %bitcast.222), channel_id=1, source_target_pairs={{0,24},{4,28},{8,16},{12,20},{16,8},{20,12},{24,0},{28,4},{1,25},{... | collective-permute-start | bytes 786440 | tf_op jit(solution)/shard_map/ppermute | solution.py:180
  41.6 5.8 %collective-permute-done = bf16[1024,128]{1,0:T(8,128)(2,1)S(1)} collective-permute-done((bf16[1024,128]{1,0:T(8,128)(2,1)S(1)}, bf16[1024,128]{1,0:T(8,128)(2,1)S(1)}, u32[]{:S(2)}, u32[]{:S(2)}) %collective-permute-start) | collective-permute-done | bytes 262176 | tf_op jit(solution)/shard_map/ppermute | solution.py:180
  47.4 4.9 %collective-permute-done.1 = bf16[1024,128]{1,0:T(8,128)(2,1)S(1)} collective-permute-done((bf16[1024,128]{1,0:T(8,128)(2,1)S(1)}, bf16[1024,128]{1,0:T(8,128)(2,1)S(1)}, u32[]{:S(2)}, u32[]{:S(2)}) %collective-permute-start.1) | collective-permute-done | bytes 262176 | tf_op jit(solution)/shard_map/ppermute | solution.py:180
  53.5 2.2 %convolution_convert_fusion.1 = bf16[128,512]{1,0:T(8,128)(2,1)} fusion(bf16[128,1024]{1,0:T(8,128)(2,1)S(1)} %fusion.30, bf16[1024,1536]{1,0:T(8,128)(2,1)} %param.9), kind=kOutput, calls=%fused_computation.38 | convolution fusion | flops 134283264 | bytes 1441792 | tf_op jit(solution)/shard_map/dot_general | solution.py:239
  61.1 4.1 %all-to-all-start.2 = ((bf16[8,24,1024]{2,1,0:T(8,128)(2,1)}), bf16[8,24,1024]{2,1,0:T(8,128)(2,1)}, u32[]{:S(2)}, u32[]{:S(2)}) async-start(bf16[8,24,1024]{2,1,0:T(8,128)(2,1)} %get-tuple-element.7), calls=%async_computation.2 | async-start | bytes 786432 | tf_op jit(solution)/shard_map/all_to_all | solution.py:250
  68.0 1.6 fusion.51
  70.3 3.2 %all-to-all-done.2 = bf16[8,24,1024]{2,1,0:T(8,128)(2,1)} async-done(((bf16[8,24,1024]{2,1,0:T(8,128)(2,1)}), bf16[8,24,1024]{2,1,0:T(8,128)(2,1)}, u32[]{:S(2)}, u32[]{:S(2)}) %all-to-all-start.2) | async-done | bytes 393248 | tf_op jit(solution)/shard_map/all_to_all | solution.py:250
  73.6 2.1 %scatter_custom_fusion.1 = bf16[128,1024]{1,0:T(8,128)(2,1)S(1)} fusion(s32[192]{0:T(256)} %bitcast.229, bf16[192,1024]{1,0:T(8,128)(2,1)} %bitcast.23, bf16[]{:T(256)} %constant.162.clone.1), kind=kCustom, calls=%fused_computation.116 | custom fusion | bytes 262656 | tf_op jit(solution)/shard_map/scatter | solution.py:254
  79.5 3.9 %fusion.16 = bf16[8,8,64,128]{3,2,1,0:T(8,128)(2,1)S(1)} fusion(f32[8,8,128,128]{2,3,1,0:T(8,128)} %copy-done.1, f32[8,128]{1,0:T(8,128)S(1)} %log_add_fusion, bf16[8,128,64]{1,2,0:T(8,128)(2,1)S(1)} %bitcast.205), kind=kOutput, calls=%fused_computation.30 | convolution fusion | flops 137887744 | bytes 5378048 | tf_op jit(solution)/shard_map/ihqd,ihqt->ihdt/dot_general | solution.py:295
  83.4 2.6 %multiply_convert_fusion = bf16[8,8,128,128]{2,3,1,0:T(8,128)(2,1)S(1)} fusion(f32[8,8,128,128]{2,3,1,0:T(8,128)S(1)} %copy-done.2, f32[8,128]{1,0:T(8,128)S(1)} %multiply_reduce_fusion.4, f32[8,128]{1,0:T(8,128)S(1)} %log_add_fusion, bf16[8,8,2,64,128]{4,3,2,1,0:T(8,128)(2,1)} %bitcast.203, bf16[8,128,64]{1,2,0:T(8,128)(2,1)S(1)} %bitcast.206), kind=kOutput, calls=%fused_computation.6 | convolution fusion | flops 139460608 | bytes 7479296 | tf_op jit(solution)/shard_map/ihqd,ihdt->ihqt/dot_general | solution.py:298
  90.5 1.8 %copy.62 = bf16[128,1024]{0,1:T(8,128)(2,1)} copy(bf16[128,1024]{1,0:T(8,128)(2,1)} %copy-done.18) | data formatting | bytes 524288 | tf_op jit(solution)/shard_map/convert_element_type | solution.py:22
  93.9 1.7 fusion.74
  99.7 5.1 %collective-permute-done.5 = bf16[1024,128]{1,0:T(8,128)(2,1)S(1)} collective-permute-done((bf16[1024,128]{1,0:T(8,128)(2,1)S(1)}, bf16[1024,128]{1,0:T(8,128)(2,1)S(1)}, u32[]{:S(2)}, u32[]{:S(2)}) %collective-permute-start.5) | collective-permute-done | bytes 262176 | tf_op jit(solution)/shard_map/ppermute | solution.py:192
  104.8 5.3 %collective-permute-done.7 = bf16[1024,128]{1,0:T(8,128)(2,1)S(1)} collective-permute-done((bf16[1024,128]{1,0:T(8,128)(2,1)S(1)}, bf16[1024,128]{1,0:T(8,128)(2,1)S(1)}, u32[]{:S(2)}, u32[]{:S(2)}) %collective-permute-start.7) | collective-permute-done | bytes 262176 | tf_op jit(solution)/shard_map/ppermute | solution.py:192
  112.6 2.6 %copy-done.5 = f32[2,2,2,2,2,32,1536]{6,5,4,3,2,1,0:T(8,128)} copy-done((f32[2,2,2,2,2,32,1536]{6,5,4,3,2,1,0:T(8,128)}, f32[2,2,2,2,2,32,1536]{6,5,4,3,2,1,0:T(8,128)S(1)}, u32[]{:S(2)}) %copy-start.5) | copy-done | bytes 6291480
  119.3 1.7 collective-permute-done.18
  123.9 2.9 %bitcast_add_fusion = f32[2,2,2,2,32,1536]{5,4,3,2,1,0:T(8,128)S(1)} fusion(bf16[2,2,2,2,32,1536]{5,4,3,2,1,0:T(8,128)(2,1)} %collective-permute-done.13, f32[2,2,2,2,2,32,1536]{6,5,4,3,2,1,0:T(8,128)} %copy-done.5, s32[]{:T(128)S(6)} %select_n.233), kind=kLoop, calls=%fused_computation.13 | loop fusion | flops 1572864 | bytes 7864324 | tf_op jit(solution)/shard_map/add | solution.py:158
  126.8 1.6 copy-done.3
  132.0 1.6 collective-permute-start.20
  133.5 3.1 %fusion.22 = f32[1024]{0:T(1024)S(1)} fusion(bf16[1024,1536]{1,0:T(8,128)(2,1)} %param.9, bf16[128,1024]{1,0:T(8,128)(2,1)S(1)} %scatter_custom_fusion, f32[128]{0:T(128)S(1)} %copy-done.37, f32[128]{0:T(128)S(1)} %broadcast_multiply_fusion.1, bf16[1024,128]{1,0:T(8,128)(2,1)S(1)} %fusion.38, bf16[512,128]{1,0:T(8,128)(2,1)S(1)} %bitcast.216), kind=kOutput, calls=%fused_computation.34 | convolution fusion | flops 404093952 | bytes 3806208 | tf_op jit(solution)/shard_map/ct,fc->tf/dot_general | solution.py:314
  137.4 5.7 %collective-permute-done.14 = bf16[2,2,2,32,1536]{4,3,2,1,0:T(8,128)(2,1)S(1)} collective-permute-done((bf16[2,2,2,32,1536]{4,3,2,1,0:T(8,128)(2,1)}, bf16[2,2,2,32,1536]{4,3,2,1,0:T(8,128)(2,1)S(1)}, u32[]{:S(2)}, u32[]{:S(2)}) %collective-permute-start.14) | collective-permute-done | bytes 786464 | tf_op jit(solution)/shard_map/ppermute | solution.py:156
  147.4 1.6 collective-permute-start.21
  151.7 1.6 collective-permute-start.16
  153.4 1.6 collective-permute-start.11
  154.9 2.6 %collective-permute-start.22 = (bf16[16,1024]{1,0:T(8,128)(2,1)S(1)}, bf16[16,1024]{1,0:T(8,128)(2,1)S(1)}, u32[]{:S(2)}, u32[]{:S(2)}) collective-permute-start(bf16[16,1024]{1,0:T(8,128)(2,1)S(1)} %fusion.65), channel_id=1, source_target_pairs={{0,2},{1,3},{2,0},{3,1},{4,6},{5,7},{6,4},{7,5},{8,10},{9,11},{10,... | collective-permute-start | bytes 98312 | tf_op jit(solution)/shard_map/ppermute | solution.py:165
  158.3 2.6 %collective-permute-start.12 = (f32[1025]{0:T(1024)S(1)}, f32[1025]{0:T(1024)S(1)}, u32[]{:S(2)}, u32[]{:S(2)}) collective-permute-start(f32[1025]{0:T(1024)S(1)} %add.317), channel_id=1, source_target_pairs={{0,2},{1,3},{2,0},{3,1},{4,6},{5,7},{6,4},{7,5},{8,10},{9,11},{10,... | collective-permute-start | bytes 12308 | tf_op jit(solution)/shard_map/ppermute | solution.py:167
  164.7 1.9 %collective-permute-done.17 = bf16[32,1536]{1,0:T(8,128)(2,1)S(1)} collective-permute-done((bf16[32,1536]{1,0:T(8,128)(2,1)S(1)}, bf16[32,1536]{1,0:T(8,128)(2,1)S(1)}, u32[]{:S(2)}, u32[]{:S(2)}) %collective-permute-start.17) | collective-permute-done | bytes 98336 | tf_op jit(solution)/shard_map/ppermute | solution.py:167
  (193 shorter events, 64.4 us)
Async XLA Ops:
  0.6 15.2 %copy-start = (bf16[1,512,1024]{2,1,0:T(8,128)(2,1)S(1)}, bf16[1,512,1024]{2,1,0:T(8,128)(2,1)}, u32[]{:S(2)}) copy-start(bf16[1,512,1024]{2,1,0:T(8,128)(2,1)} %param.6) | copy-start | bytes 3145732
  0.6 16.2 %copy-start.6 = (bf16[1,512,1024]{2,1,0:T(8,128)(2,1)S(1)}, bf16[1,512,1024]{2,1,0:T(8,128)(2,1)}, u32[]{:S(2)}) copy-start(bf16[1,512,1024]{2,1,0:T(8,128)(2,1)} %param.7) | copy-start | bytes 3145732
  3.4 9.8 %all-to-all-start = ((s32[8,1,1]{2,1,0:T(1,128)}), s32[8,1,1]{2,1,0:T(1,128)S(1)}, u32[]{:S(2)}, u32[]{:S(2)}) async-start(s32[8,1,1]{2,1,0:T(1,128)} %broadcast_in_dim.46), calls=%async_computation | async-start | bytes 8192 | tf_op jit(solution)/shard_map/all_to_all | solution.py:207
  20.0 15.1 %copy-start.26 = (f32[1024]{0:T(1024)S(1)}, f32[1024]{0:T(1024)}, u32[]{:S(2)}) copy-start(f32[1024]{0:T(1024)} %param.11) | copy-start | bytes 12292
  21.1 11.7 %all-to-all-start.1 = ((bf16[8,24,1024]{2,1,0:T(8,128)(2,1)}), bf16[8,24,1024]{2,1,0:T(8,128)(2,1)S(1)}, u32[]{:S(2)}, u32[]{:S(2)}) async-start(bf16[8,24,1024]{2,1,0:T(8,128)(2,1)} %get-tuple-element.21), calls=%async_computation.1 | async-start | bytes 786432 | tf_op jit(solution)/shard_map/all_to_all | solution.py:224
  35.4 18.0 %copy-start.18 = (bf16[128,1024]{1,0:T(8,128)(2,1)}, bf16[128,1024]{1,0:T(8,128)(2,1)S(1)}, u32[]{:S(2)}) copy-start(bf16[128,1024]{1,0:T(8,128)(2,1)S(1)} %fusion.30) | copy-start | bytes 786436
  38.1 9.3 %collective-permute-start = (bf16[1024,128]{1,0:T(8,128)(2,1)S(1)}, bf16[1024,128]{1,0:T(8,128)(2,1)S(1)}, u32[]{:S(2)}, u32[]{:S(2)}) collective-permute-start(bf16[1024,128]{1,0:T(8,128)(2,1)S(1)} %bitcast.220), channel_id=1, source_target_pairs={{0,8},{4,12},{8,0},{12,4},{16,24},{20,28},{24,16},{28,20},{1,9},{5... | collective-permute-start | bytes 786440 | tf_op jit(solution)/shard_map/ppermute | solution.py:180
  38.7 13.6 %collective-permute-start.1 = (bf16[1024,128]{1,0:T(8,128)(2,1)S(1)}, bf16[1024,128]{1,0:T(8,128)(2,1)S(1)}, u32[]{:S(2)}, u32[]{:S(2)}) collective-permute-start(bf16[1024,128]{1,0:T(8,128)(2,1)S(1)} %bitcast.221), channel_id=1, source_target_pairs={{0,16},{4,20},{8,24},{12,28},{16,0},{20,4},{24,8},{28,12},{1,17},{... | collective-permute-start | bytes 786440 | tf_op jit(solution)/shard_map/ppermute | solution.py:180
  39.2 13.1 %collective-permute-start.2 = (bf16[1024,128]{1,0:T(8,128)(2,1)S(1)}, bf16[1024,128]{1,0:T(8,128)(2,1)S(1)}, u32[]{:S(2)}, u32[]{:S(2)}) collective-permute-start(bf16[1024,128]{1,0:T(8,128)(2,1)S(1)} %bitcast.222), channel_id=1, source_target_pairs={{0,24},{4,28},{8,16},{12,20},{16,8},{20,12},{24,0},{28,4},{1,25},{... | collective-permute-start | bytes 786440 | tf_op jit(solution)/shard_map/ppermute | solution.py:180
  53.4 6.3 %collective-permute-start.3 = (bf16[4,1024,128]{2,1,0:T(8,128)(2,1)}, bf16[4,1024,128]{2,1,0:T(8,128)(2,1)}, u32[]{:S(2)}, u32[]{:S(2)}) collective-permute-start(bf16[4,1024,128]{2,1,0:T(8,128)(2,1)} %pad_maximum_fusion), channel_id=1, source_target_pairs={{0,4},{4,0},{8,12},{12,8},{16,20},{20,16},{24,28},{28,24},{1,5},{5... | collective-permute-start | bytes 3145736 | tf_op jit(solution)/shard_map/ppermute | solution.py:182
  61.1 12.5 %all-to-all-start.2 = ((bf16[8,24,1024]{2,1,0:T(8,128)(2,1)}), bf16[8,24,1024]{2,1,0:T(8,128)(2,1)}, u32[]{:S(2)}, u32[]{:S(2)}) async-start(bf16[8,24,1024]{2,1,0:T(8,128)(2,1)} %get-tuple-element.7), calls=%async_computation.2 | async-start | bytes 786432 | tf_op jit(solution)/shard_map/all_to_all | solution.py:250
  90.5 3.4 %collective-permute-start.4 = (bf16[4,1024,128]{2,1,0:T(8,128)(2,1)}, bf16[4,1024,128]{2,1,0:T(8,128)(2,1)}, u32[]{:S(2)}, u32[]{:S(2)}) collective-permute-start(bf16[4,1024,128]{2,1,0:T(8,128)(2,1)} %bitcast.34), channel_id=1, source_target_pairs={{0,4},{4,0},{8,12},{12,8},{16,20},{20,16},{24,28},{28,24},{1,5},{5... | collective-permute-start | bytes 3145736 | tf_op jit(solution)/shard_map/ppermute | solution.py:188
  95.6 9.2 %collective-permute-start.5 = (bf16[1024,128]{1,0:T(8,128)(2,1)S(1)}, bf16[1024,128]{1,0:T(8,128)(2,1)S(1)}, u32[]{:S(2)}, u32[]{:S(2)}) collective-permute-start(bf16[1024,128]{1,0:T(8,128)(2,1)S(1)} %get-tuple-element.14), channel_id=1, source_target_pairs={{0,8},{4,12},{8,0},{12,4},{16,24},{20,28},{24,16},{28,20},{1,9},{5... | collective-permute-start | bytes 786440 | tf_op jit(solution)/shard_map/ppermute | solution.py:192
  96.3 13.8 %collective-permute-start.7 = (bf16[1024,128]{1,0:T(8,128)(2,1)S(1)}, bf16[1024,128]{1,0:T(8,128)(2,1)S(1)}, u32[]{:S(2)}, u32[]{:S(2)}) collective-permute-start(bf16[1024,128]{1,0:T(8,128)(2,1)S(1)} %get-tuple-element.15), channel_id=1, source_target_pairs={{0,24},{4,28},{8,16},{12,20},{16,8},{20,12},{24,0},{28,4},{1,25},{... | collective-permute-start | bytes 786440 | tf_op jit(solution)/shard_map/ppermute | solution.py:192
  97.7 13.9 %copy-start.22 = (bf16[128,1024]{0,1:T(8,128)(2,1)S(1)}, bf16[128,1024]{0,1:T(8,128)(2,1)}, u32[]{:S(2)}) copy-start(bf16[128,1024]{0,1:T(8,128)(2,1)} %copy.62) | copy-start | bytes 786436
  97.7 13.8 %collective-permute-start.6 = (bf16[1024,128]{1,0:T(8,128)(2,1)S(1)}, bf16[1024,128]{1,0:T(8,128)(2,1)S(1)}, u32[]{:S(2)}, u32[]{:S(2)}) collective-permute-start(bf16[1024,128]{1,0:T(8,128)(2,1)S(1)} %get-tuple-element.16), channel_id=1, source_target_pairs={{0,16},{4,20},{8,24},{12,28},{16,0},{20,4},{24,8},{28,12},{1,17},{... | collective-permute-start | bytes 786440 | tf_op jit(solution)/shard_map/ppermute | solution.py:192
  116.7 7.2 %collective-permute-start.13 = (bf16[2,2,2,2,32,1536]{5,4,3,2,1,0:T(8,128)(2,1)}, bf16[2,2,2,2,32,1536]{5,4,3,2,1,0:T(8,128)(2,1)}, u32[]{:S(2)}, u32[]{:S(2)}) collective-permute-start(bf16[2,2,2,2,32,1536]{5,4,3,2,1,0:T(8,128)(2,1)} %fusion.13), channel_id=1, source_target_pairs={{0,4},{4,0},{8,12},{12,8},{16,20},{20,16},{24,28},{28,24},{1,5},{5... | collective-permute-start | bytes 4718600 | tf_op jit(solution)/shard_map/ppermute | solution.py:156
  118.8 2.2 %collective-permute-start.18 = (bf16[2,2,2,2,16,1024]{5,4,3,2,1,0:T(8,128)(2,1)S(1)}, bf16[2,2,2,2,16,1024]{5,4,3,2,1,0:T(8,128)(2,1)}, u32[]{:S(2)}, u32[]{:S(2)}) collective-permute-start(bf16[2,2,2,2,16,1024]{5,4,3,2,1,0:T(8,128)(2,1)S(1)} %fusion.34), channel_id=1, source_target_pairs={{0,4},{4,0},{8,12},{12,8},{16,20},{20,16},{24,28},{28,24},{1,5},{5... | collective-permute-start | bytes 1572872 | tf_op jit(solution)/shard_map/ppermute | solution.py:154
  123.3 7.6 %collective-permute-start.19 = (bf16[2,2,2,16,1024]{4,3,2,1,0:T(8,128)(2,1)}, bf16[2,2,2,16,1024]{4,3,2,1,0:T(8,128)(2,1)}, u32[]{:S(2)}, u32[]{:S(2)}) collective-permute-start(bf16[2,2,2,16,1024]{4,3,2,1,0:T(8,128)(2,1)} %fusion.39), channel_id=1, source_target_pairs={{0,8},{4,20},{8,0},{12,28},{16,24},{20,4},{24,16},{28,12},{1,9},{5... | collective-permute-start | bytes 786440 | tf_op jit(solution)/shard_map/ppermute | solution.py:154
  129.4 13.6 %collective-permute-start.14 = (bf16[2,2,2,32,1536]{4,3,2,1,0:T(8,128)(2,1)}, bf16[2,2,2,32,1536]{4,3,2,1,0:T(8,128)(2,1)S(1)}, u32[]{:S(2)}, u32[]{:S(2)}) collective-permute-start(bf16[2,2,2,32,1536]{4,3,2,1,0:T(8,128)(2,1)} %fusion.14), channel_id=1, source_target_pairs={{0,8},{4,20},{8,0},{12,28},{16,24},{20,4},{24,16},{28,12},{1,9},{5... | collective-permute-start | bytes 2359304 | tf_op jit(solution)/shard_map/ppermute | solution.py:156
  132.0 11.1 %copy-start.4 = (f32[2,2,2,2,32,1536]{5,4,3,2,1,0:T(8,128)S(1)}, f32[2,2,2,2,32,1536]{5,4,3,2,1,0:T(8,128)}, u32[]{:S(2)}) copy-start(f32[2,2,2,2,32,1536]{5,4,3,2,1,0:T(8,128)} %copy-done.3) | copy-start | bytes 9437188
  132.0 13.1 %collective-permute-start.20 = (bf16[2,2,16,1024]{3,2,1,0:T(8,128)(2,1)S(1)}, bf16[2,2,16,1024]{3,2,1,0:T(8,128)(2,1)S(1)}, u32[]{:S(2)}, u32[]{:S(2)}) collective-permute-start(bf16[2,2,16,1024]{3,2,1,0:T(8,128)(2,1)S(1)} %fusion.55), channel_id=1, source_target_pairs={{0,16},{4,12},{8,24},{12,4},{16,0},{20,28},{24,8},{28,20},{1,17},{... | collective-permute-start | bytes 393224 | tf_op jit(solution)/shard_map/ppermute | solution.py:154
  137.3 7.9 %collective-permute-start.8 = (f32[1025]{0:T(1024)S(1)}, f32[1025]{0:T(1024)S(1)}, u32[]{:S(2)}, u32[]{:S(2)}) collective-permute-start(f32[1025]{0:T(1024)S(1)} %pad_maximum_fusion.5), channel_id=1, source_target_pairs={{0,4},{4,0},{8,12},{12,8},{16,20},{20,16},{24,28},{28,24},{1,5},{5... | collective-permute-start | bytes 12308 | tf_op jit(solution)/shard_map/ppermute | solution.py:156
  143.6 7.9 %collective-permute-start.15 = (bf16[2,2,32,1536]{3,2,1,0:T(8,128)(2,1)S(1)}, bf16[2,2,32,1536]{3,2,1,0:T(8,128)(2,1)S(1)}, u32[]{:S(2)}, u32[]{:S(2)}) collective-permute-start(bf16[2,2,32,1536]{3,2,1,0:T(8,128)(2,1)S(1)} %fusion.45), channel_id=1, source_target_pairs={{0,16},{4,12},{8,24},{12,4},{16,0},{20,28},{24,8},{28,20},{1,17},{... | collective-permute-start | bytes 1179656 | tf_op jit(solution)/shard_map/ppermute | solution.py:156
  145.8 3.9 %collective-permute-start.9 = (f32[1025]{0:T(1024)S(1)}, f32[1025]{0:T(1024)S(1)}, u32[]{:S(2)}, u32[]{:S(2)}) collective-permute-start(f32[1025]{0:T(1024)S(1)} %fusion.69), channel_id=1, source_target_pairs={{0,8},{4,20},{8,0},{12,28},{16,24},{20,4},{24,16},{28,12},{1,9},{5... | collective-permute-start | bytes 12308 | tf_op jit(solution)/shard_map/ppermute | solution.py:156
  147.4 6.0 %collective-permute-start.21 = (bf16[2,16,1024]{2,1,0:T(8,128)(2,1)S(1)}, bf16[2,16,1024]{2,1,0:T(8,128)(2,1)S(1)}, u32[]{:S(2)}, u32[]{:S(2)}) collective-permute-start(bf16[2,16,1024]{2,1,0:T(8,128)(2,1)S(1)} %fusion.63), channel_id=1, source_target_pairs={{0,1},{1,0},{2,3},{3,2},{4,5},{5,4},{6,7},{7,6},{8,9},{9,8},{10,11... | collective-permute-start | bytes 196616 | tf_op jit(solution)/shard_map/ppermute | solution.py:165
  149.7 3.7 %collective-permute-start.10 = (f32[1025]{0:T(1024)S(1)}, f32[1025]{0:T(1024)S(1)}, u32[]{:S(2)}, u32[]{:S(2)}) collective-permute-start(f32[1025]{0:T(1024)S(1)} %add.315), channel_id=1, source_target_pairs={{0,16},{4,12},{8,24},{12,4},{16,0},{20,28},{24,8},{28,20},{1,17},{... | collective-permute-start | bytes 12308 | tf_op jit(solution)/shard_map/ppermute | solution.py:156
  151.7 9.3 %collective-permute-start.16 = (bf16[2,32,1536]{2,1,0:T(8,128)(2,1)S(1)}, bf16[2,32,1536]{2,1,0:T(8,128)(2,1)S(1)}, u32[]{:S(2)}, u32[]{:S(2)}) collective-permute-start(bf16[2,32,1536]{2,1,0:T(8,128)(2,1)S(1)} %fusion.54), channel_id=1, source_target_pairs={{0,1},{1,0},{2,3},{3,2},{4,5},{5,4},{6,7},{7,6},{8,9},{9,8},{10,11... | collective-permute-start | bytes 589832 | tf_op jit(solution)/shard_map/ppermute | solution.py:167
  153.4 5.0 %collective-permute-start.11 = (f32[1025]{0:T(1024)S(1)}, f32[1025]{0:T(1024)S(1)}, u32[]{:S(2)}, u32[]{:S(2)}) collective-permute-start(f32[1025]{0:T(1024)S(1)} %add.316), channel_id=1, source_target_pairs={{0,1},{1,0},{2,3},{3,2},{4,5},{5,4},{6,7},{7,6},{8,9},{9,8},{10,11... | collective-permute-start | bytes 12308 | tf_op jit(solution)/shard_map/ppermute | solution.py:167
  154.9 6.5 %collective-permute-start.22 = (bf16[16,1024]{1,0:T(8,128)(2,1)S(1)}, bf16[16,1024]{1,0:T(8,128)(2,1)S(1)}, u32[]{:S(2)}, u32[]{:S(2)}) collective-permute-start(bf16[16,1024]{1,0:T(8,128)(2,1)S(1)} %fusion.65), channel_id=1, source_target_pairs={{0,2},{1,3},{2,0},{3,1},{4,6},{5,7},{6,4},{7,5},{8,10},{9,11},{10,... | collective-permute-start | bytes 98312 | tf_op jit(solution)/shard_map/ppermute | solution.py:165
  158.3 4.6 %collective-permute-start.12 = (f32[1025]{0:T(1024)S(1)}, f32[1025]{0:T(1024)S(1)}, u32[]{:S(2)}, u32[]{:S(2)}) collective-permute-start(f32[1025]{0:T(1024)S(1)} %add.317), channel_id=1, source_target_pairs={{0,2},{1,3},{2,0},{3,1},{4,6},{5,7},{6,4},{7,5},{8,10},{9,11},{10,... | collective-permute-start | bytes 12308 | tf_op jit(solution)/shard_map/ppermute | solution.py:167
  161.0 5.6 %collective-permute-start.17 = (bf16[32,1536]{1,0:T(8,128)(2,1)S(1)}, bf16[32,1536]{1,0:T(8,128)(2,1)S(1)}, u32[]{:S(2)}, u32[]{:S(2)}) collective-permute-start(bf16[32,1536]{1,0:T(8,128)(2,1)S(1)} %fusion.62), channel_id=1, source_target_pairs={{0,2},{1,3},{2,0},{3,1},{4,6},{5,7},{6,4},{7,5},{8,10},{9,11},{10,... | collective-permute-start | bytes 294920 | tf_op jit(solution)/shard_map/ppermute | solution.py:167
  (32 other events, 113.7 us)

commit v15 on v13

--- a/solution.py
+++ b/solution.py
@@ -244,19 +244,19 @@
         jnp.bfloat16
     )
     gathered = gather_blocks(pair_cols)
-    send_target, gathered = lax.optimization_barrier((send_target, gathered))
-    got_target = lax.all_to_all(send_target, "seq", split_axis=0, concat_axis=0, tiled=True)
-    target = (
-        jnp.zeros((TOK_DEV, width), jnp.bfloat16)
-        .at[place]
-        .set(got_target.reshape(-1, width), mode="drop")
-    )
     split_kv = gathered.reshape(shards, heads, 2, HEAD_DIM, rows)
     keys_b = split_kv[:, :, 0]
     values_b = split_kv[:, :, 1]
     queries_b = jnp.broadcast_to(queries[None], (shards,) + queries.shape)
     scores = (
         jnp.einsum("ihqd,ihdt->ihqt", queries_b, keys_b, preferred_element_type=jnp.float32) * 0.125
+    )
+    send_target, scores = lax.optimization_barrier((send_target, scores))
+    got_target = lax.all_to_all(send_target, "seq", split_axis=0, concat_axis=0, tiled=True)
+    target = (
+        jnp.zeros((TOK_DEV, width), jnp.bfloat16)
+        .at[place]
+        .set(got_target.reshape(-1, width), mode="drop")
     )
     row_max = jnp.max(scores, axis=(0, 3))
     weights = jnp.exp(scores - row_max[None, :, :, None])

time: 164 us -> 177 us (1.079)
  local copies, waits for them, and re-layouts: 30.8 us -> 36.9 us
  other arithmetic: 18.9 us -> 23.9 us
  matrix products: 20.9 us -> 23.1 us
    ppermute x0 -> x4, local copies, waits for them, and re-layouts: none -> 6.99 us  [the longest x3 5.38 us: gather_blocks(): lax.ppermute(block, 'seq', xor_pairs(2 * k))]
    optimization_barrier x1 -> x0, local copies, waits for them, and re-layouts: 3.03 us -> none  [per_device(): send_target, gathered = lax.optimization_barrier((send_target, gathered))]
    reduce_max x0 -> x1, other arithmetic: none -> 2.45 us  [per_device(): row_max = jnp.max(scores, axis=(0, 3))]
    reduce_sum x1, other arithmetic: 0.7 us -> 3.12 us  [per_device(): row_sum = jnp.sum(weights, axis=(0, 3))]
    dot_general x1, matrix products: 1.61 us -> 3.9 us  [per_device(): jnp.einsum('ihqt,ihdt->ihqd', weights.astype(jnp.bfloat16), values_b, pre...]
    dot_general x1, matrix products: 0.82 us -> 2.73 us  [per_device(): jnp.einsum('ihqd,ihdt->ihqt', queries_b, keys_b, preferred_element_type=j...]
    unnamed x60 -> x73, local copies, waits for them, and re-layouts: 10 us -> 11.2 us
  transfers between devices with their start and end apart: 26 -> 26, of which waited for: 17 -> 15; matrix products, arithmetic and copies ran while one was open for 15% -> 19% of each run, Pallas kernels for 0% -> 0%
where the time goes in v15:
time: 177 us; the launch traced here: 176 us
  waiting for transfers between devices  50.7 us (29%)
  starting transfers between devices  38 us (21%)
  local copies, waits for them, and re-layouts  36.9 us (21%)
  other arithmetic  23.9 us (14%)
  matrix products  23.1 us (13%)
  between operations  3.17 us (2%)
    ppermute x3, waiting for transfers between devices, return_blocks(): sent = lax.ppermute(summed[k].astype(jnp.bfloat16), 'seq', xor_pairs(2 * k))  11.5 us
    unnamed x73, local copies, waits for them, and re-layouts  11.2 us
    ppermute x3, waiting for transfers between devices, gather_blocks(): lax.ppermute(block, 'seq', xor_pairs(2 * k))  9.42 us
    all_to_all x1, waiting for transfers between devices, per_device(): lax.all_to_all(send_tokens, 'seq', split_axis=0, concat_axis=0, tiled=True)  8.08 us
    ppermute x6, waiting for transfers between devices, halving_scatter(): lax.ppermute((give.astype(jnp.bfloat16), small), 'seq', pairs)  7.42 us
    ppermute x4, starting transfers between devices, halving_scatter(): lax.ppermute((give.astype(jnp.bfloat16), small), 'clip', pairs)  6.19 us
    add x9, other arithmetic, halving_scatter(): data = keep + got.astype(jnp.float32)  5.76 us
    ppermute x3, local copies, waits for them, and re-layouts, gather_blocks(): lax.ppermute(block, 'seq', xor_pairs(2 * k))  5.38 us
  transfers between devices with their start and end apart: 26, of which 15 were waited for; matrix products, arithmetic and copies ran while one was open for 19% of the time, Pallas kernels for 0%

profile of v15, /device:TPU:0, one launch (start us, length us, event | category | flops | bytes accessed | tf_op | source)
XLA Modules:
  0.0 175.8 jit_solution(13116679775290335621)
XLA Ops:
  3.4 5.2 %all-to-all-start = ((s32[8,1,1]{2,1,0:T(1,128)}), s32[8,1,1]{2,1,0:T(1,128)S(1)}, u32[]{:S(2)}, u32[]{:S(2)}) async-start(s32[8,1,1]{2,1,0:T(1,128)} %broadcast_in_dim.44), calls=%async_computation | async-start | bytes 8192 | tf_op jit(solution)/shard_map/all_to_all | solution.py:206
  9.2 3.9 %all-to-all-done = s32[8,1,1]{2,1,0:T(1,128)S(1)} async-done(((s32[8,1,1]{2,1,0:T(1,128)}), s32[8,1,1]{2,1,0:T(1,128)S(1)}, u32[]{:S(2)}, u32[]{:S(2)}) %all-to-all-start) | async-done | bytes 64 | tf_op jit(solution)/shard_map/all_to_all | solution.py:206
  21.1 3.5 %all-to-all-start.1 = ((bf16[8,24,1024]{2,1,0:T(8,128)(2,1)}), bf16[8,24,1024]{2,1,0:T(8,128)(2,1)S(1)}, u32[]{:S(2)}, u32[]{:S(2)}) async-start(bf16[8,24,1024]{2,1,0:T(8,128)(2,1)} %get-tuple-element.21), calls=%async_computation.1 | async-start | bytes 786432 | tf_op jit(solution)/shard_map/all_to_all | solution.py:223
  24.7 8.1 %all-to-all-done.1 = bf16[8,24,1024]{2,1,0:T(8,128)(2,1)S(1)} async-done(((bf16[8,24,1024]{2,1,0:T(8,128)(2,1)}), bf16[8,24,1024]{2,1,0:T(8,128)(2,1)S(1)}, u32[]{:S(2)}, u32[]{:S(2)}) %all-to-all-start.1) | async-done | bytes 393248 | tf_op jit(solution)/shard_map/all_to_all | solution.py:223
  34.9 2.1 %fusion.17 = bf16[128,1024]{1,0:T(8,128)(2,1)S(1)} fusion(bf16[128,1024]{1,0:T(8,128)(2,1)S(1)} %fusion.27, bf16[1024,1536]{1,0:T(8,128)(2,1)} %param.9), kind=kOutput, calls=%fused_computation.31 | convolution fusion | flops 268566528 | bytes 2621440 | tf_op jit(solution)/shard_map/dot_general | solution.py:243
  40.6 6.6 %collective-permute-done.2 = bf16[1024,128]{0,1:T(8,128)(2,1)S(1)} collective-permute-done((bf16[1024,128]{0,1:T(8,128)(2,1)S(1)}, bf16[1024,128]{0,1:T(8,128)(2,1)S(1)}, u32[]{:S(2)}, u32[]{:S(2)}) %collective-permute-start.2) | collective-permute-done | bytes 262176 | tf_op jit(solution)/shard_map/ppermute | solution.py:179
  47.2 2.8 %collective-permute-done.1 = bf16[1024,128]{0,1:T(8,128)(2,1)S(1)} collective-permute-done((bf16[1024,128]{0,1:T(8,128)(2,1)S(1)}, bf16[1024,128]{0,1:T(8,128)(2,1)S(1)}, u32[]{:S(2)}, u32[]{:S(2)}) %collective-permute-start.1) | collective-permute-done | bytes 262176 | tf_op jit(solution)/shard_map/ppermute | solution.py:179
  53.8 1.8 %copy.62 = bf16[1024,128]{1,0:T(8,128)(2,1)} copy(bf16[1024,128]{0,1:T(8,128)(2,1)} %copy-done.13) | data formatting | bytes 524288 | tf_op jit(solution)/shard_map/ppermute | solution.py:179
  55.6 1.8 %copy.61 = bf16[1024,128]{1,0:T(8,128)(2,1)} copy(bf16[1024,128]{0,1:T(8,128)(2,1)} %copy-done.14) | data formatting | bytes 524288 | tf_op jit(solution)/shard_map/ppermute | solution.py:179
  57.4 1.8 %copy.60 = bf16[1024,128]{1,0:T(8,128)(2,1)} copy(bf16[1024,128]{0,1:T(8,128)(2,1)} %copy-done.15) | data formatting | bytes 524288 | tf_op jit(solution)/shard_map/ppermute | solution.py:179
  64.0 2.7 %convolution_multiply_fusion = f32[8,8,128,128]{3,2,1,0:T(8,128)} fusion(bf16[8,8,2,64,128]{4,3,2,1,0:T(8,128)(2,1)S(1)} %constant_dynamic-update-slice_fusion, bf16[8,128,64]{1,2,0:T(8,128)(2,1)S(1)} %bitcast.206), kind=kOutput, calls=%fused_computation.14 | convolution fusion | flops 135266304 | bytes 5373952 | tf_op jit(solution)/shard_map/ihqd,ihdt->ihqt/dot_general | solution.py:252
  66.7 2.5 %reduce_max.9 = f32[8,128]{1,0:T(8,128)S(1)} reduce(f32[8,8,128,128]{3,2,1,0:T(8,128)} %convolution_multiply_fusion, f32[]{:T(128)} %constant.173.clone.1), dimensions={0,3}, to_apply=%region_6.7 | reduce | flops 1047552 | bytes 4198404 | tf_op jit(solution)/shard_map/reduce_max | solution.py:261
  69.1 3.1 %fusion.1 = f32[8,128]{1,0:T(8,128)S(1)} fusion(f32[8,8,128,128]{3,2,1,0:T(8,128)} %convolution_multiply_fusion, f32[8,128]{1,0:T(8,128)S(1)} %reduce_max.9), kind=kLoop, calls=%fused_computation.10 | loop fusion | flops 2096128 | bytes 4202496 | tf_op jit(solution)/shard_map/reduce_sum | solution.py:263
  72.3 3.9 %all-to-all-start.2 = ((bf16[8,24,1024]{2,1,0:T(8,128)(2,1)}), bf16[8,24,1024]{2,1,0:T(8,128)(2,1)S(1)}, u32[]{:S(2)}, u32[]{:S(2)}) async-start(bf16[8,24,1024]{2,1,0:T(8,128)(2,1)} %get-tuple-element.7), calls=%async_computation.2 | async-start | bytes 786432 | tf_op jit(solution)/shard_map/all_to_all | solution.py:255
  76.1 3.9 %fusion.48 = (bf16[128,8,64]{0,2,1:T(8,128)(2,1)S(1)}, f32[8,128,64,1]{1,2,0,3:T(8,128)}) fusion(f32[128,8]{0,1:T(8,128)S(1)} %bitcast.226, bf16[8,8,2,64,128]{4,3,2,1,0:T(8,128)(2,1)S(1)} %constant_dynamic-update-slice_fusion, f32[8,8,128,128]{3,2,1,0:T(8,128)} %convolution_multiply_fusion, f32[8,128]{1,0:T(8,128)S(1)} %reduce_max.9), kind=kOutput, calls=%fused_computation.98 | convolution fusion | flops 136445952 | bytes 5644288 | tf_op jit(solution)/shard_map/ihqt,ihdt->ihqd/dot_general | solution.py:265
  80.5 4.0 %all-to-all-done.2 = bf16[8,24,1024]{2,1,0:T(8,128)(2,1)S(1)} async-done(((bf16[8,24,1024]{2,1,0:T(8,128)(2,1)}), bf16[8,24,1024]{2,1,0:T(8,128)(2,1)S(1)}, u32[]{:S(2)}, u32[]{:S(2)}) %all-to-all-start.2) | async-done | bytes 393248 | tf_op jit(solution)/shard_map/all_to_all | solution.py:255
  85.2 2.1 %scatter_custom_fusion.1 = bf16[128,1024]{1,0:T(8,128)(2,1)S(1)} fusion(s32[192]{0:T(256)} %bitcast.230, bf16[192,1024]{1,0:T(8,128)(2,1)} %bitcast.223, bf16[]{:T(256)} %constant.157.clone.1), kind=kCustom, calls=%fused_computation.113 | custom fusion | bytes 262656 | tf_op jit(solution)/shard_map/scatter | solution.py:259
  89.6 3.2 %fusion.14 = bf16[8,8,64,128]{3,2,1,0:T(8,128)(2,1)S(1)} fusion(f32[8,8,128,128]{3,2,1,0:T(8,128)} %convolution_multiply_fusion, f32[8,128]{1,0:T(8,128)S(1)} %log_add_fusion, bf16[8,128,64]{1,2,0:T(8,128)(2,1)S(1)} %bitcast.200), kind=kOutput, calls=%fused_computation.28 | convolution fusion | flops 136839168 | bytes 5378048 | tf_op jit(solution)/shard_map/ihqd,ihqt->ihdt/dot_general | solution.py:293
  93.0 2.6 %multiply_convert_fusion = bf16[8,8,128,128]{3,2,1,0:T(8,128)(2,1)S(1)} fusion(f32[8,8,128,128]{3,2,1,0:T(8,128)S(1)} %copy-done.2, f32[8,128]{1,0:T(8,128)S(1)} %multiply_reduce_fusion.3, f32[8,128]{1,0:T(8,128)S(1)} %log_add_fusion, bf16[8,8,2,64,128]{4,3,2,1,0:T(8,128)(2,1)} %copy-done.6, bf16[8,128,64]{1,2,0:T(8,128)(2,1)S(1)} %bitcast.201), kind=kOutput, calls=%fused_computation.6 | convolution fusion | flops 138412032 | bytes 7479296 | tf_op jit(solution)/shard_map/ihqd,ihdt->ihqt/dot_general | solution.py:296
  99.3 1.8 %copy.73 = bf16[128,1024]{0,1:T(8,128)(2,1)} copy(bf16[128,1024]{1,0:T(8,128)(2,1)} %copy-done.12) | data formatting | bytes 524288 | tf_op jit(solution)/shard_map/convert_element_type | solution.py:21
  102.7 1.7 fusion.69
  108.9 4.8 %collective-permute-done.5 = bf16[1024,128]{1,0:T(8,128)(2,1)S(1)} collective-permute-done((bf16[1024,128]{1,0:T(8,128)(2,1)S(1)}, bf16[1024,128]{1,0:T(8,128)(2,1)S(1)}, u32[]{:S(2)}, u32[]{:S(2)}) %collective-permute-start.5) | collective-permute-done | bytes 262176 | tf_op jit(solution)/shard_map/ppermute | solution.py:191
  113.7 5.3 %collective-permute-done.7 = bf16[1024,128]{1,0:T(8,128)(2,1)S(1)} collective-permute-done((bf16[1024,128]{1,0:T(8,128)(2,1)S(1)}, bf16[1024,128]{1,0:T(8,128)(2,1)S(1)}, u32[]{:S(2)}, u32[]{:S(2)}) %collective-permute-start.7) | collective-permute-done | bytes 262176 | tf_op jit(solution)/shard_map/ppermute | solution.py:191
  122.2 2.6 %copy-done.5 = f32[2,2,2,2,2,32,1536]{6,5,4,3,2,1,0:T(8,128)} copy-done((f32[2,2,2,2,2,32,1536]{6,5,4,3,2,1,0:T(8,128)}, f32[2,2,2,2,2,32,1536]{6,5,4,3,2,1,0:T(8,128)S(1)}, u32[]{:S(2)}) %copy-start.5) | copy-done | bytes 6291480
  127.6 3.0 %collective-permute-done.18 = bf16[2,2,2,2,16,1024]{5,4,3,2,1,0:T(8,128)(2,1)} collective-permute-done((bf16[2,2,2,2,16,1024]{5,4,3,2,1,0:T(8,128)(2,1)S(1)}, bf16[2,2,2,2,16,1024]{5,4,3,2,1,0:T(8,128)(2,1)}, u32[]{:S(2)}, u32[]{:S(2)}) %collective-permute-start.18) | collective-permute-done | bytes 524320 | tf_op jit(solution)/shard_map/ppermute | solution.py:153
  132.5 2.9 %bitcast_add_fusion = f32[2,2,2,2,32,1536]{5,4,3,2,1,0:T(8,128)S(1)} fusion(bf16[2,2,2,2,32,1536]{5,4,3,2,1,0:T(8,128)(2,1)} %collective-permute-done.13, f32[2,2,2,2,2,32,1536]{6,5,4,3,2,1,0:T(8,128)} %copy-done.5, s32[]{:T(128)S(6)} %select_n.233), kind=kLoop, calls=%fused_computation.12 | loop fusion | flops 1572864 | bytes 7864324 | tf_op jit(solution)/shard_map/add | solution.py:157
  141.3 3.1 %fusion.20 = f32[1024]{0:T(1024)S(1)} fusion(bf16[1024,1536]{1,0:T(8,128)(2,1)} %param.9, bf16[128,1024]{1,0:T(8,128)(2,1)S(1)} %scatter_custom_fusion, f32[128]{0:T(128)S(1)} %copy-done.33, f32[128]{0:T(128)S(1)} %copy-done.22, bf16[1024,128]{1,0:T(8,128)(2,1)S(1)} %copy-done.18, bf16[512,128]{1,0:T(8,128)(2,1)S(1)} %bitcast.222), kind=kOutput, calls=%fused_computation.32 | convolution fusion | flops 404093952 | bytes 3806208 | tf_op jit(solution)/shard_map/ct,fc->tf/dot_general | solution.py:312
  145.1 5.5 %collective-permute-done.14 = bf16[2,2,2,32,1536]{4,3,2,1,0:T(8,128)(2,1)S(1)} collective-permute-done((bf16[2,2,2,32,1536]{4,3,2,1,0:T(8,128)(2,1)S(1)}, bf16[2,2,2,32,1536]{4,3,2,1,0:T(8,128)(2,1)S(1)}, u32[]{:S(2)}, u32[]{:S(2)}) %collective-permute-start.14) | collective-permute-done | bytes 786464 | tf_op jit(solution)/shard_map/ppermute | solution.py:155
  159.2 1.6 collective-permute-start.16
  162.5 2.6 %collective-permute-start.22 = (bf16[16,1024]{1,0:T(8,128)(2,1)S(1)}, bf16[16,1024]{1,0:T(8,128)(2,1)S(1)}, u32[]{:S(2)}, u32[]{:S(2)}) collective-permute-start(bf16[16,1024]{1,0:T(8,128)(2,1)S(1)} %fusion.62), channel_id=1, source_target_pairs={{0,2},{1,3},{2,0},{3,1},{4,6},{5,7},{6,4},{7,5},{8,10},{9,11},{10,... | collective-permute-start | bytes 98312 | tf_op jit(solution)/shard_map/ppermute | solution.py:164
  165.7 2.6 %collective-permute-start.12 = (f32[1025]{0:T(1024)S(1)}, f32[1025]{0:T(1024)S(1)}, u32[]{:S(2)}, u32[]{:S(2)}) collective-permute-start(f32[1025]{0:T(1024)S(1)} %add.317), channel_id=1, source_target_pairs={{0,2},{1,3},{2,0},{3,1},{4,6},{5,7},{6,4},{7,5},{8,10},{9,11},{10,... | collective-permute-start | bytes 12308 | tf_op jit(solution)/shard_map/ppermute | solution.py:166
  172.0 1.9 %collective-permute-done.17 = bf16[32,1536]{1,0:T(8,128)(2,1)S(1)} collective-permute-done((bf16[32,1536]{1,0:T(8,128)(2,1)S(1)}, bf16[32,1536]{1,0:T(8,128)(2,1)S(1)}, u32[]{:S(2)}, u32[]{:S(2)}) %collective-permute-start.17) | collective-permute-done | bytes 98336 | tf_op jit(solution)/shard_map/ppermute | solution.py:166
  (192 shorter events, 67.8 us)
Async XLA Ops:
  0.6 15.2 %copy-start = (bf16[1,512,1024]{2,1,0:T(8,128)(2,1)S(1)}, bf16[1,512,1024]{2,1,0:T(8,128)(2,1)}, u32[]{:S(2)}) copy-start(bf16[1,512,1024]{2,1,0:T(8,128)(2,1)} %param.7) | copy-start | bytes 3145732
  0.6 16.2 %copy-start.8 = (bf16[1,512,1024]{2,1,0:T(8,128)(2,1)S(1)}, bf16[1,512,1024]{2,1,0:T(8,128)(2,1)}, u32[]{:S(2)}) copy-start(bf16[1,512,1024]{2,1,0:T(8,128)(2,1)} %param.6) | copy-start | bytes 3145732
  3.4 9.8 %all-to-all-start = ((s32[8,1,1]{2,1,0:T(1,128)}), s32[8,1,1]{2,1,0:T(1,128)S(1)}, u32[]{:S(2)}, u32[]{:S(2)}) async-start(s32[8,1,1]{2,1,0:T(1,128)} %broadcast_in_dim.44), calls=%async_computation | async-start | bytes 8192 | tf_op jit(solution)/shard_map/all_to_all | solution.py:206
  21.1 11.7 %all-to-all-start.1 = ((bf16[8,24,1024]{2,1,0:T(8,128)(2,1)}), bf16[8,24,1024]{2,1,0:T(8,128)(2,1)S(1)}, u32[]{:S(2)}, u32[]{:S(2)}) async-start(bf16[8,24,1024]{2,1,0:T(8,128)(2,1)} %get-tuple-element.21), calls=%async_computation.1 | async-start | bytes 786432 | tf_op jit(solution)/shard_map/all_to_all | solution.py:223
  34.4 15.8 %copy-start.21 = (f32[128]{0:T(128)}, f32[128]{0:T(128)S(1)}, u32[]{:S(2)}) copy-start(f32[128]{0:T(128)S(1)} %broadcast_multiply_fusion.1) | copy-start | bytes 1540
  34.6 15.5 %copy-start.32 = (f32[128]{0:T(128)}, f32[128]{0:T(128)S(1)}, u32[]{:S(2)}) copy-start(f32[128]{0:T(128)S(1)} %add_rsqrt_fusion.2) | copy-start | bytes 1540
  34.9 16.2 %copy-start.12 = (bf16[128,1024]{1,0:T(8,128)(2,1)}, bf16[128,1024]{1,0:T(8,128)(2,1)S(1)}, u32[]{:S(2)}) copy-start(bf16[128,1024]{1,0:T(8,128)(2,1)S(1)} %fusion.27) | copy-start | bytes 786436
  37.0 10.2 %collective-permute-start.2 = (bf16[1024,128]{0,1:T(8,128)(2,1)S(1)}, bf16[1024,128]{0,1:T(8,128)(2,1)S(1)}, u32[]{:S(2)}, u32[]{:S(2)}) collective-permute-start(bf16[1024,128]{0,1:T(8,128)(2,1)S(1)} %bitcast.214), channel_id=1, source_target_pairs={{0,24},{4,28},{8,16},{12,20},{16,8},{20,12},{24,0},{28,4},{1,25},{... | collective-permute-start | bytes 786440 | tf_op jit(solution)/shard_map/ppermute | solution.py:179
  37.6 12.4 %collective-permute-start.1 = (bf16[1024,128]{0,1:T(8,128)(2,1)S(1)}, bf16[1024,128]{0,1:T(8,128)(2,1)S(1)}, u32[]{:S(2)}, u32[]{:S(2)}) collective-permute-start(bf16[1024,128]{0,1:T(8,128)(2,1)S(1)} %bitcast.215), channel_id=1, source_target_pairs={{0,16},{4,20},{8,24},{12,28},{16,0},{20,4},{24,8},{28,12},{1,17},{... | collective-permute-start | bytes 786440 | tf_op jit(solution)/shard_map/ppermute | solution.py:179
  39.1 10.9 %collective-permute-start = (bf16[1024,128]{0,1:T(8,128)(2,1)S(1)}, bf16[1024,128]{0,1:T(8,128)(2,1)S(1)}, u32[]{:S(2)}, u32[]{:S(2)}) collective-permute-start(bf16[1024,128]{0,1:T(8,128)(2,1)S(1)} %bitcast.216), channel_id=1, source_target_pairs={{0,8},{4,12},{8,0},{12,4},{16,24},{20,28},{24,16},{28,20},{1,9},{5... | collective-permute-start | bytes 786440 | tf_op jit(solution)/shard_map/ppermute | solution.py:179
  50.2 12.0 %collective-permute-start.3 = (bf16[4,1024,128]{1,2,0:T(8,128)(2,1)S(1)}, bf16[4,1024,128]{1,2,0:T(8,128)(2,1)}, u32[]{:S(2)}, u32[]{:S(2)}) collective-permute-start(bf16[4,1024,128]{1,2,0:T(8,128)(2,1)S(1)} %pad_maximum_fusion), channel_id=1, source_target_pairs={{0,4},{4,0},{8,12},{12,8},{16,20},{20,16},{24,28},{28,24},{1,5},{5... | collective-permute-start | bytes 3145736 | tf_op jit(solution)/shard_map/ppermute | solution.py:181
  72.3 12.2 %all-to-all-start.2 = ((bf16[8,24,1024]{2,1,0:T(8,128)(2,1)}), bf16[8,24,1024]{2,1,0:T(8,128)(2,1)S(1)}, u32[]{:S(2)}, u32[]{:S(2)}) async-start(bf16[8,24,1024]{2,1,0:T(8,128)(2,1)} %get-tuple-element.7), calls=%async_computation.2 | async-start | bytes 786432 | tf_op jit(solution)/shard_map/all_to_all | solution.py:255
  99.3 3.4 %collective-permute-start.4 = (bf16[4,1024,128]{2,1,0:T(8,128)(2,1)}, bf16[4,1024,128]{2,1,0:T(8,128)(2,1)}, u32[]{:S(2)}, u32[]{:S(2)}) collective-permute-start(bf16[4,1024,128]{2,1,0:T(8,128)(2,1)} %bitcast.37), channel_id=1, source_target_pairs={{0,4},{4,0},{8,12},{12,8},{16,20},{20,16},{24,28},{28,24},{1,5},{5... | collective-permute-start | bytes 3145736 | tf_op jit(solution)/shard_map/ppermute | solution.py:187
  104.5 9.2 %collective-permute-start.5 = (bf16[1024,128]{1,0:T(8,128)(2,1)S(1)}, bf16[1024,128]{1,0:T(8,128)(2,1)S(1)}, u32[]{:S(2)}, u32[]{:S(2)}) collective-permute-start(bf16[1024,128]{1,0:T(8,128)(2,1)S(1)} %get-tuple-element.14), channel_id=1, source_target_pairs={{0,8},{4,12},{8,0},{12,4},{16,24},{20,28},{24,16},{28,20},{1,9},{5... | collective-permute-start | bytes 786440 | tf_op jit(solution)/shard_map/ppermute | solution.py:191
  105.2 13.8 %collective-permute-start.7 = (bf16[1024,128]{1,0:T(8,128)(2,1)S(1)}, bf16[1024,128]{1,0:T(8,128)(2,1)S(1)}, u32[]{:S(2)}, u32[]{:S(2)}) collective-permute-start(bf16[1024,128]{1,0:T(8,128)(2,1)S(1)} %get-tuple-element.15), channel_id=1, source_target_pairs={{0,24},{4,28},{8,16},{12,20},{16,8},{20,12},{24,0},{28,4},{1,25},{... | collective-permute-start | bytes 786440 | tf_op jit(solution)/shard_map/ppermute | solution.py:191
  106.6 13.8 %collective-permute-start.6 = (bf16[1024,128]{1,0:T(8,128)(2,1)S(1)}, bf16[1024,128]{1,0:T(8,128)(2,1)S(1)}, u32[]{:S(2)}, u32[]{:S(2)}) collective-permute-start(bf16[1024,128]{1,0:T(8,128)(2,1)S(1)} %get-tuple-element.16), channel_id=1, source_target_pairs={{0,16},{4,20},{8,24},{12,28},{16,0},{20,4},{24,8},{28,12},{1,17},{... | collective-permute-start | bytes 786440 | tf_op jit(solution)/shard_map/ppermute | solution.py:191
  126.3 6.2 %collective-permute-start.13 = (bf16[2,2,2,2,32,1536]{5,4,3,2,1,0:T(8,128)(2,1)}, bf16[2,2,2,2,32,1536]{5,4,3,2,1,0:T(8,128)(2,1)}, u32[]{:S(2)}, u32[]{:S(2)}) collective-permute-start(bf16[2,2,2,2,32,1536]{5,4,3,2,1,0:T(8,128)(2,1)} %fusion.11), channel_id=1, source_target_pairs={{0,4},{4,0},{8,12},{12,8},{16,20},{20,16},{24,28},{28,24},{1,5},{5... | collective-permute-start | bytes 4718600 | tf_op jit(solution)/shard_map/ppermute | solution.py:155
  127.0 3.6 %collective-permute-start.18 = (bf16[2,2,2,2,16,1024]{5,4,3,2,1,0:T(8,128)(2,1)S(1)}, bf16[2,2,2,2,16,1024]{5,4,3,2,1,0:T(8,128)(2,1)}, u32[]{:S(2)}, u32[]{:S(2)}) collective-permute-start(bf16[2,2,2,2,16,1024]{5,4,3,2,1,0:T(8,128)(2,1)S(1)} %fusion.31), channel_id=1, source_target_pairs={{0,4},{4,0},{8,12},{12,8},{16,20},{20,16},{24,28},{28,24},{1,5},{5... | collective-permute-start | bytes 1572872 | tf_op jit(solution)/shard_map/ppermute | solution.py:153
  131.8 6.8 %collective-permute-start.19 = (bf16[2,2,2,16,1024]{4,3,2,1,0:T(8,128)(2,1)S(1)}, bf16[2,2,2,16,1024]{4,3,2,1,0:T(8,128)(2,1)}, u32[]{:S(2)}, u32[]{:S(2)}) collective-permute-start(bf16[2,2,2,16,1024]{4,3,2,1,0:T(8,128)(2,1)S(1)} %fusion.36), channel_id=1, source_target_pairs={{0,8},{4,20},{8,0},{12,28},{16,24},{20,4},{24,16},{28,12},{1,9},{5... | collective-permute-start | bytes 786440 | tf_op jit(solution)/shard_map/ppermute | solution.py:153
  137.2 13.5 %collective-permute-start.14 = (bf16[2,2,2,32,1536]{4,3,2,1,0:T(8,128)(2,1)S(1)}, bf16[2,2,2,32,1536]{4,3,2,1,0:T(8,128)(2,1)S(1)}, u32[]{:S(2)}, u32[]{:S(2)}) collective-permute-start(bf16[2,2,2,32,1536]{4,3,2,1,0:T(8,128)(2,1)S(1)} %fusion.12), channel_id=1, source_target_pairs={{0,8},{4,20},{8,0},{12,28},{16,24},{20,4},{24,16},{28,12},{1,9},{5... | collective-permute-start | bytes 2359304 | tf_op jit(solution)/shard_map/ppermute | solution.py:155
  139.8 12.9 %collective-permute-start.20 = (bf16[2,2,16,1024]{3,2,1,0:T(8,128)(2,1)S(1)}, bf16[2,2,16,1024]{3,2,1,0:T(8,128)(2,1)S(1)}, u32[]{:S(2)}, u32[]{:S(2)}) collective-permute-start(bf16[2,2,16,1024]{3,2,1,0:T(8,128)(2,1)S(1)} %fusion.52), channel_id=1, source_target_pairs={{0,16},{4,12},{8,24},{12,4},{16,0},{20,28},{24,8},{28,20},{1,17},{... | collective-permute-start | bytes 393224 | tf_op jit(solution)/shard_map/ppermute | solution.py:153
  145.0 7.7 %collective-permute-start.8 = (f32[1025]{0:T(1024)S(1)}, f32[1025]{0:T(1024)S(1)}, u32[]{:S(2)}, u32[]{:S(2)}) collective-permute-start(f32[1025]{0:T(1024)S(1)} %pad_maximum_fusion.5), channel_id=1, source_target_pairs={{0,4},{4,0},{8,12},{12,8},{16,20},{20,16},{24,28},{28,24},{1,5},{5... | collective-permute-start | bytes 12308 | tf_op jit(solution)/shard_map/ppermute | solution.py:155
  151.1 7.9 %collective-permute-start.15 = (bf16[2,2,32,1536]{3,2,1,0:T(8,128)(2,1)S(1)}, bf16[2,2,32,1536]{3,2,1,0:T(8,128)(2,1)S(1)}, u32[]{:S(2)}, u32[]{:S(2)}) collective-permute-start(bf16[2,2,32,1536]{3,2,1,0:T(8,128)(2,1)S(1)} %fusion.42), channel_id=1, source_target_pairs={{0,16},{4,12},{8,24},{12,4},{16,0},{20,28},{24,8},{28,20},{1,17},{... | collective-permute-start | bytes 1179656 | tf_op jit(solution)/shard_map/ppermute | solution.py:155
  153.4 3.9 %collective-permute-start.9 = (f32[1025]{0:T(1024)S(1)}, f32[1025]{0:T(1024)S(1)}, u32[]{:S(2)}, u32[]{:S(2)}) collective-permute-start(f32[1025]{0:T(1024)S(1)} %fusion.66), channel_id=1, source_target_pairs={{0,8},{4,20},{8,0},{12,28},{16,24},{20,4},{24,16},{28,12},{1,9},{5... | collective-permute-start | bytes 12308 | tf_op jit(solution)/shard_map/ppermute | solution.py:155
  154.9 6.0 %collective-permute-start.21 = (bf16[2,16,1024]{2,1,0:T(8,128)(2,1)S(1)}, bf16[2,16,1024]{2,1,0:T(8,128)(2,1)S(1)}, u32[]{:S(2)}, u32[]{:S(2)}) collective-permute-start(bf16[2,16,1024]{2,1,0:T(8,128)(2,1)S(1)} %fusion.60), channel_id=1, source_target_pairs={{0,1},{1,0},{2,3},{3,2},{4,5},{5,4},{6,7},{7,6},{8,9},{9,8},{10,11... | collective-permute-start | bytes 196616 | tf_op jit(solution)/shard_map/ppermute | solution.py:164
  157.3 3.7 %collective-permute-start.10 = (f32[1025]{0:T(1024)S(1)}, f32[1025]{0:T(1024)S(1)}, u32[]{:S(2)}, u32[]{:S(2)}) collective-permute-start(f32[1025]{0:T(1024)S(1)} %add.315), channel_id=1, source_target_pairs={{0,16},{4,12},{8,24},{12,4},{16,0},{20,28},{24,8},{28,20},{1,17},{... | collective-permute-start | bytes 12308 | tf_op jit(solution)/shard_map/ppermute | solution.py:155
  159.1 15.6 %copy-start.1 = (bf16[1,512,1024]{2,1,0:T(8,128)(2,1)S(1)}, bf16[1,512,1024]{2,1,0:T(8,128)(2,1)}, u32[]{:S(2)}) copy-start(bf16[1,512,1024]{2,1,0:T(8,128)(2,1)} %param.7) | copy-start | bytes 3145732
  159.2 9.0 %collective-permute-start.16 = (bf16[2,32,1536]{2,1,0:T(8,128)(2,1)S(1)}, bf16[2,32,1536]{2,1,0:T(8,128)(2,1)S(1)}, u32[]{:S(2)}, u32[]{:S(2)}) collective-permute-start(bf16[2,32,1536]{2,1,0:T(8,128)(2,1)S(1)} %fusion.51), channel_id=1, source_target_pairs={{0,1},{1,0},{2,3},{3,2},{4,5},{5,4},{6,7},{7,6},{8,9},{9,8},{10,11... | collective-permute-start | bytes 589832 | tf_op jit(solution)/shard_map/ppermute | solution.py:166
  160.9 4.8 %collective-permute-start.11 = (f32[1025]{0:T(1024)S(1)}, f32[1025]{0:T(1024)S(1)}, u32[]{:S(2)}, u32[]{:S(2)}) collective-permute-start(f32[1025]{0:T(1024)S(1)} %add.316), channel_id=1, source_target_pairs={{0,1},{1,0},{2,3},{3,2},{4,5},{5,4},{6,7},{7,6},{8,9},{9,8},{10,11... | collective-permute-start | bytes 12308 | tf_op jit(solution)/shard_map/ppermute | solution.py:166
  162.5 6.3 %collective-permute-start.22 = (bf16[16,1024]{1,0:T(8,128)(2,1)S(1)}, bf16[16,1024]{1,0:T(8,128)(2,1)S(1)}, u32[]{:S(2)}, u32[]{:S(2)}) collective-permute-start(bf16[16,1024]{1,0:T(8,128)(2,1)S(1)} %fusion.62), channel_id=1, source_target_pairs={{0,2},{1,3},{2,0},{3,1},{4,6},{5,7},{6,4},{7,5},{8,10},{9,11},{10,... | collective-permute-start | bytes 98312 | tf_op jit(solution)/shard_map/ppermute | solution.py:164
  165.7 4.6 %collective-permute-start.12 = (f32[1025]{0:T(1024)S(1)}, f32[1025]{0:T(1024)S(1)}, u32[]{:S(2)}, u32[]{:S(2)}) collective-permute-start(f32[1025]{0:T(1024)S(1)} %add.317), channel_id=1, source_target_pairs={{0,2},{1,3},{2,0},{3,1},{4,6},{5,7},{6,4},{7,5},{8,10},{9,11},{10,... | collective-permute-start | bytes 12308 | tf_op jit(solution)/shard_map/ppermute | solution.py:166
  168.4 5.6 %collective-permute-start.17 = (bf16[32,1536]{1,0:T(8,128)(2,1)S(1)}, bf16[32,1536]{1,0:T(8,128)(2,1)S(1)}, u32[]{:S(2)}, u32[]{:S(2)}) collective-permute-start(bf16[32,1536]{1,0:T(8,128)(2,1)S(1)} %fusion.59), channel_id=1, source_target_pairs={{0,2},{1,3},{2,0},{3,1},{4,6},{5,7},{6,4},{7,5},{8,10},{9,11},{10,... | collective-permute-start | bytes 294920 | tf_op jit(solution)/shard_map/ppermute | solution.py:166
  (28 other events, 151.1 us)

commit v16 on v15

--- a/solution.py
+++ b/solution.py
@@ -220,16 +220,20 @@
     send_target = jnp.where(
         pick_ok[:, :, None], kept_target[pick_safe], jnp.zeros((), jnp.bfloat16)
     )
-    got_tokens = lax.all_to_all(send_tokens, "seq", split_axis=0, concat_axis=0, tiled=True)
+    got_both = lax.all_to_all(
+        jnp.concatenate([send_tokens, send_target], axis=2), "seq", split_axis=0, concat_axis=0, tiled=True
+    )
     from_pick = (my_index - starts[:, None]) % shards + slot_ids[None, :] * shards
     from_ok = from_pick < count_table[:, None]
     place = jnp.where(from_ok, (starts[:, None] + from_pick) // shards, TOK_DEV).reshape(-1)
-    width = got_tokens.shape[2]
-    tokens = (
-        jnp.zeros((TOK_DEV, width), jnp.bfloat16)
+    width = send_tokens.shape[2]
+    both = (
+        jnp.zeros((TOK_DEV, 2 * width), jnp.bfloat16)
         .at[place]
-        .set(got_tokens.reshape(-1, width), mode="drop")
-    )
+        .set(got_both.reshape(-1, 2 * width), mode="drop")
+    )
+    tokens = both[:, :width]
+    target = both[:, width:]
     rows = tokens.shape[0]
     inner = w_out.shape[0]
     heads = inner // HEAD_DIM
@@ -251,13 +255,6 @@
     scores = (
         jnp.einsum("ihqd,ihdt->ihqt", queries_b, keys_b, preferred_element_type=jnp.float32) * 0.125
     )
-    send_target, scores = lax.optimization_barrier((send_target, scores))
-    got_target = lax.all_to_all(send_target, "seq", split_axis=0, concat_axis=0, tiled=True)
-    target = (
-        jnp.zeros((TOK_DEV, width), jnp.bfloat16)
-        .at[place]
-        .set(got_target.reshape(-1, width), mode="drop")
-    )
     row_max = jnp.max(scores, axis=(0, 3))
     weights = jnp.exp(scores - row_max[None, :, :, None])
     row_sum = jnp.sum(weights, axis=(0, 3))

time: 177 us -> 162 us (0.915)
  local copies, waits for them, and re-layouts: 36.9 us -> 32 us
  starting transfers between devices: 38 us -> 33.3 us
  other arithmetic: 23.9 us -> 20 us
  matrix products: 23.1 us -> 20.2 us
  waiting for transfers between devices: 50.7 us -> 53 us
    all_to_all x2 -> x1, starting transfers between devices: 7.31 us -> 3.55 us  [per_device(): lax.all_to_all(jnp.concatenate([send_tokens, send_target], axis=2), 'seq'...]
    reduce_max x1 -> x0, other arithmetic: 2.45 us -> none  [per_device(): row_max = jnp.max(scores, axis=(0, 3))]
    reduce_sum x1, other arithmetic: 3.12 us -> 0.7 us  [per_device(): row_sum = jnp.sum(weights, axis=(0, 3))]
    ppermute x6, waiting for transfers between devices: 7.42 us -> 9.71 us  [halving_scatter(): lax.ppermute((give.astype(jnp.bfloat16), small), 'seq', pairs)]
    dot_general x1, matrix products: 3.9 us -> 1.63 us  [per_device(): jnp.einsum('ihqt,ihdt->ihqd', weights.astype(jnp.bfloat16), values_b, pre...]
    unnamed x73 -> x65, local copies, waits for them, and re-layouts: 11.2 us -> 9.2 us
    dot_general x1, matrix products: 2.73 us -> 0.82 us  [per_device(): jnp.einsum('ihqd,ihdt->ihqt', queries_b, keys_b, preferred_element_type=j...]
    all_to_all x2 -> x1, waiting for transfers between devices: 12 us -> 12.3 us  [per_device(): lax.all_to_all(jnp.concatenate([send_tokens, send_target], axis=2), 'seq'...]
  transfers between devices with their start and end apart: 26 -> 25, of which waited for: 15 -> 16; matrix products, arithmetic and copies ran while one was open for 19% -> 15% of each run, Pallas kernels for 0% -> 0%
where the time goes in v16:
time: 162 us
  waiting for transfers between devices  53 us (33%)
  starting transfers between devices  33.3 us (21%)
  local copies, waits for them, and re-layouts  32 us (20%)
  matrix products  20.2 us (12%)
  other arithmetic  20 us (12%)
  between operations  3.11 us (2%)
    ppermute x3, waiting for transfers between devices, return_blocks(): sent = lax.ppermute(summed[k].astype(jnp.bfloat16), 'seq', xor_pairs(2 * k))  12.6 us
    all_to_all x1, waiting for transfers between devices, per_device(): lax.all_to_all(jnp.concatenate([send_tokens, send_target], axis=2), 'seq'...  12.3 us
    ppermute x6, waiting for transfers between devices, halving_scatter(): lax.ppermute((give.astype(jnp.bfloat16), small), 'seq', pairs)  9.71 us
    ppermute x3, waiting for transfers between devices, gather_blocks(): lax.ppermute(block, 'seq', xor_pairs(2 * k))  9.21 us
    unnamed x65, local copies, waits for them, and re-layouts  9.2 us
    ppermute x4, starting transfers between devices, halving_scatter(): lax.ppermute((give.astype(jnp.bfloat16), small), 'clip', pairs)  5.36 us
    all_to_all x1, starting transfers between devices, per_device(): lax.all_to_all(jnp.broadcast_to(kept_count.reshape(1, 1), (shards, 1)), '...  5.17 us
    add x9, other arithmetic, halving_scatter(): data = keep + got.astype(jnp.float32)  5.02 us
  transfers between devices with their start and end apart: 25, of which 16 were waited for; matrix products, arithmetic and copies ran while one was open for 15% of the time, Pallas kernels for 0%

profile of v16, /device:TPU:0, one launch (start us, length us, event | category | flops | bytes accessed | tf_op | source)
XLA Modules:
  0.0 161.7 jit_solution(2687805051318437560)
XLA Ops:
  3.4 5.2 %all-to-all-start = ((s32[8,1,1]{2,1,0:T(1,128)}), s32[8,1,1]{2,1,0:T(1,128)S(1)}, u32[]{:S(2)}, u32[]{:S(2)}) async-start(s32[8,1,1]{2,1,0:T(1,128)} %broadcast_in_dim.47), calls=%async_computation | async-start | bytes 8192 | tf_op jit(solution)/shard_map/all_to_all | solution.py:206
  9.2 3.9 %all-to-all-done = s32[8,1,1]{2,1,0:T(1,128)S(1)} async-done(((s32[8,1,1]{2,1,0:T(1,128)}), s32[8,1,1]{2,1,0:T(1,128)S(1)}, u32[]{:S(2)}, u32[]{:S(2)}) %all-to-all-start) | async-done | bytes 64 | tf_op jit(solution)/shard_map/all_to_all | solution.py:206
  21.0 3.5 %all-to-all-start.1 = ((bf16[8,24,2048]{2,1,0:T(8,128)(2,1)}), bf16[8,24,2048]{2,1,0:T(8,128)(2,1)S(1)}, u32[]{:S(2)}, u32[]{:S(2)}) async-start(bf16[8,24,2048]{2,1,0:T(8,128)(2,1)} %pad_maximum_fusion.2), calls=%async_computation.1 | async-start | bytes 1572864 | tf_op jit(solution)/shard_map/all_to_all | solution.py:223
  24.9 12.3 %all-to-all-done.1 = bf16[8,24,2048]{2,1,0:T(8,128)(2,1)S(1)} async-done(((bf16[8,24,2048]{2,1,0:T(8,128)(2,1)}), bf16[8,24,2048]{2,1,0:T(8,128)(2,1)S(1)}, u32[]{:S(2)}, u32[]{:S(2)}) %all-to-all-start.1) | async-done | bytes 786464 | tf_op jit(solution)/shard_map/all_to_all | solution.py:223
  37.1 1.8 %scatter_custom_fusion = bf16[128,2048]{1,0:T(8,128)(2,1)S(1)} fusion(s32[192]{0:T(256)S(1)} %bitcast.228, bf16[192,2048]{1,0:T(8,128)(2,1)S(1)} %bitcast.219, bf16[]{:T(256)} %constant.157.clone.1), kind=kCustom, calls=%fused_computation.108 | custom fusion | bytes 524290 | tf_op jit(solution)/shard_map/scatter | solution.py:233
  39.6 2.1 %fusion.19 = bf16[128,1024]{1,0:T(8,128)(2,1)S(1)} fusion(bf16[128,1024]{1,0:T(8,128)(2,1)S(1)} %fusion.30, bf16[1024,1536]{1,0:T(8,128)(2,1)} %param.9), kind=kOutput, calls=%fused_computation.32 | convolution fusion | flops 268566528 | bytes 2621440 | tf_op jit(solution)/shard_map/dot_general | solution.py:247
  43.8 1.5 collective-permute-start
  45.3 6.2 %collective-permute-done.2 = bf16[1024,128]{0,1:T(8,128)(2,1)S(1)} collective-permute-done((bf16[1024,128]{0,1:T(8,128)(2,1)S(1)}, bf16[1024,128]{0,1:T(8,128)(2,1)S(1)}, u32[]{:S(2)}, u32[]{:S(2)}) %collective-permute-start.2) | collective-permute-done | bytes 262176 | tf_op jit(solution)/shard_map/ppermute | solution.py:179
  51.5 2.8 %collective-permute-done.1 = bf16[1024,128]{0,1:T(8,128)(2,1)S(1)} collective-permute-done((bf16[1024,128]{0,1:T(8,128)(2,1)S(1)}, bf16[1024,128]{0,1:T(8,128)(2,1)S(1)}, u32[]{:S(2)}, u32[]{:S(2)}) %collective-permute-start.1) | collective-permute-done | bytes 262176 | tf_op jit(solution)/shard_map/ppermute | solution.py:179
  55.9 1.5 convolution_convert_fusion.1
  59.9 1.8 %copy.71 = bf16[1024,128]{1,0:T(8,128)(2,1)} copy(bf16[1024,128]{0,1:T(8,128)(2,1)} %copy-done.16) | data formatting | bytes 524288 | tf_op jit(solution)/shard_map/ppermute | solution.py:179
  62.7 2.3 %copy.74 = bf16[4,1024,128]{2,1,0:T(8,128)(2,1)} copy(bf16[4,1024,128]{1,2,0:T(8,128)(2,1)} %collective-permute-done.3) | data formatting | bytes 2097152 | tf_op jit(solution)/shard_map/ppermute | solution.py:181
  69.2 1.6 %fusion.51 = (bf16[128,8,64]{0,2,1:T(8,128)(2,1)S(1)}, f32[8,128,64,1]{1,2,0,3:T(8,128)}) fusion(f32[128,8]{0,1:T(8,128)S(1)} %bitcast.225, f32[8,8,128,128]{2,3,1,0:T(8,128)S(1)} %get-tuple-element.30, f32[8,128]{1,0:T(8,128)S(1)} %get-tuple-element.29, bf16[8,8,2,64,128]{4,3,2,1,0:T(8,128)(2,1)S(1)} %constant_dynamic-update-slice_fusion), kind=kOutput, calls=%fused_computation.101 | convolution fusion | flops 137494528 | bytes 5644288 | tf_op jit(solution)/shard_map/ihqt,ihdt->ihqd/dot_general | solution.py:262
  73.4 3.9 %fusion.16 = bf16[8,8,64,128]{3,2,1,0:T(8,128)(2,1)S(1)} fusion(f32[8,8,128,128]{2,3,1,0:T(8,128)} %copy-done.2, f32[8,128]{1,0:T(8,128)S(1)} %log_add_fusion, bf16[8,128,64]{1,2,0:T(8,128)(2,1)S(1)} %bitcast.200), kind=kOutput, calls=%fused_computation.29 | convolution fusion | flops 137887744 | bytes 5378048 | tf_op jit(solution)/shard_map/ihqd,ihqt->ihdt/dot_general | solution.py:290
  77.3 2.6 %multiply_convert_fusion = bf16[8,8,128,128]{2,3,1,0:T(8,128)(2,1)S(1)} fusion(f32[8,8,128,128]{2,3,1,0:T(8,128)S(1)} %copy-done.3, f32[8,128]{1,0:T(8,128)S(1)} %multiply_reduce_fusion.4, f32[8,128]{1,0:T(8,128)S(1)} %log_add_fusion, bf16[8,8,2,64,128]{4,3,2,1,0:T(8,128)(2,1)} %copy-done.9, bf16[8,128,64]{1,2,0:T(8,128)(2,1)S(1)} %bitcast.201), kind=kOutput, calls=%fused_computation.5 | convolution fusion | flops 139460608 | bytes 7479296 | tf_op jit(solution)/shard_map/ihqd,ihdt->ihqt/dot_general | solution.py:293
  79.9 1.5 multiply_convert_fusion.1
  87.5 1.6 %fusion.72 = (bf16[4,1024,128]{2,1,0:T(8,128)(2,1)S(1)}, f32[4,1024,128]{2,1,0:T(8,128)S(1)}) fusion(bf16[4,1024,128]{2,1,0:T(8,128)(2,1)} %collective-permute-done.4, f32[4,8,2,64,128]{4,3,2,1,0:T(8,128)S(1)} %copy.87), kind=kLoop, calls=%fused_computation.168 | loop fusion | flops 1572864 | bytes 6291456 | tf_op jit(solution)/shard_map/convert.6
  89.2 1.9 %collective-permute-start.5 = (bf16[1024,128]{1,0:T(8,128)(2,1)S(1)}, bf16[1024,128]{1,0:T(8,128)(2,1)S(1)}, u32[]{:S(2)}, u32[]{:S(2)}) collective-permute-start(bf16[1024,128]{1,0:T(8,128)(2,1)S(1)} %get-tuple-element.12), channel_id=1, source_target_pairs={{0,8},{4,12},{8,0},{12,4},{16,24},{20,28},{24,16},{28,20},{1,9},{5... | collective-permute-start | bytes 786440 | tf_op jit(solution)/shard_map/ppermute | solution.py:191
  93.3 5.1 %collective-permute-done.5 = bf16[1024,128]{1,0:T(8,128)(2,1)S(1)} collective-permute-done((bf16[1024,128]{1,0:T(8,128)(2,1)S(1)}, bf16[1024,128]{1,0:T(8,128)(2,1)S(1)}, u32[]{:S(2)}, u32[]{:S(2)}) %collective-permute-start.5) | collective-permute-done | bytes 262176 | tf_op jit(solution)/shard_map/ppermute | solution.py:191
  98.4 6.1 %collective-permute-done.7 = bf16[1024,128]{1,0:T(8,128)(2,1)S(1)} collective-permute-done((bf16[1024,128]{1,0:T(8,128)(2,1)S(1)}, bf16[1024,128]{1,0:T(8,128)(2,1)S(1)}, u32[]{:S(2)}, u32[]{:S(2)}) %collective-permute-start.7) | collective-permute-done | bytes 262176 | tf_op jit(solution)/shard_map/ppermute | solution.py:191
  107.0 2.6 %copy-done.6 = f32[2,2,2,2,2,32,1536]{6,5,4,3,2,1,0:T(8,128)} copy-done((f32[2,2,2,2,2,32,1536]{6,5,4,3,2,1,0:T(8,128)}, f32[2,2,2,2,2,32,1536]{6,5,4,3,2,1,0:T(8,128)S(1)}, u32[]{:S(2)}) %copy-start.6) | copy-done | bytes 6291480
  113.7 1.5 collective-permute-done.18
  116.7 1.7 %collective-permute-start.19 = (bf16[2,2,2,16,1024]{4,3,2,1,0:T(8,128)(2,1)S(1)}, bf16[2,2,2,16,1024]{4,3,2,1,0:T(8,128)(2,1)S(1)}, u32[]{:S(2)}, u32[]{:S(2)}) collective-permute-start(bf16[2,2,2,16,1024]{4,3,2,1,0:T(8,128)(2,1)S(1)} %fusion.39), channel_id=1, source_target_pairs={{0,8},{4,20},{8,0},{12,28},{16,24},{20,4},{24,16},{28,12},{1,9},{5... | collective-permute-start | bytes 786440 | tf_op jit(solution)/shard_map/ppermute | solution.py:153
  118.4 2.9 %bitcast_add_fusion = f32[2,2,2,2,32,1536]{5,4,3,2,1,0:T(8,128)S(1)} fusion(bf16[2,2,2,2,32,1536]{5,4,3,2,1,0:T(8,128)(2,1)} %collective-permute-done.13, f32[2,2,2,2,2,32,1536]{6,5,4,3,2,1,0:T(8,128)} %copy-done.6, s32[]{:T(128)S(6)} %select_n.232), kind=kLoop, calls=%fused_computation.12 | loop fusion | flops 1572864 | bytes 7864324 | tf_op jit(solution)/shard_map/add | solution.py:157
  121.3 1.6 %copy-done.4 = f32[2,2,2,2,32,1536]{5,4,3,2,1,0:T(8,128)} copy-done((f32[2,2,2,2,32,1536]{5,4,3,2,1,0:T(8,128)}, f32[2,2,2,2,32,1536]{5,4,3,2,1,0:T(8,128)S(1)}, u32[]{:S(2)}) %copy-start.4) | copy-done | bytes 3145752
  125.4 3.1 %fusion.22 = f32[1024]{0:T(1024)S(1)} fusion(bf16[1024,1536]{1,0:T(8,128)(2,1)} %param.9, f32[128]{0:T(128)S(1)} %copy-done.29, f32[128]{0:T(128)S(1)} %broadcast_multiply_fusion.1, bf16[1024,128]{1,0:T(8,128)(2,1)S(1)} %fusion.38, bf16[512,128]{1,0:T(8,128)(2,1)S(1)} %bitcast.221, bf16[128,2048]{1,0:T(8,128)(2,1)S(1)} %scatter_custom_fusion), kind=kOutput, calls=%fused_computation.33 | convolution fusion | flops 404093952 | bytes 3806208 | tf_op jit(solution)/shard_map/ct,fc->tf/dot_general | solution.py:309
  129.8 7.2 %collective-permute-done.14 = bf16[2,2,2,32,1536]{4,3,2,1,0:T(8,128)(2,1)S(1)} collective-permute-done((bf16[2,2,2,32,1536]{4,3,2,1,0:T(8,128)(2,1)}, bf16[2,2,2,32,1536]{4,3,2,1,0:T(8,128)(2,1)S(1)}, u32[]{:S(2)}, u32[]{:S(2)}) %collective-permute-start.14) | collective-permute-done | bytes 786464 | tf_op jit(solution)/shard_map/ppermute | solution.py:155
  140.0 1.6 %collective-permute-start.21 = (bf16[2,16,1024]{2,1,0:T(8,128)(2,1)S(1)}, bf16[2,16,1024]{2,1,0:T(8,128)(2,1)S(1)}, u32[]{:S(2)}, u32[]{:S(2)}) collective-permute-start(bf16[2,16,1024]{2,1,0:T(8,128)(2,1)S(1)} %fusion.61), channel_id=1, source_target_pairs={{0,1},{1,0},{2,3},{3,2},{4,5},{5,4},{6,7},{7,6},{8,9},{9,8},{10,11... | collective-permute-start | bytes 196616 | tf_op jit(solution)/shard_map/ppermute | solution.py:164
  145.6 1.6 %collective-permute-start.16 = (bf16[2,32,1536]{2,1,0:T(8,128)(2,1)S(1)}, bf16[2,32,1536]{2,1,0:T(8,128)(2,1)S(1)}, u32[]{:S(2)}, u32[]{:S(2)}) collective-permute-start(bf16[2,32,1536]{2,1,0:T(8,128)(2,1)S(1)} %fusion.56), channel_id=1, source_target_pairs={{0,1},{1,0},{2,3},{3,2},{4,5},{5,4},{6,7},{7,6},{8,9},{9,8},{10,11... | collective-permute-start | bytes 589832 | tf_op jit(solution)/shard_map/ppermute | solution.py:166
  148.1 2.6 %collective-permute-start.22 = (bf16[16,1024]{1,0:T(8,128)(2,1)S(1)}, bf16[16,1024]{1,0:T(8,128)(2,1)S(1)}, u32[]{:S(2)}, u32[]{:S(2)}) collective-permute-start(bf16[16,1024]{1,0:T(8,128)(2,1)S(1)} %fusion.63), channel_id=1, source_target_pairs={{0,2},{1,3},{2,0},{3,1},{4,6},{5,7},{6,4},{7,5},{8,10},{9,11},{10,... | collective-permute-start | bytes 98312 | tf_op jit(solution)/shard_map/ppermute | solution.py:164
  151.6 2.6 %collective-permute-start.12 = (f32[1025]{0:T(1024)S(1)}, f32[1025]{0:T(1024)S(1)}, u32[]{:S(2)}, u32[]{:S(2)}) collective-permute-start(f32[1025]{0:T(1024)S(1)} %add.317), channel_id=1, source_target_pairs={{0,2},{1,3},{2,0},{3,1},{4,6},{5,7},{6,4},{7,5},{8,10},{9,11},{10,... | collective-permute-start | bytes 12308 | tf_op jit(solution)/shard_map/ppermute | solution.py:166
  158.2 1.7 %collective-permute-done.17 = bf16[32,1536]{1,0:T(8,128)(2,1)S(1)} collective-permute-done((bf16[32,1536]{1,0:T(8,128)(2,1)S(1)}, bf16[32,1536]{1,0:T(8,128)(2,1)S(1)}, u32[]{:S(2)}, u32[]{:S(2)}) %collective-permute-start.17) | collective-permute-done | bytes 98336 | tf_op jit(solution)/shard_map/ppermute | solution.py:166
  (180 shorter events, 58.5 us)
Async XLA Ops:
  0.6 15.1 %copy-start = (bf16[1,512,1024]{2,1,0:T(8,128)(2,1)S(1)}, bf16[1,512,1024]{2,1,0:T(8,128)(2,1)}, u32[]{:S(2)}) copy-start(bf16[1,512,1024]{2,1,0:T(8,128)(2,1)} %param.7) | copy-start | bytes 3145732
  0.6 16.1 %copy-start.7 = (bf16[1,512,1024]{2,1,0:T(8,128)(2,1)S(1)}, bf16[1,512,1024]{2,1,0:T(8,128)(2,1)}, u32[]{:S(2)}) copy-start(bf16[1,512,1024]{2,1,0:T(8,128)(2,1)} %param.6) | copy-start | bytes 3145732
  3.4 9.8 %all-to-all-start = ((s32[8,1,1]{2,1,0:T(1,128)}), s32[8,1,1]{2,1,0:T(1,128)S(1)}, u32[]{:S(2)}, u32[]{:S(2)}) async-start(s32[8,1,1]{2,1,0:T(1,128)} %broadcast_in_dim.47), calls=%async_computation | async-start | bytes 8192 | tf_op jit(solution)/shard_map/all_to_all | solution.py:206
  20.1 19.2 %copy-start.19 = (f32[1024]{0:T(1024)S(1)}, f32[1024]{0:T(1024)}, u32[]{:S(2)}) copy-start(f32[1024]{0:T(1024)} %param.11) | copy-start | bytes 12292
  21.0 16.1 %all-to-all-start.1 = ((bf16[8,24,2048]{2,1,0:T(8,128)(2,1)}), bf16[8,24,2048]{2,1,0:T(8,128)(2,1)S(1)}, u32[]{:S(2)}, u32[]{:S(2)}) async-start(bf16[8,24,2048]{2,1,0:T(8,128)(2,1)} %pad_maximum_fusion.2), calls=%async_computation.1 | async-start | bytes 1572864 | tf_op jit(solution)/shard_map/all_to_all | solution.py:223
  39.6 16.3 %copy-start.12 = (bf16[128,1024]{1,0:T(8,128)(2,1)}, bf16[128,1024]{1,0:T(8,128)(2,1)S(1)}, u32[]{:S(2)}) copy-start(bf16[128,1024]{1,0:T(8,128)(2,1)S(1)} %fusion.30) | copy-start | bytes 786436
  41.7 9.7 %collective-permute-start.2 = (bf16[1024,128]{0,1:T(8,128)(2,1)S(1)}, bf16[1024,128]{0,1:T(8,128)(2,1)S(1)}, u32[]{:S(2)}, u32[]{:S(2)}) collective-permute-start(bf16[1024,128]{0,1:T(8,128)(2,1)S(1)} %bitcast.213), channel_id=1, source_target_pairs={{0,24},{4,28},{8,16},{12,20},{16,8},{20,12},{24,0},{28,4},{1,25},{... | collective-permute-start | bytes 786440 | tf_op jit(solution)/shard_map/ppermute | solution.py:179
  42.4 11.9 %collective-permute-start.1 = (bf16[1024,128]{0,1:T(8,128)(2,1)S(1)}, bf16[1024,128]{0,1:T(8,128)(2,1)S(1)}, u32[]{:S(2)}, u32[]{:S(2)}) collective-permute-start(bf16[1024,128]{0,1:T(8,128)(2,1)S(1)} %bitcast.214), channel_id=1, source_target_pairs={{0,16},{4,20},{8,24},{12,28},{16,0},{20,4},{24,8},{28,12},{1,17},{... | collective-permute-start | bytes 786440 | tf_op jit(solution)/shard_map/ppermute | solution.py:179
  43.8 10.7 %collective-permute-start = (bf16[1024,128]{0,1:T(8,128)(2,1)S(1)}, bf16[1024,128]{0,1:T(8,128)(2,1)S(1)}, u32[]{:S(2)}, u32[]{:S(2)}) collective-permute-start(bf16[1024,128]{0,1:T(8,128)(2,1)S(1)} %bitcast.215), channel_id=1, source_target_pairs={{0,8},{4,12},{8,0},{12,4},{16,24},{20,28},{24,16},{28,20},{1,9},{5... | collective-permute-start | bytes 786440 | tf_op jit(solution)/shard_map/ppermute | solution.py:179
  55.6 7.1 %collective-permute-start.3 = (bf16[4,1024,128]{1,2,0:T(8,128)(2,1)}, bf16[4,1024,128]{1,2,0:T(8,128)(2,1)}, u32[]{:S(2)}, u32[]{:S(2)}) collective-permute-start(bf16[4,1024,128]{1,2,0:T(8,128)(2,1)} %pad_maximum_fusion), channel_id=1, source_target_pairs={{0,4},{4,0},{8,12},{12,8},{16,20},{20,16},{24,28},{28,24},{1,5},{5... | collective-permute-start | bytes 3145736 | tf_op jit(solution)/shard_map/ppermute | solution.py:181
  57.6 14.6 %copy-start.20 = (f32[128]{0:T(128)}, f32[128]{0:T(128)S(1)}, u32[]{:S(2)}) copy-start(f32[128]{0:T(128)S(1)} %add_rsqrt_fusion) | copy-start | bytes 1540
  84.4 3.1 %collective-permute-start.4 = (bf16[4,1024,128]{2,1,0:T(8,128)(2,1)}, bf16[4,1024,128]{2,1,0:T(8,128)(2,1)}, u32[]{:S(2)}, u32[]{:S(2)}) collective-permute-start(bf16[4,1024,128]{2,1,0:T(8,128)(2,1)} %bitcast.36), channel_id=1, source_target_pairs={{0,4},{4,0},{8,12},{12,8},{16,20},{20,16},{24,28},{28,24},{1,5},{5... | collective-permute-start | bytes 3145736 | tf_op jit(solution)/shard_map/ppermute | solution.py:187
  89.2 9.2 %collective-permute-start.5 = (bf16[1024,128]{1,0:T(8,128)(2,1)S(1)}, bf16[1024,128]{1,0:T(8,128)(2,1)S(1)}, u32[]{:S(2)}, u32[]{:S(2)}) collective-permute-start(bf16[1024,128]{1,0:T(8,128)(2,1)S(1)} %get-tuple-element.12), channel_id=1, source_target_pairs={{0,8},{4,12},{8,0},{12,4},{16,24},{20,28},{24,16},{28,20},{1,9},{5... | collective-permute-start | bytes 786440 | tf_op jit(solution)/shard_map/ppermute | solution.py:191
  91.1 13.3 %collective-permute-start.7 = (bf16[1024,128]{1,0:T(8,128)(2,1)S(1)}, bf16[1024,128]{1,0:T(8,128)(2,1)S(1)}, u32[]{:S(2)}, u32[]{:S(2)}) collective-permute-start(bf16[1024,128]{1,0:T(8,128)(2,1)S(1)} %get-tuple-element.13), channel_id=1, source_target_pairs={{0,24},{4,28},{8,16},{12,20},{16,8},{20,12},{24,0},{28,4},{1,25},{... | collective-permute-start | bytes 786440 | tf_op jit(solution)/shard_map/ppermute | solution.py:191
  92.2 13.8 %copy-start.17 = (bf16[128,1024]{0,1:T(8,128)(2,1)S(1)}, bf16[128,1024]{0,1:T(8,128)(2,1)}, u32[]{:S(2)}) copy-start(bf16[128,1024]{0,1:T(8,128)(2,1)} %copy.89) | copy-start | bytes 786436
  92.2 13.7 %collective-permute-start.6 = (bf16[1024,128]{1,0:T(8,128)(2,1)S(1)}, bf16[1024,128]{1,0:T(8,128)(2,1)S(1)}, u32[]{:S(2)}, u32[]{:S(2)}) collective-permute-start(bf16[1024,128]{1,0:T(8,128)(2,1)S(1)} %get-tuple-element.14), channel_id=1, source_target_pairs={{0,16},{4,20},{8,24},{12,28},{16,0},{20,4},{24,8},{28,12},{1,17},{... | collective-permute-start | bytes 786440 | tf_op jit(solution)/shard_map/ppermute | solution.py:191
  111.1 7.3 %collective-permute-start.13 = (bf16[2,2,2,2,32,1536]{5,4,3,2,1,0:T(8,128)(2,1)}, bf16[2,2,2,2,32,1536]{5,4,3,2,1,0:T(8,128)(2,1)}, u32[]{:S(2)}, u32[]{:S(2)}) collective-permute-start(bf16[2,2,2,2,32,1536]{5,4,3,2,1,0:T(8,128)(2,1)} %fusion.13), channel_id=1, source_target_pairs={{0,4},{4,0},{8,12},{12,8},{16,20},{20,16},{24,28},{28,24},{1,5},{5... | collective-permute-start | bytes 4718600 | tf_op jit(solution)/shard_map/ppermute | solution.py:155
  113.1 2.1 %collective-permute-start.18 = (bf16[2,2,2,2,16,1024]{5,4,3,2,1,0:T(8,128)(2,1)S(1)}, bf16[2,2,2,2,16,1024]{5,4,3,2,1,0:T(8,128)(2,1)S(1)}, u32[]{:S(2)}, u32[]{:S(2)}) collective-permute-start(bf16[2,2,2,2,16,1024]{5,4,3,2,1,0:T(8,128)(2,1)S(1)} %fusion.34), channel_id=1, source_target_pairs={{0,4},{4,0},{8,12},{12,8},{16,20},{20,16},{24,28},{28,24},{1,5},{5... | collective-permute-start | bytes 1572872 | tf_op jit(solution)/shard_map/ppermute | solution.py:153
  116.7 7.7 %collective-permute-start.19 = (bf16[2,2,2,16,1024]{4,3,2,1,0:T(8,128)(2,1)S(1)}, bf16[2,2,2,16,1024]{4,3,2,1,0:T(8,128)(2,1)S(1)}, u32[]{:S(2)}, u32[]{:S(2)}) collective-permute-start(bf16[2,2,2,16,1024]{4,3,2,1,0:T(8,128)(2,1)S(1)} %fusion.39), channel_id=1, source_target_pairs={{0,8},{4,20},{8,0},{12,28},{16,24},{20,4},{24,16},{28,12},{1,9},{5... | collective-permute-start | bytes 786440 | tf_op jit(solution)/shard_map/ppermute | solution.py:153
  124.0 13.0 %collective-permute-start.14 = (bf16[2,2,2,32,1536]{4,3,2,1,0:T(8,128)(2,1)}, bf16[2,2,2,32,1536]{4,3,2,1,0:T(8,128)(2,1)S(1)}, u32[]{:S(2)}, u32[]{:S(2)}) collective-permute-start(bf16[2,2,2,32,1536]{4,3,2,1,0:T(8,128)(2,1)} %fusion.14), channel_id=1, source_target_pairs={{0,8},{4,20},{8,0},{12,28},{16,24},{20,4},{24,16},{28,12},{1,9},{5... | collective-permute-start | bytes 2359304 | tf_op jit(solution)/shard_map/ppermute | solution.py:155
  124.5 13.8 %collective-permute-start.20 = (bf16[2,2,16,1024]{3,2,1,0:T(8,128)(2,1)S(1)}, bf16[2,2,16,1024]{3,2,1,0:T(8,128)(2,1)S(1)}, u32[]{:S(2)}, u32[]{:S(2)}) collective-permute-start(bf16[2,2,16,1024]{3,2,1,0:T(8,128)(2,1)S(1)} %fusion.57), channel_id=1, source_target_pairs={{0,16},{4,12},{8,24},{12,4},{16,0},{20,28},{24,8},{28,20},{1,17},{... | collective-permute-start | bytes 393224 | tf_op jit(solution)/shard_map/ppermute | solution.py:153
  129.1 9.1 %collective-permute-start.8 = (f32[1025]{0:T(1024)S(1)}, f32[1025]{0:T(1024)S(1)}, u32[]{:S(2)}, u32[]{:S(2)}) collective-permute-start(f32[1025]{0:T(1024)S(1)} %pad_maximum_fusion.6), channel_id=1, source_target_pairs={{0,4},{4,0},{8,12},{12,8},{16,20},{20,16},{24,28},{28,24},{1,5},{5... | collective-permute-start | bytes 12308 | tf_op jit(solution)/shard_map/ppermute | solution.py:155
  137.5 7.9 %collective-permute-start.15 = (bf16[2,2,32,1536]{3,2,1,0:T(8,128)(2,1)S(1)}, bf16[2,2,32,1536]{3,2,1,0:T(8,128)(2,1)S(1)}, u32[]{:S(2)}, u32[]{:S(2)}) collective-permute-start(bf16[2,2,32,1536]{3,2,1,0:T(8,128)(2,1)S(1)} %fusion.45), channel_id=1, source_target_pairs={{0,16},{4,12},{8,24},{12,4},{16,0},{20,28},{24,8},{28,20},{1,17},{... | collective-permute-start | bytes 1179656 | tf_op jit(solution)/shard_map/ppermute | solution.py:155
  138.9 3.9 %collective-permute-start.9 = (f32[1025]{0:T(1024)S(1)}, f32[1025]{0:T(1024)S(1)}, u32[]{:S(2)}, u32[]{:S(2)}) collective-permute-start(f32[1025]{0:T(1024)S(1)} %fusion.67), channel_id=1, source_target_pairs={{0,8},{4,20},{8,0},{12,28},{16,24},{20,4},{24,16},{28,12},{1,9},{5... | collective-permute-start | bytes 12308 | tf_op jit(solution)/shard_map/ppermute | solution.py:155
  140.0 7.3 %collective-permute-start.21 = (bf16[2,16,1024]{2,1,0:T(8,128)(2,1)S(1)}, bf16[2,16,1024]{2,1,0:T(8,128)(2,1)S(1)}, u32[]{:S(2)}, u32[]{:S(2)}) collective-permute-start(bf16[2,16,1024]{2,1,0:T(8,128)(2,1)S(1)} %fusion.61), channel_id=1, source_target_pairs={{0,1},{1,0},{2,3},{3,2},{4,5},{5,4},{6,7},{7,6},{8,9},{9,8},{10,11... | collective-permute-start | bytes 196616 | tf_op jit(solution)/shard_map/ppermute | solution.py:164
  142.8 4.5 %collective-permute-start.10 = (f32[1025]{0:T(1024)S(1)}, f32[1025]{0:T(1024)S(1)}, u32[]{:S(2)}, u32[]{:S(2)}) collective-permute-start(f32[1025]{0:T(1024)S(1)} %add.315), channel_id=1, source_target_pairs={{0,16},{4,12},{8,24},{12,4},{16,0},{20,28},{24,8},{28,20},{1,17},{... | collective-permute-start | bytes 12308 | tf_op jit(solution)/shard_map/ppermute | solution.py:155
  145.4 15.1 %copy-start.1 = (bf16[1,512,1024]{2,1,0:T(8,128)(2,1)S(1)}, bf16[1,512,1024]{2,1,0:T(8,128)(2,1)}, u32[]{:S(2)}) copy-start(bf16[1,512,1024]{2,1,0:T(8,128)(2,1)} %param.7) | copy-start | bytes 3145732
  145.6 8.5 %collective-permute-start.16 = (bf16[2,32,1536]{2,1,0:T(8,128)(2,1)S(1)}, bf16[2,32,1536]{2,1,0:T(8,128)(2,1)S(1)}, u32[]{:S(2)}, u32[]{:S(2)}) collective-permute-start(bf16[2,32,1536]{2,1,0:T(8,128)(2,1)S(1)} %fusion.56), channel_id=1, source_target_pairs={{0,1},{1,0},{2,3},{3,2},{4,5},{5,4},{6,7},{7,6},{8,9},{9,8},{10,11... | collective-permute-start | bytes 589832 | tf_op jit(solution)/shard_map/ppermute | solution.py:166
  147.3 4.2 %collective-permute-start.11 = (f32[1025]{0:T(1024)S(1)}, f32[1025]{0:T(1024)S(1)}, u32[]{:S(2)}, u32[]{:S(2)}) collective-permute-start(f32[1025]{0:T(1024)S(1)} %add.316), channel_id=1, source_target_pairs={{0,1},{1,0},{2,3},{3,2},{4,5},{5,4},{6,7},{7,6},{8,9},{9,8},{10,11... | collective-permute-start | bytes 12308 | tf_op jit(solution)/shard_map/ppermute | solution.py:166
  148.1 6.6 %collective-permute-start.22 = (bf16[16,1024]{1,0:T(8,128)(2,1)S(1)}, bf16[16,1024]{1,0:T(8,128)(2,1)S(1)}, u32[]{:S(2)}, u32[]{:S(2)}) collective-permute-start(bf16[16,1024]{1,0:T(8,128)(2,1)S(1)} %fusion.63), channel_id=1, source_target_pairs={{0,2},{1,3},{2,0},{3,1},{4,6},{5,7},{6,4},{7,5},{8,10},{9,11},{10,... | collective-permute-start | bytes 98312 | tf_op jit(solution)/shard_map/ppermute | solution.py:164
  151.6 4.8 %collective-permute-start.12 = (f32[1025]{0:T(1024)S(1)}, f32[1025]{0:T(1024)S(1)}, u32[]{:S(2)}, u32[]{:S(2)}) collective-permute-start(f32[1025]{0:T(1024)S(1)} %add.317), channel_id=1, source_target_pairs={{0,2},{1,3},{2,0},{3,1},{4,6},{5,7},{6,4},{7,5},{8,10},{9,11},{10,... | collective-permute-start | bytes 12308 | tf_op jit(solution)/shard_map/ppermute | solution.py:166
  154.2 5.6 %collective-permute-start.17 = (bf16[32,1536]{1,0:T(8,128)(2,1)S(1)}, bf16[32,1536]{1,0:T(8,128)(2,1)S(1)}, u32[]{:S(2)}, u32[]{:S(2)}) collective-permute-start(bf16[32,1536]{1,0:T(8,128)(2,1)S(1)} %fusion.60), channel_id=1, source_target_pairs={{0,2},{1,3},{2,0},{3,1},{4,6},{5,7},{6,4},{7,5},{8,10},{9,11},{10,... | collective-permute-start | bytes 294920 | tf_op jit(solution)/shard_map/ppermute | solution.py:166
  (23 other events, 55.9 us)

commit v17 on v16

--- a/solution.py
+++ b/solution.py
@@ -176,16 +176,16 @@
 
 def gather_blocks(block):
     half = lax.axis_size("seq") // 2
-    same_core = [block] + [lax.ppermute(block, "seq", xor_pairs(2 * k)) for k in range(1, half)]
-    group = jnp.stack(same_core)
-    other = lax.ppermute(group, "seq", xor_pairs(1))
-    return jnp.concatenate([group, other], axis=0)
+    early = lax.ppermute(block, "seq", xor_pairs(1))
+    received = [lax.ppermute(block, "seq", xor_pairs(2 * k)) for k in range(1, half)]
+    late = lax.ppermute(jnp.stack(received), "seq", xor_pairs(1))
+    return jnp.concatenate([jnp.stack([block] + received), early[None], late], axis=0)
 
 
 def return_blocks(own_parts, other_parts):
     half = lax.axis_size("seq") // 2
     got = lax.ppermute(other_parts, "seq", xor_pairs(1))
-    summed = own_parts.astype(jnp.bfloat16).astype(jnp.float32) + got.astype(jnp.float32)
+    summed = own_parts + got.astype(jnp.float32)
     accum = summed[0]
     for k in range(1, half):
         sent = lax.ppermute(summed[k].astype(jnp.bfloat16), "seq", xor_pairs(2 * k))

time: 162 us -> 163 us (level)
  local copies, waits for them, and re-layouts: 32 us -> 37.5 us
  waiting for transfers between devices: 53 us -> 49.8 us
    unnamed x65 -> x74, local copies, waits for them, and re-layouts: 9.2 us -> 11.9 us
    ppermute x3, waiting for transfers between devices: 9.21 us -> 6.61 us  [gather_blocks(): lax.ppermute(block, 'seq', xor_pairs(2 * k))]
    ppermute x1 -> x2, local copies, waits for them, and re-layouts: 2.27 us -> 4.1 us  [the longest x1 2.33 us: gather_blocks(): late = lax.ppermute(jnp.stack(received), 'seq', xor_pairs(1))]
    another operation x4 -> x5, other arithmetic: 3.08 us -> 3.26 us
  transfers between devices with their start and end apart: 25 -> 26, of which waited for: 16 -> 15; matrix products, arithmetic and copies ran while one was open for 15% -> 18% of each run, Pallas kernels for 0% -> 0%
where the time goes in v17:
time: 163 us; the launch traced here: 162 us
  waiting for transfers between devices  49.8 us (31%)
  local copies, waits for them, and re-layouts  37.5 us (23%)
  starting transfers between devices  32.9 us (20%)
  matrix products  20.2 us (12%)
  other arithmetic  18.9 us (12%)
  between operations  3.19 us (2%)
    all_to_all x1, waiting for transfers between devices, per_device(): lax.all_to_all(jnp.concatenate([send_tokens, send_target], axis=2), 'seq'...  12.3 us
    ppermute x3, waiting for transfers between devices, return_blocks(): sent = lax.ppermute(summed[k].astype(jnp.bfloat16), 'seq', xor_pairs(2 * k))  12.3 us
    unnamed x74, local copies, waits for them, and re-layouts  11.9 us
    ppermute x6, waiting for transfers between devices, halving_scatter(): lax.ppermute((give.astype(jnp.bfloat16), small), 'seq', pairs)  9.49 us
    ppermute x3, waiting for transfers between devices, gather_blocks(): lax.ppermute(block, 'seq', xor_pairs(2 * k))  6.61 us
    ppermute x4, starting transfers between devices, halving_scatter(): lax.ppermute((give.astype(jnp.bfloat16), small), 'clip', pairs)  5.31 us
    all_to_all x1, starting transfers between devices, per_device(): lax.all_to_all(jnp.broadcast_to(kept_count.reshape(1, 1), (shards, 1)), '...  5.17 us
    add x9, other arithmetic, halving_scatter(): data = keep + got.astype(jnp.float32)  5.02 us
  transfers between devices with their start and end apart: 26, of which 15 were waited for; matrix products, arithmetic and copies ran while one was open for 18% of the time, Pallas kernels for 0%

profile of v17, /device:TPU:0, one launch (start us, length us, event | category | flops | bytes accessed | tf_op | source)
XLA Modules:
  0.0 162.4 jit_solution(3813308408968504862)
XLA Ops:
  3.4 5.2 %all-to-all-start = ((s32[8,1,1]{2,1,0:T(1,128)}), s32[8,1,1]{2,1,0:T(1,128)S(1)}, u32[]{:S(2)}, u32[]{:S(2)}) async-start(s32[8,1,1]{2,1,0:T(1,128)} %broadcast_in_dim.47), calls=%async_computation | async-start | bytes 8192 | tf_op jit(solution)/shard_map/all_to_all | solution.py:206
  9.2 3.9 %all-to-all-done = s32[8,1,1]{2,1,0:T(1,128)S(1)} async-done(((s32[8,1,1]{2,1,0:T(1,128)}), s32[8,1,1]{2,1,0:T(1,128)S(1)}, u32[]{:S(2)}, u32[]{:S(2)}) %all-to-all-start) | async-done | bytes 64 | tf_op jit(solution)/shard_map/all_to_all | solution.py:206
  21.1 3.5 %all-to-all-start.1 = ((bf16[8,24,2048]{2,1,0:T(8,128)(2,1)}), bf16[8,24,2048]{2,1,0:T(8,128)(2,1)S(1)}, u32[]{:S(2)}, u32[]{:S(2)}) async-start(bf16[8,24,2048]{2,1,0:T(8,128)(2,1)} %pad_maximum_fusion.2), calls=%async_computation.1 | async-start | bytes 1572864 | tf_op jit(solution)/shard_map/all_to_all | solution.py:223
  24.9 12.3 %all-to-all-done.1 = bf16[8,24,2048]{2,1,0:T(8,128)(2,1)S(1)} async-done(((bf16[8,24,2048]{2,1,0:T(8,128)(2,1)}), bf16[8,24,2048]{2,1,0:T(8,128)(2,1)S(1)}, u32[]{:S(2)}, u32[]{:S(2)}) %all-to-all-start.1) | async-done | bytes 786464 | tf_op jit(solution)/shard_map/all_to_all | solution.py:223
  37.1 2.0 %scatter_custom_fusion = bf16[128,2048]{1,0:T(8,128)(2,1)S(1)} fusion(s32[192]{0:T(256)S(1)} %bitcast.224, bf16[192,2048]{1,0:T(8,128)(2,1)S(1)} %bitcast.215, bf16[]{:T(256)} %constant.157.clone.1), kind=kCustom, calls=%fused_computation.110 | custom fusion | bytes 524290 | tf_op jit(solution)/shard_map/scatter | solution.py:233
  39.8 2.8 %fusion.20 = bf16[1024,128]{0,1:T(8,128)(2,1)} fusion(bf16[128,1024]{1,0:T(8,128)(2,1)S(1)} %fusion.30, bf16[1024,1536]{1,0:T(8,128)(2,1)} %param.9), kind=kOutput, calls=%fused_computation.34 | convolution fusion | flops 268566528 | bytes 2621440 | tf_op jit(solution)/shard_map/dot_general | solution.py:247
  44.6 1.5 collective-permute-start
  47.3 1.5 convolution_convert_fusion.1
  48.9 3.6 %collective-permute-done.2 = bf16[1024,128]{0,1:T(8,128)(2,1)S(1)} collective-permute-done((bf16[1024,128]{0,1:T(8,128)(2,1)}, bf16[1024,128]{0,1:T(8,128)(2,1)S(1)}, u32[]{:S(2)}, u32[]{:S(2)}) %collective-permute-start.2) | collective-permute-done | bytes 262176 | tf_op jit(solution)/shard_map/ppermute | solution.py:180
  52.5 2.8 %collective-permute-done.1 = bf16[1024,128]{0,1:T(8,128)(2,1)S(1)} collective-permute-done((bf16[1024,128]{0,1:T(8,128)(2,1)}, bf16[1024,128]{0,1:T(8,128)(2,1)S(1)}, u32[]{:S(2)}, u32[]{:S(2)}) %collective-permute-start.1) | collective-permute-done | bytes 262176 | tf_op jit(solution)/shard_map/ppermute | solution.py:180
  59.0 1.8 %copy.76 = bf16[1024,128]{1,0:T(8,128)(2,1)} copy(bf16[1024,128]{0,1:T(8,128)(2,1)} %copy-done.20) | data formatting | bytes 524288 | tf_op jit(solution)/shard_map/ppermute | solution.py:180
  60.8 1.8 %copy.79 = bf16[1024,128]{1,0:T(8,128)(2,1)} copy(bf16[1024,128]{0,1:T(8,128)(2,1)} %collective-permute-done.3) | data formatting | bytes 524288 | tf_op jit(solution)/shard_map/ppermute | solution.py:179
  64.6 2.3 %copy.80 = bf16[3,1024,128]{2,1,0:T(8,128)(2,1)} copy(bf16[3,1024,128]{1,2,0:T(8,128)(2,1)} %collective-permute-done.4) | data formatting | bytes 1572864 | tf_op jit(solution)/shard_map/ppermute | solution.py:181
  71.0 1.6 fusion.53
  75.2 3.9 %fusion.3 = f32[8,8,64,128]{3,2,1,0:T(8,128)S(1)} fusion(f32[8,8,128,128]{2,3,1,0:T(8,128)} %copy-done.2, f32[8,128]{1,0:T(8,128)S(1)} %log_add_fusion, bf16[8,128,64]{1,2,0:T(8,128)(2,1)S(1)} %bitcast.200), kind=kOutput, calls=%fused_computation.14 | convolution fusion | flops 137363456 | bytes 6426624 | tf_op jit(solution)/shard_map/ihqd,ihqt->ihdt/dot_general | solution.py:290
  80.7 1.5 convolution_multiply_fusion
  88.5 1.7 %fusion.74 = (bf16[4,1024,128]{2,1,0:T(8,128)(2,1)S(1)}, f32[4,1024,128]{2,1,0:T(8,128)S(1)}) fusion(bf16[4,1024,128]{2,1,0:T(8,128)(2,1)} %collective-permute-done.5, f32[4,8,2,64,128]{4,3,2,1,0:T(8,128)S(1)} %copy.94), kind=kLoop, calls=%fused_computation.171 | loop fusion | flops 1572864 | bytes 6291456 | tf_op jit(solution)/shard_map/convert.5
  90.2 1.9 %collective-permute-start.6 = (bf16[1024,128]{1,0:T(8,128)(2,1)S(1)}, bf16[1024,128]{1,0:T(8,128)(2,1)S(1)}, u32[]{:S(2)}, u32[]{:S(2)}) collective-permute-start(bf16[1024,128]{1,0:T(8,128)(2,1)S(1)} %get-tuple-element.12), channel_id=1, source_target_pairs={{0,8},{4,12},{8,0},{12,4},{16,24},{20,28},{24,16},{28,20},{1,9},{5... | collective-permute-start | bytes 786440 | tf_op jit(solution)/shard_map/ppermute | solution.py:191
  94.3 5.1 %collective-permute-done.6 = bf16[1024,128]{1,0:T(8,128)(2,1)S(1)} collective-permute-done((bf16[1024,128]{1,0:T(8,128)(2,1)S(1)}, bf16[1024,128]{1,0:T(8,128)(2,1)S(1)}, u32[]{:S(2)}, u32[]{:S(2)}) %collective-permute-start.6) | collective-permute-done | bytes 262176 | tf_op jit(solution)/shard_map/ppermute | solution.py:191
  99.4 5.7 %collective-permute-done.8 = bf16[1024,128]{1,0:T(8,128)(2,1)S(1)} collective-permute-done((bf16[1024,128]{1,0:T(8,128)(2,1)S(1)}, bf16[1024,128]{1,0:T(8,128)(2,1)S(1)}, u32[]{:S(2)}, u32[]{:S(2)}) %collective-permute-start.8) | collective-permute-done | bytes 262176 | tf_op jit(solution)/shard_map/ppermute | solution.py:191
  108.0 2.6 %copy-done.6 = f32[2,2,2,2,2,32,1536]{6,5,4,3,2,1,0:T(8,128)} copy-done((f32[2,2,2,2,2,32,1536]{6,5,4,3,2,1,0:T(8,128)}, f32[2,2,2,2,2,32,1536]{6,5,4,3,2,1,0:T(8,128)S(1)}, u32[]{:S(2)}) %copy-start.6) | copy-done | bytes 6291480
  114.6 1.5 collective-permute-done.19
  117.6 1.7 %collective-permute-start.20 = (bf16[2,2,2,16,1024]{4,3,2,1,0:T(8,128)(2,1)S(1)}, bf16[2,2,2,16,1024]{4,3,2,1,0:T(8,128)(2,1)S(1)}, u32[]{:S(2)}, u32[]{:S(2)}) collective-permute-start(bf16[2,2,2,16,1024]{4,3,2,1,0:T(8,128)(2,1)S(1)} %fusion.41), channel_id=1, source_target_pairs={{0,8},{4,20},{8,0},{12,28},{16,24},{20,4},{24,16},{28,12},{1,9},{5... | collective-permute-start | bytes 786440 | tf_op jit(solution)/shard_map/ppermute | solution.py:153
  119.3 2.9 %bitcast_add_fusion = f32[2,2,2,2,32,1536]{5,4,3,2,1,0:T(8,128)S(1)} fusion(bf16[2,2,2,2,32,1536]{5,4,3,2,1,0:T(8,128)(2,1)} %collective-permute-done.14, f32[2,2,2,2,2,32,1536]{6,5,4,3,2,1,0:T(8,128)} %copy-done.6, s32[]{:T(128)S(6)} %select_n.232), kind=kLoop, calls=%fused_computation.12 | loop fusion | flops 1572864 | bytes 7864324 | tf_op jit(solution)/shard_map/add | solution.py:157
  122.2 1.6 %copy-done.4 = f32[2,2,2,2,32,1536]{5,4,3,2,1,0:T(8,128)} copy-done((f32[2,2,2,2,32,1536]{5,4,3,2,1,0:T(8,128)}, f32[2,2,2,2,32,1536]{5,4,3,2,1,0:T(8,128)S(1)}, u32[]{:S(2)}) %copy-start.4) | copy-done | bytes 3145752
  126.1 3.3 %fusion.19 = f32[1024]{0:T(1024)S(1)} fusion(bf16[1024,1536]{1,0:T(8,128)(2,1)} %param.9, f32[128]{0:T(128)S(1)} %copy-done.33, f32[128]{0:T(128)S(1)} %broadcast_multiply_fusion.1, bf16[1024,128]{1,0:T(8,128)(2,1)S(1)} %fusion.40, bf16[512,128]{1,0:T(8,128)(2,1)S(1)} %bitcast.217, bf16[128,2048]{1,0:T(8,128)(2,1)S(1)} %scatter_custom_fusion), kind=kOutput, calls=%fused_computation.33 | convolution fusion | flops 404093952 | bytes 3806208 | tf_op jit(solution)/shard_map/ct,fc->tf/dot_general | solution.py:309
  130.5 7.2 %collective-permute-done.15 = bf16[2,2,2,32,1536]{4,3,2,1,0:T(8,128)(2,1)S(1)} collective-permute-done((bf16[2,2,2,32,1536]{4,3,2,1,0:T(8,128)(2,1)}, bf16[2,2,2,32,1536]{4,3,2,1,0:T(8,128)(2,1)S(1)}, u32[]{:S(2)}, u32[]{:S(2)}) %collective-permute-start.15) | collective-permute-done | bytes 786464 | tf_op jit(solution)/shard_map/ppermute | solution.py:155
  140.8 1.6 %collective-permute-start.22 = (bf16[2,16,1024]{2,1,0:T(8,128)(2,1)S(1)}, bf16[2,16,1024]{2,1,0:T(8,128)(2,1)S(1)}, u32[]{:S(2)}, u32[]{:S(2)}) collective-permute-start(bf16[2,16,1024]{2,1,0:T(8,128)(2,1)S(1)} %fusion.63), channel_id=1, source_target_pairs={{0,1},{1,0},{2,3},{3,2},{4,5},{5,4},{6,7},{7,6},{8,9},{9,8},{10,11... | collective-permute-start | bytes 196616 | tf_op jit(solution)/shard_map/ppermute | solution.py:164
  146.4 1.6 %collective-permute-start.17 = (bf16[2,32,1536]{2,1,0:T(8,128)(2,1)S(1)}, bf16[2,32,1536]{2,1,0:T(8,128)(2,1)S(1)}, u32[]{:S(2)}, u32[]{:S(2)}) collective-permute-start(bf16[2,32,1536]{2,1,0:T(8,128)(2,1)S(1)} %fusion.58), channel_id=1, source_target_pairs={{0,1},{1,0},{2,3},{3,2},{4,5},{5,4},{6,7},{7,6},{8,9},{9,8},{10,11... | collective-permute-start | bytes 589832 | tf_op jit(solution)/shard_map/ppermute | solution.py:166
  148.7 2.6 %collective-permute-start.23 = (bf16[16,1024]{1,0:T(8,128)(2,1)S(1)}, bf16[16,1024]{1,0:T(8,128)(2,1)S(1)}, u32[]{:S(2)}, u32[]{:S(2)}) collective-permute-start(bf16[16,1024]{1,0:T(8,128)(2,1)S(1)} %fusion.65), channel_id=1, source_target_pairs={{0,2},{1,3},{2,0},{3,1},{4,6},{5,7},{6,4},{7,5},{8,10},{9,11},{10,... | collective-permute-start | bytes 98312 | tf_op jit(solution)/shard_map/ppermute | solution.py:164
  152.5 2.4 %collective-permute-start.13 = (f32[1025]{0:T(1024)S(1)}, f32[1025]{0:T(1024)S(1)}, u32[]{:S(2)}, u32[]{:S(2)}) collective-permute-start(f32[1025]{0:T(1024)S(1)} %add.317), channel_id=1, source_target_pairs={{0,2},{1,3},{2,0},{3,1},{4,6},{5,7},{6,4},{7,5},{8,10},{9,11},{10,... | collective-permute-start | bytes 12308 | tf_op jit(solution)/shard_map/ppermute | solution.py:166
  159.1 1.5 collective-permute-done.18
  (194 shorter events, 62.0 us)
Async XLA Ops:
  0.6 15.1 %copy-start = (bf16[1,512,1024]{2,1,0:T(8,128)(2,1)S(1)}, bf16[1,512,1024]{2,1,0:T(8,128)(2,1)}, u32[]{:S(2)}) copy-start(bf16[1,512,1024]{2,1,0:T(8,128)(2,1)} %param.7) | copy-start | bytes 3145732
  0.6 16.1 %copy-start.7 = (bf16[1,512,1024]{2,1,0:T(8,128)(2,1)S(1)}, bf16[1,512,1024]{2,1,0:T(8,128)(2,1)}, u32[]{:S(2)}) copy-start(bf16[1,512,1024]{2,1,0:T(8,128)(2,1)} %param.6) | copy-start | bytes 3145732
  3.4 9.8 %all-to-all-start = ((s32[8,1,1]{2,1,0:T(1,128)}), s32[8,1,1]{2,1,0:T(1,128)S(1)}, u32[]{:S(2)}, u32[]{:S(2)}) async-start(s32[8,1,1]{2,1,0:T(1,128)} %broadcast_in_dim.47), calls=%async_computation | async-start | bytes 8192 | tf_op jit(solution)/shard_map/all_to_all | solution.py:206
  20.1 19.4 %copy-start.23 = (f32[1024]{0:T(1024)S(1)}, f32[1024]{0:T(1024)}, u32[]{:S(2)}) copy-start(f32[1024]{0:T(1024)} %param.11) | copy-start | bytes 12292
  21.1 16.1 %all-to-all-start.1 = ((bf16[8,24,2048]{2,1,0:T(8,128)(2,1)}), bf16[8,24,2048]{2,1,0:T(8,128)(2,1)S(1)}, u32[]{:S(2)}, u32[]{:S(2)}) async-start(bf16[8,24,2048]{2,1,0:T(8,128)(2,1)} %pad_maximum_fusion.2), calls=%async_computation.1 | async-start | bytes 1572864 | tf_op jit(solution)/shard_map/all_to_all | solution.py:223
  42.6 9.9 %collective-permute-start.2 = (bf16[1024,128]{0,1:T(8,128)(2,1)}, bf16[1024,128]{0,1:T(8,128)(2,1)S(1)}, u32[]{:S(2)}, u32[]{:S(2)}) collective-permute-start(bf16[1024,128]{0,1:T(8,128)(2,1)} %fusion.20), channel_id=1, source_target_pairs={{0,24},{4,28},{8,16},{12,20},{16,8},{20,12},{24,0},{28,4},{1,25},{... | collective-permute-start | bytes 786440 | tf_op jit(solution)/shard_map/ppermute | solution.py:180
  43.2 12.1 %collective-permute-start.1 = (bf16[1024,128]{0,1:T(8,128)(2,1)}, bf16[1024,128]{0,1:T(8,128)(2,1)S(1)}, u32[]{:S(2)}, u32[]{:S(2)}) collective-permute-start(bf16[1024,128]{0,1:T(8,128)(2,1)} %fusion.20), channel_id=1, source_target_pairs={{0,16},{4,20},{8,24},{12,28},{16,0},{20,4},{24,8},{28,12},{1,17},{... | collective-permute-start | bytes 786440 | tf_op jit(solution)/shard_map/ppermute | solution.py:180
  44.6 10.9 %collective-permute-start = (bf16[1024,128]{0,1:T(8,128)(2,1)}, bf16[1024,128]{0,1:T(8,128)(2,1)S(1)}, u32[]{:S(2)}, u32[]{:S(2)}) collective-permute-start(bf16[1024,128]{0,1:T(8,128)(2,1)} %fusion.20), channel_id=1, source_target_pairs={{0,8},{4,12},{8,0},{12,4},{16,24},{20,28},{24,16},{28,20},{1,9},{5... | collective-permute-start | bytes 786440 | tf_op jit(solution)/shard_map/ppermute | solution.py:180
  47.3 13.5 %collective-permute-start.3 = (bf16[1024,128]{0,1:T(8,128)(2,1)}, bf16[1024,128]{0,1:T(8,128)(2,1)}, u32[]{:S(2)}, u32[]{:S(2)}) collective-permute-start(bf16[1024,128]{0,1:T(8,128)(2,1)} %fusion.20), channel_id=1, source_target_pairs={{0,4},{4,0},{8,12},{12,8},{16,20},{20,16},{24,28},{28,24},{1,5},{5... | collective-permute-start | bytes 786440 | tf_op jit(solution)/shard_map/ppermute | solution.py:179
  56.5 8.1 %collective-permute-start.4 = (bf16[3,1024,128]{1,2,0:T(8,128)(2,1)}, bf16[3,1024,128]{1,2,0:T(8,128)(2,1)}, u32[]{:S(2)}, u32[]{:S(2)}) collective-permute-start(bf16[3,1024,128]{1,2,0:T(8,128)(2,1)} %pad_maximum_fusion.3), channel_id=1, source_target_pairs={{0,4},{4,0},{8,12},{12,8},{16,20},{20,16},{24,28},{28,24},{1,5},{5... | collective-permute-start | bytes 2359304 | tf_op jit(solution)/shard_map/ppermute | solution.py:181
  56.7 17.3 %copy-start.24 = (f32[128]{0:T(128)}, f32[128]{0:T(128)S(1)}, u32[]{:S(2)}) copy-start(f32[128]{0:T(128)S(1)} %add_rsqrt_fusion) | copy-start | bytes 1540
  84.6 3.9 %collective-permute-start.5 = (bf16[4,1024,128]{2,1,0:T(8,128)(2,1)}, bf16[4,1024,128]{2,1,0:T(8,128)(2,1)}, u32[]{:S(2)}, u32[]{:S(2)}) collective-permute-start(bf16[4,1024,128]{2,1,0:T(8,128)(2,1)} %bitcast.36), channel_id=1, source_target_pairs={{0,4},{4,0},{8,12},{12,8},{16,20},{20,16},{24,28},{28,24},{1,5},{5... | collective-permute-start | bytes 3145736 | tf_op jit(solution)/shard_map/ppermute | solution.py:187
  90.2 9.2 %collective-permute-start.6 = (bf16[1024,128]{1,0:T(8,128)(2,1)S(1)}, bf16[1024,128]{1,0:T(8,128)(2,1)S(1)}, u32[]{:S(2)}, u32[]{:S(2)}) collective-permute-start(bf16[1024,128]{1,0:T(8,128)(2,1)S(1)} %get-tuple-element.12), channel_id=1, source_target_pairs={{0,8},{4,12},{8,0},{12,4},{16,24},{20,28},{24,16},{28,20},{1,9},{5... | collective-permute-start | bytes 786440 | tf_op jit(solution)/shard_map/ppermute | solution.py:191
  92.1 13.1 %collective-permute-start.8 = (bf16[1024,128]{1,0:T(8,128)(2,1)S(1)}, bf16[1024,128]{1,0:T(8,128)(2,1)S(1)}, u32[]{:S(2)}, u32[]{:S(2)}) collective-permute-start(bf16[1024,128]{1,0:T(8,128)(2,1)S(1)} %get-tuple-element.13), channel_id=1, source_target_pairs={{0,24},{4,28},{8,16},{12,20},{16,8},{20,12},{24,0},{28,4},{1,25},{... | collective-permute-start | bytes 786440 | tf_op jit(solution)/shard_map/ppermute | solution.py:191
  93.2 13.5 %copy-start.21 = (bf16[128,1024]{0,1:T(8,128)(2,1)S(1)}, bf16[128,1024]{0,1:T(8,128)(2,1)}, u32[]{:S(2)}) copy-start(bf16[128,1024]{0,1:T(8,128)(2,1)} %copy.96) | copy-start | bytes 786436
  93.2 13.3 %collective-permute-start.7 = (bf16[1024,128]{1,0:T(8,128)(2,1)S(1)}, bf16[1024,128]{1,0:T(8,128)(2,1)S(1)}, u32[]{:S(2)}, u32[]{:S(2)}) collective-permute-start(bf16[1024,128]{1,0:T(8,128)(2,1)S(1)} %get-tuple-element.14), channel_id=1, source_target_pairs={{0,16},{4,20},{8,24},{12,28},{16,0},{20,4},{24,8},{28,12},{1,17},{... | collective-permute-start | bytes 786440 | tf_op jit(solution)/shard_map/ppermute | solution.py:191
  112.0 7.4 %collective-permute-start.14 = (bf16[2,2,2,2,32,1536]{5,4,3,2,1,0:T(8,128)(2,1)}, bf16[2,2,2,2,32,1536]{5,4,3,2,1,0:T(8,128)(2,1)}, u32[]{:S(2)}, u32[]{:S(2)}) collective-permute-start(bf16[2,2,2,2,32,1536]{5,4,3,2,1,0:T(8,128)(2,1)} %fusion.13), channel_id=1, source_target_pairs={{0,4},{4,0},{8,12},{12,8},{16,20},{20,16},{24,28},{28,24},{1,5},{5... | collective-permute-start | bytes 4718600 | tf_op jit(solution)/shard_map/ppermute | solution.py:155
  114.1 2.1 %collective-permute-start.19 = (bf16[2,2,2,2,16,1024]{5,4,3,2,1,0:T(8,128)(2,1)S(1)}, bf16[2,2,2,2,16,1024]{5,4,3,2,1,0:T(8,128)(2,1)S(1)}, u32[]{:S(2)}, u32[]{:S(2)}) collective-permute-start(bf16[2,2,2,2,16,1024]{5,4,3,2,1,0:T(8,128)(2,1)S(1)} %fusion.34), channel_id=1, source_target_pairs={{0,4},{4,0},{8,12},{12,8},{16,20},{20,16},{24,28},{28,24},{1,5},{5... | collective-permute-start | bytes 1572872 | tf_op jit(solution)/shard_map/ppermute | solution.py:153
  117.6 7.7 %collective-permute-start.20 = (bf16[2,2,2,16,1024]{4,3,2,1,0:T(8,128)(2,1)S(1)}, bf16[2,2,2,16,1024]{4,3,2,1,0:T(8,128)(2,1)S(1)}, u32[]{:S(2)}, u32[]{:S(2)}) collective-permute-start(bf16[2,2,2,16,1024]{4,3,2,1,0:T(8,128)(2,1)S(1)} %fusion.41), channel_id=1, source_target_pairs={{0,8},{4,20},{8,0},{12,28},{16,24},{20,4},{24,16},{28,12},{1,9},{5... | collective-permute-start | bytes 786440 | tf_op jit(solution)/shard_map/ppermute | solution.py:153
  124.9 12.8 %collective-permute-start.15 = (bf16[2,2,2,32,1536]{4,3,2,1,0:T(8,128)(2,1)}, bf16[2,2,2,32,1536]{4,3,2,1,0:T(8,128)(2,1)S(1)}, u32[]{:S(2)}, u32[]{:S(2)}) collective-permute-start(bf16[2,2,2,32,1536]{4,3,2,1,0:T(8,128)(2,1)} %fusion.14), channel_id=1, source_target_pairs={{0,8},{4,20},{8,0},{12,28},{16,24},{20,4},{24,16},{28,12},{1,9},{5... | collective-permute-start | bytes 2359304 | tf_op jit(solution)/shard_map/ppermute | solution.py:155
  125.4 13.5 %collective-permute-start.21 = (bf16[2,2,16,1024]{3,2,1,0:T(8,128)(2,1)S(1)}, bf16[2,2,16,1024]{3,2,1,0:T(8,128)(2,1)S(1)}, u32[]{:S(2)}, u32[]{:S(2)}) collective-permute-start(bf16[2,2,16,1024]{3,2,1,0:T(8,128)(2,1)S(1)} %fusion.59), channel_id=1, source_target_pairs={{0,16},{4,12},{8,24},{12,4},{16,0},{20,28},{24,8},{28,20},{1,17},{... | collective-permute-start | bytes 393224 | tf_op jit(solution)/shard_map/ppermute | solution.py:153
  130.1 8.9 %collective-permute-start.9 = (f32[1025]{0:T(1024)S(1)}, f32[1025]{0:T(1024)S(1)}, u32[]{:S(2)}, u32[]{:S(2)}) collective-permute-start(f32[1025]{0:T(1024)S(1)} %pad_maximum_fusion.7), channel_id=1, source_target_pairs={{0,4},{4,0},{8,12},{12,8},{16,20},{20,16},{24,28},{28,24},{1,5},{5... | collective-permute-start | bytes 12308 | tf_op jit(solution)/shard_map/ppermute | solution.py:155
  138.2 7.9 %collective-permute-start.16 = (bf16[2,2,32,1536]{3,2,1,0:T(8,128)(2,1)S(1)}, bf16[2,2,32,1536]{3,2,1,0:T(8,128)(2,1)S(1)}, u32[]{:S(2)}, u32[]{:S(2)}) collective-permute-start(bf16[2,2,32,1536]{3,2,1,0:T(8,128)(2,1)S(1)} %fusion.47), channel_id=1, source_target_pairs={{0,16},{4,12},{8,24},{12,4},{16,0},{20,28},{24,8},{28,20},{1,17},{... | collective-permute-start | bytes 1179656 | tf_op jit(solution)/shard_map/ppermute | solution.py:155
  139.6 3.9 %collective-permute-start.10 = (f32[1025]{0:T(1024)S(1)}, f32[1025]{0:T(1024)S(1)}, u32[]{:S(2)}, u32[]{:S(2)}) collective-permute-start(f32[1025]{0:T(1024)S(1)} %fusion.69), channel_id=1, source_target_pairs={{0,8},{4,20},{8,0},{12,28},{16,24},{20,4},{24,16},{28,12},{1,9},{5... | collective-permute-start | bytes 12308 | tf_op jit(solution)/shard_map/ppermute | solution.py:155
  140.8 7.2 %collective-permute-start.22 = (bf16[2,16,1024]{2,1,0:T(8,128)(2,1)S(1)}, bf16[2,16,1024]{2,1,0:T(8,128)(2,1)S(1)}, u32[]{:S(2)}, u32[]{:S(2)}) collective-permute-start(bf16[2,16,1024]{2,1,0:T(8,128)(2,1)S(1)} %fusion.63), channel_id=1, source_target_pairs={{0,1},{1,0},{2,3},{3,2},{4,5},{5,4},{6,7},{7,6},{8,9},{9,8},{10,11... | collective-permute-start | bytes 196616 | tf_op jit(solution)/shard_map/ppermute | solution.py:164
  143.5 4.5 %collective-permute-start.11 = (f32[1025]{0:T(1024)S(1)}, f32[1025]{0:T(1024)S(1)}, u32[]{:S(2)}, u32[]{:S(2)}) collective-permute-start(f32[1025]{0:T(1024)S(1)} %add.315), channel_id=1, source_target_pairs={{0,16},{4,12},{8,24},{12,4},{16,0},{20,28},{24,8},{28,20},{1,17},{... | collective-permute-start | bytes 12308 | tf_op jit(solution)/shard_map/ppermute | solution.py:155
  146.2 15.1 %copy-start.1 = (bf16[1,512,1024]{2,1,0:T(8,128)(2,1)S(1)}, bf16[1,512,1024]{2,1,0:T(8,128)(2,1)}, u32[]{:S(2)}) copy-start(bf16[1,512,1024]{2,1,0:T(8,128)(2,1)} %param.7) | copy-start | bytes 3145732
  146.4 8.5 %collective-permute-start.17 = (bf16[2,32,1536]{2,1,0:T(8,128)(2,1)S(1)}, bf16[2,32,1536]{2,1,0:T(8,128)(2,1)S(1)}, u32[]{:S(2)}, u32[]{:S(2)}) collective-permute-start(bf16[2,32,1536]{2,1,0:T(8,128)(2,1)S(1)} %fusion.58), channel_id=1, source_target_pairs={{0,1},{1,0},{2,3},{3,2},{4,5},{5,4},{6,7},{7,6},{8,9},{9,8},{10,11... | collective-permute-start | bytes 589832 | tf_op jit(solution)/shard_map/ppermute | solution.py:166
  148.0 4.4 %collective-permute-start.12 = (f32[1025]{0:T(1024)S(1)}, f32[1025]{0:T(1024)S(1)}, u32[]{:S(2)}, u32[]{:S(2)}) collective-permute-start(f32[1025]{0:T(1024)S(1)} %add.316), channel_id=1, source_target_pairs={{0,1},{1,0},{2,3},{3,2},{4,5},{5,4},{6,7},{7,6},{8,9},{9,8},{10,11... | collective-permute-start | bytes 12308 | tf_op jit(solution)/shard_map/ppermute | solution.py:166
  148.7 6.8 %collective-permute-start.23 = (bf16[16,1024]{1,0:T(8,128)(2,1)S(1)}, bf16[16,1024]{1,0:T(8,128)(2,1)S(1)}, u32[]{:S(2)}, u32[]{:S(2)}) collective-permute-start(bf16[16,1024]{1,0:T(8,128)(2,1)S(1)} %fusion.65), channel_id=1, source_target_pairs={{0,2},{1,3},{2,0},{3,1},{4,6},{5,7},{6,4},{7,5},{8,10},{9,11},{10,... | collective-permute-start | bytes 98312 | tf_op jit(solution)/shard_map/ppermute | solution.py:164
  152.5 4.8 %collective-permute-start.13 = (f32[1025]{0:T(1024)S(1)}, f32[1025]{0:T(1024)S(1)}, u32[]{:S(2)}, u32[]{:S(2)}) collective-permute-start(f32[1025]{0:T(1024)S(1)} %add.317), channel_id=1, source_target_pairs={{0,2},{1,3},{2,0},{3,1},{4,6},{5,7},{6,4},{7,5},{8,10},{9,11},{10,... | collective-permute-start | bytes 12308 | tf_op jit(solution)/shard_map/ppermute | solution.py:166
  154.9 5.6 %collective-permute-start.18 = (bf16[32,1536]{1,0:T(8,128)(2,1)S(1)}, bf16[32,1536]{1,0:T(8,128)(2,1)S(1)}, u32[]{:S(2)}, u32[]{:S(2)}) collective-permute-start(bf16[32,1536]{1,0:T(8,128)(2,1)S(1)} %fusion.62), channel_id=1, source_target_pairs={{0,2},{1,3},{2,0},{3,1},{4,6},{5,7},{6,4},{7,5},{8,10},{9,11},{10,... | collective-permute-start | bytes 294920 | tf_op jit(solution)/shard_map/ppermute | solution.py:166
  (28 other events, 82.3 us)

commit v18 on v16

--- a/solution.py
+++ b/solution.py
@@ -203,6 +203,9 @@
     safe_ids = jnp.maximum(row_ids, 0)
     kept_tokens = jnp.where(is_kept[:, None], raw_tokens[0][safe_ids], jnp.zeros((), jnp.bfloat16))
     kept_target = jnp.where(is_kept[:, None], teacher[0][safe_ids], jnp.zeros((), jnp.bfloat16))
+    kept_tokens, kept_target, kept_count = lax.optimization_barrier(
+        (kept_tokens, kept_target, kept_count)
+    )
     count_table = lax.all_to_all(
         jnp.broadcast_to(kept_count.reshape(1, 1), (shards, 1)), "seq", 0, 0, tiled=True
     ).reshape(shards)

time: 162 us -> 163 us (level)
  transfers between devices with their start and end apart: 25 -> 25, of which waited for: 16 -> 16; matrix products, arithmetic and copies ran while one was open for 15% -> 14% of each run, Pallas kernels for 0% -> 0%
where the time goes in v18:
time: 163 us; the launch traced here: 162 us
  waiting for transfers between devices  53.7 us (33%)
  starting transfers between devices  33.3 us (20%)
  local copies, waits for them, and re-layouts  31.5 us (19%)
  matrix products  20.2 us (12%)
  other arithmetic  20 us (12%)
  between operations  3.12 us (2%)
    ppermute x3, waiting for transfers between devices, return_blocks(): sent = lax.ppermute(summed[k].astype(jnp.bfloat16), 'seq', xor_pairs(2 * k))  12.6 us
    all_to_all x1, waiting for transfers between devices, per_device(): lax.all_to_all(jnp.concatenate([send_tokens, send_target], axis=2), 'seq'...  12.3 us
    ppermute x6, waiting for transfers between devices, halving_scatter(): lax.ppermute((give.astype(jnp.bfloat16), small), 'seq', pairs)  9.69 us
    ppermute x3, waiting for transfers between devices, gather_blocks(): lax.ppermute(block, 'seq', xor_pairs(2 * k))  9.21 us
    unnamed x65, local copies, waits for them, and re-layouts  8.71 us
    ppermute x4, starting transfers between devices, halving_scatter(): lax.ppermute((give.astype(jnp.bfloat16), small), 'clip', pairs)  5.36 us
    all_to_all x1, starting transfers between devices, per_device(): lax.all_to_all(jnp.broadcast_to(kept_count.reshape(1, 1), (shards, 1)), '...  5.17 us
    add x9, other arithmetic, halving_scatter(): data = keep + got.astype(jnp.float32)  5.02 us
  transfers between devices with their start and end apart: 25, of which 16 were waited for; matrix products, arithmetic and copies ran while one was open for 14% of the time, Pallas kernels for 0%

profile of v18, /device:TPU:0, one launch (start us, length us, event | category | flops | bytes accessed | tf_op | source)
XLA Modules:
  0.0 161.8 jit_solution(14622179673412159107)
XLA Ops:
  6.2 5.2 %all-to-all-start = ((s32[8,1,1]{2,1,0:T(1,128)}), s32[8,1,1]{2,1,0:T(1,128)S(1)}, u32[]{:S(2)}, u32[]{:S(2)}) async-start(s32[8,1,1]{2,1,0:T(1,128)} %broadcast_in_dim.49), calls=%async_computation | async-start | bytes 8192 | tf_op jit(solution)/shard_map/all_to_all | solution.py:209
  11.4 4.6 %all-to-all-done = s32[8,1,1]{2,1,0:T(1,128)S(1)} async-done(((s32[8,1,1]{2,1,0:T(1,128)}), s32[8,1,1]{2,1,0:T(1,128)S(1)}, u32[]{:S(2)}, u32[]{:S(2)}) %all-to-all-start) | async-done | bytes 64 | tf_op jit(solution)/shard_map/all_to_all | solution.py:209
  21.7 3.5 %all-to-all-start.1 = ((bf16[8,24,2048]{2,1,0:T(8,128)(2,1)}), bf16[8,24,2048]{2,1,0:T(8,128)(2,1)S(1)}, u32[]{:S(2)}, u32[]{:S(2)}) async-start(bf16[8,24,2048]{2,1,0:T(8,128)(2,1)} %pad_maximum_fusion.2), calls=%async_computation.1 | async-start | bytes 1572864 | tf_op jit(solution)/shard_map/all_to_all | solution.py:226
  25.5 12.3 %all-to-all-done.1 = bf16[8,24,2048]{2,1,0:T(8,128)(2,1)S(1)} async-done(((bf16[8,24,2048]{2,1,0:T(8,128)(2,1)}), bf16[8,24,2048]{2,1,0:T(8,128)(2,1)S(1)}, u32[]{:S(2)}, u32[]{:S(2)}) %all-to-all-start.1) | async-done | bytes 786464 | tf_op jit(solution)/shard_map/all_to_all | solution.py:226
  37.8 1.8 %scatter_custom_fusion = bf16[128,2048]{1,0:T(8,128)(2,1)S(1)} fusion(s32[192]{0:T(256)S(1)} %bitcast.228, bf16[192,2048]{1,0:T(8,128)(2,1)S(1)} %bitcast.219, bf16[]{:T(256)} %constant.157.clone.1), kind=kCustom, calls=%fused_computation.108 | custom fusion | bytes 524290 | tf_op jit(solution)/shard_map/scatter | solution.py:236
  40.3 2.1 %fusion.19 = bf16[128,1024]{1,0:T(8,128)(2,1)S(1)} fusion(bf16[128,1024]{1,0:T(8,128)(2,1)S(1)} %fusion.30, bf16[1024,1536]{1,0:T(8,128)(2,1)} %param.9), kind=kOutput, calls=%fused_computation.32 | convolution fusion | flops 268566528 | bytes 2621440 | tf_op jit(solution)/shard_map/dot_general | solution.py:250
  44.5 1.5 collective-permute-start
  46.0 6.2 %collective-permute-done.2 = bf16[1024,128]{0,1:T(8,128)(2,1)S(1)} collective-permute-done((bf16[1024,128]{0,1:T(8,128)(2,1)S(1)}, bf16[1024,128]{0,1:T(8,128)(2,1)S(1)}, u32[]{:S(2)}, u32[]{:S(2)}) %collective-permute-start.2) | collective-permute-done | bytes 262176 | tf_op jit(solution)/shard_map/ppermute | solution.py:179
  52.2 2.8 %collective-permute-done.1 = bf16[1024,128]{0,1:T(8,128)(2,1)S(1)} collective-permute-done((bf16[1024,128]{0,1:T(8,128)(2,1)S(1)}, bf16[1024,128]{0,1:T(8,128)(2,1)S(1)}, u32[]{:S(2)}, u32[]{:S(2)}) %collective-permute-start.1) | collective-permute-done | bytes 262176 | tf_op jit(solution)/shard_map/ppermute | solution.py:179
  56.6 1.5 convolution_convert_fusion.1
  60.5 1.8 %copy.71 = bf16[1024,128]{1,0:T(8,128)(2,1)} copy(bf16[1024,128]{0,1:T(8,128)(2,1)} %copy-done.16) | data formatting | bytes 524288 | tf_op jit(solution)/shard_map/ppermute | solution.py:179
  63.4 2.3 %copy.74 = bf16[4,1024,128]{2,1,0:T(8,128)(2,1)} copy(bf16[4,1024,128]{1,2,0:T(8,128)(2,1)} %collective-permute-done.3) | data formatting | bytes 2097152 | tf_op jit(solution)/shard_map/ppermute | solution.py:181
  69.9 1.6 %fusion.51 = (bf16[128,8,64]{0,2,1:T(8,128)(2,1)S(1)}, f32[8,128,64,1]{1,2,0,3:T(8,128)}) fusion(f32[128,8]{0,1:T(8,128)S(1)} %bitcast.225, f32[8,8,128,128]{2,3,1,0:T(8,128)S(1)} %get-tuple-element.36, f32[8,128]{1,0:T(8,128)S(1)} %get-tuple-element.35, bf16[8,8,2,64,128]{4,3,2,1,0:T(8,128)(2,1)S(1)} %constant_dynamic-update-slice_fusion), kind=kOutput, calls=%fused_computation.101 | convolution fusion | flops 137494528 | bytes 5644288 | tf_op jit(solution)/shard_map/ihqt,ihdt->ihqd/dot_general | solution.py:265
  73.6 3.9 %fusion.16 = bf16[8,8,64,128]{3,2,1,0:T(8,128)(2,1)S(1)} fusion(f32[8,8,128,128]{2,3,1,0:T(8,128)} %copy-done.2, f32[8,128]{1,0:T(8,128)S(1)} %log_add_fusion, bf16[8,128,64]{1,2,0:T(8,128)(2,1)S(1)} %bitcast.200), kind=kOutput, calls=%fused_computation.29 | convolution fusion | flops 137887744 | bytes 5378048 | tf_op jit(solution)/shard_map/ihqd,ihqt->ihdt/dot_general | solution.py:293
  77.5 2.6 %multiply_convert_fusion = bf16[8,8,128,128]{2,3,1,0:T(8,128)(2,1)S(1)} fusion(f32[8,8,128,128]{2,3,1,0:T(8,128)S(1)} %copy-done.3, f32[8,128]{1,0:T(8,128)S(1)} %multiply_reduce_fusion.4, f32[8,128]{1,0:T(8,128)S(1)} %log_add_fusion, bf16[8,8,2,64,128]{4,3,2,1,0:T(8,128)(2,1)} %copy-done.9, bf16[8,128,64]{1,2,0:T(8,128)(2,1)S(1)} %bitcast.201), kind=kOutput, calls=%fused_computation.5 | convolution fusion | flops 139460608 | bytes 7479296 | tf_op jit(solution)/shard_map/ihqd,ihdt->ihqt/dot_general | solution.py:296
  80.1 1.5 multiply_convert_fusion.1
  87.7 1.6 %fusion.72 = (bf16[4,1024,128]{2,1,0:T(8,128)(2,1)S(1)}, f32[4,1024,128]{2,1,0:T(8,128)S(1)}) fusion(bf16[4,1024,128]{2,1,0:T(8,128)(2,1)} %collective-permute-done.4, f32[4,8,2,64,128]{4,3,2,1,0:T(8,128)S(1)} %copy.87), kind=kLoop, calls=%fused_computation.168 | loop fusion | flops 1572864 | bytes 6291456 | tf_op jit(solution)/shard_map/convert.6
  89.4 1.9 %collective-permute-start.5 = (bf16[1024,128]{1,0:T(8,128)(2,1)S(1)}, bf16[1024,128]{1,0:T(8,128)(2,1)S(1)}, u32[]{:S(2)}, u32[]{:S(2)}) collective-permute-start(bf16[1024,128]{1,0:T(8,128)(2,1)S(1)} %get-tuple-element.18), channel_id=1, source_target_pairs={{0,8},{4,12},{8,0},{12,4},{16,24},{20,28},{24,16},{28,20},{1,9},{5... | collective-permute-start | bytes 786440 | tf_op jit(solution)/shard_map/ppermute | solution.py:191
  93.5 5.1 %collective-permute-done.5 = bf16[1024,128]{1,0:T(8,128)(2,1)S(1)} collective-permute-done((bf16[1024,128]{1,0:T(8,128)(2,1)S(1)}, bf16[1024,128]{1,0:T(8,128)(2,1)S(1)}, u32[]{:S(2)}, u32[]{:S(2)}) %collective-permute-start.5) | collective-permute-done | bytes 262176 | tf_op jit(solution)/shard_map/ppermute | solution.py:191
  98.6 6.1 %collective-permute-done.7 = bf16[1024,128]{1,0:T(8,128)(2,1)S(1)} collective-permute-done((bf16[1024,128]{1,0:T(8,128)(2,1)S(1)}, bf16[1024,128]{1,0:T(8,128)(2,1)S(1)}, u32[]{:S(2)}, u32[]{:S(2)}) %collective-permute-start.7) | collective-permute-done | bytes 262176 | tf_op jit(solution)/shard_map/ppermute | solution.py:191
  107.2 2.6 %copy-done.6 = f32[2,2,2,2,2,32,1536]{6,5,4,3,2,1,0:T(8,128)} copy-done((f32[2,2,2,2,2,32,1536]{6,5,4,3,2,1,0:T(8,128)}, f32[2,2,2,2,2,32,1536]{6,5,4,3,2,1,0:T(8,128)S(1)}, u32[]{:S(2)}) %copy-start.6) | copy-done | bytes 6291480
  113.9 1.5 collective-permute-done.18
  116.8 1.7 %collective-permute-start.19 = (bf16[2,2,2,16,1024]{4,3,2,1,0:T(8,128)(2,1)S(1)}, bf16[2,2,2,16,1024]{4,3,2,1,0:T(8,128)(2,1)S(1)}, u32[]{:S(2)}, u32[]{:S(2)}) collective-permute-start(bf16[2,2,2,16,1024]{4,3,2,1,0:T(8,128)(2,1)S(1)} %fusion.39), channel_id=1, source_target_pairs={{0,8},{4,20},{8,0},{12,28},{16,24},{20,4},{24,16},{28,12},{1,9},{5... | collective-permute-start | bytes 786440 | tf_op jit(solution)/shard_map/ppermute | solution.py:153
  118.6 2.9 %bitcast_add_fusion = f32[2,2,2,2,32,1536]{5,4,3,2,1,0:T(8,128)S(1)} fusion(bf16[2,2,2,2,32,1536]{5,4,3,2,1,0:T(8,128)(2,1)} %collective-permute-done.13, f32[2,2,2,2,2,32,1536]{6,5,4,3,2,1,0:T(8,128)} %copy-done.6, s32[]{:T(128)S(6)} %select_n.232), kind=kLoop, calls=%fused_computation.12 | loop fusion | flops 1572864 | bytes 7864324 | tf_op jit(solution)/shard_map/add | solution.py:157
  121.5 1.6 %copy-done.4 = f32[2,2,2,2,32,1536]{5,4,3,2,1,0:T(8,128)} copy-done((f32[2,2,2,2,32,1536]{5,4,3,2,1,0:T(8,128)}, f32[2,2,2,2,32,1536]{5,4,3,2,1,0:T(8,128)S(1)}, u32[]{:S(2)}) %copy-start.4) | copy-done | bytes 3145752
  125.6 3.1 %fusion.22 = f32[1024]{0:T(1024)S(1)} fusion(bf16[1024,1536]{1,0:T(8,128)(2,1)} %param.9, f32[128]{0:T(128)S(1)} %copy-done.23, f32[128]{0:T(128)S(1)} %copy-done.21, bf16[1024,128]{1,0:T(8,128)(2,1)S(1)} %fusion.38, bf16[512,128]{1,0:T(8,128)(2,1)S(1)} %bitcast.221, bf16[128,2048]{1,0:T(8,128)(2,1)S(1)} %scatter_custom_fusion), kind=kOutput, calls=%fused_computation.33 | convolution fusion | flops 404093952 | bytes 3806208 | tf_op jit(solution)/shard_map/ct,fc->tf/dot_general | solution.py:312
  129.9 7.2 %collective-permute-done.14 = bf16[2,2,2,32,1536]{4,3,2,1,0:T(8,128)(2,1)S(1)} collective-permute-done((bf16[2,2,2,32,1536]{4,3,2,1,0:T(8,128)(2,1)}, bf16[2,2,2,32,1536]{4,3,2,1,0:T(8,128)(2,1)S(1)}, u32[]{:S(2)}, u32[]{:S(2)}) %collective-permute-start.14) | collective-permute-done | bytes 786464 | tf_op jit(solution)/shard_map/ppermute | solution.py:155
  140.1 1.6 %collective-permute-start.21 = (bf16[2,16,1024]{2,1,0:T(8,128)(2,1)S(1)}, bf16[2,16,1024]{2,1,0:T(8,128)(2,1)S(1)}, u32[]{:S(2)}, u32[]{:S(2)}) collective-permute-start(bf16[2,16,1024]{2,1,0:T(8,128)(2,1)S(1)} %fusion.61), channel_id=1, source_target_pairs={{0,1},{1,0},{2,3},{3,2},{4,5},{5,4},{6,7},{7,6},{8,9},{9,8},{10,11... | collective-permute-start | bytes 196616 | tf_op jit(solution)/shard_map/ppermute | solution.py:164
  145.8 1.6 %collective-permute-start.16 = (bf16[2,32,1536]{2,1,0:T(8,128)(2,1)S(1)}, bf16[2,32,1536]{2,1,0:T(8,128)(2,1)S(1)}, u32[]{:S(2)}, u32[]{:S(2)}) collective-permute-start(bf16[2,32,1536]{2,1,0:T(8,128)(2,1)S(1)} %fusion.56), channel_id=1, source_target_pairs={{0,1},{1,0},{2,3},{3,2},{4,5},{5,4},{6,7},{7,6},{8,9},{9,8},{10,11... | collective-permute-start | bytes 589832 | tf_op jit(solution)/shard_map/ppermute | solution.py:166
  148.2 2.6 %collective-permute-start.22 = (bf16[16,1024]{1,0:T(8,128)(2,1)S(1)}, bf16[16,1024]{1,0:T(8,128)(2,1)S(1)}, u32[]{:S(2)}, u32[]{:S(2)}) collective-permute-start(bf16[16,1024]{1,0:T(8,128)(2,1)S(1)} %fusion.63), channel_id=1, source_target_pairs={{0,2},{1,3},{2,0},{3,1},{4,6},{5,7},{6,4},{7,5},{8,10},{9,11},{10,... | collective-permute-start | bytes 98312 | tf_op jit(solution)/shard_map/ppermute | solution.py:164
  151.7 2.6 %collective-permute-start.12 = (f32[1025]{0:T(1024)S(1)}, f32[1025]{0:T(1024)S(1)}, u32[]{:S(2)}, u32[]{:S(2)}) collective-permute-start(f32[1025]{0:T(1024)S(1)} %add.317), channel_id=1, source_target_pairs={{0,2},{1,3},{2,0},{3,1},{4,6},{5,7},{6,4},{7,5},{8,10},{9,11},{10,... | collective-permute-start | bytes 12308 | tf_op jit(solution)/shard_map/ppermute | solution.py:166
  158.3 1.7 %collective-permute-done.17 = bf16[32,1536]{1,0:T(8,128)(2,1)S(1)} collective-permute-done((bf16[32,1536]{1,0:T(8,128)(2,1)S(1)}, bf16[32,1536]{1,0:T(8,128)(2,1)S(1)}, u32[]{:S(2)}, u32[]{:S(2)}) %collective-permute-start.17) | collective-permute-done | bytes 98336 | tf_op jit(solution)/shard_map/ppermute | solution.py:166
  (180 shorter events, 57.9 us)
Async XLA Ops:
  6.2 9.8 %all-to-all-start = ((s32[8,1,1]{2,1,0:T(1,128)}), s32[8,1,1]{2,1,0:T(1,128)S(1)}, u32[]{:S(2)}, u32[]{:S(2)}) async-start(s32[8,1,1]{2,1,0:T(1,128)} %broadcast_in_dim.49), calls=%async_computation | async-start | bytes 8192 | tf_op jit(solution)/shard_map/all_to_all | solution.py:209
  20.8 19.3 %copy-start.19 = (f32[1024]{0:T(1024)S(1)}, f32[1024]{0:T(1024)}, u32[]{:S(2)}) copy-start(f32[1024]{0:T(1024)} %param.11) | copy-start | bytes 12292
  21.7 16.1 %all-to-all-start.1 = ((bf16[8,24,2048]{2,1,0:T(8,128)(2,1)}), bf16[8,24,2048]{2,1,0:T(8,128)(2,1)S(1)}, u32[]{:S(2)}, u32[]{:S(2)}) async-start(bf16[8,24,2048]{2,1,0:T(8,128)(2,1)} %pad_maximum_fusion.2), calls=%async_computation.1 | async-start | bytes 1572864 | tf_op jit(solution)/shard_map/all_to_all | solution.py:226
  40.3 16.3 %copy-start.12 = (bf16[128,1024]{1,0:T(8,128)(2,1)}, bf16[128,1024]{1,0:T(8,128)(2,1)S(1)}, u32[]{:S(2)}) copy-start(bf16[128,1024]{1,0:T(8,128)(2,1)S(1)} %fusion.30) | copy-start | bytes 786436
  42.4 9.8 %collective-permute-start.2 = (bf16[1024,128]{0,1:T(8,128)(2,1)S(1)}, bf16[1024,128]{0,1:T(8,128)(2,1)S(1)}, u32[]{:S(2)}, u32[]{:S(2)}) collective-permute-start(bf16[1024,128]{0,1:T(8,128)(2,1)S(1)} %bitcast.212), channel_id=1, source_target_pairs={{0,24},{4,28},{8,16},{12,20},{16,8},{20,12},{24,0},{28,4},{1,25},{... | collective-permute-start | bytes 786440 | tf_op jit(solution)/shard_map/ppermute | solution.py:179
  43.1 11.9 %collective-permute-start.1 = (bf16[1024,128]{0,1:T(8,128)(2,1)S(1)}, bf16[1024,128]{0,1:T(8,128)(2,1)S(1)}, u32[]{:S(2)}, u32[]{:S(2)}) collective-permute-start(bf16[1024,128]{0,1:T(8,128)(2,1)S(1)} %bitcast.213), channel_id=1, source_target_pairs={{0,16},{4,20},{8,24},{12,28},{16,0},{20,4},{24,8},{28,12},{1,17},{... | collective-permute-start | bytes 786440 | tf_op jit(solution)/shard_map/ppermute | solution.py:179
  44.5 10.7 %collective-permute-start = (bf16[1024,128]{0,1:T(8,128)(2,1)S(1)}, bf16[1024,128]{0,1:T(8,128)(2,1)S(1)}, u32[]{:S(2)}, u32[]{:S(2)}) collective-permute-start(bf16[1024,128]{0,1:T(8,128)(2,1)S(1)} %bitcast.214), channel_id=1, source_target_pairs={{0,8},{4,12},{8,0},{12,4},{16,24},{20,28},{24,16},{28,20},{1,9},{5... | collective-permute-start | bytes 786440 | tf_op jit(solution)/shard_map/ppermute | solution.py:179
  52.2 4.1 %copy-start.14 = (bf16[1024,128]{0,1:T(8,128)(2,1)}, bf16[1024,128]{0,1:T(8,128)(2,1)S(1)}, u32[]{:S(2)}) copy-start(bf16[1024,128]{0,1:T(8,128)(2,1)S(1)} %collective-permute-done.2) | copy-start | bytes 786436
  56.3 7.1 %collective-permute-start.3 = (bf16[4,1024,128]{1,2,0:T(8,128)(2,1)}, bf16[4,1024,128]{1,2,0:T(8,128)(2,1)}, u32[]{:S(2)}, u32[]{:S(2)}) collective-permute-start(bf16[4,1024,128]{1,2,0:T(8,128)(2,1)} %pad_maximum_fusion), channel_id=1, source_target_pairs={{0,4},{4,0},{8,12},{12,8},{16,20},{20,16},{24,28},{28,24},{1,5},{5... | collective-permute-start | bytes 3145736 | tf_op jit(solution)/shard_map/ppermute | solution.py:181
  84.6 3.1 %collective-permute-start.4 = (bf16[4,1024,128]{2,1,0:T(8,128)(2,1)}, bf16[4,1024,128]{2,1,0:T(8,128)(2,1)}, u32[]{:S(2)}, u32[]{:S(2)}) collective-permute-start(bf16[4,1024,128]{2,1,0:T(8,128)(2,1)} %bitcast.36), channel_id=1, source_target_pairs={{0,4},{4,0},{8,12},{12,8},{16,20},{20,16},{24,28},{28,24},{1,5},{5... | collective-permute-start | bytes 3145736 | tf_op jit(solution)/shard_map/ppermute | solution.py:187
  87.5 5.5 %copy-start.10 = (bf16[8,8,2,64,128]{4,3,2,1,0:T(8,128)(2,1)S(1)}, bf16[8,8,2,64,128]{4,3,2,1,0:T(8,128)(2,1)}, u32[]{:S(2)}) copy-start(bf16[8,8,2,64,128]{4,3,2,1,0:T(8,128)(2,1)} %copy-done.9) | copy-start | bytes 6291460
  89.4 9.2 %collective-permute-start.5 = (bf16[1024,128]{1,0:T(8,128)(2,1)S(1)}, bf16[1024,128]{1,0:T(8,128)(2,1)S(1)}, u32[]{:S(2)}, u32[]{:S(2)}) collective-permute-start(bf16[1024,128]{1,0:T(8,128)(2,1)S(1)} %get-tuple-element.18), channel_id=1, source_target_pairs={{0,8},{4,12},{8,0},{12,4},{16,24},{20,28},{24,16},{28,20},{1,9},{5... | collective-permute-start | bytes 786440 | tf_op jit(solution)/shard_map/ppermute | solution.py:191
  91.3 13.3 %collective-permute-start.7 = (bf16[1024,128]{1,0:T(8,128)(2,1)S(1)}, bf16[1024,128]{1,0:T(8,128)(2,1)S(1)}, u32[]{:S(2)}, u32[]{:S(2)}) collective-permute-start(bf16[1024,128]{1,0:T(8,128)(2,1)S(1)} %get-tuple-element.19), channel_id=1, source_target_pairs={{0,24},{4,28},{8,16},{12,20},{16,8},{20,12},{24,0},{28,4},{1,25},{... | collective-permute-start | bytes 786440 | tf_op jit(solution)/shard_map/ppermute | solution.py:191
  92.4 13.8 %copy-start.17 = (bf16[128,1024]{0,1:T(8,128)(2,1)S(1)}, bf16[128,1024]{0,1:T(8,128)(2,1)}, u32[]{:S(2)}) copy-start(bf16[128,1024]{0,1:T(8,128)(2,1)} %copy.89) | copy-start | bytes 786436
  92.4 13.7 %collective-permute-start.6 = (bf16[1024,128]{1,0:T(8,128)(2,1)S(1)}, bf16[1024,128]{1,0:T(8,128)(2,1)S(1)}, u32[]{:S(2)}, u32[]{:S(2)}) collective-permute-start(bf16[1024,128]{1,0:T(8,128)(2,1)S(1)} %get-tuple-element.20), channel_id=1, source_target_pairs={{0,16},{4,20},{8,24},{12,28},{16,0},{20,4},{24,8},{28,12},{1,17},{... | collective-permute-start | bytes 786440 | tf_op jit(solution)/shard_map/ppermute | solution.py:191
  111.3 7.3 %collective-permute-start.13 = (bf16[2,2,2,2,32,1536]{5,4,3,2,1,0:T(8,128)(2,1)}, bf16[2,2,2,2,32,1536]{5,4,3,2,1,0:T(8,128)(2,1)}, u32[]{:S(2)}, u32[]{:S(2)}) collective-permute-start(bf16[2,2,2,2,32,1536]{5,4,3,2,1,0:T(8,128)(2,1)} %fusion.13), channel_id=1, source_target_pairs={{0,4},{4,0},{8,12},{12,8},{16,20},{20,16},{24,28},{28,24},{1,5},{5... | collective-permute-start | bytes 4718600 | tf_op jit(solution)/shard_map/ppermute | solution.py:155
  113.3 2.1 %collective-permute-start.18 = (bf16[2,2,2,2,16,1024]{5,4,3,2,1,0:T(8,128)(2,1)S(1)}, bf16[2,2,2,2,16,1024]{5,4,3,2,1,0:T(8,128)(2,1)S(1)}, u32[]{:S(2)}, u32[]{:S(2)}) collective-permute-start(bf16[2,2,2,2,16,1024]{5,4,3,2,1,0:T(8,128)(2,1)S(1)} %fusion.34), channel_id=1, source_target_pairs={{0,4},{4,0},{8,12},{12,8},{16,20},{20,16},{24,28},{28,24},{1,5},{5... | collective-permute-start | bytes 1572872 | tf_op jit(solution)/shard_map/ppermute | solution.py:153
  116.8 7.7 %collective-permute-start.19 = (bf16[2,2,2,16,1024]{4,3,2,1,0:T(8,128)(2,1)S(1)}, bf16[2,2,2,16,1024]{4,3,2,1,0:T(8,128)(2,1)S(1)}, u32[]{:S(2)}, u32[]{:S(2)}) collective-permute-start(bf16[2,2,2,16,1024]{4,3,2,1,0:T(8,128)(2,1)S(1)} %fusion.39), channel_id=1, source_target_pairs={{0,8},{4,20},{8,0},{12,28},{16,24},{20,4},{24,16},{28,12},{1,9},{5... | collective-permute-start | bytes 786440 | tf_op jit(solution)/shard_map/ppermute | solution.py:153
  124.1 13.0 %collective-permute-start.14 = (bf16[2,2,2,32,1536]{4,3,2,1,0:T(8,128)(2,1)}, bf16[2,2,2,32,1536]{4,3,2,1,0:T(8,128)(2,1)S(1)}, u32[]{:S(2)}, u32[]{:S(2)}) collective-permute-start(bf16[2,2,2,32,1536]{4,3,2,1,0:T(8,128)(2,1)} %fusion.14), channel_id=1, source_target_pairs={{0,8},{4,20},{8,0},{12,28},{16,24},{20,4},{24,16},{28,12},{1,9},{5... | collective-permute-start | bytes 2359304 | tf_op jit(solution)/shard_map/ppermute | solution.py:155
  124.6 12.5 %copy-start.5 = (f32[2,2,2,2,32,1536]{5,4,3,2,1,0:T(8,128)S(1)}, f32[2,2,2,2,32,1536]{5,4,3,2,1,0:T(8,128)}, u32[]{:S(2)}) copy-start(f32[2,2,2,2,32,1536]{5,4,3,2,1,0:T(8,128)} %copy-done.4) | copy-start | bytes 9437188
  124.7 13.8 %collective-permute-start.20 = (bf16[2,2,16,1024]{3,2,1,0:T(8,128)(2,1)S(1)}, bf16[2,2,16,1024]{3,2,1,0:T(8,128)(2,1)S(1)}, u32[]{:S(2)}, u32[]{:S(2)}) collective-permute-start(bf16[2,2,16,1024]{3,2,1,0:T(8,128)(2,1)S(1)} %fusion.57), channel_id=1, source_target_pairs={{0,16},{4,12},{8,24},{12,4},{16,0},{20,28},{24,8},{28,20},{1,17},{... | collective-permute-start | bytes 393224 | tf_op jit(solution)/shard_map/ppermute | solution.py:153
  129.4 9.1 %collective-permute-start.8 = (f32[1025]{0:T(1024)S(1)}, f32[1025]{0:T(1024)S(1)}, u32[]{:S(2)}, u32[]{:S(2)}) collective-permute-start(f32[1025]{0:T(1024)S(1)} %pad_maximum_fusion.6), channel_id=1, source_target_pairs={{0,4},{4,0},{8,12},{12,8},{16,20},{20,16},{24,28},{28,24},{1,5},{5... | collective-permute-start | bytes 12308 | tf_op jit(solution)/shard_map/ppermute | solution.py:155
  137.7 7.9 %collective-permute-start.15 = (bf16[2,2,32,1536]{3,2,1,0:T(8,128)(2,1)S(1)}, bf16[2,2,32,1536]{3,2,1,0:T(8,128)(2,1)S(1)}, u32[]{:S(2)}, u32[]{:S(2)}) collective-permute-start(bf16[2,2,32,1536]{3,2,1,0:T(8,128)(2,1)S(1)} %fusion.45), channel_id=1, source_target_pairs={{0,16},{4,12},{8,24},{12,4},{16,0},{20,28},{24,8},{28,20},{1,17},{... | collective-permute-start | bytes 1179656 | tf_op jit(solution)/shard_map/ppermute | solution.py:155
  139.1 3.9 %collective-permute-start.9 = (f32[1025]{0:T(1024)S(1)}, f32[1025]{0:T(1024)S(1)}, u32[]{:S(2)}, u32[]{:S(2)}) collective-permute-start(f32[1025]{0:T(1024)S(1)} %fusion.67), channel_id=1, source_target_pairs={{0,8},{4,20},{8,0},{12,28},{16,24},{20,4},{24,16},{28,12},{1,9},{5... | collective-permute-start | bytes 12308 | tf_op jit(solution)/shard_map/ppermute | solution.py:155
  140.1 7.3 %collective-permute-start.21 = (bf16[2,16,1024]{2,1,0:T(8,128)(2,1)S(1)}, bf16[2,16,1024]{2,1,0:T(8,128)(2,1)S(1)}, u32[]{:S(2)}, u32[]{:S(2)}) collective-permute-start(bf16[2,16,1024]{2,1,0:T(8,128)(2,1)S(1)} %fusion.61), channel_id=1, source_target_pairs={{0,1},{1,0},{2,3},{3,2},{4,5},{5,4},{6,7},{7,6},{8,9},{9,8},{10,11... | collective-permute-start | bytes 196616 | tf_op jit(solution)/shard_map/ppermute | solution.py:164
  143.0 4.5 %collective-permute-start.10 = (f32[1025]{0:T(1024)S(1)}, f32[1025]{0:T(1024)S(1)}, u32[]{:S(2)}, u32[]{:S(2)}) collective-permute-start(f32[1025]{0:T(1024)S(1)} %add.315), channel_id=1, source_target_pairs={{0,16},{4,12},{8,24},{12,4},{16,0},{20,28},{24,8},{28,20},{1,17},{... | collective-permute-start | bytes 12308 | tf_op jit(solution)/shard_map/ppermute | solution.py:155
  145.6 15.1 %copy-start.1 = (bf16[1,512,1024]{2,1,0:T(8,128)(2,1)S(1)}, bf16[1,512,1024]{2,1,0:T(8,128)(2,1)}, u32[]{:S(2)}) copy-start(bf16[1,512,1024]{2,1,0:T(8,128)(2,1)} %param.7) | copy-start | bytes 3145732
  145.8 8.5 %collective-permute-start.16 = (bf16[2,32,1536]{2,1,0:T(8,128)(2,1)S(1)}, bf16[2,32,1536]{2,1,0:T(8,128)(2,1)S(1)}, u32[]{:S(2)}, u32[]{:S(2)}) collective-permute-start(bf16[2,32,1536]{2,1,0:T(8,128)(2,1)S(1)} %fusion.56), channel_id=1, source_target_pairs={{0,1},{1,0},{2,3},{3,2},{4,5},{5,4},{6,7},{7,6},{8,9},{9,8},{10,11... | collective-permute-start | bytes 589832 | tf_op jit(solution)/shard_map/ppermute | solution.py:166
  147.5 4.2 %collective-permute-start.11 = (f32[1025]{0:T(1024)S(1)}, f32[1025]{0:T(1024)S(1)}, u32[]{:S(2)}, u32[]{:S(2)}) collective-permute-start(f32[1025]{0:T(1024)S(1)} %add.316), channel_id=1, source_target_pairs={{0,1},{1,0},{2,3},{3,2},{4,5},{5,4},{6,7},{7,6},{8,9},{9,8},{10,11... | collective-permute-start | bytes 12308 | tf_op jit(solution)/shard_map/ppermute | solution.py:166
  148.2 6.6 %collective-permute-start.22 = (bf16[16,1024]{1,0:T(8,128)(2,1)S(1)}, bf16[16,1024]{1,0:T(8,128)(2,1)S(1)}, u32[]{:S(2)}, u32[]{:S(2)}) collective-permute-start(bf16[16,1024]{1,0:T(8,128)(2,1)S(1)} %fusion.63), channel_id=1, source_target_pairs={{0,2},{1,3},{2,0},{3,1},{4,6},{5,7},{6,4},{7,5},{8,10},{9,11},{10,... | collective-permute-start | bytes 98312 | tf_op jit(solution)/shard_map/ppermute | solution.py:164
  151.7 4.8 %collective-permute-start.12 = (f32[1025]{0:T(1024)S(1)}, f32[1025]{0:T(1024)S(1)}, u32[]{:S(2)}, u32[]{:S(2)}) collective-permute-start(f32[1025]{0:T(1024)S(1)} %add.317), channel_id=1, source_target_pairs={{0,2},{1,3},{2,0},{3,1},{4,6},{5,7},{6,4},{7,5},{8,10},{9,11},{10,... | collective-permute-start | bytes 12308 | tf_op jit(solution)/shard_map/ppermute | solution.py:166
  154.4 5.6 %collective-permute-start.17 = (bf16[32,1536]{1,0:T(8,128)(2,1)S(1)}, bf16[32,1536]{1,0:T(8,128)(2,1)S(1)}, u32[]{:S(2)}, u32[]{:S(2)}) collective-permute-start(bf16[32,1536]{1,0:T(8,128)(2,1)S(1)} %fusion.60), channel_id=1, source_target_pairs={{0,2},{1,3},{2,0},{3,1},{4,6},{5,7},{6,4},{7,5},{8,10},{9,11},{10,... | collective-permute-start | bytes 294920 | tf_op jit(solution)/shard_map/ppermute | solution.py:166
  (23 other events, 43.9 us)

commit v19 on v16

--- a/solution.py
+++ b/solution.py
@@ -121,22 +121,38 @@
 def halving_scatter(grad, small=None):
     seq_bits, clip_bits = exchange_bits()
     total = seq_bits + clip_bits
+    seq_n = lax.axis_size("seq")
+    clip_n = lax.axis_size("clip")
     data = grad.reshape([2] * total + [-1, grad.shape[1]])
-    order_a = list(range(seq_bits))
-    order_b = [0] + list(range(seq_bits - 1, 0, -1))
-    core_bit = lax.axis_index("seq") & 1
-    left_a = list(range(seq_bits))
-    left_b = list(range(seq_bits))
-    for step in range(seq_bits):
-        bit_a, bit_b = order_a[step], order_b[step]
-        dim_a, dim_b = left_a.index(bit_a), left_b.index(bit_b)
-        me = lax.axis_index("seq")
-        mine_a = (me >> bit_a) & 1
-        mine_b = (me >> bit_b) & 1
+    seq_keys = [("seq", bit) for bit in range(seq_bits)]
+    clip_keys = [("clip", bit) for bit in range(clip_bits)]
+    order_a = seq_keys + clip_keys
+    order_b = [seq_keys[0]] + seq_keys[1:][::-1][:1] + clip_keys[:1] + seq_keys[1:][::-1][1:] + clip_keys[1:]
+    me_seq = lax.axis_index("seq")
+    me_clip = lax.axis_index("clip")
+    core_bit = me_seq & 1
+    left_a = list(order_a)
+    left_b = list(order_a)
+
+    def own_bit(key):
+        axis, bit = key
+        return ((me_seq if axis == "seq" else me_clip) >> bit) & 1
+
+    def flip(seq_i, clip_i, key):
+        axis, bit = key
+        if axis == "seq":
+            return (seq_i ^ (1 << bit)) * clip_n + clip_i
+        return seq_i * clip_n + (clip_i ^ (1 << bit))
+
+    for step in range(total):
+        key_a, key_b = order_a[step], order_b[step]
+        dim_a, dim_b = left_a.index(key_a), left_b.index(key_b)
+        mine_a, mine_b = own_bit(key_a), own_bit(key_b)
         pairs = []
-        for src in range(lax.axis_size("seq")):
-            bit = bit_a if (src & 1) == 0 else bit_b
-            pairs.append((src, src ^ (1 << bit)))
+        for seq_i in range(seq_n):
+            for clip_i in range(clip_n):
+                key = key_a if (seq_i & 1) == 0 else key_b
+                pairs.append((seq_i * clip_n + clip_i, flip(seq_i, clip_i, key)))
         keep = jnp.where(
             core_bit == 0,
             lax.dynamic_index_in_dim(data, mine_a, axis=dim_a, keepdims=False),
@@ -150,20 +166,9 @@
         left_a.pop(dim_a)
         left_b.pop(dim_b)
         if small is None:
-            got = lax.ppermute(give.astype(jnp.bfloat16), "seq", pairs)
+            got = lax.ppermute(give.astype(jnp.bfloat16), ("seq", "clip"), pairs)
         else:
-            got, got_small = lax.ppermute((give.astype(jnp.bfloat16), small), "seq", pairs)
-            small = small + got_small
-        data = keep + got.astype(jnp.float32)
-    for bit in range(clip_bits):
-        mine = (lax.axis_index("clip") >> bit) & 1
-        pairs = [(src, src ^ (1 << bit)) for src in range(lax.axis_size("clip"))]
-        keep = lax.dynamic_index_in_dim(data, mine, axis=0, keepdims=False)
-        give = lax.dynamic_index_in_dim(data, 1 - mine, axis=0, keepdims=False)
-        if small is None:
-            got = lax.ppermute(give.astype(jnp.bfloat16), "clip", pairs)
-        else:
-            got, got_small = lax.ppermute((give.astype(jnp.bfloat16), small), "clip", pairs)
+            got, got_small = lax.ppermute((give.astype(jnp.bfloat16), small), ("seq", "clip"), pairs)
             small = small + got_small
         data = keep + got.astype(jnp.float32)
     return data, small

time: 162 us -> 162 us (level)
  no operation moved by 1% of the time
where the time goes in v19:
time: 162 us; the launch traced here: 161 us
  waiting for transfers between devices  53.1 us (33%)
  starting transfers between devices  32.5 us (20%)
  local copies, waits for them, and re-layouts  31.9 us (20%)
  matrix products  20.2 us (12%)
  other arithmetic  20.1 us (12%)
  between operations  3.11 us (2%)
    ppermute x10, waiting for transfers between devices, halving_scatter(): lax.ppermute((give.astype(jnp.bfloat16), small), ('seq', 'clip'), pairs)  13.4 us
    ppermute x3, waiting for transfers between devices, return_blocks(): sent = lax.ppermute(summed[k].astype(jnp.bfloat16), 'seq', xor_pairs(2 * k))  12.6 us
    all_to_all x1, waiting for transfers between devices, per_device(): lax.all_to_all(jnp.concatenate([send_tokens, send_target], axis=2), 'seq'...  12.3 us
    ppermute x3, waiting for transfers between devices, gather_blocks(): lax.ppermute(block, 'seq', xor_pairs(2 * k))  9.21 us
    unnamed x65, local copies, waits for them, and re-layouts  9.2 us
    ppermute x10, starting transfers between devices, halving_scatter(): lax.ppermute((give.astype(jnp.bfloat16), small), ('seq', 'clip'), pairs)  8.68 us
    ppermute x5, starting transfers between devices, halving_scatter(): got = lax.ppermute(give.astype(jnp.bfloat16), ('seq', 'clip'), pairs)  7.45 us
    all_to_all x1, starting transfers between devices, per_device(): lax.all_to_all(jnp.broadcast_to(kept_count.reshape(1, 1), (shards, 1)), '...  5.17 us
  transfers between devices with their start and end apart: 25, of which 16 were waited for; matrix products, arithmetic and copies ran while one was open for 15% of the time, Pallas kernels for 0%

profile of v19, /device:TPU:0, one launch (start us, length us, event | category | flops | bytes accessed | tf_op | source)
XLA Modules:
  0.0 161.0 jit_solution(4921422198894999363)
XLA Ops:
  3.4 5.2 %all-to-all-start = ((s32[8,1,1]{2,1,0:T(1,128)}), s32[8,1,1]{2,1,0:T(1,128)S(1)}, u32[]{:S(2)}, u32[]{:S(2)}) async-start(s32[8,1,1]{2,1,0:T(1,128)} %broadcast_in_dim.47), calls=%async_computation | async-start | bytes 8192 | tf_op jit(solution)/shard_map/all_to_all | solution.py:211
  9.2 3.9 %all-to-all-done = s32[8,1,1]{2,1,0:T(1,128)S(1)} async-done(((s32[8,1,1]{2,1,0:T(1,128)}), s32[8,1,1]{2,1,0:T(1,128)S(1)}, u32[]{:S(2)}, u32[]{:S(2)}) %all-to-all-start) | async-done | bytes 64 | tf_op jit(solution)/shard_map/all_to_all | solution.py:211
  21.0 3.5 %all-to-all-start.1 = ((bf16[8,24,2048]{2,1,0:T(8,128)(2,1)}), bf16[8,24,2048]{2,1,0:T(8,128)(2,1)S(1)}, u32[]{:S(2)}, u32[]{:S(2)}) async-start(bf16[8,24,2048]{2,1,0:T(8,128)(2,1)} %pad_maximum_fusion.2), calls=%async_computation.1 | async-start | bytes 1572864 | tf_op jit(solution)/shard_map/all_to_all | solution.py:228
  24.9 12.3 %all-to-all-done.1 = bf16[8,24,2048]{2,1,0:T(8,128)(2,1)S(1)} async-done(((bf16[8,24,2048]{2,1,0:T(8,128)(2,1)}), bf16[8,24,2048]{2,1,0:T(8,128)(2,1)S(1)}, u32[]{:S(2)}, u32[]{:S(2)}) %all-to-all-start.1) | async-done | bytes 786464 | tf_op jit(solution)/shard_map/all_to_all | solution.py:228
  37.1 1.8 %scatter_custom_fusion = bf16[128,2048]{1,0:T(8,128)(2,1)S(1)} fusion(s32[192]{0:T(256)S(1)} %bitcast.244, bf16[192,2048]{1,0:T(8,128)(2,1)S(1)} %bitcast.235, bf16[]{:T(256)} %constant.177.clone.1), kind=kCustom, calls=%fused_computation.111 | custom fusion | bytes 524290 | tf_op jit(solution)/shard_map/scatter | solution.py:238
  39.6 2.1 %fusion.19 = bf16[128,1024]{1,0:T(8,128)(2,1)S(1)} fusion(bf16[128,1024]{1,0:T(8,128)(2,1)S(1)} %fusion.32, bf16[1024,1536]{1,0:T(8,128)(2,1)} %param.9), kind=kOutput, calls=%fused_computation.32 | convolution fusion | flops 268566528 | bytes 2621440 | tf_op jit(solution)/shard_map/dot_general | solution.py:252
  45.3 6.2 %collective-permute-done.2 = bf16[1024,128]{0,1:T(8,128)(2,1)S(1)} collective-permute-done((bf16[1024,128]{0,1:T(8,128)(2,1)S(1)}, bf16[1024,128]{0,1:T(8,128)(2,1)S(1)}, u32[]{:S(2)}, u32[]{:S(2)}) %collective-permute-start.2) | collective-permute-done | bytes 262176 | tf_op jit(solution)/shard_map/ppermute | solution.py:184
  51.5 2.8 %collective-permute-done.1 = bf16[1024,128]{0,1:T(8,128)(2,1)S(1)} collective-permute-done((bf16[1024,128]{0,1:T(8,128)(2,1)S(1)}, bf16[1024,128]{0,1:T(8,128)(2,1)S(1)}, u32[]{:S(2)}, u32[]{:S(2)}) %collective-permute-start.1) | collective-permute-done | bytes 262176 | tf_op jit(solution)/shard_map/ppermute | solution.py:184
  55.9 1.5 convolution_convert_fusion.1
  59.9 1.8 %copy.71 = bf16[1024,128]{1,0:T(8,128)(2,1)} copy(bf16[1024,128]{0,1:T(8,128)(2,1)} %copy-done.16) | data formatting | bytes 524288 | tf_op jit(solution)/shard_map/ppermute | solution.py:184
  62.7 2.3 %copy.74 = bf16[4,1024,128]{2,1,0:T(8,128)(2,1)} copy(bf16[4,1024,128]{1,2,0:T(8,128)(2,1)} %collective-permute-done.3) | data formatting | bytes 2097152 | tf_op jit(solution)/shard_map/ppermute | solution.py:186
  69.2 1.6 %fusion.52 = (bf16[128,8,64]{0,2,1:T(8,128)(2,1)S(1)}, f32[8,128,64,1]{1,2,0,3:T(8,128)}) fusion(f32[128,8]{0,1:T(8,128)S(1)} %bitcast.241, f32[8,8,128,128]{2,3,1,0:T(8,128)S(1)} %get-tuple-element.30, f32[8,128]{1,0:T(8,128)S(1)} %get-tuple-element.29, bf16[8,8,2,64,128]{4,3,2,1,0:T(8,128)(2,1)S(1)} %constant_dynamic-update-slice_fusion), kind=kOutput, calls=%fused_computation.102 | convolution fusion | flops 137494528 | bytes 5644288 | tf_op jit(solution)/shard_map/ihqt,ihdt->ihqd/dot_general | solution.py:267
  73.4 3.9 %fusion.16 = bf16[8,8,64,128]{3,2,1,0:T(8,128)(2,1)S(1)} fusion(f32[8,8,128,128]{2,3,1,0:T(8,128)} %copy-done.2, f32[8,128]{1,0:T(8,128)S(1)} %log_add_fusion, bf16[8,128,64]{1,2,0:T(8,128)(2,1)S(1)} %bitcast.216), kind=kOutput, calls=%fused_computation.29 | convolution fusion | flops 137887744 | bytes 5378048 | tf_op jit(solution)/shard_map/ihqd,ihqt->ihdt/dot_general | solution.py:295
  77.3 2.6 %multiply_convert_fusion = bf16[8,8,128,128]{2,3,1,0:T(8,128)(2,1)S(1)} fusion(f32[8,8,128,128]{2,3,1,0:T(8,128)S(1)} %copy-done.3, f32[8,128]{1,0:T(8,128)S(1)} %multiply_reduce_fusion.4, f32[8,128]{1,0:T(8,128)S(1)} %log_add_fusion, bf16[8,8,2,64,128]{4,3,2,1,0:T(8,128)(2,1)} %copy-done.9, bf16[8,128,64]{1,2,0:T(8,128)(2,1)S(1)} %bitcast.217), kind=kOutput, calls=%fused_computation.5 | convolution fusion | flops 139460608 | bytes 7479296 | tf_op jit(solution)/shard_map/ihqd,ihdt->ihqt/dot_general | solution.py:298
  79.9 1.5 multiply_convert_fusion.1
  87.5 1.6 %fusion.74 = (bf16[4,1024,128]{2,1,0:T(8,128)(2,1)S(1)}, f32[4,1024,128]{2,1,0:T(8,128)S(1)}) fusion(bf16[4,1024,128]{2,1,0:T(8,128)(2,1)} %collective-permute-done.4, f32[4,8,2,64,128]{4,3,2,1,0:T(8,128)S(1)} %copy.87), kind=kLoop, calls=%fused_computation.170 | loop fusion | flops 1572864 | bytes 6291456 | tf_op jit(solution)/shard_map/convert.6
  89.2 1.9 %collective-permute-start.5 = (bf16[1024,128]{1,0:T(8,128)(2,1)S(1)}, bf16[1024,128]{1,0:T(8,128)(2,1)S(1)}, u32[]{:S(2)}, u32[]{:S(2)}) collective-permute-start(bf16[1024,128]{1,0:T(8,128)(2,1)S(1)} %get-tuple-element.12), channel_id=1, source_target_pairs={{0,8},{4,12},{8,0},{12,4},{16,24},{20,28},{24,16},{28,20},{1,9},{5... | collective-permute-start | bytes 786440 | tf_op jit(solution)/shard_map/ppermute | solution.py:196
  93.3 5.1 %collective-permute-done.5 = bf16[1024,128]{1,0:T(8,128)(2,1)S(1)} collective-permute-done((bf16[1024,128]{1,0:T(8,128)(2,1)S(1)}, bf16[1024,128]{1,0:T(8,128)(2,1)S(1)}, u32[]{:S(2)}, u32[]{:S(2)}) %collective-permute-start.5) | collective-permute-done | bytes 262176 | tf_op jit(solution)/shard_map/ppermute | solution.py:196
  98.4 6.1 %collective-permute-done.7 = bf16[1024,128]{1,0:T(8,128)(2,1)S(1)} collective-permute-done((bf16[1024,128]{1,0:T(8,128)(2,1)S(1)}, bf16[1024,128]{1,0:T(8,128)(2,1)S(1)}, u32[]{:S(2)}, u32[]{:S(2)}) %collective-permute-start.7) | collective-permute-done | bytes 262176 | tf_op jit(solution)/shard_map/ppermute | solution.py:196
  107.0 2.6 %copy-done.6 = f32[2,2,2,2,2,32,1536]{6,5,4,3,2,1,0:T(8,128)} copy-done((f32[2,2,2,2,2,32,1536]{6,5,4,3,2,1,0:T(8,128)}, f32[2,2,2,2,2,32,1536]{6,5,4,3,2,1,0:T(8,128)S(1)}, u32[]{:S(2)}) %copy-start.6) | copy-done | bytes 6291480
  113.7 1.5 collective-permute-done.18
  116.7 1.7 %collective-permute-start.19 = (bf16[2,2,2,16,1024]{4,3,2,1,0:T(8,128)(2,1)S(1)}, bf16[2,2,2,16,1024]{4,3,2,1,0:T(8,128)(2,1)S(1)}, u32[]{:S(2)}, u32[]{:S(2)}) collective-permute-start(bf16[2,2,2,16,1024]{4,3,2,1,0:T(8,128)(2,1)S(1)} %fusion.41), channel_id=1, source_target_pairs={{0,8},{1,9},{2,10},{3,11},{4,20},{5,21},{6,22},{7,23},{8,0},{9,1},... | collective-permute-start | bytes 786440 | tf_op jit(solution)/shard_map/ppermute | solution.py:169
  118.4 2.9 %bitcast_add_fusion = f32[2,2,2,2,32,1536]{5,4,3,2,1,0:T(8,128)S(1)} fusion(bf16[2,2,2,2,32,1536]{5,4,3,2,1,0:T(8,128)(2,1)} %collective-permute-done.13, f32[2,2,2,2,2,32,1536]{6,5,4,3,2,1,0:T(8,128)} %copy-done.6, s32[]{:T(128)S(6)} %select_n.279), kind=kLoop, calls=%fused_computation.12 | loop fusion | flops 1572864 | bytes 7864324 | tf_op jit(solution)/shard_map/add | solution.py:173
  121.3 1.6 %copy-done.4 = f32[2,2,2,2,32,1536]{5,4,3,2,1,0:T(8,128)} copy-done((f32[2,2,2,2,32,1536]{5,4,3,2,1,0:T(8,128)}, f32[2,2,2,2,32,1536]{5,4,3,2,1,0:T(8,128)S(1)}, u32[]{:S(2)}) %copy-start.4) | copy-done | bytes 3145752
  125.4 3.1 %fusion.22 = f32[1024]{0:T(1024)S(1)} fusion(bf16[1024,1536]{1,0:T(8,128)(2,1)} %param.9, f32[128]{0:T(128)S(1)} %copy-done.29, f32[128]{0:T(128)S(1)} %broadcast_multiply_fusion.1, bf16[1024,128]{1,0:T(8,128)(2,1)S(1)} %fusion.40, bf16[512,128]{1,0:T(8,128)(2,1)S(1)} %bitcast.237, bf16[128,2048]{1,0:T(8,128)(2,1)S(1)} %scatter_custom_fusion), kind=kOutput, calls=%fused_computation.33 | convolution fusion | flops 404093952 | bytes 3806208 | tf_op jit(solution)/shard_map/ct,fc->tf/dot_general | solution.py:314
  129.7 6.5 %collective-permute-done.14 = bf16[2,2,2,32,1536]{4,3,2,1,0:T(8,128)(2,1)S(1)} collective-permute-done((bf16[2,2,2,32,1536]{4,3,2,1,0:T(8,128)(2,1)}, bf16[2,2,2,32,1536]{4,3,2,1,0:T(8,128)(2,1)S(1)}, u32[]{:S(2)}, u32[]{:S(2)}) %collective-permute-start.14) | collective-permute-done | bytes 786464 | tf_op jit(solution)/shard_map/ppermute | solution.py:171
  138.6 1.6 %collective-permute-start.21 = (bf16[2,16,1024]{2,1,0:T(8,128)(2,1)S(1)}, bf16[2,16,1024]{2,1,0:T(8,128)(2,1)S(1)}, u32[]{:S(2)}, u32[]{:S(2)}) collective-permute-start(bf16[2,16,1024]{2,1,0:T(8,128)(2,1)S(1)} %fusion.63), channel_id=1, source_target_pairs={{0,1},{1,0},{2,3},{3,2},{4,12},{5,13},{6,14},{7,15},{8,9},{9,8},{1... | collective-permute-start | bytes 196616 | tf_op jit(solution)/shard_map/ppermute | solution.py:169
  140.2 1.6 %collective-permute-done.9 = f32[1025]{0:T(1024)S(1)} collective-permute-done((f32[1025]{0:T(1024)S(1)}, f32[1025]{0:T(1024)S(1)}, u32[]{:S(2)}, u32[]{:S(2)}) %collective-permute-start.9) | collective-permute-done | bytes 4132 | tf_op jit(solution)/shard_map/ppermute | solution.py:171
  144.8 1.6 collective-permute-start.16
  147.1 2.6 %collective-permute-start.22 = (bf16[16,1024]{1,0:T(8,128)(2,1)S(1)}, bf16[16,1024]{1,0:T(8,128)(2,1)S(1)}, u32[]{:S(2)}, u32[]{:S(2)}) collective-permute-start(bf16[16,1024]{1,0:T(8,128)(2,1)S(1)} %fusion.65), channel_id=1, source_target_pairs={{0,2},{1,3},{2,0},{3,1},{4,6},{5,7},{6,4},{7,5},{8,10},{9,11},{10,... | collective-permute-start | bytes 98312 | tf_op jit(solution)/shard_map/ppermute | solution.py:169
  151.0 2.5 %collective-permute-start.12 = (f32[1025]{0:T(1024)S(1)}, f32[1025]{0:T(1024)S(1)}, u32[]{:S(2)}, u32[]{:S(2)}) collective-permute-start(f32[1025]{0:T(1024)S(1)} %add.327), channel_id=1, source_target_pairs={{0,2},{1,3},{2,0},{3,1},{4,6},{5,7},{6,4},{7,5},{8,10},{9,11},{10,... | collective-permute-start | bytes 12308 | tf_op jit(solution)/shard_map/ppermute | solution.py:171
  157.4 1.8 %collective-permute-done.17 = bf16[32,1536]{1,0:T(8,128)(2,1)S(1)} collective-permute-done((bf16[32,1536]{1,0:T(8,128)(2,1)S(1)}, bf16[32,1536]{1,0:T(8,128)(2,1)S(1)}, u32[]{:S(2)}, u32[]{:S(2)}) %collective-permute-start.17) | collective-permute-done | bytes 98336 | tf_op jit(solution)/shard_map/ppermute | solution.py:171
  (180 shorter events, 58.6 us)
Async XLA Ops:
  0.6 15.1 %copy-start = (bf16[1,512,1024]{2,1,0:T(8,128)(2,1)S(1)}, bf16[1,512,1024]{2,1,0:T(8,128)(2,1)}, u32[]{:S(2)}) copy-start(bf16[1,512,1024]{2,1,0:T(8,128)(2,1)} %param.7) | copy-start | bytes 3145732
  0.6 16.1 %copy-start.7 = (bf16[1,512,1024]{2,1,0:T(8,128)(2,1)S(1)}, bf16[1,512,1024]{2,1,0:T(8,128)(2,1)}, u32[]{:S(2)}) copy-start(bf16[1,512,1024]{2,1,0:T(8,128)(2,1)} %param.6) | copy-start | bytes 3145732
  3.4 9.8 %all-to-all-start = ((s32[8,1,1]{2,1,0:T(1,128)}), s32[8,1,1]{2,1,0:T(1,128)S(1)}, u32[]{:S(2)}, u32[]{:S(2)}) async-start(s32[8,1,1]{2,1,0:T(1,128)} %broadcast_in_dim.47), calls=%async_computation | async-start | bytes 8192 | tf_op jit(solution)/shard_map/all_to_all | solution.py:211
  20.1 19.2 %copy-start.19 = (f32[1024]{0:T(1024)S(1)}, f32[1024]{0:T(1024)}, u32[]{:S(2)}) copy-start(f32[1024]{0:T(1024)} %param.11) | copy-start | bytes 12292
  21.0 16.1 %all-to-all-start.1 = ((bf16[8,24,2048]{2,1,0:T(8,128)(2,1)}), bf16[8,24,2048]{2,1,0:T(8,128)(2,1)S(1)}, u32[]{:S(2)}, u32[]{:S(2)}) async-start(bf16[8,24,2048]{2,1,0:T(8,128)(2,1)} %pad_maximum_fusion.2), calls=%async_computation.1 | async-start | bytes 1572864 | tf_op jit(solution)/shard_map/all_to_all | solution.py:228
  39.6 16.3 %copy-start.12 = (bf16[128,1024]{1,0:T(8,128)(2,1)}, bf16[128,1024]{1,0:T(8,128)(2,1)S(1)}, u32[]{:S(2)}) copy-start(bf16[128,1024]{1,0:T(8,128)(2,1)S(1)} %fusion.32) | copy-start | bytes 786436
  41.7 9.7 %collective-permute-start.2 = (bf16[1024,128]{0,1:T(8,128)(2,1)S(1)}, bf16[1024,128]{0,1:T(8,128)(2,1)S(1)}, u32[]{:S(2)}, u32[]{:S(2)}) collective-permute-start(bf16[1024,128]{0,1:T(8,128)(2,1)S(1)} %bitcast.229), channel_id=1, source_target_pairs={{0,24},{4,28},{8,16},{12,20},{16,8},{20,12},{24,0},{28,4},{1,25},{... | collective-permute-start | bytes 786440 | tf_op jit(solution)/shard_map/ppermute | solution.py:184
  42.4 11.9 %collective-permute-start.1 = (bf16[1024,128]{0,1:T(8,128)(2,1)S(1)}, bf16[1024,128]{0,1:T(8,128)(2,1)S(1)}, u32[]{:S(2)}, u32[]{:S(2)}) collective-permute-start(bf16[1024,128]{0,1:T(8,128)(2,1)S(1)} %bitcast.230), channel_id=1, source_target_pairs={{0,16},{4,20},{8,24},{12,28},{16,0},{20,4},{24,8},{28,12},{1,17},{... | collective-permute-start | bytes 786440 | tf_op jit(solution)/shard_map/ppermute | solution.py:184
  43.8 10.7 %collective-permute-start = (bf16[1024,128]{0,1:T(8,128)(2,1)S(1)}, bf16[1024,128]{0,1:T(8,128)(2,1)S(1)}, u32[]{:S(2)}, u32[]{:S(2)}) collective-permute-start(bf16[1024,128]{0,1:T(8,128)(2,1)S(1)} %bitcast.231), channel_id=1, source_target_pairs={{0,8},{4,12},{8,0},{12,4},{16,24},{20,28},{24,16},{28,20},{1,9},{5... | collective-permute-start | bytes 786440 | tf_op jit(solution)/shard_map/ppermute | solution.py:184
  55.6 7.1 %collective-permute-start.3 = (bf16[4,1024,128]{1,2,0:T(8,128)(2,1)}, bf16[4,1024,128]{1,2,0:T(8,128)(2,1)}, u32[]{:S(2)}, u32[]{:S(2)}) collective-permute-start(bf16[4,1024,128]{1,2,0:T(8,128)(2,1)} %pad_maximum_fusion), channel_id=1, source_target_pairs={{0,4},{4,0},{8,12},{12,8},{16,20},{20,16},{24,28},{28,24},{1,5},{5... | collective-permute-start | bytes 3145736 | tf_op jit(solution)/shard_map/ppermute | solution.py:186
  57.6 14.6 %copy-start.20 = (f32[128]{0:T(128)}, f32[128]{0:T(128)S(1)}, u32[]{:S(2)}) copy-start(f32[128]{0:T(128)S(1)} %add_rsqrt_fusion) | copy-start | bytes 1540
  84.4 3.1 %collective-permute-start.4 = (bf16[4,1024,128]{2,1,0:T(8,128)(2,1)}, bf16[4,1024,128]{2,1,0:T(8,128)(2,1)}, u32[]{:S(2)}, u32[]{:S(2)}) collective-permute-start(bf16[4,1024,128]{2,1,0:T(8,128)(2,1)} %bitcast.36), channel_id=1, source_target_pairs={{0,4},{4,0},{8,12},{12,8},{16,20},{20,16},{24,28},{28,24},{1,5},{5... | collective-permute-start | bytes 3145736 | tf_op jit(solution)/shard_map/ppermute | solution.py:192
  89.2 9.2 %collective-permute-start.5 = (bf16[1024,128]{1,0:T(8,128)(2,1)S(1)}, bf16[1024,128]{1,0:T(8,128)(2,1)S(1)}, u32[]{:S(2)}, u32[]{:S(2)}) collective-permute-start(bf16[1024,128]{1,0:T(8,128)(2,1)S(1)} %get-tuple-element.12), channel_id=1, source_target_pairs={{0,8},{4,12},{8,0},{12,4},{16,24},{20,28},{24,16},{28,20},{1,9},{5... | collective-permute-start | bytes 786440 | tf_op jit(solution)/shard_map/ppermute | solution.py:196
  91.1 13.3 %collective-permute-start.7 = (bf16[1024,128]{1,0:T(8,128)(2,1)S(1)}, bf16[1024,128]{1,0:T(8,128)(2,1)S(1)}, u32[]{:S(2)}, u32[]{:S(2)}) collective-permute-start(bf16[1024,128]{1,0:T(8,128)(2,1)S(1)} %get-tuple-element.13), channel_id=1, source_target_pairs={{0,24},{4,28},{8,16},{12,20},{16,8},{20,12},{24,0},{28,4},{1,25},{... | collective-permute-start | bytes 786440 | tf_op jit(solution)/shard_map/ppermute | solution.py:196
  92.2 13.8 %copy-start.17 = (bf16[128,1024]{0,1:T(8,128)(2,1)S(1)}, bf16[128,1024]{0,1:T(8,128)(2,1)}, u32[]{:S(2)}) copy-start(bf16[128,1024]{0,1:T(8,128)(2,1)} %copy.89) | copy-start | bytes 786436
  92.2 13.7 %collective-permute-start.6 = (bf16[1024,128]{1,0:T(8,128)(2,1)S(1)}, bf16[1024,128]{1,0:T(8,128)(2,1)S(1)}, u32[]{:S(2)}, u32[]{:S(2)}) collective-permute-start(bf16[1024,128]{1,0:T(8,128)(2,1)S(1)} %get-tuple-element.14), channel_id=1, source_target_pairs={{0,16},{4,20},{8,24},{12,28},{16,0},{20,4},{24,8},{28,12},{1,17},{... | collective-permute-start | bytes 786440 | tf_op jit(solution)/shard_map/ppermute | solution.py:196
  111.1 7.3 %collective-permute-start.13 = (bf16[2,2,2,2,32,1536]{5,4,3,2,1,0:T(8,128)(2,1)}, bf16[2,2,2,2,32,1536]{5,4,3,2,1,0:T(8,128)(2,1)}, u32[]{:S(2)}, u32[]{:S(2)}) collective-permute-start(bf16[2,2,2,2,32,1536]{5,4,3,2,1,0:T(8,128)(2,1)} %fusion.13), channel_id=1, source_target_pairs={{0,4},{1,5},{2,6},{3,7},{4,0},{5,1},{6,2},{7,3},{8,12},{9,13},{10,... | collective-permute-start | bytes 4718600 | tf_op jit(solution)/shard_map/ppermute | solution.py:171
  113.1 2.1 %collective-permute-start.18 = (bf16[2,2,2,2,16,1024]{5,4,3,2,1,0:T(8,128)(2,1)S(1)}, bf16[2,2,2,2,16,1024]{5,4,3,2,1,0:T(8,128)(2,1)S(1)}, u32[]{:S(2)}, u32[]{:S(2)}) collective-permute-start(bf16[2,2,2,2,16,1024]{5,4,3,2,1,0:T(8,128)(2,1)S(1)} %fusion.36), channel_id=1, source_target_pairs={{0,4},{1,5},{2,6},{3,7},{4,0},{5,1},{6,2},{7,3},{8,12},{9,13},{10,... | collective-permute-start | bytes 1572872 | tf_op jit(solution)/shard_map/ppermute | solution.py:169
  116.7 7.7 %collective-permute-start.19 = (bf16[2,2,2,16,1024]{4,3,2,1,0:T(8,128)(2,1)S(1)}, bf16[2,2,2,16,1024]{4,3,2,1,0:T(8,128)(2,1)S(1)}, u32[]{:S(2)}, u32[]{:S(2)}) collective-permute-start(bf16[2,2,2,16,1024]{4,3,2,1,0:T(8,128)(2,1)S(1)} %fusion.41), channel_id=1, source_target_pairs={{0,8},{1,9},{2,10},{3,11},{4,20},{5,21},{6,22},{7,23},{8,0},{9,1},... | collective-permute-start | bytes 786440 | tf_op jit(solution)/shard_map/ppermute | solution.py:169
  124.0 12.2 %collective-permute-start.14 = (bf16[2,2,2,32,1536]{4,3,2,1,0:T(8,128)(2,1)}, bf16[2,2,2,32,1536]{4,3,2,1,0:T(8,128)(2,1)S(1)}, u32[]{:S(2)}, u32[]{:S(2)}) collective-permute-start(bf16[2,2,2,32,1536]{4,3,2,1,0:T(8,128)(2,1)} %fusion.14), channel_id=1, source_target_pairs={{0,8},{1,9},{2,10},{3,11},{4,20},{5,21},{6,22},{7,23},{8,0},{9,1},... | collective-permute-start | bytes 2359304 | tf_op jit(solution)/shard_map/ppermute | solution.py:171
  124.5 12.9 %collective-permute-start.20 = (bf16[2,2,16,1024]{3,2,1,0:T(8,128)(2,1)S(1)}, bf16[2,2,16,1024]{3,2,1,0:T(8,128)(2,1)S(1)}, u32[]{:S(2)}, u32[]{:S(2)}) collective-permute-start(bf16[2,2,16,1024]{3,2,1,0:T(8,128)(2,1)S(1)} %fusion.53), channel_id=1, source_target_pairs={{0,16},{1,17},{2,18},{3,19},{4,5},{5,4},{6,7},{7,6},{8,24},{9,25},... | collective-permute-start | bytes 393224 | tf_op jit(solution)/shard_map/ppermute | solution.py:169
  129.1 8.3 %collective-permute-start.8 = (f32[1025]{0:T(1024)S(1)}, f32[1025]{0:T(1024)S(1)}, u32[]{:S(2)}, u32[]{:S(2)}) collective-permute-start(f32[1025]{0:T(1024)S(1)} %pad_maximum_fusion.6), channel_id=1, source_target_pairs={{0,4},{1,5},{2,6},{3,7},{4,0},{5,1},{6,2},{7,3},{8,12},{9,13},{10,... | collective-permute-start | bytes 12308 | tf_op jit(solution)/shard_map/ppermute | solution.py:171
  136.7 7.9 %collective-permute-start.15 = (bf16[2,2,32,1536]{3,2,1,0:T(8,128)(2,1)S(1)}, bf16[2,2,32,1536]{3,2,1,0:T(8,128)(2,1)S(1)}, u32[]{:S(2)}, u32[]{:S(2)}) collective-permute-start(bf16[2,2,32,1536]{3,2,1,0:T(8,128)(2,1)S(1)} %fusion.27), channel_id=1, source_target_pairs={{0,16},{1,17},{2,18},{3,19},{4,5},{5,4},{6,7},{7,6},{8,24},{9,25},... | collective-permute-start | bytes 1179656 | tf_op jit(solution)/shard_map/ppermute | solution.py:171
  138.1 3.7 %collective-permute-start.9 = (f32[1025]{0:T(1024)S(1)}, f32[1025]{0:T(1024)S(1)}, u32[]{:S(2)}, u32[]{:S(2)}) collective-permute-start(f32[1025]{0:T(1024)S(1)} %fusion.69), channel_id=1, source_target_pairs={{0,8},{1,9},{2,10},{3,11},{4,20},{5,21},{6,22},{7,23},{8,0},{9,1},... | collective-permute-start | bytes 12308 | tf_op jit(solution)/shard_map/ppermute | solution.py:171
  138.6 7.8 %collective-permute-start.21 = (bf16[2,16,1024]{2,1,0:T(8,128)(2,1)S(1)}, bf16[2,16,1024]{2,1,0:T(8,128)(2,1)S(1)}, u32[]{:S(2)}, u32[]{:S(2)}) collective-permute-start(bf16[2,16,1024]{2,1,0:T(8,128)(2,1)S(1)} %fusion.63), channel_id=1, source_target_pairs={{0,1},{1,0},{2,3},{3,2},{4,12},{5,13},{6,14},{7,15},{8,9},{9,8},{1... | collective-permute-start | bytes 196616 | tf_op jit(solution)/shard_map/ppermute | solution.py:169
  141.8 4.6 %collective-permute-start.10 = (f32[1025]{0:T(1024)S(1)}, f32[1025]{0:T(1024)S(1)}, u32[]{:S(2)}, u32[]{:S(2)}) collective-permute-start(f32[1025]{0:T(1024)S(1)} %add.325), channel_id=1, source_target_pairs={{0,16},{1,17},{2,18},{3,19},{4,5},{5,4},{6,7},{7,6},{8,24},{9,25},... | collective-permute-start | bytes 12308 | tf_op jit(solution)/shard_map/ppermute | solution.py:171
  144.6 15.3 %copy-start.1 = (bf16[1,512,1024]{2,1,0:T(8,128)(2,1)S(1)}, bf16[1,512,1024]{2,1,0:T(8,128)(2,1)}, u32[]{:S(2)}) copy-start(bf16[1,512,1024]{2,1,0:T(8,128)(2,1)} %param.7) | copy-start | bytes 3145732
  144.8 8.7 %collective-permute-start.16 = (bf16[2,32,1536]{2,1,0:T(8,128)(2,1)S(1)}, bf16[2,32,1536]{2,1,0:T(8,128)(2,1)S(1)}, u32[]{:S(2)}, u32[]{:S(2)}) collective-permute-start(bf16[2,32,1536]{2,1,0:T(8,128)(2,1)S(1)} %fusion.59), channel_id=1, source_target_pairs={{0,1},{1,0},{2,3},{3,2},{4,12},{5,13},{6,14},{7,15},{8,9},{9,8},{1... | collective-permute-start | bytes 589832 | tf_op jit(solution)/shard_map/ppermute | solution.py:171
  146.4 4.6 %collective-permute-start.11 = (f32[1025]{0:T(1024)S(1)}, f32[1025]{0:T(1024)S(1)}, u32[]{:S(2)}, u32[]{:S(2)}) collective-permute-start(f32[1025]{0:T(1024)S(1)} %add.326), channel_id=1, source_target_pairs={{0,1},{1,0},{2,3},{3,2},{4,12},{5,13},{6,14},{7,15},{8,9},{9,8},{1... | collective-permute-start | bytes 12308 | tf_op jit(solution)/shard_map/ppermute | solution.py:171
  147.1 7.0 %collective-permute-start.22 = (bf16[16,1024]{1,0:T(8,128)(2,1)S(1)}, bf16[16,1024]{1,0:T(8,128)(2,1)S(1)}, u32[]{:S(2)}, u32[]{:S(2)}) collective-permute-start(bf16[16,1024]{1,0:T(8,128)(2,1)S(1)} %fusion.65), channel_id=1, source_target_pairs={{0,2},{1,3},{2,0},{3,1},{4,6},{5,7},{6,4},{7,5},{8,10},{9,11},{10,... | collective-permute-start | bytes 98312 | tf_op jit(solution)/shard_map/ppermute | solution.py:169
  151.0 4.6 %collective-permute-start.12 = (f32[1025]{0:T(1024)S(1)}, f32[1025]{0:T(1024)S(1)}, u32[]{:S(2)}, u32[]{:S(2)}) collective-permute-start(f32[1025]{0:T(1024)S(1)} %add.327), channel_id=1, source_target_pairs={{0,2},{1,3},{2,0},{3,1},{4,6},{5,7},{6,4},{7,5},{8,10},{9,11},{10,... | collective-permute-start | bytes 12308 | tf_op jit(solution)/shard_map/ppermute | solution.py:171
  153.6 5.6 %collective-permute-start.17 = (bf16[32,1536]{1,0:T(8,128)(2,1)S(1)}, bf16[32,1536]{1,0:T(8,128)(2,1)S(1)}, u32[]{:S(2)}, u32[]{:S(2)}) collective-permute-start(bf16[32,1536]{1,0:T(8,128)(2,1)S(1)} %fusion.62), channel_id=1, source_target_pairs={{0,2},{1,3},{2,0},{3,1},{4,6},{5,7},{6,4},{7,5},{8,10},{9,11},{10,... | collective-permute-start | bytes 294920 | tf_op jit(solution)/shard_map/ppermute | solution.py:171
  (23 other events, 55.0 us)

commit v20 on v19

--- a/solution.py
+++ b/solution.py
@@ -315,8 +315,16 @@
     grad_ln = jnp.sum(d_hidden * normed, axis=0)
     loss_part = jnp.sum(token_loss)
     small = jnp.concatenate([grad_ln, loss_part.reshape(1)])
-    grad_out, unused = halving_scatter(grad_wout)
-    grad_qkv, small = halving_scatter(grad_wqkv, small)
+    blocks = shards * lax.axis_size("clip")
+    width = grad_wout.shape[1]
+    extra = jnp.zeros((2, width), jnp.float32).at[0].set(grad_ln).at[1, 0].set(loss_part)
+    joined = jnp.concatenate(
+        [grad_wout.reshape(blocks, -1, width), jnp.broadcast_to(extra[None], (blocks, 2, width))], axis=1
+    )
+    joined, unused = halving_scatter(joined.reshape(-1, width))
+    grad_qkv, unused = halving_scatter(grad_wqkv)
+    grad_out = joined[:-2]
+    small = jnp.concatenate([joined[-2], joined[-1, :1]])
     count_all = shards * lax.axis_size("clip") * TOK_DEV
     return (small[-1] / count_all, grad_qkv.reshape(-1), grad_out.reshape(-1), small[:-1])
 

time: 162 us -> 164 us (1.012)
  starting transfers between devices: 32.5 us -> 28.6 us
  local copies, waits for them, and re-layouts: 31.9 us -> 35.7 us
  waiting for transfers between devices: 53.1 us -> 55.9 us
  matrix products: 20.2 us -> 18.3 us
    ppermute x5 -> x10, waiting for transfers between devices: 1.55 us -> 18.4 us  [halving_scatter(): got = lax.ppermute(give.astype(jnp.bfloat16), ('seq', 'clip'), pairs)]
    ppermute x10 -> x0, waiting for transfers between devices: 13.4 us -> none  [halving_scatter(): lax.ppermute((give.astype(jnp.bfloat16), small), ('seq', 'clip'), pairs)]
    ppermute x10 -> x0, starting transfers between devices: 8.68 us -> none  [halving_scatter(): lax.ppermute((give.astype(jnp.bfloat16), small), ('seq', 'clip'), pairs)]
    ppermute x5 -> x10, starting transfers between devices: 7.45 us -> 12.3 us  [halving_scatter(): got = lax.ppermute(give.astype(jnp.bfloat16), ('seq', 'clip'), pairs)]
    add x9 -> x10, other arithmetic: 5.05 us -> 7.32 us  [halving_scatter(): data = keep + got.astype(jnp.float32)]
    dot_general x1, matrix products: 3.06 us -> 1.18 us  [per_device(): jnp.einsum('ct,fc->tf', d_proj_t, w_qkv, preferred_element_type=jnp.float32)]
    unnamed x65 -> x68, local copies, waits for them, and re-layouts: 9.2 us -> 10.1 us
  transfers between devices with their start and end apart: 25 -> 20, of which waited for: 16 -> 15; matrix products, arithmetic and copies ran while one was open for 15% -> 16% of each run, Pallas kernels for 0% -> 0%
where the time goes in v20:
time: 164 us; the launch traced here: 163 us
  waiting for transfers between devices  55.9 us (34%)
  local copies, waits for them, and re-layouts  35.7 us (22%)
  starting transfers between devices  28.6 us (17%)
  other arithmetic  20.9 us (13%)
  matrix products  18.3 us (11%)
  between operations  3.2 us (2%)
    ppermute x10, waiting for transfers between devices, halving_scatter(): got = lax.ppermute(give.astype(jnp.bfloat16), ('seq', 'clip'), pairs)  18.4 us
    all_to_all x1, waiting for transfers between devices, per_device(): lax.all_to_all(jnp.concatenate([send_tokens, send_target], axis=2), 'seq'...  12.3 us
    ppermute x10, starting transfers between devices, halving_scatter(): got = lax.ppermute(give.astype(jnp.bfloat16), ('seq', 'clip'), pairs)  12.3 us
    ppermute x3, waiting for transfers between devices, return_blocks(): sent = lax.ppermute(summed[k].astype(jnp.bfloat16), 'seq', xor_pairs(2 * k))  12.2 us
    unnamed x68, local copies, waits for them, and re-layouts  10.1 us
    ppermute x3, waiting for transfers between devices, gather_blocks(): lax.ppermute(block, 'seq', xor_pairs(2 * k))  9.21 us
    add x10, other arithmetic, halving_scatter(): data = keep + got.astype(jnp.float32)  7.32 us
    all_to_all x1, starting transfers between devices, per_device(): lax.all_to_all(jnp.broadcast_to(kept_count.reshape(1, 1), (shards, 1)), '...  5.17 us
  transfers between devices with their start and end apart: 20, of which 15 were waited for; matrix products, arithmetic and copies ran while one was open for 16% of the time, Pallas kernels for 0%

profile of v20, /device:TPU:0, one launch (start us, length us, event | category | flops | bytes accessed | tf_op | source)
XLA Modules:
  0.0 162.7 jit_solution(8455192075281515597)
XLA Ops:
  3.4 5.2 %all-to-all-start = ((s32[8,1,1]{2,1,0:T(1,128)}), s32[8,1,1]{2,1,0:T(1,128)S(1)}, u32[]{:S(2)}, u32[]{:S(2)}) async-start(s32[8,1,1]{2,1,0:T(1,128)} %broadcast_in_dim.51), calls=%async_computation | async-start | bytes 8192 | tf_op jit(solution)/shard_map/all_to_all | solution.py:211
  9.2 3.9 %all-to-all-done = s32[8,1,1]{2,1,0:T(1,128)S(1)} async-done(((s32[8,1,1]{2,1,0:T(1,128)}), s32[8,1,1]{2,1,0:T(1,128)S(1)}, u32[]{:S(2)}, u32[]{:S(2)}) %all-to-all-start) | async-done | bytes 64 | tf_op jit(solution)/shard_map/all_to_all | solution.py:211
  21.0 3.5 %all-to-all-start.1 = ((bf16[8,24,2048]{2,1,0:T(8,128)(2,1)}), bf16[8,24,2048]{2,1,0:T(8,128)(2,1)S(1)}, u32[]{:S(2)}, u32[]{:S(2)}) async-start(bf16[8,24,2048]{2,1,0:T(8,128)(2,1)} %pad_maximum_fusion.3), calls=%async_computation.1 | async-start | bytes 1572864 | tf_op jit(solution)/shard_map/all_to_all | solution.py:228
  24.9 12.3 %all-to-all-done.1 = bf16[8,24,2048]{2,1,0:T(8,128)(2,1)S(1)} async-done(((bf16[8,24,2048]{2,1,0:T(8,128)(2,1)}), bf16[8,24,2048]{2,1,0:T(8,128)(2,1)S(1)}, u32[]{:S(2)}, u32[]{:S(2)}) %all-to-all-start.1) | async-done | bytes 786464 | tf_op jit(solution)/shard_map/all_to_all | solution.py:228
  37.1 1.8 %scatter_custom_fusion = bf16[128,2048]{1,0:T(8,128)(2,1)S(1)} fusion(s32[192]{0:T(256)S(1)} %bitcast.251, bf16[192,2048]{1,0:T(8,128)(2,1)S(1)} %bitcast.237, bf16[]{:T(256)} %constant.238.clone.1), kind=kCustom, calls=%fused_computation.112 | custom fusion | bytes 524290 | tf_op jit(solution)/shard_map/scatter | solution.py:238
  39.6 2.1 %fusion.19 = bf16[128,1024]{1,0:T(8,128)(2,1)S(1)} fusion(bf16[128,1024]{1,0:T(8,128)(2,1)S(1)} %fusion.34, bf16[1024,1536]{1,0:T(8,128)(2,1)} %param.13), kind=kOutput, calls=%fused_computation.34 | convolution fusion | flops 268566528 | bytes 2621440 | tf_op jit(solution)/shard_map/dot_general | solution.py:252
  45.3 6.2 %collective-permute-done.2 = bf16[1024,128]{0,1:T(8,128)(2,1)S(1)} collective-permute-done((bf16[1024,128]{0,1:T(8,128)(2,1)S(1)}, bf16[1024,128]{0,1:T(8,128)(2,1)S(1)}, u32[]{:S(2)}, u32[]{:S(2)}) %collective-permute-start.2) | collective-permute-done | bytes 262176 | tf_op jit(solution)/shard_map/ppermute | solution.py:184
  51.5 2.8 %collective-permute-done.1 = bf16[1024,128]{0,1:T(8,128)(2,1)S(1)} collective-permute-done((bf16[1024,128]{0,1:T(8,128)(2,1)S(1)}, bf16[1024,128]{0,1:T(8,128)(2,1)S(1)}, u32[]{:S(2)}, u32[]{:S(2)}) %collective-permute-start.1) | collective-permute-done | bytes 262176 | tf_op jit(solution)/shard_map/ppermute | solution.py:184
  55.9 1.5 convolution_convert_fusion.1
  59.9 1.8 %copy.100 = bf16[1024,128]{1,0:T(8,128)(2,1)} copy(bf16[1024,128]{0,1:T(8,128)(2,1)} %copy-done.15) | data formatting | bytes 524288 | tf_op jit(solution)/shard_map/ppermute | solution.py:184
  62.7 2.5 %copy.103 = bf16[4,1024,128]{2,1,0:T(8,128)(2,1)} copy(bf16[4,1024,128]{1,2,0:T(8,128)(2,1)} %collective-permute-done.3) | data formatting | bytes 2097152 | tf_op jit(solution)/shard_map/ppermute | solution.py:186
  69.4 1.6 %fusion.51 = (bf16[128,8,64]{0,2,1:T(8,128)(2,1)S(1)}, f32[8,128,64,1]{1,2,0,3:T(8,128)}) fusion(f32[128,8]{0,1:T(8,128)S(1)} %bitcast.246, f32[8,8,128,128]{2,3,1,0:T(8,128)S(1)} %get-tuple-element.54, f32[8,128]{1,0:T(8,128)S(1)} %get-tuple-element.53, bf16[8,8,2,64,128]{4,3,2,1,0:T(8,128)(2,1)S(1)} %constant_dynamic-update-slice_fusion), kind=kOutput, calls=%fused_computation.105 | convolution fusion | flops 137494528 | bytes 5644288 | tf_op jit(solution)/shard_map/ihqt,ihdt->ihqd/dot_general | solution.py:267
  73.6 3.9 %fusion.16 = bf16[8,8,64,128]{3,2,1,0:T(8,128)(2,1)S(1)} fusion(f32[8,8,128,128]{2,3,1,0:T(8,128)} %copy-done.2, f32[8,128]{1,0:T(8,128)S(1)} %log_add_fusion, bf16[8,128,64]{1,2,0:T(8,128)(2,1)S(1)} %bitcast.218), kind=kOutput, calls=%fused_computation.31 | convolution fusion | flops 137887744 | bytes 5378048 | tf_op jit(solution)/shard_map/ihqd,ihqt->ihdt/dot_general | solution.py:295
  77.5 2.6 %multiply_convert_fusion = bf16[8,8,128,128]{2,3,1,0:T(8,128)(2,1)S(1)} fusion(f32[8,8,128,128]{2,3,1,0:T(8,128)S(1)} %copy-done.3, f32[8,128]{1,0:T(8,128)S(1)} %multiply_reduce_fusion.4, f32[8,128]{1,0:T(8,128)S(1)} %log_add_fusion, bf16[8,8,2,64,128]{4,3,2,1,0:T(8,128)(2,1)} %copy-done.8, bf16[8,128,64]{1,2,0:T(8,128)(2,1)S(1)} %bitcast.219), kind=kOutput, calls=%fused_computation.5 | convolution fusion | flops 139460608 | bytes 7479296 | tf_op jit(solution)/shard_map/ihqd,ihdt->ihqt/dot_general | solution.py:298
  80.1 1.5 multiply_convert_fusion.1
  89.5 1.5 fusion.68
  91.1 1.9 %collective-permute-start.5 = (bf16[1024,128]{1,0:T(8,128)(2,1)S(1)}, bf16[1024,128]{1,0:T(8,128)(2,1)S(1)}, u32[]{:S(2)}, u32[]{:S(2)}) collective-permute-start(bf16[1024,128]{1,0:T(8,128)(2,1)S(1)} %get-tuple-element.36), channel_id=1, source_target_pairs={{0,8},{4,12},{8,0},{12,4},{16,24},{20,28},{24,16},{28,20},{1,9},{5... | collective-permute-start | bytes 786440 | tf_op jit(solution)/shard_map/ppermute | solution.py:196
  95.3 5.1 %collective-permute-done.5 = bf16[1024,128]{1,0:T(8,128)(2,1)S(1)} collective-permute-done((bf16[1024,128]{1,0:T(8,128)(2,1)S(1)}, bf16[1024,128]{1,0:T(8,128)(2,1)S(1)}, u32[]{:S(2)}, u32[]{:S(2)}) %collective-permute-start.5) | collective-permute-done | bytes 262176 | tf_op jit(solution)/shard_map/ppermute | solution.py:196
  100.3 5.7 %collective-permute-done.7 = bf16[1024,128]{1,0:T(8,128)(2,1)S(1)} collective-permute-done((bf16[1024,128]{1,0:T(8,128)(2,1)S(1)}, bf16[1024,128]{1,0:T(8,128)(2,1)S(1)}, u32[]{:S(2)}, u32[]{:S(2)}) %collective-permute-start.7) | collective-permute-done | bytes 262176 | tf_op jit(solution)/shard_map/ppermute | solution.py:196
  110.0 2.8 %copy-done.29 = bf16[1024,1536]{1,0:T(8,128)(2,1)S(1)} copy-done((bf16[1024,1536]{1,0:T(8,128)(2,1)S(1)}, bf16[1024,1536]{1,0:T(8,128)(2,1)}, u32[]{:S(2)}) %copy-start.29) | copy-done | bytes 3145752
  115.4 1.7 %copy-done.6 = f32[32,18,1024]{2,1,0:T(8,128)} copy-done((f32[32,18,1024]{2,1,0:T(8,128)}, f32[32,18,1024]{2,1,0:T(8,128)S(1)}, u32[]{:S(2)}) %copy-start.6) | copy-done | bytes 2359320
  121.4 1.7 %collective-permute-start.9 = (bf16[2,2,2,18,1024]{4,2,3,1,0:T(2,128)(2,1)S(1)}, bf16[2,2,2,18,1024]{4,2,3,1,0:T(2,128)(2,1)S(1)}, u32[]{:S(2)}, u32[]{:S(2)}) collective-permute-start(bf16[2,2,2,18,1024]{4,2,3,1,0:T(2,128)(2,1)S(1)} %fusion.32), channel_id=1, source_target_pairs={{0,8},{1,9},{2,10},{3,11},{4,20},{5,21},{6,22},{7,23},{8,0},{9,1},... | collective-permute-start | bytes 884744 | tf_op jit(solution)/shard_map/ppermute | solution.py:169
  123.2 2.9 %bitcast_add_fusion = f32[2,2,2,2,32,1536]{5,4,3,2,1,0:T(8,128)S(1)} fusion(bf16[2,2,2,2,32,1536]{5,4,3,2,1,0:T(8,128)(2,1)} %collective-permute-done.13, f32[2,2,2,2,2,32,1536]{6,5,4,3,2,1,0:T(8,128)} %copy-done.5, s32[]{:T(128)S(6)} %select_n.279), kind=kLoop, calls=%fused_computation.13 | loop fusion | flops 1572864 | bytes 7864324 | tf_op jit(solution)/shard_map/add | solution.py:173
  126.6 1.6 collective-permute-done.9
  129.6 6.1 %collective-permute-done.10 = bf16[2,2,18,1024]{3,1,2,0:T(2,128)(2,1)S(1)} collective-permute-done((bf16[2,2,18,1024]{3,1,2,0:T(2,128)(2,1)S(1)}, bf16[2,2,18,1024]{3,1,2,0:T(2,128)(2,1)S(1)}, u32[]{:S(2)}, u32[]{:S(2)}) %collective-permute-start.10) | collective-permute-done | bytes 147488 | tf_op jit(solution)/shard_map/ppermute | solution.py:169
  136.0 1.6 %collective-permute-start.11 = (bf16[2,18,1024]{2,0,1:T(2,128)(2,1)S(1)}, bf16[2,18,1024]{2,0,1:T(2,128)(2,1)S(1)}, u32[]{:S(2)}, u32[]{:S(2)}) collective-permute-start(bf16[2,18,1024]{2,0,1:T(2,128)(2,1)S(1)} %fusion.60), channel_id=1, source_target_pairs={{0,1},{1,0},{2,3},{3,2},{4,12},{5,13},{6,14},{7,15},{8,9},{9,8},{1... | collective-permute-start | bytes 221192 | tf_op jit(solution)/shard_map/ppermute | solution.py:169
  139.1 2.2 %fusion.15 = f32[2,2,2,32,1536]{4,3,2,1,0:T(8,128)S(1)} fusion(bf16[2,2,2,32,1536]{4,3,2,1,0:T(8,128)(2,1)S(1)} %collective-permute-done.14, f32[2,2,2,2,32,1536]{5,4,3,2,1,0:T(8,128)} %copy-done.4, s32[]{:T(128)S(6)} %select_n.282, s32[]{:T(128)S(6)} %select_n.281, pred[]{:T(512)S(6)} %eq.5), kind=kLoop, calls=%fused_computation.29 | loop fusion | flops 1179648 | bytes 5505033 | tf_op jit(solution)/shard_map/add | solution.py:173
  142.3 2.7 %collective-permute-start.12 = (bf16[18,1024]{1,0:T(8,128)(2,1)S(1)}, bf16[18,1024]{1,0:T(8,128)(2,1)S(1)}, u32[]{:S(2)}, u32[]{:S(2)}) collective-permute-start(bf16[18,1024]{1,0:T(8,128)(2,1)S(1)} %bitcast.245), channel_id=1, source_target_pairs={{0,2},{1,3},{2,0},{3,1},{4,6},{5,7},{6,4},{7,5},{8,10},{9,11},{10,... | collective-permute-start | bytes 110600 | tf_op jit(solution)/shard_map/ppermute | solution.py:169
  145.1 4.2 %collective-permute-done.15 = bf16[2,2,32,1536]{3,2,1,0:T(8,128)(2,1)S(1)} collective-permute-done((bf16[2,2,32,1536]{3,2,1,0:T(8,128)(2,1)S(1)}, bf16[2,2,32,1536]{3,2,1,0:T(8,128)(2,1)S(1)}, u32[]{:S(2)}, u32[]{:S(2)}) %collective-permute-start.15) | collective-permute-done | bytes 393248 | tf_op jit(solution)/shard_map/ppermute | solution.py:169
  149.4 1.6 %collective-permute-start.16 = (bf16[2,32,1536]{2,1,0:T(8,128)(2,1)S(1)}, bf16[2,32,1536]{2,1,0:T(8,128)(2,1)S(1)}, u32[]{:S(2)}, u32[]{:S(2)}) collective-permute-start(bf16[2,32,1536]{2,1,0:T(8,128)(2,1)S(1)} %fusion.58), channel_id=1, source_target_pairs={{0,1},{1,0},{2,3},{3,2},{4,12},{5,13},{6,14},{7,15},{8,9},{9,8},{1... | collective-permute-start | bytes 589832 | tf_op jit(solution)/shard_map/ppermute | solution.py:169
  151.1 4.1 %collective-permute-done.16 = bf16[2,32,1536]{2,1,0:T(8,128)(2,1)S(1)} collective-permute-done((bf16[2,32,1536]{2,1,0:T(8,128)(2,1)S(1)}, bf16[2,32,1536]{2,1,0:T(8,128)(2,1)S(1)}, u32[]{:S(2)}, u32[]{:S(2)}) %collective-permute-start.16) | collective-permute-done | bytes 196640 | tf_op jit(solution)/shard_map/ppermute | solution.py:169
  155.3 2.7 %collective-permute-start.17 = (bf16[32,1536]{1,0:T(8,128)(2,1)S(1)}, bf16[32,1536]{1,0:T(8,128)(2,1)S(1)}, u32[]{:S(2)}, u32[]{:S(2)}) collective-permute-start(bf16[32,1536]{1,0:T(8,128)(2,1)S(1)} %fusion.59), channel_id=1, source_target_pairs={{0,2},{1,3},{2,0},{3,1},{4,6},{5,7},{6,4},{7,5},{8,10},{9,11},{10,... | collective-permute-start | bytes 294920 | tf_op jit(solution)/shard_map/ppermute | solution.py:169
  (174 shorter events, 56.1 us)
Async XLA Ops:
  0.6 15.1 %copy-start = (bf16[1,512,1024]{2,1,0:T(8,128)(2,1)S(1)}, bf16[1,512,1024]{2,1,0:T(8,128)(2,1)}, u32[]{:S(2)}) copy-start(bf16[1,512,1024]{2,1,0:T(8,128)(2,1)} %param.11) | copy-start | bytes 3145732
  0.6 16.1 %copy-start.7 = (bf16[1,512,1024]{2,1,0:T(8,128)(2,1)S(1)}, bf16[1,512,1024]{2,1,0:T(8,128)(2,1)}, u32[]{:S(2)}) copy-start(bf16[1,512,1024]{2,1,0:T(8,128)(2,1)} %param.10) | copy-start | bytes 3145732
  3.4 9.8 %all-to-all-start = ((s32[8,1,1]{2,1,0:T(1,128)}), s32[8,1,1]{2,1,0:T(1,128)S(1)}, u32[]{:S(2)}, u32[]{:S(2)}) async-start(s32[8,1,1]{2,1,0:T(1,128)} %broadcast_in_dim.51), calls=%async_computation | async-start | bytes 8192 | tf_op jit(solution)/shard_map/all_to_all | solution.py:211
  20.1 19.3 %copy-start.18 = (f32[1024]{0:T(1024)S(1)}, f32[1024]{0:T(1024)}, u32[]{:S(2)}) copy-start(f32[1024]{0:T(1024)} %param.15) | copy-start | bytes 12292
  21.0 16.1 %all-to-all-start.1 = ((bf16[8,24,2048]{2,1,0:T(8,128)(2,1)}), bf16[8,24,2048]{2,1,0:T(8,128)(2,1)S(1)}, u32[]{:S(2)}, u32[]{:S(2)}) async-start(bf16[8,24,2048]{2,1,0:T(8,128)(2,1)} %pad_maximum_fusion.3), calls=%async_computation.1 | async-start | bytes 1572864 | tf_op jit(solution)/shard_map/all_to_all | solution.py:228
  39.6 16.3 %copy-start.11 = (bf16[128,1024]{1,0:T(8,128)(2,1)}, bf16[128,1024]{1,0:T(8,128)(2,1)S(1)}, u32[]{:S(2)}) copy-start(bf16[128,1024]{1,0:T(8,128)(2,1)S(1)} %fusion.34) | copy-start | bytes 786436
  41.8 9.7 %collective-permute-start.2 = (bf16[1024,128]{0,1:T(8,128)(2,1)S(1)}, bf16[1024,128]{0,1:T(8,128)(2,1)S(1)}, u32[]{:S(2)}, u32[]{:S(2)}) collective-permute-start(bf16[1024,128]{0,1:T(8,128)(2,1)S(1)} %bitcast.231), channel_id=1, source_target_pairs={{0,24},{4,28},{8,16},{12,20},{16,8},{20,12},{24,0},{28,4},{1,25},{... | collective-permute-start | bytes 786440 | tf_op jit(solution)/shard_map/ppermute | solution.py:184
  42.4 11.9 %collective-permute-start.1 = (bf16[1024,128]{0,1:T(8,128)(2,1)S(1)}, bf16[1024,128]{0,1:T(8,128)(2,1)S(1)}, u32[]{:S(2)}, u32[]{:S(2)}) collective-permute-start(bf16[1024,128]{0,1:T(8,128)(2,1)S(1)} %bitcast.232), channel_id=1, source_target_pairs={{0,16},{4,20},{8,24},{12,28},{16,0},{20,4},{24,8},{28,12},{1,17},{... | collective-permute-start | bytes 786440 | tf_op jit(solution)/shard_map/ppermute | solution.py:184
  43.8 10.7 %collective-permute-start = (bf16[1024,128]{0,1:T(8,128)(2,1)S(1)}, bf16[1024,128]{0,1:T(8,128)(2,1)S(1)}, u32[]{:S(2)}, u32[]{:S(2)}) collective-permute-start(bf16[1024,128]{0,1:T(8,128)(2,1)S(1)} %bitcast.233), channel_id=1, source_target_pairs={{0,8},{4,12},{8,0},{12,4},{16,24},{20,28},{24,16},{28,20},{1,9},{5... | collective-permute-start | bytes 786440 | tf_op jit(solution)/shard_map/ppermute | solution.py:184
  55.6 7.1 %collective-permute-start.3 = (bf16[4,1024,128]{1,2,0:T(8,128)(2,1)}, bf16[4,1024,128]{1,2,0:T(8,128)(2,1)}, u32[]{:S(2)}, u32[]{:S(2)}) collective-permute-start(bf16[4,1024,128]{1,2,0:T(8,128)(2,1)} %pad_maximum_fusion.1), channel_id=1, source_target_pairs={{0,4},{4,0},{8,12},{12,8},{16,20},{20,16},{24,28},{28,24},{1,5},{5... | collective-permute-start | bytes 3145736 | tf_op jit(solution)/shard_map/ppermute | solution.py:186
  57.6 14.8 %copy-start.19 = (f32[128]{0:T(128)}, f32[128]{0:T(128)S(1)}, u32[]{:S(2)}) copy-start(f32[128]{0:T(128)S(1)} %add_rsqrt_fusion) | copy-start | bytes 1540
  84.6 4.9 %collective-permute-start.4 = (bf16[4,1024,128]{2,1,0:T(8,128)(2,1)}, bf16[4,1024,128]{2,1,0:T(8,128)(2,1)}, u32[]{:S(2)}, u32[]{:S(2)}) collective-permute-start(bf16[4,1024,128]{2,1,0:T(8,128)(2,1)} %bitcast.42), channel_id=1, source_target_pairs={{0,4},{4,0},{8,12},{12,8},{16,20},{20,16},{24,28},{28,24},{1,5},{5... | collective-permute-start | bytes 3145736 | tf_op jit(solution)/shard_map/ppermute | solution.py:192
  89.4 5.2 %copy-start.20 = (f32[128]{0:T(128)S(1)}, f32[128]{0:T(128)}, u32[]{:S(2)}) copy-start(f32[128]{0:T(128)} %copy-done.19) | copy-start | bytes 1540
  89.5 5.2 %copy-start.22 = (f32[128]{0:T(128)S(1)}, f32[128]{0:T(128)}, u32[]{:S(2)}) copy-start(f32[128]{0:T(128)} %copy-done.21) | copy-start | bytes 1540
  89.5 5.2 %copy-start.24 = (f32[128]{0:T(128)S(1)}, f32[128]{0:T(128)}, u32[]{:S(2)}) copy-start(f32[128]{0:T(128)} %copy-done.23) | copy-start | bytes 1540
  89.5 5.2 %copy-start.26 = (f32[128]{0:T(128)S(1)}, f32[128]{0:T(128)}, u32[]{:S(2)}) copy-start(f32[128]{0:T(128)} %copy-done.25) | copy-start | bytes 1540
  91.1 9.2 %collective-permute-start.5 = (bf16[1024,128]{1,0:T(8,128)(2,1)S(1)}, bf16[1024,128]{1,0:T(8,128)(2,1)S(1)}, u32[]{:S(2)}, u32[]{:S(2)}) collective-permute-start(bf16[1024,128]{1,0:T(8,128)(2,1)S(1)} %get-tuple-element.36), channel_id=1, source_target_pairs={{0,8},{4,12},{8,0},{12,4},{16,24},{20,28},{24,16},{28,20},{1,9},{5... | collective-permute-start | bytes 786440 | tf_op jit(solution)/shard_map/ppermute | solution.py:196
  93.0 13.0 %collective-permute-start.7 = (bf16[1024,128]{1,0:T(8,128)(2,1)S(1)}, bf16[1024,128]{1,0:T(8,128)(2,1)S(1)}, u32[]{:S(2)}, u32[]{:S(2)}) collective-permute-start(bf16[1024,128]{1,0:T(8,128)(2,1)S(1)} %get-tuple-element.37), channel_id=1, source_target_pairs={{0,24},{4,28},{8,16},{12,20},{16,8},{20,12},{24,0},{28,4},{1,25},{... | collective-permute-start | bytes 786440 | tf_op jit(solution)/shard_map/ppermute | solution.py:196
  94.1 13.4 %collective-permute-start.6 = (bf16[1024,128]{1,0:T(8,128)(2,1)S(1)}, bf16[1024,128]{1,0:T(8,128)(2,1)S(1)}, u32[]{:S(2)}, u32[]{:S(2)}) collective-permute-start(bf16[1024,128]{1,0:T(8,128)(2,1)S(1)} %get-tuple-element.38), channel_id=1, source_target_pairs={{0,16},{4,20},{8,24},{12,28},{16,0},{20,4},{24,8},{28,12},{1,17},{... | collective-permute-start | bytes 786440 | tf_op jit(solution)/shard_map/ppermute | solution.py:196
  94.7 12.9 %copy-start.16 = (bf16[128,1024]{0,1:T(8,128)(2,1)S(1)}, bf16[128,1024]{0,1:T(8,128)(2,1)}, u32[]{:S(2)}) copy-start(bf16[128,1024]{0,1:T(8,128)(2,1)} %copy.120) | copy-start | bytes 786436
  108.6 5.5 %copy-start.5 = (f32[2,2,2,2,2,32,1536]{6,5,4,3,2,1,0:T(8,128)}, f32[2,2,2,2,2,32,1536]{6,5,4,3,2,1,0:T(8,128)S(1)}, u32[]{:S(2)}) copy-start(f32[2,2,2,2,2,32,1536]{6,5,4,3,2,1,0:T(8,128)S(1)} %fusion.46) | copy-start | bytes 18874372
  110.0 13.2 %collective-permute-start.13 = (bf16[2,2,2,2,32,1536]{5,4,3,2,1,0:T(8,128)(2,1)}, bf16[2,2,2,2,32,1536]{5,4,3,2,1,0:T(8,128)(2,1)}, u32[]{:S(2)}, u32[]{:S(2)}) collective-permute-start(bf16[2,2,2,2,32,1536]{5,4,3,2,1,0:T(8,128)(2,1)} %fusion.13), channel_id=1, source_target_pairs={{0,4},{1,5},{2,6},{3,7},{4,0},{5,1},{6,2},{7,3},{8,12},{9,13},{10,... | collective-permute-start | bytes 4718600 | tf_op jit(solution)/shard_map/ppermute | solution.py:169
  117.8 2.1 %collective-permute-start.8 = (bf16[2,2,2,2,18,1024]{5,3,4,2,1,0:T(2,128)(2,1)S(1)}, bf16[2,2,2,2,18,1024]{5,3,4,2,1,0:T(2,128)(2,1)S(1)}, u32[]{:S(2)}, u32[]{:S(2)}) collective-permute-start(bf16[2,2,2,2,18,1024]{5,3,4,2,1,0:T(2,128)(2,1)S(1)} %bitcast.238), channel_id=1, source_target_pairs={{0,4},{1,5},{2,6},{3,7},{4,0},{5,1},{6,2},{7,3},{8,12},{9,13},{10,... | collective-permute-start | bytes 1769480 | tf_op jit(solution)/shard_map/ppermute | solution.py:169
  121.4 6.8 %collective-permute-start.9 = (bf16[2,2,2,18,1024]{4,2,3,1,0:T(2,128)(2,1)S(1)}, bf16[2,2,2,18,1024]{4,2,3,1,0:T(2,128)(2,1)S(1)}, u32[]{:S(2)}, u32[]{:S(2)}) collective-permute-start(bf16[2,2,2,18,1024]{4,2,3,1,0:T(2,128)(2,1)S(1)} %fusion.32), channel_id=1, source_target_pairs={{0,8},{1,9},{2,10},{3,11},{4,20},{5,21},{6,22},{7,23},{8,0},{9,1},... | collective-permute-start | bytes 884744 | tf_op jit(solution)/shard_map/ppermute | solution.py:169
  126.2 12.8 %collective-permute-start.14 = (bf16[2,2,2,32,1536]{4,3,2,1,0:T(8,128)(2,1)S(1)}, bf16[2,2,2,32,1536]{4,3,2,1,0:T(8,128)(2,1)S(1)}, u32[]{:S(2)}, u32[]{:S(2)}) collective-permute-start(bf16[2,2,2,32,1536]{4,3,2,1,0:T(8,128)(2,1)S(1)} %fusion.14), channel_id=1, source_target_pairs={{0,8},{1,9},{2,10},{3,11},{4,20},{5,21},{6,22},{7,23},{8,0},{9,1},... | collective-permute-start | bytes 2359304 | tf_op jit(solution)/shard_map/ppermute | solution.py:169
  128.8 6.8 %collective-permute-start.10 = (bf16[2,2,18,1024]{3,1,2,0:T(2,128)(2,1)S(1)}, bf16[2,2,18,1024]{3,1,2,0:T(2,128)(2,1)S(1)}, u32[]{:S(2)}, u32[]{:S(2)}) collective-permute-start(bf16[2,2,18,1024]{3,1,2,0:T(2,128)(2,1)S(1)} %fusion.48), channel_id=1, source_target_pairs={{0,16},{1,17},{2,18},{3,19},{4,5},{5,4},{6,7},{7,6},{8,24},{9,25},... | collective-permute-start | bytes 442376 | tf_op jit(solution)/shard_map/ppermute | solution.py:169
  136.0 6.1 %collective-permute-start.11 = (bf16[2,18,1024]{2,0,1:T(2,128)(2,1)S(1)}, bf16[2,18,1024]{2,0,1:T(2,128)(2,1)S(1)}, u32[]{:S(2)}, u32[]{:S(2)}) collective-permute-start(bf16[2,18,1024]{2,0,1:T(2,128)(2,1)S(1)} %fusion.60), channel_id=1, source_target_pairs={{0,1},{1,0},{2,3},{3,2},{4,12},{5,13},{6,14},{7,15},{8,9},{9,8},{1... | collective-permute-start | bytes 221192 | tf_op jit(solution)/shard_map/ppermute | solution.py:169
  141.4 7.8 %collective-permute-start.15 = (bf16[2,2,32,1536]{3,2,1,0:T(8,128)(2,1)S(1)}, bf16[2,2,32,1536]{3,2,1,0:T(8,128)(2,1)S(1)}, u32[]{:S(2)}, u32[]{:S(2)}) collective-permute-start(bf16[2,2,32,1536]{3,2,1,0:T(8,128)(2,1)S(1)} %fusion.27), channel_id=1, source_target_pairs={{0,16},{1,17},{2,18},{3,19},{4,5},{5,4},{6,7},{7,6},{8,24},{9,25},... | collective-permute-start | bytes 1179656 | tf_op jit(solution)/shard_map/ppermute | solution.py:169
  142.3 8.8 %collective-permute-start.12 = (bf16[18,1024]{1,0:T(8,128)(2,1)S(1)}, bf16[18,1024]{1,0:T(8,128)(2,1)S(1)}, u32[]{:S(2)}, u32[]{:S(2)}) collective-permute-start(bf16[18,1024]{1,0:T(8,128)(2,1)S(1)} %bitcast.245), channel_id=1, source_target_pairs={{0,2},{1,3},{2,0},{3,1},{4,6},{5,7},{6,4},{7,5},{8,10},{9,11},{10,... | collective-permute-start | bytes 110600 | tf_op jit(solution)/shard_map/ppermute | solution.py:169
  149.2 12.4 %copy-start.1 = (bf16[1,512,1024]{2,1,0:T(8,128)(2,1)S(1)}, bf16[1,512,1024]{2,1,0:T(8,128)(2,1)}, u32[]{:S(2)}) copy-start(bf16[1,512,1024]{2,1,0:T(8,128)(2,1)} %param.11) | copy-start | bytes 3145732
  149.4 5.7 %collective-permute-start.16 = (bf16[2,32,1536]{2,1,0:T(8,128)(2,1)S(1)}, bf16[2,32,1536]{2,1,0:T(8,128)(2,1)S(1)}, u32[]{:S(2)}, u32[]{:S(2)}) collective-permute-start(bf16[2,32,1536]{2,1,0:T(8,128)(2,1)S(1)} %fusion.58), channel_id=1, source_target_pairs={{0,1},{1,0},{2,3},{3,2},{4,12},{5,13},{6,14},{7,15},{8,9},{9,8},{1... | collective-permute-start | bytes 589832 | tf_op jit(solution)/shard_map/ppermute | solution.py:169
  155.3 5.6 %collective-permute-start.17 = (bf16[32,1536]{1,0:T(8,128)(2,1)S(1)}, bf16[32,1536]{1,0:T(8,128)(2,1)S(1)}, u32[]{:S(2)}, u32[]{:S(2)}) collective-permute-start(bf16[32,1536]{1,0:T(8,128)(2,1)S(1)} %fusion.59), channel_id=1, source_target_pairs={{0,2},{1,3},{2,0},{3,1},{4,6},{5,7},{6,4},{7,5},{8,10},{9,11},{10,... | collective-permute-start | bytes 294920 | tf_op jit(solution)/shard_map/ppermute | solution.py:169
  (18 other events, 35.8 us)

commit v21 on v19

--- a/solution.py
+++ b/solution.py
@@ -190,7 +190,7 @@
 def return_blocks(own_parts, other_parts):
     half = lax.axis_size("seq") // 2
     got = lax.ppermute(other_parts, "seq", xor_pairs(1))
-    summed = own_parts.astype(jnp.bfloat16).astype(jnp.float32) + got.astype(jnp.float32)
+    summed = own_parts + got.astype(jnp.float32)
     accum = summed[0]
     for k in range(1, half):
         sent = lax.ppermute(summed[k].astype(jnp.bfloat16), "seq", xor_pairs(2 * k))

time: 162 us -> 161 us (level)
    unnamed x65 -> x73, local copies, waits for them, and re-layouts: 9.2 us -> 10.9 us
  transfers between devices with their start and end apart: 25 -> 25, of which waited for: 16 -> 15; matrix products, arithmetic and copies ran while one was open for 15% -> 15% of each run, Pallas kernels for 0% -> 0%
where the time goes in v21:
time: 161 us; the launch traced here: 160 us
  waiting for transfers between devices  52.8 us (33%)
  local copies, waits for them, and re-layouts  33.5 us (21%)
  starting transfers between devices  32.1 us (20%)
  matrix products  19.2 us (12%)
  other arithmetic  19.1 us (12%)
  between operations  3.18 us (2%)
    ppermute x10, waiting for transfers between devices, halving_scatter(): lax.ppermute((give.astype(jnp.bfloat16), small), ('seq', 'clip'), pairs)  13.6 us
    all_to_all x1, waiting for transfers between devices, per_device(): lax.all_to_all(jnp.concatenate([send_tokens, send_target], axis=2), 'seq'...  12.3 us
    ppermute x3, waiting for transfers between devices, return_blocks(): sent = lax.ppermute(summed[k].astype(jnp.bfloat16), 'seq', xor_pairs(2 * k))  12.2 us
    unnamed x73, local copies, waits for them, and re-layouts  10.9 us
    ppermute x3, waiting for transfers between devices, gather_blocks(): lax.ppermute(block, 'seq', xor_pairs(2 * k))  9.21 us
    ppermute x10, starting transfers between devices, halving_scatter(): lax.ppermute((give.astype(jnp.bfloat16), small), ('seq', 'clip'), pairs)  8.48 us
    ppermute x5, starting transfers between devices, halving_scatter(): got = lax.ppermute(give.astype(jnp.bfloat16), ('seq', 'clip'), pairs)  7.26 us
    all_to_all x1, starting transfers between devices, per_device(): lax.all_to_all(jnp.broadcast_to(kept_count.reshape(1, 1), (shards, 1)), '...  5.17 us
  transfers between devices with their start and end apart: 25, of which 15 were waited for; matrix products, arithmetic and copies ran while one was open for 15% of the time, Pallas kernels for 0%

profile of v21, /device:TPU:0, one launch (start us, length us, event | category | flops | bytes accessed | tf_op | source)
XLA Modules:
  0.0 159.9 jit_solution(4569810870491909575)
XLA Ops:
  3.4 5.2 %all-to-all-start = ((s32[8,1,1]{2,1,0:T(1,128)}), s32[8,1,1]{2,1,0:T(1,128)S(1)}, u32[]{:S(2)}, u32[]{:S(2)}) async-start(s32[8,1,1]{2,1,0:T(1,128)} %broadcast_in_dim.47), calls=%async_computation | async-start | bytes 8192 | tf_op jit(solution)/shard_map/all_to_all | solution.py:211
  9.2 3.9 %all-to-all-done = s32[8,1,1]{2,1,0:T(1,128)S(1)} async-done(((s32[8,1,1]{2,1,0:T(1,128)}), s32[8,1,1]{2,1,0:T(1,128)S(1)}, u32[]{:S(2)}, u32[]{:S(2)}) %all-to-all-start) | async-done | bytes 64 | tf_op jit(solution)/shard_map/all_to_all | solution.py:211
  21.0 3.5 %all-to-all-start.1 = ((bf16[8,24,2048]{2,1,0:T(8,128)(2,1)}), bf16[8,24,2048]{2,1,0:T(8,128)(2,1)S(1)}, u32[]{:S(2)}, u32[]{:S(2)}) async-start(bf16[8,24,2048]{2,1,0:T(8,128)(2,1)} %pad_maximum_fusion.3), calls=%async_computation.1 | async-start | bytes 1572864 | tf_op jit(solution)/shard_map/all_to_all | solution.py:228
  24.9 12.3 %all-to-all-done.1 = bf16[8,24,2048]{2,1,0:T(8,128)(2,1)S(1)} async-done(((bf16[8,24,2048]{2,1,0:T(8,128)(2,1)}), bf16[8,24,2048]{2,1,0:T(8,128)(2,1)S(1)}, u32[]{:S(2)}, u32[]{:S(2)}) %all-to-all-start.1) | async-done | bytes 786464 | tf_op jit(solution)/shard_map/all_to_all | solution.py:228
  37.1 1.8 %scatter_custom_fusion = bf16[128,2048]{1,0:T(8,128)(2,1)S(1)} fusion(s32[192]{0:T(256)S(1)} %bitcast.244, bf16[192,2048]{1,0:T(8,128)(2,1)S(1)} %bitcast.235, bf16[]{:T(256)} %constant.177.clone.1), kind=kCustom, calls=%fused_computation.112 | custom fusion | bytes 524290 | tf_op jit(solution)/shard_map/scatter | solution.py:238
  39.6 2.1 %fusion.16 = bf16[128,1024]{1,0:T(8,128)(2,1)S(1)} fusion(bf16[128,1024]{1,0:T(8,128)(2,1)S(1)} %fusion.29, bf16[1024,1536]{1,0:T(8,128)(2,1)} %param.9), kind=kOutput, calls=%fused_computation.32 | convolution fusion | flops 268566528 | bytes 2621440 | tf_op jit(solution)/shard_map/dot_general | solution.py:252
  43.8 1.5 collective-permute-start
  45.3 6.2 %collective-permute-done.2 = bf16[1024,128]{0,1:T(8,128)(2,1)S(1)} collective-permute-done((bf16[1024,128]{0,1:T(8,128)(2,1)S(1)}, bf16[1024,128]{0,1:T(8,128)(2,1)S(1)}, u32[]{:S(2)}, u32[]{:S(2)}) %collective-permute-start.2) | collective-permute-done | bytes 262176 | tf_op jit(solution)/shard_map/ppermute | solution.py:184
  51.5 2.8 %collective-permute-done.1 = bf16[1024,128]{0,1:T(8,128)(2,1)S(1)} collective-permute-done((bf16[1024,128]{0,1:T(8,128)(2,1)S(1)}, bf16[1024,128]{0,1:T(8,128)(2,1)S(1)}, u32[]{:S(2)}, u32[]{:S(2)}) %collective-permute-start.1) | collective-permute-done | bytes 262176 | tf_op jit(solution)/shard_map/ppermute | solution.py:184
  55.9 1.5 convolution_convert_fusion.1
  59.8 1.8 %copy.71 = bf16[1024,128]{1,0:T(8,128)(2,1)} copy(bf16[1024,128]{0,1:T(8,128)(2,1)} %copy-done.20) | data formatting | bytes 524288 | tf_op jit(solution)/shard_map/ppermute | solution.py:184
  62.7 2.3 %copy.74 = bf16[4,1024,128]{2,1,0:T(8,128)(2,1)} copy(bf16[4,1024,128]{1,2,0:T(8,128)(2,1)} %collective-permute-done.3) | data formatting | bytes 2097152 | tf_op jit(solution)/shard_map/ppermute | solution.py:186
  69.2 1.6 %fusion.51 = (bf16[128,8,64]{0,2,1:T(8,128)(2,1)S(1)}, f32[8,128,64,1]{1,2,0,3:T(8,128)}) fusion(f32[128,8]{0,1:T(8,128)S(1)} %bitcast.241, f32[8,8,128,128]{2,3,1,0:T(8,128)S(1)} %get-tuple-element.26, f32[8,128]{1,0:T(8,128)S(1)} %get-tuple-element.25, bf16[8,8,2,64,128]{4,3,2,1,0:T(8,128)(2,1)S(1)} %constant_dynamic-update-slice_fusion), kind=kOutput, calls=%fused_computation.103 | convolution fusion | flops 137494528 | bytes 5644288 | tf_op jit(solution)/shard_map/ihqt,ihdt->ihqd/dot_general | solution.py:267
  73.4 3.9 %fusion.3 = f32[8,8,64,128]{3,2,1,0:T(8,128)S(1)} fusion(f32[8,8,128,128]{2,3,1,0:T(8,128)} %copy-done.2, f32[8,128]{1,0:T(8,128)S(1)} %log_add_fusion, bf16[8,128,64]{1,2,0:T(8,128)(2,1)S(1)} %bitcast.216), kind=kOutput, calls=%fused_computation.14 | convolution fusion | flops 137363456 | bytes 6426624 | tf_op jit(solution)/shard_map/ihqd,ihqt->ihdt/dot_general | solution.py:295
  78.9 1.5 convolution_multiply_fusion
  86.6 1.7 %fusion.73 = (bf16[4,1024,128]{2,1,0:T(8,128)(2,1)S(1)}, f32[4,1024,128]{2,1,0:T(8,128)S(1)}) fusion(bf16[4,1024,128]{2,1,0:T(8,128)(2,1)} %collective-permute-done.4, f32[4,8,2,64,128]{4,3,2,1,0:T(8,128)S(1)} %copy.87), kind=kLoop, calls=%fused_computation.171 | loop fusion | flops 1572864 | bytes 6291456 | tf_op jit(solution)/shard_map/convert.5
  88.4 1.9 %collective-permute-start.5 = (bf16[1024,128]{1,0:T(8,128)(2,1)S(1)}, bf16[1024,128]{1,0:T(8,128)(2,1)S(1)}, u32[]{:S(2)}, u32[]{:S(2)}) collective-permute-start(bf16[1024,128]{1,0:T(8,128)(2,1)S(1)} %get-tuple-element.12), channel_id=1, source_target_pairs={{0,8},{4,12},{8,0},{12,4},{16,24},{20,28},{24,16},{28,20},{1,9},{5... | collective-permute-start | bytes 786440 | tf_op jit(solution)/shard_map/ppermute | solution.py:196
  92.5 5.1 %collective-permute-done.5 = bf16[1024,128]{1,0:T(8,128)(2,1)S(1)} collective-permute-done((bf16[1024,128]{1,0:T(8,128)(2,1)S(1)}, bf16[1024,128]{1,0:T(8,128)(2,1)S(1)}, u32[]{:S(2)}, u32[]{:S(2)}) %collective-permute-start.5) | collective-permute-done | bytes 262176 | tf_op jit(solution)/shard_map/ppermute | solution.py:196
  97.6 5.7 %collective-permute-done.7 = bf16[1024,128]{1,0:T(8,128)(2,1)S(1)} collective-permute-done((bf16[1024,128]{1,0:T(8,128)(2,1)S(1)}, bf16[1024,128]{1,0:T(8,128)(2,1)S(1)}, u32[]{:S(2)}, u32[]{:S(2)}) %collective-permute-start.7) | collective-permute-done | bytes 262176 | tf_op jit(solution)/shard_map/ppermute | solution.py:196
  105.9 2.6 %copy-done.6 = f32[2,2,2,2,2,32,1536]{6,5,4,3,2,1,0:T(8,128)} copy-done((f32[2,2,2,2,2,32,1536]{6,5,4,3,2,1,0:T(8,128)}, f32[2,2,2,2,2,32,1536]{6,5,4,3,2,1,0:T(8,128)S(1)}, u32[]{:S(2)}) %copy-start.6) | copy-done | bytes 6291480
  112.5 1.5 collective-permute-done.18
  115.5 1.7 %collective-permute-start.19 = (bf16[2,2,2,16,1024]{4,3,2,1,0:T(8,128)(2,1)S(1)}, bf16[2,2,2,16,1024]{4,3,2,1,0:T(8,128)(2,1)S(1)}, u32[]{:S(2)}, u32[]{:S(2)}) collective-permute-start(bf16[2,2,2,16,1024]{4,3,2,1,0:T(8,128)(2,1)S(1)} %fusion.40), channel_id=1, source_target_pairs={{0,8},{1,9},{2,10},{3,11},{4,20},{5,21},{6,22},{7,23},{8,0},{9,1},... | collective-permute-start | bytes 786440 | tf_op jit(solution)/shard_map/ppermute | solution.py:169
  117.2 2.9 %bitcast_add_fusion = f32[2,2,2,2,32,1536]{5,4,3,2,1,0:T(8,128)S(1)} fusion(bf16[2,2,2,2,32,1536]{5,4,3,2,1,0:T(8,128)(2,1)} %collective-permute-done.13, f32[2,2,2,2,2,32,1536]{6,5,4,3,2,1,0:T(8,128)} %copy-done.6, s32[]{:T(128)S(6)} %select_n.279), kind=kLoop, calls=%fused_computation.12 | loop fusion | flops 1572864 | bytes 7864324 | tf_op jit(solution)/shard_map/add | solution.py:173
  120.1 1.6 %copy-done.4 = f32[2,2,2,2,32,1536]{5,4,3,2,1,0:T(8,128)} copy-done((f32[2,2,2,2,32,1536]{5,4,3,2,1,0:T(8,128)}, f32[2,2,2,2,32,1536]{5,4,3,2,1,0:T(8,128)S(1)}, u32[]{:S(2)}) %copy-start.4) | copy-done | bytes 3145752
  124.1 3.3 %fusion.19 = f32[1024]{0:T(1024)S(1)} fusion(bf16[1024,1536]{1,0:T(8,128)(2,1)} %param.9, f32[128]{0:T(128)S(1)} %copy-done.33, f32[128]{0:T(128)S(1)} %broadcast_multiply_fusion.1, bf16[1024,128]{1,0:T(8,128)(2,1)S(1)} %fusion.39, bf16[512,128]{1,0:T(8,128)(2,1)S(1)} %bitcast.237, bf16[128,2048]{1,0:T(8,128)(2,1)S(1)} %scatter_custom_fusion), kind=kOutput, calls=%fused_computation.33 | convolution fusion | flops 404093952 | bytes 3806208 | tf_op jit(solution)/shard_map/ct,fc->tf/dot_general | solution.py:314
  128.3 6.7 %collective-permute-done.14 = bf16[2,2,2,32,1536]{4,3,2,1,0:T(8,128)(2,1)S(1)} collective-permute-done((bf16[2,2,2,32,1536]{4,3,2,1,0:T(8,128)(2,1)}, bf16[2,2,2,32,1536]{4,3,2,1,0:T(8,128)(2,1)S(1)}, u32[]{:S(2)}, u32[]{:S(2)}) %collective-permute-start.14) | collective-permute-done | bytes 786464 | tf_op jit(solution)/shard_map/ppermute | solution.py:171
  137.4 1.6 %collective-permute-start.21 = (bf16[2,16,1024]{2,1,0:T(8,128)(2,1)S(1)}, bf16[2,16,1024]{2,1,0:T(8,128)(2,1)S(1)}, u32[]{:S(2)}, u32[]{:S(2)}) collective-permute-start(bf16[2,16,1024]{2,1,0:T(8,128)(2,1)S(1)} %fusion.62), channel_id=1, source_target_pairs={{0,1},{1,0},{2,3},{3,2},{4,12},{5,13},{6,14},{7,15},{8,9},{9,8},{1... | collective-permute-start | bytes 196616 | tf_op jit(solution)/shard_map/ppermute | solution.py:169
  139.1 1.6 %collective-permute-done.9 = f32[1025]{0:T(1024)S(1)} collective-permute-done((f32[1025]{0:T(1024)S(1)}, f32[1025]{0:T(1024)S(1)}, u32[]{:S(2)}, u32[]{:S(2)}) %collective-permute-start.9) | collective-permute-done | bytes 4132 | tf_op jit(solution)/shard_map/ppermute | solution.py:171
  143.7 1.6 collective-permute-start.16
  145.9 2.6 %collective-permute-start.22 = (bf16[16,1024]{1,0:T(8,128)(2,1)S(1)}, bf16[16,1024]{1,0:T(8,128)(2,1)S(1)}, u32[]{:S(2)}, u32[]{:S(2)}) collective-permute-start(bf16[16,1024]{1,0:T(8,128)(2,1)S(1)} %fusion.64), channel_id=1, source_target_pairs={{0,2},{1,3},{2,0},{3,1},{4,6},{5,7},{6,4},{7,5},{8,10},{9,11},{10,... | collective-permute-start | bytes 98312 | tf_op jit(solution)/shard_map/ppermute | solution.py:169
  149.8 2.5 %collective-permute-start.12 = (f32[1025]{0:T(1024)S(1)}, f32[1025]{0:T(1024)S(1)}, u32[]{:S(2)}, u32[]{:S(2)}) collective-permute-start(f32[1025]{0:T(1024)S(1)} %add.327), channel_id=1, source_target_pairs={{0,2},{1,3},{2,0},{3,1},{4,6},{5,7},{6,4},{7,5},{8,10},{9,11},{10,... | collective-permute-start | bytes 12308 | tf_op jit(solution)/shard_map/ppermute | solution.py:171
  156.2 1.8 %collective-permute-done.17 = bf16[32,1536]{1,0:T(8,128)(2,1)S(1)} collective-permute-done((bf16[32,1536]{1,0:T(8,128)(2,1)S(1)}, bf16[32,1536]{1,0:T(8,128)(2,1)S(1)}, u32[]{:S(2)}, u32[]{:S(2)}) %collective-permute-start.17) | collective-permute-done | bytes 98336 | tf_op jit(solution)/shard_map/ppermute | solution.py:171
  (190 shorter events, 58.2 us)
Async XLA Ops:
  0.6 15.1 %copy-start = (bf16[1,512,1024]{2,1,0:T(8,128)(2,1)S(1)}, bf16[1,512,1024]{2,1,0:T(8,128)(2,1)}, u32[]{:S(2)}) copy-start(bf16[1,512,1024]{2,1,0:T(8,128)(2,1)} %param.7) | copy-start | bytes 3145732
  0.6 16.1 %copy-start.7 = (bf16[1,512,1024]{2,1,0:T(8,128)(2,1)S(1)}, bf16[1,512,1024]{2,1,0:T(8,128)(2,1)}, u32[]{:S(2)}) copy-start(bf16[1,512,1024]{2,1,0:T(8,128)(2,1)} %param.6) | copy-start | bytes 3145732
  3.4 9.8 %all-to-all-start = ((s32[8,1,1]{2,1,0:T(1,128)}), s32[8,1,1]{2,1,0:T(1,128)S(1)}, u32[]{:S(2)}, u32[]{:S(2)}) async-start(s32[8,1,1]{2,1,0:T(1,128)} %broadcast_in_dim.47), calls=%async_computation | async-start | bytes 8192 | tf_op jit(solution)/shard_map/all_to_all | solution.py:211
  20.1 19.3 %copy-start.23 = (f32[1024]{0:T(1024)S(1)}, f32[1024]{0:T(1024)}, u32[]{:S(2)}) copy-start(f32[1024]{0:T(1024)} %param.11) | copy-start | bytes 12292
  21.0 16.1 %all-to-all-start.1 = ((bf16[8,24,2048]{2,1,0:T(8,128)(2,1)}), bf16[8,24,2048]{2,1,0:T(8,128)(2,1)S(1)}, u32[]{:S(2)}, u32[]{:S(2)}) async-start(bf16[8,24,2048]{2,1,0:T(8,128)(2,1)} %pad_maximum_fusion.3), calls=%async_computation.1 | async-start | bytes 1572864 | tf_op jit(solution)/shard_map/all_to_all | solution.py:228
  39.6 16.3 %copy-start.16 = (bf16[128,1024]{1,0:T(8,128)(2,1)}, bf16[128,1024]{1,0:T(8,128)(2,1)S(1)}, u32[]{:S(2)}) copy-start(bf16[128,1024]{1,0:T(8,128)(2,1)S(1)} %fusion.29) | copy-start | bytes 786436
  41.8 9.7 %collective-permute-start.2 = (bf16[1024,128]{0,1:T(8,128)(2,1)S(1)}, bf16[1024,128]{0,1:T(8,128)(2,1)S(1)}, u32[]{:S(2)}, u32[]{:S(2)}) collective-permute-start(bf16[1024,128]{0,1:T(8,128)(2,1)S(1)} %bitcast.229), channel_id=1, source_target_pairs={{0,24},{4,28},{8,16},{12,20},{16,8},{20,12},{24,0},{28,4},{1,25},{... | collective-permute-start | bytes 786440 | tf_op jit(solution)/shard_map/ppermute | solution.py:184
  42.4 11.9 %collective-permute-start.1 = (bf16[1024,128]{0,1:T(8,128)(2,1)S(1)}, bf16[1024,128]{0,1:T(8,128)(2,1)S(1)}, u32[]{:S(2)}, u32[]{:S(2)}) collective-permute-start(bf16[1024,128]{0,1:T(8,128)(2,1)S(1)} %bitcast.230), channel_id=1, source_target_pairs={{0,16},{4,20},{8,24},{12,28},{16,0},{20,4},{24,8},{28,12},{1,17},{... | collective-permute-start | bytes 786440 | tf_op jit(solution)/shard_map/ppermute | solution.py:184
  43.8 10.7 %collective-permute-start = (bf16[1024,128]{0,1:T(8,128)(2,1)S(1)}, bf16[1024,128]{0,1:T(8,128)(2,1)S(1)}, u32[]{:S(2)}, u32[]{:S(2)}) collective-permute-start(bf16[1024,128]{0,1:T(8,128)(2,1)S(1)} %bitcast.231), channel_id=1, source_target_pairs={{0,8},{4,12},{8,0},{12,4},{16,24},{20,28},{24,16},{28,20},{1,9},{5... | collective-permute-start | bytes 786440 | tf_op jit(solution)/shard_map/ppermute | solution.py:184
  55.6 7.1 %collective-permute-start.3 = (bf16[4,1024,128]{1,2,0:T(8,128)(2,1)}, bf16[4,1024,128]{1,2,0:T(8,128)(2,1)}, u32[]{:S(2)}, u32[]{:S(2)}) collective-permute-start(bf16[4,1024,128]{1,2,0:T(8,128)(2,1)} %pad_maximum_fusion.1), channel_id=1, source_target_pairs={{0,4},{4,0},{8,12},{12,8},{16,20},{20,16},{24,28},{28,24},{1,5},{5... | collective-permute-start | bytes 3145736 | tf_op jit(solution)/shard_map/ppermute | solution.py:186
  57.6 14.6 %copy-start.24 = (f32[128]{0:T(128)}, f32[128]{0:T(128)S(1)}, u32[]{:S(2)}) copy-start(f32[128]{0:T(128)S(1)} %add_rsqrt_fusion) | copy-start | bytes 1540
  82.8 3.8 %collective-permute-start.4 = (bf16[4,1024,128]{2,1,0:T(8,128)(2,1)}, bf16[4,1024,128]{2,1,0:T(8,128)(2,1)}, u32[]{:S(2)}, u32[]{:S(2)}) collective-permute-start(bf16[4,1024,128]{2,1,0:T(8,128)(2,1)} %bitcast.36), channel_id=1, source_target_pairs={{0,4},{4,0},{8,12},{12,8},{16,20},{20,16},{24,28},{28,24},{1,5},{5... | collective-permute-start | bytes 3145736 | tf_op jit(solution)/shard_map/ppermute | solution.py:192
  88.4 9.2 %collective-permute-start.5 = (bf16[1024,128]{1,0:T(8,128)(2,1)S(1)}, bf16[1024,128]{1,0:T(8,128)(2,1)S(1)}, u32[]{:S(2)}, u32[]{:S(2)}) collective-permute-start(bf16[1024,128]{1,0:T(8,128)(2,1)S(1)} %get-tuple-element.12), channel_id=1, source_target_pairs={{0,8},{4,12},{8,0},{12,4},{16,24},{20,28},{24,16},{28,20},{1,9},{5... | collective-permute-start | bytes 786440 | tf_op jit(solution)/shard_map/ppermute | solution.py:196
  90.3 13.0 %collective-permute-start.7 = (bf16[1024,128]{1,0:T(8,128)(2,1)S(1)}, bf16[1024,128]{1,0:T(8,128)(2,1)S(1)}, u32[]{:S(2)}, u32[]{:S(2)}) collective-permute-start(bf16[1024,128]{1,0:T(8,128)(2,1)S(1)} %get-tuple-element.13), channel_id=1, source_target_pairs={{0,24},{4,28},{8,16},{12,20},{16,8},{20,12},{24,0},{28,4},{1,25},{... | collective-permute-start | bytes 786440 | tf_op jit(solution)/shard_map/ppermute | solution.py:196
  91.4 13.5 %copy-start.21 = (bf16[128,1024]{0,1:T(8,128)(2,1)S(1)}, bf16[128,1024]{0,1:T(8,128)(2,1)}, u32[]{:S(2)}) copy-start(bf16[128,1024]{0,1:T(8,128)(2,1)} %copy.89) | copy-start | bytes 786436
  91.4 13.3 %collective-permute-start.6 = (bf16[1024,128]{1,0:T(8,128)(2,1)S(1)}, bf16[1024,128]{1,0:T(8,128)(2,1)S(1)}, u32[]{:S(2)}, u32[]{:S(2)}) collective-permute-start(bf16[1024,128]{1,0:T(8,128)(2,1)S(1)} %get-tuple-element.14), channel_id=1, source_target_pairs={{0,16},{4,20},{8,24},{12,28},{16,0},{20,4},{24,8},{28,12},{1,17},{... | collective-permute-start | bytes 786440 | tf_op jit(solution)/shard_map/ppermute | solution.py:196
  109.9 7.3 %collective-permute-start.13 = (bf16[2,2,2,2,32,1536]{5,4,3,2,1,0:T(8,128)(2,1)}, bf16[2,2,2,2,32,1536]{5,4,3,2,1,0:T(8,128)(2,1)}, u32[]{:S(2)}, u32[]{:S(2)}) collective-permute-start(bf16[2,2,2,2,32,1536]{5,4,3,2,1,0:T(8,128)(2,1)} %fusion.13), channel_id=1, source_target_pairs={{0,4},{1,5},{2,6},{3,7},{4,0},{5,1},{6,2},{7,3},{8,12},{9,13},{10,... | collective-permute-start | bytes 4718600 | tf_op jit(solution)/shard_map/ppermute | solution.py:171
  112.0 2.1 %collective-permute-start.18 = (bf16[2,2,2,2,16,1024]{5,4,3,2,1,0:T(8,128)(2,1)S(1)}, bf16[2,2,2,2,16,1024]{5,4,3,2,1,0:T(8,128)(2,1)S(1)}, u32[]{:S(2)}, u32[]{:S(2)}) collective-permute-start(bf16[2,2,2,2,16,1024]{5,4,3,2,1,0:T(8,128)(2,1)S(1)} %fusion.33), channel_id=1, source_target_pairs={{0,4},{1,5},{2,6},{3,7},{4,0},{5,1},{6,2},{7,3},{8,12},{9,13},{10,... | collective-permute-start | bytes 1572872 | tf_op jit(solution)/shard_map/ppermute | solution.py:169
  115.5 7.7 %collective-permute-start.19 = (bf16[2,2,2,16,1024]{4,3,2,1,0:T(8,128)(2,1)S(1)}, bf16[2,2,2,16,1024]{4,3,2,1,0:T(8,128)(2,1)S(1)}, u32[]{:S(2)}, u32[]{:S(2)}) collective-permute-start(bf16[2,2,2,16,1024]{4,3,2,1,0:T(8,128)(2,1)S(1)} %fusion.40), channel_id=1, source_target_pairs={{0,8},{1,9},{2,10},{3,11},{4,20},{5,21},{6,22},{7,23},{8,0},{9,1},... | collective-permute-start | bytes 786440 | tf_op jit(solution)/shard_map/ppermute | solution.py:169
  122.8 12.2 %collective-permute-start.14 = (bf16[2,2,2,32,1536]{4,3,2,1,0:T(8,128)(2,1)}, bf16[2,2,2,32,1536]{4,3,2,1,0:T(8,128)(2,1)S(1)}, u32[]{:S(2)}, u32[]{:S(2)}) collective-permute-start(bf16[2,2,2,32,1536]{4,3,2,1,0:T(8,128)(2,1)} %fusion.14), channel_id=1, source_target_pairs={{0,8},{1,9},{2,10},{3,11},{4,20},{5,21},{6,22},{7,23},{8,0},{9,1},... | collective-permute-start | bytes 2359304 | tf_op jit(solution)/shard_map/ppermute | solution.py:171
  123.3 12.9 %collective-permute-start.20 = (bf16[2,2,16,1024]{3,2,1,0:T(8,128)(2,1)S(1)}, bf16[2,2,16,1024]{3,2,1,0:T(8,128)(2,1)S(1)}, u32[]{:S(2)}, u32[]{:S(2)}) collective-permute-start(bf16[2,2,16,1024]{3,2,1,0:T(8,128)(2,1)S(1)} %fusion.52), channel_id=1, source_target_pairs={{0,16},{1,17},{2,18},{3,19},{4,5},{5,4},{6,7},{7,6},{8,24},{9,25},... | collective-permute-start | bytes 393224 | tf_op jit(solution)/shard_map/ppermute | solution.py:169
  128.0 8.3 %collective-permute-start.8 = (f32[1025]{0:T(1024)S(1)}, f32[1025]{0:T(1024)S(1)}, u32[]{:S(2)}, u32[]{:S(2)}) collective-permute-start(f32[1025]{0:T(1024)S(1)} %pad_maximum_fusion.7), channel_id=1, source_target_pairs={{0,4},{1,5},{2,6},{3,7},{4,0},{5,1},{6,2},{7,3},{8,12},{9,13},{10,... | collective-permute-start | bytes 12308 | tf_op jit(solution)/shard_map/ppermute | solution.py:171
  135.5 7.9 %collective-permute-start.15 = (bf16[2,2,32,1536]{3,2,1,0:T(8,128)(2,1)S(1)}, bf16[2,2,32,1536]{3,2,1,0:T(8,128)(2,1)S(1)}, u32[]{:S(2)}, u32[]{:S(2)}) collective-permute-start(bf16[2,2,32,1536]{3,2,1,0:T(8,128)(2,1)S(1)} %fusion.24), channel_id=1, source_target_pairs={{0,16},{1,17},{2,18},{3,19},{4,5},{5,4},{6,7},{7,6},{8,24},{9,25},... | collective-permute-start | bytes 1179656 | tf_op jit(solution)/shard_map/ppermute | solution.py:171
  137.0 3.7 %collective-permute-start.9 = (f32[1025]{0:T(1024)S(1)}, f32[1025]{0:T(1024)S(1)}, u32[]{:S(2)}, u32[]{:S(2)}) collective-permute-start(f32[1025]{0:T(1024)S(1)} %fusion.68), channel_id=1, source_target_pairs={{0,8},{1,9},{2,10},{3,11},{4,20},{5,21},{6,22},{7,23},{8,0},{9,1},... | collective-permute-start | bytes 12308 | tf_op jit(solution)/shard_map/ppermute | solution.py:171
  137.4 7.8 %collective-permute-start.21 = (bf16[2,16,1024]{2,1,0:T(8,128)(2,1)S(1)}, bf16[2,16,1024]{2,1,0:T(8,128)(2,1)S(1)}, u32[]{:S(2)}, u32[]{:S(2)}) collective-permute-start(bf16[2,16,1024]{2,1,0:T(8,128)(2,1)S(1)} %fusion.62), channel_id=1, source_target_pairs={{0,1},{1,0},{2,3},{3,2},{4,12},{5,13},{6,14},{7,15},{8,9},{9,8},{1... | collective-permute-start | bytes 196616 | tf_op jit(solution)/shard_map/ppermute | solution.py:169
  140.7 4.5 %collective-permute-start.10 = (f32[1025]{0:T(1024)S(1)}, f32[1025]{0:T(1024)S(1)}, u32[]{:S(2)}, u32[]{:S(2)}) collective-permute-start(f32[1025]{0:T(1024)S(1)} %add.325), channel_id=1, source_target_pairs={{0,16},{1,17},{2,18},{3,19},{4,5},{5,4},{6,7},{7,6},{8,24},{9,25},... | collective-permute-start | bytes 12308 | tf_op jit(solution)/shard_map/ppermute | solution.py:171
  143.4 15.3 %copy-start.1 = (bf16[1,512,1024]{2,1,0:T(8,128)(2,1)S(1)}, bf16[1,512,1024]{2,1,0:T(8,128)(2,1)}, u32[]{:S(2)}) copy-start(bf16[1,512,1024]{2,1,0:T(8,128)(2,1)} %param.7) | copy-start | bytes 3145732
  143.7 8.7 %collective-permute-start.16 = (bf16[2,32,1536]{2,1,0:T(8,128)(2,1)S(1)}, bf16[2,32,1536]{2,1,0:T(8,128)(2,1)S(1)}, u32[]{:S(2)}, u32[]{:S(2)}) collective-permute-start(bf16[2,32,1536]{2,1,0:T(8,128)(2,1)S(1)} %fusion.58), channel_id=1, source_target_pairs={{0,1},{1,0},{2,3},{3,2},{4,12},{5,13},{6,14},{7,15},{8,9},{9,8},{1... | collective-permute-start | bytes 589832 | tf_op jit(solution)/shard_map/ppermute | solution.py:171
  145.3 4.6 %collective-permute-start.11 = (f32[1025]{0:T(1024)S(1)}, f32[1025]{0:T(1024)S(1)}, u32[]{:S(2)}, u32[]{:S(2)}) collective-permute-start(f32[1025]{0:T(1024)S(1)} %add.326), channel_id=1, source_target_pairs={{0,1},{1,0},{2,3},{3,2},{4,12},{5,13},{6,14},{7,15},{8,9},{9,8},{1... | collective-permute-start | bytes 12308 | tf_op jit(solution)/shard_map/ppermute | solution.py:171
  145.9 7.0 %collective-permute-start.22 = (bf16[16,1024]{1,0:T(8,128)(2,1)S(1)}, bf16[16,1024]{1,0:T(8,128)(2,1)S(1)}, u32[]{:S(2)}, u32[]{:S(2)}) collective-permute-start(bf16[16,1024]{1,0:T(8,128)(2,1)S(1)} %fusion.64), channel_id=1, source_target_pairs={{0,2},{1,3},{2,0},{3,1},{4,6},{5,7},{6,4},{7,5},{8,10},{9,11},{10,... | collective-permute-start | bytes 98312 | tf_op jit(solution)/shard_map/ppermute | solution.py:169
  149.8 4.6 %collective-permute-start.12 = (f32[1025]{0:T(1024)S(1)}, f32[1025]{0:T(1024)S(1)}, u32[]{:S(2)}, u32[]{:S(2)}) collective-permute-start(f32[1025]{0:T(1024)S(1)} %add.327), channel_id=1, source_target_pairs={{0,2},{1,3},{2,0},{3,1},{4,6},{5,7},{6,4},{7,5},{8,10},{9,11},{10,... | collective-permute-start | bytes 12308 | tf_op jit(solution)/shard_map/ppermute | solution.py:171
  152.4 5.6 %collective-permute-start.17 = (bf16[32,1536]{1,0:T(8,128)(2,1)S(1)}, bf16[32,1536]{1,0:T(8,128)(2,1)S(1)}, u32[]{:S(2)}, u32[]{:S(2)}) collective-permute-start(bf16[32,1536]{1,0:T(8,128)(2,1)S(1)} %fusion.61), channel_id=1, source_target_pairs={{0,2},{1,3},{2,0},{3,1},{4,6},{5,7},{6,4},{7,5},{8,10},{9,11},{10,... | collective-permute-start | bytes 294920 | tf_op jit(solution)/shard_map/ppermute | solution.py:171
  (27 other events, 65.9 us)

commit v22 on v21

--- a/solution.py
+++ b/solution.py
@@ -118,7 +118,7 @@
     return split.transpose(perm).reshape(values.shape)
 
 
-def halving_scatter(grad, small=None):
+def halving_scatter(grad, small=None, split=True):
     seq_bits, clip_bits = exchange_bits()
     total = seq_bits + clip_bits
     seq_n = lax.axis_size("seq")
@@ -128,6 +128,8 @@
     clip_keys = [("clip", bit) for bit in range(clip_bits)]
     order_a = seq_keys + clip_keys
     order_b = [seq_keys[0]] + seq_keys[1:][::-1][:1] + clip_keys[:1] + seq_keys[1:][::-1][1:] + clip_keys[1:]
+    if not split:
+        order_b = list(order_a)
     me_seq = lax.axis_index("seq")
     me_clip = lax.axis_index("clip")
     core_bit = me_seq & 1
@@ -315,7 +317,7 @@
     grad_ln = jnp.sum(d_hidden * normed, axis=0)
     loss_part = jnp.sum(token_loss)
     small = jnp.concatenate([grad_ln, loss_part.reshape(1)])
-    grad_out, unused = halving_scatter(grad_wout)
+    grad_out, unused = halving_scatter(grad_wout, split=False)
     grad_qkv, small = halving_scatter(grad_wqkv, small)
     count_all = shards * lax.axis_size("clip") * TOK_DEV
     return (small[-1] / count_all, grad_qkv.reshape(-1), grad_out.reshape(-1), small[:-1])

time: 161 us -> 160 us (level)
  local copies, waits for them, and re-layouts: 33.5 us -> 31.8 us
    unnamed x73 -> x71, local copies, waits for them, and re-layouts: 10.9 us -> 8.99 us
    ppermute x5, waiting for transfers between devices: 1.55 us -> 3.3 us  [halving_scatter(): got = lax.ppermute(give.astype(jnp.bfloat16), ('seq', 'clip'), pairs)]
  transfers between devices with their start and end apart: 25 -> 25, of which waited for: 15 -> 16; matrix products, arithmetic and copies ran while one was open for 15% -> 15% of each run, Pallas kernels for 0% -> 0%
where the time goes in v22:
time: 160 us; the launch traced here: 159 us
  waiting for transfers between devices  53.6 us (34%)
  starting transfers between devices  32.8 us (20%)
  local copies, waits for them, and re-layouts  31.8 us (20%)
  matrix products  19.2 us (12%)
  other arithmetic  19 us (12%)
  between operations  3.18 us (2%)
    ppermute x10, waiting for transfers between devices, halving_scatter(): lax.ppermute((give.astype(jnp.bfloat16), small), ('seq', 'clip'), pairs)  12.7 us
    all_to_all x1, waiting for transfers between devices, per_device(): lax.all_to_all(jnp.concatenate([send_tokens, send_target], axis=2), 'seq'...  12.3 us
    ppermute x3, waiting for transfers between devices, return_blocks(): sent = lax.ppermute(summed[k].astype(jnp.bfloat16), 'seq', xor_pairs(2 * k))  12.2 us
    ppermute x3, waiting for transfers between devices, gather_blocks(): lax.ppermute(block, 'seq', xor_pairs(2 * k))  9.21 us
    ppermute x10, starting transfers between devices, halving_scatter(): lax.ppermute((give.astype(jnp.bfloat16), small), ('seq', 'clip'), pairs)  9.17 us
    unnamed x71, local copies, waits for them, and re-layouts  8.99 us
    ppermute x5, starting transfers between devices, halving_scatter(): got = lax.ppermute(give.astype(jnp.bfloat16), ('seq', 'clip'), pairs)  7.25 us
    all_to_all x1, starting transfers between devices, per_device(): lax.all_to_all(jnp.broadcast_to(kept_count.reshape(1, 1), (shards, 1)), '...  5.17 us
  transfers between devices with their start and end apart: 25, of which 16 were waited for; matrix products, arithmetic and copies ran while one was open for 15% of the time, Pallas kernels for 0%

profile of v22, /device:TPU:0, one launch (start us, length us, event | category | flops | bytes accessed | tf_op | source)
XLA Modules:
  0.0 159.5 jit_solution(4582471953488298411)
XLA Ops:
  3.4 5.2 %all-to-all-start = ((s32[8,1,1]{2,1,0:T(1,128)}), s32[8,1,1]{2,1,0:T(1,128)S(1)}, u32[]{:S(2)}, u32[]{:S(2)}) async-start(s32[8,1,1]{2,1,0:T(1,128)} %broadcast_in_dim.47), calls=%async_computation | async-start | bytes 8192 | tf_op jit(solution)/shard_map/all_to_all | solution.py:213
  9.2 3.9 %all-to-all-done = s32[8,1,1]{2,1,0:T(1,128)S(1)} async-done(((s32[8,1,1]{2,1,0:T(1,128)}), s32[8,1,1]{2,1,0:T(1,128)S(1)}, u32[]{:S(2)}, u32[]{:S(2)}) %all-to-all-start) | async-done | bytes 64 | tf_op jit(solution)/shard_map/all_to_all | solution.py:213
  21.1 3.5 %all-to-all-start.1 = ((bf16[8,24,2048]{2,1,0:T(8,128)(2,1)}), bf16[8,24,2048]{2,1,0:T(8,128)(2,1)S(1)}, u32[]{:S(2)}, u32[]{:S(2)}) async-start(bf16[8,24,2048]{2,1,0:T(8,128)(2,1)} %pad_maximum_fusion.3), calls=%async_computation.1 | async-start | bytes 1572864 | tf_op jit(solution)/shard_map/all_to_all | solution.py:230
  24.9 12.3 %all-to-all-done.1 = bf16[8,24,2048]{2,1,0:T(8,128)(2,1)S(1)} async-done(((bf16[8,24,2048]{2,1,0:T(8,128)(2,1)}), bf16[8,24,2048]{2,1,0:T(8,128)(2,1)S(1)}, u32[]{:S(2)}, u32[]{:S(2)}) %all-to-all-start.1) | async-done | bytes 786464 | tf_op jit(solution)/shard_map/all_to_all | solution.py:230
  37.1 1.8 %scatter_custom_fusion = bf16[128,2048]{1,0:T(8,128)(2,1)S(1)} fusion(s32[192]{0:T(256)S(1)} %bitcast.228, bf16[192,2048]{1,0:T(8,128)(2,1)S(1)} %bitcast.219, bf16[]{:T(256)} %constant.173.clone.1), kind=kCustom, calls=%fused_computation.109 | custom fusion | bytes 524290 | tf_op jit(solution)/shard_map/scatter | solution.py:240
  39.6 2.1 %fusion.16 = bf16[128,1024]{1,0:T(8,128)(2,1)S(1)} fusion(bf16[128,1024]{1,0:T(8,128)(2,1)S(1)} %fusion.29, bf16[1024,1536]{1,0:T(8,128)(2,1)} %param.9), kind=kOutput, calls=%fused_computation.32 | convolution fusion | flops 268566528 | bytes 2621440 | tf_op jit(solution)/shard_map/dot_general | solution.py:254
  43.8 1.5 collective-permute-start
  45.3 6.2 %collective-permute-done.2 = bf16[1024,128]{0,1:T(8,128)(2,1)S(1)} collective-permute-done((bf16[1024,128]{0,1:T(8,128)(2,1)S(1)}, bf16[1024,128]{0,1:T(8,128)(2,1)S(1)}, u32[]{:S(2)}, u32[]{:S(2)}) %collective-permute-start.2) | collective-permute-done | bytes 262176 | tf_op jit(solution)/shard_map/ppermute | solution.py:186
  51.5 2.8 %collective-permute-done.1 = bf16[1024,128]{0,1:T(8,128)(2,1)S(1)} collective-permute-done((bf16[1024,128]{0,1:T(8,128)(2,1)S(1)}, bf16[1024,128]{0,1:T(8,128)(2,1)S(1)}, u32[]{:S(2)}, u32[]{:S(2)}) %collective-permute-start.1) | collective-permute-done | bytes 262176 | tf_op jit(solution)/shard_map/ppermute | solution.py:186
  55.9 1.5 convolution_convert_fusion.1
  59.9 1.8 %copy.71 = bf16[1024,128]{1,0:T(8,128)(2,1)} copy(bf16[1024,128]{0,1:T(8,128)(2,1)} %copy-done.21) | data formatting | bytes 524288 | tf_op jit(solution)/shard_map/ppermute | solution.py:186
  62.7 2.3 %copy.74 = bf16[4,1024,128]{2,1,0:T(8,128)(2,1)} copy(bf16[4,1024,128]{1,2,0:T(8,128)(2,1)} %collective-permute-done.3) | data formatting | bytes 2097152 | tf_op jit(solution)/shard_map/ppermute | solution.py:188
  69.2 1.6 %fusion.50 = (bf16[128,8,64]{0,2,1:T(8,128)(2,1)S(1)}, f32[8,128,64,1]{1,2,0,3:T(8,128)}) fusion(f32[128,8]{0,1:T(8,128)S(1)} %bitcast.225, f32[8,8,128,128]{2,3,1,0:T(8,128)S(1)} %get-tuple-element.26, f32[8,128]{1,0:T(8,128)S(1)} %get-tuple-element.25, bf16[8,8,2,64,128]{4,3,2,1,0:T(8,128)(2,1)S(1)} %constant_dynamic-update-slice_fusion), kind=kOutput, calls=%fused_computation.102 | convolution fusion | flops 137494528 | bytes 5644288 | tf_op jit(solution)/shard_map/ihqt,ihdt->ihqd/dot_general | solution.py:269
  72.9 3.9 %fusion.3 = f32[8,8,64,128]{3,2,1,0:T(8,128)S(1)} fusion(f32[8,8,128,128]{2,3,1,0:T(8,128)} %copy-done.2, f32[8,128]{1,0:T(8,128)S(1)} %log_add_fusion, bf16[8,128,64]{1,2,0:T(8,128)(2,1)S(1)} %bitcast.200), kind=kOutput, calls=%fused_computation.14 | convolution fusion | flops 137363456 | bytes 6426624 | tf_op jit(solution)/shard_map/ihqd,ihqt->ihdt/dot_general | solution.py:297
  78.4 1.5 convolution_multiply_fusion
  86.1 1.7 %fusion.71 = (bf16[4,1024,128]{2,1,0:T(8,128)(2,1)S(1)}, f32[4,1024,128]{2,1,0:T(8,128)S(1)}) fusion(bf16[4,1024,128]{2,1,0:T(8,128)(2,1)} %collective-permute-done.4, f32[4,8,2,64,128]{4,3,2,1,0:T(8,128)S(1)} %copy.87), kind=kLoop, calls=%fused_computation.169 | loop fusion | flops 1572864 | bytes 6291456 | tf_op jit(solution)/shard_map/convert.5
  87.8 1.9 %collective-permute-start.5 = (bf16[1024,128]{1,0:T(8,128)(2,1)S(1)}, bf16[1024,128]{1,0:T(8,128)(2,1)S(1)}, u32[]{:S(2)}, u32[]{:S(2)}) collective-permute-start(bf16[1024,128]{1,0:T(8,128)(2,1)S(1)} %get-tuple-element.12), channel_id=1, source_target_pairs={{0,8},{4,12},{8,0},{12,4},{16,24},{20,28},{24,16},{28,20},{1,9},{5... | collective-permute-start | bytes 786440 | tf_op jit(solution)/shard_map/ppermute | solution.py:198
  92.0 5.1 %collective-permute-done.5 = bf16[1024,128]{1,0:T(8,128)(2,1)S(1)} collective-permute-done((bf16[1024,128]{1,0:T(8,128)(2,1)S(1)}, bf16[1024,128]{1,0:T(8,128)(2,1)S(1)}, u32[]{:S(2)}, u32[]{:S(2)}) %collective-permute-start.5) | collective-permute-done | bytes 262176 | tf_op jit(solution)/shard_map/ppermute | solution.py:198
  97.1 5.7 %collective-permute-done.7 = bf16[1024,128]{1,0:T(8,128)(2,1)S(1)} collective-permute-done((bf16[1024,128]{1,0:T(8,128)(2,1)S(1)}, bf16[1024,128]{1,0:T(8,128)(2,1)S(1)}, u32[]{:S(2)}, u32[]{:S(2)}) %collective-permute-start.7) | collective-permute-done | bytes 262176 | tf_op jit(solution)/shard_map/ppermute | solution.py:198
  105.3 2.6 %copy-done.6 = f32[2,2,2,2,2,32,1536]{6,5,4,3,2,1,0:T(8,128)} copy-done((f32[2,2,2,2,2,32,1536]{6,5,4,3,2,1,0:T(8,128)}, f32[2,2,2,2,2,32,1536]{6,5,4,3,2,1,0:T(8,128)S(1)}, u32[]{:S(2)}) %copy-start.6) | copy-done | bytes 6291480
  108.0 1.5 fusion.13
  110.7 3.0 %collective-permute-done.18 = bf16[2,2,2,2,16,1024]{5,4,3,2,1,0:T(8,128)(2,1)} collective-permute-done((bf16[2,2,2,2,16,1024]{5,4,3,2,1,0:T(8,128)(2,1)S(1)}, bf16[2,2,2,2,16,1024]{5,4,3,2,1,0:T(8,128)(2,1)}, u32[]{:S(2)}, u32[]{:S(2)}) %collective-permute-start.18) | collective-permute-done | bytes 524320 | tf_op jit(solution)/shard_map/ppermute | solution.py:171
  115.0 1.7 %collective-permute-start.19 = (bf16[2,2,2,16,1024]{4,3,2,1,0:T(8,128)(2,1)S(1)}, bf16[2,2,2,16,1024]{4,3,2,1,0:T(8,128)(2,1)S(1)}, u32[]{:S(2)}, u32[]{:S(2)}) collective-permute-start(bf16[2,2,2,16,1024]{4,3,2,1,0:T(8,128)(2,1)S(1)} %fusion.46), channel_id=1, source_target_pairs={{0,8},{1,9},{2,10},{3,11},{4,12},{5,13},{6,14},{7,15},{8,0},{9,1},... | collective-permute-start | bytes 786440 | tf_op jit(solution)/shard_map/ppermute | solution.py:171
  116.8 2.9 %bitcast_add_fusion = f32[2,2,2,2,32,1536]{5,4,3,2,1,0:T(8,128)S(1)} fusion(bf16[2,2,2,2,32,1536]{5,4,3,2,1,0:T(8,128)(2,1)} %collective-permute-done.13, f32[2,2,2,2,2,32,1536]{6,5,4,3,2,1,0:T(8,128)} %copy-done.6, s32[]{:T(128)S(6)} %select_n.255), kind=kLoop, calls=%fused_computation.12 | loop fusion | flops 1572864 | bytes 7864324 | tf_op jit(solution)/shard_map/add | solution.py:175
  119.7 1.6 %copy-done.4 = f32[2,2,2,2,32,1536]{5,4,3,2,1,0:T(8,128)} copy-done((f32[2,2,2,2,32,1536]{5,4,3,2,1,0:T(8,128)}, f32[2,2,2,2,32,1536]{5,4,3,2,1,0:T(8,128)S(1)}, u32[]{:S(2)}) %copy-start.4) | copy-done | bytes 3145752
  124.5 3.3 %fusion.19 = f32[1024]{0:T(1024)S(1)} fusion(bf16[1024,1536]{1,0:T(8,128)(2,1)} %param.9, f32[128]{0:T(128)S(1)} %copy-done.32, f32[128]{0:T(128)S(1)} %broadcast_multiply_fusion.1, bf16[1024,128]{1,0:T(8,128)(2,1)S(1)} %fusion.39, bf16[512,128]{1,0:T(8,128)(2,1)S(1)} %bitcast.221, bf16[128,2048]{1,0:T(8,128)(2,1)S(1)} %scatter_custom_fusion), kind=kOutput, calls=%fused_computation.33 | convolution fusion | flops 404093952 | bytes 3806208 | tf_op jit(solution)/shard_map/ct,fc->tf/dot_general | solution.py:316
  128.5 6.0 %collective-permute-done.14 = bf16[2,2,2,32,1536]{4,3,2,1,0:T(8,128)(2,1)S(1)} collective-permute-done((bf16[2,2,2,32,1536]{4,3,2,1,0:T(8,128)(2,1)}, bf16[2,2,2,32,1536]{4,3,2,1,0:T(8,128)(2,1)S(1)}, u32[]{:S(2)}, u32[]{:S(2)}) %collective-permute-start.14) | collective-permute-done | bytes 786464 | tf_op jit(solution)/shard_map/ppermute | solution.py:173
  137.4 1.6 %collective-permute-start.21 = (bf16[2,16,1024]{2,1,0:T(8,128)(2,1)S(1)}, bf16[2,16,1024]{2,1,0:T(8,128)(2,1)S(1)}, u32[]{:S(2)}, u32[]{:S(2)}) collective-permute-start(bf16[2,16,1024]{2,1,0:T(8,128)(2,1)S(1)} %fusion.60), channel_id=1, source_target_pairs={{0,1},{1,0},{2,3},{3,2},{4,5},{5,4},{6,7},{7,6},{8,9},{9,8},{10,11... | collective-permute-start | bytes 196616 | tf_op jit(solution)/shard_map/ppermute | solution.py:171
  143.2 1.6 %collective-permute-start.16 = (bf16[2,32,1536]{2,1,0:T(8,128)(2,1)S(1)}, bf16[2,32,1536]{2,1,0:T(8,128)(2,1)S(1)}, u32[]{:S(2)}, u32[]{:S(2)}) collective-permute-start(bf16[2,32,1536]{2,1,0:T(8,128)(2,1)S(1)} %fusion.55), channel_id=1, source_target_pairs={{0,1},{1,0},{2,3},{3,2},{4,12},{5,13},{6,14},{7,15},{8,9},{9,8},{1... | collective-permute-start | bytes 589832 | tf_op jit(solution)/shard_map/ppermute | solution.py:173
  145.4 2.6 %collective-permute-start.22 = (bf16[16,1024]{1,0:T(8,128)(2,1)S(1)}, bf16[16,1024]{1,0:T(8,128)(2,1)S(1)}, u32[]{:S(2)}, u32[]{:S(2)}) collective-permute-start(bf16[16,1024]{1,0:T(8,128)(2,1)S(1)} %fusion.62), channel_id=1, source_target_pairs={{0,2},{1,3},{2,0},{3,1},{4,6},{5,7},{6,4},{7,5},{8,10},{9,11},{10,... | collective-permute-start | bytes 98312 | tf_op jit(solution)/shard_map/ppermute | solution.py:171
  149.3 2.6 %collective-permute-start.12 = (f32[1025]{0:T(1024)S(1)}, f32[1025]{0:T(1024)S(1)}, u32[]{:S(2)}, u32[]{:S(2)}) collective-permute-start(f32[1025]{0:T(1024)S(1)} %add.325), channel_id=1, source_target_pairs={{0,2},{1,3},{2,0},{3,1},{4,6},{5,7},{6,4},{7,5},{8,10},{9,11},{10,... | collective-permute-start | bytes 12308 | tf_op jit(solution)/shard_map/ppermute | solution.py:173
  155.7 2.0 %collective-permute-done.17 = bf16[32,1536]{1,0:T(8,128)(2,1)S(1)} collective-permute-done((bf16[32,1536]{1,0:T(8,128)(2,1)S(1)}, bf16[32,1536]{1,0:T(8,128)(2,1)S(1)}, u32[]{:S(2)}, u32[]{:S(2)}) %collective-permute-start.17) | collective-permute-done | bytes 98336 | tf_op jit(solution)/shard_map/ppermute | solution.py:173
  (188 shorter events, 56.9 us)
Async XLA Ops:
  0.6 15.1 %copy-start = (bf16[1,512,1024]{2,1,0:T(8,128)(2,1)S(1)}, bf16[1,512,1024]{2,1,0:T(8,128)(2,1)}, u32[]{:S(2)}) copy-start(bf16[1,512,1024]{2,1,0:T(8,128)(2,1)} %param.7) | copy-start | bytes 3145732
  0.6 16.1 %copy-start.7 = (bf16[1,512,1024]{2,1,0:T(8,128)(2,1)S(1)}, bf16[1,512,1024]{2,1,0:T(8,128)(2,1)}, u32[]{:S(2)}) copy-start(bf16[1,512,1024]{2,1,0:T(8,128)(2,1)} %param.6) | copy-start | bytes 3145732
  3.4 9.8 %all-to-all-start = ((s32[8,1,1]{2,1,0:T(1,128)}), s32[8,1,1]{2,1,0:T(1,128)S(1)}, u32[]{:S(2)}, u32[]{:S(2)}) async-start(s32[8,1,1]{2,1,0:T(1,128)} %broadcast_in_dim.47), calls=%async_computation | async-start | bytes 8192 | tf_op jit(solution)/shard_map/all_to_all | solution.py:213
  20.1 19.3 %copy-start.26 = (f32[1024]{0:T(1024)S(1)}, f32[1024]{0:T(1024)}, u32[]{:S(2)}) copy-start(f32[1024]{0:T(1024)} %param.11) | copy-start | bytes 12292
  21.1 16.1 %all-to-all-start.1 = ((bf16[8,24,2048]{2,1,0:T(8,128)(2,1)}), bf16[8,24,2048]{2,1,0:T(8,128)(2,1)S(1)}, u32[]{:S(2)}, u32[]{:S(2)}) async-start(bf16[8,24,2048]{2,1,0:T(8,128)(2,1)} %pad_maximum_fusion.3), calls=%async_computation.1 | async-start | bytes 1572864 | tf_op jit(solution)/shard_map/all_to_all | solution.py:230
  39.6 16.3 %copy-start.17 = (bf16[128,1024]{1,0:T(8,128)(2,1)}, bf16[128,1024]{1,0:T(8,128)(2,1)S(1)}, u32[]{:S(2)}) copy-start(bf16[128,1024]{1,0:T(8,128)(2,1)S(1)} %fusion.29) | copy-start | bytes 786436
  41.8 9.7 %collective-permute-start.2 = (bf16[1024,128]{0,1:T(8,128)(2,1)S(1)}, bf16[1024,128]{0,1:T(8,128)(2,1)S(1)}, u32[]{:S(2)}, u32[]{:S(2)}) collective-permute-start(bf16[1024,128]{0,1:T(8,128)(2,1)S(1)} %bitcast.213), channel_id=1, source_target_pairs={{0,24},{4,28},{8,16},{12,20},{16,8},{20,12},{24,0},{28,4},{1,25},{... | collective-permute-start | bytes 786440 | tf_op jit(solution)/shard_map/ppermute | solution.py:186
  42.4 11.9 %collective-permute-start.1 = (bf16[1024,128]{0,1:T(8,128)(2,1)S(1)}, bf16[1024,128]{0,1:T(8,128)(2,1)S(1)}, u32[]{:S(2)}, u32[]{:S(2)}) collective-permute-start(bf16[1024,128]{0,1:T(8,128)(2,1)S(1)} %bitcast.214), channel_id=1, source_target_pairs={{0,16},{4,20},{8,24},{12,28},{16,0},{20,4},{24,8},{28,12},{1,17},{... | collective-permute-start | bytes 786440 | tf_op jit(solution)/shard_map/ppermute | solution.py:186
  43.8 10.7 %collective-permute-start = (bf16[1024,128]{0,1:T(8,128)(2,1)S(1)}, bf16[1024,128]{0,1:T(8,128)(2,1)S(1)}, u32[]{:S(2)}, u32[]{:S(2)}) collective-permute-start(bf16[1024,128]{0,1:T(8,128)(2,1)S(1)} %bitcast.215), channel_id=1, source_target_pairs={{0,8},{4,12},{8,0},{12,4},{16,24},{20,28},{24,16},{28,20},{1,9},{5... | collective-permute-start | bytes 786440 | tf_op jit(solution)/shard_map/ppermute | solution.py:186
  55.6 7.1 %collective-permute-start.3 = (bf16[4,1024,128]{1,2,0:T(8,128)(2,1)}, bf16[4,1024,128]{1,2,0:T(8,128)(2,1)}, u32[]{:S(2)}, u32[]{:S(2)}) collective-permute-start(bf16[4,1024,128]{1,2,0:T(8,128)(2,1)} %pad_maximum_fusion.1), channel_id=1, source_target_pairs={{0,4},{4,0},{8,12},{12,8},{16,20},{20,16},{24,28},{28,24},{1,5},{5... | collective-permute-start | bytes 3145736 | tf_op jit(solution)/shard_map/ppermute | solution.py:188
  82.3 3.8 %collective-permute-start.4 = (bf16[4,1024,128]{2,1,0:T(8,128)(2,1)}, bf16[4,1024,128]{2,1,0:T(8,128)(2,1)}, u32[]{:S(2)}, u32[]{:S(2)}) collective-permute-start(bf16[4,1024,128]{2,1,0:T(8,128)(2,1)} %bitcast.36), channel_id=1, source_target_pairs={{0,4},{4,0},{8,12},{12,8},{16,20},{20,16},{24,28},{28,24},{1,5},{5... | collective-permute-start | bytes 3145736 | tf_op jit(solution)/shard_map/ppermute | solution.py:194
  87.8 9.2 %collective-permute-start.5 = (bf16[1024,128]{1,0:T(8,128)(2,1)S(1)}, bf16[1024,128]{1,0:T(8,128)(2,1)S(1)}, u32[]{:S(2)}, u32[]{:S(2)}) collective-permute-start(bf16[1024,128]{1,0:T(8,128)(2,1)S(1)} %get-tuple-element.12), channel_id=1, source_target_pairs={{0,8},{4,12},{8,0},{12,4},{16,24},{20,28},{24,16},{28,20},{1,9},{5... | collective-permute-start | bytes 786440 | tf_op jit(solution)/shard_map/ppermute | solution.py:198
  89.8 13.0 %collective-permute-start.7 = (bf16[1024,128]{1,0:T(8,128)(2,1)S(1)}, bf16[1024,128]{1,0:T(8,128)(2,1)S(1)}, u32[]{:S(2)}, u32[]{:S(2)}) collective-permute-start(bf16[1024,128]{1,0:T(8,128)(2,1)S(1)} %get-tuple-element.13), channel_id=1, source_target_pairs={{0,24},{4,28},{8,16},{12,20},{16,8},{20,12},{24,0},{28,4},{1,25},{... | collective-permute-start | bytes 786440 | tf_op jit(solution)/shard_map/ppermute | solution.py:198
  90.9 13.5 %copy-start.22 = (bf16[128,1024]{0,1:T(8,128)(2,1)S(1)}, bf16[128,1024]{0,1:T(8,128)(2,1)}, u32[]{:S(2)}) copy-start(bf16[128,1024]{0,1:T(8,128)(2,1)} %copy.89) | copy-start | bytes 786436
  90.9 13.3 %collective-permute-start.6 = (bf16[1024,128]{1,0:T(8,128)(2,1)S(1)}, bf16[1024,128]{1,0:T(8,128)(2,1)S(1)}, u32[]{:S(2)}, u32[]{:S(2)}) collective-permute-start(bf16[1024,128]{1,0:T(8,128)(2,1)S(1)} %get-tuple-element.14), channel_id=1, source_target_pairs={{0,16},{4,20},{8,24},{12,28},{16,0},{20,4},{24,8},{28,12},{1,17},{... | collective-permute-start | bytes 786440 | tf_op jit(solution)/shard_map/ppermute | solution.py:198
  109.4 7.3 %collective-permute-start.13 = (bf16[2,2,2,2,32,1536]{5,4,3,2,1,0:T(8,128)(2,1)}, bf16[2,2,2,2,32,1536]{5,4,3,2,1,0:T(8,128)(2,1)}, u32[]{:S(2)}, u32[]{:S(2)}) collective-permute-start(bf16[2,2,2,2,32,1536]{5,4,3,2,1,0:T(8,128)(2,1)} %fusion.13), channel_id=1, source_target_pairs={{0,4},{1,5},{2,6},{3,7},{4,0},{5,1},{6,2},{7,3},{8,12},{9,13},{10,... | collective-permute-start | bytes 4718600 | tf_op jit(solution)/shard_map/ppermute | solution.py:173
  110.1 3.6 %collective-permute-start.18 = (bf16[2,2,2,2,16,1024]{5,4,3,2,1,0:T(8,128)(2,1)S(1)}, bf16[2,2,2,2,16,1024]{5,4,3,2,1,0:T(8,128)(2,1)}, u32[]{:S(2)}, u32[]{:S(2)}) collective-permute-start(bf16[2,2,2,2,16,1024]{5,4,3,2,1,0:T(8,128)(2,1)S(1)} %fusion.33), channel_id=1, source_target_pairs={{0,4},{1,5},{2,6},{3,7},{4,0},{5,1},{6,2},{7,3},{8,12},{9,13},{10,... | collective-permute-start | bytes 1572872 | tf_op jit(solution)/shard_map/ppermute | solution.py:171
  115.0 8.4 %collective-permute-start.19 = (bf16[2,2,2,16,1024]{4,3,2,1,0:T(8,128)(2,1)S(1)}, bf16[2,2,2,16,1024]{4,3,2,1,0:T(8,128)(2,1)S(1)}, u32[]{:S(2)}, u32[]{:S(2)}) collective-permute-start(bf16[2,2,2,16,1024]{4,3,2,1,0:T(8,128)(2,1)S(1)} %fusion.46), channel_id=1, source_target_pairs={{0,8},{1,9},{2,10},{3,11},{4,12},{5,13},{6,14},{7,15},{8,0},{9,1},... | collective-permute-start | bytes 786440 | tf_op jit(solution)/shard_map/ppermute | solution.py:171
  122.3 12.2 %collective-permute-start.14 = (bf16[2,2,2,32,1536]{4,3,2,1,0:T(8,128)(2,1)}, bf16[2,2,2,32,1536]{4,3,2,1,0:T(8,128)(2,1)S(1)}, u32[]{:S(2)}, u32[]{:S(2)}) collective-permute-start(bf16[2,2,2,32,1536]{4,3,2,1,0:T(8,128)(2,1)} %fusion.14), channel_id=1, source_target_pairs={{0,8},{1,9},{2,10},{3,11},{4,20},{5,21},{6,22},{7,23},{8,0},{9,1},... | collective-permute-start | bytes 2359304 | tf_op jit(solution)/shard_map/ppermute | solution.py:173
  123.7 10.8 %copy-start.5 = (f32[2,2,2,2,32,1536]{5,4,3,2,1,0:T(8,128)S(1)}, f32[2,2,2,2,32,1536]{5,4,3,2,1,0:T(8,128)}, u32[]{:S(2)}) copy-start(f32[2,2,2,2,32,1536]{5,4,3,2,1,0:T(8,128)} %copy-done.4) | copy-start | bytes 9437188
  123.8 12.0 %collective-permute-start.20 = (bf16[2,2,16,1024]{3,2,1,0:T(8,128)(2,1)S(1)}, bf16[2,2,16,1024]{3,2,1,0:T(8,128)(2,1)S(1)}, u32[]{:S(2)}, u32[]{:S(2)}) collective-permute-start(bf16[2,2,16,1024]{3,2,1,0:T(8,128)(2,1)S(1)} %fusion.56), channel_id=1, source_target_pairs={{0,16},{1,17},{2,18},{3,19},{4,20},{5,21},{6,22},{7,23},{8,24},{9,... | collective-permute-start | bytes 393224 | tf_op jit(solution)/shard_map/ppermute | solution.py:171
  128.4 7.4 %collective-permute-start.8 = (f32[1025]{0:T(1024)S(1)}, f32[1025]{0:T(1024)S(1)}, u32[]{:S(2)}, u32[]{:S(2)}) collective-permute-start(f32[1025]{0:T(1024)S(1)} %pad_maximum_fusion.7), channel_id=1, source_target_pairs={{0,4},{1,5},{2,6},{3,7},{4,0},{5,1},{6,2},{7,3},{8,12},{9,13},{10,... | collective-permute-start | bytes 12308 | tf_op jit(solution)/shard_map/ppermute | solution.py:173
  135.0 7.9 %collective-permute-start.15 = (bf16[2,2,32,1536]{3,2,1,0:T(8,128)(2,1)S(1)}, bf16[2,2,32,1536]{3,2,1,0:T(8,128)(2,1)S(1)}, u32[]{:S(2)}, u32[]{:S(2)}) collective-permute-start(bf16[2,2,32,1536]{3,2,1,0:T(8,128)(2,1)S(1)} %fusion.24), channel_id=1, source_target_pairs={{0,16},{1,17},{2,18},{3,19},{4,5},{5,4},{6,7},{7,6},{8,24},{9,25},... | collective-permute-start | bytes 1179656 | tf_op jit(solution)/shard_map/ppermute | solution.py:173
  136.5 3.7 %collective-permute-start.9 = (f32[1025]{0:T(1024)S(1)}, f32[1025]{0:T(1024)S(1)}, u32[]{:S(2)}, u32[]{:S(2)}) collective-permute-start(f32[1025]{0:T(1024)S(1)} %fusion.66), channel_id=1, source_target_pairs={{0,8},{1,9},{2,10},{3,11},{4,20},{5,21},{6,22},{7,23},{8,0},{9,1},... | collective-permute-start | bytes 12308 | tf_op jit(solution)/shard_map/ppermute | solution.py:173
  137.4 7.4 %collective-permute-start.21 = (bf16[2,16,1024]{2,1,0:T(8,128)(2,1)S(1)}, bf16[2,16,1024]{2,1,0:T(8,128)(2,1)S(1)}, u32[]{:S(2)}, u32[]{:S(2)}) collective-permute-start(bf16[2,16,1024]{2,1,0:T(8,128)(2,1)S(1)} %fusion.60), channel_id=1, source_target_pairs={{0,1},{1,0},{2,3},{3,2},{4,5},{5,4},{6,7},{7,6},{8,9},{9,8},{10,11... | collective-permute-start | bytes 196616 | tf_op jit(solution)/shard_map/ppermute | solution.py:171
  140.2 4.7 %collective-permute-start.10 = (f32[1025]{0:T(1024)S(1)}, f32[1025]{0:T(1024)S(1)}, u32[]{:S(2)}, u32[]{:S(2)}) collective-permute-start(f32[1025]{0:T(1024)S(1)} %add.323), channel_id=1, source_target_pairs={{0,16},{1,17},{2,18},{3,19},{4,5},{5,4},{6,7},{7,6},{8,24},{9,25},... | collective-permute-start | bytes 12308 | tf_op jit(solution)/shard_map/ppermute | solution.py:173
  143.0 15.4 %copy-start.1 = (bf16[1,512,1024]{2,1,0:T(8,128)(2,1)S(1)}, bf16[1,512,1024]{2,1,0:T(8,128)(2,1)}, u32[]{:S(2)}) copy-start(bf16[1,512,1024]{2,1,0:T(8,128)(2,1)} %param.7) | copy-start | bytes 3145732
  143.2 8.8 %collective-permute-start.16 = (bf16[2,32,1536]{2,1,0:T(8,128)(2,1)S(1)}, bf16[2,32,1536]{2,1,0:T(8,128)(2,1)S(1)}, u32[]{:S(2)}, u32[]{:S(2)}) collective-permute-start(bf16[2,32,1536]{2,1,0:T(8,128)(2,1)S(1)} %fusion.55), channel_id=1, source_target_pairs={{0,1},{1,0},{2,3},{3,2},{4,12},{5,13},{6,14},{7,15},{8,9},{9,8},{1... | collective-permute-start | bytes 589832 | tf_op jit(solution)/shard_map/ppermute | solution.py:173
  144.9 4.5 %collective-permute-start.11 = (f32[1025]{0:T(1024)S(1)}, f32[1025]{0:T(1024)S(1)}, u32[]{:S(2)}, u32[]{:S(2)}) collective-permute-start(f32[1025]{0:T(1024)S(1)} %add.324), channel_id=1, source_target_pairs={{0,1},{1,0},{2,3},{3,2},{4,12},{5,13},{6,14},{7,15},{8,9},{9,8},{1... | collective-permute-start | bytes 12308 | tf_op jit(solution)/shard_map/ppermute | solution.py:173
  145.4 7.0 %collective-permute-start.22 = (bf16[16,1024]{1,0:T(8,128)(2,1)S(1)}, bf16[16,1024]{1,0:T(8,128)(2,1)S(1)}, u32[]{:S(2)}, u32[]{:S(2)}) collective-permute-start(bf16[16,1024]{1,0:T(8,128)(2,1)S(1)} %fusion.62), channel_id=1, source_target_pairs={{0,2},{1,3},{2,0},{3,1},{4,6},{5,7},{6,4},{7,5},{8,10},{9,11},{10,... | collective-permute-start | bytes 98312 | tf_op jit(solution)/shard_map/ppermute | solution.py:171
  149.3 4.5 %collective-permute-start.12 = (f32[1025]{0:T(1024)S(1)}, f32[1025]{0:T(1024)S(1)}, u32[]{:S(2)}, u32[]{:S(2)}) collective-permute-start(f32[1025]{0:T(1024)S(1)} %add.325), channel_id=1, source_target_pairs={{0,2},{1,3},{2,0},{3,1},{4,6},{5,7},{6,4},{7,5},{8,10},{9,11},{10,... | collective-permute-start | bytes 12308 | tf_op jit(solution)/shard_map/ppermute | solution.py:173
  152.0 5.6 %collective-permute-start.17 = (bf16[32,1536]{1,0:T(8,128)(2,1)S(1)}, bf16[32,1536]{1,0:T(8,128)(2,1)S(1)}, u32[]{:S(2)}, u32[]{:S(2)}) collective-permute-start(bf16[32,1536]{1,0:T(8,128)(2,1)S(1)} %fusion.59), channel_id=1, source_target_pairs={{0,2},{1,3},{2,0},{3,1},{4,6},{5,7},{6,4},{7,5},{8,10},{9,11},{10,... | collective-permute-start | bytes 294920 | tf_op jit(solution)/shard_map/ppermute | solution.py:173
  (26 other events, 66.1 us)
